TPU v7x, 32 devices: a whole 2x2x4 slice. The times are simulated.
32 devices in a mesh: gx: 16 (over z, y, core), gy: 2 (over x).
Axes of the slice: x: 2, y: 2, z: 4, core: 2. Of those that a mesh axis runs over, the one named last changes fastest.
Arguments:
- eigen_vecs: bfloat16 [2, 3, 4, 64, 32, 512], P(None, None, None, 'gx', 'gy'), may hold values from -6 to 6
- gauge_links: float32 [2, 2, 3, 3, 4, 64, 32], P(None, None, None, None, None, 'gx', 'gy'), may hold values from -4 to 4
- directions: int32 [4], replicated, may hold values from 0 to 3, each once
- spin_map: int32 [4], replicated, may hold values from 0 to 3, each once
- perambulator: bfloat16 [2, 2048, 2048], P(None, ('gx', 'gy')), may hold values from -0.125 to 0.125
Outputs:
- elementals: float32 [4, 2, 512, 512], P(None, None, 'gx')
- contracted: bfloat16 [4, 2, 2048, 2048], P(None, None, ('gx', 'gy'))
Inputs may be any that keep to these rules, and one draw needn't show every extreme that they name: `directions`: a permutation of the four hops: 0 and 1 are forward hops along x and y, 2 and 3 backward hops along x and y. `spin_map`: a permutation of the four spins.
All inputs are finite; a program needn't handle non-finite values.
Results may differ from a plain program's by a relative error of at most 0.0058.
Values may be sent and summed in bfloat16 or wider, within the bound.
No kernel may reach another device: no remote copies, remote signals or barrier semaphores. Data moves between devices by JAX's collectives and lax.ppermute only.
A program may use at most 128 MiB of HBM per device.

v0:
```python
import math

import jax
import jax.numpy as jnp
from jax import lax
from jax.sharding import PartitionSpec as P

ALL = ("gx", "gy")
STREAMS = 3


def colour_apply(gauge_link, colour_field, dagger):
    values = colour_field.astype(jnp.float32)
    rows_re = []
    rows_im = []
    for row in range(3):
        acc_re = jnp.zeros(values.shape[2:], jnp.float32)
        acc_im = jnp.zeros(values.shape[2:], jnp.float32)
        for column in range(3):
            if dagger:
                coef_re = gauge_link[0, column, row][..., None]
                coef_im = -gauge_link[1, column, row][..., None]
            else:
                coef_re = gauge_link[0, row, column][..., None]
                coef_im = gauge_link[1, row, column][..., None]
            acc_re = acc_re + coef_re * values[0, column] - coef_im * values[1, column]
            acc_im = acc_im + coef_re * values[1, column] + coef_im * values[0, column]
        rows_re.append(acc_re)
        rows_im.append(acc_im)
    return jnp.stack([jnp.stack(rows_re, 0), jnp.stack(rows_im, 0)], 0)


def bit_orders(mesh):
    devs = list(mesh.devices.reshape(-1))
    count = len(devs)
    nbits = count.bit_length() - 1

    def dist(a, b):
        try:
            da, db = devs[a], devs[b]
            return sum(abs(p - q) for p, q in zip(da.coords, db.coords))
        except Exception:
            return 1

    near, core, far = [], [], []
    for b in range(nbits):
        d = max(dist(i, i ^ (1 << b)) for i in range(count))
        (core if d == 0 else near if d == 1 else far).append(b)
    orders = []
    for s in range(STREAMS):
        k = s % max(len(near), 1)
        orders.append(core + near[k:] + near[:k] + far)
    return nbits, orders


def xor_pairs(count, b):
    return [(i, i ^ (1 << b)) for i in range(count)]


def reduce_scatter(buf, bits, nbits, count, lead):
    idx = lax.axis_index(ALL)
    for b in bits:
        ax = lead + nbits - 1 - b
        mine = (idx >> b) & 1
        keep = lax.dynamic_slice_in_dim(buf, mine, 1, axis=ax)
        send = lax.dynamic_slice_in_dim(buf, 1 - mine, 1, axis=ax)
        buf = keep + lax.ppermute(send, ALL, xor_pairs(count, b))
    return buf


def all_gather(buf, bits, nbits, count, lead):
    idx = lax.axis_index(ALL)
    for b in bits:
        ax = lead + nbits - 1 - b
        mine = (idx >> b) & 1
        other = lax.ppermute(buf, ALL, xor_pairs(count, b))
        lo = jnp.where(mine == 0, buf, other)
        hi = jnp.where(mine == 0, other, buf)
        buf = jnp.concatenate([lo, hi], axis=ax)
    return buf


def make_local(nbits, orders):
    def local(eigen_vecs, gauge_links, directions, spin_map, perambulator):
        nx = lax.axis_size("gx")
        ny = lax.axis_size("gy")
        count = nx * ny
        _, ncol, nz, lx, ly, nev = eigen_vecs.shape
        norm_factor = 1.0 / math.sqrt(3.0 * nz * lx * ly * count)
        ev = eigen_vecs

        src_x = colour_apply(gauge_links[0], ev, True).astype(jnp.bfloat16)
        src_y = colour_apply(gauge_links[1], ev, True).astype(jnp.bfloat16)
        up_x = lax.ppermute(ev[:, :, :, 0:1], "gx", [(i, (i - 1) % nx) for i in range(nx)])
        dn_x = lax.ppermute(src_x[:, :, :, lx - 1:], "gx", [(i, (i + 1) % nx) for i in range(nx)])
        up_y = lax.ppermute(ev[:, :, :, :, 0:1], "gy", [(i, (i - 1) % ny) for i in range(ny)])
        dn_y = lax.ppermute(src_y[:, :, :, :, ly - 1:], "gy", [(i, (i + 1) % ny) for i in range(ny)])
        ahead_x = jnp.concatenate([ev[:, :, :, 1:], up_x], axis=3)
        ahead_y = jnp.concatenate([ev[:, :, :, :, 1:], up_y], axis=4)
        disp = [
            colour_apply(gauge_links[0], ahead_x, False).astype(jnp.bfloat16),
            colour_apply(gauge_links[1], ahead_y, False).astype(jnp.bfloat16),
            jnp.concatenate([dn_x, src_x[:, :, :, : lx - 1]], axis=3),
            jnp.concatenate([dn_y, src_y[:, :, :, :, : ly - 1]], axis=4),
        ]
        depth = ncol * nz * lx * ly
        flat = ev.reshape(2, depth, nev)
        swapped = jnp.concatenate([-flat[1], flat[0]], axis=0)
        left = jnp.concatenate([flat.reshape(2 * depth, nev), swapped], axis=1)
        rows = nev // count

        prows = perambulator.shape[1]
        nspin = perambulator.shape[2] // nev
        chosen = jnp.take(perambulator.reshape(2, prows, nspin, nev), spin_map, axis=2)
        p_re, p_im = chosen[0], chosen[1]
        lhs = jnp.stack(
            [jnp.concatenate([p_re, -p_im], -1), jnp.concatenate([p_im, p_re], -1)], 0
        ).reshape(2 * prows * nspin, 2 * nev)

        own = []
        products = []
        for d, field in enumerate(disp):
            order = orders[d % len(orders)]
            gram = lax.dot_general(
                left, field.reshape(2 * depth, nev), (((0,), (0,)), ((), ())),
                preferred_element_type=jnp.float32,
            )
            buf = gram.reshape([2] + [2] * nbits + [rows, nev])
            part = reduce_scatter(buf, order, nbits, count, 1).reshape(2, rows, nev)
            part = part * norm_factor
            own.append(part)
            blk = part.astype(jnp.bfloat16).reshape([2] + [1] * nbits + [rows, nev])
            rhs = all_gather(blk, list(reversed(order)), nbits, count, 1).reshape(2 * nev, nev)
            product = jnp.dot(lhs, rhs, preferred_element_type=jnp.float32)
            products.append(product.astype(jnp.bfloat16).reshape(2, prows, nspin * nev))
        own = jnp.take(jnp.stack(own, 0), directions, axis=0)
        ndisp = own.shape[0]
        gy_bits = [b for b in range(nbits) if (1 << b) < ny]
        grown = all_gather(
            own.reshape([ndisp, 2] + [1] * nbits + [rows, nev]), gy_bits, nbits, count, 2
        )
        elem = grown.reshape(ndisp, 2, ny * rows, nev)
        contracted = jnp.take(jnp.stack(products, 0), directions, axis=0)
        return (elem, contracted)

    return local


def solution(mesh):
    nbits, orders = bit_orders(mesh)
    in_specs = (
        P(None, None, None, "gx", "gy", None),
        P(None, None, None, None, None, "gx", "gy"),
        P(),
        P(),
        P(None, ("gx", "gy"), None),
    )
    out_specs = (P(None, None, "gx", None), P(None, None, ("gx", "gy"), None))
    return jax.shard_map(
        make_local(nbits, orders), mesh=mesh, in_specs=in_specs, out_specs=out_specs, check_vma=False
    )
```

profile of v0, /device:TPU:0, one launch (start us, length us, event | category | flops | bytes accessed | tf_op | source)
XLA Modules:
  0.0 163.9 jit_solution(11854911339744077089)
XLA Ops:
  0.6 1.0 slice_bitcast_fusion.21
  2.4 1.9 %convert_element_type.66 = f32[2,3,4,4,16,512]{5,4,3,2,1,0:T(8,128)S(1)} convert(bf16[2,3,4,4,16,512]{5,4,3,2,1,0:T(8,128)(2,1)} %param.5) | non-fusion elementwise | flops 786432 | bytes 4718592 | tf_op jit(solution)/shard_map/convert_element_type | solution.py:13
  6.8 1.1 pad_maximum_fusion.21
  7.9 3.0 %collective-permute-start.18 = (bf16[2,3,4,4,1,512]{5,4,3,2,1,0:T(2,128)(2,1)}, bf16[2,3,4,4,1,512]{5,4,3,2,1,0:T(2,128)(2,1)}, u32[]{:S(2)}, u32[]{:S(2)}) collective-permute-start(bf16[2,3,4,4,1,512]{5,4,3,2,1,0:T(2,128)(2,1)} %pad_maximum_fusion.21), channel_id=1, source_target_pairs={{0,1},{1,0},{2,3},{3,2},{4,5},{5,4},{6,7},{7,6},{8,9},{9,8},{10,11... | collective-permute-start | bytes 294920 | tf_op jit(solution)/shard_map/ppermute | solution.py:97
  15.9 4.0 %collective-permute-start = (bf16[2,3,4,1,16,512]{5,4,3,2,1,0:T(8,128)(2,1)}, bf16[2,3,4,1,16,512]{5,4,3,2,1,0:T(8,128)(2,1)}, u32[]{:S(2)}, u32[]{:S(2)}) collective-permute-start(bf16[2,3,4,1,16,512]{5,4,3,2,1,0:T(8,128)(2,1)} %slice.143), channel_id=1, source_target_pairs={{0,30},{2,0},{4,2},{6,4},{8,6},{10,8},{12,10},{14,12},{16,14},{18,... | collective-permute-start | bytes 1179656 | tf_op jit(solution)/shard_map/ppermute | solution.py:94
  19.9 1.2 slice_negate_fusion
  21.1 1.8 %slice.169 = bf16[2,3,4,4,15,512]{5,4,3,2,1,0:T(8,128)(2,1)} slice(bf16[2,3,4,4,16,512]{5,4,3,2,1,0:T(8,128)(2,1)S(1)} %copy-done), slice={[0:2], [0:3], [0:4], [0:4], [1:16], [0:512]} | slice | bytes 2949120 | tf_op jit(solution)/shard_map/slice | solution.py:99
  23.0 1.2 slice.142
  25.2 1.9 %copy.93 = bf16[2,8,4,8,512]{4,3,1,2,0:T(8,128)(2,1)} copy(bf16[2,8,4,8,512]{4,3,2,1,0:T(8,128)(2,1)} %bitcast.561) | data formatting | bytes 1048576 | tf_op jit(solution)/shard_map/reshape | solution.py:114
  27.1 2.4 %gather_fusion.1 = bf16[4,2,64,512]{3,2,1,0:T(8,128)(2,1)} fusion(bf16[2,64,4,512]{3,1,2,0:T(8,128)(2,1)} %bitcast.552, s32[1024]{0:T(1024)S(1)} %pad_clamp_fusion), kind=kCustom, calls=%fused_computation.1 | custom fusion | bytes 1048592 | tf_op jit(solution)/shard_map/jit(_take)/gather | solution.py:114
  29.5 1.2 select_bitcast_fusion
  31.5 2.4 %copy.58 = bf16[768,512]{0,1:T(8,128)(2,1)} copy(bf16[768,512]{1,0:T(8,128)(2,1)} %bitcast.551) | data formatting | bytes 1572864 | tf_op jit(solution)/shard_map/squeeze | solution.py:108
  33.9 2.3 %copy.57 = bf16[768,512]{0,1:T(8,128)(2,1)} copy(bf16[768,512]{1,0:T(8,128)(2,1)} %bitcast.550) | data formatting | bytes 1572864 | tf_op jit(solution)/shard_map/neg | solution.py:108
  36.2 1.6 copy.59
  37.7 1.2 maximum_bitcast_fusion.8
  39.1 1.8 %copy.71 = bf16[2,64,4,1024]{3,2,1,0:T(4,128)(2,1)} copy(bf16[2,64,4,1024]{3,1,2,0:T(8,128)(2,1)S(1)} %pad_maximum_fusion.5) | data formatting | bytes 2097152 | tf_op jit(solution)/shard_map/stack | solution.py:116
  40.9 2.2 %reshape.2103 = bf16[512,1024]{1,0:T(8,128)(2,1)} reshape(bf16[2,64,4,1024]{3,2,1,0:T(4,128)(2,1)} %copy.71) | data formatting | bytes 2097152 | tf_op jit(solution)/shard_map/reshape | solution.py:118
  43.1 1.7 %maximum_maximum_fusion = bf16[1536,1024]{0,1:T(8,128)(2,1)S(1)} fusion(bf16[768,512]{0,1:T(8,128)(2,1)} %copy.58, bf16[768,512]{0,1:T(8,128)(2,1)} %copy.57, bf16[1536,512]{0,1:T(8,128)(2,1)S(1)} %copy-done.6), kind=kLoop, calls=%fused_computation.3 | loop fusion | flops 9437184 | bytes 6291456 | tf_op jit(solution)/shard_map/concatenate | solution.py:109
  44.9 1.8 %fusion.4 = bf16[2,3,4,4,16,512]{5,4,3,2,1,0:T(8,128)(2,1)S(1)} fusion(bf16[1,3,4,4,16,512]{5,4,3,2,1,0:T(8,128)(2,1)S(1)} %copy-done.2, bf16[1,3,4,4,16,512]{5,4,3,2,1,0:T(8,128)(2,1)S(1)} %copy-done.4, bf16[2,3,4,4,1,512]{5,4,3,2,1,0:T(2,128)(2,1)} %collective-permute-done.18), kind=kLoop, calls=%fused_computation.11 | loop fusion | flops 4718592 | bytes 3244032 | tf_op jit(solution)/shard_map/concatenate | solution.py:104
  46.7 1.8 %fusion = f32[2,2,2,2,2,2,16,512]{7,6,0,5,4,3,2,1:T(8,128)S(1)} fusion(bf16[1536,512,1,1,1,1,1,1]{1,0,2,7,6,5,4,3:T(8,128)(2,1)S(1)} %bitcast.554, bf16[2,2,2,2,2,2,16,1536]{7,6,5,4,3,2,1,0:T(8,128)(2,1)S(1)} %bitcast.546), kind=kOutput, calls=%fused_computation.4 | convolution fusion | flops 1610612736 | bytes 6815744 | tf_op jit(solution)/shard_map/dot_general | solution.py:124
  48.7 1.2 copy.62
  52.8 1.8 %fusion.2 = f32[2,2,2,2,2,2,16,512]{7,6,0,5,4,3,2,1:T(8,128)S(1)} fusion(bf16[1536,512,1,1,1,1,1,1]{1,0,2,7,6,5,4,3:T(8,128)(2,1)S(1)} %bitcast.556, bf16[2,2,2,2,2,2,16,1536]{7,6,5,4,3,2,1,0:T(8,128)(2,1)S(1)} %bitcast.547), kind=kOutput, calls=%fused_computation.6 | convolution fusion | flops 1610612736 | bytes 6815744 | tf_op jit(solution)/shard_map/dot_general | solution.py:124
  55.1 1.2 fusion.5
  56.3 1.8 %fusion.33 = f32[2,2,2,2,2,2,16,512]{7,6,5,4,3,2,1,0:T(8,128)S(1)} fusion(bf16[2,2,2,2,2,2,16,1536]{7,6,5,4,3,2,1,0:T(8,128)(2,1)S(1)} %bitcast.548, bf16[1536,512,1,1,1,1,1,1]{1,0,7,6,5,4,3,2:T(8,128)(2,1)S(1)} %bitcast.553), kind=kOutput, calls=%fused_computation.259 | convolution fusion | flops 1610612736 | bytes 6815744 | tf_op jit(solution)/shard_map/dot_general | solution.py:124
  59.3 1.2 maximum_convert_fusion
  62.8 1.8 %fusion.32 = f32[2,2,2,2,2,2,16,512]{7,6,5,4,3,2,1,0:T(8,128)S(1)} fusion(bf16[2,2,2,2,2,2,16,1536]{7,6,5,4,3,2,1,0:T(8,128)(2,1)S(1)} %bitcast.549, bf16[1536,512,1,1,1,1,1,1]{1,0,7,6,5,4,3,2:T(8,128)(2,1)S(1)} %bitcast.555), kind=kOutput, calls=%fused_computation.258 | convolution fusion | flops 1610612736 | bytes 6815744 | tf_op jit(solution)/shard_map/dot_general | solution.py:124
  65.2 1.7 %collective-permute-start.20 = (f32[2,2,2,2,1,1,16,512]{7,6,0,5,4,3,2,1:T(8,128)S(1)}, f32[2,2,2,2,1,1,16,512]{7,6,0,5,4,3,2,1:T(8,128)S(1)}, u32[]{:S(2)}, u32[]{:S(2)}) collective-permute-start(f32[2,2,2,2,1,1,16,512]{7,6,0,5,4,3,2,1:T(8,128)S(1)} %constant_dynamic-slice_fusion.3), channel_id=1, source_target_pairs={{0,1},{1,0},{2,3},{3,2},{4,5},{5,4},{6,7},{7,6},{8,9},{9,8},{10,11... | collective-permute-start | bytes 1572872 | tf_op jit(solution)/shard_map/ppermute | solution.py:67
  68.2 1.1 collective-permute-start.2
  69.3 10.7 %collective-permute-done.20 = f32[2,2,2,2,1,1,16,512]{7,6,0,5,4,3,2,1:T(8,128)S(1)} collective-permute-done((f32[2,2,2,2,1,1,16,512]{7,6,0,5,4,3,2,1:T(8,128)S(1)}, f32[2,2,2,2,1,1,16,512]{7,6,0,5,4,3,2,1:T(8,128)S(1)}, u32[]{:S(2)}, u32[]{:S(2)}) %collective-permute-start.20) | collective-permute-done | bytes 524320 | tf_op jit(solution)/shard_map/ppermute | solution.py:67
  81.2 6.0 %collective-permute-done.21 = f32[2,2,2,1,1,1,16,512]{7,6,0,5,4,3,2,1:T(8,128)S(1)} collective-permute-done((f32[2,2,2,1,1,1,16,512]{7,6,0,5,4,3,2,1:T(8,128)S(1)}, f32[2,2,2,1,1,1,16,512]{7,6,0,5,4,3,2,1:T(8,128)S(1)}, u32[]{:S(2)}, u32[]{:S(2)}) %collective-permute-start.21) | collective-permute-done | bytes 262176 | tf_op jit(solution)/shard_map/ppermute | solution.py:67
  87.4 1.9 %collective-permute-done.9 = f32[2,2,1,1,1,2,16,512]{7,6,0,5,4,3,2,1:T(8,128)S(1)} collective-permute-done((f32[2,2,1,1,1,2,16,512]{7,6,0,5,4,3,2,1:T(8,128)S(1)}, f32[2,2,1,1,1,2,16,512]{7,6,0,5,4,3,2,1:T(8,128)S(1)}, u32[]{:S(2)}, u32[]{:S(2)}) %collective-permute-start.9) | collective-permute-done | bytes 262176 | tf_op jit(solution)/shard_map/ppermute | solution.py:67
  89.6 2.3 %collective-permute-start.15 = (f32[2,2,1,2,1,1,16,512]{7,6,5,4,3,2,1,0:T(8,128)S(1)}, f32[2,2,1,2,1,1,16,512]{7,6,5,4,3,2,1,0:T(8,128)S(1)}, u32[]{:S(2)}, u32[]{:S(2)}) collective-permute-start(f32[2,2,1,2,1,1,16,512]{7,6,5,4,3,2,1,0:T(8,128)S(1)} %constant_dynamic-slice_fusion.7), channel_id=1, source_target_pairs={{0,1},{1,0},{2,3},{3,2},{4,5},{5,4},{6,7},{7,6},{8,9},{9,8},{10,11... | collective-permute-start | bytes 786440 | tf_op jit(solution)/shard_map/ppermute | solution.py:67
  93.5 2.3 %collective-permute-done.10 = f32[2,2,1,1,1,1,16,512]{7,6,0,5,4,3,2,1:T(8,128)S(1)} collective-permute-done((f32[2,2,1,1,1,1,16,512]{7,6,0,5,4,3,2,1:T(8,128)S(1)}, f32[2,2,1,1,1,1,16,512]{7,6,0,5,4,3,2,1:T(8,128)S(1)}, u32[]{:S(2)}, u32[]{:S(2)}) %collective-permute-start.10) | collective-permute-done | bytes 131104 | tf_op jit(solution)/shard_map/ppermute | solution.py:67
  96.6 2.5 %collective-permute-done.23 = f32[2,1,1,1,1,1,16,512]{7,6,0,5,4,3,2,1:T(8,128)S(1)} collective-permute-done((f32[2,1,1,1,1,1,16,512]{7,6,0,5,4,3,2,1:T(8,128)S(1)}, f32[2,1,1,1,1,1,16,512]{7,6,0,5,4,3,2,1:T(8,128)S(1)}, u32[]{:S(2)}, u32[]{:S(2)}) %collective-permute-start.23) | collective-permute-done | bytes 65568 | tf_op jit(solution)/shard_map/ppermute | solution.py:67
  99.2 2.7 %collective-permute-done.11 = f32[2,1,1,1,1,1,16,512]{7,6,0,5,4,3,2,1:T(8,128)S(1)} collective-permute-done((f32[2,1,1,1,1,1,16,512]{7,6,0,5,4,3,2,1:T(8,128)S(1)}, f32[2,1,1,1,1,1,16,512]{7,6,0,5,4,3,2,1:T(8,128)S(1)}, u32[]{:S(2)}, u32[]{:S(2)}) %collective-permute-start.11) | collective-permute-done | bytes 65568 | tf_op jit(solution)/shard_map/ppermute | solution.py:67
  102.2 1.8 %collective-permute-done.40 = bf16[2,1,1,1,1,1,16,512]{7,6,5,4,3,2,1,0:T(8,128)(2,1)S(1)} collective-permute-done((bf16[2,1,1,1,1,1,16,512]{7,6,5,4,3,2,1,0:T(8,128)(2,1)S(1)}, bf16[2,1,1,1,1,1,16,512]{7,6,5,4,3,2,1,0:T(8,128)(2,1)S(1)}, u32[]{:S(2)}, u32[]{:S(2)}) %collective-permute-start.40) | collective-permute-done | bytes 32800 | tf_op jit(solution)/shard_map/ppermute | solution.py:76
  104.8 2.0 %collective-permute-done.30 = bf16[2,1,1,1,1,1,16,512]{7,6,0,5,4,3,2,1:T(8,128)(2,1)S(1)} collective-permute-done((bf16[2,1,1,1,1,1,16,512]{7,6,0,5,4,3,2,1:T(8,128)(2,1)S(1)}, bf16[2,1,1,1,1,1,16,512]{7,6,0,5,4,3,2,1:T(8,128)(2,1)S(1)}, u32[]{:S(2)}, u32[]{:S(2)}) %collective-permute-start.30) | collective-permute-done | bytes 32800 | tf_op jit(solution)/shard_map/ppermute | solution.py:76
  106.9 0.9 collective-permute-start.31
  109.1 1.4 collective-permute-start.42
  111.2 1.1 collective-permute-start.32
  112.9 1.5 collective-permute-start.17
  115.0 1.0 collective-permute-start.5
  116.1 1.2 collective-permute-start.43
  118.8 1.5 collective-permute-start.35
  121.7 1.2 collective-permute-start.24
  122.9 1.0 collective-permute-start.25
  124.8 3.0 %collective-permute-done.25 = bf16[2,1,1,1,1,1,16,512]{7,6,5,4,3,2,1,0:T(8,128)(2,1)S(1)} collective-permute-done((bf16[2,1,1,1,1,1,16,512]{7,6,5,4,3,2,1,0:T(8,128)(2,1)S(1)}, bf16[2,1,1,1,1,1,16,512]{7,6,5,4,3,2,1,0:T(8,128)(2,1)S(1)}, u32[]{:S(2)}, u32[]{:S(2)}) %collective-permute-start.25) | collective-permute-done | bytes 32800 | tf_op jit(solution)/shard_map/ppermute | solution.py:76
  127.8 1.0 collective-permute-start.26
  129.0 1.3 collective-permute-start.37
  130.3 1.8 %collective-permute-done.26 = bf16[2,2,1,1,1,1,16,512]{7,6,5,4,3,2,1,0:T(8,128)(2,1)S(1)} collective-permute-done((bf16[2,2,1,1,1,1,16,512]{7,6,5,4,3,2,1,0:T(8,128)(2,1)S(1)}, bf16[2,2,1,1,1,1,16,512]{7,6,5,4,3,2,1,0:T(8,128)(2,1)S(1)}, u32[]{:S(2)}, u32[]{:S(2)}) %collective-permute-start.26) | collective-permute-done | bytes 65568 | tf_op jit(solution)/shard_map/ppermute | solution.py:76
  132.2 1.5 collective-permute-start.27
  135.1 2.1 %collective-permute-done.27 = bf16[2,2,2,1,1,1,16,512]{7,6,5,4,3,2,1,0:T(8,128)(2,1)S(1)} collective-permute-done((bf16[2,2,2,1,1,1,16,512]{7,6,5,4,3,2,1,0:T(8,128)(2,1)S(1)}, bf16[2,2,2,1,1,1,16,512]{7,6,5,4,3,2,1,0:T(8,128)(2,1)S(1)}, u32[]{:S(2)}, u32[]{:S(2)}) %collective-permute-start.27) | collective-permute-done | bytes 131104 | tf_op jit(solution)/shard_map/ppermute | solution.py:76
  137.3 0.9 collective-permute-start.28
  139.2 3.7 %collective-permute-done.38 = bf16[2,2,1,2,1,2,16,512]{7,6,5,4,3,2,1,0:T(8,128)(2,1)S(1)} collective-permute-done((bf16[2,2,1,2,1,2,16,512]{7,6,5,4,3,2,1,0:T(8,128)(2,1)S(1)}, bf16[2,2,1,2,1,2,16,512]{7,6,5,4,3,2,1,0:T(8,128)(2,1)S(1)}, u32[]{:S(2)}, u32[]{:S(2)}) %collective-permute-start.38) | collective-permute-done | bytes 262176 | tf_op jit(solution)/shard_map/ppermute | solution.py:76
  147.2 1.0 copy-done.9
  148.2 1.5 convolution_convert_fusion.2
  149.7 1.4 stack_reshape.13
  151.1 1.2 broadcast_select_fusion.4
  153.2 1.1 stack_reshape.14
  154.3 1.1 broadcast_select_fusion.8
  156.2 1.1 stack_reshape.12
  157.3 1.5 pad_maximum_fusion
  158.8 2.0 %gather_fusion.2 = bf16[4,2,64,2048]{3,2,1,0:T(8,128)(2,1)} fusion(bf16[4,2,64,2048]{3,2,1,0:T(8,128)(2,1)S(1)} %pad_maximum_fusion, s32[1024]{0:T(1024)S(1)} %pad_clamp_fusion.1), kind=kCustom, calls=%fused_computation.2 | custom fusion | bytes 4194320 | tf_op jit(solution)/shard_map/jit(_take)/gather | solution.py:143
  160.8 3.2 %broadcast_select_fusion = bf16[4,2,64,2048]{3,2,1,0:T(8,128)(2,1)} fusion(bf16[4,2,64,2048]{3,2,1,0:T(8,128)(2,1)} %gather_fusion.2, pred[4]{0:T(512)(128)(4,1)S(1)} %copy-done.53), kind=kLoop, calls=%fused_computation.9 | loop fusion | flops 1048576 | bytes 4194308 | tf_op jit(solution)/shard_map/jit(_take)/select_n | solution.py:143
  (298 shorter events, 39.4 us)
Async XLA Ops:
  2.3 2.0 %copy-start.11 = (f32[4,4,16]{2,1,0:T(4,128)}, f32[4,4,16]{2,1,0:T(4,128)S(1)}, u32[]{:S(2)}) copy-start(f32[4,4,16]{2,1,0:T(4,128)S(1)} %get-tuple-element.94) | copy-start | bytes 3076
  2.3 2.0 %copy-start.23 = (f32[4,4,16]{2,1,0:T(4,128)}, f32[4,4,16]{2,1,0:T(4,128)S(1)}, u32[]{:S(2)}) copy-start(f32[4,4,16]{2,1,0:T(4,128)S(1)} %get-tuple-element.88) | copy-start | bytes 3076
  2.3 2.5 %copy-start.13 = (f32[4,4,16]{2,1,0:T(4,128)}, f32[4,4,16]{2,1,0:T(4,128)S(1)}, u32[]{:S(2)}) copy-start(f32[4,4,16]{2,1,0:T(4,128)S(1)} %get-tuple-element.96) | copy-start | bytes 3076
  2.3 2.5 %copy-start.25 = (f32[4,4,16]{2,1,0:T(4,128)}, f32[4,4,16]{2,1,0:T(4,128)S(1)}, u32[]{:S(2)}) copy-start(f32[4,4,16]{2,1,0:T(4,128)S(1)} %get-tuple-element.90) | copy-start | bytes 3076
  2.3 3.0 %copy-start.15 = (f32[4,4,16]{2,1,0:T(4,128)}, f32[4,4,16]{2,1,0:T(4,128)S(1)}, u32[]{:S(2)}) copy-start(f32[4,4,16]{2,1,0:T(4,128)S(1)} %get-tuple-element.98) | copy-start | bytes 3076
  2.3 3.0 %copy-start.27 = (f32[4,4,16]{2,1,0:T(4,128)}, f32[4,4,16]{2,1,0:T(4,128)S(1)}, u32[]{:S(2)}) copy-start(f32[4,4,16]{2,1,0:T(4,128)S(1)} %get-tuple-element.92) | copy-start | bytes 3076
  7.9 36.9 %collective-permute-start.18 = (bf16[2,3,4,4,1,512]{5,4,3,2,1,0:T(2,128)(2,1)}, bf16[2,3,4,4,1,512]{5,4,3,2,1,0:T(2,128)(2,1)}, u32[]{:S(2)}, u32[]{:S(2)}) collective-permute-start(bf16[2,3,4,4,1,512]{5,4,3,2,1,0:T(2,128)(2,1)} %pad_maximum_fusion.21), channel_id=1, source_target_pairs={{0,1},{1,0},{2,3},{3,2},{4,5},{5,4},{6,7},{7,6},{8,9},{9,8},{10,11... | collective-permute-start | bytes 294920 | tf_op jit(solution)/shard_map/ppermute | solution.py:97
  14.2 40.9 %collective-permute-start.12 = (bf16[2,3,4,1,16,512]{5,4,3,2,1,0:T(8,128)(2,1)}, bf16[2,3,4,1,16,512]{5,4,3,2,1,0:T(8,128)(2,1)}, u32[]{:S(2)}, u32[]{:S(2)}) collective-permute-start(bf16[2,3,4,1,16,512]{5,4,3,2,1,0:T(8,128)(2,1)} %pad_maximum_fusion.15), channel_id=1, source_target_pairs={{0,2},{2,4},{4,6},{6,8},{8,10},{10,12},{12,14},{14,16},{16,18},{18... | collective-permute-start | bytes 1179656 | tf_op jit(solution)/shard_map/ppermute | solution.py:95
  15.1 33.6 %collective-permute-start.6 = (bf16[2,3,4,4,1,512]{5,3,4,2,1,0:T(4,128)(2,1)S(1)}, bf16[2,3,4,4,1,512]{5,3,4,2,1,0:T(4,128)(2,1)}, u32[]{:S(2)}, u32[]{:S(2)}) collective-permute-start(bf16[2,3,4,4,1,512]{5,3,4,2,1,0:T(4,128)(2,1)S(1)} %copy.85), channel_id=1, source_target_pairs={{0,1},{1,0},{2,3},{3,2},{4,5},{5,4},{6,7},{7,6},{8,9},{9,8},{10,11... | collective-permute-start | bytes 294920 | tf_op jit(solution)/shard_map/ppermute | solution.py:96
  15.9 42.6 %collective-permute-start = (bf16[2,3,4,1,16,512]{5,4,3,2,1,0:T(8,128)(2,1)}, bf16[2,3,4,1,16,512]{5,4,3,2,1,0:T(8,128)(2,1)}, u32[]{:S(2)}, u32[]{:S(2)}) collective-permute-start(bf16[2,3,4,1,16,512]{5,4,3,2,1,0:T(8,128)(2,1)} %slice.143), channel_id=1, source_target_pairs={{0,30},{2,0},{4,2},{6,4},{8,6},{10,8},{12,10},{14,12},{16,14},{18,... | collective-permute-start | bytes 1179656 | tf_op jit(solution)/shard_map/ppermute | solution.py:94
  21.1 3.0 %copy-start.55 = (s32[4]{0:T(128)S(1)}, s32[4]{0:T(128)}, u32[]{:S(2)}) copy-start(s32[4]{0:T(128)} %param.7) | copy-start | bytes 52
  21.1 3.5 %copy-start.56 = (s32[4]{0:T(128)S(1)}, s32[4]{0:T(128)}, u32[]{:S(2)}) copy-start(s32[4]{0:T(128)} %param.8) | copy-start | bytes 52
  39.1 4.0 %copy-start.6 = (bf16[1536,512]{0,1:T(8,128)(2,1)S(1)}, bf16[1536,512]{0,1:T(8,128)(2,1)}, u32[]{:S(2)}) copy-start(bf16[1536,512]{0,1:T(8,128)(2,1)} %copy.59) | copy-start | bytes 4718596
  43.1 1.7 %copy-start.54 = (s32[4]{0:T(128)S(1)}, s32[4]{0:T(128)}, u32[]{:S(2)}) copy-start(s32[4]{0:T(128)} %compare_select_fusion.1) | copy-start | bytes 52
  43.1 1.8 %copy-start.2 = (bf16[1,3,4,4,16,512]{5,4,3,2,1,0:T(8,128)(2,1)S(1)}, bf16[1,3,4,4,16,512]{5,4,3,2,1,0:T(8,128)(2,1)}, u32[]{:S(2)}) copy-start(bf16[1,3,4,4,16,512]{5,4,3,2,1,0:T(8,128)(2,1)} %copy-done.1) | copy-start | bytes 2359300
  43.1 1.8 %copy-start.4 = (bf16[1,3,4,4,16,512]{5,4,3,2,1,0:T(8,128)(2,1)S(1)}, bf16[1,3,4,4,16,512]{5,4,3,2,1,0:T(8,128)(2,1)}, u32[]{:S(2)}) copy-start(bf16[1,3,4,4,16,512]{5,4,3,2,1,0:T(8,128)(2,1)} %copy-done.3) | copy-start | bytes 2359300
  48.6 16.3 %collective-permute-start.19 = (f32[2,2,2,2,1,2,16,512]{7,6,0,5,4,3,2,1:T(8,128)S(1)}, f32[2,2,2,2,1,2,16,512]{7,6,0,5,4,3,2,1:T(8,128)S(1)}, u32[]{:S(2)}, u32[]{:S(2)}) collective-permute-start(f32[2,2,2,2,1,2,16,512]{7,6,0,5,4,3,2,1:T(8,128)S(1)} %constant_dynamic-slice_fusion.4), channel_id=1, source_target_pairs={{0,2},{1,3},{2,0},{3,1},{4,6},{5,7},{6,4},{7,5},{8,10},{9,11},{10,... | collective-permute-start | bytes 3145736 | tf_op jit(solution)/shard_map/ppermute | solution.py:67
  54.7 12.1 %collective-permute-start.7 = (f32[2,2,2,2,1,2,16,512]{7,6,0,5,4,3,2,1:T(8,128)S(1)}, f32[2,2,2,2,1,2,16,512]{7,6,0,5,4,3,2,1:T(8,128)S(1)}, u32[]{:S(2)}, u32[]{:S(2)}) collective-permute-start(f32[2,2,2,2,1,2,16,512]{7,6,0,5,4,3,2,1:T(8,128)S(1)} %constant_dynamic-slice_fusion.14), channel_id=1, source_target_pairs={{0,2},{1,3},{2,0},{3,1},{4,6},{5,7},{6,4},{7,5},{8,10},{9,11},{10,... | collective-permute-start | bytes 3145736 | tf_op jit(solution)/shard_map/ppermute | solution.py:67
  58.2 2.4 %copy-start.30 = (f32[4,4,16]{2,1,0:T(4,128)S(1)}, f32[4,4,16]{2,1,0:T(4,128)}, u32[]{:S(2)}) copy-start(f32[4,4,16]{2,1,0:T(4,128)} %copy-done.29) | copy-start | bytes 3076
  58.2 2.4 %copy-start.32 = (f32[4,4,16]{2,1,0:T(4,128)S(1)}, f32[4,4,16]{2,1,0:T(4,128)}, u32[]{:S(2)}) copy-start(f32[4,4,16]{2,1,0:T(4,128)} %copy-done.31) | copy-start | bytes 3076
  58.2 2.4 %copy-start.34 = (f32[4,4,16]{2,1,0:T(4,128)S(1)}, f32[4,4,16]{2,1,0:T(4,128)}, u32[]{:S(2)}) copy-start(f32[4,4,16]{2,1,0:T(4,128)} %copy-done.33) | copy-start | bytes 3076
  58.2 2.4 %copy-start.50 = (f32[4,4,16]{2,1,0:T(4,128)S(1)}, f32[4,4,16]{2,1,0:T(4,128)}, u32[]{:S(2)}) copy-start(f32[4,4,16]{2,1,0:T(4,128)} %get-tuple-element.69) | copy-start | bytes 3076
  58.2 2.4 %copy-start.51 = (f32[4,4,16]{2,1,0:T(4,128)S(1)}, f32[4,4,16]{2,1,0:T(4,128)}, u32[]{:S(2)}) copy-start(f32[4,4,16]{2,1,0:T(4,128)} %get-tuple-element.71) | copy-start | bytes 3076
  58.2 2.4 %copy-start.52 = (f32[4,4,16]{2,1,0:T(4,128)S(1)}, f32[4,4,16]{2,1,0:T(4,128)}, u32[]{:S(2)}) copy-start(f32[4,4,16]{2,1,0:T(4,128)} %get-tuple-element.73) | copy-start | bytes 3076
  58.2 8.9 %collective-permute-start.13 = (f32[2,2,2,2,1,2,16,512]{7,6,5,4,3,2,1,0:T(8,128)S(1)}, f32[2,2,2,2,1,2,16,512]{7,6,5,4,3,2,1,0:T(8,128)S(1)}, u32[]{:S(2)}, u32[]{:S(2)}) collective-permute-start(f32[2,2,2,2,1,2,16,512]{7,6,5,4,3,2,1,0:T(8,128)S(1)} %constant_dynamic-slice_fusion.9), channel_id=1, source_target_pairs={{0,2},{1,3},{2,0},{3,1},{4,6},{5,7},{6,4},{7,5},{8,10},{9,11},{10,... | collective-permute-start | bytes 3145736 | tf_op jit(solution)/shard_map/ppermute | solution.py:67
  64.7 3.2 %collective-permute-start.1 = (f32[2,2,2,2,1,2,16,512]{7,6,5,4,3,2,1,0:T(8,128)S(1)}, f32[2,2,2,2,1,2,16,512]{7,6,5,4,3,2,1,0:T(8,128)S(1)}, u32[]{:S(2)}, u32[]{:S(2)}) collective-permute-start(f32[2,2,2,2,1,2,16,512]{7,6,5,4,3,2,1,0:T(8,128)S(1)} %constant_dynamic-slice_fusion.19), channel_id=1, source_target_pairs={{0,2},{1,3},{2,0},{3,1},{4,6},{5,7},{6,4},{7,5},{8,10},{9,11},{10,... | collective-permute-start | bytes 3145736 | tf_op jit(solution)/shard_map/ppermute | solution.py:67
  65.2 14.9 %collective-permute-start.20 = (f32[2,2,2,2,1,1,16,512]{7,6,0,5,4,3,2,1:T(8,128)S(1)}, f32[2,2,2,2,1,1,16,512]{7,6,0,5,4,3,2,1:T(8,128)S(1)}, u32[]{:S(2)}, u32[]{:S(2)}) collective-permute-start(f32[2,2,2,2,1,1,16,512]{7,6,0,5,4,3,2,1:T(8,128)S(1)} %constant_dynamic-slice_fusion.3), channel_id=1, source_target_pairs={{0,1},{1,0},{2,3},{3,2},{4,5},{5,4},{6,7},{7,6},{8,9},{9,8},{10,11... | collective-permute-start | bytes 1572872 | tf_op jit(solution)/shard_map/ppermute | solution.py:67
  67.1 13.9 %collective-permute-start.8 = (f32[2,2,2,1,1,2,16,512]{7,6,0,5,4,3,2,1:T(8,128)S(1)}, f32[2,2,2,1,1,2,16,512]{7,6,0,5,4,3,2,1:T(8,128)S(1)}, u32[]{:S(2)}, u32[]{:S(2)}) collective-permute-start(f32[2,2,2,1,1,2,16,512]{7,6,0,5,4,3,2,1:T(8,128)S(1)} %constant_dynamic-slice_fusion.13), channel_id=1, source_target_pairs={{0,4},{1,5},{2,6},{3,7},{4,0},{5,1},{6,2},{7,3},{8,12},{9,13},{10,... | collective-permute-start | bytes 1572872 | tf_op jit(solution)/shard_map/ppermute | solution.py:67
  67.5 22.0 %collective-permute-start.14 = (f32[2,2,1,2,1,2,16,512]{7,6,5,4,3,2,1,0:T(8,128)S(1)}, f32[2,2,1,2,1,2,16,512]{7,6,5,4,3,2,1,0:T(8,128)S(1)}, u32[]{:S(2)}, u32[]{:S(2)}) collective-permute-start(f32[2,2,1,2,1,2,16,512]{7,6,5,4,3,2,1,0:T(8,128)S(1)} %constant_dynamic-slice_fusion.8), channel_id=1, source_target_pairs={{0,8},{1,9},{2,10},{3,11},{4,12},{5,13},{6,14},{7,15},{8,0},{9,1},... | collective-permute-start | bytes 1572872 | tf_op jit(solution)/shard_map/ppermute | solution.py:67
  68.2 23.7 %collective-permute-start.2 = (f32[2,2,2,2,1,1,16,512]{7,6,5,4,3,2,1,0:T(8,128)S(1)}, f32[2,2,2,2,1,1,16,512]{7,6,5,4,3,2,1,0:T(8,128)S(1)}, u32[]{:S(2)}, u32[]{:S(2)}) collective-permute-start(f32[2,2,2,2,1,1,16,512]{7,6,5,4,3,2,1,0:T(8,128)S(1)} %constant_dynamic-slice_fusion.18), channel_id=1, source_target_pairs={{0,1},{1,0},{2,3},{3,2},{4,5},{5,4},{6,7},{7,6},{8,9},{9,8},{10,11... | collective-permute-start | bytes 1572872 | tf_op jit(solution)/shard_map/ppermute | solution.py:67
  80.2 7.1 %collective-permute-start.21 = (f32[2,2,2,1,1,1,16,512]{7,6,0,5,4,3,2,1:T(8,128)S(1)}, f32[2,2,2,1,1,1,16,512]{7,6,0,5,4,3,2,1:T(8,128)S(1)}, u32[]{:S(2)}, u32[]{:S(2)}) collective-permute-start(f32[2,2,2,1,1,1,16,512]{7,6,0,5,4,3,2,1:T(8,128)S(1)} %constant_dynamic-slice_fusion.2), channel_id=1, source_target_pairs={{0,4},{1,5},{2,6},{3,7},{4,0},{5,1},{6,2},{7,3},{8,12},{9,13},{10,... | collective-permute-start | bytes 786440 | tf_op jit(solution)/shard_map/ppermute | solution.py:67
  81.2 8.1 %collective-permute-start.9 = (f32[2,2,1,1,1,2,16,512]{7,6,0,5,4,3,2,1:T(8,128)S(1)}, f32[2,2,1,1,1,2,16,512]{7,6,0,5,4,3,2,1:T(8,128)S(1)}, u32[]{:S(2)}, u32[]{:S(2)}) collective-permute-start(f32[2,2,1,1,1,2,16,512]{7,6,0,5,4,3,2,1:T(8,128)S(1)} %constant_dynamic-slice_fusion.12), channel_id=1, source_target_pairs={{0,8},{1,9},{2,10},{3,11},{4,12},{5,13},{6,14},{7,15},{8,0},{9,1},... | collective-permute-start | bytes 786440 | tf_op jit(solution)/shard_map/ppermute | solution.py:67
  87.3 5.3 %collective-permute-start.22 = (f32[2,2,1,1,1,1,16,512]{7,6,0,5,4,3,2,1:T(8,128)S(1)}, f32[2,2,1,1,1,1,16,512]{7,6,0,5,4,3,2,1:T(8,128)S(1)}, u32[]{:S(2)}, u32[]{:S(2)}) collective-permute-start(f32[2,2,1,1,1,1,16,512]{7,6,0,5,4,3,2,1:T(8,128)S(1)} %constant_dynamic-slice_fusion.1), channel_id=1, source_target_pairs={{0,8},{1,9},{2,10},{3,11},{4,12},{5,13},{6,14},{7,15},{8,0},{9,1},... | collective-permute-start | bytes 393224 | tf_op jit(solution)/shard_map/ppermute | solution.py:67
  89.4 6.4 %collective-permute-start.10 = (f32[2,2,1,1,1,1,16,512]{7,6,0,5,4,3,2,1:T(8,128)S(1)}, f32[2,2,1,1,1,1,16,512]{7,6,0,5,4,3,2,1:T(8,128)S(1)}, u32[]{:S(2)}, u32[]{:S(2)}) collective-permute-start(f32[2,2,1,1,1,1,16,512]{7,6,0,5,4,3,2,1:T(8,128)S(1)} %constant_dynamic-slice_fusion.11), channel_id=1, source_target_pairs={{0,1},{1,0},{2,3},{3,2},{4,5},{5,4},{6,7},{7,6},{8,9},{9,8},{10,11... | collective-permute-start | bytes 393224 | tf_op jit(solution)/shard_map/ppermute | solution.py:67
  89.6 18.2 %collective-permute-start.15 = (f32[2,2,1,2,1,1,16,512]{7,6,5,4,3,2,1,0:T(8,128)S(1)}, f32[2,2,1,2,1,1,16,512]{7,6,5,4,3,2,1,0:T(8,128)S(1)}, u32[]{:S(2)}, u32[]{:S(2)}) collective-permute-start(f32[2,2,1,2,1,1,16,512]{7,6,5,4,3,2,1,0:T(8,128)S(1)} %constant_dynamic-slice_fusion.7), channel_id=1, source_target_pairs={{0,1},{1,0},{2,3},{3,2},{4,5},{5,4},{6,7},{7,6},{8,9},{9,8},{10,11... | collective-permute-start | bytes 786440 | tf_op jit(solution)/shard_map/ppermute | solution.py:67
  92.0 16.7 %collective-permute-start.3 = (f32[2,2,2,1,1,1,16,512]{7,6,5,4,3,2,1,0:T(8,128)S(1)}, f32[2,2,2,1,1,1,16,512]{7,6,5,4,3,2,1,0:T(8,128)S(1)}, u32[]{:S(2)}, u32[]{:S(2)}) collective-permute-start(f32[2,2,2,1,1,1,16,512]{7,6,5,4,3,2,1,0:T(8,128)S(1)} %constant_dynamic-slice_fusion.17), channel_id=1, source_target_pairs={{0,4},{1,5},{2,6},{3,7},{4,0},{5,1},{6,2},{7,3},{8,12},{9,13},{10,... | collective-permute-start | bytes 786440 | tf_op jit(solution)/shard_map/ppermute | solution.py:67
  92.7 6.4 %collective-permute-start.23 = (f32[2,1,1,1,1,1,16,512]{7,6,0,5,4,3,2,1:T(8,128)S(1)}, f32[2,1,1,1,1,1,16,512]{7,6,0,5,4,3,2,1:T(8,128)S(1)}, u32[]{:S(2)}, u32[]{:S(2)}) collective-permute-start(f32[2,1,1,1,1,1,16,512]{7,6,0,5,4,3,2,1:T(8,128)S(1)} %constant_dynamic-slice_fusion), channel_id=1, source_target_pairs={{0,16},{1,17},{2,18},{3,19},{4,20},{5,21},{6,22},{7,23},{8,24},{9,... | collective-permute-start | bytes 196616 | tf_op jit(solution)/shard_map/ppermute | solution.py:67
  95.8 6.1 %collective-permute-start.11 = (f32[2,1,1,1,1,1,16,512]{7,6,0,5,4,3,2,1:T(8,128)S(1)}, f32[2,1,1,1,1,1,16,512]{7,6,0,5,4,3,2,1:T(8,128)S(1)}, u32[]{:S(2)}, u32[]{:S(2)}) collective-permute-start(f32[2,1,1,1,1,1,16,512]{7,6,0,5,4,3,2,1:T(8,128)S(1)} %constant_dynamic-slice_fusion.10), channel_id=1, source_target_pairs={{0,16},{1,17},{2,18},{3,19},{4,20},{5,21},{6,22},{7,23},{8,24},{9,... | collective-permute-start | bytes 196616 | tf_op jit(solution)/shard_map/ppermute | solution.py:67
  99.2 4.9 %collective-permute-start.40 = (bf16[2,1,1,1,1,1,16,512]{7,6,5,4,3,2,1,0:T(8,128)(2,1)S(1)}, bf16[2,1,1,1,1,1,16,512]{7,6,5,4,3,2,1,0:T(8,128)(2,1)S(1)}, u32[]{:S(2)}, u32[]{:S(2)}) collective-permute-start(bf16[2,1,1,1,1,1,16,512]{7,6,5,4,3,2,1,0:T(8,128)(2,1)S(1)} %get-tuple-element.66), channel_id=1, source_target_pairs={{0,16},{1,17},{2,18},{3,19},{4,20},{5,21},{6,22},{7,23},{8,24},{9,... | collective-permute-start | bytes 98312 | tf_op jit(solution)/shard_map/ppermute | solution.py:76
  102.0 4.9 %collective-permute-start.30 = (bf16[2,1,1,1,1,1,16,512]{7,6,0,5,4,3,2,1:T(8,128)(2,1)S(1)}, bf16[2,1,1,1,1,1,16,512]{7,6,0,5,4,3,2,1:T(8,128)(2,1)S(1)}, u32[]{:S(2)}, u32[]{:S(2)}) collective-permute-start(bf16[2,1,1,1,1,1,16,512]{7,6,0,5,4,3,2,1:T(8,128)(2,1)S(1)} %get-tuple-element.62), channel_id=1, source_target_pairs={{0,16},{1,17},{2,18},{3,19},{4,20},{5,21},{6,22},{7,23},{8,24},{9,... | collective-permute-start | bytes 98312 | tf_op jit(solution)/shard_map/ppermute | solution.py:76
  104.1 5.0 %collective-permute-start.41 = (bf16[2,2,1,1,1,1,16,512]{7,6,5,4,3,2,1,0:T(8,128)(2,1)S(1)}, bf16[2,2,1,1,1,1,16,512]{7,6,5,4,3,2,1,0:T(8,128)(2,1)S(1)}, u32[]{:S(2)}, u32[]{:S(2)}) collective-permute-start(bf16[2,2,1,1,1,1,16,512]{7,6,5,4,3,2,1,0:T(8,128)(2,1)S(1)} %pad_maximum_fusion.29), channel_id=1, source_target_pairs={{0,8},{1,9},{2,10},{3,11},{4,12},{5,13},{6,14},{7,15},{8,0},{9,1},... | collective-permute-start | bytes 196616 | tf_op jit(solution)/shard_map/ppermute | solution.py:76
  106.9 4.3 %collective-permute-start.31 = (bf16[2,2,1,1,1,1,16,512]{7,6,0,5,4,3,2,1:T(8,128)(2,1)S(1)}, bf16[2,2,1,1,1,1,16,512]{7,6,0,5,4,3,2,1:T(8,128)(2,1)S(1)}, u32[]{:S(2)}, u32[]{:S(2)}) collective-permute-start(bf16[2,2,1,1,1,1,16,512]{7,6,0,5,4,3,2,1:T(8,128)(2,1)S(1)} %pad_maximum_fusion.27), channel_id=1, source_target_pairs={{0,1},{1,0},{2,3},{3,2},{4,5},{5,4},{6,7},{7,6},{8,9},{9,8},{10,11... | collective-permute-start | bytes 196616 | tf_op jit(solution)/shard_map/ppermute | solution.py:76
  107.9 5.0 %collective-permute-start.16 = (f32[2,2,1,1,1,1,16,512]{7,6,5,4,3,2,1,0:T(8,128)S(1)}, f32[2,2,1,1,1,1,16,512]{7,6,5,4,3,2,1,0:T(8,128)S(1)}, u32[]{:S(2)}, u32[]{:S(2)}) collective-permute-start(f32[2,2,1,1,1,1,16,512]{7,6,5,4,3,2,1,0:T(8,128)S(1)} %constant_dynamic-slice_fusion.6), channel_id=1, source_target_pairs={{0,4},{1,5},{2,6},{3,7},{4,0},{5,1},{6,2},{7,3},{8,12},{9,13},{10,... | collective-permute-start | bytes 393224 | tf_op jit(solution)/shard_map/ppermute | solution.py:67
  108.8 6.2 %collective-permute-start.4 = (f32[2,2,1,1,1,1,16,512]{7,6,5,4,3,2,1,0:T(8,128)S(1)}, f32[2,2,1,1,1,1,16,512]{7,6,5,4,3,2,1,0:T(8,128)S(1)}, u32[]{:S(2)}, u32[]{:S(2)}) collective-permute-start(f32[2,2,1,1,1,1,16,512]{7,6,5,4,3,2,1,0:T(8,128)S(1)} %constant_dynamic-slice_fusion.16), channel_id=1, source_target_pairs={{0,8},{1,9},{2,10},{3,11},{4,12},{5,13},{6,14},{7,15},{8,0},{9,1},... | collective-permute-start | bytes 393224 | tf_op jit(solution)/shard_map/ppermute | solution.py:67
  109.1 6.9 %collective-permute-start.42 = (bf16[2,2,2,1,1,1,16,512]{7,6,5,4,3,2,1,0:T(8,128)(2,1)S(1)}, bf16[2,2,2,1,1,1,16,512]{7,6,5,4,3,2,1,0:T(8,128)(2,1)S(1)}, u32[]{:S(2)}, u32[]{:S(2)}) collective-permute-start(bf16[2,2,2,1,1,1,16,512]{7,6,5,4,3,2,1,0:T(8,128)(2,1)S(1)} %pad_maximum_fusion.25), channel_id=1, source_target_pairs={{0,4},{1,5},{2,6},{3,7},{4,0},{5,1},{6,2},{7,3},{8,12},{9,13},{10,... | collective-permute-start | bytes 393224 | tf_op jit(solution)/shard_map/ppermute | solution.py:76
  111.2 6.1 %collective-permute-start.32 = (bf16[2,2,1,1,1,2,16,512]{7,6,0,5,4,3,2,1:T(8,128)(2,1)S(1)}, bf16[2,2,1,1,1,2,16,512]{7,6,0,5,4,3,2,1:T(8,128)(2,1)S(1)}, u32[]{:S(2)}, u32[]{:S(2)}) collective-permute-start(bf16[2,2,1,1,1,2,16,512]{7,6,0,5,4,3,2,1:T(8,128)(2,1)S(1)} %pad_maximum_fusion.23), channel_id=1, source_target_pairs={{0,8},{1,9},{2,10},{3,11},{4,12},{5,13},{6,14},{7,15},{8,0},{9,1},... | collective-permute-start | bytes 393224 | tf_op jit(solution)/shard_map/ppermute | solution.py:76
  112.9 8.7 %copy-start.53 = (pred[4]{0:T(512)(128)(4,1)S(1)}, pred[4]{0:T(512)(128)(4,1)}, u32[]{:S(2)}) copy-start(pred[4]{0:T(512)(128)(4,1)} %get-tuple-element.148) | copy-start | bytes 16
  112.9 5.8 %collective-permute-start.17 = (f32[2,1,1,1,1,1,16,512]{7,6,5,4,3,2,1,0:T(8,128)S(1)}, f32[2,1,1,1,1,1,16,512]{7,6,5,4,3,2,1,0:T(8,128)S(1)}, u32[]{:S(2)}, u32[]{:S(2)}) collective-permute-start(f32[2,1,1,1,1,1,16,512]{7,6,5,4,3,2,1,0:T(8,128)S(1)} %constant_dynamic-slice_fusion.5), channel_id=1, source_target_pairs={{0,16},{1,17},{2,18},{3,19},{4,20},{5,21},{6,22},{7,23},{8,24},{9,... | collective-permute-start | bytes 196616 | tf_op jit(solution)/shard_map/ppermute | solution.py:67
  115.0 6.0 %collective-permute-start.5 = (f32[2,1,1,1,1,1,16,512]{7,6,5,4,3,2,1,0:T(8,128)S(1)}, f32[2,1,1,1,1,1,16,512]{7,6,5,4,3,2,1,0:T(8,128)S(1)}, u32[]{:S(2)}, u32[]{:S(2)}) collective-permute-start(f32[2,1,1,1,1,1,16,512]{7,6,5,4,3,2,1,0:T(8,128)S(1)} %constant_dynamic-slice_fusion.15), channel_id=1, source_target_pairs={{0,16},{1,17},{2,18},{3,19},{4,20},{5,21},{6,22},{7,23},{8,24},{9,... | collective-permute-start | bytes 196616 | tf_op jit(solution)/shard_map/ppermute | solution.py:67
  116.1 17.5 %collective-permute-start.43 = (bf16[2,2,2,2,1,1,16,512]{7,6,5,4,3,2,1,0:T(8,128)(2,1)S(1)}, bf16[2,2,2,2,1,1,16,512]{7,6,5,4,3,2,1,0:T(8,128)(2,1)S(1)}, u32[]{:S(2)}, u32[]{:S(2)}) collective-permute-start(bf16[2,2,2,2,1,1,16,512]{7,6,5,4,3,2,1,0:T(8,128)(2,1)S(1)} %pad_maximum_fusion.20), channel_id=1, source_target_pairs={{0,1},{1,0},{2,3},{3,2},{4,5},{5,4},{6,7},{7,6},{8,9},{9,8},{10,11... | collective-permute-start | bytes 786440 | tf_op jit(solution)/shard_map/ppermute | solution.py:76
  117.4 16.4 %collective-permute-start.33 = (bf16[2,2,2,1,1,2,16,512]{7,6,0,5,4,3,2,1:T(8,128)(2,1)S(1)}, bf16[2,2,2,1,1,2,16,512]{7,6,0,5,4,3,2,1:T(8,128)(2,1)S(1)}, u32[]{:S(2)}, u32[]{:S(2)}) collective-permute-start(bf16[2,2,2,1,1,2,16,512]{7,6,0,5,4,3,2,1:T(8,128)(2,1)S(1)} %pad_maximum_fusion.18), channel_id=1, source_target_pairs={{0,4},{1,5},{2,6},{3,7},{4,0},{5,1},{6,2},{7,3},{8,12},{9,13},{10,... | collective-permute-start | bytes 786440 | tf_op jit(solution)/shard_map/ppermute | solution.py:76
  118.8 5.2 %collective-permute-start.35 = (bf16[2,1,1,1,1,1,16,512]{7,6,5,4,3,2,1,0:T(8,128)(2,1)S(1)}, bf16[2,1,1,1,1,1,16,512]{7,6,5,4,3,2,1,0:T(8,128)(2,1)S(1)}, u32[]{:S(2)}, u32[]{:S(2)}) collective-permute-start(bf16[2,1,1,1,1,1,16,512]{7,6,5,4,3,2,1,0:T(8,128)(2,1)S(1)} %get-tuple-element.64), channel_id=1, source_target_pairs={{0,16},{1,17},{2,18},{3,19},{4,20},{5,21},{6,22},{7,23},{8,24},{9,... | collective-permute-start | bytes 98312 | tf_op jit(solution)/shard_map/ppermute | solution.py:76
  121.7 16.5 %collective-permute-start.24 = (f32[4,2,1,1,1,1,1,16,512]{8,7,1,0,6,5,4,3,2:T(8,128)S(1)}, f32[4,2,1,1,1,1,1,16,512]{8,7,1,0,6,5,4,3,2:T(8,128)S(1)}, u32[]{:S(2)}, u32[]{:S(2)}) collective-permute-start(f32[4,2,1,1,1,1,1,16,512]{8,7,1,0,6,5,4,3,2:T(8,128)S(1)} %bitcast_select_fusion), channel_id=1, source_target_pairs={{0,1},{1,0},{2,3},{3,2},{4,5},{5,4},{6,7},{7,6},{8,9},{9,8},{10,11... | collective-permute-start | bytes 786440 | tf_op jit(solution)/shard_map/ppermute | solution.py:76
  122.9 4.8 %collective-permute-start.25 = (bf16[2,1,1,1,1,1,16,512]{7,6,5,4,3,2,1,0:T(8,128)(2,1)S(1)}, bf16[2,1,1,1,1,1,16,512]{7,6,5,4,3,2,1,0:T(8,128)(2,1)S(1)}, u32[]{:S(2)}, u32[]{:S(2)}) collective-permute-start(bf16[2,1,1,1,1,1,16,512]{7,6,5,4,3,2,1,0:T(8,128)(2,1)S(1)} %get-tuple-element.60), channel_id=1, source_target_pairs={{0,16},{1,17},{2,18},{3,19},{4,20},{5,21},{6,22},{7,23},{8,24},{9,... | collective-permute-start | bytes 98312 | tf_op jit(solution)/shard_map/ppermute | solution.py:76
  124.0 5.0 %collective-permute-start.36 = (bf16[2,2,1,1,1,1,16,512]{7,6,5,4,3,2,1,0:T(8,128)(2,1)S(1)}, bf16[2,2,1,1,1,1,16,512]{7,6,5,4,3,2,1,0:T(8,128)(2,1)S(1)}, u32[]{:S(2)}, u32[]{:S(2)}) collective-permute-start(bf16[2,2,1,1,1,1,16,512]{7,6,5,4,3,2,1,0:T(8,128)(2,1)S(1)} %pad_maximum_fusion.28), channel_id=1, source_target_pairs={{0,4},{1,5},{2,6},{3,7},{4,0},{5,1},{6,2},{7,3},{8,12},{9,13},{10,... | collective-permute-start | bytes 196616 | tf_op jit(solution)/shard_map/ppermute | solution.py:76
  127.8 4.3 %collective-permute-start.26 = (bf16[2,2,1,1,1,1,16,512]{7,6,5,4,3,2,1,0:T(8,128)(2,1)S(1)}, bf16[2,2,1,1,1,1,16,512]{7,6,5,4,3,2,1,0:T(8,128)(2,1)S(1)}, u32[]{:S(2)}, u32[]{:S(2)}) collective-permute-start(bf16[2,2,1,1,1,1,16,512]{7,6,5,4,3,2,1,0:T(8,128)(2,1)S(1)} %pad_maximum_fusion.26), channel_id=1, source_target_pairs={{0,8},{1,9},{2,10},{3,11},{4,12},{5,13},{6,14},{7,15},{8,0},{9,1},... | collective-permute-start | bytes 196616 | tf_op jit(solution)/shard_map/ppermute | solution.py:76
  129.0 5.5 %collective-permute-start.37 = (bf16[2,2,1,2,1,1,16,512]{7,6,5,4,3,2,1,0:T(8,128)(2,1)S(1)}, bf16[2,2,1,2,1,1,16,512]{7,6,5,4,3,2,1,0:T(8,128)(2,1)S(1)}, u32[]{:S(2)}, u32[]{:S(2)}) collective-permute-start(bf16[2,2,1,2,1,1,16,512]{7,6,5,4,3,2,1,0:T(8,128)(2,1)S(1)} %pad_maximum_fusion.24), channel_id=1, source_target_pairs={{0,1},{1,0},{2,3},{3,2},{4,5},{5,4},{6,7},{7,6},{8,9},{9,8},{10,11... | collective-permute-start | bytes 393224 | tf_op jit(solution)/shard_map/ppermute | solution.py:76
  132.2 5.0 %collective-permute-start.27 = (bf16[2,2,2,1,1,1,16,512]{7,6,5,4,3,2,1,0:T(8,128)(2,1)S(1)}, bf16[2,2,2,1,1,1,16,512]{7,6,5,4,3,2,1,0:T(8,128)(2,1)S(1)}, u32[]{:S(2)}, u32[]{:S(2)}) collective-permute-start(bf16[2,2,2,1,1,1,16,512]{7,6,5,4,3,2,1,0:T(8,128)(2,1)S(1)} %pad_maximum_fusion.22), channel_id=1, source_target_pairs={{0,4},{1,5},{2,6},{3,7},{4,0},{5,1},{6,2},{7,3},{8,12},{9,13},{10,... | collective-permute-start | bytes 393224 | tf_op jit(solution)/shard_map/ppermute | solution.py:76
  133.7 11.4 %collective-permute-start.44 = (bf16[2,2,2,2,1,2,16,512]{7,6,5,4,3,2,1,0:T(8,128)(2,1)S(1)}, bf16[2,2,2,2,1,2,16,512]{7,6,5,4,3,2,1,0:T(8,128)(2,1)S(1)}, u32[]{:S(2)}, u32[]{:S(2)}) collective-permute-start(bf16[2,2,2,2,1,2,16,512]{7,6,5,4,3,2,1,0:T(8,128)(2,1)S(1)} %pad_maximum_fusion.14), channel_id=1, source_target_pairs={{0,2},{1,3},{2,0},{3,1},{4,6},{5,7},{6,4},{7,5},{8,10},{9,11},{10,... | collective-permute-start | bytes 1572872 | tf_op jit(solution)/shard_map/ppermute | solution.py:76
  133.9 12.6 %collective-permute-start.34 = (bf16[2,2,2,2,1,2,16,512]{7,6,0,5,4,3,2,1:T(8,128)(2,1)S(1)}, bf16[2,2,2,2,1,2,16,512]{7,6,0,5,4,3,2,1:T(8,128)(2,1)S(1)}, u32[]{:S(2)}, u32[]{:S(2)}) collective-permute-start(bf16[2,2,2,2,1,2,16,512]{7,6,0,5,4,3,2,1:T(8,128)(2,1)S(1)} %pad_maximum_fusion.12), channel_id=1, source_target_pairs={{0,2},{1,3},{2,0},{3,1},{4,6},{5,7},{6,4},{7,5},{8,10},{9,11},{10,... | collective-permute-start | bytes 1572872 | tf_op jit(solution)/shard_map/ppermute | solution.py:76
  134.5 8.3 %collective-permute-start.38 = (bf16[2,2,1,2,1,2,16,512]{7,6,5,4,3,2,1,0:T(8,128)(2,1)S(1)}, bf16[2,2,1,2,1,2,16,512]{7,6,5,4,3,2,1,0:T(8,128)(2,1)S(1)}, u32[]{:S(2)}, u32[]{:S(2)}) collective-permute-start(bf16[2,2,1,2,1,2,16,512]{7,6,5,4,3,2,1,0:T(8,128)(2,1)S(1)} %pad_maximum_fusion.19), channel_id=1, source_target_pairs={{0,8},{1,9},{2,10},{3,11},{4,12},{5,13},{6,14},{7,15},{8,0},{9,1},... | collective-permute-start | bytes 786440 | tf_op jit(solution)/shard_map/ppermute | solution.py:76
  137.3 6.5 %collective-permute-start.28 = (bf16[2,2,2,2,1,1,16,512]{7,6,5,4,3,2,1,0:T(8,128)(2,1)S(1)}, bf16[2,2,2,2,1,1,16,512]{7,6,5,4,3,2,1,0:T(8,128)(2,1)S(1)}, u32[]{:S(2)}, u32[]{:S(2)}) collective-permute-start(bf16[2,2,2,2,1,1,16,512]{7,6,5,4,3,2,1,0:T(8,128)(2,1)S(1)} %pad_maximum_fusion.17), channel_id=1, source_target_pairs={{0,1},{1,0},{2,3},{3,2},{4,5},{5,4},{6,7},{7,6},{8,9},{9,8},{10,11... | collective-permute-start | bytes 786440 | tf_op jit(solution)/shard_map/ppermute | solution.py:76
  143.7 7.3 %collective-permute-start.39 = (bf16[2,2,2,2,1,2,16,512]{7,6,5,4,3,2,1,0:T(8,128)(2,1)}, bf16[2,2,2,2,1,2,16,512]{7,6,5,4,3,2,1,0:T(8,128)(2,1)}, u32[]{:S(2)}, u32[]{:S(2)}) collective-permute-start(bf16[2,2,2,2,1,2,16,512]{7,6,5,4,3,2,1,0:T(8,128)(2,1)} %pad_maximum_fusion.13), channel_id=1, source_target_pairs={{0,2},{1,3},{2,0},{3,1},{4,6},{5,7},{6,4},{7,5},{8,10},{9,11},{10,... | collective-permute-start | bytes 1572872 | tf_op jit(solution)/shard_map/ppermute | solution.py:76
  144.6 9.6 %collective-permute-start.29 = (bf16[2,2,2,2,1,2,16,512]{7,6,5,4,3,2,1,0:T(8,128)(2,1)}, bf16[2,2,2,2,1,2,16,512]{7,6,5,4,3,2,1,0:T(8,128)(2,1)}, u32[]{:S(2)}, u32[]{:S(2)}) collective-permute-start(bf16[2,2,2,2,1,2,16,512]{7,6,5,4,3,2,1,0:T(8,128)(2,1)} %pad_maximum_fusion.11), channel_id=1, source_target_pairs={{0,2},{1,3},{2,0},{3,1},{4,6},{5,7},{6,4},{7,5},{8,10},{9,11},{10,... | collective-permute-start | bytes 1572872 | tf_op jit(solution)/shard_map/ppermute | solution.py:76
  (38 other events, 33.1 us)
where the time goes:
time: 165 us; the launch traced here: 164 us
  waiting for transfers between devices  44.7 us (27%)
  starting transfers between devices  37 us (22%)
  local copies, waits for them, and re-layouts  35.6 us (22%)
  other arithmetic  33.7 us (20%)
  matrix products  10.7 us (6%)
  between operations  2.19 us (1%)
    ppermute x20, waiting for transfers between devices, reduce_scatter(): buf = keep + lax.ppermute(send, ALL, xor_pairs(count, b))  29.3 us
    ppermute x21, starting transfers between devices, all_gather(): other = lax.ppermute(buf, ALL, xor_pairs(count, b))  17.3 us
    ppermute x21, waiting for transfers between devices, all_gather(): other = lax.ppermute(buf, ALL, xor_pairs(count, b))  15.4 us
    ppermute x20, starting transfers between devices, reduce_scatter(): buf = keep + lax.ppermute(send, ALL, xor_pairs(count, b))  12.7 us
    dot_general x4, matrix products, local(): lax.dot_general(left, field.reshape(2 * depth, nev), (((0,), (0,)), ((),...  7.11 us
    another operation x12, other arithmetic  6.06 us
    unnamed x115, local copies, waits for them, and re-layouts  4.66 us
    ppermute x1, starting transfers between devices, local(): lax.ppermute(ev[:, :, :, 0:1], 'gx', [(i, (i - 1) % nx) for i in range(nx)])  3.96 us
  transfers between devices with their start and end apart: 45, of which 19 were waited for; matrix products, arithmetic and copies ran while one was open for 36% of the time, Pallas kernels for 0%

commit v1 on v0

--- a/solution.py
+++ b/solution.py
@@ -104,27 +104,30 @@
             jnp.concatenate([dn_y, src_y[:, :, :, :, : ly - 1]], axis=4),
         ]
         depth = ncol * nz * lx * ly
-        flat = ev.reshape(2, depth, nev)
-        swapped = jnp.concatenate([-flat[1], flat[0]], axis=0)
-        left = jnp.concatenate([flat.reshape(2 * depth, nev), swapped], axis=1)
+        turned = ev.reshape(2, depth, nev).transpose(0, 2, 1)
+        left = jnp.concatenate(
+            [
+                jnp.concatenate([turned[0], turned[1]], axis=1),
+                jnp.concatenate([-turned[1], turned[0]], axis=1),
+            ],
+            axis=0,
+        )
         rows = nev // count
 
         prows = perambulator.shape[1]
         nspin = perambulator.shape[2] // nev
-        chosen = jnp.take(perambulator.reshape(2, prows, nspin, nev), spin_map, axis=2)
-        p_re, p_im = chosen[0], chosen[1]
+        p_re = perambulator[0].reshape(prows * nspin, nev)
+        p_im = perambulator[1].reshape(prows * nspin, nev)
         lhs = jnp.stack(
             [jnp.concatenate([p_re, -p_im], -1), jnp.concatenate([p_im, p_re], -1)], 0
-        ).reshape(2 * prows * nspin, 2 * nev)
+        ).reshape(2, prows, nspin, 2 * nev)
+        lhs = jnp.take(lhs, spin_map, axis=2).reshape(2 * prows * nspin, 2 * nev)
 
         own = []
         products = []
         for d, field in enumerate(disp):
             order = orders[d % len(orders)]
-            gram = lax.dot_general(
-                left, field.reshape(2 * depth, nev), (((0,), (0,)), ((), ())),
-                preferred_element_type=jnp.float32,
-            )
+            gram = jnp.dot(left, field.reshape(2 * depth, nev), preferred_element_type=jnp.float32)
             buf = gram.reshape([2] + [2] * nbits + [rows, nev])
             part = reduce_scatter(buf, order, nbits, count, 1).reshape(2, rows, nev)
             part = part * norm_factor

time: 165 us -> 159 us (0.964)
  local copies, waits for them, and re-layouts: 35.6 us -> 27.7 us
  starting transfers between devices: 37 us -> 41.7 us
  waiting for transfers between devices: 44.7 us -> 40.8 us
    ppermute x21, starting transfers between devices: 17.3 us -> 21.8 us  [all_gather(): other = lax.ppermute(buf, ALL, xor_pairs(count, b))]
    ppermute x21, waiting for transfers between devices: 15.4 us -> 12 us  [all_gather(): other = lax.ppermute(buf, ALL, xor_pairs(count, b))]
    reshape x2 -> x1, local copies, waits for them, and re-layouts: 4.06 us -> 0.69 us  [local(): turned = ev.reshape(2, depth, nev).transpose(0, 2, 1)]
    another operation x2 -> x1, local copies, waits for them, and re-layouts: 3.38 us -> 0.04 us  [local(): p_im = perambulator[1].reshape(prows * nspin, nev)]
    neg x1 -> x0, local copies, waits for them, and re-layouts: 2.29 us -> none  [local(): swapped = jnp.concatenate([-flat[1], flat[0]], axis=0)]
    squeeze x2 -> x1, local copies, waits for them, and re-layouts: 3.21 us -> 1.26 us  [local(): turned[1]]
    select_n x0 -> x2, local copies, waits for them, and re-layouts: none -> 1.95 us  [local(): lhs = jnp.take(lhs, spin_map, axis=2).reshape(2 * prows * nspin, 2 * nev)]
    unnamed x115 -> x131, local copies, waits for them, and re-layouts: 4.66 us -> 6.1 us
  transfers between devices with their start and end apart: 45 -> 45, of which waited for: 19 -> 18; matrix products, arithmetic and copies ran while one was open for 36% -> 33% of each run, Pallas kernels for 0% -> 0%
where the time goes in v1:
time: 159 us; the launch traced here: 158 us
  starting transfers between devices  41.7 us (26%)
  waiting for transfers between devices  40.8 us (26%)
  other arithmetic  35 us (22%)
  local copies, waits for them, and re-layouts  27.7 us (17%)
  matrix products  10.8 us (7%)
  between operations  2.34 us (1%)
    ppermute x20, waiting for transfers between devices, reduce_scatter(): buf = keep + lax.ppermute(send, ALL, xor_pairs(count, b))  28.8 us
    ppermute x21, starting transfers between devices, all_gather(): other = lax.ppermute(buf, ALL, xor_pairs(count, b))  21.8 us
    ppermute x20, starting transfers between devices, reduce_scatter(): buf = keep + lax.ppermute(send, ALL, xor_pairs(count, b))  12.9 us
    ppermute x21, waiting for transfers between devices, all_gather(): other = lax.ppermute(buf, ALL, xor_pairs(count, b))  12 us
    dot_general x4, matrix products, local(): jnp.dot(left, field.reshape(2 * depth, nev), preferred_element_type=jnp.f...  7.13 us
    unnamed x131, local copies, waits for them, and re-layouts  6.1 us
    another operation x12, other arithmetic  6.05 us
    ppermute x1, starting transfers between devices, local(): lax.ppermute(ev[:, :, :, 0:1], 'gx', [(i, (i - 1) % nx) for i in range(nx)])  3.97 us
  transfers between devices with their start and end apart: 45, of which 18 were waited for; matrix products, arithmetic and copies ran while one was open for 33% of the time, Pallas kernels for 0%

profile of v1, /device:TPU:0, one launch (start us, length us, event | category | flops | bytes accessed | tf_op | source)
XLA Modules:
  0.0 158.3 jit_solution(2326776553647345794)
XLA Ops:
  0.6 1.0 slice_bitcast_fusion.21
  2.4 1.9 %convert_element_type.66 = f32[2,3,4,4,16,512]{5,4,3,2,1,0:T(8,128)S(1)} convert(bf16[2,3,4,4,16,512]{5,4,3,2,1,0:T(8,128)(2,1)} %param.5) | non-fusion elementwise | flops 786432 | bytes 4718592 | tf_op jit(solution)/shard_map/convert_element_type | solution.py:13
  6.8 1.0 pad_maximum_fusion.20
  7.8 3.0 %collective-permute-start.18 = (bf16[2,3,4,4,1,512]{5,4,3,2,1,0:T(2,128)(2,1)}, bf16[2,3,4,4,1,512]{5,4,3,2,1,0:T(2,128)(2,1)}, u32[]{:S(2)}, u32[]{:S(2)}) collective-permute-start(bf16[2,3,4,4,1,512]{5,4,3,2,1,0:T(2,128)(2,1)} %pad_maximum_fusion.20), channel_id=1, source_target_pairs={{0,1},{1,0},{2,3},{3,2},{4,5},{5,4},{6,7},{7,6},{8,9},{9,8},{10,11... | collective-permute-start | bytes 294920 | tf_op jit(solution)/shard_map/ppermute | solution.py:97
  14.1 1.2 copy-done
  17.0 4.0 %collective-permute-start = (bf16[2,3,4,1,16,512]{5,4,3,2,1,0:T(8,128)(2,1)}, bf16[2,3,4,1,16,512]{5,4,3,2,1,0:T(8,128)(2,1)S(1)}, u32[]{:S(2)}, u32[]{:S(2)}) collective-permute-start(bf16[2,3,4,1,16,512]{5,4,3,2,1,0:T(8,128)(2,1)} %slice.141), channel_id=1, source_target_pairs={{0,30},{2,0},{4,2},{6,4},{8,6},{10,8},{12,10},{14,12},{16,14},{18,... | collective-permute-start | bytes 1179656 | tf_op jit(solution)/shard_map/ppermute | solution.py:94
  21.6 1.3 slice_bitcast_fusion
  22.9 1.0 fusion.32
  24.6 1.1 slice.140
  25.8 1.2 compare_select_fusion.1
  27.0 1.2 compare_and_fusion
  28.8 1.1 fusion.33
  30.7 1.7 %gather_fusion.1 = bf16[4,2,64,1024]{3,2,1,0:T(8,128)(2,1)} fusion(bf16[2,64,4,1024]{3,1,2,0:T(8,128)(2,1)S(1)} %maximum_maximum_fusion.1, s32[1024]{0:T(1024)} %pad_clamp_fusion), kind=kCustom, calls=%fused_computation.1 | custom fusion | bytes 2097168 | tf_op jit(solution)/shard_map/jit(_take)/gather | solution.py:124
  32.4 1.4 select_bitcast_fusion
  34.6 1.1 select_n.341
  35.8 2.2 %maximum_maximum_fusion = bf16[1024,1536]{1,0:T(8,128)(2,1)S(1)} fusion(bf16[512,768]{1,0:T(8,128)(2,1)} %get-tuple-element.27, bf16[512,768]{1,0:T(8,128)(2,1)} %fusion.32, bf16[512,768]{1,0:T(8,128)(2,1)} %get-tuple-element.26), kind=kLoop, calls=%fused_computation.3 | loop fusion | flops 12582912 | bytes 5505024 | tf_op jit(solution)/shard_map/concatenate | solution.py:108
  38.6 1.7 %fusion.4 = bf16[2,3,4,4,16,512]{5,4,3,2,1,0:T(8,128)(2,1)S(1)} fusion(bf16[1,3,4,4,16,512]{5,4,3,2,1,0:T(8,128)(2,1)S(1)} %copy-done.6, bf16[1,3,4,4,16,512]{5,4,3,2,1,0:T(8,128)(2,1)S(1)} %copy-done.8, bf16[2,3,4,4,1,512]{5,4,3,2,1,0:T(2,128)(2,1)} %collective-permute-done.18), kind=kLoop, calls=%fused_computation.11 | loop fusion | flops 4718592 | bytes 3244032 | tf_op jit(solution)/shard_map/concatenate | solution.py:104
  40.3 1.8 %fusion = f32[2,2,2,2,2,2,16,512]{7,6,0,5,4,3,2,1:T(8,128)S(1)} fusion(bf16[1536,512,1,1,1,1,1,1]{1,0,2,7,6,5,4,3:T(8,128)(2,1)S(1)} %bitcast.550, bf16[2,2,2,2,2,2,16,1536]{7,6,5,4,3,2,1,0:T(8,128)(2,1)S(1)} %bitcast.543), kind=kOutput, calls=%fused_computation.4 | convolution fusion | flops 1610612736 | bytes 6815744 | tf_op jit(solution)/shard_map/dot_general | solution.py:130
  42.3 1.1 copy.55
  46.3 1.8 %fusion.2 = f32[2,2,2,2,2,2,16,512]{7,6,0,5,4,3,2,1:T(8,128)S(1)} fusion(bf16[1536,512,1,1,1,1,1,1]{1,0,2,7,6,5,4,3:T(8,128)(2,1)S(1)} %bitcast.552, bf16[2,2,2,2,2,2,16,1536]{7,6,5,4,3,2,1,0:T(8,128)(2,1)S(1)} %bitcast.544), kind=kOutput, calls=%fused_computation.6 | convolution fusion | flops 1610612736 | bytes 6815744 | tf_op jit(solution)/shard_map/dot_general | solution.py:130
  49.5 1.2 fusion.5
  50.6 1.8 %fusion.35 = f32[2,2,2,2,2,2,16,512]{7,6,5,4,3,2,1,0:T(8,128)S(1)} fusion(bf16[2,2,2,2,2,2,16,1536]{7,6,5,4,3,2,1,0:T(8,128)(2,1)S(1)} %bitcast.545, bf16[1536,512,1,1,1,1,1,1]{1,0,7,6,5,4,3,2:T(8,128)(2,1)S(1)} %bitcast.549), kind=kOutput, calls=%fused_computation.259 | convolution fusion | flops 1610612736 | bytes 6815744 | tf_op jit(solution)/shard_map/dot_general | solution.py:130
  56.2 1.8 %fusion.34 = f32[2,2,2,2,2,2,16,512]{7,6,5,4,3,2,1,0:T(8,128)S(1)} fusion(bf16[2,2,2,2,2,2,16,1536]{7,6,5,4,3,2,1,0:T(8,128)(2,1)S(1)} %bitcast.546, bf16[1536,512,1,1,1,1,1,1]{1,0,7,6,5,4,3,2:T(8,128)(2,1)S(1)} %bitcast.551), kind=kOutput, calls=%fused_computation.258 | convolution fusion | flops 1610612736 | bytes 6815744 | tf_op jit(solution)/shard_map/dot_general | solution.py:130
  58.9 1.6 collective-permute-start.20
  61.5 1.3 collective-permute-start.2
  62.8 10.9 %collective-permute-done.20 = f32[2,2,2,2,1,1,16,512]{7,6,0,5,4,3,2,1:T(8,128)S(1)} collective-permute-done((f32[2,2,2,2,1,1,16,512]{7,6,0,5,4,3,2,1:T(8,128)S(1)}, f32[2,2,2,2,1,1,16,512]{7,6,0,5,4,3,2,1:T(8,128)S(1)}, u32[]{:S(2)}, u32[]{:S(2)}) %collective-permute-start.20) | collective-permute-done | bytes 524320 | tf_op jit(solution)/shard_map/ppermute | solution.py:67
  74.6 5.8 %collective-permute-done.21 = f32[2,2,2,1,1,1,16,512]{7,6,0,5,4,3,2,1:T(8,128)S(1)} collective-permute-done((f32[2,2,2,1,1,1,16,512]{7,6,0,5,4,3,2,1:T(8,128)S(1)}, f32[2,2,2,1,1,1,16,512]{7,6,0,5,4,3,2,1:T(8,128)S(1)}, u32[]{:S(2)}, u32[]{:S(2)}) %collective-permute-start.21) | collective-permute-done | bytes 262176 | tf_op jit(solution)/shard_map/ppermute | solution.py:67
  80.6 2.3 %collective-permute-done.9 = f32[2,2,1,1,1,2,16,512]{7,6,0,5,4,3,2,1:T(8,128)S(1)} collective-permute-done((f32[2,2,1,1,1,2,16,512]{7,6,0,5,4,3,2,1:T(8,128)S(1)}, f32[2,2,1,1,1,2,16,512]{7,6,0,5,4,3,2,1:T(8,128)S(1)}, u32[]{:S(2)}, u32[]{:S(2)}) %collective-permute-start.9) | collective-permute-done | bytes 262176 | tf_op jit(solution)/shard_map/ppermute | solution.py:67
  83.4 2.1 %collective-permute-start.15 = (f32[2,2,1,2,1,1,16,512]{7,6,5,4,3,2,1,0:T(8,128)S(1)}, f32[2,2,1,2,1,1,16,512]{7,6,5,4,3,2,1,0:T(8,128)S(1)}, u32[]{:S(2)}, u32[]{:S(2)}) collective-permute-start(f32[2,2,1,2,1,1,16,512]{7,6,5,4,3,2,1,0:T(8,128)S(1)} %constant_dynamic-slice_fusion.7), channel_id=1, source_target_pairs={{0,1},{1,0},{2,3},{3,2},{4,5},{5,4},{6,7},{7,6},{8,9},{9,8},{10,11... | collective-permute-start | bytes 786440 | tf_op jit(solution)/shard_map/ppermute | solution.py:67
  85.6 1.2 collective-permute-start.3
  86.9 2.5 %collective-permute-done.10 = f32[2,2,1,1,1,1,16,512]{7,6,0,5,4,3,2,1:T(8,128)S(1)} collective-permute-done((f32[2,2,1,1,1,1,16,512]{7,6,0,5,4,3,2,1:T(8,128)S(1)}, f32[2,2,1,1,1,1,16,512]{7,6,0,5,4,3,2,1:T(8,128)S(1)}, u32[]{:S(2)}, u32[]{:S(2)}) %collective-permute-start.10) | collective-permute-done | bytes 131104 | tf_op jit(solution)/shard_map/ppermute | solution.py:67
  89.9 2.9 %collective-permute-done.23 = f32[2,1,1,1,1,1,16,512]{7,6,0,5,4,3,2,1:T(8,128)S(1)} collective-permute-done((f32[2,1,1,1,1,1,16,512]{7,6,0,5,4,3,2,1:T(8,128)S(1)}, f32[2,1,1,1,1,1,16,512]{7,6,0,5,4,3,2,1:T(8,128)S(1)}, u32[]{:S(2)}, u32[]{:S(2)}) %collective-permute-start.23) | collective-permute-done | bytes 65568 | tf_op jit(solution)/shard_map/ppermute | solution.py:67
  92.9 2.2 %collective-permute-done.11 = f32[2,1,1,1,1,1,16,512]{7,6,0,5,4,3,2,1:T(8,128)S(1)} collective-permute-done((f32[2,1,1,1,1,1,16,512]{7,6,0,5,4,3,2,1:T(8,128)S(1)}, f32[2,1,1,1,1,1,16,512]{7,6,0,5,4,3,2,1:T(8,128)S(1)}, u32[]{:S(2)}, u32[]{:S(2)}) %collective-permute-start.11) | collective-permute-done | bytes 65568 | tf_op jit(solution)/shard_map/ppermute | solution.py:67
  95.9 1.8 %collective-permute-done.40 = bf16[2,1,1,1,1,1,16,512]{7,6,5,4,3,2,1,0:T(8,128)(2,1)S(1)} collective-permute-done((bf16[2,1,1,1,1,1,16,512]{7,6,5,4,3,2,1,0:T(8,128)(2,1)S(1)}, bf16[2,1,1,1,1,1,16,512]{7,6,5,4,3,2,1,0:T(8,128)(2,1)S(1)}, u32[]{:S(2)}, u32[]{:S(2)}) %collective-permute-start.40) | collective-permute-done | bytes 32800 | tf_op jit(solution)/shard_map/ppermute | solution.py:76
  97.9 2.1 %collective-permute-done.30 = bf16[2,1,1,1,1,1,16,512]{7,6,0,5,4,3,2,1:T(8,128)(2,1)S(1)} collective-permute-done((bf16[2,1,1,1,1,1,16,512]{7,6,0,5,4,3,2,1:T(8,128)(2,1)S(1)}, bf16[2,1,1,1,1,1,16,512]{7,6,0,5,4,3,2,1:T(8,128)(2,1)S(1)}, u32[]{:S(2)}, u32[]{:S(2)}) %collective-permute-start.30) | collective-permute-done | bytes 32800 | tf_op jit(solution)/shard_map/ppermute | solution.py:76
  100.0 1.5 collective-permute-start.31
  101.6 0.9 collective-permute-start.16
  102.8 1.9 %collective-permute-start.42 = (bf16[2,2,2,1,1,1,16,512]{7,6,5,4,3,2,1,0:T(8,128)(2,1)S(1)}, bf16[2,2,2,1,1,1,16,512]{7,6,5,4,3,2,1,0:T(8,128)(2,1)S(1)}, u32[]{:S(2)}, u32[]{:S(2)}) collective-permute-start(bf16[2,2,2,1,1,1,16,512]{7,6,5,4,3,2,1,0:T(8,128)(2,1)S(1)} %pad_maximum_fusion.24), channel_id=1, source_target_pairs={{0,4},{1,5},{2,6},{3,7},{4,0},{5,1},{6,2},{7,3},{8,12},{9,13},{10,... | collective-permute-start | bytes 393224 | tf_op jit(solution)/shard_map/ppermute | solution.py:76
  104.7 1.3 collective-permute-start.32
  106.0 1.1 collective-permute-done.16
  107.2 1.2 collective-permute-start.17
  108.5 1.8 %collective-permute-start.5 = (f32[2,1,1,1,1,1,16,512]{7,6,5,4,3,2,1,0:T(8,128)S(1)}, f32[2,1,1,1,1,1,16,512]{7,6,5,4,3,2,1,0:T(8,128)S(1)}, u32[]{:S(2)}, u32[]{:S(2)}) collective-permute-start(f32[2,1,1,1,1,1,16,512]{7,6,5,4,3,2,1,0:T(8,128)S(1)} %constant_dynamic-slice_fusion.15), channel_id=1, source_target_pairs={{0,16},{1,17},{2,18},{3,19},{4,20},{5,21},{6,22},{7,23},{8,24},{9,... | collective-permute-start | bytes 196616 | tf_op jit(solution)/shard_map/ppermute | solution.py:67
  110.4 1.1 collective-permute-start.43
  113.0 2.3 %collective-permute-start.35 = (bf16[2,1,1,1,1,1,16,512]{7,6,5,4,3,2,1,0:T(8,128)(2,1)S(1)}, bf16[2,1,1,1,1,1,16,512]{7,6,5,4,3,2,1,0:T(8,128)(2,1)S(1)}, u32[]{:S(2)}, u32[]{:S(2)}) collective-permute-start(bf16[2,1,1,1,1,1,16,512]{7,6,5,4,3,2,1,0:T(8,128)(2,1)S(1)} %get-tuple-element.62), channel_id=1, source_target_pairs={{0,16},{1,17},{2,18},{3,19},{4,20},{5,21},{6,22},{7,23},{8,24},{9,... | collective-permute-start | bytes 98312 | tf_op jit(solution)/shard_map/ppermute | solution.py:76
  116.3 1.5 collective-permute-start.25
  118.2 1.8 %collective-permute-start.36 = (bf16[2,2,1,1,1,1,16,512]{7,6,5,4,3,2,1,0:T(8,128)(2,1)S(1)}, bf16[2,2,1,1,1,1,16,512]{7,6,5,4,3,2,1,0:T(8,128)(2,1)S(1)}, u32[]{:S(2)}, u32[]{:S(2)}) collective-permute-start(bf16[2,2,1,1,1,1,16,512]{7,6,5,4,3,2,1,0:T(8,128)(2,1)S(1)} %pad_maximum_fusion.27), channel_id=1, source_target_pairs={{0,4},{1,5},{2,6},{3,7},{4,0},{5,1},{6,2},{7,3},{8,12},{9,13},{10,... | collective-permute-start | bytes 196616 | tf_op jit(solution)/shard_map/ppermute | solution.py:76
  120.1 1.1 collective-permute-done.25
  121.2 1.0 collective-permute-start.26
  122.6 1.5 collective-permute-start.37
  124.1 1.4 collective-permute-done.26
  125.5 2.3 %collective-permute-start.27 = (bf16[2,2,2,1,1,1,16,512]{7,6,5,4,3,2,1,0:T(8,128)(2,1)S(1)}, bf16[2,2,2,1,1,1,16,512]{7,6,5,4,3,2,1,0:T(8,128)(2,1)S(1)}, u32[]{:S(2)}, u32[]{:S(2)}) collective-permute-start(bf16[2,2,2,1,1,1,16,512]{7,6,5,4,3,2,1,0:T(8,128)(2,1)S(1)} %pad_maximum_fusion.21), channel_id=1, source_target_pairs={{0,4},{1,5},{2,6},{3,7},{4,0},{5,1},{6,2},{7,3},{8,12},{9,13},{10,... | collective-permute-start | bytes 393224 | tf_op jit(solution)/shard_map/ppermute | solution.py:76
  129.2 1.6 %collective-permute-done.27 = bf16[2,2,2,1,1,1,16,512]{7,6,5,4,3,2,1,0:T(8,128)(2,1)S(1)} collective-permute-done((bf16[2,2,2,1,1,1,16,512]{7,6,5,4,3,2,1,0:T(8,128)(2,1)S(1)}, bf16[2,2,2,1,1,1,16,512]{7,6,5,4,3,2,1,0:T(8,128)(2,1)S(1)}, u32[]{:S(2)}, u32[]{:S(2)}) %collective-permute-start.27) | collective-permute-done | bytes 131104 | tf_op jit(solution)/shard_map/ppermute | solution.py:76
  130.8 2.1 %collective-permute-start.28 = (bf16[2,2,2,2,1,1,16,512]{7,6,5,4,3,2,1,0:T(8,128)(2,1)S(1)}, bf16[2,2,2,2,1,1,16,512]{7,6,5,4,3,2,1,0:T(8,128)(2,1)S(1)}, u32[]{:S(2)}, u32[]{:S(2)}) collective-permute-start(bf16[2,2,2,2,1,1,16,512]{7,6,5,4,3,2,1,0:T(8,128)(2,1)S(1)} %pad_maximum_fusion.16), channel_id=1, source_target_pairs={{0,1},{1,0},{2,3},{3,2},{4,5},{5,4},{6,7},{7,6},{8,9},{9,8},{10,11... | collective-permute-start | bytes 786440 | tf_op jit(solution)/shard_map/ppermute | solution.py:76
  134.0 3.1 %collective-permute-done.38 = bf16[2,2,1,2,1,2,16,512]{7,6,5,4,3,2,1,0:T(8,128)(2,1)S(1)} collective-permute-done((bf16[2,2,1,2,1,2,16,512]{7,6,5,4,3,2,1,0:T(8,128)(2,1)S(1)}, bf16[2,2,1,2,1,2,16,512]{7,6,5,4,3,2,1,0:T(8,128)(2,1)S(1)}, u32[]{:S(2)}, u32[]{:S(2)}) %collective-permute-start.38) | collective-permute-done | bytes 262176 | tf_op jit(solution)/shard_map/ppermute | solution.py:76
  141.4 1.0 copy-done.11
  142.4 1.5 convolution_convert_fusion.2
  143.9 1.4 stack_reshape.13
  145.3 1.2 broadcast_select_fusion.4
  147.4 1.1 stack_reshape.14
  148.5 1.1 broadcast_select_fusion.8
  150.4 1.1 stack_reshape.12
  151.5 1.5 pad_maximum_fusion
  153.0 2.1 %gather_fusion.2 = bf16[4,2,64,2048]{3,2,1,0:T(8,128)(2,1)} fusion(bf16[4,2,64,2048]{3,2,1,0:T(8,128)(2,1)S(1)} %pad_maximum_fusion, s32[1024]{0:T(1024)} %pad_clamp_fusion.1), kind=kCustom, calls=%fused_computation.2 | custom fusion | bytes 4194320 | tf_op jit(solution)/shard_map/jit(_take)/gather | solution.py:146
  155.1 3.2 %broadcast_select_fusion = bf16[4,2,64,2048]{3,2,1,0:T(8,128)(2,1)} fusion(bf16[4,2,64,2048]{3,2,1,0:T(8,128)(2,1)} %gather_fusion.2, pred[4]{0:T(512)(128)(4,1)S(1)} %copy-done.63), kind=kLoop, calls=%fused_computation.9 | loop fusion | flops 1048576 | bytes 4194308 | tf_op jit(solution)/shard_map/jit(_take)/select_n | solution.py:146
  (312 shorter events, 37.3 us)
Async XLA Ops:
  2.3 2.0 %copy-start.21 = (f32[4,4,16]{2,1,0:T(4,128)}, f32[4,4,16]{2,1,0:T(4,128)S(1)}, u32[]{:S(2)}) copy-start(f32[4,4,16]{2,1,0:T(4,128)S(1)} %get-tuple-element.92) | copy-start | bytes 3076
  2.3 2.0 %copy-start.33 = (f32[4,4,16]{2,1,0:T(4,128)}, f32[4,4,16]{2,1,0:T(4,128)S(1)}, u32[]{:S(2)}) copy-start(f32[4,4,16]{2,1,0:T(4,128)S(1)} %get-tuple-element.86) | copy-start | bytes 3076
  2.3 2.5 %copy-start.23 = (f32[4,4,16]{2,1,0:T(4,128)}, f32[4,4,16]{2,1,0:T(4,128)S(1)}, u32[]{:S(2)}) copy-start(f32[4,4,16]{2,1,0:T(4,128)S(1)} %get-tuple-element.94) | copy-start | bytes 3076
  2.3 2.5 %copy-start.35 = (f32[4,4,16]{2,1,0:T(4,128)}, f32[4,4,16]{2,1,0:T(4,128)S(1)}, u32[]{:S(2)}) copy-start(f32[4,4,16]{2,1,0:T(4,128)S(1)} %get-tuple-element.88) | copy-start | bytes 3076
  2.3 3.0 %copy-start.13 = (f32[4,4,16]{2,1,0:T(4,128)}, f32[4,4,16]{2,1,0:T(4,128)S(1)}, u32[]{:S(2)}) copy-start(f32[4,4,16]{2,1,0:T(4,128)S(1)} %get-tuple-element.101) | copy-start | bytes 3076
  2.3 3.0 %copy-start.25 = (f32[4,4,16]{2,1,0:T(4,128)}, f32[4,4,16]{2,1,0:T(4,128)S(1)}, u32[]{:S(2)}) copy-start(f32[4,4,16]{2,1,0:T(4,128)S(1)} %get-tuple-element.96) | copy-start | bytes 3076
  2.3 3.0 %copy-start.37 = (f32[4,4,16]{2,1,0:T(4,128)}, f32[4,4,16]{2,1,0:T(4,128)S(1)}, u32[]{:S(2)}) copy-start(f32[4,4,16]{2,1,0:T(4,128)S(1)} %get-tuple-element.90) | copy-start | bytes 3076
  7.8 30.8 %collective-permute-start.18 = (bf16[2,3,4,4,1,512]{5,4,3,2,1,0:T(2,128)(2,1)}, bf16[2,3,4,4,1,512]{5,4,3,2,1,0:T(2,128)(2,1)}, u32[]{:S(2)}, u32[]{:S(2)}) collective-permute-start(bf16[2,3,4,4,1,512]{5,4,3,2,1,0:T(2,128)(2,1)} %pad_maximum_fusion.20), channel_id=1, source_target_pairs={{0,1},{1,0},{2,3},{3,2},{4,5},{5,4},{6,7},{7,6},{8,9},{9,8},{10,11... | collective-permute-start | bytes 294920 | tf_op jit(solution)/shard_map/ppermute | solution.py:97
  13.2 3.0 %copy-start.1 = (bf16[1,3,4,4,16,512]{5,4,3,2,1,0:T(8,128)(2,1)}, bf16[1,3,4,4,16,512]{5,4,3,2,1,0:T(8,128)(2,1)S(1)}, u32[]{:S(2)}) copy-start(bf16[1,3,4,4,16,512]{5,4,3,2,1,0:T(8,128)(2,1)S(1)} %maximum_bitcast_fusion.5) | copy-start | bytes 2359300
  13.2 2.1 %copy-start = (bf16[2,3,4,4,16,512]{5,4,3,2,1,0:T(8,128)(2,1)S(1)}, bf16[2,3,4,4,16,512]{5,4,3,2,1,0:T(8,128)(2,1)}, u32[]{:S(2)}) copy-start(bf16[2,3,4,4,16,512]{5,4,3,2,1,0:T(8,128)(2,1)} %param.5) | copy-start | bytes 4718596
  13.3 7.6 %copy-start.3 = (bf16[1,3,4,4,16,512]{5,4,3,2,1,0:T(8,128)(2,1)}, bf16[1,3,4,4,16,512]{5,4,3,2,1,0:T(8,128)(2,1)S(1)}, u32[]{:S(2)}) copy-start(bf16[1,3,4,4,16,512]{5,4,3,2,1,0:T(8,128)(2,1)S(1)} %maximum_bitcast_fusion.4) | copy-start | bytes 2359300
  14.1 34.7 %collective-permute-start.12 = (bf16[2,3,4,1,16,512]{5,4,3,2,1,0:T(8,128)(2,1)}, bf16[2,3,4,1,16,512]{5,4,3,2,1,0:T(8,128)(2,1)}, u32[]{:S(2)}, u32[]{:S(2)}) collective-permute-start(bf16[2,3,4,1,16,512]{5,4,3,2,1,0:T(8,128)(2,1)} %pad_maximum_fusion.14), channel_id=1, source_target_pairs={{0,2},{2,4},{4,6},{6,8},{8,10},{10,12},{12,14},{14,16},{16,18},{18... | collective-permute-start | bytes 1179656 | tf_op jit(solution)/shard_map/ppermute | solution.py:95
  16.2 26.1 %collective-permute-start.6 = (bf16[2,3,4,4,1,512]{5,3,4,2,1,0:T(4,128)(2,1)}, bf16[2,3,4,4,1,512]{5,3,4,2,1,0:T(4,128)(2,1)}, u32[]{:S(2)}, u32[]{:S(2)}) collective-permute-start(bf16[2,3,4,4,1,512]{5,3,4,2,1,0:T(4,128)(2,1)} %copy.80), channel_id=1, source_target_pairs={{0,1},{1,0},{2,3},{3,2},{4,5},{5,4},{6,7},{7,6},{8,9},{9,8},{10,11... | collective-permute-start | bytes 294920 | tf_op jit(solution)/shard_map/ppermute | solution.py:96
  17.0 36.2 %collective-permute-start = (bf16[2,3,4,1,16,512]{5,4,3,2,1,0:T(8,128)(2,1)}, bf16[2,3,4,1,16,512]{5,4,3,2,1,0:T(8,128)(2,1)S(1)}, u32[]{:S(2)}, u32[]{:S(2)}) collective-permute-start(bf16[2,3,4,1,16,512]{5,4,3,2,1,0:T(8,128)(2,1)} %slice.141), channel_id=1, source_target_pairs={{0,30},{2,0},{4,2},{6,4},{8,6},{10,8},{12,10},{14,12},{16,14},{18,... | collective-permute-start | bytes 1179656 | tf_op jit(solution)/shard_map/ppermute | solution.py:94
  35.8 2.2 %copy-start.64 = (s32[4]{0:T(128)S(1)}, s32[4]{0:T(128)}, u32[]{:S(2)}) copy-start(s32[4]{0:T(128)} %compare_select_fusion.1) | copy-start | bytes 52
  35.8 2.8 %copy-start.6 = (bf16[1,3,4,4,16,512]{5,4,3,2,1,0:T(8,128)(2,1)S(1)}, bf16[1,3,4,4,16,512]{5,4,3,2,1,0:T(8,128)(2,1)}, u32[]{:S(2)}) copy-start(bf16[1,3,4,4,16,512]{5,4,3,2,1,0:T(8,128)(2,1)} %copy-done.5) | copy-start | bytes 2359300
  35.8 2.8 %copy-start.8 = (bf16[1,3,4,4,16,512]{5,4,3,2,1,0:T(8,128)(2,1)S(1)}, bf16[1,3,4,4,16,512]{5,4,3,2,1,0:T(8,128)(2,1)}, u32[]{:S(2)}) copy-start(bf16[1,3,4,4,16,512]{5,4,3,2,1,0:T(8,128)(2,1)} %copy-done.7) | copy-start | bytes 2359300
  42.2 16.4 %collective-permute-start.19 = (f32[2,2,2,2,1,2,16,512]{7,6,0,5,4,3,2,1:T(8,128)S(1)}, f32[2,2,2,2,1,2,16,512]{7,6,0,5,4,3,2,1:T(8,128)S(1)}, u32[]{:S(2)}, u32[]{:S(2)}) collective-permute-start(f32[2,2,2,2,1,2,16,512]{7,6,0,5,4,3,2,1:T(8,128)S(1)} %constant_dynamic-slice_fusion.4), channel_id=1, source_target_pairs={{0,2},{1,3},{2,0},{3,1},{4,6},{5,7},{6,4},{7,5},{8,10},{9,11},{10,... | collective-permute-start | bytes 3145736 | tf_op jit(solution)/shard_map/ppermute | solution.py:67
  48.2 12.3 %collective-permute-start.7 = (f32[2,2,2,2,1,2,16,512]{7,6,0,5,4,3,2,1:T(8,128)S(1)}, f32[2,2,2,2,1,2,16,512]{7,6,0,5,4,3,2,1:T(8,128)S(1)}, u32[]{:S(2)}, u32[]{:S(2)}) collective-permute-start(f32[2,2,2,2,1,2,16,512]{7,6,0,5,4,3,2,1:T(8,128)S(1)} %constant_dynamic-slice_fusion.14), channel_id=1, source_target_pairs={{0,2},{1,3},{2,0},{3,1},{4,6},{5,7},{6,4},{7,5},{8,10},{9,11},{10,... | collective-permute-start | bytes 3145736 | tf_op jit(solution)/shard_map/ppermute | solution.py:67
  52.6 1.4 copy-start.40
  52.6 1.4 copy-start.42
  52.6 1.4 copy-start.44
  52.6 1.4 copy-start.60
  52.6 1.4 copy-start.61
  52.6 8.2 %collective-permute-start.13 = (f32[2,2,2,2,1,2,16,512]{7,6,5,4,3,2,1,0:T(8,128)S(1)}, f32[2,2,2,2,1,2,16,512]{7,6,5,4,3,2,1,0:T(8,128)S(1)}, u32[]{:S(2)}, u32[]{:S(2)}) collective-permute-start(f32[2,2,2,2,1,2,16,512]{7,6,5,4,3,2,1,0:T(8,128)S(1)} %constant_dynamic-slice_fusion.9), channel_id=1, source_target_pairs={{0,2},{1,3},{2,0},{3,1},{4,6},{5,7},{6,4},{7,5},{8,10},{9,11},{10,... | collective-permute-start | bytes 3145736 | tf_op jit(solution)/shard_map/ppermute | solution.py:67
  58.1 3.1 %collective-permute-start.1 = (f32[2,2,2,2,1,2,16,512]{7,6,5,4,3,2,1,0:T(8,128)S(1)}, f32[2,2,2,2,1,2,16,512]{7,6,5,4,3,2,1,0:T(8,128)S(1)}, u32[]{:S(2)}, u32[]{:S(2)}) collective-permute-start(f32[2,2,2,2,1,2,16,512]{7,6,5,4,3,2,1,0:T(8,128)S(1)} %constant_dynamic-slice_fusion.19), channel_id=1, source_target_pairs={{0,2},{1,3},{2,0},{3,1},{4,6},{5,7},{6,4},{7,5},{8,10},{9,11},{10,... | collective-permute-start | bytes 3145736 | tf_op jit(solution)/shard_map/ppermute | solution.py:67
  58.9 14.9 %collective-permute-start.20 = (f32[2,2,2,2,1,1,16,512]{7,6,0,5,4,3,2,1:T(8,128)S(1)}, f32[2,2,2,2,1,1,16,512]{7,6,0,5,4,3,2,1:T(8,128)S(1)}, u32[]{:S(2)}, u32[]{:S(2)}) collective-permute-start(f32[2,2,2,2,1,1,16,512]{7,6,0,5,4,3,2,1:T(8,128)S(1)} %constant_dynamic-slice_fusion.3), channel_id=1, source_target_pairs={{0,1},{1,0},{2,3},{3,2},{4,5},{5,4},{6,7},{7,6},{8,9},{9,8},{10,11... | collective-permute-start | bytes 1572872 | tf_op jit(solution)/shard_map/ppermute | solution.py:67
  60.7 13.6 %collective-permute-start.8 = (f32[2,2,2,1,1,2,16,512]{7,6,0,5,4,3,2,1:T(8,128)S(1)}, f32[2,2,2,1,1,2,16,512]{7,6,0,5,4,3,2,1:T(8,128)S(1)}, u32[]{:S(2)}, u32[]{:S(2)}) collective-permute-start(f32[2,2,2,1,1,2,16,512]{7,6,0,5,4,3,2,1:T(8,128)S(1)} %constant_dynamic-slice_fusion.13), channel_id=1, source_target_pairs={{0,4},{1,5},{2,6},{3,7},{4,0},{5,1},{6,2},{7,3},{8,12},{9,13},{10,... | collective-permute-start | bytes 1572872 | tf_op jit(solution)/shard_map/ppermute | solution.py:67
  61.1 21.9 %collective-permute-start.14 = (f32[2,2,1,2,1,2,16,512]{7,6,5,4,3,2,1,0:T(8,128)S(1)}, f32[2,2,1,2,1,2,16,512]{7,6,5,4,3,2,1,0:T(8,128)S(1)}, u32[]{:S(2)}, u32[]{:S(2)}) collective-permute-start(f32[2,2,1,2,1,2,16,512]{7,6,5,4,3,2,1,0:T(8,128)S(1)} %constant_dynamic-slice_fusion.8), channel_id=1, source_target_pairs={{0,8},{1,9},{2,10},{3,11},{4,12},{5,13},{6,14},{7,15},{8,0},{9,1},... | collective-permute-start | bytes 1572872 | tf_op jit(solution)/shard_map/ppermute | solution.py:67
  61.5 23.9 %collective-permute-start.2 = (f32[2,2,2,2,1,1,16,512]{7,6,5,4,3,2,1,0:T(8,128)S(1)}, f32[2,2,2,2,1,1,16,512]{7,6,5,4,3,2,1,0:T(8,128)S(1)}, u32[]{:S(2)}, u32[]{:S(2)}) collective-permute-start(f32[2,2,2,2,1,1,16,512]{7,6,5,4,3,2,1,0:T(8,128)S(1)} %constant_dynamic-slice_fusion.18), channel_id=1, source_target_pairs={{0,1},{1,0},{2,3},{3,2},{4,5},{5,4},{6,7},{7,6},{8,9},{9,8},{10,11... | collective-permute-start | bytes 1572872 | tf_op jit(solution)/shard_map/ppermute | solution.py:67
  73.9 6.5 %collective-permute-start.21 = (f32[2,2,2,1,1,1,16,512]{7,6,0,5,4,3,2,1:T(8,128)S(1)}, f32[2,2,2,1,1,1,16,512]{7,6,0,5,4,3,2,1:T(8,128)S(1)}, u32[]{:S(2)}, u32[]{:S(2)}) collective-permute-start(f32[2,2,2,1,1,1,16,512]{7,6,0,5,4,3,2,1:T(8,128)S(1)} %constant_dynamic-slice_fusion.2), channel_id=1, source_target_pairs={{0,4},{1,5},{2,6},{3,7},{4,0},{5,1},{6,2},{7,3},{8,12},{9,13},{10,... | collective-permute-start | bytes 786440 | tf_op jit(solution)/shard_map/ppermute | solution.py:67
  74.5 8.3 %collective-permute-start.9 = (f32[2,2,1,1,1,2,16,512]{7,6,0,5,4,3,2,1:T(8,128)S(1)}, f32[2,2,1,1,1,2,16,512]{7,6,0,5,4,3,2,1:T(8,128)S(1)}, u32[]{:S(2)}, u32[]{:S(2)}) collective-permute-start(f32[2,2,1,1,1,2,16,512]{7,6,0,5,4,3,2,1:T(8,128)S(1)} %constant_dynamic-slice_fusion.12), channel_id=1, source_target_pairs={{0,8},{1,9},{2,10},{3,11},{4,12},{5,13},{6,14},{7,15},{8,0},{9,1},... | collective-permute-start | bytes 786440 | tf_op jit(solution)/shard_map/ppermute | solution.py:67
  80.5 6.3 %collective-permute-start.22 = (f32[2,2,1,1,1,1,16,512]{7,6,0,5,4,3,2,1:T(8,128)S(1)}, f32[2,2,1,1,1,1,16,512]{7,6,0,5,4,3,2,1:T(8,128)S(1)}, u32[]{:S(2)}, u32[]{:S(2)}) collective-permute-start(f32[2,2,1,1,1,1,16,512]{7,6,0,5,4,3,2,1:T(8,128)S(1)} %constant_dynamic-slice_fusion.1), channel_id=1, source_target_pairs={{0,8},{1,9},{2,10},{3,11},{4,12},{5,13},{6,14},{7,15},{8,0},{9,1},... | collective-permute-start | bytes 393224 | tf_op jit(solution)/shard_map/ppermute | solution.py:67
  82.9 6.4 %collective-permute-start.10 = (f32[2,2,1,1,1,1,16,512]{7,6,0,5,4,3,2,1:T(8,128)S(1)}, f32[2,2,1,1,1,1,16,512]{7,6,0,5,4,3,2,1:T(8,128)S(1)}, u32[]{:S(2)}, u32[]{:S(2)}) collective-permute-start(f32[2,2,1,1,1,1,16,512]{7,6,0,5,4,3,2,1:T(8,128)S(1)} %constant_dynamic-slice_fusion.11), channel_id=1, source_target_pairs={{0,1},{1,0},{2,3},{3,2},{4,5},{5,4},{6,7},{7,6},{8,9},{9,8},{10,11... | collective-permute-start | bytes 393224 | tf_op jit(solution)/shard_map/ppermute | solution.py:67
  83.4 18.2 %collective-permute-start.15 = (f32[2,2,1,2,1,1,16,512]{7,6,5,4,3,2,1,0:T(8,128)S(1)}, f32[2,2,1,2,1,1,16,512]{7,6,5,4,3,2,1,0:T(8,128)S(1)}, u32[]{:S(2)}, u32[]{:S(2)}) collective-permute-start(f32[2,2,1,2,1,1,16,512]{7,6,5,4,3,2,1,0:T(8,128)S(1)} %constant_dynamic-slice_fusion.7), channel_id=1, source_target_pairs={{0,1},{1,0},{2,3},{3,2},{4,5},{5,4},{6,7},{7,6},{8,9},{9,8},{10,11... | collective-permute-start | bytes 786440 | tf_op jit(solution)/shard_map/ppermute | solution.py:67
  85.6 16.9 %collective-permute-start.3 = (f32[2,2,2,1,1,1,16,512]{7,6,5,4,3,2,1,0:T(8,128)S(1)}, f32[2,2,2,1,1,1,16,512]{7,6,5,4,3,2,1,0:T(8,128)S(1)}, u32[]{:S(2)}, u32[]{:S(2)}) collective-permute-start(f32[2,2,2,1,1,1,16,512]{7,6,5,4,3,2,1,0:T(8,128)S(1)} %constant_dynamic-slice_fusion.17), channel_id=1, source_target_pairs={{0,4},{1,5},{2,6},{3,7},{4,0},{5,1},{6,2},{7,3},{8,12},{9,13},{10,... | collective-permute-start | bytes 786440 | tf_op jit(solution)/shard_map/ppermute | solution.py:67
  86.8 6.0 %collective-permute-start.23 = (f32[2,1,1,1,1,1,16,512]{7,6,0,5,4,3,2,1:T(8,128)S(1)}, f32[2,1,1,1,1,1,16,512]{7,6,0,5,4,3,2,1:T(8,128)S(1)}, u32[]{:S(2)}, u32[]{:S(2)}) collective-permute-start(f32[2,1,1,1,1,1,16,512]{7,6,0,5,4,3,2,1:T(8,128)S(1)} %constant_dynamic-slice_fusion), channel_id=1, source_target_pairs={{0,16},{1,17},{2,18},{3,19},{4,20},{5,21},{6,22},{7,23},{8,24},{9,... | collective-permute-start | bytes 196616 | tf_op jit(solution)/shard_map/ppermute | solution.py:67
  89.4 5.7 %collective-permute-start.11 = (f32[2,1,1,1,1,1,16,512]{7,6,0,5,4,3,2,1:T(8,128)S(1)}, f32[2,1,1,1,1,1,16,512]{7,6,0,5,4,3,2,1:T(8,128)S(1)}, u32[]{:S(2)}, u32[]{:S(2)}) collective-permute-start(f32[2,1,1,1,1,1,16,512]{7,6,0,5,4,3,2,1:T(8,128)S(1)} %constant_dynamic-slice_fusion.10), channel_id=1, source_target_pairs={{0,16},{1,17},{2,18},{3,19},{4,20},{5,21},{6,22},{7,23},{8,24},{9,... | collective-permute-start | bytes 196616 | tf_op jit(solution)/shard_map/ppermute | solution.py:67
  92.8 4.9 %collective-permute-start.40 = (bf16[2,1,1,1,1,1,16,512]{7,6,5,4,3,2,1,0:T(8,128)(2,1)S(1)}, bf16[2,1,1,1,1,1,16,512]{7,6,5,4,3,2,1,0:T(8,128)(2,1)S(1)}, u32[]{:S(2)}, u32[]{:S(2)}) collective-permute-start(bf16[2,1,1,1,1,1,16,512]{7,6,5,4,3,2,1,0:T(8,128)(2,1)S(1)} %get-tuple-element.64), channel_id=1, source_target_pairs={{0,16},{1,17},{2,18},{3,19},{4,20},{5,21},{6,22},{7,23},{8,24},{9,... | collective-permute-start | bytes 98312 | tf_op jit(solution)/shard_map/ppermute | solution.py:76
  95.1 4.9 %collective-permute-start.30 = (bf16[2,1,1,1,1,1,16,512]{7,6,0,5,4,3,2,1:T(8,128)(2,1)S(1)}, bf16[2,1,1,1,1,1,16,512]{7,6,0,5,4,3,2,1:T(8,128)(2,1)S(1)}, u32[]{:S(2)}, u32[]{:S(2)}) collective-permute-start(bf16[2,1,1,1,1,1,16,512]{7,6,0,5,4,3,2,1:T(8,128)(2,1)S(1)} %get-tuple-element.60), channel_id=1, source_target_pairs={{0,16},{1,17},{2,18},{3,19},{4,20},{5,21},{6,22},{7,23},{8,24},{9,... | collective-permute-start | bytes 98312 | tf_op jit(solution)/shard_map/ppermute | solution.py:76
  97.7 5.0 %collective-permute-start.41 = (bf16[2,2,1,1,1,1,16,512]{7,6,5,4,3,2,1,0:T(8,128)(2,1)S(1)}, bf16[2,2,1,1,1,1,16,512]{7,6,5,4,3,2,1,0:T(8,128)(2,1)S(1)}, u32[]{:S(2)}, u32[]{:S(2)}) collective-permute-start(bf16[2,2,1,1,1,1,16,512]{7,6,5,4,3,2,1,0:T(8,128)(2,1)S(1)} %pad_maximum_fusion.28), channel_id=1, source_target_pairs={{0,8},{1,9},{2,10},{3,11},{4,12},{5,13},{6,14},{7,15},{8,0},{9,1},... | collective-permute-start | bytes 196616 | tf_op jit(solution)/shard_map/ppermute | solution.py:76
  100.0 4.6 %collective-permute-start.31 = (bf16[2,2,1,1,1,1,16,512]{7,6,0,5,4,3,2,1:T(8,128)(2,1)S(1)}, bf16[2,2,1,1,1,1,16,512]{7,6,0,5,4,3,2,1:T(8,128)(2,1)S(1)}, u32[]{:S(2)}, u32[]{:S(2)}) collective-permute-start(bf16[2,2,1,1,1,1,16,512]{7,6,0,5,4,3,2,1:T(8,128)(2,1)S(1)} %pad_maximum_fusion.26), channel_id=1, source_target_pairs={{0,1},{1,0},{2,3},{3,2},{4,5},{5,4},{6,7},{7,6},{8,9},{9,8},{10,11... | collective-permute-start | bytes 196616 | tf_op jit(solution)/shard_map/ppermute | solution.py:76
  101.6 5.6 %collective-permute-start.16 = (f32[2,2,1,1,1,1,16,512]{7,6,5,4,3,2,1,0:T(8,128)S(1)}, f32[2,2,1,1,1,1,16,512]{7,6,5,4,3,2,1,0:T(8,128)S(1)}, u32[]{:S(2)}, u32[]{:S(2)}) collective-permute-start(f32[2,2,1,1,1,1,16,512]{7,6,5,4,3,2,1,0:T(8,128)S(1)} %constant_dynamic-slice_fusion.6), channel_id=1, source_target_pairs={{0,4},{1,5},{2,6},{3,7},{4,0},{5,1},{6,2},{7,3},{8,12},{9,13},{10,... | collective-permute-start | bytes 393224 | tf_op jit(solution)/shard_map/ppermute | solution.py:67
  102.5 5.9 %collective-permute-start.4 = (f32[2,2,1,1,1,1,16,512]{7,6,5,4,3,2,1,0:T(8,128)S(1)}, f32[2,2,1,1,1,1,16,512]{7,6,5,4,3,2,1,0:T(8,128)S(1)}, u32[]{:S(2)}, u32[]{:S(2)}) collective-permute-start(f32[2,2,1,1,1,1,16,512]{7,6,5,4,3,2,1,0:T(8,128)S(1)} %constant_dynamic-slice_fusion.16), channel_id=1, source_target_pairs={{0,8},{1,9},{2,10},{3,11},{4,12},{5,13},{6,14},{7,15},{8,0},{9,1},... | collective-permute-start | bytes 393224 | tf_op jit(solution)/shard_map/ppermute | solution.py:67
  102.8 7.5 %collective-permute-start.42 = (bf16[2,2,2,1,1,1,16,512]{7,6,5,4,3,2,1,0:T(8,128)(2,1)S(1)}, bf16[2,2,2,1,1,1,16,512]{7,6,5,4,3,2,1,0:T(8,128)(2,1)S(1)}, u32[]{:S(2)}, u32[]{:S(2)}) collective-permute-start(bf16[2,2,2,1,1,1,16,512]{7,6,5,4,3,2,1,0:T(8,128)(2,1)S(1)} %pad_maximum_fusion.24), channel_id=1, source_target_pairs={{0,4},{1,5},{2,6},{3,7},{4,0},{5,1},{6,2},{7,3},{8,12},{9,13},{10,... | collective-permute-start | bytes 393224 | tf_op jit(solution)/shard_map/ppermute | solution.py:76
  104.7 6.7 %collective-permute-start.32 = (bf16[2,2,1,1,1,2,16,512]{7,6,0,5,4,3,2,1:T(8,128)(2,1)S(1)}, bf16[2,2,1,1,1,2,16,512]{7,6,0,5,4,3,2,1:T(8,128)(2,1)S(1)}, u32[]{:S(2)}, u32[]{:S(2)}) collective-permute-start(bf16[2,2,1,1,1,2,16,512]{7,6,0,5,4,3,2,1:T(8,128)(2,1)S(1)} %pad_maximum_fusion.22), channel_id=1, source_target_pairs={{0,8},{1,9},{2,10},{3,11},{4,12},{5,13},{6,14},{7,15},{8,0},{9,1},... | collective-permute-start | bytes 393224 | tf_op jit(solution)/shard_map/ppermute | solution.py:76
  107.2 8.8 %copy-start.63 = (pred[4]{0:T(512)(128)(4,1)S(1)}, pred[4]{0:T(512)(128)(4,1)}, u32[]{:S(2)}) copy-start(pred[4]{0:T(512)(128)(4,1)} %get-tuple-element.146) | copy-start | bytes 16
  107.2 5.7 %collective-permute-start.17 = (f32[2,1,1,1,1,1,16,512]{7,6,5,4,3,2,1,0:T(8,128)S(1)}, f32[2,1,1,1,1,1,16,512]{7,6,5,4,3,2,1,0:T(8,128)S(1)}, u32[]{:S(2)}, u32[]{:S(2)}) collective-permute-start(f32[2,1,1,1,1,1,16,512]{7,6,5,4,3,2,1,0:T(8,128)S(1)} %constant_dynamic-slice_fusion.5), channel_id=1, source_target_pairs={{0,16},{1,17},{2,18},{3,19},{4,20},{5,21},{6,22},{7,23},{8,24},{9,... | collective-permute-start | bytes 196616 | tf_op jit(solution)/shard_map/ppermute | solution.py:67
  108.5 6.8 %collective-permute-start.5 = (f32[2,1,1,1,1,1,16,512]{7,6,5,4,3,2,1,0:T(8,128)S(1)}, f32[2,1,1,1,1,1,16,512]{7,6,5,4,3,2,1,0:T(8,128)S(1)}, u32[]{:S(2)}, u32[]{:S(2)}) collective-permute-start(f32[2,1,1,1,1,1,16,512]{7,6,5,4,3,2,1,0:T(8,128)S(1)} %constant_dynamic-slice_fusion.15), channel_id=1, source_target_pairs={{0,16},{1,17},{2,18},{3,19},{4,20},{5,21},{6,22},{7,23},{8,24},{9,... | collective-permute-start | bytes 196616 | tf_op jit(solution)/shard_map/ppermute | solution.py:67
  110.4 17.4 %collective-permute-start.43 = (bf16[2,2,2,2,1,1,16,512]{7,6,5,4,3,2,1,0:T(8,128)(2,1)S(1)}, bf16[2,2,2,2,1,1,16,512]{7,6,5,4,3,2,1,0:T(8,128)(2,1)S(1)}, u32[]{:S(2)}, u32[]{:S(2)}) collective-permute-start(bf16[2,2,2,2,1,1,16,512]{7,6,5,4,3,2,1,0:T(8,128)(2,1)S(1)} %pad_maximum_fusion.19), channel_id=1, source_target_pairs={{0,1},{1,0},{2,3},{3,2},{4,5},{5,4},{6,7},{7,6},{8,9},{9,8},{10,11... | collective-permute-start | bytes 786440 | tf_op jit(solution)/shard_map/ppermute | solution.py:76
  111.5 16.5 %collective-permute-start.33 = (bf16[2,2,2,1,1,2,16,512]{7,6,0,5,4,3,2,1:T(8,128)(2,1)S(1)}, bf16[2,2,2,1,1,2,16,512]{7,6,0,5,4,3,2,1:T(8,128)(2,1)S(1)}, u32[]{:S(2)}, u32[]{:S(2)}) collective-permute-start(bf16[2,2,2,1,1,2,16,512]{7,6,0,5,4,3,2,1:T(8,128)(2,1)S(1)} %pad_maximum_fusion.17), channel_id=1, source_target_pairs={{0,4},{1,5},{2,6},{3,7},{4,0},{5,1},{6,2},{7,3},{8,12},{9,13},{10,... | collective-permute-start | bytes 786440 | tf_op jit(solution)/shard_map/ppermute | solution.py:76
  113.0 5.2 %collective-permute-start.35 = (bf16[2,1,1,1,1,1,16,512]{7,6,5,4,3,2,1,0:T(8,128)(2,1)S(1)}, bf16[2,1,1,1,1,1,16,512]{7,6,5,4,3,2,1,0:T(8,128)(2,1)S(1)}, u32[]{:S(2)}, u32[]{:S(2)}) collective-permute-start(bf16[2,1,1,1,1,1,16,512]{7,6,5,4,3,2,1,0:T(8,128)(2,1)S(1)} %get-tuple-element.62), channel_id=1, source_target_pairs={{0,16},{1,17},{2,18},{3,19},{4,20},{5,21},{6,22},{7,23},{8,24},{9,... | collective-permute-start | bytes 98312 | tf_op jit(solution)/shard_map/ppermute | solution.py:76
  116.1 16.8 %collective-permute-start.24 = (f32[4,2,1,1,1,1,1,16,512]{8,7,1,0,6,5,4,3,2:T(8,128)S(1)}, f32[4,2,1,1,1,1,1,16,512]{8,7,1,0,6,5,4,3,2:T(8,128)S(1)}, u32[]{:S(2)}, u32[]{:S(2)}) collective-permute-start(f32[4,2,1,1,1,1,1,16,512]{8,7,1,0,6,5,4,3,2:T(8,128)S(1)} %bitcast_select_fusion), channel_id=1, source_target_pairs={{0,1},{1,0},{2,3},{3,2},{4,5},{5,4},{6,7},{7,6},{8,9},{9,8},{10,11... | collective-permute-start | bytes 786440 | tf_op jit(solution)/shard_map/ppermute | solution.py:76
  116.3 4.8 %collective-permute-start.25 = (bf16[2,1,1,1,1,1,16,512]{7,6,5,4,3,2,1,0:T(8,128)(2,1)S(1)}, bf16[2,1,1,1,1,1,16,512]{7,6,5,4,3,2,1,0:T(8,128)(2,1)S(1)}, u32[]{:S(2)}, u32[]{:S(2)}) collective-permute-start(bf16[2,1,1,1,1,1,16,512]{7,6,5,4,3,2,1,0:T(8,128)(2,1)S(1)} %get-tuple-element.58), channel_id=1, source_target_pairs={{0,16},{1,17},{2,18},{3,19},{4,20},{5,21},{6,22},{7,23},{8,24},{9,... | collective-permute-start | bytes 98312 | tf_op jit(solution)/shard_map/ppermute | solution.py:76
  118.2 4.3 %collective-permute-start.36 = (bf16[2,2,1,1,1,1,16,512]{7,6,5,4,3,2,1,0:T(8,128)(2,1)S(1)}, bf16[2,2,1,1,1,1,16,512]{7,6,5,4,3,2,1,0:T(8,128)(2,1)S(1)}, u32[]{:S(2)}, u32[]{:S(2)}) collective-permute-start(bf16[2,2,1,1,1,1,16,512]{7,6,5,4,3,2,1,0:T(8,128)(2,1)S(1)} %pad_maximum_fusion.27), channel_id=1, source_target_pairs={{0,4},{1,5},{2,6},{3,7},{4,0},{5,1},{6,2},{7,3},{8,12},{9,13},{10,... | collective-permute-start | bytes 196616 | tf_op jit(solution)/shard_map/ppermute | solution.py:76
  121.2 4.3 %collective-permute-start.26 = (bf16[2,2,1,1,1,1,16,512]{7,6,5,4,3,2,1,0:T(8,128)(2,1)S(1)}, bf16[2,2,1,1,1,1,16,512]{7,6,5,4,3,2,1,0:T(8,128)(2,1)S(1)}, u32[]{:S(2)}, u32[]{:S(2)}) collective-permute-start(bf16[2,2,1,1,1,1,16,512]{7,6,5,4,3,2,1,0:T(8,128)(2,1)S(1)} %pad_maximum_fusion.25), channel_id=1, source_target_pairs={{0,8},{1,9},{2,10},{3,11},{4,12},{5,13},{6,14},{7,15},{8,0},{9,1},... | collective-permute-start | bytes 196616 | tf_op jit(solution)/shard_map/ppermute | solution.py:76
  122.6 6.1 %collective-permute-start.37 = (bf16[2,2,1,2,1,1,16,512]{7,6,5,4,3,2,1,0:T(8,128)(2,1)S(1)}, bf16[2,2,1,2,1,1,16,512]{7,6,5,4,3,2,1,0:T(8,128)(2,1)S(1)}, u32[]{:S(2)}, u32[]{:S(2)}) collective-permute-start(bf16[2,2,1,2,1,1,16,512]{7,6,5,4,3,2,1,0:T(8,128)(2,1)S(1)} %pad_maximum_fusion.23), channel_id=1, source_target_pairs={{0,1},{1,0},{2,3},{3,2},{4,5},{5,4},{6,7},{7,6},{8,9},{9,8},{10,11... | collective-permute-start | bytes 393224 | tf_op jit(solution)/shard_map/ppermute | solution.py:76
  125.5 5.2 %collective-permute-start.27 = (bf16[2,2,2,1,1,1,16,512]{7,6,5,4,3,2,1,0:T(8,128)(2,1)S(1)}, bf16[2,2,2,1,1,1,16,512]{7,6,5,4,3,2,1,0:T(8,128)(2,1)S(1)}, u32[]{:S(2)}, u32[]{:S(2)}) collective-permute-start(bf16[2,2,2,1,1,1,16,512]{7,6,5,4,3,2,1,0:T(8,128)(2,1)S(1)} %pad_maximum_fusion.21), channel_id=1, source_target_pairs={{0,4},{1,5},{2,6},{3,7},{4,0},{5,1},{6,2},{7,3},{8,12},{9,13},{10,... | collective-permute-start | bytes 393224 | tf_op jit(solution)/shard_map/ppermute | solution.py:76
  127.9 11.4 %collective-permute-start.44 = (bf16[2,2,2,2,1,2,16,512]{7,6,5,4,3,2,1,0:T(8,128)(2,1)S(1)}, bf16[2,2,2,2,1,2,16,512]{7,6,5,4,3,2,1,0:T(8,128)(2,1)S(1)}, u32[]{:S(2)}, u32[]{:S(2)}) collective-permute-start(bf16[2,2,2,2,1,2,16,512]{7,6,5,4,3,2,1,0:T(8,128)(2,1)S(1)} %pad_maximum_fusion.13), channel_id=1, source_target_pairs={{0,2},{1,3},{2,0},{3,1},{4,6},{5,7},{6,4},{7,5},{8,10},{9,11},{10,... | collective-permute-start | bytes 1572872 | tf_op jit(solution)/shard_map/ppermute | solution.py:76
  128.1 12.7 %collective-permute-start.34 = (bf16[2,2,2,2,1,2,16,512]{7,6,0,5,4,3,2,1:T(8,128)(2,1)S(1)}, bf16[2,2,2,2,1,2,16,512]{7,6,0,5,4,3,2,1:T(8,128)(2,1)S(1)}, u32[]{:S(2)}, u32[]{:S(2)}) collective-permute-start(bf16[2,2,2,2,1,2,16,512]{7,6,0,5,4,3,2,1:T(8,128)(2,1)S(1)} %pad_maximum_fusion.11), channel_id=1, source_target_pairs={{0,2},{1,3},{2,0},{3,1},{4,6},{5,7},{6,4},{7,5},{8,10},{9,11},{10,... | collective-permute-start | bytes 1572872 | tf_op jit(solution)/shard_map/ppermute | solution.py:76
  128.7 8.3 %collective-permute-start.38 = (bf16[2,2,1,2,1,2,16,512]{7,6,5,4,3,2,1,0:T(8,128)(2,1)S(1)}, bf16[2,2,1,2,1,2,16,512]{7,6,5,4,3,2,1,0:T(8,128)(2,1)S(1)}, u32[]{:S(2)}, u32[]{:S(2)}) collective-permute-start(bf16[2,2,1,2,1,2,16,512]{7,6,5,4,3,2,1,0:T(8,128)(2,1)S(1)} %pad_maximum_fusion.18), channel_id=1, source_target_pairs={{0,8},{1,9},{2,10},{3,11},{4,12},{5,13},{6,14},{7,15},{8,0},{9,1},... | collective-permute-start | bytes 786440 | tf_op jit(solution)/shard_map/ppermute | solution.py:76
  130.8 7.1 %collective-permute-start.28 = (bf16[2,2,2,2,1,1,16,512]{7,6,5,4,3,2,1,0:T(8,128)(2,1)S(1)}, bf16[2,2,2,2,1,1,16,512]{7,6,5,4,3,2,1,0:T(8,128)(2,1)S(1)}, u32[]{:S(2)}, u32[]{:S(2)}) collective-permute-start(bf16[2,2,2,2,1,1,16,512]{7,6,5,4,3,2,1,0:T(8,128)(2,1)S(1)} %pad_maximum_fusion.16), channel_id=1, source_target_pairs={{0,1},{1,0},{2,3},{3,2},{4,5},{5,4},{6,7},{7,6},{8,9},{9,8},{10,11... | collective-permute-start | bytes 786440 | tf_op jit(solution)/shard_map/ppermute | solution.py:76
  137.9 7.4 %collective-permute-start.39 = (bf16[2,2,2,2,1,2,16,512]{7,6,5,4,3,2,1,0:T(8,128)(2,1)}, bf16[2,2,2,2,1,2,16,512]{7,6,5,4,3,2,1,0:T(8,128)(2,1)}, u32[]{:S(2)}, u32[]{:S(2)}) collective-permute-start(bf16[2,2,2,2,1,2,16,512]{7,6,5,4,3,2,1,0:T(8,128)(2,1)} %pad_maximum_fusion.12), channel_id=1, source_target_pairs={{0,2},{1,3},{2,0},{3,1},{4,6},{5,7},{6,4},{7,5},{8,10},{9,11},{10,... | collective-permute-start | bytes 1572872 | tf_op jit(solution)/shard_map/ppermute | solution.py:76
  138.8 9.7 %collective-permute-start.29 = (bf16[2,2,2,2,1,2,16,512]{7,6,5,4,3,2,1,0:T(8,128)(2,1)}, bf16[2,2,2,2,1,2,16,512]{7,6,5,4,3,2,1,0:T(8,128)(2,1)}, u32[]{:S(2)}, u32[]{:S(2)}) collective-permute-start(bf16[2,2,2,2,1,2,16,512]{7,6,5,4,3,2,1,0:T(8,128)(2,1)} %pad_maximum_fusion.10), channel_id=1, source_target_pairs={{0,2},{1,3},{2,0},{3,1},{4,6},{5,7},{6,4},{7,5},{8,10},{9,11},{10,... | collective-permute-start | bytes 1572872 | tf_op jit(solution)/shard_map/ppermute | solution.py:76
  (46 other events, 39.6 us)

commit v2 on v1

--- a/solution.py
+++ b/solution.py
@@ -6,7 +6,7 @@
 from jax.sharding import PartitionSpec as P
 
 ALL = ("gx", "gy")
-STREAMS = 3
+SPLITS = 2
 
 
 def colour_apply(gauge_link, colour_field, dagger):
@@ -46,10 +46,10 @@
     for b in range(nbits):
         d = max(dist(i, i ^ (1 << b)) for i in range(count))
         (core if d == 0 else near if d == 1 else far).append(b)
-    orders = []
-    for s in range(STREAMS):
-        k = s % max(len(near), 1)
-        orders.append(core + near[k:] + near[:k] + far)
+    turns = [near[k:] + near[:k] for k in range(len(near))]
+    back = near[::-1]
+    turns += [back[k:] + back[:k] for k in range(len(near)) if len(near) > 2]
+    orders = [core + t + far for t in turns] or [core + far]
     return nbits, orders
 
 
@@ -121,29 +121,36 @@
         lhs = jnp.stack(
             [jnp.concatenate([p_re, -p_im], -1), jnp.concatenate([p_im, p_re], -1)], 0
         ).reshape(2, prows, nspin, 2 * nev)
-        lhs = jnp.take(lhs, spin_map, axis=2).reshape(2 * prows * nspin, 2 * nev)
+        lhs = jnp.take(lhs, spin_map, axis=2, mode="clip").reshape(2 * prows * nspin, 2 * nev)
 
         own = []
         products = []
+        width = nev // SPLITS
         for d, field in enumerate(disp):
-            order = orders[d % len(orders)]
             gram = jnp.dot(left, field.reshape(2 * depth, nev), preferred_element_type=jnp.float32)
-            buf = gram.reshape([2] + [2] * nbits + [rows, nev])
-            part = reduce_scatter(buf, order, nbits, count, 1).reshape(2, rows, nev)
-            part = part * norm_factor
-            own.append(part)
-            blk = part.astype(jnp.bfloat16).reshape([2] + [1] * nbits + [rows, nev])
-            rhs = all_gather(blk, list(reversed(order)), nbits, count, 1).reshape(2 * nev, nev)
-            product = jnp.dot(lhs, rhs, preferred_element_type=jnp.float32)
-            products.append(product.astype(jnp.bfloat16).reshape(2, prows, nspin * nev))
-        own = jnp.take(jnp.stack(own, 0), directions, axis=0)
+            gram = gram.reshape([2] + [2] * nbits + [rows, nev])
+            own_parts = []
+            prod_parts = []
+            for h in range(SPLITS):
+                order = orders[(d * SPLITS + h) % len(orders)]
+                buf = lax.slice_in_dim(gram, h * width, (h + 1) * width, axis=nbits + 2)
+                part = reduce_scatter(buf, order, nbits, count, 1).reshape(2, rows, width)
+                part = part * norm_factor
+                own_parts.append(part)
+                blk = part.astype(jnp.bfloat16).reshape([2] + [1] * nbits + [rows, width])
+                rhs = all_gather(blk, list(reversed(order)), nbits, count, 1).reshape(2 * nev, width)
+                product = jnp.dot(lhs, rhs, preferred_element_type=jnp.float32)
+                prod_parts.append(product.astype(jnp.bfloat16).reshape(2, prows, nspin, width))
+            own.append(jnp.concatenate(own_parts, axis=-1))
+            products.append(jnp.concatenate(prod_parts, axis=-1).reshape(2, prows, nspin * nev))
+        own = jnp.take(jnp.stack(own, 0), directions, axis=0, mode="clip")
         ndisp = own.shape[0]
         gy_bits = [b for b in range(nbits) if (1 << b) < ny]
         grown = all_gather(
             own.reshape([ndisp, 2] + [1] * nbits + [rows, nev]), gy_bits, nbits, count, 2
         )
         elem = grown.reshape(ndisp, 2, ny * rows, nev)
-        contracted = jnp.take(jnp.stack(products, 0), directions, axis=0)
+        contracted = jnp.take(jnp.stack(products, 0), directions, axis=0, mode="clip")
         return (elem, contracted)
 
     return local

time: 159 us -> 295 us (1.86)
  waiting for transfers between devices: 40.8 us -> 127 us
  starting transfers between devices: 41.7 us -> 80.6 us
  other arithmetic: 35 us -> 42 us
    ppermute x21 -> x41, waiting for transfers between devices: 12 us -> 61.8 us  [all_gather(): other = lax.ppermute(buf, ALL, xor_pairs(count, b))]
    ppermute x20 -> x40, waiting for transfers between devices: 28.8 us -> 65.6 us  [reduce_scatter(): buf = keep + lax.ppermute(send, ALL, xor_pairs(count, b))]
    ppermute x20 -> x40, starting transfers between devices: 12.9 us -> 32.4 us  [reduce_scatter(): buf = keep + lax.ppermute(send, ALL, xor_pairs(count, b))]
    ppermute x21 -> x41, starting transfers between devices: 21.8 us -> 41.2 us  [all_gather(): other = lax.ppermute(buf, ALL, xor_pairs(count, b))]
    select_n x21 -> x40, other arithmetic: 2.91 us -> 11.1 us  [all_gather(): lo = jnp.where(mine == 0, buf, other)]
    select_n x5 -> x2, other arithmetic: 6.49 us -> 0.02 us  [all_gather(): hi = jnp.where(mine == 0, other, buf)]
    concatenate x21 -> x41, other arithmetic: 2.47 us -> 7.75 us  [all_gather(): buf = jnp.concatenate([lo, hi], axis=ax)]
    reshape x0 -> x9, local copies, waits for them, and re-layouts: none -> 3.55 us  [the longest x8 2.45 us: local(): product.astype(jnp.bfloat16).reshape(2, prows, nspin, width)]
  transfers between devices with their start and end apart: 45 -> 85, of which waited for: 18 -> 40; matrix products, arithmetic and copies ran while one was open for 33% -> 22% of each run, Pallas kernels for 0% -> 0%
where the time goes in v2:
time: 295 us; the launch traced here: 294 us
  waiting for transfers between devices  127 us (43%)
  starting transfers between devices  80.6 us (27%)
  other arithmetic  42 us (14%)
  local copies, waits for them, and re-layouts  29.5 us (10%)
  matrix products  11.4 us (4%)
  between operations  2.95 us (1%)
    ppermute x40, waiting for transfers between devices, reduce_scatter(): buf = keep + lax.ppermute(send, ALL, xor_pairs(count, b))  65.6 us
    ppermute x41, waiting for transfers between devices, all_gather(): other = lax.ppermute(buf, ALL, xor_pairs(count, b))  61.8 us
    ppermute x41, starting transfers between devices, all_gather(): other = lax.ppermute(buf, ALL, xor_pairs(count, b))  41.2 us
    ppermute x40, starting transfers between devices, reduce_scatter(): buf = keep + lax.ppermute(send, ALL, xor_pairs(count, b))  32.4 us
    select_n x40, other arithmetic, all_gather(): lo = jnp.where(mine == 0, buf, other)  11.1 us
    concatenate x41, other arithmetic, all_gather(): buf = jnp.concatenate([lo, hi], axis=ax)  7.75 us
    dot_general x4, matrix products, local(): jnp.dot(left, field.reshape(2 * depth, nev), preferred_element_type=jnp.f...  7.13 us
    another operation x12, other arithmetic  6.02 us
  transfers between devices with their start and end apart: 85, of which 40 were waited for; matrix products, arithmetic and copies ran while one was open for 22% of the time, Pallas kernels for 0%

profile of v2, /device:TPU:0, one launch (start us, length us, event | category | flops | bytes accessed | tf_op | source)
XLA Modules:
  0.0 293.9 jit_solution(2239410775806549188)
XLA Ops:
  2.4 1.9 convert_element_type.94
  7.8 3.0 %collective-permute-start.33 = (bf16[2,3,4,4,1,512]{5,4,3,2,1,0:T(2,128)(2,1)}, bf16[2,3,4,4,1,512]{5,4,3,2,1,0:T(2,128)(2,1)}, u32[]{:S(2)}, u32[]{:S(2)}) collective-permute-start(bf16[2,3,4,4,1,512]{5,4,3,2,1,0:T(2,128)(2,1)} %pad_maximum_fusion.28), channel_id=1, source_target_pairs={{0,1},{1,0},{2,3},{3,2},{4,5},{5,4},{6,7},{7,6},{8,9},{9,8},{10,11... | collective-permute-start | bytes 294920 | tf_op jit(solution)/shard_map/ppermute | solution.py:97
  16.4 4.0 %collective-permute-start = (bf16[2,3,4,1,16,512]{5,4,3,2,1,0:T(8,128)(2,1)}, bf16[2,3,4,1,16,512]{5,4,3,2,1,0:T(8,128)(2,1)}, u32[]{:S(2)}, u32[]{:S(2)}) collective-permute-start(bf16[2,3,4,1,16,512]{5,4,3,2,1,0:T(8,128)(2,1)} %slice.157), channel_id=1, source_target_pairs={{0,30},{2,0},{4,2},{6,4},{8,6},{10,8},{12,10},{14,12},{16,14},{18,... | collective-permute-start | bytes 1179656 | tf_op jit(solution)/shard_map/ppermute | solution.py:94
  28.1 2.1 copy.155
  31.4 1.9 maximum_maximum_fusion
  33.4 1.7 fusion.4
  35.2 1.8 fusion.53
  42.0 1.8 fusion.2
  46.6 1.8 fusion
  53.1 1.8 fusion.52
  56.8 7.9 %collective-permute-done.40 = f32[2,2,2,1,1,2,16,256]{7,6,0,5,4,3,2,1:T(8,128)S(1)} collective-permute-done((f32[2,2,2,1,1,2,16,256]{7,6,0,5,4,3,2,1:T(8,128)S(1)}, f32[2,2,2,1,1,2,16,256]{7,6,0,5,4,3,2,1:T(8,128)S(1)}, u32[]{:S(2)}, u32[]{:S(2)}) %collective-permute-start.40) | collective-permute-done | bytes 262176 | tf_op jit(solution)/shard_map/ppermute | solution.py:67
  66.4 7.0 %collective-permute-done.13 = f32[2,2,1,2,1,2,16,256]{7,6,0,5,4,3,2,1:T(8,128)S(1)} collective-permute-done((f32[2,2,1,2,1,2,16,256]{7,6,0,5,4,3,2,1:T(8,128)S(1)}, f32[2,2,1,2,1,2,16,256]{7,6,0,5,4,3,2,1:T(8,128)S(1)}, u32[]{:S(2)}, u32[]{:S(2)}) %collective-permute-start.13) | collective-permute-done | bytes 262176 | tf_op jit(solution)/shard_map/ppermute | solution.py:67
  81.5 1.8 collective-permute-done.19
  85.6 8.8 %collective-permute-done.42 = f32[2,2,1,1,1,1,16,256]{7,6,0,5,4,3,2,1:T(8,128)S(1)} collective-permute-done((f32[2,2,1,1,1,1,16,256]{7,6,0,5,4,3,2,1:T(8,128)S(1)}, f32[2,2,1,1,1,1,16,256]{7,6,0,5,4,3,2,1:T(8,128)S(1)}, u32[]{:S(2)}, u32[]{:S(2)}) %collective-permute-start.42) | collective-permute-done | bytes 65568 | tf_op jit(solution)/shard_map/ppermute | solution.py:67
  94.4 1.7 collective-permute-start.37
  96.1 2.5 collective-permute-done.37
  99.3 3.6 %collective-permute-done.20 = f32[2,2,1,1,1,1,16,256]{7,6,0,5,4,3,2,1:T(8,128)S(1)} collective-permute-done((f32[2,2,1,1,1,1,16,256]{7,6,0,5,4,3,2,1:T(8,128)S(1)}, f32[2,2,1,1,1,1,16,256]{7,6,0,5,4,3,2,1:T(8,128)S(1)}, u32[]{:S(2)}, u32[]{:S(2)}) %collective-permute-start.20) | collective-permute-done | bytes 65568 | tf_op jit(solution)/shard_map/ppermute | solution.py:67
  103.5 3.6 %collective-permute-done.15 = f32[2,2,1,1,1,1,16,256]{7,6,0,5,4,3,2,1:T(8,128)S(1)} collective-permute-done((f32[2,2,1,1,1,1,16,256]{7,6,0,5,4,3,2,1:T(8,128)S(1)}, f32[2,2,1,1,1,1,16,256]{7,6,0,5,4,3,2,1:T(8,128)S(1)}, u32[]{:S(2)}, u32[]{:S(2)}) %collective-permute-start.15) | collective-permute-done | bytes 65568 | tf_op jit(solution)/shard_map/ppermute | solution.py:67
  108.8 3.2 %collective-permute-done.43 = f32[2,1,1,1,1,1,16,256]{7,6,0,5,4,3,2,1:T(8,128)S(1)} collective-permute-done((f32[2,1,1,1,1,1,16,256]{7,6,0,5,4,3,2,1:T(8,128)S(1)}, f32[2,1,1,1,1,1,16,256]{7,6,0,5,4,3,2,1:T(8,128)S(1)}, u32[]{:S(2)}, u32[]{:S(2)}) %collective-permute-start.43) | collective-permute-done | bytes 32800 | tf_op jit(solution)/shard_map/ppermute | solution.py:67
  113.6 3.2 %collective-permute-done.38 = f32[2,1,1,1,1,1,16,256]{7,6,5,4,3,2,1,0:T(8,128)S(1)} collective-permute-done((f32[2,1,1,1,1,1,16,256]{7,6,5,4,3,2,1,0:T(8,128)S(1)}, f32[2,1,1,1,1,1,16,256]{7,6,5,4,3,2,1,0:T(8,128)S(1)}, u32[]{:S(2)}, u32[]{:S(2)}) %collective-permute-start.38) | collective-permute-done | bytes 32800 | tf_op jit(solution)/shard_map/ppermute | solution.py:67
  116.8 1.7 collective-permute-start.21
  118.5 3.1 %collective-permute-done.21 = f32[2,1,1,1,1,1,16,256]{7,6,0,5,4,3,2,1:T(8,128)S(1)} collective-permute-done((f32[2,1,1,1,1,1,16,256]{7,6,0,5,4,3,2,1:T(8,128)S(1)}, f32[2,1,1,1,1,1,16,256]{7,6,0,5,4,3,2,1:T(8,128)S(1)}, u32[]{:S(2)}, u32[]{:S(2)}) %collective-permute-start.21) | collective-permute-done | bytes 32800 | tf_op jit(solution)/shard_map/ppermute | solution.py:67
  121.6 1.7 collective-permute-start.16
  123.3 3.1 %collective-permute-done.16 = f32[2,1,1,1,1,1,16,256]{7,6,0,5,4,3,2,1:T(8,128)S(1)} collective-permute-done((f32[2,1,1,1,1,1,16,256]{7,6,0,5,4,3,2,1:T(8,128)S(1)}, f32[2,1,1,1,1,1,16,256]{7,6,0,5,4,3,2,1:T(8,128)S(1)}, u32[]{:S(2)}, u32[]{:S(2)}) %collective-permute-start.16) | collective-permute-done | bytes 32800 | tf_op jit(solution)/shard_map/ppermute | solution.py:67
  126.4 1.7 collective-permute-start.80
  128.1 2.9 collective-permute-done.80
  131.0 1.7 collective-permute-start.75
  132.8 2.9 collective-permute-done.75
  135.7 1.7 collective-permute-start.60
  137.4 2.9 collective-permute-done.60
  140.3 1.7 collective-permute-start.55
  142.0 2.9 collective-permute-done.55
  145.8 3.5 %collective-permute-done.81 = bf16[2,2,1,1,1,1,16,256]{7,6,5,4,3,2,1,0:T(8,128)(2,1)S(1)} collective-permute-done((bf16[2,2,1,1,1,1,16,256]{7,6,5,4,3,2,1,0:T(8,128)(2,1)S(1)}, bf16[2,2,1,1,1,1,16,256]{7,6,5,4,3,2,1,0:T(8,128)(2,1)S(1)}, u32[]{:S(2)}, u32[]{:S(2)}) %collective-permute-start.81) | collective-permute-done | bytes 32800 | tf_op jit(solution)/shard_map/ppermute | solution.py:76
  150.0 3.2 %collective-permute-done.61 = bf16[2,2,1,1,1,1,16,256]{7,6,5,4,3,2,1,0:T(8,128)(2,1)S(1)} collective-permute-done((bf16[2,2,1,1,1,1,16,256]{7,6,5,4,3,2,1,0:T(8,128)(2,1)S(1)}, bf16[2,2,1,1,1,1,16,256]{7,6,5,4,3,2,1,0:T(8,128)(2,1)S(1)}, u32[]{:S(2)}, u32[]{:S(2)}) %collective-permute-start.61) | collective-permute-done | bytes 32800 | tf_op jit(solution)/shard_map/ppermute | solution.py:76
  153.7 3.3 %collective-permute-done.56 = bf16[2,2,1,1,1,1,16,256]{7,6,0,5,4,3,2,1:T(8,128)(2,1)S(1)} collective-permute-done((bf16[2,2,1,1,1,1,16,256]{7,6,0,5,4,3,2,1:T(8,128)(2,1)S(1)}, bf16[2,2,1,1,1,1,16,256]{7,6,0,5,4,3,2,1:T(8,128)(2,1)S(1)}, u32[]{:S(2)}, u32[]{:S(2)}) %collective-permute-start.56) | collective-permute-done | bytes 32800 | tf_op jit(solution)/shard_map/ppermute | solution.py:76
  157.1 1.9 collective-permute-start.76
  159.0 2.0 collective-permute-done.76
  161.0 1.9 collective-permute-start.82
  163.5 1.6 collective-permute-start.62
  167.8 2.0 collective-permute-start.8
  184.3 4.1 %collective-permute-done.32 = f32[2,1,1,1,1,1,16,256]{7,6,0,5,4,3,2,1:T(8,128)S(1)} collective-permute-done((f32[2,1,1,1,1,1,16,256]{7,6,0,5,4,3,2,1:T(8,128)S(1)}, f32[2,1,1,1,1,1,16,256]{7,6,0,5,4,3,2,1:T(8,128)S(1)}, u32[]{:S(2)}, u32[]{:S(2)}) %collective-permute-start.32) | collective-permute-done | bytes 32800 | tf_op jit(solution)/shard_map/ppermute | solution.py:67
  189.2 4.0 %collective-permute-done.27 = f32[2,1,1,1,1,1,16,256]{7,6,0,5,4,3,2,1:T(8,128)S(1)} collective-permute-done((f32[2,1,1,1,1,1,16,256]{7,6,0,5,4,3,2,1:T(8,128)S(1)}, f32[2,1,1,1,1,1,16,256]{7,6,0,5,4,3,2,1:T(8,128)S(1)}, u32[]{:S(2)}, u32[]{:S(2)}) %collective-permute-start.27) | collective-permute-done | bytes 32800 | tf_op jit(solution)/shard_map/ppermute | solution.py:67
  194.0 4.2 %collective-permute-done.10 = f32[2,1,1,1,1,1,16,256]{7,6,5,4,3,2,1,0:T(8,128)S(1)} collective-permute-done((f32[2,1,1,1,1,1,16,256]{7,6,5,4,3,2,1,0:T(8,128)S(1)}, f32[2,1,1,1,1,1,16,256]{7,6,5,4,3,2,1,0:T(8,128)S(1)}, u32[]{:S(2)}, u32[]{:S(2)}) %collective-permute-start.10) | collective-permute-done | bytes 32800 | tf_op jit(solution)/shard_map/ppermute | solution.py:67
  198.8 4.3 %collective-permute-done.5 = f32[2,1,1,1,1,1,16,256]{7,6,0,5,4,3,2,1:T(8,128)S(1)} collective-permute-done((f32[2,1,1,1,1,1,16,256]{7,6,0,5,4,3,2,1:T(8,128)S(1)}, f32[2,1,1,1,1,1,16,256]{7,6,0,5,4,3,2,1:T(8,128)S(1)}, u32[]{:S(2)}, u32[]{:S(2)}) %collective-permute-start.5) | collective-permute-done | bytes 32800 | tf_op jit(solution)/shard_map/ppermute | solution.py:67
  204.3 3.4 %collective-permute-done.70 = bf16[2,1,1,1,1,1,16,256]{7,6,0,5,4,3,2,1:T(8,128)(2,1)S(1)} collective-permute-done((bf16[2,1,1,1,1,1,16,256]{7,6,0,5,4,3,2,1:T(8,128)(2,1)S(1)}, bf16[2,1,1,1,1,1,16,256]{7,6,0,5,4,3,2,1:T(8,128)(2,1)S(1)}, u32[]{:S(2)}, u32[]{:S(2)}) %collective-permute-start.70) | collective-permute-done | bytes 16416 | tf_op jit(solution)/shard_map/ppermute | solution.py:76
  208.3 4.1 %collective-permute-done.65 = bf16[2,1,1,1,1,1,16,256]{7,6,0,5,4,3,2,1:T(8,128)(2,1)S(1)} collective-permute-done((bf16[2,1,1,1,1,1,16,256]{7,6,0,5,4,3,2,1:T(8,128)(2,1)S(1)}, bf16[2,1,1,1,1,1,16,256]{7,6,0,5,4,3,2,1:T(8,128)(2,1)S(1)}, u32[]{:S(2)}, u32[]{:S(2)}) %collective-permute-start.65) | collective-permute-done | bytes 16416 | tf_op jit(solution)/shard_map/ppermute | solution.py:76
  212.9 4.1 %collective-permute-done.50 = bf16[2,1,1,1,1,1,16,256]{7,6,5,4,3,2,1,0:T(8,128)(2,1)S(1)} collective-permute-done((bf16[2,1,1,1,1,1,16,256]{7,6,5,4,3,2,1,0:T(8,128)(2,1)S(1)}, bf16[2,1,1,1,1,1,16,256]{7,6,5,4,3,2,1,0:T(8,128)(2,1)S(1)}, u32[]{:S(2)}, u32[]{:S(2)}) %collective-permute-start.50) | collective-permute-done | bytes 16416 | tf_op jit(solution)/shard_map/ppermute | solution.py:76
  217.6 4.1 %collective-permute-done.45 = bf16[2,1,1,1,1,1,16,256]{7,6,0,5,4,3,2,1:T(8,128)(2,1)S(1)} collective-permute-done((bf16[2,1,1,1,1,1,16,256]{7,6,0,5,4,3,2,1:T(8,128)(2,1)S(1)}, bf16[2,1,1,1,1,1,16,256]{7,6,0,5,4,3,2,1:T(8,128)(2,1)S(1)}, u32[]{:S(2)}, u32[]{:S(2)}) %collective-permute-start.45) | collective-permute-done | bytes 16416 | tf_op jit(solution)/shard_map/ppermute | solution.py:76
  221.7 2.1 collective-permute-start.71
  223.8 1.9 collective-permute-done.71
  226.6 3.0 %collective-permute-done.66 = bf16[2,2,1,1,1,1,16,256]{7,6,5,4,3,2,1,0:T(8,128)(2,1)S(1)} collective-permute-done((bf16[2,2,1,1,1,1,16,256]{7,6,5,4,3,2,1,0:T(8,128)(2,1)S(1)}, bf16[2,2,1,1,1,1,16,256]{7,6,5,4,3,2,1,0:T(8,128)(2,1)S(1)}, u32[]{:S(2)}, u32[]{:S(2)}) %collective-permute-start.66) | collective-permute-done | bytes 32800 | tf_op jit(solution)/shard_map/ppermute | solution.py:76
  229.6 2.2 collective-permute-start.51
  231.8 1.9 collective-permute-done.51
  234.4 3.2 %collective-permute-done.46 = bf16[2,2,1,1,1,1,16,256]{7,6,0,5,4,3,2,1:T(8,128)(2,1)S(1)} collective-permute-done((bf16[2,2,1,1,1,1,16,256]{7,6,0,5,4,3,2,1:T(8,128)(2,1)S(1)}, bf16[2,2,1,1,1,1,16,256]{7,6,0,5,4,3,2,1:T(8,128)(2,1)S(1)}, u32[]{:S(2)}, u32[]{:S(2)}) %collective-permute-start.46) | collective-permute-done | bytes 32800 | tf_op jit(solution)/shard_map/ppermute | solution.py:76
  238.4 3.5 %collective-permute-done.72 = bf16[2,2,1,2,1,1,16,256]{7,6,5,4,3,2,1,0:T(8,128)(2,1)S(1)} collective-permute-done((bf16[2,2,1,2,1,1,16,256]{7,6,5,4,3,2,1,0:T(8,128)(2,1)S(1)}, bf16[2,2,1,2,1,1,16,256]{7,6,5,4,3,2,1,0:T(8,128)(2,1)S(1)}, u32[]{:S(2)}, u32[]{:S(2)}) %collective-permute-start.72) | collective-permute-done | bytes 65568 | tf_op jit(solution)/shard_map/ppermute | solution.py:76
  241.9 2.0 collective-permute-start.67
  243.9 2.2 collective-permute-done.67
  246.9 3.5 %collective-permute-done.52 = bf16[2,2,1,1,1,2,16,256]{7,6,5,4,3,2,1,0:T(8,128)(2,1)S(1)} collective-permute-done((bf16[2,2,1,1,1,2,16,256]{7,6,5,4,3,2,1,0:T(8,128)(2,1)S(1)}, bf16[2,2,1,1,1,2,16,256]{7,6,5,4,3,2,1,0:T(8,128)(2,1)S(1)}, u32[]{:S(2)}, u32[]{:S(2)}) %collective-permute-start.52) | collective-permute-done | bytes 65568 | tf_op jit(solution)/shard_map/ppermute | solution.py:76
  250.4 1.8 collective-permute-start.47
  252.9 1.8 collective-permute-done.47
  254.7 2.0 collective-permute-start.44
  260.3 1.9 collective-permute-start.68
  265.5 2.1 collective-permute-start.48
  291.8 2.1 gather_fusion.2
  (478 shorter events, 109.0 us)
Async XLA Ops:
  7.8 25.5 %collective-permute-start.33 = (bf16[2,3,4,4,1,512]{5,4,3,2,1,0:T(2,128)(2,1)}, bf16[2,3,4,4,1,512]{5,4,3,2,1,0:T(2,128)(2,1)}, u32[]{:S(2)}, u32[]{:S(2)}) collective-permute-start(bf16[2,3,4,4,1,512]{5,4,3,2,1,0:T(2,128)(2,1)} %pad_maximum_fusion.28), channel_id=1, source_target_pairs={{0,1},{1,0},{2,3},{3,2},{4,5},{5,4},{6,7},{7,6},{8,9},{9,8},{10,11... | collective-permute-start | bytes 294920 | tf_op jit(solution)/shard_map/ppermute | solution.py:97
  14.1 30.2 %collective-permute-start.22 = (bf16[2,3,4,1,16,512]{5,4,3,2,1,0:T(8,128)(2,1)}, bf16[2,3,4,1,16,512]{5,4,3,2,1,0:T(8,128)(2,1)}, u32[]{:S(2)}, u32[]{:S(2)}) collective-permute-start(bf16[2,3,4,1,16,512]{5,4,3,2,1,0:T(8,128)(2,1)} %pad_maximum_fusion.18), channel_id=1, source_target_pairs={{0,2},{2,4},{4,6},{6,8},{8,10},{10,12},{12,14},{14,16},{16,18},{18... | collective-permute-start | bytes 1179656 | tf_op jit(solution)/shard_map/ppermute | solution.py:95
  15.6 22.4 %collective-permute-start.11 = (bf16[2,3,4,4,1,512]{5,3,4,2,1,0:T(4,128)(2,1)S(1)}, bf16[2,3,4,4,1,512]{5,3,4,2,1,0:T(4,128)(2,1)}, u32[]{:S(2)}, u32[]{:S(2)}) collective-permute-start(bf16[2,3,4,4,1,512]{5,3,4,2,1,0:T(4,128)(2,1)S(1)} %copy.199), channel_id=1, source_target_pairs={{0,1},{1,0},{2,3},{3,2},{4,5},{5,4},{6,7},{7,6},{8,9},{9,8},{10,11... | collective-permute-start | bytes 294920 | tf_op jit(solution)/shard_map/ppermute | solution.py:96
  16.4 32.3 %collective-permute-start = (bf16[2,3,4,1,16,512]{5,4,3,2,1,0:T(8,128)(2,1)}, bf16[2,3,4,1,16,512]{5,4,3,2,1,0:T(8,128)(2,1)}, u32[]{:S(2)}, u32[]{:S(2)}) collective-permute-start(bf16[2,3,4,1,16,512]{5,4,3,2,1,0:T(8,128)(2,1)} %slice.157), channel_id=1, source_target_pairs={{0,30},{2,0},{4,2},{6,4},{8,6},{10,8},{12,10},{14,12},{16,14},{18,... | collective-permute-start | bytes 1179656 | tf_op jit(solution)/shard_map/ppermute | solution.py:94
  37.3 18.2 %collective-permute-start.39 = (f32[2,2,2,2,1,2,16,256]{7,6,0,5,4,3,2,1:T(8,128)S(1)}, f32[2,2,2,2,1,2,16,256]{7,6,0,5,4,3,2,1:T(8,128)S(1)}, u32[]{:S(2)}, u32[]{:S(2)}) collective-permute-start(f32[2,2,2,2,1,2,16,256]{7,6,0,5,4,3,2,1:T(8,128)S(1)} %copy.202), channel_id=1, source_target_pairs={{0,2},{1,3},{2,0},{3,1},{4,6},{5,7},{6,4},{7,5},{8,10},{9,11},{10,... | collective-permute-start | bytes 1572872 | tf_op jit(solution)/shard_map/ppermute | solution.py:67
  37.4 18.9 %collective-permute-start.34 = (f32[2,2,2,2,1,2,16,256]{7,6,5,4,3,2,1,0:T(8,128)S(1)}, f32[2,2,2,2,1,2,16,256]{7,6,5,4,3,2,1,0:T(8,128)S(1)}, u32[]{:S(2)}, u32[]{:S(2)}) collective-permute-start(f32[2,2,2,2,1,2,16,256]{7,6,5,4,3,2,1,0:T(8,128)S(1)} %constant_dynamic-slice_fusion.10), channel_id=1, source_target_pairs={{0,2},{1,3},{2,0},{3,1},{4,6},{5,7},{6,4},{7,5},{8,10},{9,11},{10,... | collective-permute-start | bytes 1572872 | tf_op jit(solution)/shard_map/ppermute | solution.py:67
  44.2 11.5 %collective-permute-start.17 = (f32[2,2,2,2,1,2,16,256]{7,6,0,5,4,3,2,1:T(8,128)S(1)}, f32[2,2,2,2,1,2,16,256]{7,6,0,5,4,3,2,1:T(8,128)S(1)}, u32[]{:S(2)}, u32[]{:S(2)}) collective-permute-start(f32[2,2,2,2,1,2,16,256]{7,6,0,5,4,3,2,1:T(8,128)S(1)} %constant_dynamic-slice_fusion.25), channel_id=1, source_target_pairs={{0,2},{1,3},{2,0},{3,1},{4,6},{5,7},{6,4},{7,5},{8,10},{9,11},{10,... | collective-permute-start | bytes 1572872 | tf_op jit(solution)/shard_map/ppermute | solution.py:67
  44.3 12.2 %collective-permute-start.12 = (f32[2,2,2,2,1,2,16,256]{7,6,0,5,4,3,2,1:T(8,128)S(1)}, f32[2,2,2,2,1,2,16,256]{7,6,0,5,4,3,2,1:T(8,128)S(1)}, u32[]{:S(2)}, u32[]{:S(2)}) collective-permute-start(f32[2,2,2,2,1,2,16,256]{7,6,0,5,4,3,2,1:T(8,128)S(1)} %constant_dynamic-slice_fusion.30), channel_id=1, source_target_pairs={{0,2},{1,3},{2,0},{3,1},{4,6},{5,7},{6,4},{7,5},{8,10},{9,11},{10,... | collective-permute-start | bytes 1572872 | tf_op jit(solution)/shard_map/ppermute | solution.py:67
  48.8 25.1 %collective-permute-start.28 = (f32[2,2,2,2,1,2,16,256]{7,6,0,5,4,3,2,1:T(8,128)S(1)}, f32[2,2,2,2,1,2,16,256]{7,6,0,5,4,3,2,1:T(8,128)S(1)}, u32[]{:S(2)}, u32[]{:S(2)}) collective-permute-start(f32[2,2,2,2,1,2,16,256]{7,6,0,5,4,3,2,1:T(8,128)S(1)} %constant_dynamic-slice_fusion.15), channel_id=1, source_target_pairs={{0,2},{1,3},{2,0},{3,1},{4,6},{5,7},{6,4},{7,5},{8,10},{9,11},{10,... | collective-permute-start | bytes 1572872 | tf_op jit(solution)/shard_map/ppermute | solution.py:67
  55.5 19.4 %collective-permute-start.23 = (f32[2,2,2,2,1,2,16,256]{7,6,0,5,4,3,2,1:T(8,128)S(1)}, f32[2,2,2,2,1,2,16,256]{7,6,0,5,4,3,2,1:T(8,128)S(1)}, u32[]{:S(2)}, u32[]{:S(2)}) collective-permute-start(f32[2,2,2,2,1,2,16,256]{7,6,0,5,4,3,2,1:T(8,128)S(1)} %constant_dynamic-slice_fusion.20), channel_id=1, source_target_pairs={{0,2},{1,3},{2,0},{3,1},{4,6},{5,7},{6,4},{7,5},{8,10},{9,11},{10,... | collective-permute-start | bytes 1572872 | tf_op jit(solution)/shard_map/ppermute | solution.py:67
  55.6 20.9 %collective-permute-start.6 = (f32[2,2,2,2,1,2,16,256]{7,6,5,4,3,2,1,0:T(8,128)S(1)}, f32[2,2,2,2,1,2,16,256]{7,6,5,4,3,2,1,0:T(8,128)S(1)}, u32[]{:S(2)}, u32[]{:S(2)}) collective-permute-start(f32[2,2,2,2,1,2,16,256]{7,6,5,4,3,2,1,0:T(8,128)S(1)} %constant_dynamic-slice_fusion.35), channel_id=1, source_target_pairs={{0,2},{1,3},{2,0},{3,1},{4,6},{5,7},{6,4},{7,5},{8,10},{9,11},{10,... | collective-permute-start | bytes 1572872 | tf_op jit(solution)/shard_map/ppermute | solution.py:67
  56.4 8.3 %collective-permute-start.40 = (f32[2,2,2,1,1,2,16,256]{7,6,0,5,4,3,2,1:T(8,128)S(1)}, f32[2,2,2,1,1,2,16,256]{7,6,0,5,4,3,2,1:T(8,128)S(1)}, u32[]{:S(2)}, u32[]{:S(2)}) collective-permute-start(f32[2,2,2,1,1,2,16,256]{7,6,0,5,4,3,2,1:T(8,128)S(1)} %constant_dynamic-slice_fusion.3), channel_id=1, source_target_pairs={{0,4},{1,5},{2,6},{3,7},{4,0},{5,1},{6,2},{7,3},{8,12},{9,13},{10,... | collective-permute-start | bytes 786440 | tf_op jit(solution)/shard_map/ppermute | solution.py:67
  56.6 9.6 %collective-permute-start.18 = (f32[2,2,1,2,1,2,16,256]{7,6,0,5,4,3,2,1:T(8,128)S(1)}, f32[2,2,1,2,1,2,16,256]{7,6,0,5,4,3,2,1:T(8,128)S(1)}, u32[]{:S(2)}, u32[]{:S(2)}) collective-permute-start(f32[2,2,1,2,1,2,16,256]{7,6,0,5,4,3,2,1:T(8,128)S(1)} %constant_dynamic-slice_fusion.24), channel_id=1, source_target_pairs={{0,8},{1,9},{2,10},{3,11},{4,12},{5,13},{6,14},{7,15},{8,0},{9,1},... | collective-permute-start | bytes 786440 | tf_op jit(solution)/shard_map/ppermute | solution.py:67
  64.7 8.7 %collective-permute-start.35 = (f32[2,2,2,2,1,1,16,256]{7,6,5,4,3,2,1,0:T(8,128)S(1)}, f32[2,2,2,2,1,1,16,256]{7,6,5,4,3,2,1,0:T(8,128)S(1)}, u32[]{:S(2)}, u32[]{:S(2)}) collective-permute-start(f32[2,2,2,2,1,1,16,256]{7,6,5,4,3,2,1,0:T(8,128)S(1)} %constant_dynamic-slice_fusion.9), channel_id=1, source_target_pairs={{0,1},{1,0},{2,3},{3,2},{4,5},{5,4},{6,7},{7,6},{8,9},{9,8},{10,11... | collective-permute-start | bytes 786440 | tf_op jit(solution)/shard_map/ppermute | solution.py:67
  66.2 7.2 %collective-permute-start.13 = (f32[2,2,1,2,1,2,16,256]{7,6,0,5,4,3,2,1:T(8,128)S(1)}, f32[2,2,1,2,1,2,16,256]{7,6,0,5,4,3,2,1:T(8,128)S(1)}, u32[]{:S(2)}, u32[]{:S(2)}) collective-permute-start(f32[2,2,1,2,1,2,16,256]{7,6,0,5,4,3,2,1:T(8,128)S(1)} %constant_dynamic-slice_fusion.29), channel_id=1, source_target_pairs={{0,8},{1,9},{2,10},{3,11},{4,12},{5,13},{6,14},{7,15},{8,0},{9,1},... | collective-permute-start | bytes 786440 | tf_op jit(solution)/shard_map/ppermute | solution.py:67
  73.4 6.0 %collective-permute-start.41 = (f32[2,2,1,1,1,2,16,256]{7,6,0,5,4,3,2,1:T(8,128)S(1)}, f32[2,2,1,1,1,2,16,256]{7,6,0,5,4,3,2,1:T(8,128)S(1)}, u32[]{:S(2)}, u32[]{:S(2)}) collective-permute-start(f32[2,2,1,1,1,2,16,256]{7,6,0,5,4,3,2,1:T(8,128)S(1)} %constant_dynamic-slice_fusion.2), channel_id=1, source_target_pairs={{0,8},{1,9},{2,10},{3,11},{4,12},{5,13},{6,14},{7,15},{8,0},{9,1},... | collective-permute-start | bytes 393224 | tf_op jit(solution)/shard_map/ppermute | solution.py:67
  73.9 6.7 %collective-permute-start.36 = (f32[2,2,2,1,1,1,16,256]{7,6,5,4,3,2,1,0:T(8,128)S(1)}, f32[2,2,2,1,1,1,16,256]{7,6,5,4,3,2,1,0:T(8,128)S(1)}, u32[]{:S(2)}, u32[]{:S(2)}) collective-permute-start(f32[2,2,2,1,1,1,16,256]{7,6,5,4,3,2,1,0:T(8,128)S(1)} %constant_dynamic-slice_fusion.8), channel_id=1, source_target_pairs={{0,4},{1,5},{2,6},{3,7},{4,0},{5,1},{6,2},{7,3},{8,12},{9,13},{10,... | collective-permute-start | bytes 393224 | tf_op jit(solution)/shard_map/ppermute | solution.py:67
  74.9 8.5 %collective-permute-start.19 = (f32[2,2,1,1,1,2,16,256]{7,6,0,5,4,3,2,1:T(8,128)S(1)}, f32[2,2,1,1,1,2,16,256]{7,6,0,5,4,3,2,1:T(8,128)S(1)}, u32[]{:S(2)}, u32[]{:S(2)}) collective-permute-start(f32[2,2,1,1,1,2,16,256]{7,6,0,5,4,3,2,1:T(8,128)S(1)} %constant_dynamic-slice_fusion.23), channel_id=1, source_target_pairs={{0,4},{1,5},{2,6},{3,7},{4,0},{5,1},{6,2},{7,3},{8,12},{9,13},{10,... | collective-permute-start | bytes 393224 | tf_op jit(solution)/shard_map/ppermute | solution.py:67
  76.6 7.5 %collective-permute-start.14 = (f32[2,2,1,2,1,1,16,256]{7,6,0,5,4,3,2,1:T(8,128)S(1)}, f32[2,2,1,2,1,1,16,256]{7,6,0,5,4,3,2,1:T(8,128)S(1)}, u32[]{:S(2)}, u32[]{:S(2)}) collective-permute-start(f32[2,2,1,2,1,1,16,256]{7,6,0,5,4,3,2,1:T(8,128)S(1)} %constant_dynamic-slice_fusion.28), channel_id=1, source_target_pairs={{0,1},{1,0},{2,3},{3,2},{4,5},{5,4},{6,7},{7,6},{8,9},{9,8},{10,11... | collective-permute-start | bytes 393224 | tf_op jit(solution)/shard_map/ppermute | solution.py:67
  77.4 85.6 %collective-permute-start.29 = (f32[2,2,2,2,1,1,16,256]{7,6,0,5,4,3,2,1:T(8,128)S(1)}, f32[2,2,2,2,1,1,16,256]{7,6,0,5,4,3,2,1:T(8,128)S(1)}, u32[]{:S(2)}, u32[]{:S(2)}) collective-permute-start(f32[2,2,2,2,1,1,16,256]{7,6,0,5,4,3,2,1:T(8,128)S(1)} %constant_dynamic-slice_fusion.14), channel_id=1, source_target_pairs={{0,1},{1,0},{2,3},{3,2},{4,5},{5,4},{6,7},{7,6},{8,9},{9,8},{10,11... | collective-permute-start | bytes 786440 | tf_op jit(solution)/shard_map/ppermute | solution.py:67
  79.4 84.1 %collective-permute-start.24 = (f32[2,2,2,1,1,2,16,256]{7,6,0,5,4,3,2,1:T(8,128)S(1)}, f32[2,2,2,1,1,2,16,256]{7,6,0,5,4,3,2,1:T(8,128)S(1)}, u32[]{:S(2)}, u32[]{:S(2)}) collective-permute-start(f32[2,2,2,1,1,2,16,256]{7,6,0,5,4,3,2,1:T(8,128)S(1)} %constant_dynamic-slice_fusion.19), channel_id=1, source_target_pairs={{0,4},{1,5},{2,6},{3,7},{4,0},{5,1},{6,2},{7,3},{8,12},{9,13},{10,... | collective-permute-start | bytes 786440 | tf_op jit(solution)/shard_map/ppermute | solution.py:67
  80.5 84.7 %collective-permute-start.7 = (f32[2,2,2,1,1,2,16,256]{7,6,5,4,3,2,1,0:T(8,128)S(1)}, f32[2,2,2,1,1,2,16,256]{7,6,5,4,3,2,1,0:T(8,128)S(1)}, u32[]{:S(2)}, u32[]{:S(2)}) collective-permute-start(f32[2,2,2,1,1,2,16,256]{7,6,5,4,3,2,1,0:T(8,128)S(1)} %constant_dynamic-slice_fusion.34), channel_id=1, source_target_pairs={{0,4},{1,5},{2,6},{3,7},{4,0},{5,1},{6,2},{7,3},{8,12},{9,13},{10,... | collective-permute-start | bytes 786440 | tf_op jit(solution)/shard_map/ppermute | solution.py:67
  83.4 82.2 %collective-permute-start.2 = (f32[2,2,2,2,1,1,16,256]{7,6,0,5,4,3,2,1:T(8,128)S(1)}, f32[2,2,2,2,1,1,16,256]{7,6,0,5,4,3,2,1:T(8,128)S(1)}, u32[]{:S(2)}, u32[]{:S(2)}) collective-permute-start(f32[2,2,2,2,1,1,16,256]{7,6,0,5,4,3,2,1:T(8,128)S(1)} %constant_dynamic-slice_fusion.39), channel_id=1, source_target_pairs={{0,1},{1,0},{2,3},{3,2},{4,5},{5,4},{6,7},{7,6},{8,9},{9,8},{10,11... | collective-permute-start | bytes 786440 | tf_op jit(solution)/shard_map/ppermute | solution.py:67
  84.1 10.3 %collective-permute-start.42 = (f32[2,2,1,1,1,1,16,256]{7,6,0,5,4,3,2,1:T(8,128)S(1)}, f32[2,2,1,1,1,1,16,256]{7,6,0,5,4,3,2,1:T(8,128)S(1)}, u32[]{:S(2)}, u32[]{:S(2)}) collective-permute-start(f32[2,2,1,1,1,1,16,256]{7,6,0,5,4,3,2,1:T(8,128)S(1)} %constant_dynamic-slice_fusion.1), channel_id=1, source_target_pairs={{0,1},{1,0},{2,3},{3,2},{4,5},{5,4},{6,7},{7,6},{8,9},{9,8},{10,11... | collective-permute-start | bytes 196616 | tf_op jit(solution)/shard_map/ppermute | solution.py:67
  107.2 4.8 %collective-permute-start.43 = (f32[2,1,1,1,1,1,16,256]{7,6,0,5,4,3,2,1:T(8,128)S(1)}, f32[2,1,1,1,1,1,16,256]{7,6,0,5,4,3,2,1:T(8,128)S(1)}, u32[]{:S(2)}, u32[]{:S(2)}) collective-permute-start(f32[2,1,1,1,1,1,16,256]{7,6,0,5,4,3,2,1:T(8,128)S(1)} %constant_dynamic-slice_fusion), channel_id=1, source_target_pairs={{0,16},{1,17},{2,18},{3,19},{4,20},{5,21},{6,22},{7,23},{8,24},{9,... | collective-permute-start | bytes 98312 | tf_op jit(solution)/shard_map/ppermute | solution.py:67
  112.0 4.8 %collective-permute-start.38 = (f32[2,1,1,1,1,1,16,256]{7,6,5,4,3,2,1,0:T(8,128)S(1)}, f32[2,1,1,1,1,1,16,256]{7,6,5,4,3,2,1,0:T(8,128)S(1)}, u32[]{:S(2)}, u32[]{:S(2)}) collective-permute-start(f32[2,1,1,1,1,1,16,256]{7,6,5,4,3,2,1,0:T(8,128)S(1)} %constant_dynamic-slice_fusion.6), channel_id=1, source_target_pairs={{0,16},{1,17},{2,18},{3,19},{4,20},{5,21},{6,22},{7,23},{8,24},{9,... | collective-permute-start | bytes 98312 | tf_op jit(solution)/shard_map/ppermute | solution.py:67
  116.8 4.8 %collective-permute-start.21 = (f32[2,1,1,1,1,1,16,256]{7,6,0,5,4,3,2,1:T(8,128)S(1)}, f32[2,1,1,1,1,1,16,256]{7,6,0,5,4,3,2,1:T(8,128)S(1)}, u32[]{:S(2)}, u32[]{:S(2)}) collective-permute-start(f32[2,1,1,1,1,1,16,256]{7,6,0,5,4,3,2,1:T(8,128)S(1)} %constant_dynamic-slice_fusion.21), channel_id=1, source_target_pairs={{0,16},{1,17},{2,18},{3,19},{4,20},{5,21},{6,22},{7,23},{8,24},{9,... | collective-permute-start | bytes 98312 | tf_op jit(solution)/shard_map/ppermute | solution.py:67
  121.6 4.8 %collective-permute-start.16 = (f32[2,1,1,1,1,1,16,256]{7,6,0,5,4,3,2,1:T(8,128)S(1)}, f32[2,1,1,1,1,1,16,256]{7,6,0,5,4,3,2,1:T(8,128)S(1)}, u32[]{:S(2)}, u32[]{:S(2)}) collective-permute-start(f32[2,1,1,1,1,1,16,256]{7,6,0,5,4,3,2,1:T(8,128)S(1)} %constant_dynamic-slice_fusion.26), channel_id=1, source_target_pairs={{0,16},{1,17},{2,18},{3,19},{4,20},{5,21},{6,22},{7,23},{8,24},{9,... | collective-permute-start | bytes 98312 | tf_op jit(solution)/shard_map/ppermute | solution.py:67
  126.4 4.6 %collective-permute-start.80 = (bf16[2,1,1,1,1,1,16,256]{7,6,5,4,3,2,1,0:T(8,128)(2,1)S(1)}, bf16[2,1,1,1,1,1,16,256]{7,6,5,4,3,2,1,0:T(8,128)(2,1)S(1)}, u32[]{:S(2)}, u32[]{:S(2)}) collective-permute-start(bf16[2,1,1,1,1,1,16,256]{7,6,5,4,3,2,1,0:T(8,128)(2,1)S(1)} %get-tuple-element.160), channel_id=1, source_target_pairs={{0,16},{1,17},{2,18},{3,19},{4,20},{5,21},{6,22},{7,23},{8,24},{9,... | collective-permute-start | bytes 49160 | tf_op jit(solution)/shard_map/ppermute | solution.py:76
  161.0 6.8 %collective-permute-start.82 = (bf16[2,2,1,1,1,2,16,256]{7,6,5,4,3,2,1,0:T(8,128)(2,1)S(1)}, bf16[2,2,1,1,1,2,16,256]{7,6,5,4,3,2,1,0:T(8,128)(2,1)S(1)}, u32[]{:S(2)}, u32[]{:S(2)}) collective-permute-start(bf16[2,2,1,1,1,2,16,256]{7,6,5,4,3,2,1,0:T(8,128)(2,1)S(1)} %pad_maximum_fusion.44), channel_id=1, source_target_pairs={{0,8},{1,9},{2,10},{3,11},{4,12},{5,13},{6,14},{7,15},{8,0},{9,1},... | collective-permute-start | bytes 196616 | tf_op jit(solution)/shard_map/ppermute | solution.py:76
  163.5 6.3 %collective-permute-start.62 = (bf16[2,2,1,1,1,2,16,256]{7,6,5,4,3,2,1,0:T(8,128)(2,1)S(1)}, bf16[2,2,1,1,1,2,16,256]{7,6,5,4,3,2,1,0:T(8,128)(2,1)S(1)}, u32[]{:S(2)}, u32[]{:S(2)}) collective-permute-start(bf16[2,2,1,1,1,2,16,256]{7,6,5,4,3,2,1,0:T(8,128)(2,1)S(1)} %pad_maximum_fusion.40), channel_id=1, source_target_pairs={{0,4},{1,5},{2,6},{3,7},{4,0},{5,1},{6,2},{7,3},{8,12},{9,13},{10,... | collective-permute-start | bytes 196616 | tf_op jit(solution)/shard_map/ppermute | solution.py:76
  165.2 5.2 %collective-permute-start.57 = (bf16[2,2,1,2,1,1,16,256]{7,6,5,4,3,2,1,0:T(8,128)(2,1)S(1)}, bf16[2,2,1,2,1,1,16,256]{7,6,5,4,3,2,1,0:T(8,128)(2,1)S(1)}, u32[]{:S(2)}, u32[]{:S(2)}) collective-permute-start(bf16[2,2,1,2,1,1,16,256]{7,6,5,4,3,2,1,0:T(8,128)(2,1)S(1)} %pad_maximum_fusion.39), channel_id=1, source_target_pairs={{0,1},{1,0},{2,3},{3,2},{4,5},{5,4},{6,7},{7,6},{8,9},{9,8},{10,11... | collective-permute-start | bytes 196616 | tf_op jit(solution)/shard_map/ppermute | solution.py:76
  165.5 6.6 %collective-permute-start.30 = (f32[2,2,1,2,1,1,16,256]{7,6,0,5,4,3,2,1:T(8,128)S(1)}, f32[2,2,1,2,1,1,16,256]{7,6,0,5,4,3,2,1:T(8,128)S(1)}, u32[]{:S(2)}, u32[]{:S(2)}) collective-permute-start(f32[2,2,1,2,1,1,16,256]{7,6,0,5,4,3,2,1:T(8,128)S(1)} %constant_dynamic-slice_fusion.13), channel_id=1, source_target_pairs={{0,8},{1,9},{2,10},{3,11},{4,12},{5,13},{6,14},{7,15},{8,0},{9,1},... | collective-permute-start | bytes 393224 | tf_op jit(solution)/shard_map/ppermute | solution.py:67
  167.3 5.2 %collective-permute-start.25 = (f32[2,2,2,1,1,1,16,256]{7,6,0,5,4,3,2,1:T(8,128)S(1)}, f32[2,2,2,1,1,1,16,256]{7,6,0,5,4,3,2,1:T(8,128)S(1)}, u32[]{:S(2)}, u32[]{:S(2)}) collective-permute-start(f32[2,2,2,1,1,1,16,256]{7,6,0,5,4,3,2,1:T(8,128)S(1)} %constant_dynamic-slice_fusion.18), channel_id=1, source_target_pairs={{0,1},{1,0},{2,3},{3,2},{4,5},{5,4},{6,7},{7,6},{8,9},{9,8},{10,11... | collective-permute-start | bytes 393224 | tf_op jit(solution)/shard_map/ppermute | solution.py:67
  167.8 6.2 %collective-permute-start.8 = (f32[2,2,1,1,1,2,16,256]{7,6,5,4,3,2,1,0:T(8,128)S(1)}, f32[2,2,1,1,1,2,16,256]{7,6,5,4,3,2,1,0:T(8,128)S(1)}, u32[]{:S(2)}, u32[]{:S(2)}) collective-permute-start(f32[2,2,1,1,1,2,16,256]{7,6,5,4,3,2,1,0:T(8,128)S(1)} %constant_dynamic-slice_fusion.33), channel_id=1, source_target_pairs={{0,8},{1,9},{2,10},{3,11},{4,12},{5,13},{6,14},{7,15},{8,0},{9,1},... | collective-permute-start | bytes 393224 | tf_op jit(solution)/shard_map/ppermute | solution.py:67
  169.8 5.0 %collective-permute-start.3 = (f32[2,2,2,1,1,1,16,256]{7,6,0,5,4,3,2,1:T(8,128)S(1)}, f32[2,2,2,1,1,1,16,256]{7,6,0,5,4,3,2,1:T(8,128)S(1)}, u32[]{:S(2)}, u32[]{:S(2)}) collective-permute-start(f32[2,2,2,1,1,1,16,256]{7,6,0,5,4,3,2,1:T(8,128)S(1)} %constant_dynamic-slice_fusion.38), channel_id=1, source_target_pairs={{0,4},{1,5},{2,6},{3,7},{4,0},{5,1},{6,2},{7,3},{8,12},{9,13},{10,... | collective-permute-start | bytes 393224 | tf_op jit(solution)/shard_map/ppermute | solution.py:67
  170.4 6.9 %collective-permute-start.83 = (bf16[2,2,2,1,1,2,16,256]{7,6,5,4,3,2,1,0:T(8,128)(2,1)S(1)}, bf16[2,2,2,1,1,2,16,256]{7,6,5,4,3,2,1,0:T(8,128)(2,1)S(1)}, u32[]{:S(2)}, u32[]{:S(2)}) collective-permute-start(bf16[2,2,2,1,1,2,16,256]{7,6,5,4,3,2,1,0:T(8,128)(2,1)S(1)} %pad_maximum_fusion.36), channel_id=1, source_target_pairs={{0,4},{1,5},{2,6},{3,7},{4,0},{5,1},{6,2},{7,3},{8,12},{9,13},{10,... | collective-permute-start | bytes 393224 | tf_op jit(solution)/shard_map/ppermute | solution.py:76
  172.1 5.0 %collective-permute-start.78 = (bf16[2,2,2,2,1,1,16,256]{7,6,5,4,3,2,1,0:T(8,128)(2,1)S(1)}, bf16[2,2,2,2,1,1,16,256]{7,6,5,4,3,2,1,0:T(8,128)(2,1)S(1)}, u32[]{:S(2)}, u32[]{:S(2)}) collective-permute-start(bf16[2,2,2,2,1,1,16,256]{7,6,5,4,3,2,1,0:T(8,128)(2,1)S(1)} %pad_maximum_fusion.35), channel_id=1, source_target_pairs={{0,1},{1,0},{2,3},{3,2},{4,5},{5,4},{6,7},{7,6},{8,9},{9,8},{10,11... | collective-permute-start | bytes 393224 | tf_op jit(solution)/shard_map/ppermute | solution.py:76
  172.5 6.5 %collective-permute-start.63 = (bf16[2,2,1,2,1,2,16,256]{7,6,5,4,3,2,1,0:T(8,128)(2,1)S(1)}, bf16[2,2,1,2,1,2,16,256]{7,6,5,4,3,2,1,0:T(8,128)(2,1)S(1)}, u32[]{:S(2)}, u32[]{:S(2)}) collective-permute-start(bf16[2,2,1,2,1,2,16,256]{7,6,5,4,3,2,1,0:T(8,128)(2,1)S(1)} %pad_maximum_fusion.32), channel_id=1, source_target_pairs={{0,8},{1,9},{2,10},{3,11},{4,12},{5,13},{6,14},{7,15},{8,0},{9,1},... | collective-permute-start | bytes 393224 | tf_op jit(solution)/shard_map/ppermute | solution.py:76
  174.0 7.2 %collective-permute-start.58 = (bf16[2,2,1,2,1,2,16,256]{7,6,5,4,3,2,1,0:T(8,128)(2,1)S(1)}, bf16[2,2,1,2,1,2,16,256]{7,6,5,4,3,2,1,0:T(8,128)(2,1)S(1)}, u32[]{:S(2)}, u32[]{:S(2)}) collective-permute-start(bf16[2,2,1,2,1,2,16,256]{7,6,5,4,3,2,1,0:T(8,128)(2,1)S(1)} %pad_maximum_fusion.31), channel_id=1, source_target_pairs={{0,8},{1,9},{2,10},{3,11},{4,12},{5,13},{6,14},{7,15},{8,0},{9,1},... | collective-permute-start | bytes 393224 | tf_op jit(solution)/shard_map/ppermute | solution.py:76
  174.9 7.1 %collective-permute-start.31 = (f32[2,2,1,1,1,1,16,256]{7,6,0,5,4,3,2,1:T(8,128)S(1)}, f32[2,2,1,1,1,1,16,256]{7,6,0,5,4,3,2,1:T(8,128)S(1)}, u32[]{:S(2)}, u32[]{:S(2)}) collective-permute-start(f32[2,2,1,1,1,1,16,256]{7,6,0,5,4,3,2,1:T(8,128)S(1)} %constant_dynamic-slice_fusion.12), channel_id=1, source_target_pairs={{0,4},{1,5},{2,6},{3,7},{4,0},{5,1},{6,2},{7,3},{8,12},{9,13},{10,... | collective-permute-start | bytes 196616 | tf_op jit(solution)/shard_map/ppermute | solution.py:67
  177.2 5.4 %collective-permute-start.26 = (f32[2,2,1,1,1,1,16,256]{7,6,0,5,4,3,2,1:T(8,128)S(1)}, f32[2,2,1,1,1,1,16,256]{7,6,0,5,4,3,2,1:T(8,128)S(1)}, u32[]{:S(2)}, u32[]{:S(2)}) collective-permute-start(f32[2,2,1,1,1,1,16,256]{7,6,0,5,4,3,2,1:T(8,128)S(1)} %constant_dynamic-slice_fusion.17), channel_id=1, source_target_pairs={{0,8},{1,9},{2,10},{3,11},{4,12},{5,13},{6,14},{7,15},{8,0},{9,1},... | collective-permute-start | bytes 196616 | tf_op jit(solution)/shard_map/ppermute | solution.py:67
  177.4 5.3 %collective-permute-start.9 = (f32[2,2,1,1,1,1,16,256]{7,6,5,4,3,2,1,0:T(8,128)S(1)}, f32[2,2,1,1,1,1,16,256]{7,6,5,4,3,2,1,0:T(8,128)S(1)}, u32[]{:S(2)}, u32[]{:S(2)}) collective-permute-start(f32[2,2,1,1,1,1,16,256]{7,6,5,4,3,2,1,0:T(8,128)S(1)} %constant_dynamic-slice_fusion.32), channel_id=1, source_target_pairs={{0,1},{1,0},{2,3},{3,2},{4,5},{5,4},{6,7},{7,6},{8,9},{9,8},{10,11... | collective-permute-start | bytes 196616 | tf_op jit(solution)/shard_map/ppermute | solution.py:67
  181.2 77.5 %collective-permute-start.84 = (bf16[2,2,2,2,1,2,16,256]{7,6,5,4,3,2,1,0:T(8,128)(2,1)S(1)}, bf16[2,2,2,2,1,2,16,256]{7,6,5,4,3,2,1,0:T(8,128)(2,1)}, u32[]{:S(2)}, u32[]{:S(2)}) collective-permute-start(bf16[2,2,2,2,1,2,16,256]{7,6,5,4,3,2,1,0:T(8,128)(2,1)S(1)} %pad_maximum_fusion.27), channel_id=1, source_target_pairs={{0,2},{1,3},{2,0},{3,1},{4,6},{5,7},{6,4},{7,5},{8,10},{9,11},{10,... | collective-permute-start | bytes 786440 | tf_op jit(solution)/shard_map/ppermute | solution.py:76
  182.0 78.3 %collective-permute-start.79 = (bf16[2,2,2,2,1,2,16,256]{7,6,5,4,3,2,1,0:T(8,128)(2,1)}, bf16[2,2,2,2,1,2,16,256]{7,6,5,4,3,2,1,0:T(8,128)(2,1)}, u32[]{:S(2)}, u32[]{:S(2)}) collective-permute-start(bf16[2,2,2,2,1,2,16,256]{7,6,5,4,3,2,1,0:T(8,128)(2,1)} %pad_maximum_fusion.26), channel_id=1, source_target_pairs={{0,2},{1,3},{2,0},{3,1},{4,6},{5,7},{6,4},{7,5},{8,10},{9,11},{10,... | collective-permute-start | bytes 786440 | tf_op jit(solution)/shard_map/ppermute | solution.py:76
  182.6 81.2 %collective-permute-start.64 = (bf16[2,2,2,2,1,2,16,256]{7,6,5,4,3,2,1,0:T(8,128)(2,1)}, bf16[2,2,2,2,1,2,16,256]{7,6,5,4,3,2,1,0:T(8,128)(2,1)}, u32[]{:S(2)}, u32[]{:S(2)}) collective-permute-start(bf16[2,2,2,2,1,2,16,256]{7,6,5,4,3,2,1,0:T(8,128)(2,1)} %pad_maximum_fusion.23), channel_id=1, source_target_pairs={{0,2},{1,3},{2,0},{3,1},{4,6},{5,7},{6,4},{7,5},{8,10},{9,11},{10,... | collective-permute-start | bytes 786440 | tf_op jit(solution)/shard_map/ppermute | solution.py:76
  182.7 82.8 %collective-permute-start.59 = (bf16[2,2,2,2,1,2,16,256]{7,6,5,4,3,2,1,0:T(8,128)(2,1)}, bf16[2,2,2,2,1,2,16,256]{7,6,5,4,3,2,1,0:T(8,128)(2,1)}, u32[]{:S(2)}, u32[]{:S(2)}) collective-permute-start(bf16[2,2,2,2,1,2,16,256]{7,6,5,4,3,2,1,0:T(8,128)(2,1)} %pad_maximum_fusion.22), channel_id=1, source_target_pairs={{0,2},{1,3},{2,0},{3,1},{4,6},{5,7},{6,4},{7,5},{8,10},{9,11},{10,... | collective-permute-start | bytes 786440 | tf_op jit(solution)/shard_map/ppermute | solution.py:76
  183.4 5.0 %collective-permute-start.32 = (f32[2,1,1,1,1,1,16,256]{7,6,0,5,4,3,2,1:T(8,128)S(1)}, f32[2,1,1,1,1,1,16,256]{7,6,0,5,4,3,2,1:T(8,128)S(1)}, u32[]{:S(2)}, u32[]{:S(2)}) collective-permute-start(f32[2,1,1,1,1,1,16,256]{7,6,0,5,4,3,2,1:T(8,128)S(1)} %constant_dynamic-slice_fusion.11), channel_id=1, source_target_pairs={{0,16},{1,17},{2,18},{3,19},{4,20},{5,21},{6,22},{7,23},{8,24},{9,... | collective-permute-start | bytes 98312 | tf_op jit(solution)/shard_map/ppermute | solution.py:67
  188.4 4.8 %collective-permute-start.27 = (f32[2,1,1,1,1,1,16,256]{7,6,0,5,4,3,2,1:T(8,128)S(1)}, f32[2,1,1,1,1,1,16,256]{7,6,0,5,4,3,2,1:T(8,128)S(1)}, u32[]{:S(2)}, u32[]{:S(2)}) collective-permute-start(f32[2,1,1,1,1,1,16,256]{7,6,0,5,4,3,2,1:T(8,128)S(1)} %constant_dynamic-slice_fusion.16), channel_id=1, source_target_pairs={{0,16},{1,17},{2,18},{3,19},{4,20},{5,21},{6,22},{7,23},{8,24},{9,... | collective-permute-start | bytes 98312 | tf_op jit(solution)/shard_map/ppermute | solution.py:67
  193.2 5.0 %collective-permute-start.10 = (f32[2,1,1,1,1,1,16,256]{7,6,5,4,3,2,1,0:T(8,128)S(1)}, f32[2,1,1,1,1,1,16,256]{7,6,5,4,3,2,1,0:T(8,128)S(1)}, u32[]{:S(2)}, u32[]{:S(2)}) collective-permute-start(f32[2,1,1,1,1,1,16,256]{7,6,5,4,3,2,1,0:T(8,128)S(1)} %constant_dynamic-slice_fusion.31), channel_id=1, source_target_pairs={{0,16},{1,17},{2,18},{3,19},{4,20},{5,21},{6,22},{7,23},{8,24},{9,... | collective-permute-start | bytes 98312 | tf_op jit(solution)/shard_map/ppermute | solution.py:67
  198.2 4.9 %collective-permute-start.5 = (f32[2,1,1,1,1,1,16,256]{7,6,0,5,4,3,2,1:T(8,128)S(1)}, f32[2,1,1,1,1,1,16,256]{7,6,0,5,4,3,2,1:T(8,128)S(1)}, u32[]{:S(2)}, u32[]{:S(2)}) collective-permute-start(f32[2,1,1,1,1,1,16,256]{7,6,0,5,4,3,2,1:T(8,128)S(1)} %constant_dynamic-slice_fusion.36), channel_id=1, source_target_pairs={{0,16},{1,17},{2,18},{3,19},{4,20},{5,21},{6,22},{7,23},{8,24},{9,... | collective-permute-start | bytes 98312 | tf_op jit(solution)/shard_map/ppermute | solution.py:67
  203.1 4.6 %collective-permute-start.70 = (bf16[2,1,1,1,1,1,16,256]{7,6,0,5,4,3,2,1:T(8,128)(2,1)S(1)}, bf16[2,1,1,1,1,1,16,256]{7,6,0,5,4,3,2,1:T(8,128)(2,1)S(1)}, u32[]{:S(2)}, u32[]{:S(2)}) collective-permute-start(bf16[2,1,1,1,1,1,16,256]{7,6,0,5,4,3,2,1:T(8,128)(2,1)S(1)} %get-tuple-element.156), channel_id=1, source_target_pairs={{0,16},{1,17},{2,18},{3,19},{4,20},{5,21},{6,22},{7,23},{8,24},{9,... | collective-permute-start | bytes 49160 | tf_op jit(solution)/shard_map/ppermute | solution.py:76
  207.7 4.6 %collective-permute-start.65 = (bf16[2,1,1,1,1,1,16,256]{7,6,0,5,4,3,2,1:T(8,128)(2,1)S(1)}, bf16[2,1,1,1,1,1,16,256]{7,6,0,5,4,3,2,1:T(8,128)(2,1)S(1)}, u32[]{:S(2)}, u32[]{:S(2)}) collective-permute-start(bf16[2,1,1,1,1,1,16,256]{7,6,0,5,4,3,2,1:T(8,128)(2,1)S(1)} %get-tuple-element.154), channel_id=1, source_target_pairs={{0,16},{1,17},{2,18},{3,19},{4,20},{5,21},{6,22},{7,23},{8,24},{9,... | collective-permute-start | bytes 49160 | tf_op jit(solution)/shard_map/ppermute | solution.py:76
  212.4 4.6 %collective-permute-start.50 = (bf16[2,1,1,1,1,1,16,256]{7,6,5,4,3,2,1,0:T(8,128)(2,1)S(1)}, bf16[2,1,1,1,1,1,16,256]{7,6,5,4,3,2,1,0:T(8,128)(2,1)S(1)}, u32[]{:S(2)}, u32[]{:S(2)}) collective-permute-start(bf16[2,1,1,1,1,1,16,256]{7,6,5,4,3,2,1,0:T(8,128)(2,1)S(1)} %get-tuple-element.148), channel_id=1, source_target_pairs={{0,16},{1,17},{2,18},{3,19},{4,20},{5,21},{6,22},{7,23},{8,24},{9,... | collective-permute-start | bytes 49160 | tf_op jit(solution)/shard_map/ppermute | solution.py:76
  217.0 4.6 %collective-permute-start.45 = (bf16[2,1,1,1,1,1,16,256]{7,6,0,5,4,3,2,1:T(8,128)(2,1)S(1)}, bf16[2,1,1,1,1,1,16,256]{7,6,0,5,4,3,2,1:T(8,128)(2,1)S(1)}, u32[]{:S(2)}, u32[]{:S(2)}) collective-permute-start(bf16[2,1,1,1,1,1,16,256]{7,6,0,5,4,3,2,1:T(8,128)(2,1)S(1)} %get-tuple-element.146), channel_id=1, source_target_pairs={{0,16},{1,17},{2,18},{3,19},{4,20},{5,21},{6,22},{7,23},{8,24},{9,... | collective-permute-start | bytes 49160 | tf_op jit(solution)/shard_map/ppermute | solution.py:76
  254.7 23.6 %collective-permute-start.44 = (f32[4,2,1,1,1,1,1,16,512]{8,7,1,0,6,5,4,3,2:T(8,128)S(1)}, f32[4,2,1,1,1,1,1,16,512]{8,7,1,0,6,5,4,3,2:T(8,128)}, u32[]{:S(2)}, u32[]{:S(2)}) collective-permute-start(f32[4,2,1,1,1,1,1,16,512]{8,7,1,0,6,5,4,3,2:T(8,128)S(1)} %bitcast.620), channel_id=1, source_target_pairs={{0,1},{1,0},{2,3},{3,2},{4,5},{5,4},{6,7},{7,6},{8,9},{9,8},{10,11... | collective-permute-start | bytes 786440 | tf_op jit(solution)/shard_map/ppermute | solution.py:76
  258.7 13.4 %collective-permute-start.73 = (bf16[2,2,2,2,1,1,16,256]{7,6,5,4,3,2,1,0:T(8,128)(2,1)}, bf16[2,2,2,2,1,1,16,256]{7,6,5,4,3,2,1,0:T(8,128)(2,1)S(1)}, u32[]{:S(2)}, u32[]{:S(2)}) collective-permute-start(bf16[2,2,2,2,1,1,16,256]{7,6,5,4,3,2,1,0:T(8,128)(2,1)} %pad_maximum_fusion.34), channel_id=1, source_target_pairs={{0,1},{1,0},{2,3},{3,2},{4,5},{5,4},{6,7},{7,6},{8,9},{9,8},{10,11... | collective-permute-start | bytes 393224 | tf_op jit(solution)/shard_map/ppermute | solution.py:76
  260.3 12.0 %collective-permute-start.68 = (bf16[2,2,2,1,1,2,16,256]{7,6,5,4,3,2,1,0:T(8,128)(2,1)}, bf16[2,2,2,1,1,2,16,256]{7,6,5,4,3,2,1,0:T(8,128)(2,1)}, u32[]{:S(2)}, u32[]{:S(2)}) collective-permute-start(bf16[2,2,2,1,1,2,16,256]{7,6,5,4,3,2,1,0:T(8,128)(2,1)} %pad_maximum_fusion.33), channel_id=1, source_target_pairs={{0,4},{1,5},{2,6},{3,7},{4,0},{5,1},{6,2},{7,3},{8,12},{9,13},{10,... | collective-permute-start | bytes 393224 | tf_op jit(solution)/shard_map/ppermute | solution.py:76
  263.8 10.7 %collective-permute-start.53 = (bf16[2,2,2,1,1,2,16,256]{7,6,5,4,3,2,1,0:T(8,128)(2,1)}, bf16[2,2,2,1,1,2,16,256]{7,6,5,4,3,2,1,0:T(8,128)(2,1)}, u32[]{:S(2)}, u32[]{:S(2)}) collective-permute-start(bf16[2,2,2,1,1,2,16,256]{7,6,5,4,3,2,1,0:T(8,128)(2,1)} %pad_maximum_fusion.30), channel_id=1, source_target_pairs={{0,4},{1,5},{2,6},{3,7},{4,0},{5,1},{6,2},{7,3},{8,12},{9,13},{10,... | collective-permute-start | bytes 393224 | tf_op jit(solution)/shard_map/ppermute | solution.py:76
  265.5 10.6 %collective-permute-start.48 = (bf16[2,2,2,2,1,1,16,256]{7,6,0,5,4,3,2,1:T(8,128)(2,1)}, bf16[2,2,2,2,1,1,16,256]{7,6,0,5,4,3,2,1:T(8,128)(2,1)}, u32[]{:S(2)}, u32[]{:S(2)}) collective-permute-start(bf16[2,2,2,2,1,1,16,256]{7,6,0,5,4,3,2,1:T(8,128)(2,1)} %pad_maximum_fusion.29), channel_id=1, source_target_pairs={{0,1},{1,0},{2,3},{3,2},{4,5},{5,4},{6,7},{7,6},{8,9},{9,8},{10,11... | collective-permute-start | bytes 393224 | tf_op jit(solution)/shard_map/ppermute | solution.py:76
  272.2 8.0 %collective-permute-start.74 = (bf16[2,2,2,2,1,2,16,256]{7,6,5,4,3,2,1,0:T(8,128)(2,1)S(1)}, bf16[2,2,2,2,1,2,16,256]{7,6,5,4,3,2,1,0:T(8,128)(2,1)S(1)}, u32[]{:S(2)}, u32[]{:S(2)}) collective-permute-start(bf16[2,2,2,2,1,2,16,256]{7,6,5,4,3,2,1,0:T(8,128)(2,1)S(1)} %pad_maximum_fusion.25), channel_id=1, source_target_pairs={{0,2},{1,3},{2,0},{3,1},{4,6},{5,7},{6,4},{7,5},{8,10},{9,11},{10,... | collective-permute-start | bytes 786440 | tf_op jit(solution)/shard_map/ppermute | solution.py:76
  274.0 7.1 %collective-permute-start.69 = (bf16[2,2,2,2,1,2,16,256]{7,6,5,4,3,2,1,0:T(8,128)(2,1)}, bf16[2,2,2,2,1,2,16,256]{7,6,5,4,3,2,1,0:T(8,128)(2,1)}, u32[]{:S(2)}, u32[]{:S(2)}) collective-permute-start(bf16[2,2,2,2,1,2,16,256]{7,6,5,4,3,2,1,0:T(8,128)(2,1)} %pad_maximum_fusion.24), channel_id=1, source_target_pairs={{0,2},{1,3},{2,0},{3,1},{4,6},{5,7},{6,4},{7,5},{8,10},{9,11},{10,... | collective-permute-start | bytes 786440 | tf_op jit(solution)/shard_map/ppermute | solution.py:76
  276.1 9.6 %collective-permute-start.54 = (bf16[2,2,2,2,1,2,16,256]{7,6,5,4,3,2,1,0:T(8,128)(2,1)}, bf16[2,2,2,2,1,2,16,256]{7,6,5,4,3,2,1,0:T(8,128)(2,1)}, u32[]{:S(2)}, u32[]{:S(2)}) collective-permute-start(bf16[2,2,2,2,1,2,16,256]{7,6,5,4,3,2,1,0:T(8,128)(2,1)} %pad_maximum_fusion.21), channel_id=1, source_target_pairs={{0,2},{1,3},{2,0},{3,1},{4,6},{5,7},{6,4},{7,5},{8,10},{9,11},{10,... | collective-permute-start | bytes 786440 | tf_op jit(solution)/shard_map/ppermute | solution.py:76
  277.8 9.5 %collective-permute-start.49 = (bf16[2,2,2,2,1,2,16,256]{7,6,0,5,4,3,2,1:T(8,128)(2,1)}, bf16[2,2,2,2,1,2,16,256]{7,6,0,5,4,3,2,1:T(8,128)(2,1)}, u32[]{:S(2)}, u32[]{:S(2)}) collective-permute-start(bf16[2,2,2,2,1,2,16,256]{7,6,0,5,4,3,2,1:T(8,128)(2,1)} %pad_maximum_fusion.20), channel_id=1, source_target_pairs={{0,2},{1,3},{2,0},{3,1},{4,6},{5,7},{6,4},{7,5},{8,10},{9,11},{10,... | collective-permute-start | bytes 786440 | tf_op jit(solution)/shard_map/ppermute | solution.py:76
  (78 other events, 365.2 us)

commit v3 on v1

--- a/solution.py
+++ b/solution.py
@@ -80,6 +80,17 @@
     return buf
 
 
+def column_splits(total, parts):
+    unit = 128
+    units = total // unit
+    sizes = [units // parts + (1 if s < units % parts else 0) for s in range(parts)]
+    edges = [0]
+    for s in sizes:
+        edges.append(edges[-1] + s * unit)
+    edges[-1] = total
+    return [(edges[s], edges[s + 1]) for s in range(parts) if edges[s + 1] > edges[s]]
+
+
 def make_local(nbits, orders):
     def local(eigen_vecs, gauge_links, directions, spin_map, perambulator):
         nx = lax.axis_size("gx")
@@ -120,30 +131,33 @@
         p_im = perambulator[1].reshape(prows * nspin, nev)
         lhs = jnp.stack(
             [jnp.concatenate([p_re, -p_im], -1), jnp.concatenate([p_im, p_re], -1)], 0
-        ).reshape(2, prows, nspin, 2 * nev)
-        lhs = jnp.take(lhs, spin_map, axis=2).reshape(2 * prows * nspin, 2 * nev)
+        ).reshape(2 * prows * nspin, 2 * nev)
 
+        ndisp = len(disp)
+        fields = jnp.stack([d.reshape(2 * depth, nev) for d in disp], axis=1)
+        gram = jnp.dot(left, fields.reshape(2 * depth, ndisp * nev), preferred_element_type=jnp.float32)
+        gram = gram.reshape([2] + [2] * nbits + [rows, ndisp * nev])
         own = []
         products = []
-        for d, field in enumerate(disp):
-            order = orders[d % len(orders)]
-            gram = jnp.dot(left, field.reshape(2 * depth, nev), preferred_element_type=jnp.float32)
-            buf = gram.reshape([2] + [2] * nbits + [rows, nev])
-            part = reduce_scatter(buf, order, nbits, count, 1).reshape(2, rows, nev)
+        for (a, b), order in zip(column_splits(ndisp * nev, len(orders)), orders):
+            buf = lax.slice_in_dim(gram, a, b, axis=nbits + 2)
+            part = reduce_scatter(buf, order, nbits, count, 1).reshape(2, rows, b - a)
             part = part * norm_factor
             own.append(part)
-            blk = part.astype(jnp.bfloat16).reshape([2] + [1] * nbits + [rows, nev])
-            rhs = all_gather(blk, list(reversed(order)), nbits, count, 1).reshape(2 * nev, nev)
-            product = jnp.dot(lhs, rhs, preferred_element_type=jnp.float32)
-            products.append(product.astype(jnp.bfloat16).reshape(2, prows, nspin * nev))
-        own = jnp.take(jnp.stack(own, 0), directions, axis=0)
-        ndisp = own.shape[0]
+            blk = part.astype(jnp.bfloat16).reshape([2] + [1] * nbits + [rows, b - a])
+            rhs = all_gather(blk, list(reversed(order)), nbits, count, 1).reshape(2 * nev, b - a)
+            products.append(jnp.dot(lhs, rhs, preferred_element_type=jnp.float32).astype(jnp.bfloat16))
+        own = jnp.concatenate(own, axis=-1).reshape(2, rows, ndisp, nev)
+        own = jnp.take(own, directions, axis=2, mode="clip").transpose(2, 0, 1, 3)
         gy_bits = [b for b in range(nbits) if (1 << b) < ny]
         grown = all_gather(
             own.reshape([ndisp, 2] + [1] * nbits + [rows, nev]), gy_bits, nbits, count, 2
         )
         elem = grown.reshape(ndisp, 2, ny * rows, nev)
-        contracted = jnp.take(jnp.stack(products, 0), directions, axis=0)
+        product = jnp.concatenate(products, axis=-1).reshape(2, prows, nspin, ndisp, nev)
+        product = jnp.take(product, spin_map, axis=2, mode="clip")
+        product = jnp.take(product, directions, axis=3, mode="clip")
+        contracted = product.transpose(3, 0, 1, 2, 4).reshape(ndisp, 2, prows, nspin * nev)
         return (elem, contracted)
 
     return local

time: 159 us -> 268 us (1.69); the launches traced: 158 us -> 263 us
  local copies, waits for them, and re-layouts: 27.7 us -> 96.2 us
  other arithmetic: 35 us -> 54.7 us
  waiting for transfers between devices: 40.8 us -> 59 us
  starting transfers between devices: 41.7 us -> 37.9 us
    convert_element_type x0 -> x2, local copies, waits for them, and re-layouts: none -> 23.5 us  [the longest x1 11.8 us: local(): colour_apply(gauge_links[0], ahead_x, False).astype(jnp.bfloat16)]
    another operation x4 -> x3, local copies, waits for them, and re-layouts: 3.9 us -> 25.6 us  [the longest x2 23.7 us: local(): fields = jnp.stack([d.reshape(2 * depth, nev) for d in disp], axis=1)]
    reshape x0 -> x5, local copies, waits for them, and re-layouts: none -> 20 us  [the longest x1 11.3 us: local(): fields.reshape(2 * depth, ndisp * nev)]
    another operation x14 -> x13, other arithmetic: 7.53 us -> 21.7 us  [the longest x1 15.6 us: local(): fields = jnp.stack([d.reshape(2 * depth, nev) for d in disp], axis=1)]
    ppermute x21 -> x16, waiting for transfers between devices: 12 us -> 26 us  [all_gather(): other = lax.ppermute(buf, ALL, xor_pairs(count, b))]
    concatenate x1, other arithmetic: 2.18 us -> 14.1 us  [local(): jnp.concatenate([jnp.concatenate([turned[0], turned[1]], axis=1), jnp.con...]
    ppermute x21 -> x16, starting transfers between devices: 21.8 us -> 11.7 us  [all_gather(): other = lax.ppermute(buf, ALL, xor_pairs(count, b))]
    select_n x5 -> x0, other arithmetic: 6.49 us -> none  [the longest x1 3.17 us: local(): contracted = jnp.take(jnp.stack(products, 0), directions, axis=0)]
  transfers between devices with their start and end apart: 45 -> 35, of which waited for: 18 -> 19; matrix products, arithmetic and copies ran while one was open for 33% -> 34% of each run, Pallas kernels for 0% -> 0%
where the time goes in v3:
time: 268 us; the launch traced here: 263 us
  local copies, waits for them, and re-layouts  96.2 us (36%)
  waiting for transfers between devices  59 us (22%)
  other arithmetic  54.7 us (20%)
  starting transfers between devices  37.9 us (14%)
  matrix products  11.9 us (4%)
  between operations  2.72 us (1%)
    ppermute x15, waiting for transfers between devices, reduce_scatter(): buf = keep + lax.ppermute(send, ALL, xor_pairs(count, b))  33.1 us
    ppermute x16, waiting for transfers between devices, all_gather(): other = lax.ppermute(buf, ALL, xor_pairs(count, b))  26 us
    another operation x2, local copies, waits for them, and re-layouts, local(): fields = jnp.stack([d.reshape(2 * depth, nev) for d in disp], axis=1)  23.7 us
    ppermute x15, starting transfers between devices, reduce_scatter(): buf = keep + lax.ppermute(send, ALL, xor_pairs(count, b))  18.7 us
    another operation x1, other arithmetic, local(): fields = jnp.stack([d.reshape(2 * depth, nev) for d in disp], axis=1)  15.6 us
    concatenate x1, other arithmetic, local(): jnp.concatenate([jnp.concatenate([turned[0], turned[1]], axis=1), jnp.con...  14.1 us
    convert_element_type x1, local copies, waits for them, and re-layouts, local(): colour_apply(gauge_links[0], ahead_x, False).astype(jnp.bfloat16)  11.8 us
    convert_element_type x1, local copies, waits for them, and re-layouts, local(): colour_apply(gauge_links[1], ahead_y, False).astype(jnp.bfloat16)  11.8 us
  transfers between devices with their start and end apart: 35, of which 19 were waited for; matrix products, arithmetic and copies ran while one was open for 34% of the time, Pallas kernels for 0%

profile of v3, /device:TPU:0, one launch (start us, length us, event | category | flops | bytes accessed | tf_op | source)
XLA Modules:
  0.0 262.6 jit_solution(9896651969264677597)
XLA Ops:
  0.6 1.8 slice.147
  2.4 5.5 %collective-permute-start = (bf16[2,3,4,1,16,512]{5,4,3,2,1,0:T(8,128)(2,1)}, bf16[2,3,4,1,16,512]{5,4,3,2,1,0:T(8,128)(2,1)S(1)}, u32[]{:S(2)}, u32[]{:S(2)}) collective-permute-start(bf16[2,3,4,1,16,512]{5,4,3,2,1,0:T(8,128)(2,1)} %slice.147), channel_id=1, source_target_pairs={{0,30},{2,0},{4,2},{6,4},{8,6},{10,8},{12,10},{14,12},{16,14},{18,... | collective-permute-start | bytes 1179656 | tf_op jit(solution)/shard_map/ppermute | solution.py:105
  7.9 1.2 slice.174
  9.9 1.5 collective-permute-start.1
  11.4 1.9 convert_element_type.59
  23.1 14.1 %maximum_maximum_fusion = bf16[1024,1536]{1,0:T(8,128)(2,1)} fusion(bf16[512,768]{1,0:T(8,128)(2,1)S(1)} %get-tuple-element.31, bf16[512,768]{1,0:T(8,128)(2,1)S(1)} %fusion.28, bf16[512,768]{1,0:T(8,128)(2,1)S(1)} %get-tuple-element.30), kind=kLoop, calls=%fused_computation.6 | loop fusion | flops 12582912 | bytes 5505024 | tf_op jit(solution)/shard_map/concatenate | solution.py:119
  37.2 1.1 slice.146
  39.1 1.1 copy.32
  43.1 11.8 %copy.34 = bf16[1536,1,512]{2,1,0:T(2,128)(2,1)S(1)} copy(bf16[1536,1,512]{2,0,1:T(8,128)(2,1)S(1)} %bitcast.507) | data formatting | bytes 3145728 | tf_op jit(solution)/shard_map/convert_element_type | solution.py:113
  54.9 1.7 fusion.2
  56.7 12.0 %copy.36 = bf16[1536,1,512]{2,1,0:T(2,128)(2,1)S(1)} copy(bf16[1536,1,512]{2,0,1:T(8,128)(2,1)S(1)} %bitcast.506) | data formatting | bytes 3145728 | tf_op jit(solution)/shard_map/stack;reshape | solution.py:137
  71.5 11.8 %copy.33 = bf16[1536,1,512]{2,1,0:T(2,128)(2,1)S(1)} copy(bf16[1536,1,512]{2,0,1:T(8,128)(2,1)S(1)} %bitcast.508) | data formatting | bytes 3145728 | tf_op jit(solution)/shard_map/convert_element_type | solution.py:112
  83.3 1.2 fusion.3
  84.5 11.8 %copy.35 = bf16[1536,1,512]{2,1,0:T(2,128)(2,1)S(1)} copy(bf16[1536,1,512]{2,0,1:T(8,128)(2,1)S(1)} %bitcast.505) | data formatting | bytes 3145728 | tf_op jit(solution)/shard_map/stack;reshape | solution.py:137
  96.3 15.6 %pad_maximum_fusion = bf16[1536,4,512]{2,1,0:T(4,128)(2,1)} fusion(bf16[1536,1,512]{2,1,0:T(2,128)(2,1)S(1)} %copy.36, bf16[1536,1,512]{2,1,0:T(2,128)(2,1)S(1)} %copy.35, bf16[1536,1,512]{2,1,0:T(2,128)(2,1)S(1)} %copy.34, bf16[1536,1,512]{2,1,0:T(2,128)(2,1)S(1)} %copy.33), kind=kLoop, calls=%fused_computation.3 | loop fusion | flops 25165824 | bytes 12582912 | tf_op jit(solution)/shard_map/stack | solution.py:137
  111.9 11.3 %reshape.2073 = bf16[1536,2048,1,1,1,1,1,1]{1,0,2,3,4,5,6,7:T(8,128)(2,1)} reshape(bf16[1536,4,512]{2,1,0:T(4,128)(2,1)} %pad_maximum_fusion) | data formatting | bytes 12582912 | tf_op jit(solution)/shard_map/reshape | solution.py:138
  123.2 9.0 %fusion = f32[2,2,2,2,2,2,16,2048]{7,6,5,4,3,2,1,0:T(8,128)S(1)} fusion(bf16[2,2,2,2,2,2,16,1536]{7,6,5,4,3,2,1,0:T(8,128)(2,1)S(1)} %bitcast.509, bf16[1536,2048,1,1,1,1,1,1]{1,0,2,3,4,5,6,7:T(8,128)(2,1)} %reshape.2073), kind=kOutput, calls=%fused_computation.4 | convolution fusion | flops 6442450944 | bytes 17825792 | tf_op jit(solution)/shard_map/dot_general | solution.py:138
  132.9 1.3 constant_dynamic-slice_fusion.9
  134.8 1.3 constant_dynamic-slice_fusion.14
  136.2 1.2 constant_dynamic-slice_fusion.4
  138.7 1.1 reshape_squeeze.7
  140.6 1.8 reshape_squeeze.6
  142.4 1.4 maximum_bitcast_fusion.8
  143.8 1.1 pad_maximum_fusion.9
  144.9 1.6 dynamic-slice_add_fusion.2
  147.0 1.5 dynamic-slice_add_fusion.1
  149.4 1.6 dynamic-slice_add_fusion
  152.0 11.4 %collective-permute-done.10 = f32[2,2,2,1,1,2,16,640]{7,6,5,4,3,2,1,0:T(8,128)S(1)} collective-permute-done((f32[2,2,2,1,1,2,16,640]{7,6,5,4,3,2,1,0:T(8,128)S(1)}, f32[2,2,2,1,1,2,16,640]{7,6,5,4,3,2,1,0:T(8,128)S(1)}, u32[]{:S(2)}, u32[]{:S(2)}) %collective-permute-start.10) | collective-permute-done | bytes 655392 | tf_op jit(solution)/shard_map/ppermute | solution.py:67
  163.6 1.8 collective-permute-done.15
  165.5 1.2 collective-permute-start.16
  166.7 5.7 %collective-permute-done.11 = f32[2,2,1,1,1,2,16,640]{7,6,5,4,3,2,1,0:T(8,128)S(1)} collective-permute-done((f32[2,2,1,1,1,2,16,640]{7,6,5,4,3,2,1,0:T(8,128)S(1)}, f32[2,2,1,1,1,2,16,640]{7,6,5,4,3,2,1,0:T(8,128)S(1)}, u32[]{:S(2)}, u32[]{:S(2)}) %collective-permute-start.11) | collective-permute-done | bytes 327712 | tf_op jit(solution)/shard_map/ppermute | solution.py:67
  172.5 1.2 collective-permute-start.12
  173.7 5.0 %collective-permute-done.16 = f32[2,2,1,2,1,1,16,640]{7,6,5,4,3,2,1,0:T(8,128)S(1)} collective-permute-done((f32[2,2,1,2,1,1,16,640]{7,6,5,4,3,2,1,0:T(8,128)S(1)}, f32[2,2,1,2,1,1,16,640]{7,6,5,4,3,2,1,0:T(8,128)S(1)}, u32[]{:S(2)}, u32[]{:S(2)}) %collective-permute-start.16) | collective-permute-done | bytes 327712 | tf_op jit(solution)/shard_map/ppermute | solution.py:67
  178.7 1.0 collective-permute-start.17
  179.8 1.2 collective-permute-start.6
  181.1 4.5 %collective-permute-start.13 = (f32[2,1,1,1,1,1,16,640]{7,6,5,4,3,2,1,0:T(8,128)S(1)}, f32[2,1,1,1,1,1,16,640]{7,6,5,4,3,2,1,0:T(8,128)S(1)}, u32[]{:S(2)}, u32[]{:S(2)}) collective-permute-start(f32[2,1,1,1,1,1,16,640]{7,6,5,4,3,2,1,0:T(8,128)S(1)} %constant_dynamic-slice_fusion.5), channel_id=1, source_target_pairs={{0,16},{1,17},{2,18},{3,19},{4,20},{5,21},{6,22},{7,23},{8,24},{9,... | collective-permute-start | bytes 245768 | tf_op jit(solution)/shard_map/ppermute | solution.py:67
  185.9 4.5 %collective-permute-start.18 = (f32[2,1,1,1,1,1,16,640]{7,6,5,4,3,2,1,0:T(8,128)S(1)}, f32[2,1,1,1,1,1,16,640]{7,6,5,4,3,2,1,0:T(8,128)S(1)}, u32[]{:S(2)}, u32[]{:S(2)}) collective-permute-start(f32[2,1,1,1,1,1,16,640]{7,6,5,4,3,2,1,0:T(8,128)S(1)} %constant_dynamic-slice_fusion), channel_id=1, source_target_pairs={{0,16},{1,17},{2,18},{3,19},{4,20},{5,21},{6,22},{7,23},{8,24},{9,... | collective-permute-start | bytes 245768 | tf_op jit(solution)/shard_map/ppermute | solution.py:67
  191.0 2.2 collective-permute-done.18
  193.2 2.5 collective-permute-start.30
  197.0 1.7 collective-permute-done.30
  199.2 1.4 collective-permute-done.26
  200.8 2.4 collective-permute-done.31
  204.8 1.7 collective-permute-done.27
  206.6 1.0 collective-permute-start.28
  207.6 1.0 collective-permute-done.32
  208.7 3.2 %collective-permute-done.7 = f32[2,2,1,1,1,1,16,768]{7,6,5,4,3,2,1,0:T(8,128)S(1)} collective-permute-done((f32[2,2,1,1,1,1,16,768]{7,6,5,4,3,2,1,0:T(8,128)S(1)}, f32[2,2,1,1,1,1,16,768]{7,6,5,4,3,2,1,0:T(8,128)S(1)}, u32[]{:S(2)}, u32[]{:S(2)}) %collective-permute-start.7) | collective-permute-done | bytes 196640 | tf_op jit(solution)/shard_map/ppermute | solution.py:67
  211.9 2.3 collective-permute-start.8
  214.3 1.0 collective-permute-start.33
  215.2 3.1 %collective-permute-done.8 = f32[2,1,1,1,1,1,16,768]{7,6,5,4,3,2,1,0:T(8,128)S(1)} collective-permute-done((f32[2,1,1,1,1,1,16,768]{7,6,5,4,3,2,1,0:T(8,128)S(1)}, f32[2,1,1,1,1,1,16,768]{7,6,5,4,3,2,1,0:T(8,128)S(1)}, u32[]{:S(2)}, u32[]{:S(2)}) %collective-permute-start.8) | collective-permute-done | bytes 98336 | tf_op jit(solution)/shard_map/ppermute | solution.py:67
  218.3 1.6 collective-permute-start.20
  220.5 1.4 collective-permute-start.19
  221.9 2.0 collective-permute-done.20
  224.4 4.2 %collective-permute-done.21 = bf16[2,2,1,1,1,1,16,768]{7,6,5,4,3,2,1,0:T(8,128)(2,1)S(1)} collective-permute-done((bf16[2,2,1,1,1,1,16,768]{7,6,5,4,3,2,1,0:T(8,128)(2,1)S(1)}, bf16[2,2,1,1,1,1,16,768]{7,6,5,4,3,2,1,0:T(8,128)(2,1)S(1)}, u32[]{:S(2)}, u32[]{:S(2)}) %collective-permute-start.21) | collective-permute-done | bytes 98336 | tf_op jit(solution)/shard_map/ppermute | solution.py:76
  229.1 5.3 %collective-permute-done.22 = bf16[2,2,2,1,1,1,16,768]{7,6,5,4,3,2,1,0:T(8,128)(2,1)S(1)} collective-permute-done((bf16[2,2,2,1,1,1,16,768]{7,6,5,4,3,2,1,0:T(8,128)(2,1)S(1)}, bf16[2,2,2,1,1,1,16,768]{7,6,5,4,3,2,1,0:T(8,128)(2,1)S(1)}, u32[]{:S(2)}, u32[]{:S(2)}) %collective-permute-start.22) | collective-permute-done | bytes 196640 | tf_op jit(solution)/shard_map/ppermute | solution.py:76
  236.4 5.9 %collective-permute-done.23 = bf16[2,2,2,2,1,1,16,768]{7,6,5,4,3,2,1,0:T(8,128)(2,1)S(1)} collective-permute-done((bf16[2,2,2,2,1,1,16,768]{7,6,5,4,3,2,1,0:T(8,128)(2,1)S(1)}, bf16[2,2,2,2,1,1,16,768]{7,6,5,4,3,2,1,0:T(8,128)(2,1)S(1)}, u32[]{:S(2)}, u32[]{:S(2)}) %collective-permute-start.23) | collective-permute-done | bytes 393248 | tf_op jit(solution)/shard_map/ppermute | solution.py:76
  244.1 1.0 convolution_convert_fusion.2
  245.1 1.0 convolution_convert_fusion.1
  246.3 1.0 convolution_convert_fusion
  247.6 2.8 %reshape.2044 = bf16[2,64,4,4,512]{4,3,2,1,0:T(4,128)(2,1)} reshape(bf16[512,2048]{1,0:T(8,128)(2,1)S(1)} %pad_maximum_fusion.1) | data formatting | bytes 4194304 | tf_op jit(solution)/shard_map/reshape | solution.py:157
  250.4 2.7 %copy.39 = bf16[2,64,4,4,512]{4,1,3,2,0:T(8,128)(2,1)S(1)} copy(bf16[2,64,4,4,512]{4,3,2,1,0:T(4,128)(2,1)} %reshape.2044) | data formatting | bytes 4194304 | tf_op jit(solution)/shard_map/reshape | solution.py:157
  253.1 2.0 gather_fusion.1
  255.1 1.8 copy.40
  256.9 2.0 gather_fusion.2
  258.9 3.2 %copy.45 = bf16[4,2,4,8,8,512]{5,4,2,3,1,0:T(8,128)(2,1)} copy(bf16[4,2,4,8,8,512]{5,4,3,2,1,0:T(8,128)(2,1)} %bitcast.504) | data formatting | bytes 4194304 | tf_op jit(solution)/shard_map/reshape | solution.py:160
  (280 shorter events, 33.1 us)
Async XLA Ops:
  2.4 66.2 %collective-permute-start = (bf16[2,3,4,1,16,512]{5,4,3,2,1,0:T(8,128)(2,1)}, bf16[2,3,4,1,16,512]{5,4,3,2,1,0:T(8,128)(2,1)S(1)}, u32[]{:S(2)}, u32[]{:S(2)}) collective-permute-start(bf16[2,3,4,1,16,512]{5,4,3,2,1,0:T(8,128)(2,1)} %slice.147), channel_id=1, source_target_pairs={{0,30},{2,0},{4,2},{6,4},{8,6},{10,8},{12,10},{14,12},{16,14},{18,... | collective-permute-start | bytes 1179656 | tf_op jit(solution)/shard_map/ppermute | solution.py:105
  9.9 3.4 %copy-start.17 = (f32[2,2,3,3,4,4,16]{6,5,4,3,2,1,0:T(4,128)S(1)}, f32[2,2,3,3,4,4,16]{6,5,4,3,2,1,0:T(4,128)}, u32[]{:S(2)}) copy-start(f32[2,2,3,3,4,4,16]{6,5,4,3,2,1,0:T(4,128)} %param.6) | copy-start | bytes 110596
  9.9 29.2 %collective-permute-start.1 = (bf16[2,3,4,4,1,512]{5,3,4,2,1,0:T(4,128)(2,1)}, bf16[2,3,4,4,1,512]{5,3,4,2,1,0:T(4,128)(2,1)}, u32[]{:S(2)}, u32[]{:S(2)}) collective-permute-start(bf16[2,3,4,4,1,512]{5,3,4,2,1,0:T(4,128)(2,1)} %copy.43), channel_id=1, source_target_pairs={{0,1},{1,0},{2,3},{3,2},{4,5},{5,4},{6,7},{7,6},{8,9},{9,8},{10,11... | collective-permute-start | bytes 294920 | tf_op jit(solution)/shard_map/ppermute | solution.py:107
  13.9 1.1 copy-start.22
  13.9 1.1 copy-start.28
  13.9 1.1 copy-start.20
  13.9 1.1 copy-start.26
  17.6 65.7 %collective-permute-start.2 = (bf16[2,3,4,1,16,512]{5,4,3,2,1,0:T(8,128)(2,1)}, bf16[2,3,4,1,16,512]{5,4,3,2,1,0:T(8,128)(2,1)}, u32[]{:S(2)}, u32[]{:S(2)}) collective-permute-start(bf16[2,3,4,1,16,512]{5,4,3,2,1,0:T(8,128)(2,1)} %pad_maximum_fusion.14), channel_id=1, source_target_pairs={{0,2},{2,4},{4,6},{6,8},{8,10},{10,12},{12,14},{14,16},{16,18},{18... | collective-permute-start | bytes 1179656 | tf_op jit(solution)/shard_map/ppermute | solution.py:106
  18.3 1.1 copy-start.40
  18.3 1.1 copy-start.42
  18.3 1.1 copy-start.46
  18.3 1.1 copy-start.48
  18.3 1.1 copy-start.32
  18.3 1.1 copy-start.38
  18.3 1.1 copy-start.44
  20.0 2.0 copy-start
  20.1 1.5 copy-start.9
  20.2 1.4 copy-start.11
  21.1 33.8 %collective-permute-start.3 = (bf16[2,3,4,4,1,512]{5,4,3,2,1,0:T(2,128)(2,1)}, bf16[2,3,4,4,1,512]{5,4,3,2,1,0:T(2,128)(2,1)}, u32[]{:S(2)}, u32[]{:S(2)}) collective-permute-start(bf16[2,3,4,4,1,512]{5,4,3,2,1,0:T(2,128)(2,1)} %pad_maximum_fusion.19), channel_id=1, source_target_pairs={{0,1},{1,0},{2,3},{3,2},{4,5},{5,4},{6,7},{7,6},{8,9},{9,8},{10,11... | collective-permute-start | bytes 294920 | tf_op jit(solution)/shard_map/ppermute | solution.py:108
  43.1 11.8 %copy-start.10 = (bf16[1,3,4,4,16,512]{5,4,3,2,1,0:T(8,128)(2,1)S(1)}, bf16[1,3,4,4,16,512]{5,4,3,2,1,0:T(8,128)(2,1)}, u32[]{:S(2)}) copy-start(bf16[1,3,4,4,16,512]{5,4,3,2,1,0:T(8,128)(2,1)} %copy-done.9) | copy-start | bytes 2359300
  43.1 11.8 %copy-start.12 = (bf16[1,3,4,4,16,512]{5,4,3,2,1,0:T(8,128)(2,1)S(1)}, bf16[1,3,4,4,16,512]{5,4,3,2,1,0:T(8,128)(2,1)}, u32[]{:S(2)}) copy-start(bf16[1,3,4,4,16,512]{5,4,3,2,1,0:T(8,128)(2,1)} %copy-done.11) | copy-start | bytes 2359300
  56.6 12.1 %copy-start.13 = (bf16[2,3,4,3,16,512]{5,4,3,2,1,0:T(8,128)(2,1)S(1)}, bf16[2,3,4,3,16,512]{5,4,3,2,1,0:T(8,128)(2,1)}, u32[]{:S(2)}) copy-start(bf16[2,3,4,3,16,512]{5,4,3,2,1,0:T(8,128)(2,1)} %slice.146) | copy-start | bytes 3538948
  71.5 11.8 %copy-start.6 = (bf16[1,3,4,4,16,512]{5,4,3,2,1,0:T(8,128)(2,1)S(1)}, bf16[1,3,4,4,16,512]{5,4,3,2,1,0:T(8,128)(2,1)}, u32[]{:S(2)}) copy-start(bf16[1,3,4,4,16,512]{5,4,3,2,1,0:T(8,128)(2,1)} %copy-done.5) | copy-start | bytes 2359300
  71.5 11.8 %copy-start.8 = (bf16[1,3,4,4,16,512]{5,4,3,2,1,0:T(8,128)(2,1)S(1)}, bf16[1,3,4,4,16,512]{5,4,3,2,1,0:T(8,128)(2,1)}, u32[]{:S(2)}) copy-start(bf16[1,3,4,4,16,512]{5,4,3,2,1,0:T(8,128)(2,1)} %copy-done.7) | copy-start | bytes 2359300
  111.9 11.3 %copy-start.14 = (bf16[1024,1536]{1,0:T(8,128)(2,1)S(1)}, bf16[1024,1536]{1,0:T(8,128)(2,1)}, u32[]{:S(2)}) copy-start(bf16[1024,1536]{1,0:T(8,128)(2,1)} %maximum_maximum_fusion) | copy-start | bytes 9437188
  132.9 1.9 copy-start.3
  132.9 3.3 %copy-start.1 = (f32[2,2,2,2,2,2,16,640]{7,6,5,4,3,2,1,0:T(8,128)}, f32[2,2,2,2,2,2,16,640]{7,6,5,4,3,2,1,0:T(8,128)S(1)}, u32[]{:S(2)}) copy-start(f32[2,2,2,2,2,2,16,640]{7,6,5,4,3,2,1,0:T(8,128)S(1)} %get-tuple-element.3) | copy-start | bytes 7864324
  134.2 10.7 %collective-permute-start.9 = (f32[2,2,2,2,1,2,16,640]{7,6,5,4,3,2,1,0:T(8,128)}, f32[2,2,2,2,1,2,16,640]{7,6,5,4,3,2,1,0:T(8,128)}, u32[]{:S(2)}, u32[]{:S(2)}) collective-permute-start(f32[2,2,2,2,1,2,16,640]{7,6,5,4,3,2,1,0:T(8,128)} %constant_dynamic-slice_fusion.9), channel_id=1, source_target_pairs={{0,2},{1,3},{2,0},{3,1},{4,6},{5,7},{6,4},{7,5},{8,10},{9,11},{10,... | collective-permute-start | bytes 3932168 | tf_op jit(solution)/shard_map/ppermute | solution.py:67
  136.2 1.7 copy-start.16
  136.2 13.3 %collective-permute-start.4 = (f32[2,2,2,2,1,2,16,768]{7,6,5,4,3,2,1,0:T(8,128)}, f32[2,2,2,2,1,2,16,768]{7,6,5,4,3,2,1,0:T(8,128)}, u32[]{:S(2)}, u32[]{:S(2)}) collective-permute-start(f32[2,2,2,2,1,2,16,768]{7,6,5,4,3,2,1,0:T(8,128)} %constant_dynamic-slice_fusion.14), channel_id=1, source_target_pairs={{0,2},{1,3},{2,0},{3,1},{4,6},{5,7},{6,4},{7,5},{8,10},{9,11},{10,... | collective-permute-start | bytes 4718600 | tf_op jit(solution)/shard_map/ppermute | solution.py:67
  136.2 6.2 %copy-start.68 = (s32[4]{0:T(128)S(1)}, s32[4]{0:T(128)}, u32[]{:S(2)}) copy-start(s32[4]{0:T(128)} %param.8) | copy-start | bytes 52
  136.2 6.2 %copy-start.69 = (s32[4]{0:T(128)S(1)}, s32[4]{0:T(128)}, u32[]{:S(2)}) copy-start(s32[4]{0:T(128)} %param.7) | copy-start | bytes 52
  137.4 9.2 %collective-permute-start.14 = (f32[2,2,2,2,1,2,16,640]{7,6,5,4,3,2,1,0:T(8,128)}, f32[2,2,2,2,1,2,16,640]{7,6,5,4,3,2,1,0:T(8,128)}, u32[]{:S(2)}, u32[]{:S(2)}) collective-permute-start(f32[2,2,2,2,1,2,16,640]{7,6,5,4,3,2,1,0:T(8,128)} %constant_dynamic-slice_fusion.4), channel_id=1, source_target_pairs={{0,2},{1,3},{2,0},{3,1},{4,6},{5,7},{6,4},{7,5},{8,10},{9,11},{10,... | collective-permute-start | bytes 3932168 | tf_op jit(solution)/shard_map/ppermute | solution.py:67
  142.4 2.5 copy-start.4
  144.9 2.1 copy-start.2
  146.6 16.8 %collective-permute-start.10 = (f32[2,2,2,1,1,2,16,640]{7,6,5,4,3,2,1,0:T(8,128)S(1)}, f32[2,2,2,1,1,2,16,640]{7,6,5,4,3,2,1,0:T(8,128)S(1)}, u32[]{:S(2)}, u32[]{:S(2)}) collective-permute-start(f32[2,2,2,1,1,2,16,640]{7,6,5,4,3,2,1,0:T(8,128)S(1)} %constant_dynamic-slice_fusion.8), channel_id=1, source_target_pairs={{0,4},{1,5},{2,6},{3,7},{4,0},{5,1},{6,2},{7,3},{8,12},{9,13},{10,... | collective-permute-start | bytes 1966088 | tf_op jit(solution)/shard_map/ppermute | solution.py:67
  148.6 16.8 %collective-permute-start.15 = (f32[2,2,1,2,1,2,16,640]{7,6,5,4,3,2,1,0:T(8,128)S(1)}, f32[2,2,1,2,1,2,16,640]{7,6,5,4,3,2,1,0:T(8,128)S(1)}, u32[]{:S(2)}, u32[]{:S(2)}) collective-permute-start(f32[2,2,1,2,1,2,16,640]{7,6,5,4,3,2,1,0:T(8,128)S(1)} %constant_dynamic-slice_fusion.3), channel_id=1, source_target_pairs={{0,8},{1,9},{2,10},{3,11},{4,12},{5,13},{6,14},{7,15},{8,0},{9,1},... | collective-permute-start | bytes 1966088 | tf_op jit(solution)/shard_map/ppermute | solution.py:67
  151.1 28.6 %collective-permute-start.5 = (f32[2,2,2,2,1,1,16,768]{7,6,5,4,3,2,1,0:T(8,128)S(1)}, f32[2,2,2,2,1,1,16,768]{7,6,5,4,3,2,1,0:T(8,128)S(1)}, u32[]{:S(2)}, u32[]{:S(2)}) collective-permute-start(f32[2,2,2,2,1,1,16,768]{7,6,5,4,3,2,1,0:T(8,128)S(1)} %constant_dynamic-slice_fusion.13), channel_id=1, source_target_pairs={{0,1},{1,0},{2,3},{3,2},{4,5},{5,4},{6,7},{7,6},{8,9},{9,8},{10,11... | collective-permute-start | bytes 2359304 | tf_op jit(solution)/shard_map/ppermute | solution.py:67
  163.5 8.9 %collective-permute-start.11 = (f32[2,2,1,1,1,2,16,640]{7,6,5,4,3,2,1,0:T(8,128)S(1)}, f32[2,2,1,1,1,2,16,640]{7,6,5,4,3,2,1,0:T(8,128)S(1)}, u32[]{:S(2)}, u32[]{:S(2)}) collective-permute-start(f32[2,2,1,1,1,2,16,640]{7,6,5,4,3,2,1,0:T(8,128)S(1)} %constant_dynamic-slice_fusion.7), channel_id=1, source_target_pairs={{0,8},{1,9},{2,10},{3,11},{4,12},{5,13},{6,14},{7,15},{8,0},{9,1},... | collective-permute-start | bytes 983048 | tf_op jit(solution)/shard_map/ppermute | solution.py:67
  165.5 13.2 %collective-permute-start.16 = (f32[2,2,1,2,1,1,16,640]{7,6,5,4,3,2,1,0:T(8,128)S(1)}, f32[2,2,1,2,1,1,16,640]{7,6,5,4,3,2,1,0:T(8,128)S(1)}, u32[]{:S(2)}, u32[]{:S(2)}) collective-permute-start(f32[2,2,1,2,1,1,16,640]{7,6,5,4,3,2,1,0:T(8,128)S(1)} %constant_dynamic-slice_fusion.2), channel_id=1, source_target_pairs={{0,1},{1,0},{2,3},{3,2},{4,5},{5,4},{6,7},{7,6},{8,9},{9,8},{10,11... | collective-permute-start | bytes 983048 | tf_op jit(solution)/shard_map/ppermute | solution.py:67
  172.5 8.6 %collective-permute-start.12 = (f32[2,2,1,1,1,1,16,640]{7,6,5,4,3,2,1,0:T(8,128)S(1)}, f32[2,2,1,1,1,1,16,640]{7,6,5,4,3,2,1,0:T(8,128)S(1)}, u32[]{:S(2)}, u32[]{:S(2)}) collective-permute-start(f32[2,2,1,1,1,1,16,640]{7,6,5,4,3,2,1,0:T(8,128)S(1)} %constant_dynamic-slice_fusion.6), channel_id=1, source_target_pairs={{0,1},{1,0},{2,3},{3,2},{4,5},{5,4},{6,7},{7,6},{8,9},{9,8},{10,11... | collective-permute-start | bytes 491528 | tf_op jit(solution)/shard_map/ppermute | solution.py:67
  178.7 7.1 %collective-permute-start.17 = (f32[2,2,1,1,1,1,16,640]{7,6,5,4,3,2,1,0:T(8,128)S(1)}, f32[2,2,1,1,1,1,16,640]{7,6,5,4,3,2,1,0:T(8,128)S(1)}, u32[]{:S(2)}, u32[]{:S(2)}) collective-permute-start(f32[2,2,1,1,1,1,16,640]{7,6,5,4,3,2,1,0:T(8,128)S(1)} %constant_dynamic-slice_fusion.1), channel_id=1, source_target_pairs={{0,4},{1,5},{2,6},{3,7},{4,0},{5,1},{6,2},{7,3},{8,12},{9,13},{10,... | collective-permute-start | bytes 491528 | tf_op jit(solution)/shard_map/ppermute | solution.py:67
  179.8 24.3 %collective-permute-start.6 = (f32[2,2,2,1,1,1,16,768]{7,6,5,4,3,2,1,0:T(8,128)S(1)}, f32[2,2,2,1,1,1,16,768]{7,6,5,4,3,2,1,0:T(8,128)S(1)}, u32[]{:S(2)}, u32[]{:S(2)}) collective-permute-start(f32[2,2,2,1,1,1,16,768]{7,6,5,4,3,2,1,0:T(8,128)S(1)} %constant_dynamic-slice_fusion.12), channel_id=1, source_target_pairs={{0,4},{1,5},{2,6},{3,7},{4,0},{5,1},{6,2},{7,3},{8,12},{9,13},{10,... | collective-permute-start | bytes 1179656 | tf_op jit(solution)/shard_map/ppermute | solution.py:67
  181.1 9.7 %collective-permute-start.13 = (f32[2,1,1,1,1,1,16,640]{7,6,5,4,3,2,1,0:T(8,128)S(1)}, f32[2,1,1,1,1,1,16,640]{7,6,5,4,3,2,1,0:T(8,128)S(1)}, u32[]{:S(2)}, u32[]{:S(2)}) collective-permute-start(f32[2,1,1,1,1,1,16,640]{7,6,5,4,3,2,1,0:T(8,128)S(1)} %constant_dynamic-slice_fusion.5), channel_id=1, source_target_pairs={{0,16},{1,17},{2,18},{3,19},{4,20},{5,21},{6,22},{7,23},{8,24},{9,... | collective-permute-start | bytes 245768 | tf_op jit(solution)/shard_map/ppermute | solution.py:67
  185.9 7.3 %collective-permute-start.18 = (f32[2,1,1,1,1,1,16,640]{7,6,5,4,3,2,1,0:T(8,128)S(1)}, f32[2,1,1,1,1,1,16,640]{7,6,5,4,3,2,1,0:T(8,128)S(1)}, u32[]{:S(2)}, u32[]{:S(2)}) collective-permute-start(f32[2,1,1,1,1,1,16,640]{7,6,5,4,3,2,1,0:T(8,128)S(1)} %constant_dynamic-slice_fusion), channel_id=1, source_target_pairs={{0,16},{1,17},{2,18},{3,19},{4,20},{5,21},{6,22},{7,23},{8,24},{9,... | collective-permute-start | bytes 245768 | tf_op jit(solution)/shard_map/ppermute | solution.py:67
  190.8 5.3 %collective-permute-start.25 = (bf16[2,1,1,1,1,1,16,640]{7,6,5,4,3,2,1,0:T(8,128)(2,1)S(1)}, bf16[2,1,1,1,1,1,16,640]{7,6,5,4,3,2,1,0:T(8,128)(2,1)S(1)}, u32[]{:S(2)}, u32[]{:S(2)}) collective-permute-start(bf16[2,1,1,1,1,1,16,640]{7,6,5,4,3,2,1,0:T(8,128)(2,1)S(1)} %get-tuple-element.58), channel_id=1, source_target_pairs={{0,16},{1,17},{2,18},{3,19},{4,20},{5,21},{6,22},{7,23},{8,24},{9,... | collective-permute-start | bytes 122888 | tf_op jit(solution)/shard_map/ppermute | solution.py:76
  193.2 5.4 %collective-permute-start.30 = (bf16[2,1,1,1,1,1,16,640]{7,6,5,4,3,2,1,0:T(8,128)(2,1)S(1)}, bf16[2,1,1,1,1,1,16,640]{7,6,5,4,3,2,1,0:T(8,128)(2,1)S(1)}, u32[]{:S(2)}, u32[]{:S(2)}) collective-permute-start(bf16[2,1,1,1,1,1,16,640]{7,6,5,4,3,2,1,0:T(8,128)(2,1)S(1)} %get-tuple-element.60), channel_id=1, source_target_pairs={{0,16},{1,17},{2,18},{3,19},{4,20},{5,21},{6,22},{7,23},{8,24},{9,... | collective-permute-start | bytes 122888 | tf_op jit(solution)/shard_map/ppermute | solution.py:76
  196.1 4.5 %collective-permute-start.26 = (bf16[2,2,1,1,1,1,16,640]{7,6,5,4,3,2,1,0:T(8,128)(2,1)S(1)}, bf16[2,2,1,1,1,1,16,640]{7,6,5,4,3,2,1,0:T(8,128)(2,1)S(1)}, u32[]{:S(2)}, u32[]{:S(2)}) collective-permute-start(bf16[2,2,1,1,1,1,16,640]{7,6,5,4,3,2,1,0:T(8,128)(2,1)S(1)} %pad_maximum_fusion.24), channel_id=1, source_target_pairs={{0,1},{1,0},{2,3},{3,2},{4,5},{5,4},{6,7},{7,6},{8,9},{9,8},{10,11... | collective-permute-start | bytes 245768 | tf_op jit(solution)/shard_map/ppermute | solution.py:76
  198.7 4.5 %collective-permute-start.31 = (bf16[2,2,1,1,1,1,16,640]{7,6,5,4,3,2,1,0:T(8,128)(2,1)S(1)}, bf16[2,2,1,1,1,1,16,640]{7,6,5,4,3,2,1,0:T(8,128)(2,1)S(1)}, u32[]{:S(2)}, u32[]{:S(2)}) collective-permute-start(bf16[2,2,1,1,1,1,16,640]{7,6,5,4,3,2,1,0:T(8,128)(2,1)S(1)} %pad_maximum_fusion.25), channel_id=1, source_target_pairs={{0,4},{1,5},{2,6},{3,7},{4,0},{5,1},{6,2},{7,3},{8,12},{9,13},{10,... | collective-permute-start | bytes 245768 | tf_op jit(solution)/shard_map/ppermute | solution.py:76
  200.6 5.9 %collective-permute-start.27 = (bf16[2,2,1,1,1,2,16,640]{7,6,5,4,3,2,1,0:T(8,128)(2,1)S(1)}, bf16[2,2,1,1,1,2,16,640]{7,6,5,4,3,2,1,0:T(8,128)(2,1)S(1)}, u32[]{:S(2)}, u32[]{:S(2)}) collective-permute-start(bf16[2,2,1,1,1,2,16,640]{7,6,5,4,3,2,1,0:T(8,128)(2,1)S(1)} %pad_maximum_fusion.21), channel_id=1, source_target_pairs={{0,8},{1,9},{2,10},{3,11},{4,12},{5,13},{6,14},{7,15},{8,0},{9,1},... | collective-permute-start | bytes 491528 | tf_op jit(solution)/shard_map/ppermute | solution.py:76
  203.3 5.4 %collective-permute-start.32 = (bf16[2,2,1,2,1,1,16,640]{7,6,5,4,3,2,1,0:T(8,128)(2,1)S(1)}, bf16[2,2,1,2,1,1,16,640]{7,6,5,4,3,2,1,0:T(8,128)(2,1)S(1)}, u32[]{:S(2)}, u32[]{:S(2)}) collective-permute-start(bf16[2,2,1,2,1,1,16,640]{7,6,5,4,3,2,1,0:T(8,128)(2,1)S(1)} %pad_maximum_fusion.22), channel_id=1, source_target_pairs={{0,1},{1,0},{2,3},{3,2},{4,5},{5,4},{6,7},{7,6},{8,9},{9,8},{10,11... | collective-permute-start | bytes 491528 | tf_op jit(solution)/shard_map/ppermute | solution.py:76
  204.3 7.6 %collective-permute-start.7 = (f32[2,2,1,1,1,1,16,768]{7,6,5,4,3,2,1,0:T(8,128)S(1)}, f32[2,2,1,1,1,1,16,768]{7,6,5,4,3,2,1,0:T(8,128)S(1)}, u32[]{:S(2)}, u32[]{:S(2)}) collective-permute-start(f32[2,2,1,1,1,1,16,768]{7,6,5,4,3,2,1,0:T(8,128)S(1)} %constant_dynamic-slice_fusion.11), channel_id=1, source_target_pairs={{0,8},{1,9},{2,10},{3,11},{4,12},{5,13},{6,14},{7,15},{8,0},{9,1},... | collective-permute-start | bytes 589832 | tf_op jit(solution)/shard_map/ppermute | solution.py:67
  206.6 17.5 %collective-permute-start.28 = (bf16[2,2,2,1,1,2,16,640]{7,6,5,4,3,2,1,0:T(8,128)(2,1)S(1)}, bf16[2,2,2,1,1,2,16,640]{7,6,5,4,3,2,1,0:T(8,128)(2,1)S(1)}, u32[]{:S(2)}, u32[]{:S(2)}) collective-permute-start(bf16[2,2,2,1,1,2,16,640]{7,6,5,4,3,2,1,0:T(8,128)(2,1)S(1)} %pad_maximum_fusion.16), channel_id=1, source_target_pairs={{0,4},{1,5},{2,6},{3,7},{4,0},{5,1},{6,2},{7,3},{8,12},{9,13},{10,... | collective-permute-start | bytes 983048 | tf_op jit(solution)/shard_map/ppermute | solution.py:76
  211.9 6.4 %collective-permute-start.8 = (f32[2,1,1,1,1,1,16,768]{7,6,5,4,3,2,1,0:T(8,128)S(1)}, f32[2,1,1,1,1,1,16,768]{7,6,5,4,3,2,1,0:T(8,128)S(1)}, u32[]{:S(2)}, u32[]{:S(2)}) collective-permute-start(f32[2,1,1,1,1,1,16,768]{7,6,5,4,3,2,1,0:T(8,128)S(1)} %constant_dynamic-slice_fusion.10), channel_id=1, source_target_pairs={{0,16},{1,17},{2,18},{3,19},{4,20},{5,21},{6,22},{7,23},{8,24},{9,... | collective-permute-start | bytes 294920 | tf_op jit(solution)/shard_map/ppermute | solution.py:67
  214.3 14.8 %collective-permute-start.33 = (bf16[2,2,1,2,1,2,16,640]{7,6,5,4,3,2,1,0:T(8,128)(2,1)S(1)}, bf16[2,2,1,2,1,2,16,640]{7,6,5,4,3,2,1,0:T(8,128)(2,1)S(1)}, u32[]{:S(2)}, u32[]{:S(2)}) collective-permute-start(bf16[2,2,1,2,1,2,16,640]{7,6,5,4,3,2,1,0:T(8,128)(2,1)S(1)} %pad_maximum_fusion.17), channel_id=1, source_target_pairs={{0,8},{1,9},{2,10},{3,11},{4,12},{5,13},{6,14},{7,15},{8,0},{9,1},... | collective-permute-start | bytes 983048 | tf_op jit(solution)/shard_map/ppermute | solution.py:76
  218.3 5.6 %collective-permute-start.20 = (bf16[2,1,1,1,1,1,16,768]{7,6,5,4,3,2,1,0:T(8,128)(2,1)S(1)}, bf16[2,1,1,1,1,1,16,768]{7,6,5,4,3,2,1,0:T(8,128)(2,1)S(1)}, u32[]{:S(2)}, u32[]{:S(2)}) collective-permute-start(bf16[2,1,1,1,1,1,16,768]{7,6,5,4,3,2,1,0:T(8,128)(2,1)S(1)} %get-tuple-element.52), channel_id=1, source_target_pairs={{0,16},{1,17},{2,18},{3,19},{4,20},{5,21},{6,22},{7,23},{8,24},{9,... | collective-permute-start | bytes 147464 | tf_op jit(solution)/shard_map/ppermute | solution.py:76
  220.5 14.9 %collective-permute-start.19 = (f32[4,2,1,1,1,1,1,16,512]{8,7,1,0,6,5,4,3,2:T(8,128)S(1)}, f32[4,2,1,1,1,1,1,16,512]{8,7,1,0,6,5,4,3,2:T(8,128)S(1)}, u32[]{:S(2)}, u32[]{:S(2)}) collective-permute-start(f32[4,2,1,1,1,1,1,16,512]{8,7,1,0,6,5,4,3,2:T(8,128)S(1)} %bitcast.519), channel_id=1, source_target_pairs={{0,1},{1,0},{2,3},{3,2},{4,5},{5,4},{6,7},{7,6},{8,9},{9,8},{10,11... | collective-permute-start | bytes 786440 | tf_op jit(solution)/shard_map/ppermute | solution.py:76
  223.9 4.7 %collective-permute-start.21 = (bf16[2,2,1,1,1,1,16,768]{7,6,5,4,3,2,1,0:T(8,128)(2,1)S(1)}, bf16[2,2,1,1,1,1,16,768]{7,6,5,4,3,2,1,0:T(8,128)(2,1)S(1)}, u32[]{:S(2)}, u32[]{:S(2)}) collective-permute-start(bf16[2,2,1,1,1,1,16,768]{7,6,5,4,3,2,1,0:T(8,128)(2,1)S(1)} %pad_maximum_fusion.23), channel_id=1, source_target_pairs={{0,8},{1,9},{2,10},{3,11},{4,12},{5,13},{6,14},{7,15},{8,0},{9,1},... | collective-permute-start | bytes 294920 | tf_op jit(solution)/shard_map/ppermute | solution.py:76
  224.3 18.2 %collective-permute-start.29 = (bf16[2,2,2,2,1,2,16,640]{7,6,5,4,3,2,1,0:T(8,128)(2,1)S(1)}, bf16[2,2,2,2,1,2,16,640]{7,6,5,4,3,2,1,0:T(8,128)(2,1)S(1)}, u32[]{:S(2)}, u32[]{:S(2)}) collective-permute-start(bf16[2,2,2,2,1,2,16,640]{7,6,5,4,3,2,1,0:T(8,128)(2,1)S(1)} %pad_maximum_fusion.11), channel_id=1, source_target_pairs={{0,2},{1,3},{2,0},{3,1},{4,6},{5,7},{6,4},{7,5},{8,10},{9,11},{10,... | collective-permute-start | bytes 1966088 | tf_op jit(solution)/shard_map/ppermute | solution.py:76
  228.7 5.7 %collective-permute-start.22 = (bf16[2,2,2,1,1,1,16,768]{7,6,5,4,3,2,1,0:T(8,128)(2,1)S(1)}, bf16[2,2,2,1,1,1,16,768]{7,6,5,4,3,2,1,0:T(8,128)(2,1)S(1)}, u32[]{:S(2)}, u32[]{:S(2)}) collective-permute-start(bf16[2,2,2,1,1,1,16,768]{7,6,5,4,3,2,1,0:T(8,128)(2,1)S(1)} %pad_maximum_fusion.20), channel_id=1, source_target_pairs={{0,4},{1,5},{2,6},{3,7},{4,0},{5,1},{6,2},{7,3},{8,12},{9,13},{10,... | collective-permute-start | bytes 589832 | tf_op jit(solution)/shard_map/ppermute | solution.py:76
  234.5 7.8 %collective-permute-start.23 = (bf16[2,2,2,2,1,1,16,768]{7,6,5,4,3,2,1,0:T(8,128)(2,1)S(1)}, bf16[2,2,2,2,1,1,16,768]{7,6,5,4,3,2,1,0:T(8,128)(2,1)S(1)}, u32[]{:S(2)}, u32[]{:S(2)}) collective-permute-start(bf16[2,2,2,2,1,1,16,768]{7,6,5,4,3,2,1,0:T(8,128)(2,1)S(1)} %pad_maximum_fusion.15), channel_id=1, source_target_pairs={{0,1},{1,0},{2,3},{3,2},{4,5},{5,4},{6,7},{7,6},{8,9},{9,8},{10,11... | collective-permute-start | bytes 1179656 | tf_op jit(solution)/shard_map/ppermute | solution.py:76
  235.4 7.3 %collective-permute-start.34 = (bf16[2,2,2,2,1,2,16,640]{7,6,5,4,3,2,1,0:T(8,128)(2,1)S(1)}, bf16[2,2,2,2,1,2,16,640]{7,6,5,4,3,2,1,0:T(8,128)(2,1)S(1)}, u32[]{:S(2)}, u32[]{:S(2)}) collective-permute-start(bf16[2,2,2,2,1,2,16,640]{7,6,5,4,3,2,1,0:T(8,128)(2,1)S(1)} %pad_maximum_fusion.12), channel_id=1, source_target_pairs={{0,2},{1,3},{2,0},{3,1},{4,6},{5,7},{6,4},{7,5},{8,10},{9,11},{10,... | collective-permute-start | bytes 1966088 | tf_op jit(solution)/shard_map/ppermute | solution.py:76
  242.5 3.6 %collective-permute-start.24 = (bf16[2,2,2,2,1,2,16,768]{7,6,5,4,3,2,1,0:T(8,128)(2,1)S(1)}, bf16[2,2,2,2,1,2,16,768]{7,6,5,4,3,2,1,0:T(8,128)(2,1)S(1)}, u32[]{:S(2)}, u32[]{:S(2)}) collective-permute-start(bf16[2,2,2,2,1,2,16,768]{7,6,5,4,3,2,1,0:T(8,128)(2,1)S(1)} %pad_maximum_fusion.10), channel_id=1, source_target_pairs={{0,2},{1,3},{2,0},{3,1},{4,6},{5,7},{6,4},{7,5},{8,10},{9,11},{10,... | collective-permute-start | bytes 2359304 | tf_op jit(solution)/shard_map/ppermute | solution.py:76
  242.9 1.2 copy-start.15
  (41 other events, 32.5 us)

commit v4 on v1

--- a/solution.py
+++ b/solution.py
@@ -116,13 +116,19 @@
 
         prows = perambulator.shape[1]
         nspin = perambulator.shape[2] // nev
-        p_re = perambulator[0].reshape(prows * nspin, nev)
-        p_im = perambulator[1].reshape(prows * nspin, nev)
-        lhs = jnp.stack(
-            [jnp.concatenate([p_re, -p_im], -1), jnp.concatenate([p_im, p_re], -1)], 0
-        ).reshape(2, prows, nspin, 2 * nev)
-        lhs = jnp.take(lhs, spin_map, axis=2).reshape(2 * prows * nspin, 2 * nev)
 
+        def contraction_lhs(peram):
+            chosen = jnp.stack(
+                [lax.dynamic_slice_in_dim(peram, spin_map[u] * nev, nev, axis=2) for u in range(nspin)],
+                axis=2,
+            )
+            p_re = chosen[0].reshape(prows * nspin, nev)
+            p_im = chosen[1].reshape(prows * nspin, nev)
+            return jnp.stack(
+                [jnp.concatenate([p_re, -p_im], -1), jnp.concatenate([p_im, p_re], -1)], 0
+            ).reshape(2 * prows * nspin, 2 * nev)
+
+        lhs = None
         own = []
         products = []
         for d, field in enumerate(disp):
@@ -132,18 +138,21 @@
             part = reduce_scatter(buf, order, nbits, count, 1).reshape(2, rows, nev)
             part = part * norm_factor
             own.append(part)
+            if lhs is None:
+                peram, _ = lax.optimization_barrier((perambulator, part))
+                lhs = contraction_lhs(peram)
             blk = part.astype(jnp.bfloat16).reshape([2] + [1] * nbits + [rows, nev])
             rhs = all_gather(blk, list(reversed(order)), nbits, count, 1).reshape(2 * nev, nev)
             product = jnp.dot(lhs, rhs, preferred_element_type=jnp.float32)
             products.append(product.astype(jnp.bfloat16).reshape(2, prows, nspin * nev))
-        own = jnp.take(jnp.stack(own, 0), directions, axis=0)
+        own = jnp.take(jnp.stack(own, 0), directions, axis=0, mode="clip")
         ndisp = own.shape[0]
         gy_bits = [b for b in range(nbits) if (1 << b) < ny]
         grown = all_gather(
             own.reshape([ndisp, 2] + [1] * nbits + [rows, nev]), gy_bits, nbits, count, 2
         )
         elem = grown.reshape(ndisp, 2, ny * rows, nev)
-        contracted = jnp.take(jnp.stack(products, 0), directions, axis=0)
+        contracted = jnp.take(jnp.stack(products, 0), directions, axis=0, mode="clip")
         return (elem, contracted)
 
     return local

time: 159 us -> 165 us (1.038)
  other arithmetic: 35 us -> 41.2 us
  starting transfers between devices: 41.7 us -> 37 us
  waiting for transfers between devices: 40.8 us -> 44.4 us
  between operations: 2.34 us -> 4.92 us
  local copies, waits for them, and re-layouts: 27.7 us -> 25.4 us
    concatenate x1, other arithmetic: 2.18 us -> 13.2 us  [local(): jnp.concatenate([jnp.concatenate([turned[0], turned[1]], axis=1), jnp.con...]
    select_n x5 -> x0, other arithmetic: 6.49 us -> none  [the longest x1 3.17 us: local(): contracted = jnp.take(jnp.stack(products, 0), directions, axis=0)]
    ppermute x21, starting transfers between devices: 21.8 us -> 17 us  [all_gather(): other = lax.ppermute(buf, ALL, xor_pairs(count, b))]
    ppermute x21, waiting for transfers between devices: 12 us -> 14.7 us  [all_gather(): other = lax.ppermute(buf, ALL, xor_pairs(count, b))]
    another operation x15 -> x17, other arithmetic: 7.65 us -> 10 us
    gather x3 -> x2, local copies, waits for them, and re-layouts: 4.54 us -> 2.56 us  [the longest x1 2 us: local(): jnp.take(jnp.stack(products, 0), directions, axis=0, mode='clip')]
    select_n x2 -> x0, local copies, waits for them, and re-layouts: 1.95 us -> none  [local(): lhs = jnp.take(lhs, spin_map, axis=2).reshape(2 * prows * nspin, 2 * nev)]
    another operation x5 -> x7, local copies, waits for them, and re-layouts: 3.94 us -> 5.87 us  [the longest x4 3.9 us: local(): jnp.stack(products, 0)]
  transfers between devices with their start and end apart: 45 -> 45, of which waited for: 18 -> 22; matrix products, arithmetic and copies ran while one was open for 33% -> 36% of each run, Pallas kernels for 0% -> 0%
where the time goes in v4:
time: 165 us; the launch traced here: 164 us
  waiting for transfers between devices  44.4 us (27%)
  other arithmetic  41.2 us (25%)
  starting transfers between devices  37 us (22%)
  local copies, waits for them, and re-layouts  25.4 us (15%)
  matrix products  10.8 us (7%)
  between operations  4.92 us (3%)
    ppermute x20, waiting for transfers between devices, reduce_scatter(): buf = keep + lax.ppermute(send, ALL, xor_pairs(count, b))  29.7 us
    ppermute x21, starting transfers between devices, all_gather(): other = lax.ppermute(buf, ALL, xor_pairs(count, b))  17 us
    ppermute x21, waiting for transfers between devices, all_gather(): other = lax.ppermute(buf, ALL, xor_pairs(count, b))  14.7 us
    concatenate x1, other arithmetic, local(): jnp.concatenate([jnp.concatenate([turned[0], turned[1]], axis=1), jnp.con...  13.2 us
    ppermute x20, starting transfers between devices, reduce_scatter(): buf = keep + lax.ppermute(send, ALL, xor_pairs(count, b))  13 us
    dot_general x4, matrix products, local(): jnp.dot(left, field.reshape(2 * depth, nev), preferred_element_type=jnp.f...  7.12 us
    another operation x12, other arithmetic  6.05 us
    unnamed x121, local copies, waits for them, and re-layouts  5.94 us
  transfers between devices with their start and end apart: 45, of which 22 were waited for; matrix products, arithmetic and copies ran while one was open for 36% of the time, Pallas kernels for 0%

profile of v4, /device:TPU:0, one launch (start us, length us, event | category | flops | bytes accessed | tf_op | source)
XLA Modules:
  0.0 163.7 jit_solution(7154398687543717824)
XLA Ops:
  0.6 1.0 slice_bitcast_fusion.21
  2.4 1.9 %convert_element_type.66 = f32[2,3,4,4,16,512]{5,4,3,2,1,0:T(8,128)S(1)} convert(bf16[2,3,4,4,16,512]{5,4,3,2,1,0:T(8,128)(2,1)} %param.5) | non-fusion elementwise | flops 786432 | bytes 4718592 | tf_op jit(solution)/shard_map/convert_element_type | solution.py:13
  6.8 1.0 pad_maximum_fusion.22
  7.8 3.0 %collective-permute-start.18 = (bf16[2,3,4,4,1,512]{5,4,3,2,1,0:T(2,128)(2,1)}, bf16[2,3,4,4,1,512]{5,4,3,2,1,0:T(2,128)(2,1)}, u32[]{:S(2)}, u32[]{:S(2)}) collective-permute-start(bf16[2,3,4,4,1,512]{5,4,3,2,1,0:T(2,128)(2,1)} %pad_maximum_fusion.22), channel_id=1, source_target_pairs={{0,1},{1,0},{2,3},{3,2},{4,5},{5,4},{6,7},{7,6},{8,9},{9,8},{10,11... | collective-permute-start | bytes 294920 | tf_op jit(solution)/shard_map/ppermute | solution.py:97
  14.1 1.2 copy-done
  16.4 4.0 %collective-permute-start = (bf16[2,3,4,1,16,512]{5,4,3,2,1,0:T(8,128)(2,1)}, bf16[2,3,4,1,16,512]{5,4,3,2,1,0:T(8,128)(2,1)}, u32[]{:S(2)}, u32[]{:S(2)}) collective-permute-start(bf16[2,3,4,1,16,512]{5,4,3,2,1,0:T(8,128)(2,1)} %slice.149), channel_id=1, source_target_pairs={{0,30},{2,0},{4,2},{6,4},{8,6},{10,8},{12,10},{14,12},{16,14},{18,... | collective-permute-start | bytes 1179656 | tf_op jit(solution)/shard_map/ppermute | solution.py:94
  21.1 1.2 slice_bitcast_fusion
  22.3 1.0 fusion.31
  24.0 1.1 slice.148
  28.4 1.1 dynamic-slice_bitcast_fusion.3
  31.7 1.4 maximum_bitcast_fusion.8
  33.1 1.1 pad_maximum_fusion.5
  34.2 13.2 %maximum_maximum_fusion = bf16[1024,1536]{1,0:T(8,128)(2,1)S(1)} fusion(bf16[512,768]{1,0:T(8,128)(2,1)S(1)} %copy-done.12, bf16[512,768]{1,0:T(8,128)(2,1)S(1)} %copy-done.10, bf16[512,768]{1,0:T(8,128)(2,1)S(1)} %copy-done.11), kind=kLoop, calls=%fused_computation.2 | loop fusion | flops 12582912 | bytes 5505024 | tf_op jit(solution)/shard_map/concatenate | solution.py:108
  47.5 1.7 %fusion.4 = bf16[2,3,4,4,16,512]{5,4,3,2,1,0:T(8,128)(2,1)S(1)} fusion(bf16[1,3,4,4,16,512]{5,4,3,2,1,0:T(8,128)(2,1)S(1)} %copy-done.6, bf16[1,3,4,4,16,512]{5,4,3,2,1,0:T(8,128)(2,1)S(1)} %copy-done.8, bf16[2,3,4,4,1,512]{5,4,3,2,1,0:T(2,128)(2,1)} %collective-permute-done.18), kind=kLoop, calls=%fused_computation.9 | loop fusion | flops 4718592 | bytes 3244032 | tf_op jit(solution)/shard_map/concatenate | solution.py:104
  49.2 1.8 %fusion = f32[2,2,2,2,2,2,16,512]{7,6,0,5,4,3,2,1:T(8,128)S(1)} fusion(bf16[1536,512,1,1,1,1,1,1]{1,0,2,7,6,5,4,3:T(8,128)(2,1)S(1)} %bitcast.554, bf16[2,2,2,2,2,2,16,1536]{7,6,5,4,3,2,1,0:T(8,128)(2,1)S(1)} %bitcast.549), kind=kOutput, calls=%fused_computation.3 | convolution fusion | flops 1610612736 | bytes 6815744 | tf_op jit(solution)/shard_map/dot_general | solution.py:136
  51.2 1.1 copy.52
  55.2 1.8 %fusion.2 = f32[2,2,2,2,2,2,16,512]{7,6,0,5,4,3,2,1:T(8,128)S(1)} fusion(bf16[1536,512,1,1,1,1,1,1]{1,0,2,7,6,5,4,3:T(8,128)(2,1)S(1)} %bitcast.556, bf16[2,2,2,2,2,2,16,1536]{7,6,5,4,3,2,1,0:T(8,128)(2,1)S(1)} %bitcast.550), kind=kOutput, calls=%fused_computation.5 | convolution fusion | flops 1610612736 | bytes 6815744 | tf_op jit(solution)/shard_map/dot_general | solution.py:136
  58.3 1.2 fusion.5
  59.5 1.8 %fusion.35 = f32[2,2,2,2,2,2,16,512]{7,6,5,4,3,2,1,0:T(8,128)S(1)} fusion(bf16[2,2,2,2,2,2,16,1536]{7,6,5,4,3,2,1,0:T(8,128)(2,1)S(1)} %bitcast.551, bf16[1536,512,1,1,1,1,1,1]{1,0,7,6,5,4,3,2:T(8,128)(2,1)S(1)} %bitcast.553), kind=kOutput, calls=%fused_computation.255 | convolution fusion | flops 1610612736 | bytes 6815744 | tf_op jit(solution)/shard_map/dot_general | solution.py:136
  62.6 1.2 maximum_convert_fusion
  66.0 1.8 %fusion.34 = f32[2,2,2,2,2,2,16,512]{7,6,5,4,3,2,1,0:T(8,128)S(1)} fusion(bf16[2,2,2,2,2,2,16,1536]{7,6,5,4,3,2,1,0:T(8,128)(2,1)S(1)} %bitcast.552, bf16[1536,512,1,1,1,1,1,1]{1,0,7,6,5,4,3,2:T(8,128)(2,1)S(1)} %bitcast.555), kind=kOutput, calls=%fused_computation.254 | convolution fusion | flops 1610612736 | bytes 6815744 | tf_op jit(solution)/shard_map/dot_general | solution.py:136
  68.7 1.6 collective-permute-start.20
  71.3 1.3 collective-permute-start.2
  72.6 11.0 %collective-permute-done.20 = f32[2,2,2,2,1,1,16,512]{7,6,0,5,4,3,2,1:T(8,128)S(1)} collective-permute-done((f32[2,2,2,2,1,1,16,512]{7,6,0,5,4,3,2,1:T(8,128)S(1)}, f32[2,2,2,2,1,1,16,512]{7,6,0,5,4,3,2,1:T(8,128)S(1)}, u32[]{:S(2)}, u32[]{:S(2)}) %collective-permute-start.20) | collective-permute-done | bytes 524320 | tf_op jit(solution)/shard_map/ppermute | solution.py:67
  84.4 5.8 %collective-permute-done.21 = f32[2,2,2,1,1,1,16,512]{7,6,0,5,4,3,2,1:T(8,128)S(1)} collective-permute-done((f32[2,2,2,1,1,1,16,512]{7,6,0,5,4,3,2,1:T(8,128)S(1)}, f32[2,2,2,1,1,1,16,512]{7,6,0,5,4,3,2,1:T(8,128)S(1)}, u32[]{:S(2)}, u32[]{:S(2)}) %collective-permute-start.21) | collective-permute-done | bytes 262176 | tf_op jit(solution)/shard_map/ppermute | solution.py:67
  90.4 2.3 %collective-permute-done.9 = f32[2,2,1,1,1,2,16,512]{7,6,0,5,4,3,2,1:T(8,128)S(1)} collective-permute-done((f32[2,2,1,1,1,2,16,512]{7,6,0,5,4,3,2,1:T(8,128)S(1)}, f32[2,2,1,1,1,2,16,512]{7,6,0,5,4,3,2,1:T(8,128)S(1)}, u32[]{:S(2)}, u32[]{:S(2)}) %collective-permute-start.9) | collective-permute-done | bytes 262176 | tf_op jit(solution)/shard_map/ppermute | solution.py:67
  92.9 2.1 %collective-permute-start.15 = (f32[2,2,1,2,1,1,16,512]{7,6,5,4,3,2,1,0:T(8,128)S(1)}, f32[2,2,1,2,1,1,16,512]{7,6,5,4,3,2,1,0:T(8,128)S(1)}, u32[]{:S(2)}, u32[]{:S(2)}) collective-permute-start(f32[2,2,1,2,1,1,16,512]{7,6,5,4,3,2,1,0:T(8,128)S(1)} %constant_dynamic-slice_fusion.7), channel_id=1, source_target_pairs={{0,1},{1,0},{2,3},{3,2},{4,5},{5,4},{6,7},{7,6},{8,9},{9,8},{10,11... | collective-permute-start | bytes 786440 | tf_op jit(solution)/shard_map/ppermute | solution.py:67
  95.2 1.2 collective-permute-start.3
  96.5 2.7 %collective-permute-done.10 = f32[2,2,1,1,1,1,16,512]{7,6,0,5,4,3,2,1:T(8,128)S(1)} collective-permute-done((f32[2,2,1,1,1,1,16,512]{7,6,0,5,4,3,2,1:T(8,128)S(1)}, f32[2,2,1,1,1,1,16,512]{7,6,0,5,4,3,2,1:T(8,128)S(1)}, u32[]{:S(2)}, u32[]{:S(2)}) %collective-permute-start.10) | collective-permute-done | bytes 131104 | tf_op jit(solution)/shard_map/ppermute | solution.py:67
  99.6 2.8 %collective-permute-done.23 = f32[2,1,1,1,1,1,16,512]{7,6,0,5,4,3,2,1:T(8,128)S(1)} collective-permute-done((f32[2,1,1,1,1,1,16,512]{7,6,0,5,4,3,2,1:T(8,128)S(1)}, f32[2,1,1,1,1,1,16,512]{7,6,0,5,4,3,2,1:T(8,128)S(1)}, u32[]{:S(2)}, u32[]{:S(2)}) %collective-permute-start.23) | collective-permute-done | bytes 65568 | tf_op jit(solution)/shard_map/ppermute | solution.py:67
  102.5 2.4 %collective-permute-done.11 = f32[2,1,1,1,1,1,16,512]{7,6,0,5,4,3,2,1:T(8,128)S(1)} collective-permute-done((f32[2,1,1,1,1,1,16,512]{7,6,0,5,4,3,2,1:T(8,128)S(1)}, f32[2,1,1,1,1,1,16,512]{7,6,0,5,4,3,2,1:T(8,128)S(1)}, u32[]{:S(2)}, u32[]{:S(2)}) %collective-permute-start.11) | collective-permute-done | bytes 65568 | tf_op jit(solution)/shard_map/ppermute | solution.py:67
  105.5 1.8 %collective-permute-done.40 = bf16[2,1,1,1,1,1,16,512]{7,6,5,4,3,2,1,0:T(8,128)(2,1)S(1)} collective-permute-done((bf16[2,1,1,1,1,1,16,512]{7,6,5,4,3,2,1,0:T(8,128)(2,1)S(1)}, bf16[2,1,1,1,1,1,16,512]{7,6,5,4,3,2,1,0:T(8,128)(2,1)S(1)}, u32[]{:S(2)}, u32[]{:S(2)}) %collective-permute-start.40) | collective-permute-done | bytes 32800 | tf_op jit(solution)/shard_map/ppermute | solution.py:76
  107.8 2.0 %collective-permute-done.30 = bf16[2,1,1,1,1,1,16,512]{7,6,0,5,4,3,2,1:T(8,128)(2,1)S(1)} collective-permute-done((bf16[2,1,1,1,1,1,16,512]{7,6,0,5,4,3,2,1:T(8,128)(2,1)S(1)}, bf16[2,1,1,1,1,1,16,512]{7,6,0,5,4,3,2,1:T(8,128)(2,1)S(1)}, u32[]{:S(2)}, u32[]{:S(2)}) %collective-permute-start.30) | collective-permute-done | bytes 32800 | tf_op jit(solution)/shard_map/ppermute | solution.py:76
  109.9 1.1 collective-permute-start.31
  111.0 1.3 collective-permute-start.16
  112.5 1.2 collective-permute-start.42
  114.2 1.3 collective-permute-start.32
  116.2 1.4 collective-permute-start.17
  117.8 1.6 collective-permute-start.5
  119.4 1.1 collective-permute-start.43
  121.3 1.3 collective-permute-done.17
  122.6 1.2 collective-permute-start.35
  124.6 1.2 collective-permute-start.24
  125.8 1.6 collective-permute-start.25
  127.7 0.9 collective-permute-start.36
  128.6 2.0 %collective-permute-done.25 = bf16[2,1,1,1,1,1,16,512]{7,6,5,4,3,2,1,0:T(8,128)(2,1)S(1)} collective-permute-done((bf16[2,1,1,1,1,1,16,512]{7,6,5,4,3,2,1,0:T(8,128)(2,1)S(1)}, bf16[2,1,1,1,1,1,16,512]{7,6,5,4,3,2,1,0:T(8,128)(2,1)S(1)}, u32[]{:S(2)}, u32[]{:S(2)}) %collective-permute-start.25) | collective-permute-done | bytes 32800 | tf_op jit(solution)/shard_map/ppermute | solution.py:76
  130.7 1.1 collective-permute-start.26
  132.1 1.1 collective-permute-start.37
  133.2 1.8 %collective-permute-done.26 = bf16[2,2,1,1,1,1,16,512]{7,6,5,4,3,2,1,0:T(8,128)(2,1)S(1)} collective-permute-done((bf16[2,2,1,1,1,1,16,512]{7,6,5,4,3,2,1,0:T(8,128)(2,1)S(1)}, bf16[2,2,1,1,1,1,16,512]{7,6,5,4,3,2,1,0:T(8,128)(2,1)S(1)}, u32[]{:S(2)}, u32[]{:S(2)}) %collective-permute-start.26) | collective-permute-done | bytes 65568 | tf_op jit(solution)/shard_map/ppermute | solution.py:76
  135.0 0.9 collective-permute-start.27
  137.2 0.9 collective-permute-start.38
  138.1 2.0 %collective-permute-done.27 = bf16[2,2,2,1,1,1,16,512]{7,6,5,4,3,2,1,0:T(8,128)(2,1)S(1)} collective-permute-done((bf16[2,2,2,1,1,1,16,512]{7,6,5,4,3,2,1,0:T(8,128)(2,1)S(1)}, bf16[2,2,2,1,1,1,16,512]{7,6,5,4,3,2,1,0:T(8,128)(2,1)S(1)}, u32[]{:S(2)}, u32[]{:S(2)}) %collective-permute-start.27) | collective-permute-done | bytes 131104 | tf_op jit(solution)/shard_map/ppermute | solution.py:76
  140.1 1.0 collective-permute-start.28
  142.0 3.1 %collective-permute-done.38 = bf16[2,2,1,2,1,2,16,512]{7,6,5,4,3,2,1,0:T(8,128)(2,1)S(1)} collective-permute-done((bf16[2,2,1,2,1,2,16,512]{7,6,5,4,3,2,1,0:T(8,128)(2,1)S(1)}, bf16[2,2,1,2,1,2,16,512]{7,6,5,4,3,2,1,0:T(8,128)(2,1)S(1)}, u32[]{:S(2)}, u32[]{:S(2)}) %collective-permute-start.38) | collective-permute-done | bytes 262176 | tf_op jit(solution)/shard_map/ppermute | solution.py:76
  147.7 1.0 copy-done.13
  150.0 1.0 copy-done.14
  151.0 1.5 convolution_convert_fusion.2
  152.6 1.4 stack_reshape.13
  153.9 1.2 broadcast_select_fusion.3
  156.0 1.1 stack_reshape.14
  157.1 1.1 broadcast_select_fusion.7
  159.1 1.1 stack_reshape.12
  160.2 1.5 pad_maximum_fusion
  161.7 2.0 %gather_fusion.1 = bf16[4,2,64,2048]{3,2,1,0:T(8,128)(2,1)} fusion(bf16[4,2,64,2048]{3,2,1,0:T(8,128)(2,1)S(1)} %pad_maximum_fusion, s32[1024]{0:T(1024)S(1)} %pad_clamp_fusion), kind=kCustom, calls=%fused_computation.1 | custom fusion | bytes 4194320 | tf_op jit(solution)/shard_map/jit(_take)/gather | solution.py:155
  (299 shorter events, 35.7 us)
Async XLA Ops:
  2.3 2.5 %copy-start.18 = (f32[4,4,16]{2,1,0:T(4,128)}, f32[4,4,16]{2,1,0:T(4,128)S(1)}, u32[]{:S(2)}) copy-start(f32[4,4,16]{2,1,0:T(4,128)S(1)} %get-tuple-element.100) | copy-start | bytes 3076
  2.3 2.5 %copy-start.30 = (f32[4,4,16]{2,1,0:T(4,128)}, f32[4,4,16]{2,1,0:T(4,128)S(1)}, u32[]{:S(2)}) copy-start(f32[4,4,16]{2,1,0:T(4,128)S(1)} %get-tuple-element.94) | copy-start | bytes 3076
  2.3 3.0 %copy-start.20 = (f32[4,4,16]{2,1,0:T(4,128)}, f32[4,4,16]{2,1,0:T(4,128)S(1)}, u32[]{:S(2)}) copy-start(f32[4,4,16]{2,1,0:T(4,128)S(1)} %get-tuple-element.102) | copy-start | bytes 3076
  2.3 3.0 %copy-start.32 = (f32[4,4,16]{2,1,0:T(4,128)}, f32[4,4,16]{2,1,0:T(4,128)S(1)}, u32[]{:S(2)}) copy-start(f32[4,4,16]{2,1,0:T(4,128)S(1)} %get-tuple-element.96) | copy-start | bytes 3076
  7.8 39.7 %collective-permute-start.18 = (bf16[2,3,4,4,1,512]{5,4,3,2,1,0:T(2,128)(2,1)}, bf16[2,3,4,4,1,512]{5,4,3,2,1,0:T(2,128)(2,1)}, u32[]{:S(2)}, u32[]{:S(2)}) collective-permute-start(bf16[2,3,4,4,1,512]{5,4,3,2,1,0:T(2,128)(2,1)} %pad_maximum_fusion.22), channel_id=1, source_target_pairs={{0,1},{1,0},{2,3},{3,2},{4,5},{5,4},{6,7},{7,6},{8,9},{9,8},{10,11... | collective-permute-start | bytes 294920 | tf_op jit(solution)/shard_map/ppermute | solution.py:97
  13.2 2.3 %copy-start.1 = (bf16[1,3,4,4,16,512]{5,4,3,2,1,0:T(8,128)(2,1)}, bf16[1,3,4,4,16,512]{5,4,3,2,1,0:T(8,128)(2,1)S(1)}, u32[]{:S(2)}) copy-start(bf16[1,3,4,4,16,512]{5,4,3,2,1,0:T(8,128)(2,1)S(1)} %maximum_bitcast_fusion.5) | copy-start | bytes 2359300
  13.2 2.1 %copy-start = (bf16[2,3,4,4,16,512]{5,4,3,2,1,0:T(8,128)(2,1)S(1)}, bf16[2,3,4,4,16,512]{5,4,3,2,1,0:T(8,128)(2,1)}, u32[]{:S(2)}) copy-start(bf16[2,3,4,4,16,512]{5,4,3,2,1,0:T(8,128)(2,1)} %param.5) | copy-start | bytes 4718596
  13.3 7.1 %copy-start.3 = (bf16[1,3,4,4,16,512]{5,4,3,2,1,0:T(8,128)(2,1)}, bf16[1,3,4,4,16,512]{5,4,3,2,1,0:T(8,128)(2,1)S(1)}, u32[]{:S(2)}) copy-start(bf16[1,3,4,4,16,512]{5,4,3,2,1,0:T(8,128)(2,1)S(1)} %maximum_bitcast_fusion.4) | copy-start | bytes 2359300
  14.1 43.6 %collective-permute-start.12 = (bf16[2,3,4,1,16,512]{5,4,3,2,1,0:T(8,128)(2,1)}, bf16[2,3,4,1,16,512]{5,4,3,2,1,0:T(8,128)(2,1)}, u32[]{:S(2)}, u32[]{:S(2)}) collective-permute-start(bf16[2,3,4,1,16,512]{5,4,3,2,1,0:T(8,128)(2,1)} %pad_maximum_fusion.16), channel_id=1, source_target_pairs={{0,2},{2,4},{4,6},{6,8},{8,10},{10,12},{12,14},{14,16},{16,18},{18... | collective-permute-start | bytes 1179656 | tf_op jit(solution)/shard_map/ppermute | solution.py:95
  15.5 35.7 %collective-permute-start.6 = (bf16[2,3,4,4,1,512]{5,3,4,2,1,0:T(4,128)(2,1)S(1)}, bf16[2,3,4,4,1,512]{5,3,4,2,1,0:T(4,128)(2,1)}, u32[]{:S(2)}, u32[]{:S(2)}) collective-permute-start(bf16[2,3,4,4,1,512]{5,3,4,2,1,0:T(4,128)(2,1)S(1)} %copy.74), channel_id=1, source_target_pairs={{0,1},{1,0},{2,3},{3,2},{4,5},{5,4},{6,7},{7,6},{8,9},{9,8},{10,11... | collective-permute-start | bytes 294920 | tf_op jit(solution)/shard_map/ppermute | solution.py:96
  16.4 45.7 %collective-permute-start = (bf16[2,3,4,1,16,512]{5,4,3,2,1,0:T(8,128)(2,1)}, bf16[2,3,4,1,16,512]{5,4,3,2,1,0:T(8,128)(2,1)}, u32[]{:S(2)}, u32[]{:S(2)}) collective-permute-start(bf16[2,3,4,1,16,512]{5,4,3,2,1,0:T(8,128)(2,1)} %slice.149), channel_id=1, source_target_pairs={{0,30},{2,0},{4,2},{6,4},{8,6},{10,8},{12,10},{14,12},{16,14},{18,... | collective-permute-start | bytes 1179656 | tf_op jit(solution)/shard_map/ppermute | solution.py:94
  31.7 2.5 %copy-start.10 = (bf16[512,768]{1,0:T(8,128)(2,1)S(1)}, bf16[512,768]{1,0:T(8,128)(2,1)}, u32[]{:S(2)}) copy-start(bf16[512,768]{1,0:T(8,128)(2,1)} %fusion.31) | copy-start | bytes 2359300
  31.7 2.5 %copy-start.11 = (bf16[512,768]{1,0:T(8,128)(2,1)S(1)}, bf16[512,768]{1,0:T(8,128)(2,1)}, u32[]{:S(2)}) copy-start(bf16[512,768]{1,0:T(8,128)(2,1)} %get-tuple-element.26) | copy-start | bytes 2359300
  31.7 2.5 %copy-start.12 = (bf16[512,768]{1,0:T(8,128)(2,1)S(1)}, bf16[512,768]{1,0:T(8,128)(2,1)}, u32[]{:S(2)}) copy-start(bf16[512,768]{1,0:T(8,128)(2,1)} %get-tuple-element.27) | copy-start | bytes 2359300
  34.2 13.3 %copy-start.59 = (s32[4]{0:T(128)S(1)}, s32[4]{0:T(128)}, u32[]{:S(2)}) copy-start(s32[4]{0:T(128)} %param.7) | copy-start | bytes 52
  34.2 13.3 %copy-start.6 = (bf16[1,3,4,4,16,512]{5,4,3,2,1,0:T(8,128)(2,1)S(1)}, bf16[1,3,4,4,16,512]{5,4,3,2,1,0:T(8,128)(2,1)}, u32[]{:S(2)}) copy-start(bf16[1,3,4,4,16,512]{5,4,3,2,1,0:T(8,128)(2,1)} %copy-done.5) | copy-start | bytes 2359300
  34.2 13.3 %copy-start.8 = (bf16[1,3,4,4,16,512]{5,4,3,2,1,0:T(8,128)(2,1)S(1)}, bf16[1,3,4,4,16,512]{5,4,3,2,1,0:T(8,128)(2,1)}, u32[]{:S(2)}) copy-start(bf16[1,3,4,4,16,512]{5,4,3,2,1,0:T(8,128)(2,1)} %copy-done.7) | copy-start | bytes 2359300
  51.1 17.3 %collective-permute-start.19 = (f32[2,2,2,2,1,2,16,512]{7,6,0,5,4,3,2,1:T(8,128)S(1)}, f32[2,2,2,2,1,2,16,512]{7,6,0,5,4,3,2,1:T(8,128)S(1)}, u32[]{:S(2)}, u32[]{:S(2)}) collective-permute-start(f32[2,2,2,2,1,2,16,512]{7,6,0,5,4,3,2,1:T(8,128)S(1)} %constant_dynamic-slice_fusion.4), channel_id=1, source_target_pairs={{0,2},{1,3},{2,0},{3,1},{4,6},{5,7},{6,4},{7,5},{8,10},{9,11},{10,... | collective-permute-start | bytes 3145736 | tf_op jit(solution)/shard_map/ppermute | solution.py:67
  57.1 13.2 %collective-permute-start.7 = (f32[2,2,2,2,1,2,16,512]{7,6,0,5,4,3,2,1:T(8,128)S(1)}, f32[2,2,2,2,1,2,16,512]{7,6,0,5,4,3,2,1:T(8,128)S(1)}, u32[]{:S(2)}, u32[]{:S(2)}) collective-permute-start(f32[2,2,2,2,1,2,16,512]{7,6,0,5,4,3,2,1:T(8,128)S(1)} %constant_dynamic-slice_fusion.14), channel_id=1, source_target_pairs={{0,2},{1,3},{2,0},{3,1},{4,6},{5,7},{6,4},{7,5},{8,10},{9,11},{10,... | collective-permute-start | bytes 3145736 | tf_op jit(solution)/shard_map/ppermute | solution.py:67
  61.4 2.4 %copy-start.35 = (f32[4,4,16]{2,1,0:T(4,128)S(1)}, f32[4,4,16]{2,1,0:T(4,128)}, u32[]{:S(2)}) copy-start(f32[4,4,16]{2,1,0:T(4,128)} %copy-done.34) | copy-start | bytes 3076
  61.4 2.4 %copy-start.37 = (f32[4,4,16]{2,1,0:T(4,128)S(1)}, f32[4,4,16]{2,1,0:T(4,128)}, u32[]{:S(2)}) copy-start(f32[4,4,16]{2,1,0:T(4,128)} %copy-done.36) | copy-start | bytes 3076
  61.5 2.4 %copy-start.39 = (f32[4,4,16]{2,1,0:T(4,128)S(1)}, f32[4,4,16]{2,1,0:T(4,128)}, u32[]{:S(2)}) copy-start(f32[4,4,16]{2,1,0:T(4,128)} %copy-done.38) | copy-start | bytes 3076
  61.5 2.4 %copy-start.55 = (f32[4,4,16]{2,1,0:T(4,128)S(1)}, f32[4,4,16]{2,1,0:T(4,128)}, u32[]{:S(2)}) copy-start(f32[4,4,16]{2,1,0:T(4,128)} %get-tuple-element.73) | copy-start | bytes 3076
  61.5 2.4 %copy-start.56 = (f32[4,4,16]{2,1,0:T(4,128)S(1)}, f32[4,4,16]{2,1,0:T(4,128)}, u32[]{:S(2)}) copy-start(f32[4,4,16]{2,1,0:T(4,128)} %get-tuple-element.75) | copy-start | bytes 3076
  61.5 2.4 %copy-start.57 = (f32[4,4,16]{2,1,0:T(4,128)S(1)}, f32[4,4,16]{2,1,0:T(4,128)}, u32[]{:S(2)}) copy-start(f32[4,4,16]{2,1,0:T(4,128)} %get-tuple-element.77) | copy-start | bytes 3076
  61.5 9.1 %collective-permute-start.13 = (f32[2,2,2,2,1,2,16,512]{7,6,5,4,3,2,1,0:T(8,128)S(1)}, f32[2,2,2,2,1,2,16,512]{7,6,5,4,3,2,1,0:T(8,128)S(1)}, u32[]{:S(2)}, u32[]{:S(2)}) collective-permute-start(f32[2,2,2,2,1,2,16,512]{7,6,5,4,3,2,1,0:T(8,128)S(1)} %constant_dynamic-slice_fusion.9), channel_id=1, source_target_pairs={{0,2},{1,3},{2,0},{3,1},{4,6},{5,7},{6,4},{7,5},{8,10},{9,11},{10,... | collective-permute-start | bytes 3145736 | tf_op jit(solution)/shard_map/ppermute | solution.py:67
  67.9 3.1 %collective-permute-start.1 = (f32[2,2,2,2,1,2,16,512]{7,6,5,4,3,2,1,0:T(8,128)S(1)}, f32[2,2,2,2,1,2,16,512]{7,6,5,4,3,2,1,0:T(8,128)S(1)}, u32[]{:S(2)}, u32[]{:S(2)}) collective-permute-start(f32[2,2,2,2,1,2,16,512]{7,6,5,4,3,2,1,0:T(8,128)S(1)} %constant_dynamic-slice_fusion.19), channel_id=1, source_target_pairs={{0,2},{1,3},{2,0},{3,1},{4,6},{5,7},{6,4},{7,5},{8,10},{9,11},{10,... | collective-permute-start | bytes 3145736 | tf_op jit(solution)/shard_map/ppermute | solution.py:67
  68.7 14.9 %collective-permute-start.20 = (f32[2,2,2,2,1,1,16,512]{7,6,0,5,4,3,2,1:T(8,128)S(1)}, f32[2,2,2,2,1,1,16,512]{7,6,0,5,4,3,2,1:T(8,128)S(1)}, u32[]{:S(2)}, u32[]{:S(2)}) collective-permute-start(f32[2,2,2,2,1,1,16,512]{7,6,0,5,4,3,2,1:T(8,128)S(1)} %constant_dynamic-slice_fusion.3), channel_id=1, source_target_pairs={{0,1},{1,0},{2,3},{3,2},{4,5},{5,4},{6,7},{7,6},{8,9},{9,8},{10,11... | collective-permute-start | bytes 1572872 | tf_op jit(solution)/shard_map/ppermute | solution.py:67
  70.6 13.6 %collective-permute-start.8 = (f32[2,2,2,1,1,2,16,512]{7,6,0,5,4,3,2,1:T(8,128)S(1)}, f32[2,2,2,1,1,2,16,512]{7,6,0,5,4,3,2,1:T(8,128)S(1)}, u32[]{:S(2)}, u32[]{:S(2)}) collective-permute-start(f32[2,2,2,1,1,2,16,512]{7,6,0,5,4,3,2,1:T(8,128)S(1)} %constant_dynamic-slice_fusion.13), channel_id=1, source_target_pairs={{0,4},{1,5},{2,6},{3,7},{4,0},{5,1},{6,2},{7,3},{8,12},{9,13},{10,... | collective-permute-start | bytes 1572872 | tf_op jit(solution)/shard_map/ppermute | solution.py:67
  70.9 21.9 %collective-permute-start.14 = (f32[2,2,1,2,1,2,16,512]{7,6,5,4,3,2,1,0:T(8,128)S(1)}, f32[2,2,1,2,1,2,16,512]{7,6,5,4,3,2,1,0:T(8,128)S(1)}, u32[]{:S(2)}, u32[]{:S(2)}) collective-permute-start(f32[2,2,1,2,1,2,16,512]{7,6,5,4,3,2,1,0:T(8,128)S(1)} %constant_dynamic-slice_fusion.8), channel_id=1, source_target_pairs={{0,8},{1,9},{2,10},{3,11},{4,12},{5,13},{6,14},{7,15},{8,0},{9,1},... | collective-permute-start | bytes 1572872 | tf_op jit(solution)/shard_map/ppermute | solution.py:67
  71.3 23.7 %collective-permute-start.2 = (f32[2,2,2,2,1,1,16,512]{7,6,5,4,3,2,1,0:T(8,128)S(1)}, f32[2,2,2,2,1,1,16,512]{7,6,5,4,3,2,1,0:T(8,128)S(1)}, u32[]{:S(2)}, u32[]{:S(2)}) collective-permute-start(f32[2,2,2,2,1,1,16,512]{7,6,5,4,3,2,1,0:T(8,128)S(1)} %constant_dynamic-slice_fusion.18), channel_id=1, source_target_pairs={{0,1},{1,0},{2,3},{3,2},{4,5},{5,4},{6,7},{7,6},{8,9},{9,8},{10,11... | collective-permute-start | bytes 1572872 | tf_op jit(solution)/shard_map/ppermute | solution.py:67
  83.7 6.5 %collective-permute-start.21 = (f32[2,2,2,1,1,1,16,512]{7,6,0,5,4,3,2,1:T(8,128)S(1)}, f32[2,2,2,1,1,1,16,512]{7,6,0,5,4,3,2,1:T(8,128)S(1)}, u32[]{:S(2)}, u32[]{:S(2)}) collective-permute-start(f32[2,2,2,1,1,1,16,512]{7,6,0,5,4,3,2,1:T(8,128)S(1)} %constant_dynamic-slice_fusion.2), channel_id=1, source_target_pairs={{0,4},{1,5},{2,6},{3,7},{4,0},{5,1},{6,2},{7,3},{8,12},{9,13},{10,... | collective-permute-start | bytes 786440 | tf_op jit(solution)/shard_map/ppermute | solution.py:67
  84.3 8.3 %collective-permute-start.9 = (f32[2,2,1,1,1,2,16,512]{7,6,0,5,4,3,2,1:T(8,128)S(1)}, f32[2,2,1,1,1,2,16,512]{7,6,0,5,4,3,2,1:T(8,128)S(1)}, u32[]{:S(2)}, u32[]{:S(2)}) collective-permute-start(f32[2,2,1,1,1,2,16,512]{7,6,0,5,4,3,2,1:T(8,128)S(1)} %constant_dynamic-slice_fusion.12), channel_id=1, source_target_pairs={{0,8},{1,9},{2,10},{3,11},{4,12},{5,13},{6,14},{7,15},{8,0},{9,1},... | collective-permute-start | bytes 786440 | tf_op jit(solution)/shard_map/ppermute | solution.py:67
  90.3 6.1 %collective-permute-start.22 = (f32[2,2,1,1,1,1,16,512]{7,6,0,5,4,3,2,1:T(8,128)S(1)}, f32[2,2,1,1,1,1,16,512]{7,6,0,5,4,3,2,1:T(8,128)S(1)}, u32[]{:S(2)}, u32[]{:S(2)}) collective-permute-start(f32[2,2,1,1,1,1,16,512]{7,6,0,5,4,3,2,1:T(8,128)S(1)} %constant_dynamic-slice_fusion.1), channel_id=1, source_target_pairs={{0,8},{1,9},{2,10},{3,11},{4,12},{5,13},{6,14},{7,15},{8,0},{9,1},... | collective-permute-start | bytes 393224 | tf_op jit(solution)/shard_map/ppermute | solution.py:67
  92.7 6.4 %collective-permute-start.10 = (f32[2,2,1,1,1,1,16,512]{7,6,0,5,4,3,2,1:T(8,128)S(1)}, f32[2,2,1,1,1,1,16,512]{7,6,0,5,4,3,2,1:T(8,128)S(1)}, u32[]{:S(2)}, u32[]{:S(2)}) collective-permute-start(f32[2,2,1,1,1,1,16,512]{7,6,0,5,4,3,2,1:T(8,128)S(1)} %constant_dynamic-slice_fusion.11), channel_id=1, source_target_pairs={{0,1},{1,0},{2,3},{3,2},{4,5},{5,4},{6,7},{7,6},{8,9},{9,8},{10,11... | collective-permute-start | bytes 393224 | tf_op jit(solution)/shard_map/ppermute | solution.py:67
  92.9 18.0 %collective-permute-start.15 = (f32[2,2,1,2,1,1,16,512]{7,6,5,4,3,2,1,0:T(8,128)S(1)}, f32[2,2,1,2,1,1,16,512]{7,6,5,4,3,2,1,0:T(8,128)S(1)}, u32[]{:S(2)}, u32[]{:S(2)}) collective-permute-start(f32[2,2,1,2,1,1,16,512]{7,6,5,4,3,2,1,0:T(8,128)S(1)} %constant_dynamic-slice_fusion.7), channel_id=1, source_target_pairs={{0,1},{1,0},{2,3},{3,2},{4,5},{5,4},{6,7},{7,6},{8,9},{9,8},{10,11... | collective-permute-start | bytes 786440 | tf_op jit(solution)/shard_map/ppermute | solution.py:67
  95.2 17.1 %collective-permute-start.3 = (f32[2,2,2,1,1,1,16,512]{7,6,5,4,3,2,1,0:T(8,128)S(1)}, f32[2,2,2,1,1,1,16,512]{7,6,5,4,3,2,1,0:T(8,128)S(1)}, u32[]{:S(2)}, u32[]{:S(2)}) collective-permute-start(f32[2,2,2,1,1,1,16,512]{7,6,5,4,3,2,1,0:T(8,128)S(1)} %constant_dynamic-slice_fusion.17), channel_id=1, source_target_pairs={{0,4},{1,5},{2,6},{3,7},{4,0},{5,1},{6,2},{7,3},{8,12},{9,13},{10,... | collective-permute-start | bytes 786440 | tf_op jit(solution)/shard_map/ppermute | solution.py:67
  96.4 6.0 %collective-permute-start.23 = (f32[2,1,1,1,1,1,16,512]{7,6,0,5,4,3,2,1:T(8,128)S(1)}, f32[2,1,1,1,1,1,16,512]{7,6,0,5,4,3,2,1:T(8,128)S(1)}, u32[]{:S(2)}, u32[]{:S(2)}) collective-permute-start(f32[2,1,1,1,1,1,16,512]{7,6,0,5,4,3,2,1:T(8,128)S(1)} %constant_dynamic-slice_fusion), channel_id=1, source_target_pairs={{0,16},{1,17},{2,18},{3,19},{4,20},{5,21},{6,22},{7,23},{8,24},{9,... | collective-permute-start | bytes 196616 | tf_op jit(solution)/shard_map/ppermute | solution.py:67
  99.2 5.7 %collective-permute-start.11 = (f32[2,1,1,1,1,1,16,512]{7,6,0,5,4,3,2,1:T(8,128)S(1)}, f32[2,1,1,1,1,1,16,512]{7,6,0,5,4,3,2,1:T(8,128)S(1)}, u32[]{:S(2)}, u32[]{:S(2)}) collective-permute-start(f32[2,1,1,1,1,1,16,512]{7,6,0,5,4,3,2,1:T(8,128)S(1)} %constant_dynamic-slice_fusion.10), channel_id=1, source_target_pairs={{0,16},{1,17},{2,18},{3,19},{4,20},{5,21},{6,22},{7,23},{8,24},{9,... | collective-permute-start | bytes 196616 | tf_op jit(solution)/shard_map/ppermute | solution.py:67
  102.4 4.9 %collective-permute-start.40 = (bf16[2,1,1,1,1,1,16,512]{7,6,5,4,3,2,1,0:T(8,128)(2,1)S(1)}, bf16[2,1,1,1,1,1,16,512]{7,6,5,4,3,2,1,0:T(8,128)(2,1)S(1)}, u32[]{:S(2)}, u32[]{:S(2)}) collective-permute-start(bf16[2,1,1,1,1,1,16,512]{7,6,5,4,3,2,1,0:T(8,128)(2,1)S(1)} %get-tuple-element.70), channel_id=1, source_target_pairs={{0,16},{1,17},{2,18},{3,19},{4,20},{5,21},{6,22},{7,23},{8,24},{9,... | collective-permute-start | bytes 98312 | tf_op jit(solution)/shard_map/ppermute | solution.py:76
  104.9 4.9 %collective-permute-start.30 = (bf16[2,1,1,1,1,1,16,512]{7,6,0,5,4,3,2,1:T(8,128)(2,1)S(1)}, bf16[2,1,1,1,1,1,16,512]{7,6,0,5,4,3,2,1:T(8,128)(2,1)S(1)}, u32[]{:S(2)}, u32[]{:S(2)}) collective-permute-start(bf16[2,1,1,1,1,1,16,512]{7,6,0,5,4,3,2,1:T(8,128)(2,1)S(1)} %get-tuple-element.66), channel_id=1, source_target_pairs={{0,16},{1,17},{2,18},{3,19},{4,20},{5,21},{6,22},{7,23},{8,24},{9,... | collective-permute-start | bytes 98312 | tf_op jit(solution)/shard_map/ppermute | solution.py:76
  107.3 5.1 %collective-permute-start.41 = (bf16[2,2,1,1,1,1,16,512]{7,6,5,4,3,2,1,0:T(8,128)(2,1)S(1)}, bf16[2,2,1,1,1,1,16,512]{7,6,5,4,3,2,1,0:T(8,128)(2,1)S(1)}, u32[]{:S(2)}, u32[]{:S(2)}) collective-permute-start(bf16[2,2,1,1,1,1,16,512]{7,6,5,4,3,2,1,0:T(8,128)(2,1)S(1)} %pad_maximum_fusion.30), channel_id=1, source_target_pairs={{0,8},{1,9},{2,10},{3,11},{4,12},{5,13},{6,14},{7,15},{8,0},{9,1},... | collective-permute-start | bytes 196616 | tf_op jit(solution)/shard_map/ppermute | solution.py:76
  109.9 4.3 %collective-permute-start.31 = (bf16[2,2,1,1,1,1,16,512]{7,6,0,5,4,3,2,1:T(8,128)(2,1)S(1)}, bf16[2,2,1,1,1,1,16,512]{7,6,0,5,4,3,2,1:T(8,128)(2,1)S(1)}, u32[]{:S(2)}, u32[]{:S(2)}) collective-permute-start(bf16[2,2,1,1,1,1,16,512]{7,6,0,5,4,3,2,1:T(8,128)(2,1)S(1)} %pad_maximum_fusion.28), channel_id=1, source_target_pairs={{0,1},{1,0},{2,3},{3,2},{4,5},{5,4},{6,7},{7,6},{8,9},{9,8},{10,11... | collective-permute-start | bytes 196616 | tf_op jit(solution)/shard_map/ppermute | solution.py:76
  111.0 5.2 %collective-permute-start.16 = (f32[2,2,1,1,1,1,16,512]{7,6,5,4,3,2,1,0:T(8,128)S(1)}, f32[2,2,1,1,1,1,16,512]{7,6,5,4,3,2,1,0:T(8,128)S(1)}, u32[]{:S(2)}, u32[]{:S(2)}) collective-permute-start(f32[2,2,1,1,1,1,16,512]{7,6,5,4,3,2,1,0:T(8,128)S(1)} %constant_dynamic-slice_fusion.6), channel_id=1, source_target_pairs={{0,4},{1,5},{2,6},{3,7},{4,0},{5,1},{6,2},{7,3},{8,12},{9,13},{10,... | collective-permute-start | bytes 393224 | tf_op jit(solution)/shard_map/ppermute | solution.py:67
  112.4 5.4 %collective-permute-start.4 = (f32[2,2,1,1,1,1,16,512]{7,6,5,4,3,2,1,0:T(8,128)S(1)}, f32[2,2,1,1,1,1,16,512]{7,6,5,4,3,2,1,0:T(8,128)S(1)}, u32[]{:S(2)}, u32[]{:S(2)}) collective-permute-start(f32[2,2,1,1,1,1,16,512]{7,6,5,4,3,2,1,0:T(8,128)S(1)} %constant_dynamic-slice_fusion.16), channel_id=1, source_target_pairs={{0,8},{1,9},{2,10},{3,11},{4,12},{5,13},{6,14},{7,15},{8,0},{9,1},... | collective-permute-start | bytes 393224 | tf_op jit(solution)/shard_map/ppermute | solution.py:67
  112.5 6.9 %collective-permute-start.42 = (bf16[2,2,2,1,1,1,16,512]{7,6,5,4,3,2,1,0:T(8,128)(2,1)S(1)}, bf16[2,2,2,1,1,1,16,512]{7,6,5,4,3,2,1,0:T(8,128)(2,1)S(1)}, u32[]{:S(2)}, u32[]{:S(2)}) collective-permute-start(bf16[2,2,2,1,1,1,16,512]{7,6,5,4,3,2,1,0:T(8,128)(2,1)S(1)} %pad_maximum_fusion.26), channel_id=1, source_target_pairs={{0,4},{1,5},{2,6},{3,7},{4,0},{5,1},{6,2},{7,3},{8,12},{9,13},{10,... | collective-permute-start | bytes 393224 | tf_op jit(solution)/shard_map/ppermute | solution.py:76
  114.2 6.2 %collective-permute-start.32 = (bf16[2,2,1,1,1,2,16,512]{7,6,0,5,4,3,2,1:T(8,128)(2,1)S(1)}, bf16[2,2,1,1,1,2,16,512]{7,6,0,5,4,3,2,1:T(8,128)(2,1)S(1)}, u32[]{:S(2)}, u32[]{:S(2)}) collective-permute-start(bf16[2,2,1,1,1,2,16,512]{7,6,0,5,4,3,2,1:T(8,128)(2,1)S(1)} %pad_maximum_fusion.24), channel_id=1, source_target_pairs={{0,8},{1,9},{2,10},{3,11},{4,12},{5,13},{6,14},{7,15},{8,0},{9,1},... | collective-permute-start | bytes 393224 | tf_op jit(solution)/shard_map/ppermute | solution.py:76
  116.2 6.4 %collective-permute-start.17 = (f32[2,1,1,1,1,1,16,512]{7,6,5,4,3,2,1,0:T(8,128)S(1)}, f32[2,1,1,1,1,1,16,512]{7,6,5,4,3,2,1,0:T(8,128)S(1)}, u32[]{:S(2)}, u32[]{:S(2)}) collective-permute-start(f32[2,1,1,1,1,1,16,512]{7,6,5,4,3,2,1,0:T(8,128)S(1)} %constant_dynamic-slice_fusion.5), channel_id=1, source_target_pairs={{0,16},{1,17},{2,18},{3,19},{4,20},{5,21},{6,22},{7,23},{8,24},{9,... | collective-permute-start | bytes 196616 | tf_op jit(solution)/shard_map/ppermute | solution.py:67
  117.8 6.2 %collective-permute-start.5 = (f32[2,1,1,1,1,1,16,512]{7,6,5,4,3,2,1,0:T(8,128)S(1)}, f32[2,1,1,1,1,1,16,512]{7,6,5,4,3,2,1,0:T(8,128)S(1)}, u32[]{:S(2)}, u32[]{:S(2)}) collective-permute-start(f32[2,1,1,1,1,1,16,512]{7,6,5,4,3,2,1,0:T(8,128)S(1)} %constant_dynamic-slice_fusion.15), channel_id=1, source_target_pairs={{0,16},{1,17},{2,18},{3,19},{4,20},{5,21},{6,22},{7,23},{8,24},{9,... | collective-permute-start | bytes 196616 | tf_op jit(solution)/shard_map/ppermute | solution.py:67
  119.4 16.5 %collective-permute-start.43 = (bf16[2,2,2,2,1,1,16,512]{7,6,5,4,3,2,1,0:T(8,128)(2,1)S(1)}, bf16[2,2,2,2,1,1,16,512]{7,6,5,4,3,2,1,0:T(8,128)(2,1)S(1)}, u32[]{:S(2)}, u32[]{:S(2)}) collective-permute-start(bf16[2,2,2,2,1,1,16,512]{7,6,5,4,3,2,1,0:T(8,128)(2,1)S(1)} %pad_maximum_fusion.21), channel_id=1, source_target_pairs={{0,1},{1,0},{2,3},{3,2},{4,5},{5,4},{6,7},{7,6},{8,9},{9,8},{10,11... | collective-permute-start | bytes 786440 | tf_op jit(solution)/shard_map/ppermute | solution.py:76
  120.5 15.6 %collective-permute-start.33 = (bf16[2,2,2,1,1,2,16,512]{7,6,0,5,4,3,2,1:T(8,128)(2,1)S(1)}, bf16[2,2,2,1,1,2,16,512]{7,6,0,5,4,3,2,1:T(8,128)(2,1)S(1)}, u32[]{:S(2)}, u32[]{:S(2)}) collective-permute-start(bf16[2,2,2,1,1,2,16,512]{7,6,0,5,4,3,2,1:T(8,128)(2,1)S(1)} %pad_maximum_fusion.19), channel_id=1, source_target_pairs={{0,4},{1,5},{2,6},{3,7},{4,0},{5,1},{6,2},{7,3},{8,12},{9,13},{10,... | collective-permute-start | bytes 786440 | tf_op jit(solution)/shard_map/ppermute | solution.py:76
  122.6 5.1 %collective-permute-start.35 = (bf16[2,1,1,1,1,1,16,512]{7,6,5,4,3,2,1,0:T(8,128)(2,1)S(1)}, bf16[2,1,1,1,1,1,16,512]{7,6,5,4,3,2,1,0:T(8,128)(2,1)S(1)}, u32[]{:S(2)}, u32[]{:S(2)}) collective-permute-start(bf16[2,1,1,1,1,1,16,512]{7,6,5,4,3,2,1,0:T(8,128)(2,1)S(1)} %get-tuple-element.68), channel_id=1, source_target_pairs={{0,16},{1,17},{2,18},{3,19},{4,20},{5,21},{6,22},{7,23},{8,24},{9,... | collective-permute-start | bytes 98312 | tf_op jit(solution)/shard_map/ppermute | solution.py:76
  124.6 16.5 %collective-permute-start.24 = (f32[4,2,1,1,1,1,1,16,512]{8,7,1,0,6,5,4,3,2:T(8,128)S(1)}, f32[4,2,1,1,1,1,1,16,512]{8,7,1,0,6,5,4,3,2:T(8,128)S(1)}, u32[]{:S(2)}, u32[]{:S(2)}) collective-permute-start(f32[4,2,1,1,1,1,1,16,512]{8,7,1,0,6,5,4,3,2:T(8,128)S(1)} %bitcast.565), channel_id=1, source_target_pairs={{0,1},{1,0},{2,3},{3,2},{4,5},{5,4},{6,7},{7,6},{8,9},{9,8},{10,11... | collective-permute-start | bytes 786440 | tf_op jit(solution)/shard_map/ppermute | solution.py:76
  125.8 4.8 %collective-permute-start.25 = (bf16[2,1,1,1,1,1,16,512]{7,6,5,4,3,2,1,0:T(8,128)(2,1)S(1)}, bf16[2,1,1,1,1,1,16,512]{7,6,5,4,3,2,1,0:T(8,128)(2,1)S(1)}, u32[]{:S(2)}, u32[]{:S(2)}) collective-permute-start(bf16[2,1,1,1,1,1,16,512]{7,6,5,4,3,2,1,0:T(8,128)(2,1)S(1)} %get-tuple-element.64), channel_id=1, source_target_pairs={{0,16},{1,17},{2,18},{3,19},{4,20},{5,21},{6,22},{7,23},{8,24},{9,... | collective-permute-start | bytes 98312 | tf_op jit(solution)/shard_map/ppermute | solution.py:76
  127.7 4.3 %collective-permute-start.36 = (bf16[2,2,1,1,1,1,16,512]{7,6,5,4,3,2,1,0:T(8,128)(2,1)S(1)}, bf16[2,2,1,1,1,1,16,512]{7,6,5,4,3,2,1,0:T(8,128)(2,1)S(1)}, u32[]{:S(2)}, u32[]{:S(2)}) collective-permute-start(bf16[2,2,1,1,1,1,16,512]{7,6,5,4,3,2,1,0:T(8,128)(2,1)S(1)} %pad_maximum_fusion.29), channel_id=1, source_target_pairs={{0,4},{1,5},{2,6},{3,7},{4,0},{5,1},{6,2},{7,3},{8,12},{9,13},{10,... | collective-permute-start | bytes 196616 | tf_op jit(solution)/shard_map/ppermute | solution.py:76
  130.7 4.3 %collective-permute-start.26 = (bf16[2,2,1,1,1,1,16,512]{7,6,5,4,3,2,1,0:T(8,128)(2,1)S(1)}, bf16[2,2,1,1,1,1,16,512]{7,6,5,4,3,2,1,0:T(8,128)(2,1)S(1)}, u32[]{:S(2)}, u32[]{:S(2)}) collective-permute-start(bf16[2,2,1,1,1,1,16,512]{7,6,5,4,3,2,1,0:T(8,128)(2,1)S(1)} %pad_maximum_fusion.27), channel_id=1, source_target_pairs={{0,8},{1,9},{2,10},{3,11},{4,12},{5,13},{6,14},{7,15},{8,0},{9,1},... | collective-permute-start | bytes 196616 | tf_op jit(solution)/shard_map/ppermute | solution.py:76
  132.1 5.0 %collective-permute-start.37 = (bf16[2,2,1,2,1,1,16,512]{7,6,5,4,3,2,1,0:T(8,128)(2,1)S(1)}, bf16[2,2,1,2,1,1,16,512]{7,6,5,4,3,2,1,0:T(8,128)(2,1)S(1)}, u32[]{:S(2)}, u32[]{:S(2)}) collective-permute-start(bf16[2,2,1,2,1,1,16,512]{7,6,5,4,3,2,1,0:T(8,128)(2,1)S(1)} %pad_maximum_fusion.25), channel_id=1, source_target_pairs={{0,1},{1,0},{2,3},{3,2},{4,5},{5,4},{6,7},{7,6},{8,9},{9,8},{10,11... | collective-permute-start | bytes 393224 | tf_op jit(solution)/shard_map/ppermute | solution.py:76
  135.0 5.0 %collective-permute-start.27 = (bf16[2,2,2,1,1,1,16,512]{7,6,5,4,3,2,1,0:T(8,128)(2,1)S(1)}, bf16[2,2,2,1,1,1,16,512]{7,6,5,4,3,2,1,0:T(8,128)(2,1)S(1)}, u32[]{:S(2)}, u32[]{:S(2)}) collective-permute-start(bf16[2,2,2,1,1,1,16,512]{7,6,5,4,3,2,1,0:T(8,128)(2,1)S(1)} %pad_maximum_fusion.23), channel_id=1, source_target_pairs={{0,4},{1,5},{2,6},{3,7},{4,0},{5,1},{6,2},{7,3},{8,12},{9,13},{10,... | collective-permute-start | bytes 393224 | tf_op jit(solution)/shard_map/ppermute | solution.py:76
  136.0 11.4 %collective-permute-start.44 = (bf16[2,2,2,2,1,2,16,512]{7,6,5,4,3,2,1,0:T(8,128)(2,1)S(1)}, bf16[2,2,2,2,1,2,16,512]{7,6,5,4,3,2,1,0:T(8,128)(2,1)S(1)}, u32[]{:S(2)}, u32[]{:S(2)}) collective-permute-start(bf16[2,2,2,2,1,2,16,512]{7,6,5,4,3,2,1,0:T(8,128)(2,1)S(1)} %pad_maximum_fusion.15), channel_id=1, source_target_pairs={{0,2},{1,3},{2,0},{3,1},{4,6},{5,7},{6,4},{7,5},{8,10},{9,11},{10,... | collective-permute-start | bytes 1572872 | tf_op jit(solution)/shard_map/ppermute | solution.py:76
  136.2 13.2 %collective-permute-start.34 = (bf16[2,2,2,2,1,2,16,512]{7,6,0,5,4,3,2,1:T(8,128)(2,1)S(1)}, bf16[2,2,2,2,1,2,16,512]{7,6,0,5,4,3,2,1:T(8,128)(2,1)S(1)}, u32[]{:S(2)}, u32[]{:S(2)}) collective-permute-start(bf16[2,2,2,2,1,2,16,512]{7,6,0,5,4,3,2,1:T(8,128)(2,1)S(1)} %pad_maximum_fusion.13), channel_id=1, source_target_pairs={{0,2},{1,3},{2,0},{3,1},{4,6},{5,7},{6,4},{7,5},{8,10},{9,11},{10,... | collective-permute-start | bytes 1572872 | tf_op jit(solution)/shard_map/ppermute | solution.py:76
  137.2 8.0 %collective-permute-start.38 = (bf16[2,2,1,2,1,2,16,512]{7,6,5,4,3,2,1,0:T(8,128)(2,1)S(1)}, bf16[2,2,1,2,1,2,16,512]{7,6,5,4,3,2,1,0:T(8,128)(2,1)S(1)}, u32[]{:S(2)}, u32[]{:S(2)}) collective-permute-start(bf16[2,2,1,2,1,2,16,512]{7,6,5,4,3,2,1,0:T(8,128)(2,1)S(1)} %pad_maximum_fusion.20), channel_id=1, source_target_pairs={{0,8},{1,9},{2,10},{3,11},{4,12},{5,13},{6,14},{7,15},{8,0},{9,1},... | collective-permute-start | bytes 786440 | tf_op jit(solution)/shard_map/ppermute | solution.py:76
  140.1 6.4 %collective-permute-start.28 = (bf16[2,2,2,2,1,1,16,512]{7,6,5,4,3,2,1,0:T(8,128)(2,1)S(1)}, bf16[2,2,2,2,1,1,16,512]{7,6,5,4,3,2,1,0:T(8,128)(2,1)S(1)}, u32[]{:S(2)}, u32[]{:S(2)}) collective-permute-start(bf16[2,2,2,2,1,1,16,512]{7,6,5,4,3,2,1,0:T(8,128)(2,1)S(1)} %pad_maximum_fusion.18), channel_id=1, source_target_pairs={{0,1},{1,0},{2,3},{3,2},{4,5},{5,4},{6,7},{7,6},{8,9},{9,8},{10,11... | collective-permute-start | bytes 786440 | tf_op jit(solution)/shard_map/ppermute | solution.py:76
  146.1 7.9 %collective-permute-start.39 = (bf16[2,2,2,2,1,2,16,512]{7,6,5,4,3,2,1,0:T(8,128)(2,1)}, bf16[2,2,2,2,1,2,16,512]{7,6,5,4,3,2,1,0:T(8,128)(2,1)}, u32[]{:S(2)}, u32[]{:S(2)}) collective-permute-start(bf16[2,2,2,2,1,2,16,512]{7,6,5,4,3,2,1,0:T(8,128)(2,1)} %pad_maximum_fusion.14), channel_id=1, source_target_pairs={{0,2},{1,3},{2,0},{3,1},{4,6},{5,7},{6,4},{7,5},{8,10},{9,11},{10,... | collective-permute-start | bytes 1572872 | tf_op jit(solution)/shard_map/ppermute | solution.py:76
  147.5 9.7 %collective-permute-start.29 = (bf16[2,2,2,2,1,2,16,512]{7,6,5,4,3,2,1,0:T(8,128)(2,1)}, bf16[2,2,2,2,1,2,16,512]{7,6,5,4,3,2,1,0:T(8,128)(2,1)}, u32[]{:S(2)}, u32[]{:S(2)}) collective-permute-start(bf16[2,2,2,2,1,2,16,512]{7,6,5,4,3,2,1,0:T(8,128)(2,1)} %pad_maximum_fusion.12), channel_id=1, source_target_pairs={{0,2},{1,3},{2,0},{3,1},{4,6},{5,7},{6,4},{7,5},{8,10},{9,11},{10,... | collective-permute-start | bytes 1572872 | tf_op jit(solution)/shard_map/ppermute | solution.py:76
  (41 other events, 38.2 us)

commit v5 on v1

--- a/solution.py
+++ b/solution.py
@@ -121,29 +121,37 @@
         lhs = jnp.stack(
             [jnp.concatenate([p_re, -p_im], -1), jnp.concatenate([p_im, p_re], -1)], 0
         ).reshape(2, prows, nspin, 2 * nev)
-        lhs = jnp.take(lhs, spin_map, axis=2).reshape(2 * prows * nspin, 2 * nev)
+        lhs = jnp.take(lhs, spin_map, axis=2, mode="clip").reshape(2 * prows * nspin, 2 * nev)
 
-        own = []
-        products = []
-        for d, field in enumerate(disp):
-            order = orders[d % len(orders)]
-            gram = jnp.dot(left, field.reshape(2 * depth, nev), preferred_element_type=jnp.float32)
-            buf = gram.reshape([2] + [2] * nbits + [rows, nev])
-            part = reduce_scatter(buf, order, nbits, count, 1).reshape(2, rows, nev)
+        own = [None] * len(disp)
+        products = [None] * len(disp)
+        groups = {}
+        for d in range(len(disp)):
+            groups.setdefault(d % len(orders), []).append(d)
+        for key, members in groups.items():
+            order = orders[key]
+            grams = [
+                jnp.dot(left, disp[d].reshape(2 * depth, nev), preferred_element_type=jnp.float32)
+                for d in members
+            ]
+            buf = jnp.stack(grams, 0).reshape([len(members), 2] + [2] * nbits + [rows, nev])
+            part = reduce_scatter(buf, order, nbits, count, 2).reshape(len(members), 2, rows, nev)
             part = part * norm_factor
-            own.append(part)
-            blk = part.astype(jnp.bfloat16).reshape([2] + [1] * nbits + [rows, nev])
-            rhs = all_gather(blk, list(reversed(order)), nbits, count, 1).reshape(2 * nev, nev)
-            product = jnp.dot(lhs, rhs, preferred_element_type=jnp.float32)
-            products.append(product.astype(jnp.bfloat16).reshape(2, prows, nspin * nev))
-        own = jnp.take(jnp.stack(own, 0), directions, axis=0)
+            blk = part.astype(jnp.bfloat16).reshape([len(members), 2] + [1] * nbits + [rows, nev])
+            rhs = all_gather(blk, list(reversed(order)), nbits, count, 2)
+            rhs = rhs.reshape(len(members), 2 * nev, nev)
+            for m, d in enumerate(members):
+                own[d] = part[m]
+                product = jnp.dot(lhs, rhs[m], preferred_element_type=jnp.float32)
+                products[d] = product.astype(jnp.bfloat16).reshape(2, prows, nspin * nev)
+        own = jnp.take(jnp.stack(own, 0), directions, axis=0, mode="clip")
         ndisp = own.shape[0]
         gy_bits = [b for b in range(nbits) if (1 << b) < ny]
         grown = all_gather(
             own.reshape([ndisp, 2] + [1] * nbits + [rows, nev]), gy_bits, nbits, count, 2
         )
         elem = grown.reshape(ndisp, 2, ny * rows, nev)
-        contracted = jnp.take(jnp.stack(products, 0), directions, axis=0)
+        contracted = jnp.take(jnp.stack(products, 0), directions, axis=0, mode="clip")
         return (elem, contracted)
 
     return local

time: 159 us -> 193 us (1.21)
  waiting for transfers between devices: 40.8 us -> 78.1 us
  other arithmetic: 35 us -> 27.9 us
  matrix products: 10.8 us -> 13.9 us
  local copies, waits for them, and re-layouts: 27.7 us -> 30.3 us
  starting transfers between devices: 41.7 us -> 39.6 us
    ppermute x21 -> x16, waiting for transfers between devices: 12 us -> 39.6 us  [all_gather(): other = lax.ppermute(buf, ALL, xor_pairs(count, b))]
    ppermute x20 -> x15, waiting for transfers between devices: 28.8 us -> 38.5 us  [reduce_scatter(): buf = keep + lax.ppermute(send, ALL, xor_pairs(count, b))]
    select_n x5 -> x0, other arithmetic: 6.49 us -> none  [the longest x1 3.17 us: local(): contracted = jnp.take(jnp.stack(products, 0), directions, axis=0)]
    another operation x4 -> x8, local copies, waits for them, and re-layouts: 3.9 us -> 7.69 us  [the longest x4 6 us: local(): jnp.stack(products, 0)]
    dot_general x8, matrix products: 10.8 us -> 13.9 us  [the longest x4 7.13 us: local(): jnp.dot(left, disp[d].reshape(2 * depth, nev), preferred_element_type=jnp...]
    ppermute x21 -> x16, starting transfers between devices: 21.8 us -> 18.7 us  [all_gather(): other = lax.ppermute(buf, ALL, xor_pairs(count, b))]
    ppermute x1, starting transfers between devices: 0.01 us -> 2.97 us  [local(): lax.ppermute(ev[:, :, :, :, 0:1], 'gy', [(i, (i - 1) % ny) for i in range...]
    ppermute x1, starting transfers between devices: 2.97 us -> 0.01 us  [local(): lax.ppermute(src_y[:, :, :, :, ly - 1:], 'gy', [(i, (i + 1) % ny) for i i...]
  transfers between devices with their start and end apart: 45 -> 35, of which waited for: 18 -> 17; matrix products, arithmetic and copies ran while one was open for 33% -> 28% of each run, Pallas kernels for 0% -> 0%
where the time goes in v5:
time: 193 us; the launch traced here: 192 us
  waiting for transfers between devices  78.1 us (40%)
  starting transfers between devices  39.6 us (21%)
  local copies, waits for them, and re-layouts  30.3 us (16%)
  other arithmetic  27.9 us (14%)
  matrix products  13.9 us (7%)
  between operations  2.2 us (1%)
    ppermute x16, waiting for transfers between devices, all_gather(): other = lax.ppermute(buf, ALL, xor_pairs(count, b))  39.6 us
    ppermute x15, waiting for transfers between devices, reduce_scatter(): buf = keep + lax.ppermute(send, ALL, xor_pairs(count, b))  38.5 us
    ppermute x16, starting transfers between devices, all_gather(): other = lax.ppermute(buf, ALL, xor_pairs(count, b))  18.7 us
    ppermute x15, starting transfers between devices, reduce_scatter(): buf = keep + lax.ppermute(send, ALL, xor_pairs(count, b))  13.5 us
    dot_general x4, matrix products, local(): jnp.dot(left, disp[d].reshape(2 * depth, nev), preferred_element_type=jnp...  7.13 us
    dot_general x4, matrix products, local(): product = jnp.dot(lhs, rhs[m], preferred_element_type=jnp.float32)  6.75 us
    another operation x12, other arithmetic  6.07 us
    another operation x4, local copies, waits for them, and re-layouts, local(): jnp.stack(products, 0)  6 us
  transfers between devices with their start and end apart: 35, of which 17 were waited for; matrix products, arithmetic and copies ran while one was open for 28% of the time, Pallas kernels for 0%

profile of v5, /device:TPU:0, one launch (start us, length us, event | category | flops | bytes accessed | tf_op | source)
XLA Modules:
  0.0 191.9 jit_solution(7179330306377156825)
XLA Ops:
  0.6 1.9 slice.211
  2.5 3.0 %collective-permute-start.7 = (bf16[2,3,4,4,1,512]{5,4,3,2,1,0:T(2,128)(2,1)}, bf16[2,3,4,4,1,512]{5,4,3,2,1,0:T(2,128)(2,1)}, u32[]{:S(2)}, u32[]{:S(2)}) collective-permute-start(bf16[2,3,4,4,1,512]{5,4,3,2,1,0:T(2,128)(2,1)} %slice.211), channel_id=1, source_target_pairs={{0,1},{1,0},{2,3},{3,2},{4,5},{5,4},{6,7},{7,6},{8,9},{9,8},{10,11... | collective-permute-start | bytes 294920 | tf_op jit(solution)/shard_map/ppermute | solution.py:96
  5.5 1.0 slice_bitcast_fusion.20
  7.3 1.9 convert_element_type.62
  15.3 0.9 copy-done.5
  16.2 0.9 pad_maximum_fusion.18
  17.9 4.4 %collective-permute-start = (bf16[2,3,4,1,16,512]{5,4,3,2,1,0:T(8,128)(2,1)}, bf16[2,3,4,1,16,512]{5,4,3,2,1,0:T(8,128)(2,1)}, u32[]{:S(2)}, u32[]{:S(2)}) collective-permute-start(bf16[2,3,4,1,16,512]{5,4,3,2,1,0:T(8,128)(2,1)} %slice.157), channel_id=1, source_target_pairs={{0,30},{2,0},{4,2},{6,4},{8,6},{10,8},{12,10},{14,12},{16,14},{18,... | collective-permute-start | bytes 1179656 | tf_op jit(solution)/shard_map/ppermute | solution.py:94
  22.3 1.8 slice.210
  24.9 1.3 slice_bitcast_fusion
  26.1 1.0 fusion.29
  27.3 0.9 copy-done.13
  28.4 1.6 gather_fusion.1
  30.0 2.1 %copy.33 = bf16[2,64,4,1024]{3,2,1,0:T(4,128)(2,1)S(1)} copy(bf16[2,64,4,1024]{3,1,0,2:T(8,128)(2,1)} %bitcast.540) | data formatting | bytes 2097152 | tf_op jit(solution)/shard_map/jit(_take)/gather | solution.py:124
  32.2 1.1 reshape.2099
  33.3 1.9 %maximum_maximum_fusion = bf16[1024,1536]{1,0:T(8,128)(2,1)S(1)} fusion(bf16[512,768]{1,0:T(8,128)(2,1)} %get-tuple-element.37, bf16[512,768]{1,0:T(8,128)(2,1)S(1)} %copy-done.10, bf16[512,768]{1,0:T(8,128)(2,1)} %get-tuple-element.36), kind=kLoop, calls=%fused_computation.7 | loop fusion | flops 12582912 | bytes 5505024 | tf_op jit(solution)/shard_map/concatenate | solution.py:108
  35.4 1.6 maximum_convert_fusion.1
  39.3 1.8 fusion.32
  41.1 1.7 fusion.4
  42.8 1.8 convolution_bitcast_fusion
  44.7 1.2 fusion.3
  45.8 1.8 fusion.33
  49.4 1.2 maximum_convert_fusion
  52.8 1.8 convolution_bitcast_fusion.1
  56.2 12.6 %collective-permute-done.9 = f32[1,2,2,2,1,1,2,16,512]{8,7,1,6,5,4,3,2,0:T(8,128)S(1)} collective-permute-done((f32[1,2,2,2,1,1,2,16,512]{8,7,1,6,5,4,3,2,0:T(8,128)S(1)}, f32[1,2,2,2,1,1,2,16,512]{8,7,1,6,5,4,3,2,0:T(8,128)S(1)}, u32[]{:S(2)}, u32[]{:S(2)}) %collective-permute-start.9) | collective-permute-done | bytes 524320 | tf_op jit(solution)/shard_map/ppermute | solution.py:67
  69.3 1.8 collective-permute-start.16
  71.1 5.3 %collective-permute-done.10 = f32[1,2,2,1,1,1,2,16,512]{8,7,1,6,5,4,3,2,0:T(8,128)S(1)} collective-permute-done((f32[1,2,2,1,1,1,2,16,512]{8,7,1,6,5,4,3,2,0:T(8,128)S(1)}, f32[1,2,2,1,1,1,2,16,512]{8,7,1,6,5,4,3,2,0:T(8,128)S(1)}, u32[]{:S(2)}, u32[]{:S(2)}) %collective-permute-start.10) | collective-permute-done | bytes 262176 | tf_op jit(solution)/shard_map/ppermute | solution.py:67
  76.5 1.8 collective-permute-start.11
  79.0 2.5 %collective-permute-done.11 = f32[1,2,2,1,1,1,1,16,512]{8,7,1,6,5,4,3,2,0:T(8,128)S(1)} collective-permute-done((f32[1,2,2,1,1,1,1,16,512]{8,7,1,6,5,4,3,2,0:T(8,128)S(1)}, f32[1,2,2,1,1,1,1,16,512]{8,7,1,6,5,4,3,2,0:T(8,128)S(1)}, u32[]{:S(2)}, u32[]{:S(2)}) %collective-permute-start.11) | collective-permute-done | bytes 131104 | tf_op jit(solution)/shard_map/ppermute | solution.py:67
  81.5 1.1 collective-permute-start.12
  83.4 1.2 collective-permute-start.18
  84.6 3.3 %collective-permute-done.12 = f32[1,2,1,1,1,1,1,16,512]{8,7,1,6,5,4,3,2,0:T(8,128)S(1)} collective-permute-done((f32[1,2,1,1,1,1,1,16,512]{8,7,1,6,5,4,3,2,0:T(8,128)S(1)}, f32[1,2,1,1,1,1,1,16,512]{8,7,1,6,5,4,3,2,0:T(8,128)S(1)}, u32[]{:S(2)}, u32[]{:S(2)}) %collective-permute-start.12) | collective-permute-done | bytes 65568 | tf_op jit(solution)/shard_map/ppermute | solution.py:67
  88.8 1.8 collective-permute-start.3
  90.6 3.0 %collective-permute-start.30 = (bf16[1,2,1,1,1,1,1,16,512]{8,7,1,6,5,4,3,2,0:T(8,128)(2,1)S(1)}, bf16[1,2,1,1,1,1,1,16,512]{8,7,1,6,5,4,3,2,0:T(8,128)(2,1)S(1)}, u32[]{:S(2)}, u32[]{:S(2)}) collective-permute-start(bf16[1,2,1,1,1,1,1,16,512]{8,7,1,6,5,4,3,2,0:T(8,128)(2,1)S(1)} %get-tuple-element.64), channel_id=1, source_target_pairs={{0,16},{1,17},{2,18},{3,19},{4,20},{5,21},{6,22},{7,23},{8,24},{9,... | collective-permute-start | bytes 98312 | tf_op jit(solution)/shard_map/ppermute | solution.py:76
  93.6 1.0 collective-permute-start.26
  94.6 0.9 collective-permute-done.30
  96.0 16.3 %collective-permute-done.26 = bf16[1,2,2,1,1,1,1,16,512]{8,7,1,6,5,4,3,2,0:T(8,128)(2,1)S(1)} collective-permute-done((bf16[1,2,2,1,1,1,1,16,512]{8,7,1,6,5,4,3,2,0:T(8,128)(2,1)S(1)}, bf16[1,2,2,1,1,1,1,16,512]{8,7,1,6,5,4,3,2,0:T(8,128)(2,1)S(1)}, u32[]{:S(2)}, u32[]{:S(2)}) %collective-permute-start.26) | collective-permute-done | bytes 65568 | tf_op jit(solution)/shard_map/ppermute | solution.py:76
  112.3 2.1 %collective-permute-start.27 = (bf16[1,2,2,1,1,1,2,16,512]{8,7,1,6,5,4,3,2,0:T(8,128)(2,1)S(1)}, bf16[1,2,2,1,1,1,2,16,512]{8,7,1,6,5,4,3,2,0:T(8,128)(2,1)S(1)}, u32[]{:S(2)}, u32[]{:S(2)}) collective-permute-start(bf16[1,2,2,1,1,1,2,16,512]{8,7,1,6,5,4,3,2,0:T(8,128)(2,1)S(1)} %pad_maximum_fusion.20), channel_id=1, source_target_pairs={{0,8},{1,9},{2,10},{3,11},{4,12},{5,13},{6,14},{7,15},{8,0},{9,1},... | collective-permute-start | bytes 393224 | tf_op jit(solution)/shard_map/ppermute | solution.py:76
  115.0 1.8 collective-permute-start.32
  117.4 1.2 collective-permute-start.28
  118.6 5.4 %collective-permute-done.4 = f32[2,2,2,2,1,1,1,16,512]{8,7,6,5,4,3,2,1,0:T(8,128)S(1)} collective-permute-done((f32[2,2,2,2,1,1,1,16,512]{8,7,6,5,4,3,2,1,0:T(8,128)S(1)}, f32[2,2,2,2,1,1,1,16,512]{8,7,6,5,4,3,2,1,0:T(8,128)S(1)}, u32[]{:S(2)}, u32[]{:S(2)}) %collective-permute-start.4) | collective-permute-done | bytes 524320 | tf_op jit(solution)/shard_map/ppermute | solution.py:67
  124.1 1.8 collective-permute-start.5
  126.3 4.2 %collective-permute-done.5 = f32[2,2,2,1,1,1,1,16,512]{8,7,6,5,4,3,2,1,0:T(8,128)S(1)} collective-permute-done((f32[2,2,2,1,1,1,1,16,512]{8,7,6,5,4,3,2,1,0:T(8,128)S(1)}, f32[2,2,2,1,1,1,1,16,512]{8,7,6,5,4,3,2,1,0:T(8,128)S(1)}, u32[]{:S(2)}, u32[]{:S(2)}) %collective-permute-start.5) | collective-permute-done | bytes 262176 | tf_op jit(solution)/shard_map/ppermute | solution.py:67
  130.6 1.5 collective-permute-start.6
  132.2 4.4 %collective-permute-done.6 = f32[2,2,1,1,1,1,1,16,512]{8,7,6,5,4,3,2,1,0:T(8,128)S(1)} collective-permute-done((f32[2,2,1,1,1,1,1,16,512]{8,7,6,5,4,3,2,1,0:T(8,128)S(1)}, f32[2,2,1,1,1,1,1,16,512]{8,7,6,5,4,3,2,1,0:T(8,128)S(1)}, u32[]{:S(2)}, u32[]{:S(2)}) %collective-permute-start.6) | collective-permute-done | bytes 131104 | tf_op jit(solution)/shard_map/ppermute | solution.py:67
  136.6 1.7 collective-permute-start.20
  138.4 3.4 %collective-permute-done.20 = bf16[2,2,1,1,1,1,1,16,512]{8,7,6,5,4,3,2,1,0:T(8,128)(2,1)S(1)} collective-permute-done((bf16[2,2,1,1,1,1,1,16,512]{8,7,6,5,4,3,2,1,0:T(8,128)(2,1)S(1)}, bf16[2,2,1,1,1,1,1,16,512]{8,7,6,5,4,3,2,1,0:T(8,128)(2,1)S(1)}, u32[]{:S(2)}, u32[]{:S(2)}) %collective-permute-start.20) | collective-permute-done | bytes 65568 | tf_op jit(solution)/shard_map/ppermute | solution.py:76
  141.8 3.1 %collective-permute-start.21 = (bf16[2,2,2,1,1,1,1,16,512]{8,7,6,5,4,3,2,1,0:T(8,128)(2,1)S(1)}, bf16[2,2,2,1,1,1,1,16,512]{8,7,6,5,4,3,2,1,0:T(8,128)(2,1)S(1)}, u32[]{:S(2)}, u32[]{:S(2)}) collective-permute-start(bf16[2,2,2,1,1,1,1,16,512]{8,7,6,5,4,3,2,1,0:T(8,128)(2,1)S(1)} %pad_maximum_fusion.19), channel_id=1, source_target_pairs={{0,8},{1,9},{2,10},{3,11},{4,12},{5,13},{6,14},{7,15},{8,0},{9,1},... | collective-permute-start | bytes 393224 | tf_op jit(solution)/shard_map/ppermute | solution.py:76
  145.9 2.1 %collective-permute-done.21 = bf16[2,2,2,1,1,1,1,16,512]{8,7,6,5,4,3,2,1,0:T(8,128)(2,1)S(1)} collective-permute-done((bf16[2,2,2,1,1,1,1,16,512]{8,7,6,5,4,3,2,1,0:T(8,128)(2,1)S(1)}, bf16[2,2,2,1,1,1,1,16,512]{8,7,6,5,4,3,2,1,0:T(8,128)(2,1)S(1)}, u32[]{:S(2)}, u32[]{:S(2)}) %collective-permute-start.21) | collective-permute-done | bytes 131104 | tf_op jit(solution)/shard_map/ppermute | solution.py:76
  149.0 5.7 %collective-permute-done.22 = bf16[2,2,2,2,1,1,1,16,512]{8,7,6,5,4,3,2,1,0:T(8,128)(2,1)S(1)} collective-permute-done((bf16[2,2,2,2,1,1,1,16,512]{8,7,6,5,4,3,2,1,0:T(8,128)(2,1)S(1)}, bf16[2,2,2,2,1,1,1,16,512]{8,7,6,5,4,3,2,1,0:T(8,128)(2,1)S(1)}, u32[]{:S(2)}, u32[]{:S(2)}) %collective-permute-start.22) | collective-permute-done | bytes 262176 | tf_op jit(solution)/shard_map/ppermute | solution.py:76
  155.6 2.7 %collective-permute-start.23 = (bf16[2,2,2,2,2,1,1,16,512]{8,7,6,5,4,3,2,1,0:T(8,128)(2,1)}, bf16[2,2,2,2,2,1,1,16,512]{8,7,6,5,4,3,2,1,0:T(8,128)(2,1)S(1)}, u32[]{:S(2)}, u32[]{:S(2)}) collective-permute-start(bf16[2,2,2,2,2,1,1,16,512]{8,7,6,5,4,3,2,1,0:T(8,128)(2,1)} %pad_maximum_fusion.10), channel_id=1, source_target_pairs={{0,1},{1,0},{2,3},{3,2},{4,5},{5,4},{6,7},{7,6},{8,9},{9,8},{10,11... | collective-permute-start | bytes 1572872 | tf_op jit(solution)/shard_map/ppermute | solution.py:76
  159.5 1.1 copy.35
  160.6 6.6 %collective-permute-done.23 = bf16[2,2,2,2,2,1,1,16,512]{8,7,6,5,4,3,2,1,0:T(8,128)(2,1)S(1)} collective-permute-done((bf16[2,2,2,2,2,1,1,16,512]{8,7,6,5,4,3,2,1,0:T(8,128)(2,1)}, bf16[2,2,2,2,2,1,1,16,512]{8,7,6,5,4,3,2,1,0:T(8,128)(2,1)S(1)}, u32[]{:S(2)}, u32[]{:S(2)}) %collective-permute-start.23) | collective-permute-done | bytes 524320 | tf_op jit(solution)/shard_map/ppermute | solution.py:76
  167.3 1.1 pad_maximum_fusion.6
  169.5 3.0 %convolution_convert_fusion.1 = bf16[512,512]{1,0:T(8,128)(2,1)} fusion(bf16[512,1024]{1,0:T(8,128)(2,1)} %reshape.2099, bf16[1024,512]{1,0:T(8,128)(2,1)} %bitcast.553), kind=kOutput, calls=%fused_computation.25 | convolution fusion | flops 537133056 | bytes 2621440 | tf_op jit(solution)/shard_map/dot_general | solution.py:145
  172.5 1.4 stack_reshape.14
  173.9 4.0 %collective-permute-done.19 = f32[4,2,1,1,1,1,1,16,512]{8,7,1,0,6,5,4,3,2:T(8,128)} collective-permute-done((f32[4,2,1,1,1,1,1,16,512]{8,7,1,0,6,5,4,3,2:T(8,128)S(1)}, f32[4,2,1,1,1,1,1,16,512]{8,7,1,0,6,5,4,3,2:T(8,128)}, u32[]{:S(2)}, u32[]{:S(2)}) %collective-permute-start.19) | collective-permute-done | bytes 262176 | tf_op jit(solution)/shard_map/ppermute | solution.py:76
  177.9 1.0 broadcast_select_fusion.21
  180.1 1.0 copy-done.12
  181.1 1.5 convolution_convert_fusion.3
  182.6 2.2 %stack_reshape.12 = bf16[1,2,64,2048]{3,2,1,0:T(8,128)(2,1)} reshape(bf16[512,512]{1,0:T(8,128)(2,1)} %convolution_convert_fusion.3) | data formatting | bytes 1048576 | tf_op jit(solution)/shard_map/stack;reshape | solution.py:154
  184.8 1.5 convolution_convert_fusion
  186.3 2.2 %stack_reshape.15 = bf16[1,2,64,2048]{3,2,1,0:T(8,128)(2,1)} reshape(bf16[512,512]{1,0:T(8,128)(2,1)} %convolution_convert_fusion) | data formatting | bytes 1048576 | tf_op jit(solution)/shard_map/stack;reshape | solution.py:154
  188.5 1.5 pad_maximum_fusion
  189.9 2.0 %gather_fusion.2 = bf16[4,2,64,2048]{3,2,1,0:T(8,128)(2,1)} fusion(bf16[4,2,64,2048]{3,2,1,0:T(8,128)(2,1)S(1)} %pad_maximum_fusion, s32[1024]{0:T(1024)S(1)} %pad_clamp_fusion.1), kind=kCustom, calls=%fused_computation.2 | custom fusion | bytes 4194320 | tf_op jit(solution)/shard_map/jit(_take)/gather | solution.py:154
  (271 shorter events, 27.8 us)
Async XLA Ops:
  2.5 32.8 %collective-permute-start.7 = (bf16[2,3,4,4,1,512]{5,4,3,2,1,0:T(2,128)(2,1)}, bf16[2,3,4,4,1,512]{5,4,3,2,1,0:T(2,128)(2,1)}, u32[]{:S(2)}, u32[]{:S(2)}) collective-permute-start(bf16[2,3,4,4,1,512]{5,4,3,2,1,0:T(2,128)(2,1)} %slice.211), channel_id=1, source_target_pairs={{0,1},{1,0},{2,3},{3,2},{4,5},{5,4},{6,7},{7,6},{8,9},{9,8},{10,11... | collective-permute-start | bytes 294920 | tf_op jit(solution)/shard_map/ppermute | solution.py:96
  7.2 1.9 %copy-start.14 = (f32[4,4,16]{2,1,0:T(4,128)}, f32[4,4,16]{2,1,0:T(4,128)S(1)}, u32[]{:S(2)}) copy-start(f32[4,4,16]{2,1,0:T(4,128)S(1)} %get-tuple-element.108) | copy-start | bytes 3076
  7.2 2.0 %copy-start.20 = (f32[4,4,16]{2,1,0:T(4,128)}, f32[4,4,16]{2,1,0:T(4,128)S(1)}, u32[]{:S(2)}) copy-start(f32[4,4,16]{2,1,0:T(4,128)S(1)} %get-tuple-element.114) | copy-start | bytes 3076
  7.2 2.0 %copy-start.22 = (f32[4,4,16]{2,1,0:T(4,128)}, f32[4,4,16]{2,1,0:T(4,128)S(1)}, u32[]{:S(2)}) copy-start(f32[4,4,16]{2,1,0:T(4,128)S(1)} %get-tuple-element.102) | copy-start | bytes 3076
  7.2 2.5 %copy-start.18 = (f32[4,4,16]{2,1,0:T(4,128)}, f32[4,4,16]{2,1,0:T(4,128)S(1)}, u32[]{:S(2)}) copy-start(f32[4,4,16]{2,1,0:T(4,128)S(1)} %get-tuple-element.112) | copy-start | bytes 3076
  7.2 2.5 %copy-start.26 = (f32[4,4,16]{2,1,0:T(4,128)}, f32[4,4,16]{2,1,0:T(4,128)S(1)}, u32[]{:S(2)}) copy-start(f32[4,4,16]{2,1,0:T(4,128)S(1)} %get-tuple-element.118) | copy-start | bytes 3076
  7.2 3.0 %copy-start.16 = (f32[4,4,16]{2,1,0:T(4,128)}, f32[4,4,16]{2,1,0:T(4,128)S(1)}, u32[]{:S(2)}) copy-start(f32[4,4,16]{2,1,0:T(4,128)S(1)} %get-tuple-element.110) | copy-start | bytes 3076
  7.2 3.0 %copy-start.24 = (f32[4,4,16]{2,1,0:T(4,128)}, f32[4,4,16]{2,1,0:T(4,128)S(1)}, u32[]{:S(2)}) copy-start(f32[4,4,16]{2,1,0:T(4,128)S(1)} %get-tuple-element.116) | copy-start | bytes 3076
  12.8 31.9 %collective-permute-start.13 = (bf16[2,3,4,1,16,512]{5,4,3,2,1,0:T(8,128)(2,1)}, bf16[2,3,4,1,16,512]{5,4,3,2,1,0:T(8,128)(2,1)}, u32[]{:S(2)}, u32[]{:S(2)}) collective-permute-start(bf16[2,3,4,1,16,512]{5,4,3,2,1,0:T(8,128)(2,1)} %pad_maximum_fusion.13), channel_id=1, source_target_pairs={{0,2},{2,4},{4,6},{6,8},{8,10},{10,12},{12,14},{14,16},{16,18},{18... | collective-permute-start | bytes 1179656 | tf_op jit(solution)/shard_map/ppermute | solution.py:95
  15.1 2.0 %copy-start = (bf16[2,3,4,4,16,512]{5,4,3,2,1,0:T(8,128)(2,1)S(1)}, bf16[2,3,4,4,16,512]{5,4,3,2,1,0:T(8,128)(2,1)}, u32[]{:S(2)}) copy-start(bf16[2,3,4,4,16,512]{5,4,3,2,1,0:T(8,128)(2,1)} %param.5) | copy-start | bytes 4718596
  15.3 1.8 copy-start.7
  17.1 23.9 %collective-permute-start.1 = (bf16[2,3,4,4,1,512]{5,4,3,2,1,0:T(2,128)(2,1)}, bf16[2,3,4,4,1,512]{5,4,3,2,1,0:T(2,128)(2,1)}, u32[]{:S(2)}, u32[]{:S(2)}) collective-permute-start(bf16[2,3,4,4,1,512]{5,4,3,2,1,0:T(2,128)(2,1)} %pad_maximum_fusion.18), channel_id=1, source_target_pairs={{0,1},{1,0},{2,3},{3,2},{4,5},{5,4},{6,7},{7,6},{8,9},{9,8},{10,11... | collective-permute-start | bytes 294920 | tf_op jit(solution)/shard_map/ppermute | solution.py:97
  17.9 31.5 %collective-permute-start = (bf16[2,3,4,1,16,512]{5,4,3,2,1,0:T(8,128)(2,1)}, bf16[2,3,4,1,16,512]{5,4,3,2,1,0:T(8,128)(2,1)}, u32[]{:S(2)}, u32[]{:S(2)}) collective-permute-start(bf16[2,3,4,1,16,512]{5,4,3,2,1,0:T(8,128)(2,1)} %slice.157), channel_id=1, source_target_pairs={{0,30},{2,0},{4,2},{6,4},{8,6},{10,8},{12,10},{14,12},{16,14},{18,... | collective-permute-start | bytes 1179656 | tf_op jit(solution)/shard_map/ppermute | solution.py:94
  30.0 3.2 %copy-start.10 = (bf16[512,768]{1,0:T(8,128)(2,1)S(1)}, bf16[512,768]{1,0:T(8,128)(2,1)}, u32[]{:S(2)}) copy-start(bf16[512,768]{1,0:T(8,128)(2,1)} %fusion.29) | copy-start | bytes 2359300
  33.3 2.0 %copy-start.65 = (s32[4]{0:T(128)S(1)}, s32[4]{0:T(128)}, u32[]{:S(2)}) copy-start(s32[4]{0:T(128)} %param.7) | copy-start | bytes 52
  33.3 2.1 %copy-start.9 = (bf16[2,3,4,4,15,512]{5,4,3,2,1,0:T(8,128)(2,1)S(1)}, bf16[2,3,4,4,15,512]{5,4,3,2,1,0:T(8,128)(2,1)}, u32[]{:S(2)}) copy-start(bf16[2,3,4,4,15,512]{5,4,3,2,1,0:T(8,128)(2,1)} %slice.210) | copy-start | bytes 4423684
  35.3 1.8 copy-start.41
  35.3 1.8 copy-start.43
  35.3 1.8 copy-start.45
  35.3 1.8 copy-start.61
  35.3 1.8 copy-start.62
  35.3 1.8 copy-start.63
  39.2 1.8 copy-start.6
  39.3 1.8 copy-start.8
  42.8 1.8 copy-start.2
  42.8 1.8 copy-start.4
  48.6 6.1 %collective-permute-start.8 = (f32[1,2,2,2,2,1,2,16,512]{8,7,1,6,5,4,3,2,0:T(8,128)S(1)}, f32[1,2,2,2,2,1,2,16,512]{8,7,1,6,5,4,3,2,0:T(8,128)S(1)}, u32[]{:S(2)}, u32[]{:S(2)}) collective-permute-start(f32[1,2,2,2,2,1,2,16,512]{8,7,1,6,5,4,3,2,0:T(8,128)S(1)} %bitcast.552), channel_id=1, source_target_pairs={{0,2},{1,3},{2,0},{3,1},{4,6},{5,7},{6,4},{7,5},{8,10},{9,11},{10,... | collective-permute-start | bytes 3145736 | tf_op jit(solution)/shard_map/ppermute | solution.py:67
  48.8 1.9 copy-start.23
  48.8 1.9 copy-start.25
  48.8 1.9 copy-start.27
  48.8 1.9 copy-start.52
  48.8 1.9 copy-start.53
  48.8 1.9 copy-start.54
  48.8 6.2 %collective-permute-start.14 = (f32[1,2,2,2,2,1,2,16,512]{8,7,1,6,5,4,3,2,0:T(8,128)S(1)}, f32[1,2,2,2,2,1,2,16,512]{8,7,1,6,5,4,3,2,0:T(8,128)S(1)}, u32[]{:S(2)}, u32[]{:S(2)}) collective-permute-start(f32[1,2,2,2,2,1,2,16,512]{8,7,1,6,5,4,3,2,0:T(8,128)S(1)} %bitcast.551), channel_id=1, source_target_pairs={{0,2},{1,3},{2,0},{3,1},{4,6},{5,7},{6,4},{7,5},{8,10},{9,11},{10,... | collective-permute-start | bytes 3145736 | tf_op jit(solution)/shard_map/ppermute | solution.py:67
  54.9 13.9 %collective-permute-start.9 = (f32[1,2,2,2,1,1,2,16,512]{8,7,1,6,5,4,3,2,0:T(8,128)S(1)}, f32[1,2,2,2,1,1,2,16,512]{8,7,1,6,5,4,3,2,0:T(8,128)S(1)}, u32[]{:S(2)}, u32[]{:S(2)}) collective-permute-start(f32[1,2,2,2,1,1,2,16,512]{8,7,1,6,5,4,3,2,0:T(8,128)S(1)} %constant_dynamic-slice_fusion.9), channel_id=1, source_target_pairs={{0,4},{1,5},{2,6},{3,7},{4,0},{5,1},{6,2},{7,3},{8,12},{9,13},{10,... | collective-permute-start | bytes 1572872 | tf_op jit(solution)/shard_map/ppermute | solution.py:67
  55.3 13.9 %collective-permute-start.15 = (f32[1,2,2,1,2,1,2,16,512]{8,7,1,6,5,4,3,2,0:T(8,128)S(1)}, f32[1,2,2,1,2,1,2,16,512]{8,7,1,6,5,4,3,2,0:T(8,128)S(1)}, u32[]{:S(2)}, u32[]{:S(2)}) collective-permute-start(f32[1,2,2,1,2,1,2,16,512]{8,7,1,6,5,4,3,2,0:T(8,128)S(1)} %constant_dynamic-slice_fusion.3), channel_id=1, source_target_pairs={{0,8},{1,9},{2,10},{3,11},{4,12},{5,13},{6,14},{7,15},{8,0},{9,1},... | collective-permute-start | bytes 1572872 | tf_op jit(solution)/shard_map/ppermute | solution.py:67
  56.1 31.9 %collective-permute-start.2 = (f32[2,2,2,2,2,1,2,16,512]{8,7,6,5,4,3,2,1,0:T(8,128)S(1)}, f32[2,2,2,2,2,1,2,16,512]{8,7,6,5,4,3,2,1,0:T(8,128)S(1)}, u32[]{:S(2)}, u32[]{:S(2)}) collective-permute-start(f32[2,2,2,2,2,1,2,16,512]{8,7,6,5,4,3,2,1,0:T(8,128)S(1)} %fusion), channel_id=1, source_target_pairs={{0,2},{1,3},{2,0},{3,1},{4,6},{5,7},{6,4},{7,5},{8,10},{9,11},{10,... | collective-permute-start | bytes 6291464 | tf_op jit(solution)/shard_map/ppermute | solution.py:67
  69.0 7.4 %collective-permute-start.10 = (f32[1,2,2,1,1,1,2,16,512]{8,7,1,6,5,4,3,2,0:T(8,128)S(1)}, f32[1,2,2,1,1,1,2,16,512]{8,7,1,6,5,4,3,2,0:T(8,128)S(1)}, u32[]{:S(2)}, u32[]{:S(2)}) collective-permute-start(f32[1,2,2,1,1,1,2,16,512]{8,7,1,6,5,4,3,2,0:T(8,128)S(1)} %constant_dynamic-slice_fusion.8), channel_id=1, source_target_pairs={{0,8},{1,9},{2,10},{3,11},{4,12},{5,13},{6,14},{7,15},{8,0},{9,1},... | collective-permute-start | bytes 786440 | tf_op jit(solution)/shard_map/ppermute | solution.py:67
  69.3 9.0 %collective-permute-start.16 = (f32[1,2,2,1,2,1,1,16,512]{8,7,1,6,5,4,3,2,0:T(8,128)S(1)}, f32[1,2,2,1,2,1,1,16,512]{8,7,1,6,5,4,3,2,0:T(8,128)S(1)}, u32[]{:S(2)}, u32[]{:S(2)}) collective-permute-start(f32[1,2,2,1,2,1,1,16,512]{8,7,1,6,5,4,3,2,0:T(8,128)S(1)} %constant_dynamic-slice_fusion.2), channel_id=1, source_target_pairs={{0,1},{1,0},{2,3},{3,2},{4,5},{5,4},{6,7},{7,6},{8,9},{9,8},{10,11... | collective-permute-start | bytes 786440 | tf_op jit(solution)/shard_map/ppermute | solution.py:67
  76.5 5.0 %collective-permute-start.11 = (f32[1,2,2,1,1,1,1,16,512]{8,7,1,6,5,4,3,2,0:T(8,128)S(1)}, f32[1,2,2,1,1,1,1,16,512]{8,7,1,6,5,4,3,2,0:T(8,128)S(1)}, u32[]{:S(2)}, u32[]{:S(2)}) collective-permute-start(f32[1,2,2,1,1,1,1,16,512]{8,7,1,6,5,4,3,2,0:T(8,128)S(1)} %constant_dynamic-slice_fusion.7), channel_id=1, source_target_pairs={{0,1},{1,0},{2,3},{3,2},{4,5},{5,4},{6,7},{7,6},{8,9},{9,8},{10,11... | collective-permute-start | bytes 393224 | tf_op jit(solution)/shard_map/ppermute | solution.py:67
  78.3 5.0 %collective-permute-start.17 = (f32[1,2,2,1,1,1,1,16,512]{8,7,1,6,5,4,3,2,0:T(8,128)S(1)}, f32[1,2,2,1,1,1,1,16,512]{8,7,1,6,5,4,3,2,0:T(8,128)S(1)}, u32[]{:S(2)}, u32[]{:S(2)}) collective-permute-start(f32[1,2,2,1,1,1,1,16,512]{8,7,1,6,5,4,3,2,0:T(8,128)S(1)} %constant_dynamic-slice_fusion.1), channel_id=1, source_target_pairs={{0,4},{1,5},{2,6},{3,7},{4,0},{5,1},{6,2},{7,3},{8,12},{9,13},{10,... | collective-permute-start | bytes 393224 | tf_op jit(solution)/shard_map/ppermute | solution.py:67
  81.5 6.4 %collective-permute-start.12 = (f32[1,2,1,1,1,1,1,16,512]{8,7,1,6,5,4,3,2,0:T(8,128)S(1)}, f32[1,2,1,1,1,1,1,16,512]{8,7,1,6,5,4,3,2,0:T(8,128)S(1)}, u32[]{:S(2)}, u32[]{:S(2)}) collective-permute-start(f32[1,2,1,1,1,1,1,16,512]{8,7,1,6,5,4,3,2,0:T(8,128)S(1)} %constant_dynamic-slice_fusion.6), channel_id=1, source_target_pairs={{0,16},{1,17},{2,18},{3,19},{4,20},{5,21},{6,22},{7,23},{8,24},{9,... | collective-permute-start | bytes 196616 | tf_op jit(solution)/shard_map/ppermute | solution.py:67
  83.4 7.2 %collective-permute-start.18 = (f32[1,2,1,1,1,1,1,16,512]{8,7,1,6,5,4,3,2,0:T(8,128)S(1)}, f32[1,2,1,1,1,1,1,16,512]{8,7,1,6,5,4,3,2,0:T(8,128)S(1)}, u32[]{:S(2)}, u32[]{:S(2)}) collective-permute-start(f32[1,2,1,1,1,1,1,16,512]{8,7,1,6,5,4,3,2,0:T(8,128)S(1)} %constant_dynamic-slice_fusion), channel_id=1, source_target_pairs={{0,16},{1,17},{2,18},{3,19},{4,20},{5,21},{6,22},{7,23},{8,24},{9,... | collective-permute-start | bytes 196616 | tf_op jit(solution)/shard_map/ppermute | solution.py:67
  87.9 5.7 %collective-permute-start.25 = (bf16[1,2,1,1,1,1,1,16,512]{8,7,1,6,5,4,3,2,0:T(8,128)(2,1)S(1)}, bf16[1,2,1,1,1,1,1,16,512]{8,7,1,6,5,4,3,2,0:T(8,128)(2,1)S(1)}, u32[]{:S(2)}, u32[]{:S(2)}) collective-permute-start(bf16[1,2,1,1,1,1,1,16,512]{8,7,1,6,5,4,3,2,0:T(8,128)(2,1)S(1)} %get-tuple-element.62), channel_id=1, source_target_pairs={{0,16},{1,17},{2,18},{3,19},{4,20},{5,21},{6,22},{7,23},{8,24},{9,... | collective-permute-start | bytes 98312 | tf_op jit(solution)/shard_map/ppermute | solution.py:76
  88.8 25.6 %collective-permute-start.3 = (f32[2,2,2,2,2,1,1,16,512]{8,7,6,5,4,3,2,1,0:T(8,128)S(1)}, f32[2,2,2,2,2,1,1,16,512]{8,7,6,5,4,3,2,1,0:T(8,128)S(1)}, u32[]{:S(2)}, u32[]{:S(2)}) collective-permute-start(f32[2,2,2,2,2,1,1,16,512]{8,7,6,5,4,3,2,1,0:T(8,128)S(1)} %constant_dynamic-slice_fusion.15), channel_id=1, source_target_pairs={{0,1},{1,0},{2,3},{3,2},{4,5},{5,4},{6,7},{7,6},{8,9},{9,8},{10,11... | collective-permute-start | bytes 3145736 | tf_op jit(solution)/shard_map/ppermute | solution.py:67
  90.6 4.9 %collective-permute-start.30 = (bf16[1,2,1,1,1,1,1,16,512]{8,7,1,6,5,4,3,2,0:T(8,128)(2,1)S(1)}, bf16[1,2,1,1,1,1,1,16,512]{8,7,1,6,5,4,3,2,0:T(8,128)(2,1)S(1)}, u32[]{:S(2)}, u32[]{:S(2)}) collective-permute-start(bf16[1,2,1,1,1,1,1,16,512]{8,7,1,6,5,4,3,2,0:T(8,128)(2,1)S(1)} %get-tuple-element.64), channel_id=1, source_target_pairs={{0,16},{1,17},{2,18},{3,19},{4,20},{5,21},{6,22},{7,23},{8,24},{9,... | collective-permute-start | bytes 98312 | tf_op jit(solution)/shard_map/ppermute | solution.py:76
  93.6 18.7 %collective-permute-start.26 = (bf16[1,2,2,1,1,1,1,16,512]{8,7,1,6,5,4,3,2,0:T(8,128)(2,1)S(1)}, bf16[1,2,2,1,1,1,1,16,512]{8,7,1,6,5,4,3,2,0:T(8,128)(2,1)S(1)}, u32[]{:S(2)}, u32[]{:S(2)}) collective-permute-start(bf16[1,2,2,1,1,1,1,16,512]{8,7,1,6,5,4,3,2,0:T(8,128)(2,1)S(1)} %pad_maximum_fusion.22), channel_id=1, source_target_pairs={{0,1},{1,0},{2,3},{3,2},{4,5},{5,4},{6,7},{7,6},{8,9},{9,8},{10,11... | collective-permute-start | bytes 196616 | tf_op jit(solution)/shard_map/ppermute | solution.py:76
  95.5 19.4 %collective-permute-start.31 = (bf16[1,2,2,1,1,1,1,16,512]{8,7,1,6,5,4,3,2,0:T(8,128)(2,1)S(1)}, bf16[1,2,2,1,1,1,1,16,512]{8,7,1,6,5,4,3,2,0:T(8,128)(2,1)S(1)}, u32[]{:S(2)}, u32[]{:S(2)}) collective-permute-start(bf16[1,2,2,1,1,1,1,16,512]{8,7,1,6,5,4,3,2,0:T(8,128)(2,1)S(1)} %pad_maximum_fusion.23), channel_id=1, source_target_pairs={{0,4},{1,5},{2,6},{3,7},{4,0},{5,1},{6,2},{7,3},{8,12},{9,13},{10,... | collective-permute-start | bytes 196616 | tf_op jit(solution)/shard_map/ppermute | solution.py:76
  112.3 5.0 %collective-permute-start.27 = (bf16[1,2,2,1,1,1,2,16,512]{8,7,1,6,5,4,3,2,0:T(8,128)(2,1)S(1)}, bf16[1,2,2,1,1,1,2,16,512]{8,7,1,6,5,4,3,2,0:T(8,128)(2,1)S(1)}, u32[]{:S(2)}, u32[]{:S(2)}) collective-permute-start(bf16[1,2,2,1,1,1,2,16,512]{8,7,1,6,5,4,3,2,0:T(8,128)(2,1)S(1)} %pad_maximum_fusion.20), channel_id=1, source_target_pairs={{0,8},{1,9},{2,10},{3,11},{4,12},{5,13},{6,14},{7,15},{8,0},{9,1},... | collective-permute-start | bytes 393224 | tf_op jit(solution)/shard_map/ppermute | solution.py:76
  114.7 9.3 %collective-permute-start.4 = (f32[2,2,2,2,1,1,1,16,512]{8,7,6,5,4,3,2,1,0:T(8,128)S(1)}, f32[2,2,2,2,1,1,1,16,512]{8,7,6,5,4,3,2,1,0:T(8,128)S(1)}, u32[]{:S(2)}, u32[]{:S(2)}) collective-permute-start(f32[2,2,2,2,1,1,1,16,512]{8,7,6,5,4,3,2,1,0:T(8,128)S(1)} %constant_dynamic-slice_fusion.14), channel_id=1, source_target_pairs={{0,4},{1,5},{2,6},{3,7},{4,0},{5,1},{6,2},{7,3},{8,12},{9,13},{10,... | collective-permute-start | bytes 1572872 | tf_op jit(solution)/shard_map/ppermute | solution.py:67
  115.0 10.9 %collective-permute-start.32 = (bf16[1,2,2,1,2,1,1,16,512]{8,7,1,6,5,4,3,2,0:T(8,128)(2,1)S(1)}, bf16[1,2,2,1,2,1,1,16,512]{8,7,1,6,5,4,3,2,0:T(8,128)(2,1)S(1)}, u32[]{:S(2)}, u32[]{:S(2)}) collective-permute-start(bf16[1,2,2,1,2,1,1,16,512]{8,7,1,6,5,4,3,2,0:T(8,128)(2,1)S(1)} %pad_maximum_fusion.21), channel_id=1, source_target_pairs={{0,1},{1,0},{2,3},{3,2},{4,5},{5,4},{6,7},{7,6},{8,9},{9,8},{10,11... | collective-permute-start | bytes 393224 | tf_op jit(solution)/shard_map/ppermute | solution.py:76
  117.4 14.7 %collective-permute-start.28 = (bf16[1,2,2,2,1,1,2,16,512]{8,7,1,6,5,4,3,2,0:T(8,128)(2,1)S(1)}, bf16[1,2,2,2,1,1,2,16,512]{8,7,1,6,5,4,3,2,0:T(8,128)(2,1)S(1)}, u32[]{:S(2)}, u32[]{:S(2)}) collective-permute-start(bf16[1,2,2,2,1,1,2,16,512]{8,7,1,6,5,4,3,2,0:T(8,128)(2,1)S(1)} %pad_maximum_fusion.16), channel_id=1, source_target_pairs={{0,4},{1,5},{2,6},{3,7},{4,0},{5,1},{6,2},{7,3},{8,12},{9,13},{10,... | collective-permute-start | bytes 786440 | tf_op jit(solution)/shard_map/ppermute | solution.py:76
  124.1 6.4 %collective-permute-start.5 = (f32[2,2,2,1,1,1,1,16,512]{8,7,6,5,4,3,2,1,0:T(8,128)S(1)}, f32[2,2,2,1,1,1,1,16,512]{8,7,6,5,4,3,2,1,0:T(8,128)S(1)}, u32[]{:S(2)}, u32[]{:S(2)}) collective-permute-start(f32[2,2,2,1,1,1,1,16,512]{8,7,6,5,4,3,2,1,0:T(8,128)S(1)} %constant_dynamic-slice_fusion.13), channel_id=1, source_target_pairs={{0,8},{1,9},{2,10},{3,11},{4,12},{5,13},{6,14},{7,15},{8,0},{9,1},... | collective-permute-start | bytes 786440 | tf_op jit(solution)/shard_map/ppermute | solution.py:67
  126.0 19.0 %collective-permute-start.33 = (bf16[1,2,2,1,2,1,2,16,512]{8,7,1,6,5,4,3,2,0:T(8,128)(2,1)S(1)}, bf16[1,2,2,1,2,1,2,16,512]{8,7,1,6,5,4,3,2,0:T(8,128)(2,1)S(1)}, u32[]{:S(2)}, u32[]{:S(2)}) collective-permute-start(bf16[1,2,2,1,2,1,2,16,512]{8,7,1,6,5,4,3,2,0:T(8,128)(2,1)S(1)} %pad_maximum_fusion.17), channel_id=1, source_target_pairs={{0,8},{1,9},{2,10},{3,11},{4,12},{5,13},{6,14},{7,15},{8,0},{9,1},... | collective-permute-start | bytes 786440 | tf_op jit(solution)/shard_map/ppermute | solution.py:76
  130.6 5.9 %collective-permute-start.6 = (f32[2,2,1,1,1,1,1,16,512]{8,7,6,5,4,3,2,1,0:T(8,128)S(1)}, f32[2,2,1,1,1,1,1,16,512]{8,7,6,5,4,3,2,1,0:T(8,128)S(1)}, u32[]{:S(2)}, u32[]{:S(2)}) collective-permute-start(f32[2,2,1,1,1,1,1,16,512]{8,7,6,5,4,3,2,1,0:T(8,128)S(1)} %constant_dynamic-slice_fusion.12), channel_id=1, source_target_pairs={{0,16},{1,17},{2,18},{3,19},{4,20},{5,21},{6,22},{7,23},{8,24},{9,... | collective-permute-start | bytes 393224 | tf_op jit(solution)/shard_map/ppermute | solution.py:67
  136.6 5.2 %collective-permute-start.20 = (bf16[2,2,1,1,1,1,1,16,512]{8,7,6,5,4,3,2,1,0:T(8,128)(2,1)S(1)}, bf16[2,2,1,1,1,1,1,16,512]{8,7,6,5,4,3,2,1,0:T(8,128)(2,1)S(1)}, u32[]{:S(2)}, u32[]{:S(2)}) collective-permute-start(bf16[2,2,1,1,1,1,1,16,512]{8,7,6,5,4,3,2,1,0:T(8,128)(2,1)S(1)} %get-tuple-element.2), channel_id=1, source_target_pairs={{0,16},{1,17},{2,18},{3,19},{4,20},{5,21},{6,22},{7,23},{8,24},{9,... | collective-permute-start | bytes 196616 | tf_op jit(solution)/shard_map/ppermute | solution.py:76
  138.3 10.4 %collective-permute-start.29 = (bf16[1,2,2,2,2,1,2,16,512]{8,7,1,6,5,4,3,2,0:T(8,128)(2,1)S(1)}, bf16[1,2,2,2,2,1,2,16,512]{8,7,1,6,5,4,3,2,0:T(8,128)(2,1)S(1)}, u32[]{:S(2)}, u32[]{:S(2)}) collective-permute-start(bf16[1,2,2,2,2,1,2,16,512]{8,7,1,6,5,4,3,2,0:T(8,128)(2,1)S(1)} %pad_maximum_fusion.11), channel_id=1, source_target_pairs={{0,2},{1,3},{2,0},{3,1},{4,6},{5,7},{6,4},{7,5},{8,10},{9,11},{10,... | collective-permute-start | bytes 1572872 | tf_op jit(solution)/shard_map/ppermute | solution.py:76
  141.8 6.1 %collective-permute-start.21 = (bf16[2,2,2,1,1,1,1,16,512]{8,7,6,5,4,3,2,1,0:T(8,128)(2,1)S(1)}, bf16[2,2,2,1,1,1,1,16,512]{8,7,6,5,4,3,2,1,0:T(8,128)(2,1)S(1)}, u32[]{:S(2)}, u32[]{:S(2)}) collective-permute-start(bf16[2,2,2,1,1,1,1,16,512]{8,7,6,5,4,3,2,1,0:T(8,128)(2,1)S(1)} %pad_maximum_fusion.19), channel_id=1, source_target_pairs={{0,8},{1,9},{2,10},{3,11},{4,12},{5,13},{6,14},{7,15},{8,0},{9,1},... | collective-permute-start | bytes 393224 | tf_op jit(solution)/shard_map/ppermute | solution.py:76
  145.9 13.4 %collective-permute-start.34 = (bf16[1,2,2,2,2,1,2,16,512]{8,7,1,6,5,4,3,2,0:T(8,128)(2,1)}, bf16[1,2,2,2,2,1,2,16,512]{8,7,1,6,5,4,3,2,0:T(8,128)(2,1)S(1)}, u32[]{:S(2)}, u32[]{:S(2)}) collective-permute-start(bf16[1,2,2,2,2,1,2,16,512]{8,7,1,6,5,4,3,2,0:T(8,128)(2,1)} %pad_maximum_fusion.12), channel_id=1, source_target_pairs={{0,2},{1,3},{2,0},{3,1},{4,6},{5,7},{6,4},{7,5},{8,10},{9,11},{10,... | collective-permute-start | bytes 1572872 | tf_op jit(solution)/shard_map/ppermute | solution.py:76
  148.0 6.7 %collective-permute-start.22 = (bf16[2,2,2,2,1,1,1,16,512]{8,7,6,5,4,3,2,1,0:T(8,128)(2,1)S(1)}, bf16[2,2,2,2,1,1,1,16,512]{8,7,6,5,4,3,2,1,0:T(8,128)(2,1)S(1)}, u32[]{:S(2)}, u32[]{:S(2)}) collective-permute-start(bf16[2,2,2,2,1,1,1,16,512]{8,7,6,5,4,3,2,1,0:T(8,128)(2,1)S(1)} %pad_maximum_fusion.15), channel_id=1, source_target_pairs={{0,4},{1,5},{2,6},{3,7},{4,0},{5,1},{6,2},{7,3},{8,12},{9,13},{10,... | collective-permute-start | bytes 786440 | tf_op jit(solution)/shard_map/ppermute | solution.py:76
  148.9 9.4 %copy-start.11 = (bf16[512,1024]{1,0:T(8,128)(2,1)S(1)}, bf16[512,1024]{1,0:T(8,128)(2,1)}, u32[]{:S(2)}) copy-start(bf16[512,1024]{1,0:T(8,128)(2,1)} %reshape.2099) | copy-start | bytes 3145732
  155.6 11.6 %collective-permute-start.23 = (bf16[2,2,2,2,2,1,1,16,512]{8,7,6,5,4,3,2,1,0:T(8,128)(2,1)}, bf16[2,2,2,2,2,1,1,16,512]{8,7,6,5,4,3,2,1,0:T(8,128)(2,1)S(1)}, u32[]{:S(2)}, u32[]{:S(2)}) collective-permute-start(bf16[2,2,2,2,2,1,1,16,512]{8,7,6,5,4,3,2,1,0:T(8,128)(2,1)} %pad_maximum_fusion.10), channel_id=1, source_target_pairs={{0,1},{1,0},{2,3},{3,2},{4,5},{5,4},{6,7},{7,6},{8,9},{9,8},{10,11... | collective-permute-start | bytes 1572872 | tf_op jit(solution)/shard_map/ppermute | solution.py:76
  168.4 11.4 %collective-permute-start.24 = (bf16[2,2,2,2,2,1,2,16,512]{8,7,6,5,4,3,2,1,0:T(8,128)(2,1)}, bf16[2,2,2,2,2,1,2,16,512]{8,7,6,5,4,3,2,1,0:T(8,128)(2,1)S(1)}, u32[]{:S(2)}, u32[]{:S(2)}) collective-permute-start(bf16[2,2,2,2,2,1,2,16,512]{8,7,6,5,4,3,2,1,0:T(8,128)(2,1)} %pad_maximum_fusion.6), channel_id=1, source_target_pairs={{0,2},{1,3},{2,0},{3,1},{4,6},{5,7},{6,4},{7,5},{8,10},{9,11},{10,... | collective-permute-start | bytes 3145736 | tf_op jit(solution)/shard_map/ppermute | solution.py:76
  169.0 8.9 %collective-permute-start.19 = (f32[4,2,1,1,1,1,1,16,512]{8,7,1,0,6,5,4,3,2:T(8,128)S(1)}, f32[4,2,1,1,1,1,1,16,512]{8,7,1,0,6,5,4,3,2:T(8,128)}, u32[]{:S(2)}, u32[]{:S(2)}) collective-permute-start(f32[4,2,1,1,1,1,1,16,512]{8,7,1,0,6,5,4,3,2:T(8,128)S(1)} %bitcast.555), channel_id=1, source_target_pairs={{0,1},{1,0},{2,3},{3,2},{4,5},{5,4},{6,7},{7,6},{8,9},{9,8},{10,11... | collective-permute-start | bytes 786440 | tf_op jit(solution)/shard_map/ppermute | solution.py:76
  (37 other events, 32.2 us)

commit v6 on v1

--- a/solution.py
+++ b/solution.py
@@ -121,7 +121,7 @@
         lhs = jnp.stack(
             [jnp.concatenate([p_re, -p_im], -1), jnp.concatenate([p_im, p_re], -1)], 0
         ).reshape(2, prows, nspin, 2 * nev)
-        lhs = jnp.take(lhs, spin_map, axis=2).reshape(2 * prows * nspin, 2 * nev)
+        lhs = jnp.take(lhs, spin_map, axis=2, mode="clip").reshape(2 * prows * nspin, 2 * nev)
 
         own = []
         products = []
@@ -136,14 +136,14 @@
             rhs = all_gather(blk, list(reversed(order)), nbits, count, 1).reshape(2 * nev, nev)
             product = jnp.dot(lhs, rhs, preferred_element_type=jnp.float32)
             products.append(product.astype(jnp.bfloat16).reshape(2, prows, nspin * nev))
-        own = jnp.take(jnp.stack(own, 0), directions, axis=0)
+        own = jnp.take(jnp.stack(own, 0), directions, axis=0, mode="clip")
         ndisp = own.shape[0]
         gy_bits = [b for b in range(nbits) if (1 << b) < ny]
         grown = all_gather(
             own.reshape([ndisp, 2] + [1] * nbits + [rows, nev]), gy_bits, nbits, count, 2
         )
         elem = grown.reshape(ndisp, 2, ny * rows, nev)
-        contracted = jnp.take(jnp.stack(products, 0), directions, axis=0)
+        contracted = jnp.take(jnp.stack(products, 0), directions, axis=0, mode="clip")
         return (elem, contracted)
 
     return local

time: 159 us -> 153 us (0.962)
  other arithmetic: 35 us -> 27.3 us
    select_n x5 -> x0, other arithmetic: 6.49 us -> none  [the longest x1 3.17 us: local(): contracted = jnp.take(jnp.stack(products, 0), directions, axis=0)]
    gather x3 -> x4, local copies, waits for them, and re-layouts: 4.54 us -> 6.58 us  [the longest x2 3.77 us: local(): jnp.take(lhs, spin_map, axis=2, mode='clip')]
    select_n x2 -> x0, local copies, waits for them, and re-layouts: 1.95 us -> none  [local(): lhs = jnp.take(lhs, spin_map, axis=2).reshape(2 * prows * nspin, 2 * nev)]
  transfers between devices with their start and end apart: 45 -> 45, of which waited for: 18 -> 18; matrix products, arithmetic and copies ran while one was open for 33% -> 32% of each run, Pallas kernels for 0% -> 0%
where the time goes in v6:
time: 153 us; the launch traced here: 152 us
  starting transfers between devices  41.5 us (27%)
  waiting for transfers between devices  41.1 us (27%)
  local copies, waits for them, and re-layouts  28.9 us (19%)
  other arithmetic  27.3 us (18%)
  matrix products  10.7 us (7%)
  between operations  2.31 us (2%)
    ppermute x20, waiting for transfers between devices, reduce_scatter(): buf = keep + lax.ppermute(send, ALL, xor_pairs(count, b))  28.8 us
    ppermute x21, starting transfers between devices, all_gather(): other = lax.ppermute(buf, ALL, xor_pairs(count, b))  21.6 us
    ppermute x20, starting transfers between devices, reduce_scatter(): buf = keep + lax.ppermute(send, ALL, xor_pairs(count, b))  12.9 us
    ppermute x21, waiting for transfers between devices, all_gather(): other = lax.ppermute(buf, ALL, xor_pairs(count, b))  12.2 us
    dot_general x4, matrix products, local(): jnp.dot(left, field.reshape(2 * depth, nev), preferred_element_type=jnp.f...  7.12 us
    unnamed x131, local copies, waits for them, and re-layouts  6.12 us
    another operation x12, other arithmetic  6.05 us
    ppermute x1, starting transfers between devices, local(): lax.ppermute(ev[:, :, :, 0:1], 'gx', [(i, (i - 1) % nx) for i in range(nx)])  3.97 us
  transfers between devices with their start and end apart: 45, of which 18 were waited for; matrix products, arithmetic and copies ran while one was open for 32% of the time, Pallas kernels for 0%

profile of v6, /device:TPU:0, one launch (start us, length us, event | category | flops | bytes accessed | tf_op | source)
XLA Modules:
  0.0 151.8 jit_solution(14074278344356354576)
XLA Ops:
  0.6 1.0 slice_bitcast_fusion.21
  2.4 1.9 %convert_element_type.66 = f32[2,3,4,4,16,512]{5,4,3,2,1,0:T(8,128)S(1)} convert(bf16[2,3,4,4,16,512]{5,4,3,2,1,0:T(8,128)(2,1)} %param.5) | non-fusion elementwise | flops 786432 | bytes 4718592 | tf_op jit(solution)/shard_map/convert_element_type | solution.py:13
  6.9 0.9 pad_maximum_fusion.20
  7.8 3.0 %collective-permute-start.18 = (bf16[2,3,4,4,1,512]{5,4,3,2,1,0:T(2,128)(2,1)}, bf16[2,3,4,4,1,512]{5,4,3,2,1,0:T(2,128)(2,1)}, u32[]{:S(2)}, u32[]{:S(2)}) collective-permute-start(bf16[2,3,4,4,1,512]{5,4,3,2,1,0:T(2,128)(2,1)} %pad_maximum_fusion.20), channel_id=1, source_target_pairs={{0,1},{1,0},{2,3},{3,2},{4,5},{5,4},{6,7},{7,6},{8,9},{9,8},{10,11... | collective-permute-start | bytes 294920 | tf_op jit(solution)/shard_map/ppermute | solution.py:97
  14.1 1.2 copy-done
  17.0 4.0 %collective-permute-start = (bf16[2,3,4,1,16,512]{5,4,3,2,1,0:T(8,128)(2,1)}, bf16[2,3,4,1,16,512]{5,4,3,2,1,0:T(8,128)(2,1)S(1)}, u32[]{:S(2)}, u32[]{:S(2)}) collective-permute-start(bf16[2,3,4,1,16,512]{5,4,3,2,1,0:T(8,128)(2,1)} %slice.141), channel_id=1, source_target_pairs={{0,30},{2,0},{4,2},{6,4},{8,6},{10,8},{12,10},{14,12},{16,14},{18,... | collective-permute-start | bytes 1179656 | tf_op jit(solution)/shard_map/ppermute | solution.py:94
  21.6 1.2 slice_bitcast_fusion
  22.9 1.0 fusion.32
  24.6 1.1 slice.140
  25.8 1.1 fusion.33
  27.7 1.7 %gather_fusion.1 = bf16[4,2,64,1024]{3,2,1,0:T(8,128)(2,1)} fusion(bf16[2,64,4,1024]{3,1,2,0:T(8,128)(2,1)S(1)} %maximum_maximum_fusion.1, s32[1024]{0:T(1024)} %pad_clamp_fusion), kind=kCustom, calls=%fused_computation.1 | custom fusion | bytes 2097168 | tf_op jit(solution)/shard_map/jit(_take)/gather | solution.py:124
  29.4 2.0 %copy.66 = bf16[2,64,4,1024]{3,2,1,0:T(4,128)(2,1)S(1)} copy(bf16[2,64,4,1024]{3,1,0,2:T(8,128)(2,1)} %bitcast.541) | data formatting | bytes 2097152 | tf_op jit(solution)/shard_map/jit(_take)/gather | solution.py:124
  31.4 1.1 reshape.2102
  32.6 2.2 %maximum_maximum_fusion = bf16[1024,1536]{1,0:T(8,128)(2,1)S(1)} fusion(bf16[512,768]{1,0:T(8,128)(2,1)} %get-tuple-element.27, bf16[512,768]{1,0:T(8,128)(2,1)} %fusion.32, bf16[512,768]{1,0:T(8,128)(2,1)} %get-tuple-element.26), kind=kLoop, calls=%fused_computation.3 | loop fusion | flops 12582912 | bytes 5505024 | tf_op jit(solution)/shard_map/concatenate | solution.py:108
  35.4 1.7 %fusion.4 = bf16[2,3,4,4,16,512]{5,4,3,2,1,0:T(8,128)(2,1)S(1)} fusion(bf16[1,3,4,4,16,512]{5,4,3,2,1,0:T(8,128)(2,1)S(1)} %copy-done.6, bf16[1,3,4,4,16,512]{5,4,3,2,1,0:T(8,128)(2,1)S(1)} %copy-done.8, bf16[2,3,4,4,1,512]{5,4,3,2,1,0:T(2,128)(2,1)} %collective-permute-done.18), kind=kLoop, calls=%fused_computation.10 | loop fusion | flops 4718592 | bytes 3244032 | tf_op jit(solution)/shard_map/concatenate | solution.py:104
  37.1 1.8 %fusion = f32[2,2,2,2,2,2,16,512]{7,6,0,5,4,3,2,1:T(8,128)S(1)} fusion(bf16[1536,512,1,1,1,1,1,1]{1,0,2,7,6,5,4,3:T(8,128)(2,1)S(1)} %bitcast.549, bf16[2,2,2,2,2,2,16,1536]{7,6,5,4,3,2,1,0:T(8,128)(2,1)S(1)} %bitcast.542), kind=kOutput, calls=%fused_computation.4 | convolution fusion | flops 1610612736 | bytes 6815744 | tf_op jit(solution)/shard_map/dot_general | solution.py:130
  39.1 1.1 copy.55
  43.1 1.8 %fusion.2 = f32[2,2,2,2,2,2,16,512]{7,6,0,5,4,3,2,1:T(8,128)S(1)} fusion(bf16[1536,512,1,1,1,1,1,1]{1,0,2,7,6,5,4,3:T(8,128)(2,1)S(1)} %bitcast.551, bf16[2,2,2,2,2,2,16,1536]{7,6,5,4,3,2,1,0:T(8,128)(2,1)S(1)} %bitcast.543), kind=kOutput, calls=%fused_computation.6 | convolution fusion | flops 1610612736 | bytes 6815744 | tf_op jit(solution)/shard_map/dot_general | solution.py:130
  46.3 1.2 fusion.5
  47.4 1.8 %fusion.35 = f32[2,2,2,2,2,2,16,512]{7,6,5,4,3,2,1,0:T(8,128)S(1)} fusion(bf16[2,2,2,2,2,2,16,1536]{7,6,5,4,3,2,1,0:T(8,128)(2,1)S(1)} %bitcast.544, bf16[1536,512,1,1,1,1,1,1]{1,0,7,6,5,4,3,2:T(8,128)(2,1)S(1)} %bitcast.548), kind=kOutput, calls=%fused_computation.252 | convolution fusion | flops 1610612736 | bytes 6815744 | tf_op jit(solution)/shard_map/dot_general | solution.py:130
  53.0 1.8 %fusion.34 = f32[2,2,2,2,2,2,16,512]{7,6,5,4,3,2,1,0:T(8,128)S(1)} fusion(bf16[2,2,2,2,2,2,16,1536]{7,6,5,4,3,2,1,0:T(8,128)(2,1)S(1)} %bitcast.545, bf16[1536,512,1,1,1,1,1,1]{1,0,7,6,5,4,3,2:T(8,128)(2,1)S(1)} %bitcast.550), kind=kOutput, calls=%fused_computation.251 | convolution fusion | flops 1610612736 | bytes 6815744 | tf_op jit(solution)/shard_map/dot_general | solution.py:130
  55.7 1.6 %collective-permute-start.20 = (f32[2,2,2,2,1,1,16,512]{7,6,0,5,4,3,2,1:T(8,128)S(1)}, f32[2,2,2,2,1,1,16,512]{7,6,0,5,4,3,2,1:T(8,128)S(1)}, u32[]{:S(2)}, u32[]{:S(2)}) collective-permute-start(f32[2,2,2,2,1,1,16,512]{7,6,0,5,4,3,2,1:T(8,128)S(1)} %constant_dynamic-slice_fusion.3), channel_id=1, source_target_pairs={{0,1},{1,0},{2,3},{3,2},{4,5},{5,4},{6,7},{7,6},{8,9},{9,8},{10,11... | collective-permute-start | bytes 1572872 | tf_op jit(solution)/shard_map/ppermute | solution.py:67
  58.3 1.3 collective-permute-start.2
  59.6 10.9 %collective-permute-done.20 = f32[2,2,2,2,1,1,16,512]{7,6,0,5,4,3,2,1:T(8,128)S(1)} collective-permute-done((f32[2,2,2,2,1,1,16,512]{7,6,0,5,4,3,2,1:T(8,128)S(1)}, f32[2,2,2,2,1,1,16,512]{7,6,0,5,4,3,2,1:T(8,128)S(1)}, u32[]{:S(2)}, u32[]{:S(2)}) %collective-permute-start.20) | collective-permute-done | bytes 524320 | tf_op jit(solution)/shard_map/ppermute | solution.py:67
  71.4 5.8 %collective-permute-done.21 = f32[2,2,2,1,1,1,16,512]{7,6,0,5,4,3,2,1:T(8,128)S(1)} collective-permute-done((f32[2,2,2,1,1,1,16,512]{7,6,0,5,4,3,2,1:T(8,128)S(1)}, f32[2,2,2,1,1,1,16,512]{7,6,0,5,4,3,2,1:T(8,128)S(1)}, u32[]{:S(2)}, u32[]{:S(2)}) %collective-permute-start.21) | collective-permute-done | bytes 262176 | tf_op jit(solution)/shard_map/ppermute | solution.py:67
  77.4 2.3 %collective-permute-done.9 = f32[2,2,1,1,1,2,16,512]{7,6,0,5,4,3,2,1:T(8,128)S(1)} collective-permute-done((f32[2,2,1,1,1,2,16,512]{7,6,0,5,4,3,2,1:T(8,128)S(1)}, f32[2,2,1,1,1,2,16,512]{7,6,0,5,4,3,2,1:T(8,128)S(1)}, u32[]{:S(2)}, u32[]{:S(2)}) %collective-permute-start.9) | collective-permute-done | bytes 262176 | tf_op jit(solution)/shard_map/ppermute | solution.py:67
  80.2 2.1 %collective-permute-start.15 = (f32[2,2,1,2,1,1,16,512]{7,6,5,4,3,2,1,0:T(8,128)S(1)}, f32[2,2,1,2,1,1,16,512]{7,6,5,4,3,2,1,0:T(8,128)S(1)}, u32[]{:S(2)}, u32[]{:S(2)}) collective-permute-start(f32[2,2,1,2,1,1,16,512]{7,6,5,4,3,2,1,0:T(8,128)S(1)} %constant_dynamic-slice_fusion.7), channel_id=1, source_target_pairs={{0,1},{1,0},{2,3},{3,2},{4,5},{5,4},{6,7},{7,6},{8,9},{9,8},{10,11... | collective-permute-start | bytes 786440 | tf_op jit(solution)/shard_map/ppermute | solution.py:67
  82.4 1.2 collective-permute-start.3
  83.7 2.5 %collective-permute-done.10 = f32[2,2,1,1,1,1,16,512]{7,6,0,5,4,3,2,1:T(8,128)S(1)} collective-permute-done((f32[2,2,1,1,1,1,16,512]{7,6,0,5,4,3,2,1:T(8,128)S(1)}, f32[2,2,1,1,1,1,16,512]{7,6,0,5,4,3,2,1:T(8,128)S(1)}, u32[]{:S(2)}, u32[]{:S(2)}) %collective-permute-start.10) | collective-permute-done | bytes 131104 | tf_op jit(solution)/shard_map/ppermute | solution.py:67
  86.7 2.9 %collective-permute-done.23 = f32[2,1,1,1,1,1,16,512]{7,6,0,5,4,3,2,1:T(8,128)S(1)} collective-permute-done((f32[2,1,1,1,1,1,16,512]{7,6,0,5,4,3,2,1:T(8,128)S(1)}, f32[2,1,1,1,1,1,16,512]{7,6,0,5,4,3,2,1:T(8,128)S(1)}, u32[]{:S(2)}, u32[]{:S(2)}) %collective-permute-start.23) | collective-permute-done | bytes 65568 | tf_op jit(solution)/shard_map/ppermute | solution.py:67
  89.7 2.2 %collective-permute-done.11 = f32[2,1,1,1,1,1,16,512]{7,6,0,5,4,3,2,1:T(8,128)S(1)} collective-permute-done((f32[2,1,1,1,1,1,16,512]{7,6,0,5,4,3,2,1:T(8,128)S(1)}, f32[2,1,1,1,1,1,16,512]{7,6,0,5,4,3,2,1:T(8,128)S(1)}, u32[]{:S(2)}, u32[]{:S(2)}) %collective-permute-start.11) | collective-permute-done | bytes 65568 | tf_op jit(solution)/shard_map/ppermute | solution.py:67
  92.7 1.8 %collective-permute-done.40 = bf16[2,1,1,1,1,1,16,512]{7,6,5,4,3,2,1,0:T(8,128)(2,1)S(1)} collective-permute-done((bf16[2,1,1,1,1,1,16,512]{7,6,5,4,3,2,1,0:T(8,128)(2,1)S(1)}, bf16[2,1,1,1,1,1,16,512]{7,6,5,4,3,2,1,0:T(8,128)(2,1)S(1)}, u32[]{:S(2)}, u32[]{:S(2)}) %collective-permute-start.40) | collective-permute-done | bytes 32800 | tf_op jit(solution)/shard_map/ppermute | solution.py:76
  94.7 2.1 %collective-permute-done.30 = bf16[2,1,1,1,1,1,16,512]{7,6,0,5,4,3,2,1:T(8,128)(2,1)S(1)} collective-permute-done((bf16[2,1,1,1,1,1,16,512]{7,6,0,5,4,3,2,1:T(8,128)(2,1)S(1)}, bf16[2,1,1,1,1,1,16,512]{7,6,0,5,4,3,2,1:T(8,128)(2,1)S(1)}, u32[]{:S(2)}, u32[]{:S(2)}) %collective-permute-start.30) | collective-permute-done | bytes 32800 | tf_op jit(solution)/shard_map/ppermute | solution.py:76
  96.8 1.5 collective-permute-start.31
  98.4 0.9 collective-permute-start.16
  99.6 1.9 %collective-permute-start.42 = (bf16[2,2,2,1,1,1,16,512]{7,6,5,4,3,2,1,0:T(8,128)(2,1)S(1)}, bf16[2,2,2,1,1,1,16,512]{7,6,5,4,3,2,1,0:T(8,128)(2,1)S(1)}, u32[]{:S(2)}, u32[]{:S(2)}) collective-permute-start(bf16[2,2,2,1,1,1,16,512]{7,6,5,4,3,2,1,0:T(8,128)(2,1)S(1)} %pad_maximum_fusion.24), channel_id=1, source_target_pairs={{0,4},{1,5},{2,6},{3,7},{4,0},{5,1},{6,2},{7,3},{8,12},{9,13},{10,... | collective-permute-start | bytes 393224 | tf_op jit(solution)/shard_map/ppermute | solution.py:76
  101.5 1.3 collective-permute-start.32
  102.8 1.1 collective-permute-done.16
  104.0 1.2 collective-permute-start.17
  105.3 1.8 %collective-permute-start.5 = (f32[2,1,1,1,1,1,16,512]{7,6,5,4,3,2,1,0:T(8,128)S(1)}, f32[2,1,1,1,1,1,16,512]{7,6,5,4,3,2,1,0:T(8,128)S(1)}, u32[]{:S(2)}, u32[]{:S(2)}) collective-permute-start(f32[2,1,1,1,1,1,16,512]{7,6,5,4,3,2,1,0:T(8,128)S(1)} %constant_dynamic-slice_fusion.15), channel_id=1, source_target_pairs={{0,16},{1,17},{2,18},{3,19},{4,20},{5,21},{6,22},{7,23},{8,24},{9,... | collective-permute-start | bytes 196616 | tf_op jit(solution)/shard_map/ppermute | solution.py:67
  107.2 1.1 collective-permute-start.43
  109.8 2.3 %collective-permute-start.35 = (bf16[2,1,1,1,1,1,16,512]{7,6,5,4,3,2,1,0:T(8,128)(2,1)S(1)}, bf16[2,1,1,1,1,1,16,512]{7,6,5,4,3,2,1,0:T(8,128)(2,1)S(1)}, u32[]{:S(2)}, u32[]{:S(2)}) collective-permute-start(bf16[2,1,1,1,1,1,16,512]{7,6,5,4,3,2,1,0:T(8,128)(2,1)S(1)} %get-tuple-element.62), channel_id=1, source_target_pairs={{0,16},{1,17},{2,18},{3,19},{4,20},{5,21},{6,22},{7,23},{8,24},{9,... | collective-permute-start | bytes 98312 | tf_op jit(solution)/shard_map/ppermute | solution.py:76
  113.0 1.6 %collective-permute-start.25 = (bf16[2,1,1,1,1,1,16,512]{7,6,5,4,3,2,1,0:T(8,128)(2,1)S(1)}, bf16[2,1,1,1,1,1,16,512]{7,6,5,4,3,2,1,0:T(8,128)(2,1)S(1)}, u32[]{:S(2)}, u32[]{:S(2)}) collective-permute-start(bf16[2,1,1,1,1,1,16,512]{7,6,5,4,3,2,1,0:T(8,128)(2,1)S(1)} %get-tuple-element.58), channel_id=1, source_target_pairs={{0,16},{1,17},{2,18},{3,19},{4,20},{5,21},{6,22},{7,23},{8,24},{9,... | collective-permute-start | bytes 98312 | tf_op jit(solution)/shard_map/ppermute | solution.py:76
  115.0 1.6 %collective-permute-start.36 = (bf16[2,2,1,1,1,1,16,512]{7,6,5,4,3,2,1,0:T(8,128)(2,1)S(1)}, bf16[2,2,1,1,1,1,16,512]{7,6,5,4,3,2,1,0:T(8,128)(2,1)S(1)}, u32[]{:S(2)}, u32[]{:S(2)}) collective-permute-start(bf16[2,2,1,1,1,1,16,512]{7,6,5,4,3,2,1,0:T(8,128)(2,1)S(1)} %pad_maximum_fusion.27), channel_id=1, source_target_pairs={{0,4},{1,5},{2,6},{3,7},{4,0},{5,1},{6,2},{7,3},{8,12},{9,13},{10,... | collective-permute-start | bytes 196616 | tf_op jit(solution)/shard_map/ppermute | solution.py:76
  116.6 1.2 collective-permute-done.25
  117.8 1.2 collective-permute-start.26
  119.4 1.3 collective-permute-start.37
  120.6 1.5 collective-permute-done.26
  122.2 2.3 %collective-permute-start.27 = (bf16[2,2,2,1,1,1,16,512]{7,6,5,4,3,2,1,0:T(8,128)(2,1)S(1)}, bf16[2,2,2,1,1,1,16,512]{7,6,5,4,3,2,1,0:T(8,128)(2,1)S(1)}, u32[]{:S(2)}, u32[]{:S(2)}) collective-permute-start(bf16[2,2,2,1,1,1,16,512]{7,6,5,4,3,2,1,0:T(8,128)(2,1)S(1)} %pad_maximum_fusion.21), channel_id=1, source_target_pairs={{0,4},{1,5},{2,6},{3,7},{4,0},{5,1},{6,2},{7,3},{8,12},{9,13},{10,... | collective-permute-start | bytes 393224 | tf_op jit(solution)/shard_map/ppermute | solution.py:76
  125.8 1.6 %collective-permute-done.27 = bf16[2,2,2,1,1,1,16,512]{7,6,5,4,3,2,1,0:T(8,128)(2,1)S(1)} collective-permute-done((bf16[2,2,2,1,1,1,16,512]{7,6,5,4,3,2,1,0:T(8,128)(2,1)S(1)}, bf16[2,2,2,1,1,1,16,512]{7,6,5,4,3,2,1,0:T(8,128)(2,1)S(1)}, u32[]{:S(2)}, u32[]{:S(2)}) %collective-permute-start.27) | collective-permute-done | bytes 131104 | tf_op jit(solution)/shard_map/ppermute | solution.py:76
  127.5 2.1 %collective-permute-start.28 = (bf16[2,2,2,2,1,1,16,512]{7,6,5,4,3,2,1,0:T(8,128)(2,1)S(1)}, bf16[2,2,2,2,1,1,16,512]{7,6,5,4,3,2,1,0:T(8,128)(2,1)S(1)}, u32[]{:S(2)}, u32[]{:S(2)}) collective-permute-start(bf16[2,2,2,2,1,1,16,512]{7,6,5,4,3,2,1,0:T(8,128)(2,1)S(1)} %pad_maximum_fusion.16), channel_id=1, source_target_pairs={{0,1},{1,0},{2,3},{3,2},{4,5},{5,4},{6,7},{7,6},{8,9},{9,8},{10,11... | collective-permute-start | bytes 786440 | tf_op jit(solution)/shard_map/ppermute | solution.py:76
  129.7 0.8 copy.61
  130.6 3.1 %collective-permute-done.38 = bf16[2,2,1,2,1,2,16,512]{7,6,5,4,3,2,1,0:T(8,128)(2,1)S(1)} collective-permute-done((bf16[2,2,1,2,1,2,16,512]{7,6,5,4,3,2,1,0:T(8,128)(2,1)S(1)}, bf16[2,2,1,2,1,2,16,512]{7,6,5,4,3,2,1,0:T(8,128)(2,1)S(1)}, u32[]{:S(2)}, u32[]{:S(2)}) %collective-permute-start.38) | collective-permute-done | bytes 262176 | tf_op jit(solution)/shard_map/ppermute | solution.py:76
  133.7 0.8 pad_maximum_fusion.12
  134.6 0.8 pad_maximum_fusion.10
  138.0 1.0 copy-done.11
  139.1 1.5 convolution_convert_fusion.2
  140.6 1.4 stack_reshape.13
  141.9 1.2 broadcast_select_fusion.3
  144.0 1.1 stack_reshape.14
  145.1 1.1 broadcast_select_fusion.7
  147.1 1.1 stack_reshape.12
  148.2 1.5 pad_maximum_fusion
  149.7 2.1 %gather_fusion.2 = bf16[4,2,64,2048]{3,2,1,0:T(8,128)(2,1)} fusion(bf16[4,2,64,2048]{3,2,1,0:T(8,128)(2,1)S(1)} %pad_maximum_fusion, s32[1024]{0:T(1024)} %pad_clamp_fusion.1), kind=kCustom, calls=%fused_computation.2 | custom fusion | bytes 4194320 | tf_op jit(solution)/shard_map/jit(_take)/gather | solution.py:146
  (306 shorter events, 33.1 us)
Async XLA Ops:
  2.3 2.0 %copy-start.21 = (f32[4,4,16]{2,1,0:T(4,128)}, f32[4,4,16]{2,1,0:T(4,128)S(1)}, u32[]{:S(2)}) copy-start(f32[4,4,16]{2,1,0:T(4,128)S(1)} %get-tuple-element.92) | copy-start | bytes 3076
  2.3 2.0 %copy-start.33 = (f32[4,4,16]{2,1,0:T(4,128)}, f32[4,4,16]{2,1,0:T(4,128)S(1)}, u32[]{:S(2)}) copy-start(f32[4,4,16]{2,1,0:T(4,128)S(1)} %get-tuple-element.86) | copy-start | bytes 3076
  2.3 2.5 %copy-start.23 = (f32[4,4,16]{2,1,0:T(4,128)}, f32[4,4,16]{2,1,0:T(4,128)S(1)}, u32[]{:S(2)}) copy-start(f32[4,4,16]{2,1,0:T(4,128)S(1)} %get-tuple-element.94) | copy-start | bytes 3076
  2.3 2.5 %copy-start.35 = (f32[4,4,16]{2,1,0:T(4,128)}, f32[4,4,16]{2,1,0:T(4,128)S(1)}, u32[]{:S(2)}) copy-start(f32[4,4,16]{2,1,0:T(4,128)S(1)} %get-tuple-element.88) | copy-start | bytes 3076
  2.3 3.0 %copy-start.13 = (f32[4,4,16]{2,1,0:T(4,128)}, f32[4,4,16]{2,1,0:T(4,128)S(1)}, u32[]{:S(2)}) copy-start(f32[4,4,16]{2,1,0:T(4,128)S(1)} %get-tuple-element.101) | copy-start | bytes 3076
  2.3 3.0 %copy-start.25 = (f32[4,4,16]{2,1,0:T(4,128)}, f32[4,4,16]{2,1,0:T(4,128)S(1)}, u32[]{:S(2)}) copy-start(f32[4,4,16]{2,1,0:T(4,128)S(1)} %get-tuple-element.96) | copy-start | bytes 3076
  2.3 3.0 %copy-start.37 = (f32[4,4,16]{2,1,0:T(4,128)}, f32[4,4,16]{2,1,0:T(4,128)S(1)}, u32[]{:S(2)}) copy-start(f32[4,4,16]{2,1,0:T(4,128)S(1)} %get-tuple-element.90) | copy-start | bytes 3076
  7.8 27.6 %collective-permute-start.18 = (bf16[2,3,4,4,1,512]{5,4,3,2,1,0:T(2,128)(2,1)}, bf16[2,3,4,4,1,512]{5,4,3,2,1,0:T(2,128)(2,1)}, u32[]{:S(2)}, u32[]{:S(2)}) collective-permute-start(bf16[2,3,4,4,1,512]{5,4,3,2,1,0:T(2,128)(2,1)} %pad_maximum_fusion.20), channel_id=1, source_target_pairs={{0,1},{1,0},{2,3},{3,2},{4,5},{5,4},{6,7},{7,6},{8,9},{9,8},{10,11... | collective-permute-start | bytes 294920 | tf_op jit(solution)/shard_map/ppermute | solution.py:97
  13.2 3.0 %copy-start.1 = (bf16[1,3,4,4,16,512]{5,4,3,2,1,0:T(8,128)(2,1)}, bf16[1,3,4,4,16,512]{5,4,3,2,1,0:T(8,128)(2,1)S(1)}, u32[]{:S(2)}) copy-start(bf16[1,3,4,4,16,512]{5,4,3,2,1,0:T(8,128)(2,1)S(1)} %maximum_bitcast_fusion.5) | copy-start | bytes 2359300
  13.2 2.1 %copy-start = (bf16[2,3,4,4,16,512]{5,4,3,2,1,0:T(8,128)(2,1)S(1)}, bf16[2,3,4,4,16,512]{5,4,3,2,1,0:T(8,128)(2,1)}, u32[]{:S(2)}) copy-start(bf16[2,3,4,4,16,512]{5,4,3,2,1,0:T(8,128)(2,1)} %param.5) | copy-start | bytes 4718596
  13.3 7.6 %copy-start.3 = (bf16[1,3,4,4,16,512]{5,4,3,2,1,0:T(8,128)(2,1)}, bf16[1,3,4,4,16,512]{5,4,3,2,1,0:T(8,128)(2,1)S(1)}, u32[]{:S(2)}) copy-start(bf16[1,3,4,4,16,512]{5,4,3,2,1,0:T(8,128)(2,1)S(1)} %maximum_bitcast_fusion.4) | copy-start | bytes 2359300
  14.1 31.4 %collective-permute-start.12 = (bf16[2,3,4,1,16,512]{5,4,3,2,1,0:T(8,128)(2,1)}, bf16[2,3,4,1,16,512]{5,4,3,2,1,0:T(8,128)(2,1)}, u32[]{:S(2)}, u32[]{:S(2)}) collective-permute-start(bf16[2,3,4,1,16,512]{5,4,3,2,1,0:T(8,128)(2,1)} %pad_maximum_fusion.14), channel_id=1, source_target_pairs={{0,2},{2,4},{4,6},{6,8},{8,10},{10,12},{12,14},{14,16},{16,18},{18... | collective-permute-start | bytes 1179656 | tf_op jit(solution)/shard_map/ppermute | solution.py:95
  16.2 22.9 %collective-permute-start.6 = (bf16[2,3,4,4,1,512]{5,3,4,2,1,0:T(4,128)(2,1)}, bf16[2,3,4,4,1,512]{5,3,4,2,1,0:T(4,128)(2,1)}, u32[]{:S(2)}, u32[]{:S(2)}) collective-permute-start(bf16[2,3,4,4,1,512]{5,3,4,2,1,0:T(4,128)(2,1)} %copy.80), channel_id=1, source_target_pairs={{0,1},{1,0},{2,3},{3,2},{4,5},{5,4},{6,7},{7,6},{8,9},{9,8},{10,11... | collective-permute-start | bytes 294920 | tf_op jit(solution)/shard_map/ppermute | solution.py:96
  17.0 33.0 %collective-permute-start = (bf16[2,3,4,1,16,512]{5,4,3,2,1,0:T(8,128)(2,1)}, bf16[2,3,4,1,16,512]{5,4,3,2,1,0:T(8,128)(2,1)S(1)}, u32[]{:S(2)}, u32[]{:S(2)}) collective-permute-start(bf16[2,3,4,1,16,512]{5,4,3,2,1,0:T(8,128)(2,1)} %slice.141), channel_id=1, source_target_pairs={{0,30},{2,0},{4,2},{6,4},{8,6},{10,8},{12,10},{14,12},{16,14},{18,... | collective-permute-start | bytes 1179656 | tf_op jit(solution)/shard_map/ppermute | solution.py:94
  32.6 2.2 %copy-start.64 = (s32[4]{0:T(128)S(1)}, s32[4]{0:T(128)}, u32[]{:S(2)}) copy-start(s32[4]{0:T(128)} %param.7) | copy-start | bytes 52
  32.6 2.8 %copy-start.6 = (bf16[1,3,4,4,16,512]{5,4,3,2,1,0:T(8,128)(2,1)S(1)}, bf16[1,3,4,4,16,512]{5,4,3,2,1,0:T(8,128)(2,1)}, u32[]{:S(2)}) copy-start(bf16[1,3,4,4,16,512]{5,4,3,2,1,0:T(8,128)(2,1)} %copy-done.5) | copy-start | bytes 2359300
  32.6 2.8 %copy-start.8 = (bf16[1,3,4,4,16,512]{5,4,3,2,1,0:T(8,128)(2,1)S(1)}, bf16[1,3,4,4,16,512]{5,4,3,2,1,0:T(8,128)(2,1)}, u32[]{:S(2)}) copy-start(bf16[1,3,4,4,16,512]{5,4,3,2,1,0:T(8,128)(2,1)} %copy-done.7) | copy-start | bytes 2359300
  39.0 16.4 %collective-permute-start.19 = (f32[2,2,2,2,1,2,16,512]{7,6,0,5,4,3,2,1:T(8,128)S(1)}, f32[2,2,2,2,1,2,16,512]{7,6,0,5,4,3,2,1:T(8,128)S(1)}, u32[]{:S(2)}, u32[]{:S(2)}) collective-permute-start(f32[2,2,2,2,1,2,16,512]{7,6,0,5,4,3,2,1:T(8,128)S(1)} %constant_dynamic-slice_fusion.4), channel_id=1, source_target_pairs={{0,2},{1,3},{2,0},{3,1},{4,6},{5,7},{6,4},{7,5},{8,10},{9,11},{10,... | collective-permute-start | bytes 3145736 | tf_op jit(solution)/shard_map/ppermute | solution.py:67
  45.0 12.3 %collective-permute-start.7 = (f32[2,2,2,2,1,2,16,512]{7,6,0,5,4,3,2,1:T(8,128)S(1)}, f32[2,2,2,2,1,2,16,512]{7,6,0,5,4,3,2,1:T(8,128)S(1)}, u32[]{:S(2)}, u32[]{:S(2)}) collective-permute-start(f32[2,2,2,2,1,2,16,512]{7,6,0,5,4,3,2,1:T(8,128)S(1)} %constant_dynamic-slice_fusion.14), channel_id=1, source_target_pairs={{0,2},{1,3},{2,0},{3,1},{4,6},{5,7},{6,4},{7,5},{8,10},{9,11},{10,... | collective-permute-start | bytes 3145736 | tf_op jit(solution)/shard_map/ppermute | solution.py:67
  49.3 1.4 copy-start.40
  49.4 1.4 copy-start.42
  49.4 1.4 copy-start.44
  49.4 1.4 copy-start.60
  49.4 1.4 copy-start.61
  49.4 1.4 copy-start.62
  49.4 8.2 %collective-permute-start.13 = (f32[2,2,2,2,1,2,16,512]{7,6,5,4,3,2,1,0:T(8,128)S(1)}, f32[2,2,2,2,1,2,16,512]{7,6,5,4,3,2,1,0:T(8,128)S(1)}, u32[]{:S(2)}, u32[]{:S(2)}) collective-permute-start(f32[2,2,2,2,1,2,16,512]{7,6,5,4,3,2,1,0:T(8,128)S(1)} %constant_dynamic-slice_fusion.9), channel_id=1, source_target_pairs={{0,2},{1,3},{2,0},{3,1},{4,6},{5,7},{6,4},{7,5},{8,10},{9,11},{10,... | collective-permute-start | bytes 3145736 | tf_op jit(solution)/shard_map/ppermute | solution.py:67
  54.9 3.1 %collective-permute-start.1 = (f32[2,2,2,2,1,2,16,512]{7,6,5,4,3,2,1,0:T(8,128)S(1)}, f32[2,2,2,2,1,2,16,512]{7,6,5,4,3,2,1,0:T(8,128)S(1)}, u32[]{:S(2)}, u32[]{:S(2)}) collective-permute-start(f32[2,2,2,2,1,2,16,512]{7,6,5,4,3,2,1,0:T(8,128)S(1)} %constant_dynamic-slice_fusion.19), channel_id=1, source_target_pairs={{0,2},{1,3},{2,0},{3,1},{4,6},{5,7},{6,4},{7,5},{8,10},{9,11},{10,... | collective-permute-start | bytes 3145736 | tf_op jit(solution)/shard_map/ppermute | solution.py:67
  55.7 14.9 %collective-permute-start.20 = (f32[2,2,2,2,1,1,16,512]{7,6,0,5,4,3,2,1:T(8,128)S(1)}, f32[2,2,2,2,1,1,16,512]{7,6,0,5,4,3,2,1:T(8,128)S(1)}, u32[]{:S(2)}, u32[]{:S(2)}) collective-permute-start(f32[2,2,2,2,1,1,16,512]{7,6,0,5,4,3,2,1:T(8,128)S(1)} %constant_dynamic-slice_fusion.3), channel_id=1, source_target_pairs={{0,1},{1,0},{2,3},{3,2},{4,5},{5,4},{6,7},{7,6},{8,9},{9,8},{10,11... | collective-permute-start | bytes 1572872 | tf_op jit(solution)/shard_map/ppermute | solution.py:67
  57.5 13.6 %collective-permute-start.8 = (f32[2,2,2,1,1,2,16,512]{7,6,0,5,4,3,2,1:T(8,128)S(1)}, f32[2,2,2,1,1,2,16,512]{7,6,0,5,4,3,2,1:T(8,128)S(1)}, u32[]{:S(2)}, u32[]{:S(2)}) collective-permute-start(f32[2,2,2,1,1,2,16,512]{7,6,0,5,4,3,2,1:T(8,128)S(1)} %constant_dynamic-slice_fusion.13), channel_id=1, source_target_pairs={{0,4},{1,5},{2,6},{3,7},{4,0},{5,1},{6,2},{7,3},{8,12},{9,13},{10,... | collective-permute-start | bytes 1572872 | tf_op jit(solution)/shard_map/ppermute | solution.py:67
  57.9 21.9 %collective-permute-start.14 = (f32[2,2,1,2,1,2,16,512]{7,6,5,4,3,2,1,0:T(8,128)S(1)}, f32[2,2,1,2,1,2,16,512]{7,6,5,4,3,2,1,0:T(8,128)S(1)}, u32[]{:S(2)}, u32[]{:S(2)}) collective-permute-start(f32[2,2,1,2,1,2,16,512]{7,6,5,4,3,2,1,0:T(8,128)S(1)} %constant_dynamic-slice_fusion.8), channel_id=1, source_target_pairs={{0,8},{1,9},{2,10},{3,11},{4,12},{5,13},{6,14},{7,15},{8,0},{9,1},... | collective-permute-start | bytes 1572872 | tf_op jit(solution)/shard_map/ppermute | solution.py:67
  58.3 23.9 %collective-permute-start.2 = (f32[2,2,2,2,1,1,16,512]{7,6,5,4,3,2,1,0:T(8,128)S(1)}, f32[2,2,2,2,1,1,16,512]{7,6,5,4,3,2,1,0:T(8,128)S(1)}, u32[]{:S(2)}, u32[]{:S(2)}) collective-permute-start(f32[2,2,2,2,1,1,16,512]{7,6,5,4,3,2,1,0:T(8,128)S(1)} %constant_dynamic-slice_fusion.18), channel_id=1, source_target_pairs={{0,1},{1,0},{2,3},{3,2},{4,5},{5,4},{6,7},{7,6},{8,9},{9,8},{10,11... | collective-permute-start | bytes 1572872 | tf_op jit(solution)/shard_map/ppermute | solution.py:67
  70.7 6.5 %collective-permute-start.21 = (f32[2,2,2,1,1,1,16,512]{7,6,0,5,4,3,2,1:T(8,128)S(1)}, f32[2,2,2,1,1,1,16,512]{7,6,0,5,4,3,2,1:T(8,128)S(1)}, u32[]{:S(2)}, u32[]{:S(2)}) collective-permute-start(f32[2,2,2,1,1,1,16,512]{7,6,0,5,4,3,2,1:T(8,128)S(1)} %constant_dynamic-slice_fusion.2), channel_id=1, source_target_pairs={{0,4},{1,5},{2,6},{3,7},{4,0},{5,1},{6,2},{7,3},{8,12},{9,13},{10,... | collective-permute-start | bytes 786440 | tf_op jit(solution)/shard_map/ppermute | solution.py:67
  71.3 8.3 %collective-permute-start.9 = (f32[2,2,1,1,1,2,16,512]{7,6,0,5,4,3,2,1:T(8,128)S(1)}, f32[2,2,1,1,1,2,16,512]{7,6,0,5,4,3,2,1:T(8,128)S(1)}, u32[]{:S(2)}, u32[]{:S(2)}) collective-permute-start(f32[2,2,1,1,1,2,16,512]{7,6,0,5,4,3,2,1:T(8,128)S(1)} %constant_dynamic-slice_fusion.12), channel_id=1, source_target_pairs={{0,8},{1,9},{2,10},{3,11},{4,12},{5,13},{6,14},{7,15},{8,0},{9,1},... | collective-permute-start | bytes 786440 | tf_op jit(solution)/shard_map/ppermute | solution.py:67
  77.3 6.3 %collective-permute-start.22 = (f32[2,2,1,1,1,1,16,512]{7,6,0,5,4,3,2,1:T(8,128)S(1)}, f32[2,2,1,1,1,1,16,512]{7,6,0,5,4,3,2,1:T(8,128)S(1)}, u32[]{:S(2)}, u32[]{:S(2)}) collective-permute-start(f32[2,2,1,1,1,1,16,512]{7,6,0,5,4,3,2,1:T(8,128)S(1)} %constant_dynamic-slice_fusion.1), channel_id=1, source_target_pairs={{0,8},{1,9},{2,10},{3,11},{4,12},{5,13},{6,14},{7,15},{8,0},{9,1},... | collective-permute-start | bytes 393224 | tf_op jit(solution)/shard_map/ppermute | solution.py:67
  79.7 6.4 %collective-permute-start.10 = (f32[2,2,1,1,1,1,16,512]{7,6,0,5,4,3,2,1:T(8,128)S(1)}, f32[2,2,1,1,1,1,16,512]{7,6,0,5,4,3,2,1:T(8,128)S(1)}, u32[]{:S(2)}, u32[]{:S(2)}) collective-permute-start(f32[2,2,1,1,1,1,16,512]{7,6,0,5,4,3,2,1:T(8,128)S(1)} %constant_dynamic-slice_fusion.11), channel_id=1, source_target_pairs={{0,1},{1,0},{2,3},{3,2},{4,5},{5,4},{6,7},{7,6},{8,9},{9,8},{10,11... | collective-permute-start | bytes 393224 | tf_op jit(solution)/shard_map/ppermute | solution.py:67
  80.2 18.2 %collective-permute-start.15 = (f32[2,2,1,2,1,1,16,512]{7,6,5,4,3,2,1,0:T(8,128)S(1)}, f32[2,2,1,2,1,1,16,512]{7,6,5,4,3,2,1,0:T(8,128)S(1)}, u32[]{:S(2)}, u32[]{:S(2)}) collective-permute-start(f32[2,2,1,2,1,1,16,512]{7,6,5,4,3,2,1,0:T(8,128)S(1)} %constant_dynamic-slice_fusion.7), channel_id=1, source_target_pairs={{0,1},{1,0},{2,3},{3,2},{4,5},{5,4},{6,7},{7,6},{8,9},{9,8},{10,11... | collective-permute-start | bytes 786440 | tf_op jit(solution)/shard_map/ppermute | solution.py:67
  82.4 16.9 %collective-permute-start.3 = (f32[2,2,2,1,1,1,16,512]{7,6,5,4,3,2,1,0:T(8,128)S(1)}, f32[2,2,2,1,1,1,16,512]{7,6,5,4,3,2,1,0:T(8,128)S(1)}, u32[]{:S(2)}, u32[]{:S(2)}) collective-permute-start(f32[2,2,2,1,1,1,16,512]{7,6,5,4,3,2,1,0:T(8,128)S(1)} %constant_dynamic-slice_fusion.17), channel_id=1, source_target_pairs={{0,4},{1,5},{2,6},{3,7},{4,0},{5,1},{6,2},{7,3},{8,12},{9,13},{10,... | collective-permute-start | bytes 786440 | tf_op jit(solution)/shard_map/ppermute | solution.py:67
  83.6 6.0 %collective-permute-start.23 = (f32[2,1,1,1,1,1,16,512]{7,6,0,5,4,3,2,1:T(8,128)S(1)}, f32[2,1,1,1,1,1,16,512]{7,6,0,5,4,3,2,1:T(8,128)S(1)}, u32[]{:S(2)}, u32[]{:S(2)}) collective-permute-start(f32[2,1,1,1,1,1,16,512]{7,6,0,5,4,3,2,1:T(8,128)S(1)} %constant_dynamic-slice_fusion), channel_id=1, source_target_pairs={{0,16},{1,17},{2,18},{3,19},{4,20},{5,21},{6,22},{7,23},{8,24},{9,... | collective-permute-start | bytes 196616 | tf_op jit(solution)/shard_map/ppermute | solution.py:67
  86.2 5.7 %collective-permute-start.11 = (f32[2,1,1,1,1,1,16,512]{7,6,0,5,4,3,2,1:T(8,128)S(1)}, f32[2,1,1,1,1,1,16,512]{7,6,0,5,4,3,2,1:T(8,128)S(1)}, u32[]{:S(2)}, u32[]{:S(2)}) collective-permute-start(f32[2,1,1,1,1,1,16,512]{7,6,0,5,4,3,2,1:T(8,128)S(1)} %constant_dynamic-slice_fusion.10), channel_id=1, source_target_pairs={{0,16},{1,17},{2,18},{3,19},{4,20},{5,21},{6,22},{7,23},{8,24},{9,... | collective-permute-start | bytes 196616 | tf_op jit(solution)/shard_map/ppermute | solution.py:67
  89.6 4.9 %collective-permute-start.40 = (bf16[2,1,1,1,1,1,16,512]{7,6,5,4,3,2,1,0:T(8,128)(2,1)S(1)}, bf16[2,1,1,1,1,1,16,512]{7,6,5,4,3,2,1,0:T(8,128)(2,1)S(1)}, u32[]{:S(2)}, u32[]{:S(2)}) collective-permute-start(bf16[2,1,1,1,1,1,16,512]{7,6,5,4,3,2,1,0:T(8,128)(2,1)S(1)} %get-tuple-element.64), channel_id=1, source_target_pairs={{0,16},{1,17},{2,18},{3,19},{4,20},{5,21},{6,22},{7,23},{8,24},{9,... | collective-permute-start | bytes 98312 | tf_op jit(solution)/shard_map/ppermute | solution.py:76
  91.9 4.9 %collective-permute-start.30 = (bf16[2,1,1,1,1,1,16,512]{7,6,0,5,4,3,2,1:T(8,128)(2,1)S(1)}, bf16[2,1,1,1,1,1,16,512]{7,6,0,5,4,3,2,1:T(8,128)(2,1)S(1)}, u32[]{:S(2)}, u32[]{:S(2)}) collective-permute-start(bf16[2,1,1,1,1,1,16,512]{7,6,0,5,4,3,2,1:T(8,128)(2,1)S(1)} %get-tuple-element.60), channel_id=1, source_target_pairs={{0,16},{1,17},{2,18},{3,19},{4,20},{5,21},{6,22},{7,23},{8,24},{9,... | collective-permute-start | bytes 98312 | tf_op jit(solution)/shard_map/ppermute | solution.py:76
  94.5 5.0 %collective-permute-start.41 = (bf16[2,2,1,1,1,1,16,512]{7,6,5,4,3,2,1,0:T(8,128)(2,1)S(1)}, bf16[2,2,1,1,1,1,16,512]{7,6,5,4,3,2,1,0:T(8,128)(2,1)S(1)}, u32[]{:S(2)}, u32[]{:S(2)}) collective-permute-start(bf16[2,2,1,1,1,1,16,512]{7,6,5,4,3,2,1,0:T(8,128)(2,1)S(1)} %pad_maximum_fusion.28), channel_id=1, source_target_pairs={{0,8},{1,9},{2,10},{3,11},{4,12},{5,13},{6,14},{7,15},{8,0},{9,1},... | collective-permute-start | bytes 196616 | tf_op jit(solution)/shard_map/ppermute | solution.py:76
  96.8 4.6 %collective-permute-start.31 = (bf16[2,2,1,1,1,1,16,512]{7,6,0,5,4,3,2,1:T(8,128)(2,1)S(1)}, bf16[2,2,1,1,1,1,16,512]{7,6,0,5,4,3,2,1:T(8,128)(2,1)S(1)}, u32[]{:S(2)}, u32[]{:S(2)}) collective-permute-start(bf16[2,2,1,1,1,1,16,512]{7,6,0,5,4,3,2,1:T(8,128)(2,1)S(1)} %pad_maximum_fusion.26), channel_id=1, source_target_pairs={{0,1},{1,0},{2,3},{3,2},{4,5},{5,4},{6,7},{7,6},{8,9},{9,8},{10,11... | collective-permute-start | bytes 196616 | tf_op jit(solution)/shard_map/ppermute | solution.py:76
  98.4 5.6 %collective-permute-start.16 = (f32[2,2,1,1,1,1,16,512]{7,6,5,4,3,2,1,0:T(8,128)S(1)}, f32[2,2,1,1,1,1,16,512]{7,6,5,4,3,2,1,0:T(8,128)S(1)}, u32[]{:S(2)}, u32[]{:S(2)}) collective-permute-start(f32[2,2,1,1,1,1,16,512]{7,6,5,4,3,2,1,0:T(8,128)S(1)} %constant_dynamic-slice_fusion.6), channel_id=1, source_target_pairs={{0,4},{1,5},{2,6},{3,7},{4,0},{5,1},{6,2},{7,3},{8,12},{9,13},{10,... | collective-permute-start | bytes 393224 | tf_op jit(solution)/shard_map/ppermute | solution.py:67
  99.3 5.9 %collective-permute-start.4 = (f32[2,2,1,1,1,1,16,512]{7,6,5,4,3,2,1,0:T(8,128)S(1)}, f32[2,2,1,1,1,1,16,512]{7,6,5,4,3,2,1,0:T(8,128)S(1)}, u32[]{:S(2)}, u32[]{:S(2)}) collective-permute-start(f32[2,2,1,1,1,1,16,512]{7,6,5,4,3,2,1,0:T(8,128)S(1)} %constant_dynamic-slice_fusion.16), channel_id=1, source_target_pairs={{0,8},{1,9},{2,10},{3,11},{4,12},{5,13},{6,14},{7,15},{8,0},{9,1},... | collective-permute-start | bytes 393224 | tf_op jit(solution)/shard_map/ppermute | solution.py:67
  99.6 7.5 %collective-permute-start.42 = (bf16[2,2,2,1,1,1,16,512]{7,6,5,4,3,2,1,0:T(8,128)(2,1)S(1)}, bf16[2,2,2,1,1,1,16,512]{7,6,5,4,3,2,1,0:T(8,128)(2,1)S(1)}, u32[]{:S(2)}, u32[]{:S(2)}) collective-permute-start(bf16[2,2,2,1,1,1,16,512]{7,6,5,4,3,2,1,0:T(8,128)(2,1)S(1)} %pad_maximum_fusion.24), channel_id=1, source_target_pairs={{0,4},{1,5},{2,6},{3,7},{4,0},{5,1},{6,2},{7,3},{8,12},{9,13},{10,... | collective-permute-start | bytes 393224 | tf_op jit(solution)/shard_map/ppermute | solution.py:76
  101.5 6.7 %collective-permute-start.32 = (bf16[2,2,1,1,1,2,16,512]{7,6,0,5,4,3,2,1:T(8,128)(2,1)S(1)}, bf16[2,2,1,1,1,2,16,512]{7,6,0,5,4,3,2,1:T(8,128)(2,1)S(1)}, u32[]{:S(2)}, u32[]{:S(2)}) collective-permute-start(bf16[2,2,1,1,1,2,16,512]{7,6,0,5,4,3,2,1:T(8,128)(2,1)S(1)} %pad_maximum_fusion.22), channel_id=1, source_target_pairs={{0,8},{1,9},{2,10},{3,11},{4,12},{5,13},{6,14},{7,15},{8,0},{9,1},... | collective-permute-start | bytes 393224 | tf_op jit(solution)/shard_map/ppermute | solution.py:76
  104.0 5.7 %collective-permute-start.17 = (f32[2,1,1,1,1,1,16,512]{7,6,5,4,3,2,1,0:T(8,128)S(1)}, f32[2,1,1,1,1,1,16,512]{7,6,5,4,3,2,1,0:T(8,128)S(1)}, u32[]{:S(2)}, u32[]{:S(2)}) collective-permute-start(f32[2,1,1,1,1,1,16,512]{7,6,5,4,3,2,1,0:T(8,128)S(1)} %constant_dynamic-slice_fusion.5), channel_id=1, source_target_pairs={{0,16},{1,17},{2,18},{3,19},{4,20},{5,21},{6,22},{7,23},{8,24},{9,... | collective-permute-start | bytes 196616 | tf_op jit(solution)/shard_map/ppermute | solution.py:67
  105.3 6.8 %collective-permute-start.5 = (f32[2,1,1,1,1,1,16,512]{7,6,5,4,3,2,1,0:T(8,128)S(1)}, f32[2,1,1,1,1,1,16,512]{7,6,5,4,3,2,1,0:T(8,128)S(1)}, u32[]{:S(2)}, u32[]{:S(2)}) collective-permute-start(f32[2,1,1,1,1,1,16,512]{7,6,5,4,3,2,1,0:T(8,128)S(1)} %constant_dynamic-slice_fusion.15), channel_id=1, source_target_pairs={{0,16},{1,17},{2,18},{3,19},{4,20},{5,21},{6,22},{7,23},{8,24},{9,... | collective-permute-start | bytes 196616 | tf_op jit(solution)/shard_map/ppermute | solution.py:67
  107.2 17.3 %collective-permute-start.43 = (bf16[2,2,2,2,1,1,16,512]{7,6,5,4,3,2,1,0:T(8,128)(2,1)S(1)}, bf16[2,2,2,2,1,1,16,512]{7,6,5,4,3,2,1,0:T(8,128)(2,1)S(1)}, u32[]{:S(2)}, u32[]{:S(2)}) collective-permute-start(bf16[2,2,2,2,1,1,16,512]{7,6,5,4,3,2,1,0:T(8,128)(2,1)S(1)} %pad_maximum_fusion.19), channel_id=1, source_target_pairs={{0,1},{1,0},{2,3},{3,2},{4,5},{5,4},{6,7},{7,6},{8,9},{9,8},{10,11... | collective-permute-start | bytes 786440 | tf_op jit(solution)/shard_map/ppermute | solution.py:76
  108.3 16.4 %collective-permute-start.33 = (bf16[2,2,2,1,1,2,16,512]{7,6,0,5,4,3,2,1:T(8,128)(2,1)S(1)}, bf16[2,2,2,1,1,2,16,512]{7,6,0,5,4,3,2,1:T(8,128)(2,1)S(1)}, u32[]{:S(2)}, u32[]{:S(2)}) collective-permute-start(bf16[2,2,2,1,1,2,16,512]{7,6,0,5,4,3,2,1:T(8,128)(2,1)S(1)} %pad_maximum_fusion.17), channel_id=1, source_target_pairs={{0,4},{1,5},{2,6},{3,7},{4,0},{5,1},{6,2},{7,3},{8,12},{9,13},{10,... | collective-permute-start | bytes 786440 | tf_op jit(solution)/shard_map/ppermute | solution.py:76
  109.8 5.2 %collective-permute-start.35 = (bf16[2,1,1,1,1,1,16,512]{7,6,5,4,3,2,1,0:T(8,128)(2,1)S(1)}, bf16[2,1,1,1,1,1,16,512]{7,6,5,4,3,2,1,0:T(8,128)(2,1)S(1)}, u32[]{:S(2)}, u32[]{:S(2)}) collective-permute-start(bf16[2,1,1,1,1,1,16,512]{7,6,5,4,3,2,1,0:T(8,128)(2,1)S(1)} %get-tuple-element.62), channel_id=1, source_target_pairs={{0,16},{1,17},{2,18},{3,19},{4,20},{5,21},{6,22},{7,23},{8,24},{9,... | collective-permute-start | bytes 98312 | tf_op jit(solution)/shard_map/ppermute | solution.py:76
  112.8 16.8 %collective-permute-start.24 = (f32[4,2,1,1,1,1,1,16,512]{8,7,1,0,6,5,4,3,2:T(8,128)S(1)}, f32[4,2,1,1,1,1,1,16,512]{8,7,1,0,6,5,4,3,2:T(8,128)S(1)}, u32[]{:S(2)}, u32[]{:S(2)}) collective-permute-start(f32[4,2,1,1,1,1,1,16,512]{8,7,1,0,6,5,4,3,2:T(8,128)S(1)} %bitcast.556), channel_id=1, source_target_pairs={{0,1},{1,0},{2,3},{3,2},{4,5},{5,4},{6,7},{7,6},{8,9},{9,8},{10,11... | collective-permute-start | bytes 786440 | tf_op jit(solution)/shard_map/ppermute | solution.py:76
  113.0 4.8 %collective-permute-start.25 = (bf16[2,1,1,1,1,1,16,512]{7,6,5,4,3,2,1,0:T(8,128)(2,1)S(1)}, bf16[2,1,1,1,1,1,16,512]{7,6,5,4,3,2,1,0:T(8,128)(2,1)S(1)}, u32[]{:S(2)}, u32[]{:S(2)}) collective-permute-start(bf16[2,1,1,1,1,1,16,512]{7,6,5,4,3,2,1,0:T(8,128)(2,1)S(1)} %get-tuple-element.58), channel_id=1, source_target_pairs={{0,16},{1,17},{2,18},{3,19},{4,20},{5,21},{6,22},{7,23},{8,24},{9,... | collective-permute-start | bytes 98312 | tf_op jit(solution)/shard_map/ppermute | solution.py:76
  115.0 4.3 %collective-permute-start.36 = (bf16[2,2,1,1,1,1,16,512]{7,6,5,4,3,2,1,0:T(8,128)(2,1)S(1)}, bf16[2,2,1,1,1,1,16,512]{7,6,5,4,3,2,1,0:T(8,128)(2,1)S(1)}, u32[]{:S(2)}, u32[]{:S(2)}) collective-permute-start(bf16[2,2,1,1,1,1,16,512]{7,6,5,4,3,2,1,0:T(8,128)(2,1)S(1)} %pad_maximum_fusion.27), channel_id=1, source_target_pairs={{0,4},{1,5},{2,6},{3,7},{4,0},{5,1},{6,2},{7,3},{8,12},{9,13},{10,... | collective-permute-start | bytes 196616 | tf_op jit(solution)/shard_map/ppermute | solution.py:76
  117.8 4.3 %collective-permute-start.26 = (bf16[2,2,1,1,1,1,16,512]{7,6,5,4,3,2,1,0:T(8,128)(2,1)S(1)}, bf16[2,2,1,1,1,1,16,512]{7,6,5,4,3,2,1,0:T(8,128)(2,1)S(1)}, u32[]{:S(2)}, u32[]{:S(2)}) collective-permute-start(bf16[2,2,1,1,1,1,16,512]{7,6,5,4,3,2,1,0:T(8,128)(2,1)S(1)} %pad_maximum_fusion.25), channel_id=1, source_target_pairs={{0,8},{1,9},{2,10},{3,11},{4,12},{5,13},{6,14},{7,15},{8,0},{9,1},... | collective-permute-start | bytes 196616 | tf_op jit(solution)/shard_map/ppermute | solution.py:76
  119.4 6.0 %collective-permute-start.37 = (bf16[2,2,1,2,1,1,16,512]{7,6,5,4,3,2,1,0:T(8,128)(2,1)S(1)}, bf16[2,2,1,2,1,1,16,512]{7,6,5,4,3,2,1,0:T(8,128)(2,1)S(1)}, u32[]{:S(2)}, u32[]{:S(2)}) collective-permute-start(bf16[2,2,1,2,1,1,16,512]{7,6,5,4,3,2,1,0:T(8,128)(2,1)S(1)} %pad_maximum_fusion.23), channel_id=1, source_target_pairs={{0,1},{1,0},{2,3},{3,2},{4,5},{5,4},{6,7},{7,6},{8,9},{9,8},{10,11... | collective-permute-start | bytes 393224 | tf_op jit(solution)/shard_map/ppermute | solution.py:76
  122.2 5.2 %collective-permute-start.27 = (bf16[2,2,2,1,1,1,16,512]{7,6,5,4,3,2,1,0:T(8,128)(2,1)S(1)}, bf16[2,2,2,1,1,1,16,512]{7,6,5,4,3,2,1,0:T(8,128)(2,1)S(1)}, u32[]{:S(2)}, u32[]{:S(2)}) collective-permute-start(bf16[2,2,2,1,1,1,16,512]{7,6,5,4,3,2,1,0:T(8,128)(2,1)S(1)} %pad_maximum_fusion.21), channel_id=1, source_target_pairs={{0,4},{1,5},{2,6},{3,7},{4,0},{5,1},{6,2},{7,3},{8,12},{9,13},{10,... | collective-permute-start | bytes 393224 | tf_op jit(solution)/shard_map/ppermute | solution.py:76
  124.6 11.4 %collective-permute-start.44 = (bf16[2,2,2,2,1,2,16,512]{7,6,5,4,3,2,1,0:T(8,128)(2,1)S(1)}, bf16[2,2,2,2,1,2,16,512]{7,6,5,4,3,2,1,0:T(8,128)(2,1)S(1)}, u32[]{:S(2)}, u32[]{:S(2)}) collective-permute-start(bf16[2,2,2,2,1,2,16,512]{7,6,5,4,3,2,1,0:T(8,128)(2,1)S(1)} %pad_maximum_fusion.13), channel_id=1, source_target_pairs={{0,2},{1,3},{2,0},{3,1},{4,6},{5,7},{6,4},{7,5},{8,10},{9,11},{10,... | collective-permute-start | bytes 1572872 | tf_op jit(solution)/shard_map/ppermute | solution.py:76
  124.8 12.6 %collective-permute-start.34 = (bf16[2,2,2,2,1,2,16,512]{7,6,0,5,4,3,2,1:T(8,128)(2,1)S(1)}, bf16[2,2,2,2,1,2,16,512]{7,6,0,5,4,3,2,1:T(8,128)(2,1)S(1)}, u32[]{:S(2)}, u32[]{:S(2)}) collective-permute-start(bf16[2,2,2,2,1,2,16,512]{7,6,0,5,4,3,2,1:T(8,128)(2,1)S(1)} %pad_maximum_fusion.11), channel_id=1, source_target_pairs={{0,2},{1,3},{2,0},{3,1},{4,6},{5,7},{6,4},{7,5},{8,10},{9,11},{10,... | collective-permute-start | bytes 1572872 | tf_op jit(solution)/shard_map/ppermute | solution.py:76
  125.4 8.3 %collective-permute-start.38 = (bf16[2,2,1,2,1,2,16,512]{7,6,5,4,3,2,1,0:T(8,128)(2,1)S(1)}, bf16[2,2,1,2,1,2,16,512]{7,6,5,4,3,2,1,0:T(8,128)(2,1)S(1)}, u32[]{:S(2)}, u32[]{:S(2)}) collective-permute-start(bf16[2,2,1,2,1,2,16,512]{7,6,5,4,3,2,1,0:T(8,128)(2,1)S(1)} %pad_maximum_fusion.18), channel_id=1, source_target_pairs={{0,8},{1,9},{2,10},{3,11},{4,12},{5,13},{6,14},{7,15},{8,0},{9,1},... | collective-permute-start | bytes 786440 | tf_op jit(solution)/shard_map/ppermute | solution.py:76
  127.5 7.1 %collective-permute-start.28 = (bf16[2,2,2,2,1,1,16,512]{7,6,5,4,3,2,1,0:T(8,128)(2,1)S(1)}, bf16[2,2,2,2,1,1,16,512]{7,6,5,4,3,2,1,0:T(8,128)(2,1)S(1)}, u32[]{:S(2)}, u32[]{:S(2)}) collective-permute-start(bf16[2,2,2,2,1,1,16,512]{7,6,5,4,3,2,1,0:T(8,128)(2,1)S(1)} %pad_maximum_fusion.16), channel_id=1, source_target_pairs={{0,1},{1,0},{2,3},{3,2},{4,5},{5,4},{6,7},{7,6},{8,9},{9,8},{10,11... | collective-permute-start | bytes 786440 | tf_op jit(solution)/shard_map/ppermute | solution.py:76
  134.6 7.4 %collective-permute-start.39 = (bf16[2,2,2,2,1,2,16,512]{7,6,5,4,3,2,1,0:T(8,128)(2,1)}, bf16[2,2,2,2,1,2,16,512]{7,6,5,4,3,2,1,0:T(8,128)(2,1)}, u32[]{:S(2)}, u32[]{:S(2)}) collective-permute-start(bf16[2,2,2,2,1,2,16,512]{7,6,5,4,3,2,1,0:T(8,128)(2,1)} %pad_maximum_fusion.12), channel_id=1, source_target_pairs={{0,2},{1,3},{2,0},{3,1},{4,6},{5,7},{6,4},{7,5},{8,10},{9,11},{10,... | collective-permute-start | bytes 1572872 | tf_op jit(solution)/shard_map/ppermute | solution.py:76
  135.5 9.6 %collective-permute-start.29 = (bf16[2,2,2,2,1,2,16,512]{7,6,5,4,3,2,1,0:T(8,128)(2,1)}, bf16[2,2,2,2,1,2,16,512]{7,6,5,4,3,2,1,0:T(8,128)(2,1)}, u32[]{:S(2)}, u32[]{:S(2)}) collective-permute-start(bf16[2,2,2,2,1,2,16,512]{7,6,5,4,3,2,1,0:T(8,128)(2,1)} %pad_maximum_fusion.10), channel_id=1, source_target_pairs={{0,2},{1,3},{2,0},{3,1},{4,6},{5,7},{6,4},{7,5},{8,10},{9,11},{10,... | collective-permute-start | bytes 1572872 | tf_op jit(solution)/shard_map/ppermute | solution.py:76
  (46 other events, 39.4 us)

commit v7 on v6

--- a/solution.py
+++ b/solution.py
@@ -143,7 +143,11 @@
             own.reshape([ndisp, 2] + [1] * nbits + [rows, nev]), gy_bits, nbits, count, 2
         )
         elem = grown.reshape(ndisp, 2, ny * rows, nev)
-        contracted = jnp.take(jnp.stack(products, 0), directions, axis=0, mode="clip")
+        slots = jnp.arange(ndisp, dtype=directions.dtype)
+        contracted = jnp.zeros((ndisp,) + products[0].shape, products[0].dtype)
+        for d, product in enumerate(products):
+            slot = jnp.sum(jnp.where(directions == d, slots, 0))
+            contracted = lax.dynamic_update_slice_in_dim(contracted, product[None], slot, axis=0)
         return (elem, contracted)
 
     return local

time: 153 us -> 157 us (1.026)
  between operations: 2.31 us -> 9.96 us
  starting transfers between devices: 41.5 us -> 37.4 us
  waiting for transfers between devices: 41.1 us -> 43.7 us
    ppermute x21, starting transfers between devices: 21.6 us -> 17.5 us  [all_gather(): other = lax.ppermute(buf, ALL, xor_pairs(count, b))]
    ppermute x21, waiting for transfers between devices: 12.2 us -> 14.9 us  [all_gather(): other = lax.ppermute(buf, ALL, xor_pairs(count, b))]
    gather x1 -> x0, local copies, waits for them, and re-layouts: 2.12 us -> none  [local(): jnp.take(jnp.stack(products, 0), directions, axis=0, mode='clip')]
    another operation x13 -> x12, other arithmetic: 7.51 us -> 6.04 us
    unnamed x131 -> x121, local copies, waits for them, and re-layouts: 6.12 us -> 7.31 us
  transfers between devices with their start and end apart: 45 -> 45, of which waited for: 18 -> 19; matrix products, arithmetic and copies ran while one was open for 32% -> 30% of each run, Pallas kernels for 0% -> 0%
where the time goes in v7:
time: 157 us; the launch traced here: 156 us
  waiting for transfers between devices  43.7 us (28%)
  starting transfers between devices  37.4 us (24%)
  local copies, waits for them, and re-layouts  27.5 us (18%)
  other arithmetic  26.2 us (17%)
  matrix products  11.6 us (7%)
  between operations  9.96 us (6%)
    ppermute x20, waiting for transfers between devices, reduce_scatter(): buf = keep + lax.ppermute(send, ALL, xor_pairs(count, b))  28.7 us
    ppermute x21, starting transfers between devices, all_gather(): other = lax.ppermute(buf, ALL, xor_pairs(count, b))  17.5 us
    ppermute x21, waiting for transfers between devices, all_gather(): other = lax.ppermute(buf, ALL, xor_pairs(count, b))  14.9 us
    ppermute x20, starting transfers between devices, reduce_scatter(): buf = keep + lax.ppermute(send, ALL, xor_pairs(count, b))  12.9 us
    unnamed x121, local copies, waits for them, and re-layouts  7.31 us
    dot_general x4, matrix products, local(): jnp.dot(left, field.reshape(2 * depth, nev), preferred_element_type=jnp.f...  7.12 us
    another operation x12, other arithmetic  6.04 us
    dot_general x4, matrix products, local(): product = jnp.dot(lhs, rhs, preferred_element_type=jnp.float32)  4.43 us
  transfers between devices with their start and end apart: 45, of which 19 were waited for; matrix products, arithmetic and copies ran while one was open for 30% of the time, Pallas kernels for 0%

profile of v7, /device:TPU:0, one launch (start us, length us, event | category | flops | bytes accessed | tf_op | source)
XLA Modules:
  0.0 156.2 jit_solution(8178041342888115477)
XLA Ops:
  0.6 1.0 slice_bitcast_fusion.21
  2.4 1.9 %convert_element_type.66 = f32[2,3,4,4,16,512]{5,4,3,2,1,0:T(8,128)S(1)} convert(bf16[2,3,4,4,16,512]{5,4,3,2,1,0:T(8,128)(2,1)} %param.5) | non-fusion elementwise | flops 786432 | bytes 4718592 | tf_op jit(solution)/shard_map/convert_element_type | solution.py:13
  6.8 1.0 pad_maximum_fusion.19
  7.8 3.0 %collective-permute-start.18 = (bf16[2,3,4,4,1,512]{5,4,3,2,1,0:T(2,128)(2,1)}, bf16[2,3,4,4,1,512]{5,4,3,2,1,0:T(2,128)(2,1)}, u32[]{:S(2)}, u32[]{:S(2)}) collective-permute-start(bf16[2,3,4,4,1,512]{5,4,3,2,1,0:T(2,128)(2,1)} %pad_maximum_fusion.19), channel_id=1, source_target_pairs={{0,1},{1,0},{2,3},{3,2},{4,5},{5,4},{6,7},{7,6},{8,9},{9,8},{10,11... | collective-permute-start | bytes 294920 | tf_op jit(solution)/shard_map/ppermute | solution.py:97
  14.1 1.2 copy-done
  16.4 4.0 %collective-permute-start = (bf16[2,3,4,1,16,512]{5,4,3,2,1,0:T(8,128)(2,1)}, bf16[2,3,4,1,16,512]{5,4,3,2,1,0:T(8,128)(2,1)}, u32[]{:S(2)}, u32[]{:S(2)}) collective-permute-start(bf16[2,3,4,1,16,512]{5,4,3,2,1,0:T(8,128)(2,1)} %slice.141), channel_id=1, source_target_pairs={{0,30},{2,0},{4,2},{6,4},{8,6},{10,8},{12,10},{14,12},{16,14},{18,... | collective-permute-start | bytes 1179656 | tf_op jit(solution)/shard_map/ppermute | solution.py:94
  21.1 1.3 slice_bitcast_fusion
  22.3 1.0 fusion.36
  24.1 1.1 slice.140
  31.0 1.1 fusion.37
  32.3 1.6 %gather_fusion.1 = bf16[4,2,64,1024]{3,2,1,0:T(8,128)(2,1)} fusion(bf16[2,64,4,1024]{3,1,2,0:T(8,128)(2,1)S(1)} %maximum_maximum_fusion.1, s32[1024]{0:T(1024)S(1)} %pad_clamp_fusion), kind=kCustom, calls=%fused_computation.1 | custom fusion | bytes 2097168 | tf_op jit(solution)/shard_map/jit(_take)/gather | solution.py:124
  33.9 2.1 %copy.66 = bf16[2,64,4,1024]{3,2,1,0:T(4,128)(2,1)S(1)} copy(bf16[2,64,4,1024]{3,1,0,2:T(8,128)(2,1)} %bitcast.541) | data formatting | bytes 2097152 | tf_op jit(solution)/shard_map/jit(_take)/gather | solution.py:124
  36.0 1.1 reshape.2102
  39.7 1.9 %maximum_maximum_fusion = bf16[1024,1536]{1,0:T(8,128)(2,1)S(1)} fusion(bf16[512,768]{1,0:T(8,128)(2,1)} %get-tuple-element.31, bf16[512,768]{1,0:T(8,128)(2,1)S(1)} %copy-done.10, bf16[512,768]{1,0:T(8,128)(2,1)} %get-tuple-element.30), kind=kLoop, calls=%fused_computation.2 | loop fusion | flops 12582912 | bytes 5505024 | tf_op jit(solution)/shard_map/concatenate | solution.py:108
  41.8 1.7 %fusion.4 = bf16[2,3,4,4,16,512]{5,4,3,2,1,0:T(8,128)(2,1)S(1)} fusion(bf16[1,3,4,4,16,512]{5,4,3,2,1,0:T(8,128)(2,1)S(1)} %copy-done.8, bf16[1,3,4,4,16,512]{5,4,3,2,1,0:T(8,128)(2,1)S(1)} %copy-done.6, bf16[2,3,4,4,1,512]{5,4,3,2,1,0:T(2,128)(2,1)} %collective-permute-done.18), kind=kLoop, calls=%fused_computation.8 | loop fusion | flops 4718592 | bytes 3244032 | tf_op jit(solution)/shard_map/concatenate | solution.py:104
  43.5 1.8 %fusion = f32[2,2,2,2,2,2,16,512]{7,6,0,5,4,3,2,1:T(8,128)S(1)} fusion(bf16[1536,512,1,1,1,1,1,1]{1,0,2,7,6,5,4,3:T(8,128)(2,1)S(1)} %bitcast.549, bf16[2,2,2,2,2,2,16,1536]{7,6,5,4,3,2,1,0:T(8,128)(2,1)S(1)} %bitcast.542), kind=kOutput, calls=%fused_computation.3 | convolution fusion | flops 1610612736 | bytes 6815744 | tf_op jit(solution)/shard_map/dot_general | solution.py:130
  45.5 1.1 copy.55
  49.5 1.8 %fusion.2 = f32[2,2,2,2,2,2,16,512]{7,6,0,5,4,3,2,1:T(8,128)S(1)} fusion(bf16[1536,512,1,1,1,1,1,1]{1,0,2,7,6,5,4,3:T(8,128)(2,1)S(1)} %bitcast.551, bf16[2,2,2,2,2,2,16,1536]{7,6,5,4,3,2,1,0:T(8,128)(2,1)S(1)} %bitcast.543), kind=kOutput, calls=%fused_computation.5 | convolution fusion | flops 1610612736 | bytes 6815744 | tf_op jit(solution)/shard_map/dot_general | solution.py:130
  52.6 1.2 fusion.5
  53.8 1.8 %fusion.39 = f32[2,2,2,2,2,2,16,512]{7,6,5,4,3,2,1,0:T(8,128)S(1)} fusion(bf16[2,2,2,2,2,2,16,1536]{7,6,5,4,3,2,1,0:T(8,128)(2,1)S(1)} %bitcast.544, bf16[1536,512,1,1,1,1,1,1]{1,0,7,6,5,4,3,2:T(8,128)(2,1)S(1)} %bitcast.548), kind=kOutput, calls=%fused_computation.262 | convolution fusion | flops 1610612736 | bytes 6815744 | tf_op jit(solution)/shard_map/dot_general | solution.py:130
  56.9 1.2 maximum_convert_fusion
  60.3 1.8 %fusion.38 = f32[2,2,2,2,2,2,16,512]{7,6,5,4,3,2,1,0:T(8,128)S(1)} fusion(bf16[2,2,2,2,2,2,16,1536]{7,6,5,4,3,2,1,0:T(8,128)(2,1)S(1)} %bitcast.545, bf16[1536,512,1,1,1,1,1,1]{1,0,7,6,5,4,3,2:T(8,128)(2,1)S(1)} %bitcast.550), kind=kOutput, calls=%fused_computation.261 | convolution fusion | flops 1610612736 | bytes 6815744 | tf_op jit(solution)/shard_map/dot_general | solution.py:130
  63.0 1.6 collective-permute-start.20
  65.7 1.1 collective-permute-start.2
  66.8 11.1 %collective-permute-done.20 = f32[2,2,2,2,1,1,16,512]{7,6,0,5,4,3,2,1:T(8,128)S(1)} collective-permute-done((f32[2,2,2,2,1,1,16,512]{7,6,0,5,4,3,2,1:T(8,128)S(1)}, f32[2,2,2,2,1,1,16,512]{7,6,0,5,4,3,2,1:T(8,128)S(1)}, u32[]{:S(2)}, u32[]{:S(2)}) %collective-permute-start.20) | collective-permute-done | bytes 524320 | tf_op jit(solution)/shard_map/ppermute | solution.py:67
  78.7 5.8 %collective-permute-done.21 = f32[2,2,2,1,1,1,16,512]{7,6,0,5,4,3,2,1:T(8,128)S(1)} collective-permute-done((f32[2,2,2,1,1,1,16,512]{7,6,0,5,4,3,2,1:T(8,128)S(1)}, f32[2,2,2,1,1,1,16,512]{7,6,0,5,4,3,2,1:T(8,128)S(1)}, u32[]{:S(2)}, u32[]{:S(2)}) %collective-permute-start.21) | collective-permute-done | bytes 262176 | tf_op jit(solution)/shard_map/ppermute | solution.py:67
  84.6 2.4 %collective-permute-done.9 = f32[2,2,1,1,1,2,16,512]{7,6,0,5,4,3,2,1:T(8,128)S(1)} collective-permute-done((f32[2,2,1,1,1,2,16,512]{7,6,0,5,4,3,2,1:T(8,128)S(1)}, f32[2,2,1,1,1,2,16,512]{7,6,0,5,4,3,2,1:T(8,128)S(1)}, u32[]{:S(2)}, u32[]{:S(2)}) %collective-permute-start.9) | collective-permute-done | bytes 262176 | tf_op jit(solution)/shard_map/ppermute | solution.py:67
  87.4 2.3 %collective-permute-start.15 = (f32[2,2,1,2,1,1,16,512]{7,6,5,4,3,2,1,0:T(8,128)S(1)}, f32[2,2,1,2,1,1,16,512]{7,6,5,4,3,2,1,0:T(8,128)S(1)}, u32[]{:S(2)}, u32[]{:S(2)}) collective-permute-start(f32[2,2,1,2,1,1,16,512]{7,6,5,4,3,2,1,0:T(8,128)S(1)} %constant_dynamic-slice_fusion.7), channel_id=1, source_target_pairs={{0,1},{1,0},{2,3},{3,2},{4,5},{5,4},{6,7},{7,6},{8,9},{9,8},{10,11... | collective-permute-start | bytes 786440 | tf_op jit(solution)/shard_map/ppermute | solution.py:67
  89.8 1.1 collective-permute-start.3
  91.0 2.6 %collective-permute-done.10 = f32[2,2,1,1,1,1,16,512]{7,6,0,5,4,3,2,1:T(8,128)S(1)} collective-permute-done((f32[2,2,1,1,1,1,16,512]{7,6,0,5,4,3,2,1:T(8,128)S(1)}, f32[2,2,1,1,1,1,16,512]{7,6,0,5,4,3,2,1:T(8,128)S(1)}, u32[]{:S(2)}, u32[]{:S(2)}) %collective-permute-start.10) | collective-permute-done | bytes 131104 | tf_op jit(solution)/shard_map/ppermute | solution.py:67
  94.0 2.9 %collective-permute-done.23 = f32[2,1,1,1,1,1,16,512]{7,6,0,5,4,3,2,1:T(8,128)S(1)} collective-permute-done((f32[2,1,1,1,1,1,16,512]{7,6,0,5,4,3,2,1:T(8,128)S(1)}, f32[2,1,1,1,1,1,16,512]{7,6,0,5,4,3,2,1:T(8,128)S(1)}, u32[]{:S(2)}, u32[]{:S(2)}) %collective-permute-start.23) | collective-permute-done | bytes 65568 | tf_op jit(solution)/shard_map/ppermute | solution.py:67
  97.0 2.2 %collective-permute-done.11 = f32[2,1,1,1,1,1,16,512]{7,6,0,5,4,3,2,1:T(8,128)S(1)} collective-permute-done((f32[2,1,1,1,1,1,16,512]{7,6,0,5,4,3,2,1:T(8,128)S(1)}, f32[2,1,1,1,1,1,16,512]{7,6,0,5,4,3,2,1:T(8,128)S(1)}, u32[]{:S(2)}, u32[]{:S(2)}) %collective-permute-start.11) | collective-permute-done | bytes 65568 | tf_op jit(solution)/shard_map/ppermute | solution.py:67
  100.0 1.8 %collective-permute-done.40 = bf16[2,1,1,1,1,1,16,512]{7,6,5,4,3,2,1,0:T(8,128)(2,1)S(1)} collective-permute-done((bf16[2,1,1,1,1,1,16,512]{7,6,5,4,3,2,1,0:T(8,128)(2,1)S(1)}, bf16[2,1,1,1,1,1,16,512]{7,6,5,4,3,2,1,0:T(8,128)(2,1)S(1)}, u32[]{:S(2)}, u32[]{:S(2)}) %collective-permute-start.40) | collective-permute-done | bytes 32800 | tf_op jit(solution)/shard_map/ppermute | solution.py:76
  102.0 2.1 %collective-permute-done.30 = bf16[2,1,1,1,1,1,16,512]{7,6,0,5,4,3,2,1:T(8,128)(2,1)S(1)} collective-permute-done((bf16[2,1,1,1,1,1,16,512]{7,6,0,5,4,3,2,1:T(8,128)(2,1)S(1)}, bf16[2,1,1,1,1,1,16,512]{7,6,0,5,4,3,2,1:T(8,128)(2,1)S(1)}, u32[]{:S(2)}, u32[]{:S(2)}) %collective-permute-start.30) | collective-permute-done | bytes 32800 | tf_op jit(solution)/shard_map/ppermute | solution.py:76
  104.1 1.4 collective-permute-start.31
  105.7 0.9 collective-permute-start.16
  107.0 1.9 %collective-permute-start.42 = (bf16[2,2,2,1,1,1,16,512]{7,6,5,4,3,2,1,0:T(8,128)(2,1)S(1)}, bf16[2,2,2,1,1,1,16,512]{7,6,5,4,3,2,1,0:T(8,128)(2,1)S(1)}, u32[]{:S(2)}, u32[]{:S(2)}) collective-permute-start(bf16[2,2,2,1,1,1,16,512]{7,6,5,4,3,2,1,0:T(8,128)(2,1)S(1)} %pad_maximum_fusion.23), channel_id=1, source_target_pairs={{0,4},{1,5},{2,6},{3,7},{4,0},{5,1},{6,2},{7,3},{8,12},{9,13},{10,... | collective-permute-start | bytes 393224 | tf_op jit(solution)/shard_map/ppermute | solution.py:76
  109.0 1.2 collective-permute-start.32
  110.1 1.1 collective-permute-done.16
  111.3 1.2 collective-permute-start.17
  112.5 1.9 %collective-permute-start.5 = (f32[2,1,1,1,1,1,16,512]{7,6,5,4,3,2,1,0:T(8,128)S(1)}, f32[2,1,1,1,1,1,16,512]{7,6,5,4,3,2,1,0:T(8,128)S(1)}, u32[]{:S(2)}, u32[]{:S(2)}) collective-permute-start(f32[2,1,1,1,1,1,16,512]{7,6,5,4,3,2,1,0:T(8,128)S(1)} %constant_dynamic-slice_fusion.15), channel_id=1, source_target_pairs={{0,16},{1,17},{2,18},{3,19},{4,20},{5,21},{6,22},{7,23},{8,24},{9,... | collective-permute-start | bytes 196616 | tf_op jit(solution)/shard_map/ppermute | solution.py:67
  114.5 1.3 collective-permute-start.43
  115.8 0.9 collective-permute-start.33
  116.9 2.8 %collective-permute-start.35 = (bf16[2,1,1,1,1,1,16,512]{7,6,5,4,3,2,1,0:T(8,128)(2,1)S(1)}, bf16[2,1,1,1,1,1,16,512]{7,6,5,4,3,2,1,0:T(8,128)(2,1)S(1)}, u32[]{:S(2)}, u32[]{:S(2)}) collective-permute-start(bf16[2,1,1,1,1,1,16,512]{7,6,5,4,3,2,1,0:T(8,128)(2,1)S(1)} %get-tuple-element.64), channel_id=1, source_target_pairs={{0,16},{1,17},{2,18},{3,19},{4,20},{5,21},{6,22},{7,23},{8,24},{9,... | collective-permute-start | bytes 98312 | tf_op jit(solution)/shard_map/ppermute | solution.py:76
  120.6 1.0 collective-permute-start.24
  121.8 1.9 %collective-permute-start.36 = (bf16[2,2,1,1,1,1,16,512]{7,6,5,4,3,2,1,0:T(8,128)(2,1)S(1)}, bf16[2,2,1,1,1,1,16,512]{7,6,5,4,3,2,1,0:T(8,128)(2,1)S(1)}, u32[]{:S(2)}, u32[]{:S(2)}) collective-permute-start(bf16[2,2,1,1,1,1,16,512]{7,6,5,4,3,2,1,0:T(8,128)(2,1)S(1)} %pad_maximum_fusion.26), channel_id=1, source_target_pairs={{0,4},{1,5},{2,6},{3,7},{4,0},{5,1},{6,2},{7,3},{8,12},{9,13},{10,... | collective-permute-start | bytes 196616 | tf_op jit(solution)/shard_map/ppermute | solution.py:76
  123.7 0.9 collective-permute-done.25
  124.9 1.3 collective-permute-done.36
  126.2 1.0 collective-permute-start.37
  127.2 1.8 %collective-permute-done.26 = bf16[2,2,1,1,1,1,16,512]{7,6,5,4,3,2,1,0:T(8,128)(2,1)S(1)} collective-permute-done((bf16[2,2,1,1,1,1,16,512]{7,6,5,4,3,2,1,0:T(8,128)(2,1)S(1)}, bf16[2,2,1,1,1,1,16,512]{7,6,5,4,3,2,1,0:T(8,128)(2,1)S(1)}, u32[]{:S(2)}, u32[]{:S(2)}) %collective-permute-start.26) | collective-permute-done | bytes 65568 | tf_op jit(solution)/shard_map/ppermute | solution.py:76
  130.0 1.2 collective-permute-done.37
  131.3 1.1 collective-permute-start.38
  132.4 1.7 %collective-permute-done.27 = bf16[2,2,2,1,1,1,16,512]{7,6,5,4,3,2,1,0:T(8,128)(2,1)S(1)} collective-permute-done((bf16[2,2,2,1,1,1,16,512]{7,6,5,4,3,2,1,0:T(8,128)(2,1)S(1)}, bf16[2,2,2,1,1,1,16,512]{7,6,5,4,3,2,1,0:T(8,128)(2,1)S(1)}, u32[]{:S(2)}, u32[]{:S(2)}) %collective-permute-start.27) | collective-permute-done | bytes 131104 | tf_op jit(solution)/shard_map/ppermute | solution.py:76
  135.6 2.7 %collective-permute-done.38 = bf16[2,2,1,2,1,2,16,512]{7,6,5,4,3,2,1,0:T(8,128)(2,1)S(1)} collective-permute-done((bf16[2,2,1,2,1,2,16,512]{7,6,5,4,3,2,1,0:T(8,128)(2,1)S(1)}, bf16[2,2,1,2,1,2,16,512]{7,6,5,4,3,2,1,0:T(8,128)(2,1)S(1)}, u32[]{:S(2)}, u32[]{:S(2)}) %collective-permute-start.38) | collective-permute-done | bytes 262176 | tf_op jit(solution)/shard_map/ppermute | solution.py:76
  139.3 1.3 collective-permute-done.28
  141.6 1.0 copy-done.12
  144.0 1.0 copy-done.13
  146.1 1.2 broadcast_select_fusion.3
  147.4 1.5 convolution_convert_fusion.1
  148.9 1.4 broadcast_in_dim_reshape.14
  150.3 1.1 broadcast_select_fusion.7
  151.6 1.5 convolution_convert_fusion.3
  153.1 1.4 broadcast_in_dim_reshape.12
  154.9 1.3 copy-done.11
  (300 shorter events, 32.0 us)
Async XLA Ops:
  2.3 2.0 %copy-start.31 = (f32[4,4,16]{2,1,0:T(4,128)}, f32[4,4,16]{2,1,0:T(4,128)S(1)}, u32[]{:S(2)}) copy-start(f32[4,4,16]{2,1,0:T(4,128)S(1)} %get-tuple-element.105) | copy-start | bytes 3076
  2.3 2.5 %copy-start.17 = (f32[4,4,16]{2,1,0:T(4,128)}, f32[4,4,16]{2,1,0:T(4,128)S(1)}, u32[]{:S(2)}) copy-start(f32[4,4,16]{2,1,0:T(4,128)S(1)} %get-tuple-element.98) | copy-start | bytes 3076
  2.3 2.5 %copy-start.29 = (f32[4,4,16]{2,1,0:T(4,128)}, f32[4,4,16]{2,1,0:T(4,128)S(1)}, u32[]{:S(2)}) copy-start(f32[4,4,16]{2,1,0:T(4,128)S(1)} %get-tuple-element.104) | copy-start | bytes 3076
  2.3 3.0 %copy-start.15 = (f32[4,4,16]{2,1,0:T(4,128)}, f32[4,4,16]{2,1,0:T(4,128)S(1)}, u32[]{:S(2)}) copy-start(f32[4,4,16]{2,1,0:T(4,128)S(1)} %get-tuple-element.96) | copy-start | bytes 3076
  2.3 3.0 %copy-start.27 = (f32[4,4,16]{2,1,0:T(4,128)}, f32[4,4,16]{2,1,0:T(4,128)S(1)}, u32[]{:S(2)}) copy-start(f32[4,4,16]{2,1,0:T(4,128)S(1)} %get-tuple-element.102) | copy-start | bytes 3076
  7.8 33.9 %collective-permute-start.18 = (bf16[2,3,4,4,1,512]{5,4,3,2,1,0:T(2,128)(2,1)}, bf16[2,3,4,4,1,512]{5,4,3,2,1,0:T(2,128)(2,1)}, u32[]{:S(2)}, u32[]{:S(2)}) collective-permute-start(bf16[2,3,4,4,1,512]{5,4,3,2,1,0:T(2,128)(2,1)} %pad_maximum_fusion.19), channel_id=1, source_target_pairs={{0,1},{1,0},{2,3},{3,2},{4,5},{5,4},{6,7},{7,6},{8,9},{9,8},{10,11... | collective-permute-start | bytes 294920 | tf_op jit(solution)/shard_map/ppermute | solution.py:97
  13.1 2.3 %copy-start.1 = (bf16[1,3,4,4,16,512]{5,4,3,2,1,0:T(8,128)(2,1)}, bf16[1,3,4,4,16,512]{5,4,3,2,1,0:T(8,128)(2,1)S(1)}, u32[]{:S(2)}) copy-start(bf16[1,3,4,4,16,512]{5,4,3,2,1,0:T(8,128)(2,1)S(1)} %maximum_bitcast_fusion.4) | copy-start | bytes 2359300
  13.2 2.1 %copy-start = (bf16[2,3,4,4,16,512]{5,4,3,2,1,0:T(8,128)(2,1)S(1)}, bf16[2,3,4,4,16,512]{5,4,3,2,1,0:T(8,128)(2,1)}, u32[]{:S(2)}) copy-start(bf16[2,3,4,4,16,512]{5,4,3,2,1,0:T(8,128)(2,1)} %param.5) | copy-start | bytes 4718596
  13.3 7.1 %copy-start.3 = (bf16[1,3,4,4,16,512]{5,4,3,2,1,0:T(8,128)(2,1)}, bf16[1,3,4,4,16,512]{5,4,3,2,1,0:T(8,128)(2,1)S(1)}, u32[]{:S(2)}) copy-start(bf16[1,3,4,4,16,512]{5,4,3,2,1,0:T(8,128)(2,1)S(1)} %maximum_bitcast_fusion.5) | copy-start | bytes 2359300
  14.1 37.9 %collective-permute-start.12 = (bf16[2,3,4,1,16,512]{5,4,3,2,1,0:T(8,128)(2,1)}, bf16[2,3,4,1,16,512]{5,4,3,2,1,0:T(8,128)(2,1)}, u32[]{:S(2)}, u32[]{:S(2)}) collective-permute-start(bf16[2,3,4,1,16,512]{5,4,3,2,1,0:T(8,128)(2,1)} %pad_maximum_fusion.13), channel_id=1, source_target_pairs={{0,2},{2,4},{4,6},{6,8},{8,10},{10,12},{12,14},{14,16},{16,18},{18... | collective-permute-start | bytes 1179656 | tf_op jit(solution)/shard_map/ppermute | solution.py:95
  15.5 30.0 %collective-permute-start.6 = (bf16[2,3,4,4,1,512]{5,3,4,2,1,0:T(4,128)(2,1)S(1)}, bf16[2,3,4,4,1,512]{5,3,4,2,1,0:T(4,128)(2,1)}, u32[]{:S(2)}, u32[]{:S(2)}) collective-permute-start(bf16[2,3,4,4,1,512]{5,3,4,2,1,0:T(4,128)(2,1)S(1)} %copy.80), channel_id=1, source_target_pairs={{0,1},{1,0},{2,3},{3,2},{4,5},{5,4},{6,7},{7,6},{8,9},{9,8},{10,11... | collective-permute-start | bytes 294920 | tf_op jit(solution)/shard_map/ppermute | solution.py:96
  16.4 39.9 %collective-permute-start = (bf16[2,3,4,1,16,512]{5,4,3,2,1,0:T(8,128)(2,1)}, bf16[2,3,4,1,16,512]{5,4,3,2,1,0:T(8,128)(2,1)}, u32[]{:S(2)}, u32[]{:S(2)}) collective-permute-start(bf16[2,3,4,1,16,512]{5,4,3,2,1,0:T(8,128)(2,1)} %slice.141), channel_id=1, source_target_pairs={{0,30},{2,0},{4,2},{6,4},{8,6},{10,8},{12,10},{14,12},{16,14},{18,... | collective-permute-start | bytes 1179656 | tf_op jit(solution)/shard_map/ppermute | solution.py:94
  24.1 8.1 %copy-start.59 = (s32[4]{0:T(128)S(1)}, s32[4]{0:T(128)}, u32[]{:S(2)}) copy-start(s32[4]{0:T(128)} %param.8) | copy-start | bytes 52
  33.9 5.8 %copy-start.10 = (bf16[512,768]{1,0:T(8,128)(2,1)S(1)}, bf16[512,768]{1,0:T(8,128)(2,1)}, u32[]{:S(2)}) copy-start(bf16[512,768]{1,0:T(8,128)(2,1)} %fusion.36) | copy-start | bytes 2359300
  39.7 2.0 %copy-start.58 = (s32[4]{0:T(128)S(1)}, s32[4]{0:T(128)}, u32[]{:S(2)}) copy-start(s32[4]{0:T(128)} %param.7) | copy-start | bytes 52
  39.7 2.0 %copy-start.6 = (bf16[1,3,4,4,16,512]{5,4,3,2,1,0:T(8,128)(2,1)S(1)}, bf16[1,3,4,4,16,512]{5,4,3,2,1,0:T(8,128)(2,1)}, u32[]{:S(2)}) copy-start(bf16[1,3,4,4,16,512]{5,4,3,2,1,0:T(8,128)(2,1)} %copy-done.5) | copy-start | bytes 2359300
  39.7 2.1 %copy-start.8 = (bf16[1,3,4,4,16,512]{5,4,3,2,1,0:T(8,128)(2,1)S(1)}, bf16[1,3,4,4,16,512]{5,4,3,2,1,0:T(8,128)(2,1)}, u32[]{:S(2)}) copy-start(bf16[1,3,4,4,16,512]{5,4,3,2,1,0:T(8,128)(2,1)} %copy-done.7) | copy-start | bytes 2359300
  45.4 17.3 %collective-permute-start.19 = (f32[2,2,2,2,1,2,16,512]{7,6,0,5,4,3,2,1:T(8,128)S(1)}, f32[2,2,2,2,1,2,16,512]{7,6,0,5,4,3,2,1:T(8,128)S(1)}, u32[]{:S(2)}, u32[]{:S(2)}) collective-permute-start(f32[2,2,2,2,1,2,16,512]{7,6,0,5,4,3,2,1:T(8,128)S(1)} %constant_dynamic-slice_fusion.4), channel_id=1, source_target_pairs={{0,2},{1,3},{2,0},{3,1},{4,6},{5,7},{6,4},{7,5},{8,10},{9,11},{10,... | collective-permute-start | bytes 3145736 | tf_op jit(solution)/shard_map/ppermute | solution.py:67
  51.4 13.2 %collective-permute-start.7 = (f32[2,2,2,2,1,2,16,512]{7,6,0,5,4,3,2,1:T(8,128)S(1)}, f32[2,2,2,2,1,2,16,512]{7,6,0,5,4,3,2,1:T(8,128)S(1)}, u32[]{:S(2)}, u32[]{:S(2)}) collective-permute-start(f32[2,2,2,2,1,2,16,512]{7,6,0,5,4,3,2,1:T(8,128)S(1)} %constant_dynamic-slice_fusion.14), channel_id=1, source_target_pairs={{0,2},{1,3},{2,0},{3,1},{4,6},{5,7},{6,4},{7,5},{8,10},{9,11},{10,... | collective-permute-start | bytes 3145736 | tf_op jit(solution)/shard_map/ppermute | solution.py:67
  55.7 2.4 %copy-start.34 = (f32[4,4,16]{2,1,0:T(4,128)S(1)}, f32[4,4,16]{2,1,0:T(4,128)}, u32[]{:S(2)}) copy-start(f32[4,4,16]{2,1,0:T(4,128)} %copy-done.33) | copy-start | bytes 3076
  55.7 2.4 %copy-start.36 = (f32[4,4,16]{2,1,0:T(4,128)S(1)}, f32[4,4,16]{2,1,0:T(4,128)}, u32[]{:S(2)}) copy-start(f32[4,4,16]{2,1,0:T(4,128)} %copy-done.35) | copy-start | bytes 3076
  55.7 2.4 %copy-start.38 = (f32[4,4,16]{2,1,0:T(4,128)S(1)}, f32[4,4,16]{2,1,0:T(4,128)}, u32[]{:S(2)}) copy-start(f32[4,4,16]{2,1,0:T(4,128)} %copy-done.37) | copy-start | bytes 3076
  55.7 2.4 %copy-start.54 = (f32[4,4,16]{2,1,0:T(4,128)S(1)}, f32[4,4,16]{2,1,0:T(4,128)}, u32[]{:S(2)}) copy-start(f32[4,4,16]{2,1,0:T(4,128)} %get-tuple-element.71) | copy-start | bytes 3076
  55.7 2.4 %copy-start.55 = (f32[4,4,16]{2,1,0:T(4,128)S(1)}, f32[4,4,16]{2,1,0:T(4,128)}, u32[]{:S(2)}) copy-start(f32[4,4,16]{2,1,0:T(4,128)} %get-tuple-element.73) | copy-start | bytes 3076
  55.7 2.4 %copy-start.56 = (f32[4,4,16]{2,1,0:T(4,128)S(1)}, f32[4,4,16]{2,1,0:T(4,128)}, u32[]{:S(2)}) copy-start(f32[4,4,16]{2,1,0:T(4,128)} %get-tuple-element.75) | copy-start | bytes 3076
  55.7 9.2 %collective-permute-start.13 = (f32[2,2,2,2,1,2,16,512]{7,6,5,4,3,2,1,0:T(8,128)S(1)}, f32[2,2,2,2,1,2,16,512]{7,6,5,4,3,2,1,0:T(8,128)S(1)}, u32[]{:S(2)}, u32[]{:S(2)}) collective-permute-start(f32[2,2,2,2,1,2,16,512]{7,6,5,4,3,2,1,0:T(8,128)S(1)} %constant_dynamic-slice_fusion.9), channel_id=1, source_target_pairs={{0,2},{1,3},{2,0},{3,1},{4,6},{5,7},{6,4},{7,5},{8,10},{9,11},{10,... | collective-permute-start | bytes 3145736 | tf_op jit(solution)/shard_map/ppermute | solution.py:67
  62.1 3.3 %collective-permute-start.1 = (f32[2,2,2,2,1,2,16,512]{7,6,5,4,3,2,1,0:T(8,128)S(1)}, f32[2,2,2,2,1,2,16,512]{7,6,5,4,3,2,1,0:T(8,128)S(1)}, u32[]{:S(2)}, u32[]{:S(2)}) collective-permute-start(f32[2,2,2,2,1,2,16,512]{7,6,5,4,3,2,1,0:T(8,128)S(1)} %constant_dynamic-slice_fusion.19), channel_id=1, source_target_pairs={{0,2},{1,3},{2,0},{3,1},{4,6},{5,7},{6,4},{7,5},{8,10},{9,11},{10,... | collective-permute-start | bytes 3145736 | tf_op jit(solution)/shard_map/ppermute | solution.py:67
  63.0 14.9 %collective-permute-start.20 = (f32[2,2,2,2,1,1,16,512]{7,6,0,5,4,3,2,1:T(8,128)S(1)}, f32[2,2,2,2,1,1,16,512]{7,6,0,5,4,3,2,1:T(8,128)S(1)}, u32[]{:S(2)}, u32[]{:S(2)}) collective-permute-start(f32[2,2,2,2,1,1,16,512]{7,6,0,5,4,3,2,1:T(8,128)S(1)} %constant_dynamic-slice_fusion.3), channel_id=1, source_target_pairs={{0,1},{1,0},{2,3},{3,2},{4,5},{5,4},{6,7},{7,6},{8,9},{9,8},{10,11... | collective-permute-start | bytes 1572872 | tf_op jit(solution)/shard_map/ppermute | solution.py:67
  64.9 13.6 %collective-permute-start.8 = (f32[2,2,2,1,1,2,16,512]{7,6,0,5,4,3,2,1:T(8,128)S(1)}, f32[2,2,2,1,1,2,16,512]{7,6,0,5,4,3,2,1:T(8,128)S(1)}, u32[]{:S(2)}, u32[]{:S(2)}) collective-permute-start(f32[2,2,2,1,1,2,16,512]{7,6,0,5,4,3,2,1:T(8,128)S(1)} %constant_dynamic-slice_fusion.13), channel_id=1, source_target_pairs={{0,4},{1,5},{2,6},{3,7},{4,0},{5,1},{6,2},{7,3},{8,12},{9,13},{10,... | collective-permute-start | bytes 1572872 | tf_op jit(solution)/shard_map/ppermute | solution.py:67
  65.3 21.9 %collective-permute-start.14 = (f32[2,2,1,2,1,2,16,512]{7,6,5,4,3,2,1,0:T(8,128)S(1)}, f32[2,2,1,2,1,2,16,512]{7,6,5,4,3,2,1,0:T(8,128)S(1)}, u32[]{:S(2)}, u32[]{:S(2)}) collective-permute-start(f32[2,2,1,2,1,2,16,512]{7,6,5,4,3,2,1,0:T(8,128)S(1)} %constant_dynamic-slice_fusion.8), channel_id=1, source_target_pairs={{0,8},{1,9},{2,10},{3,11},{4,12},{5,13},{6,14},{7,15},{8,0},{9,1},... | collective-permute-start | bytes 1572872 | tf_op jit(solution)/shard_map/ppermute | solution.py:67
  65.7 24.0 %collective-permute-start.2 = (f32[2,2,2,2,1,1,16,512]{7,6,5,4,3,2,1,0:T(8,128)S(1)}, f32[2,2,2,2,1,1,16,512]{7,6,5,4,3,2,1,0:T(8,128)S(1)}, u32[]{:S(2)}, u32[]{:S(2)}) collective-permute-start(f32[2,2,2,2,1,1,16,512]{7,6,5,4,3,2,1,0:T(8,128)S(1)} %constant_dynamic-slice_fusion.18), channel_id=1, source_target_pairs={{0,1},{1,0},{2,3},{3,2},{4,5},{5,4},{6,7},{7,6},{8,9},{9,8},{10,11... | collective-permute-start | bytes 1572872 | tf_op jit(solution)/shard_map/ppermute | solution.py:67
  78.0 6.5 %collective-permute-start.21 = (f32[2,2,2,1,1,1,16,512]{7,6,0,5,4,3,2,1:T(8,128)S(1)}, f32[2,2,2,1,1,1,16,512]{7,6,0,5,4,3,2,1:T(8,128)S(1)}, u32[]{:S(2)}, u32[]{:S(2)}) collective-permute-start(f32[2,2,2,1,1,1,16,512]{7,6,0,5,4,3,2,1:T(8,128)S(1)} %constant_dynamic-slice_fusion.2), channel_id=1, source_target_pairs={{0,4},{1,5},{2,6},{3,7},{4,0},{5,1},{6,2},{7,3},{8,12},{9,13},{10,... | collective-permute-start | bytes 786440 | tf_op jit(solution)/shard_map/ppermute | solution.py:67
  78.7 8.4 %collective-permute-start.9 = (f32[2,2,1,1,1,2,16,512]{7,6,0,5,4,3,2,1:T(8,128)S(1)}, f32[2,2,1,1,1,2,16,512]{7,6,0,5,4,3,2,1:T(8,128)S(1)}, u32[]{:S(2)}, u32[]{:S(2)}) collective-permute-start(f32[2,2,1,1,1,2,16,512]{7,6,0,5,4,3,2,1:T(8,128)S(1)} %constant_dynamic-slice_fusion.12), channel_id=1, source_target_pairs={{0,8},{1,9},{2,10},{3,11},{4,12},{5,13},{6,14},{7,15},{8,0},{9,1},... | collective-permute-start | bytes 786440 | tf_op jit(solution)/shard_map/ppermute | solution.py:67
  84.6 6.3 %collective-permute-start.22 = (f32[2,2,1,1,1,1,16,512]{7,6,0,5,4,3,2,1:T(8,128)S(1)}, f32[2,2,1,1,1,1,16,512]{7,6,0,5,4,3,2,1:T(8,128)S(1)}, u32[]{:S(2)}, u32[]{:S(2)}) collective-permute-start(f32[2,2,1,1,1,1,16,512]{7,6,0,5,4,3,2,1:T(8,128)S(1)} %constant_dynamic-slice_fusion.1), channel_id=1, source_target_pairs={{0,8},{1,9},{2,10},{3,11},{4,12},{5,13},{6,14},{7,15},{8,0},{9,1},... | collective-permute-start | bytes 393224 | tf_op jit(solution)/shard_map/ppermute | solution.py:67
  87.1 6.4 %collective-permute-start.10 = (f32[2,2,1,1,1,1,16,512]{7,6,0,5,4,3,2,1:T(8,128)S(1)}, f32[2,2,1,1,1,1,16,512]{7,6,0,5,4,3,2,1:T(8,128)S(1)}, u32[]{:S(2)}, u32[]{:S(2)}) collective-permute-start(f32[2,2,1,1,1,1,16,512]{7,6,0,5,4,3,2,1:T(8,128)S(1)} %constant_dynamic-slice_fusion.11), channel_id=1, source_target_pairs={{0,1},{1,0},{2,3},{3,2},{4,5},{5,4},{6,7},{7,6},{8,9},{9,8},{10,11... | collective-permute-start | bytes 393224 | tf_op jit(solution)/shard_map/ppermute | solution.py:67
  87.4 18.2 %collective-permute-start.15 = (f32[2,2,1,2,1,1,16,512]{7,6,5,4,3,2,1,0:T(8,128)S(1)}, f32[2,2,1,2,1,1,16,512]{7,6,5,4,3,2,1,0:T(8,128)S(1)}, u32[]{:S(2)}, u32[]{:S(2)}) collective-permute-start(f32[2,2,1,2,1,1,16,512]{7,6,5,4,3,2,1,0:T(8,128)S(1)} %constant_dynamic-slice_fusion.7), channel_id=1, source_target_pairs={{0,1},{1,0},{2,3},{3,2},{4,5},{5,4},{6,7},{7,6},{8,9},{9,8},{10,11... | collective-permute-start | bytes 786440 | tf_op jit(solution)/shard_map/ppermute | solution.py:67
  89.8 16.8 %collective-permute-start.3 = (f32[2,2,2,1,1,1,16,512]{7,6,5,4,3,2,1,0:T(8,128)S(1)}, f32[2,2,2,1,1,1,16,512]{7,6,5,4,3,2,1,0:T(8,128)S(1)}, u32[]{:S(2)}, u32[]{:S(2)}) collective-permute-start(f32[2,2,2,1,1,1,16,512]{7,6,5,4,3,2,1,0:T(8,128)S(1)} %constant_dynamic-slice_fusion.17), channel_id=1, source_target_pairs={{0,4},{1,5},{2,6},{3,7},{4,0},{5,1},{6,2},{7,3},{8,12},{9,13},{10,... | collective-permute-start | bytes 786440 | tf_op jit(solution)/shard_map/ppermute | solution.py:67
  90.9 6.0 %collective-permute-start.23 = (f32[2,1,1,1,1,1,16,512]{7,6,0,5,4,3,2,1:T(8,128)S(1)}, f32[2,1,1,1,1,1,16,512]{7,6,0,5,4,3,2,1:T(8,128)S(1)}, u32[]{:S(2)}, u32[]{:S(2)}) collective-permute-start(f32[2,1,1,1,1,1,16,512]{7,6,0,5,4,3,2,1:T(8,128)S(1)} %constant_dynamic-slice_fusion), channel_id=1, source_target_pairs={{0,16},{1,17},{2,18},{3,19},{4,20},{5,21},{6,22},{7,23},{8,24},{9,... | collective-permute-start | bytes 196616 | tf_op jit(solution)/shard_map/ppermute | solution.py:67
  93.6 5.6 %collective-permute-start.11 = (f32[2,1,1,1,1,1,16,512]{7,6,0,5,4,3,2,1:T(8,128)S(1)}, f32[2,1,1,1,1,1,16,512]{7,6,0,5,4,3,2,1:T(8,128)S(1)}, u32[]{:S(2)}, u32[]{:S(2)}) collective-permute-start(f32[2,1,1,1,1,1,16,512]{7,6,0,5,4,3,2,1:T(8,128)S(1)} %constant_dynamic-slice_fusion.10), channel_id=1, source_target_pairs={{0,16},{1,17},{2,18},{3,19},{4,20},{5,21},{6,22},{7,23},{8,24},{9,... | collective-permute-start | bytes 196616 | tf_op jit(solution)/shard_map/ppermute | solution.py:67
  96.9 4.9 %collective-permute-start.40 = (bf16[2,1,1,1,1,1,16,512]{7,6,5,4,3,2,1,0:T(8,128)(2,1)S(1)}, bf16[2,1,1,1,1,1,16,512]{7,6,5,4,3,2,1,0:T(8,128)(2,1)S(1)}, u32[]{:S(2)}, u32[]{:S(2)}) collective-permute-start(bf16[2,1,1,1,1,1,16,512]{7,6,5,4,3,2,1,0:T(8,128)(2,1)S(1)} %get-tuple-element.62), channel_id=1, source_target_pairs={{0,16},{1,17},{2,18},{3,19},{4,20},{5,21},{6,22},{7,23},{8,24},{9,... | collective-permute-start | bytes 98312 | tf_op jit(solution)/shard_map/ppermute | solution.py:76
  99.2 4.9 %collective-permute-start.30 = (bf16[2,1,1,1,1,1,16,512]{7,6,0,5,4,3,2,1:T(8,128)(2,1)S(1)}, bf16[2,1,1,1,1,1,16,512]{7,6,0,5,4,3,2,1:T(8,128)(2,1)S(1)}, u32[]{:S(2)}, u32[]{:S(2)}) collective-permute-start(bf16[2,1,1,1,1,1,16,512]{7,6,0,5,4,3,2,1:T(8,128)(2,1)S(1)} %get-tuple-element.66), channel_id=1, source_target_pairs={{0,16},{1,17},{2,18},{3,19},{4,20},{5,21},{6,22},{7,23},{8,24},{9,... | collective-permute-start | bytes 98312 | tf_op jit(solution)/shard_map/ppermute | solution.py:76
  101.8 5.2 %collective-permute-start.41 = (bf16[2,2,1,1,1,1,16,512]{7,6,5,4,3,2,1,0:T(8,128)(2,1)S(1)}, bf16[2,2,1,1,1,1,16,512]{7,6,5,4,3,2,1,0:T(8,128)(2,1)S(1)}, u32[]{:S(2)}, u32[]{:S(2)}) collective-permute-start(bf16[2,2,1,1,1,1,16,512]{7,6,5,4,3,2,1,0:T(8,128)(2,1)S(1)} %pad_maximum_fusion.27), channel_id=1, source_target_pairs={{0,8},{1,9},{2,10},{3,11},{4,12},{5,13},{6,14},{7,15},{8,0},{9,1},... | collective-permute-start | bytes 196616 | tf_op jit(solution)/shard_map/ppermute | solution.py:76
  104.1 4.8 %collective-permute-start.31 = (bf16[2,2,1,1,1,1,16,512]{7,6,0,5,4,3,2,1:T(8,128)(2,1)S(1)}, bf16[2,2,1,1,1,1,16,512]{7,6,0,5,4,3,2,1:T(8,128)(2,1)S(1)}, u32[]{:S(2)}, u32[]{:S(2)}) collective-permute-start(bf16[2,2,1,1,1,1,16,512]{7,6,0,5,4,3,2,1:T(8,128)(2,1)S(1)} %pad_maximum_fusion.25), channel_id=1, source_target_pairs={{0,1},{1,0},{2,3},{3,2},{4,5},{5,4},{6,7},{7,6},{8,9},{9,8},{10,11... | collective-permute-start | bytes 196616 | tf_op jit(solution)/shard_map/ppermute | solution.py:76
  105.7 5.6 %collective-permute-start.16 = (f32[2,2,1,1,1,1,16,512]{7,6,5,4,3,2,1,0:T(8,128)S(1)}, f32[2,2,1,1,1,1,16,512]{7,6,5,4,3,2,1,0:T(8,128)S(1)}, u32[]{:S(2)}, u32[]{:S(2)}) collective-permute-start(f32[2,2,1,1,1,1,16,512]{7,6,5,4,3,2,1,0:T(8,128)S(1)} %constant_dynamic-slice_fusion.6), channel_id=1, source_target_pairs={{0,4},{1,5},{2,6},{3,7},{4,0},{5,1},{6,2},{7,3},{8,12},{9,13},{10,... | collective-permute-start | bytes 393224 | tf_op jit(solution)/shard_map/ppermute | solution.py:67
  106.6 5.8 %collective-permute-start.4 = (f32[2,2,1,1,1,1,16,512]{7,6,5,4,3,2,1,0:T(8,128)S(1)}, f32[2,2,1,1,1,1,16,512]{7,6,5,4,3,2,1,0:T(8,128)S(1)}, u32[]{:S(2)}, u32[]{:S(2)}) collective-permute-start(f32[2,2,1,1,1,1,16,512]{7,6,5,4,3,2,1,0:T(8,128)S(1)} %constant_dynamic-slice_fusion.16), channel_id=1, source_target_pairs={{0,8},{1,9},{2,10},{3,11},{4,12},{5,13},{6,14},{7,15},{8,0},{9,1},... | collective-permute-start | bytes 393224 | tf_op jit(solution)/shard_map/ppermute | solution.py:67
  107.0 7.4 %collective-permute-start.42 = (bf16[2,2,2,1,1,1,16,512]{7,6,5,4,3,2,1,0:T(8,128)(2,1)S(1)}, bf16[2,2,2,1,1,1,16,512]{7,6,5,4,3,2,1,0:T(8,128)(2,1)S(1)}, u32[]{:S(2)}, u32[]{:S(2)}) collective-permute-start(bf16[2,2,2,1,1,1,16,512]{7,6,5,4,3,2,1,0:T(8,128)(2,1)S(1)} %pad_maximum_fusion.23), channel_id=1, source_target_pairs={{0,4},{1,5},{2,6},{3,7},{4,0},{5,1},{6,2},{7,3},{8,12},{9,13},{10,... | collective-permute-start | bytes 393224 | tf_op jit(solution)/shard_map/ppermute | solution.py:76
  109.0 6.8 %collective-permute-start.32 = (bf16[2,2,1,1,1,2,16,512]{7,6,0,5,4,3,2,1:T(8,128)(2,1)S(1)}, bf16[2,2,1,1,1,2,16,512]{7,6,0,5,4,3,2,1:T(8,128)(2,1)S(1)}, u32[]{:S(2)}, u32[]{:S(2)}) collective-permute-start(bf16[2,2,1,1,1,2,16,512]{7,6,0,5,4,3,2,1:T(8,128)(2,1)S(1)} %pad_maximum_fusion.21), channel_id=1, source_target_pairs={{0,8},{1,9},{2,10},{3,11},{4,12},{5,13},{6,14},{7,15},{8,0},{9,1},... | collective-permute-start | bytes 393224 | tf_op jit(solution)/shard_map/ppermute | solution.py:76
  111.3 5.6 %collective-permute-start.17 = (f32[2,1,1,1,1,1,16,512]{7,6,5,4,3,2,1,0:T(8,128)S(1)}, f32[2,1,1,1,1,1,16,512]{7,6,5,4,3,2,1,0:T(8,128)S(1)}, u32[]{:S(2)}, u32[]{:S(2)}) collective-permute-start(f32[2,1,1,1,1,1,16,512]{7,6,5,4,3,2,1,0:T(8,128)S(1)} %constant_dynamic-slice_fusion.5), channel_id=1, source_target_pairs={{0,16},{1,17},{2,18},{3,19},{4,20},{5,21},{6,22},{7,23},{8,24},{9,... | collective-permute-start | bytes 196616 | tf_op jit(solution)/shard_map/ppermute | solution.py:67
  112.5 7.2 %collective-permute-start.5 = (f32[2,1,1,1,1,1,16,512]{7,6,5,4,3,2,1,0:T(8,128)S(1)}, f32[2,1,1,1,1,1,16,512]{7,6,5,4,3,2,1,0:T(8,128)S(1)}, u32[]{:S(2)}, u32[]{:S(2)}) collective-permute-start(f32[2,1,1,1,1,1,16,512]{7,6,5,4,3,2,1,0:T(8,128)S(1)} %constant_dynamic-slice_fusion.15), channel_id=1, source_target_pairs={{0,16},{1,17},{2,18},{3,19},{4,20},{5,21},{6,22},{7,23},{8,24},{9,... | collective-permute-start | bytes 196616 | tf_op jit(solution)/shard_map/ppermute | solution.py:67
  114.5 14.7 %collective-permute-start.43 = (bf16[2,2,2,2,1,1,16,512]{7,6,5,4,3,2,1,0:T(8,128)(2,1)S(1)}, bf16[2,2,2,2,1,1,16,512]{7,6,5,4,3,2,1,0:T(8,128)(2,1)S(1)}, u32[]{:S(2)}, u32[]{:S(2)}) collective-permute-start(bf16[2,2,2,2,1,1,16,512]{7,6,5,4,3,2,1,0:T(8,128)(2,1)S(1)} %pad_maximum_fusion.18), channel_id=1, source_target_pairs={{0,1},{1,0},{2,3},{3,2},{4,5},{5,4},{6,7},{7,6},{8,9},{9,8},{10,11... | collective-permute-start | bytes 786440 | tf_op jit(solution)/shard_map/ppermute | solution.py:76
  115.8 13.5 %collective-permute-start.33 = (bf16[2,2,2,1,1,2,16,512]{7,6,0,5,4,3,2,1:T(8,128)(2,1)S(1)}, bf16[2,2,2,1,1,2,16,512]{7,6,0,5,4,3,2,1:T(8,128)(2,1)S(1)}, u32[]{:S(2)}, u32[]{:S(2)}) collective-permute-start(bf16[2,2,2,1,1,2,16,512]{7,6,0,5,4,3,2,1:T(8,128)(2,1)S(1)} %pad_maximum_fusion.16), channel_id=1, source_target_pairs={{0,4},{1,5},{2,6},{3,7},{4,0},{5,1},{6,2},{7,3},{8,12},{9,13},{10,... | collective-permute-start | bytes 786440 | tf_op jit(solution)/shard_map/ppermute | solution.py:76
  116.9 4.9 %collective-permute-start.35 = (bf16[2,1,1,1,1,1,16,512]{7,6,5,4,3,2,1,0:T(8,128)(2,1)S(1)}, bf16[2,1,1,1,1,1,16,512]{7,6,5,4,3,2,1,0:T(8,128)(2,1)S(1)}, u32[]{:S(2)}, u32[]{:S(2)}) collective-permute-start(bf16[2,1,1,1,1,1,16,512]{7,6,5,4,3,2,1,0:T(8,128)(2,1)S(1)} %get-tuple-element.64), channel_id=1, source_target_pairs={{0,16},{1,17},{2,18},{3,19},{4,20},{5,21},{6,22},{7,23},{8,24},{9,... | collective-permute-start | bytes 98312 | tf_op jit(solution)/shard_map/ppermute | solution.py:76
  119.7 4.9 %collective-permute-start.25 = (bf16[2,1,1,1,1,1,16,512]{7,6,5,4,3,2,1,0:T(8,128)(2,1)S(1)}, bf16[2,1,1,1,1,1,16,512]{7,6,5,4,3,2,1,0:T(8,128)(2,1)S(1)}, u32[]{:S(2)}, u32[]{:S(2)}) collective-permute-start(bf16[2,1,1,1,1,1,16,512]{7,6,5,4,3,2,1,0:T(8,128)(2,1)S(1)} %get-tuple-element.68), channel_id=1, source_target_pairs={{0,16},{1,17},{2,18},{3,19},{4,20},{5,21},{6,22},{7,23},{8,24},{9,... | collective-permute-start | bytes 98312 | tf_op jit(solution)/shard_map/ppermute | solution.py:76
  120.6 14.1 %collective-permute-start.24 = (f32[4,2,1,1,1,1,1,16,512]{8,7,1,0,6,5,4,3,2:T(8,128)S(1)}, f32[4,2,1,1,1,1,1,16,512]{8,7,1,0,6,5,4,3,2:T(8,128)S(1)}, u32[]{:S(2)}, u32[]{:S(2)}) collective-permute-start(f32[4,2,1,1,1,1,1,16,512]{8,7,1,0,6,5,4,3,2:T(8,128)S(1)} %bitcast.556), channel_id=1, source_target_pairs={{0,1},{1,0},{2,3},{3,2},{4,5},{5,4},{6,7},{7,6},{8,9},{9,8},{10,11... | collective-permute-start | bytes 786440 | tf_op jit(solution)/shard_map/ppermute | solution.py:76
  121.8 4.3 %collective-permute-start.36 = (bf16[2,2,1,1,1,1,16,512]{7,6,5,4,3,2,1,0:T(8,128)(2,1)S(1)}, bf16[2,2,1,1,1,1,16,512]{7,6,5,4,3,2,1,0:T(8,128)(2,1)S(1)}, u32[]{:S(2)}, u32[]{:S(2)}) collective-permute-start(bf16[2,2,1,1,1,1,16,512]{7,6,5,4,3,2,1,0:T(8,128)(2,1)S(1)} %pad_maximum_fusion.26), channel_id=1, source_target_pairs={{0,4},{1,5},{2,6},{3,7},{4,0},{5,1},{6,2},{7,3},{8,12},{9,13},{10,... | collective-permute-start | bytes 196616 | tf_op jit(solution)/shard_map/ppermute | solution.py:76
  124.6 4.3 %collective-permute-start.26 = (bf16[2,2,1,1,1,1,16,512]{7,6,5,4,3,2,1,0:T(8,128)(2,1)S(1)}, bf16[2,2,1,1,1,1,16,512]{7,6,5,4,3,2,1,0:T(8,128)(2,1)S(1)}, u32[]{:S(2)}, u32[]{:S(2)}) collective-permute-start(bf16[2,2,1,1,1,1,16,512]{7,6,5,4,3,2,1,0:T(8,128)(2,1)S(1)} %pad_maximum_fusion.24), channel_id=1, source_target_pairs={{0,8},{1,9},{2,10},{3,11},{4,12},{5,13},{6,14},{7,15},{8,0},{9,1},... | collective-permute-start | bytes 196616 | tf_op jit(solution)/shard_map/ppermute | solution.py:76
  126.2 5.0 %collective-permute-start.37 = (bf16[2,2,1,2,1,1,16,512]{7,6,5,4,3,2,1,0:T(8,128)(2,1)S(1)}, bf16[2,2,1,2,1,1,16,512]{7,6,5,4,3,2,1,0:T(8,128)(2,1)S(1)}, u32[]{:S(2)}, u32[]{:S(2)}) collective-permute-start(bf16[2,2,1,2,1,1,16,512]{7,6,5,4,3,2,1,0:T(8,128)(2,1)S(1)} %pad_maximum_fusion.22), channel_id=1, source_target_pairs={{0,1},{1,0},{2,3},{3,2},{4,5},{5,4},{6,7},{7,6},{8,9},{9,8},{10,11... | collective-permute-start | bytes 393224 | tf_op jit(solution)/shard_map/ppermute | solution.py:76
  129.0 5.0 %collective-permute-start.27 = (bf16[2,2,2,1,1,1,16,512]{7,6,5,4,3,2,1,0:T(8,128)(2,1)S(1)}, bf16[2,2,2,1,1,1,16,512]{7,6,5,4,3,2,1,0:T(8,128)(2,1)S(1)}, u32[]{:S(2)}, u32[]{:S(2)}) collective-permute-start(bf16[2,2,2,1,1,1,16,512]{7,6,5,4,3,2,1,0:T(8,128)(2,1)S(1)} %pad_maximum_fusion.20), channel_id=1, source_target_pairs={{0,4},{1,5},{2,6},{3,7},{4,0},{5,1},{6,2},{7,3},{8,12},{9,13},{10,... | collective-permute-start | bytes 393224 | tf_op jit(solution)/shard_map/ppermute | solution.py:76
  129.3 12.2 %collective-permute-start.44 = (bf16[2,2,2,2,1,2,16,512]{7,6,5,4,3,2,1,0:T(8,128)(2,1)S(1)}, bf16[2,2,2,2,1,2,16,512]{7,6,5,4,3,2,1,0:T(8,128)(2,1)S(1)}, u32[]{:S(2)}, u32[]{:S(2)}) collective-permute-start(bf16[2,2,2,2,1,2,16,512]{7,6,5,4,3,2,1,0:T(8,128)(2,1)S(1)} %pad_maximum_fusion.12), channel_id=1, source_target_pairs={{0,2},{1,3},{2,0},{3,1},{4,6},{5,7},{6,4},{7,5},{8,10},{9,11},{10,... | collective-permute-start | bytes 1572872 | tf_op jit(solution)/shard_map/ppermute | solution.py:76
  129.5 13.9 %collective-permute-start.34 = (bf16[2,2,2,2,1,2,16,512]{7,6,0,5,4,3,2,1:T(8,128)(2,1)S(1)}, bf16[2,2,2,2,1,2,16,512]{7,6,0,5,4,3,2,1:T(8,128)(2,1)S(1)}, u32[]{:S(2)}, u32[]{:S(2)}) collective-permute-start(bf16[2,2,2,2,1,2,16,512]{7,6,0,5,4,3,2,1:T(8,128)(2,1)S(1)} %pad_maximum_fusion.10), channel_id=1, source_target_pairs={{0,2},{1,3},{2,0},{3,1},{4,6},{5,7},{6,4},{7,5},{8,10},{9,11},{10,... | collective-permute-start | bytes 1572872 | tf_op jit(solution)/shard_map/ppermute | solution.py:76
  131.3 7.1 %collective-permute-start.38 = (bf16[2,2,1,2,1,2,16,512]{7,6,5,4,3,2,1,0:T(8,128)(2,1)S(1)}, bf16[2,2,1,2,1,2,16,512]{7,6,5,4,3,2,1,0:T(8,128)(2,1)S(1)}, u32[]{:S(2)}, u32[]{:S(2)}) collective-permute-start(bf16[2,2,1,2,1,2,16,512]{7,6,5,4,3,2,1,0:T(8,128)(2,1)S(1)} %pad_maximum_fusion.17), channel_id=1, source_target_pairs={{0,8},{1,9},{2,10},{3,11},{4,12},{5,13},{6,14},{7,15},{8,0},{9,1},... | collective-permute-start | bytes 786440 | tf_op jit(solution)/shard_map/ppermute | solution.py:76
  134.1 6.4 %collective-permute-start.28 = (bf16[2,2,2,2,1,1,16,512]{7,6,5,4,3,2,1,0:T(8,128)(2,1)S(1)}, bf16[2,2,2,2,1,1,16,512]{7,6,5,4,3,2,1,0:T(8,128)(2,1)S(1)}, u32[]{:S(2)}, u32[]{:S(2)}) collective-permute-start(bf16[2,2,2,2,1,1,16,512]{7,6,5,4,3,2,1,0:T(8,128)(2,1)S(1)} %pad_maximum_fusion.15), channel_id=1, source_target_pairs={{0,1},{1,0},{2,3},{3,2},{4,5},{5,4},{6,7},{7,6},{8,9},{9,8},{10,11... | collective-permute-start | bytes 786440 | tf_op jit(solution)/shard_map/ppermute | solution.py:76
  139.3 6.8 %collective-permute-start.39 = (bf16[2,2,2,2,1,2,16,512]{7,6,5,4,3,2,1,0:T(8,128)(2,1)}, bf16[2,2,2,2,1,2,16,512]{7,6,5,4,3,2,1,0:T(8,128)(2,1)}, u32[]{:S(2)}, u32[]{:S(2)}) collective-permute-start(bf16[2,2,2,2,1,2,16,512]{7,6,5,4,3,2,1,0:T(8,128)(2,1)} %pad_maximum_fusion.11), channel_id=1, source_target_pairs={{0,2},{1,3},{2,0},{3,1},{4,6},{5,7},{6,4},{7,5},{8,10},{9,11},{10,... | collective-permute-start | bytes 1572872 | tf_op jit(solution)/shard_map/ppermute | solution.py:76
  141.4 8.9 %collective-permute-start.29 = (bf16[2,2,2,2,1,2,16,512]{7,6,5,4,3,2,1,0:T(8,128)(2,1)}, bf16[2,2,2,2,1,2,16,512]{7,6,5,4,3,2,1,0:T(8,128)(2,1)}, u32[]{:S(2)}, u32[]{:S(2)}) collective-permute-start(bf16[2,2,2,2,1,2,16,512]{7,6,5,4,3,2,1,0:T(8,128)(2,1)} %pad_maximum_fusion.9), channel_id=1, source_target_pairs={{0,2},{1,3},{2,0},{3,1},{4,6},{5,7},{6,4},{7,5},{8,10},{9,11},{10,... | collective-permute-start | bytes 1572872 | tf_op jit(solution)/shard_map/ppermute | solution.py:76
  (41 other events, 38.5 us)

commit v8 on v6

--- a/solution.py
+++ b/solution.py
@@ -104,7 +104,14 @@
             jnp.concatenate([dn_y, src_y[:, :, :, :, : ly - 1]], axis=4),
         ]
         depth = ncol * nz * lx * ly
-        turned = ev.reshape(2, depth, nev).transpose(0, 2, 1)
+        flat = ev.reshape(2, depth, nev)
+        unit = jnp.eye(nev, dtype=ev.dtype)
+        turned = [
+            lax.dot_general(
+                unit, flat[c], (((1,), (1,)), ((), ())), preferred_element_type=jnp.float32
+            ).astype(ev.dtype)
+            for c in range(2)
+        ]
         left = jnp.concatenate(
             [
                 jnp.concatenate([turned[0], turned[1]], axis=1),

time: 153 us -> 153 us (level)
  starting transfers between devices: 41.5 us -> 36.2 us
  matrix products: 10.7 us -> 15.3 us
  waiting for transfers between devices: 41.1 us -> 45.2 us
  local copies, waits for them, and re-layouts: 28.9 us -> 27.2 us
    ppermute x21, starting transfers between devices: 21.6 us -> 16.5 us  [all_gather(): other = lax.ppermute(buf, ALL, xor_pairs(count, b))]
    dot_general x0 -> x2, matrix products: none -> 4.52 us  [local(): lax.dot_general(unit, flat[c], (((1,), (1,)), ((), ())), preferred_elemen...]
    ppermute x21, waiting for transfers between devices: 12.2 us -> 16.4 us  [all_gather(): other = lax.ppermute(buf, ALL, xor_pairs(count, b))]
    unnamed x131 -> x127, local copies, waits for them, and re-layouts: 6.12 us -> 5.39 us
  transfers between devices with their start and end apart: 45 -> 45, of which waited for: 18 -> 21; matrix products, arithmetic and copies ran while one was open for 32% -> 33% of each run, Pallas kernels for 0% -> 0%
where the time goes in v8:
time: 153 us; the launch traced here: 152 us
  waiting for transfers between devices  45.2 us (30%)
  starting transfers between devices  36.2 us (24%)
  local copies, waits for them, and re-layouts  27.2 us (18%)
  other arithmetic  26.2 us (17%)
  matrix products  15.3 us (10%)
  between operations  2.22 us (1%)
    ppermute x20, waiting for transfers between devices, reduce_scatter(): buf = keep + lax.ppermute(send, ALL, xor_pairs(count, b))  28.7 us
    ppermute x21, starting transfers between devices, all_gather(): other = lax.ppermute(buf, ALL, xor_pairs(count, b))  16.5 us
    ppermute x21, waiting for transfers between devices, all_gather(): other = lax.ppermute(buf, ALL, xor_pairs(count, b))  16.4 us
    ppermute x20, starting transfers between devices, reduce_scatter(): buf = keep + lax.ppermute(send, ALL, xor_pairs(count, b))  12.8 us
    dot_general x4, matrix products, local(): jnp.dot(left, field.reshape(2 * depth, nev), preferred_element_type=jnp.f...  7.13 us
    another operation x12, other arithmetic  6.02 us
    unnamed x127, local copies, waits for them, and re-layouts  5.39 us
    dot_general x2, matrix products, local(): lax.dot_general(unit, flat[c], (((1,), (1,)), ((), ())), preferred_elemen...  4.52 us
  transfers between devices with their start and end apart: 45, of which 21 were waited for; matrix products, arithmetic and copies ran while one was open for 33% of the time, Pallas kernels for 0%

profile of v8, /device:TPU:0, one launch (start us, length us, event | category | flops | bytes accessed | tf_op | source)
XLA Modules:
  0.0 152.4 jit_solution(10792949842446801631)
XLA Ops:
  0.6 1.0 slice_bitcast_fusion.19
  2.4 1.9 %convert_element_type.75 = f32[2,3,4,4,16,512]{5,4,3,2,1,0:T(8,128)S(1)} convert(bf16[2,3,4,4,16,512]{5,4,3,2,1,0:T(8,128)(2,1)} %param.5) | non-fusion elementwise | flops 786432 | bytes 4718592 | tf_op jit(solution)/shard_map/convert_element_type | solution.py:13
  6.9 1.0 pad_maximum_fusion.20
  7.8 3.0 %collective-permute-start.18 = (bf16[2,3,4,4,1,512]{5,4,3,2,1,0:T(2,128)(2,1)}, bf16[2,3,4,4,1,512]{5,4,3,2,1,0:T(2,128)(2,1)}, u32[]{:S(2)}, u32[]{:S(2)}) collective-permute-start(bf16[2,3,4,4,1,512]{5,4,3,2,1,0:T(2,128)(2,1)} %pad_maximum_fusion.20), channel_id=1, source_target_pairs={{0,1},{1,0},{2,3},{3,2},{4,5},{5,4},{6,7},{7,6},{8,9},{9,8},{10,11... | collective-permute-start | bytes 294920 | tf_op jit(solution)/shard_map/ppermute | solution.py:97
  16.4 4.0 %collective-permute-start = (bf16[2,3,4,1,16,512]{5,4,3,2,1,0:T(8,128)(2,1)}, bf16[2,3,4,1,16,512]{5,4,3,2,1,0:T(8,128)(2,1)S(1)}, u32[]{:S(2)}, u32[]{:S(2)}) collective-permute-start(bf16[2,3,4,1,16,512]{5,4,3,2,1,0:T(8,128)(2,1)} %slice.143), channel_id=1, source_target_pairs={{0,30},{2,0},{4,2},{6,4},{8,6},{10,8},{12,10},{14,12},{16,14},{18,... | collective-permute-start | bytes 1179656 | tf_op jit(solution)/shard_map/ppermute | solution.py:94
  20.4 1.3 fusion.32
  21.7 1.8 %slice.169 = bf16[2,3,4,4,15,512]{5,4,3,2,1,0:T(8,128)(2,1)} slice(bf16[2,3,4,4,16,512]{5,4,3,2,1,0:T(8,128)(2,1)S(1)} %copy-done), slice={[0:2], [0:3], [0:4], [0:4], [1:16], [0:512]} | slice | bytes 2949120 | tf_op jit(solution)/shard_map/slice | solution.py:99
  23.5 2.8 %convolution_convert_fusion.1 = bf16[512,768]{1,0:T(8,128)(2,1)} fusion(bf16[768,512]{1,0:T(8,128)(2,1)} %bitcast.552), kind=kOutput, calls=%fused_computation.18 | convolution fusion | flops 403308544 | bytes 1572864 | tf_op jit(solution)/shard_map/dot_general | solution.py:110
  26.3 1.7 %fusion.34 = (bf16[512,768]{1,0:T(8,128)(2,1)}, bf16[512,768]{1,0:T(8,128)(2,1)}) fusion(bf16[768,512]{1,0:T(8,128)(2,1)S(1)} %bitcast.551), kind=kOutput, calls=%fused_computation.252 | convolution fusion | flops 403701760 | bytes 2359296 | tf_op jit(solution)/shard_map/dot_general | solution.py:110
  29.4 1.7 %gather_fusion.1 = bf16[4,2,64,1024]{3,2,1,0:T(8,128)(2,1)} fusion(bf16[2,64,4,1024]{3,1,2,0:T(8,128)(2,1)S(1)} %maximum_maximum_fusion.1, s32[1024]{0:T(1024)} %pad_clamp_fusion), kind=kCustom, calls=%fused_computation.1 | custom fusion | bytes 2097168 | tf_op jit(solution)/shard_map/jit(_take)/gather | solution.py:131
  31.2 2.0 %copy.62 = bf16[2,64,4,1024]{3,2,1,0:T(4,128)(2,1)S(1)} copy(bf16[2,64,4,1024]{3,1,0,2:T(8,128)(2,1)} %bitcast.534) | data formatting | bytes 2097152 | tf_op jit(solution)/shard_map/jit(_take)/gather | solution.py:131
  33.2 1.1 reshape.2103
  34.4 2.2 %maximum_maximum_fusion = bf16[1024,1536]{1,0:T(8,128)(2,1)S(1)} fusion(bf16[512,768]{1,0:T(8,128)(2,1)} %convolution_convert_fusion.1, bf16[512,768]{1,0:T(8,128)(2,1)} %get-tuple-element.136, bf16[512,768]{1,0:T(8,128)(2,1)} %get-tuple-element.137), kind=kLoop, calls=%fused_computation.3 | loop fusion | flops 12582912 | bytes 5505024 | tf_op jit(solution)/shard_map/concatenate | solution.py:115
  37.2 1.7 %fusion.4 = bf16[2,3,4,4,16,512]{5,4,3,2,1,0:T(8,128)(2,1)S(1)} fusion(bf16[1,3,4,4,16,512]{5,4,3,2,1,0:T(8,128)(2,1)S(1)} %copy-done.2, bf16[1,3,4,4,16,512]{5,4,3,2,1,0:T(8,128)(2,1)S(1)} %copy-done.4, bf16[2,3,4,4,1,512]{5,4,3,2,1,0:T(2,128)(2,1)} %collective-permute-done.18), kind=kLoop, calls=%fused_computation.10 | loop fusion | flops 4718592 | bytes 3244032 | tf_op jit(solution)/shard_map/concatenate | solution.py:104
  38.9 1.8 %fusion = f32[2,2,2,2,2,2,16,512]{7,6,0,5,4,3,2,1:T(8,128)S(1)} fusion(bf16[1536,512,1,1,1,1,1,1]{1,0,2,7,6,5,4,3:T(8,128)(2,1)S(1)} %bitcast.542, bf16[2,2,2,2,2,2,16,1536]{7,6,5,4,3,2,1,0:T(8,128)(2,1)S(1)} %bitcast.535), kind=kOutput, calls=%fused_computation.4 | convolution fusion | flops 1610612736 | bytes 6815744 | tf_op jit(solution)/shard_map/dot_general | solution.py:137
  40.9 1.2 copy.51
  45.0 1.8 %fusion.2 = f32[2,2,2,2,2,2,16,512]{7,6,0,5,4,3,2,1:T(8,128)S(1)} fusion(bf16[1536,512,1,1,1,1,1,1]{1,0,2,7,6,5,4,3:T(8,128)(2,1)S(1)} %bitcast.544, bf16[2,2,2,2,2,2,16,1536]{7,6,5,4,3,2,1,0:T(8,128)(2,1)S(1)} %bitcast.536), kind=kOutput, calls=%fused_computation.6 | convolution fusion | flops 1610612736 | bytes 6815744 | tf_op jit(solution)/shard_map/dot_general | solution.py:137
  47.3 1.2 fusion.5
  48.5 1.8 %fusion.36 = f32[2,2,2,2,2,2,16,512]{7,6,5,4,3,2,1,0:T(8,128)S(1)} fusion(bf16[2,2,2,2,2,2,16,1536]{7,6,5,4,3,2,1,0:T(8,128)(2,1)S(1)} %bitcast.537, bf16[1536,512,1,1,1,1,1,1]{1,0,7,6,5,4,3,2:T(8,128)(2,1)S(1)} %bitcast.541), kind=kOutput, calls=%fused_computation.254 | convolution fusion | flops 1610612736 | bytes 6815744 | tf_op jit(solution)/shard_map/dot_general | solution.py:137
  50.7 0.9 slice-done
  54.0 1.8 %fusion.35 = f32[2,2,2,2,2,2,16,512]{7,6,5,4,3,2,1,0:T(8,128)S(1)} fusion(bf16[2,2,2,2,2,2,16,1536]{7,6,5,4,3,2,1,0:T(8,128)(2,1)S(1)} %bitcast.538, bf16[1536,512,1,1,1,1,1,1]{1,0,7,6,5,4,3,2:T(8,128)(2,1)S(1)} %bitcast.543), kind=kOutput, calls=%fused_computation.253 | convolution fusion | flops 1610612736 | bytes 6815744 | tf_op jit(solution)/shard_map/dot_general | solution.py:137
  56.4 1.6 %collective-permute-start.20 = (f32[2,2,2,2,1,1,16,512]{7,6,0,5,4,3,2,1:T(8,128)S(1)}, f32[2,2,2,2,1,1,16,512]{7,6,0,5,4,3,2,1:T(8,128)S(1)}, u32[]{:S(2)}, u32[]{:S(2)}) collective-permute-start(f32[2,2,2,2,1,1,16,512]{7,6,0,5,4,3,2,1:T(8,128)S(1)} %constant_dynamic-slice_fusion.3), channel_id=1, source_target_pairs={{0,1},{1,0},{2,3},{3,2},{4,5},{5,4},{6,7},{7,6},{8,9},{9,8},{10,11... | collective-permute-start | bytes 1572872 | tf_op jit(solution)/shard_map/ppermute | solution.py:67
  59.4 1.2 collective-permute-start.2
  60.6 10.7 %collective-permute-done.20 = f32[2,2,2,2,1,1,16,512]{7,6,0,5,4,3,2,1:T(8,128)S(1)} collective-permute-done((f32[2,2,2,2,1,1,16,512]{7,6,0,5,4,3,2,1:T(8,128)S(1)}, f32[2,2,2,2,1,1,16,512]{7,6,0,5,4,3,2,1:T(8,128)S(1)}, u32[]{:S(2)}, u32[]{:S(2)}) %collective-permute-start.20) | collective-permute-done | bytes 524320 | tf_op jit(solution)/shard_map/ppermute | solution.py:67
  72.5 6.1 %collective-permute-done.21 = f32[2,2,2,1,1,1,16,512]{7,6,0,5,4,3,2,1:T(8,128)S(1)} collective-permute-done((f32[2,2,2,1,1,1,16,512]{7,6,0,5,4,3,2,1:T(8,128)S(1)}, f32[2,2,2,1,1,1,16,512]{7,6,0,5,4,3,2,1:T(8,128)S(1)}, u32[]{:S(2)}, u32[]{:S(2)}) %collective-permute-start.21) | collective-permute-done | bytes 262176 | tf_op jit(solution)/shard_map/ppermute | solution.py:67
  78.7 1.8 %collective-permute-done.9 = f32[2,2,1,1,1,2,16,512]{7,6,0,5,4,3,2,1:T(8,128)S(1)} collective-permute-done((f32[2,2,1,1,1,2,16,512]{7,6,0,5,4,3,2,1:T(8,128)S(1)}, f32[2,2,1,1,1,2,16,512]{7,6,0,5,4,3,2,1:T(8,128)S(1)}, u32[]{:S(2)}, u32[]{:S(2)}) %collective-permute-start.9) | collective-permute-done | bytes 262176 | tf_op jit(solution)/shard_map/ppermute | solution.py:67
  80.8 2.3 %collective-permute-start.15 = (f32[2,2,1,2,1,1,16,512]{7,6,5,4,3,2,1,0:T(8,128)S(1)}, f32[2,2,1,2,1,1,16,512]{7,6,5,4,3,2,1,0:T(8,128)S(1)}, u32[]{:S(2)}, u32[]{:S(2)}) collective-permute-start(f32[2,2,1,2,1,1,16,512]{7,6,5,4,3,2,1,0:T(8,128)S(1)} %constant_dynamic-slice_fusion.7), channel_id=1, source_target_pairs={{0,1},{1,0},{2,3},{3,2},{4,5},{5,4},{6,7},{7,6},{8,9},{9,8},{10,11... | collective-permute-start | bytes 786440 | tf_op jit(solution)/shard_map/ppermute | solution.py:67
  84.0 0.9 collective-permute-start.23
  84.8 2.1 %collective-permute-done.10 = f32[2,2,1,1,1,1,16,512]{7,6,0,5,4,3,2,1:T(8,128)S(1)} collective-permute-done((f32[2,2,1,1,1,1,16,512]{7,6,0,5,4,3,2,1:T(8,128)S(1)}, f32[2,2,1,1,1,1,16,512]{7,6,0,5,4,3,2,1:T(8,128)S(1)}, u32[]{:S(2)}, u32[]{:S(2)}) %collective-permute-start.10) | collective-permute-done | bytes 131104 | tf_op jit(solution)/shard_map/ppermute | solution.py:67
  87.8 2.7 %collective-permute-done.23 = f32[2,1,1,1,1,1,16,512]{7,6,0,5,4,3,2,1:T(8,128)S(1)} collective-permute-done((f32[2,1,1,1,1,1,16,512]{7,6,0,5,4,3,2,1:T(8,128)S(1)}, f32[2,1,1,1,1,1,16,512]{7,6,0,5,4,3,2,1:T(8,128)S(1)}, u32[]{:S(2)}, u32[]{:S(2)}) %collective-permute-start.23) | collective-permute-done | bytes 65568 | tf_op jit(solution)/shard_map/ppermute | solution.py:67
  90.6 2.5 %collective-permute-done.11 = f32[2,1,1,1,1,1,16,512]{7,6,0,5,4,3,2,1:T(8,128)S(1)} collective-permute-done((f32[2,1,1,1,1,1,16,512]{7,6,0,5,4,3,2,1:T(8,128)S(1)}, f32[2,1,1,1,1,1,16,512]{7,6,0,5,4,3,2,1:T(8,128)S(1)}, u32[]{:S(2)}, u32[]{:S(2)}) %collective-permute-start.11) | collective-permute-done | bytes 65568 | tf_op jit(solution)/shard_map/ppermute | solution.py:67
  93.6 1.8 %collective-permute-done.40 = bf16[2,1,1,1,1,1,16,512]{7,6,5,4,3,2,1,0:T(8,128)(2,1)S(1)} collective-permute-done((bf16[2,1,1,1,1,1,16,512]{7,6,5,4,3,2,1,0:T(8,128)(2,1)S(1)}, bf16[2,1,1,1,1,1,16,512]{7,6,5,4,3,2,1,0:T(8,128)(2,1)S(1)}, u32[]{:S(2)}, u32[]{:S(2)}) %collective-permute-start.40) | collective-permute-done | bytes 32800 | tf_op jit(solution)/shard_map/ppermute | solution.py:76
  96.1 1.9 %collective-permute-done.30 = bf16[2,1,1,1,1,1,16,512]{7,6,0,5,4,3,2,1:T(8,128)(2,1)S(1)} collective-permute-done((bf16[2,1,1,1,1,1,16,512]{7,6,0,5,4,3,2,1:T(8,128)(2,1)S(1)}, bf16[2,1,1,1,1,1,16,512]{7,6,0,5,4,3,2,1:T(8,128)(2,1)S(1)}, u32[]{:S(2)}, u32[]{:S(2)}) %collective-permute-start.30) | collective-permute-done | bytes 32800 | tf_op jit(solution)/shard_map/ppermute | solution.py:76
  97.9 1.1 collective-permute-start.31
  99.1 0.9 collective-permute-start.16
  100.5 1.4 collective-permute-start.42
  102.3 1.2 collective-permute-start.32
  104.1 1.4 collective-permute-start.17
  106.3 1.0 collective-permute-start.5
  107.3 1.1 collective-permute-start.43
  108.5 0.8 collective-permute-start.33
  109.9 1.8 %collective-permute-start.35 = (bf16[2,1,1,1,1,1,16,512]{7,6,5,4,3,2,1,0:T(8,128)(2,1)S(1)}, bf16[2,1,1,1,1,1,16,512]{7,6,5,4,3,2,1,0:T(8,128)(2,1)S(1)}, u32[]{:S(2)}, u32[]{:S(2)}) collective-permute-start(bf16[2,1,1,1,1,1,16,512]{7,6,5,4,3,2,1,0:T(8,128)(2,1)S(1)} %get-tuple-element.62), channel_id=1, source_target_pairs={{0,16},{1,17},{2,18},{3,19},{4,20},{5,21},{6,22},{7,23},{8,24},{9,... | collective-permute-start | bytes 98312 | tf_op jit(solution)/shard_map/ppermute | solution.py:76
  112.8 1.3 collective-permute-start.24
  114.1 0.8 collective-permute-start.25
  115.0 1.3 collective-permute-start.36
  116.3 3.0 %collective-permute-done.25 = bf16[2,1,1,1,1,1,16,512]{7,6,5,4,3,2,1,0:T(8,128)(2,1)S(1)} collective-permute-done((bf16[2,1,1,1,1,1,16,512]{7,6,5,4,3,2,1,0:T(8,128)(2,1)S(1)}, bf16[2,1,1,1,1,1,16,512]{7,6,5,4,3,2,1,0:T(8,128)(2,1)S(1)}, u32[]{:S(2)}, u32[]{:S(2)}) %collective-permute-start.25) | collective-permute-done | bytes 32800 | tf_op jit(solution)/shard_map/ppermute | solution.py:76
  120.7 2.9 %collective-permute-done.26 = bf16[2,2,1,1,1,1,16,512]{7,6,5,4,3,2,1,0:T(8,128)(2,1)S(1)} collective-permute-done((bf16[2,2,1,1,1,1,16,512]{7,6,5,4,3,2,1,0:T(8,128)(2,1)S(1)}, bf16[2,2,1,1,1,1,16,512]{7,6,5,4,3,2,1,0:T(8,128)(2,1)S(1)}, u32[]{:S(2)}, u32[]{:S(2)}) %collective-permute-start.26) | collective-permute-done | bytes 65568 | tf_op jit(solution)/shard_map/ppermute | solution.py:76
  123.7 1.0 collective-permute-start.27
  125.6 1.0 collective-permute-start.38
  126.6 2.1 %collective-permute-done.27 = bf16[2,2,2,1,1,1,16,512]{7,6,5,4,3,2,1,0:T(8,128)(2,1)S(1)} collective-permute-done((bf16[2,2,2,1,1,1,16,512]{7,6,5,4,3,2,1,0:T(8,128)(2,1)S(1)}, bf16[2,2,2,1,1,1,16,512]{7,6,5,4,3,2,1,0:T(8,128)(2,1)S(1)}, u32[]{:S(2)}, u32[]{:S(2)}) %collective-permute-start.27) | collective-permute-done | bytes 131104 | tf_op jit(solution)/shard_map/ppermute | solution.py:76
  129.4 0.8 copy.57
  130.2 3.6 %collective-permute-done.38 = bf16[2,2,1,2,1,2,16,512]{7,6,5,4,3,2,1,0:T(8,128)(2,1)S(1)} collective-permute-done((bf16[2,2,1,2,1,2,16,512]{7,6,5,4,3,2,1,0:T(8,128)(2,1)S(1)}, bf16[2,2,1,2,1,2,16,512]{7,6,5,4,3,2,1,0:T(8,128)(2,1)S(1)}, u32[]{:S(2)}, u32[]{:S(2)}) %collective-permute-start.38) | collective-permute-done | bytes 262176 | tf_op jit(solution)/shard_map/ppermute | solution.py:76
  133.9 0.8 pad_maximum_fusion.12
  135.3 0.9 pad_maximum_fusion.10
  136.4 1.0 copy-done.6
  138.7 1.0 copy-done.7
  139.7 1.5 convolution_convert_fusion.4
  141.2 1.4 stack_reshape.13
  142.6 1.2 broadcast_select_fusion.3
  144.7 1.1 stack_reshape.14
  145.8 1.1 broadcast_select_fusion.7
  147.7 1.1 stack_reshape.12
  148.8 1.5 pad_maximum_fusion
  150.3 2.1 %gather_fusion.2 = bf16[4,2,64,2048]{3,2,1,0:T(8,128)(2,1)} fusion(bf16[4,2,64,2048]{3,2,1,0:T(8,128)(2,1)S(1)} %pad_maximum_fusion, s32[1024]{0:T(1024)} %pad_clamp_fusion.1), kind=kCustom, calls=%fused_computation.2 | custom fusion | bytes 4194320 | tf_op jit(solution)/shard_map/jit(_take)/gather | solution.py:153
  (303 shorter events, 33.9 us)
Async XLA Ops:
  2.3 2.0 %copy-start.19 = (f32[4,4,16]{2,1,0:T(4,128)}, f32[4,4,16]{2,1,0:T(4,128)S(1)}, u32[]{:S(2)}) copy-start(f32[4,4,16]{2,1,0:T(4,128)S(1)} %get-tuple-element.92) | copy-start | bytes 3076
  2.3 2.0 %copy-start.31 = (f32[4,4,16]{2,1,0:T(4,128)}, f32[4,4,16]{2,1,0:T(4,128)S(1)}, u32[]{:S(2)}) copy-start(f32[4,4,16]{2,1,0:T(4,128)S(1)} %get-tuple-element.86) | copy-start | bytes 3076
  2.3 2.5 %copy-start.21 = (f32[4,4,16]{2,1,0:T(4,128)}, f32[4,4,16]{2,1,0:T(4,128)S(1)}, u32[]{:S(2)}) copy-start(f32[4,4,16]{2,1,0:T(4,128)S(1)} %get-tuple-element.94) | copy-start | bytes 3076
  2.3 2.5 %copy-start.33 = (f32[4,4,16]{2,1,0:T(4,128)}, f32[4,4,16]{2,1,0:T(4,128)S(1)}, u32[]{:S(2)}) copy-start(f32[4,4,16]{2,1,0:T(4,128)S(1)} %get-tuple-element.88) | copy-start | bytes 3076
  2.3 3.0 %copy-start.11 = (f32[4,4,16]{2,1,0:T(4,128)}, f32[4,4,16]{2,1,0:T(4,128)S(1)}, u32[]{:S(2)}) copy-start(f32[4,4,16]{2,1,0:T(4,128)S(1)} %get-tuple-element.101) | copy-start | bytes 3076
  2.3 3.0 %copy-start.23 = (f32[4,4,16]{2,1,0:T(4,128)}, f32[4,4,16]{2,1,0:T(4,128)S(1)}, u32[]{:S(2)}) copy-start(f32[4,4,16]{2,1,0:T(4,128)S(1)} %get-tuple-element.96) | copy-start | bytes 3076
  2.3 3.0 %copy-start.35 = (f32[4,4,16]{2,1,0:T(4,128)}, f32[4,4,16]{2,1,0:T(4,128)S(1)}, u32[]{:S(2)}) copy-start(f32[4,4,16]{2,1,0:T(4,128)S(1)} %get-tuple-element.90) | copy-start | bytes 3076
  7.8 29.3 %collective-permute-start.18 = (bf16[2,3,4,4,1,512]{5,4,3,2,1,0:T(2,128)(2,1)}, bf16[2,3,4,4,1,512]{5,4,3,2,1,0:T(2,128)(2,1)}, u32[]{:S(2)}, u32[]{:S(2)}) collective-permute-start(bf16[2,3,4,4,1,512]{5,4,3,2,1,0:T(2,128)(2,1)} %pad_maximum_fusion.20), channel_id=1, source_target_pairs={{0,1},{1,0},{2,3},{3,2},{4,5},{5,4},{6,7},{7,6},{8,9},{9,8},{10,11... | collective-permute-start | bytes 294920 | tf_op jit(solution)/shard_map/ppermute | solution.py:97
  13.2 1.6 %copy-start = (bf16[2,3,4,4,16,512]{5,4,3,2,1,0:T(8,128)(2,1)S(1)}, bf16[2,3,4,4,16,512]{5,4,3,2,1,0:T(8,128)(2,1)}, u32[]{:S(2)}) copy-start(bf16[2,3,4,4,16,512]{5,4,3,2,1,0:T(8,128)(2,1)} %param.5) | copy-start | bytes 4718596
  14.1 33.2 %collective-permute-start.12 = (bf16[2,3,4,1,16,512]{5,4,3,2,1,0:T(8,128)(2,1)}, bf16[2,3,4,1,16,512]{5,4,3,2,1,0:T(8,128)(2,1)}, u32[]{:S(2)}, u32[]{:S(2)}) collective-permute-start(bf16[2,3,4,1,16,512]{5,4,3,2,1,0:T(8,128)(2,1)} %pad_maximum_fusion.14), channel_id=1, source_target_pairs={{0,2},{2,4},{4,6},{6,8},{8,10},{10,12},{12,14},{14,16},{16,18},{18... | collective-permute-start | bytes 1179656 | tf_op jit(solution)/shard_map/ppermute | solution.py:95
  15.6 25.3 %collective-permute-start.6 = (bf16[2,3,4,4,1,512]{5,3,4,2,1,0:T(4,128)(2,1)}, bf16[2,3,4,4,1,512]{5,3,4,2,1,0:T(4,128)(2,1)}, u32[]{:S(2)}, u32[]{:S(2)}) collective-permute-start(bf16[2,3,4,4,1,512]{5,3,4,2,1,0:T(4,128)(2,1)} %copy.76), channel_id=1, source_target_pairs={{0,1},{1,0},{2,3},{3,2},{4,5},{5,4},{6,7},{7,6},{8,9},{9,8},{10,11... | collective-permute-start | bytes 294920 | tf_op jit(solution)/shard_map/ppermute | solution.py:96
  16.4 34.3 %collective-permute-start = (bf16[2,3,4,1,16,512]{5,4,3,2,1,0:T(8,128)(2,1)}, bf16[2,3,4,1,16,512]{5,4,3,2,1,0:T(8,128)(2,1)S(1)}, u32[]{:S(2)}, u32[]{:S(2)}) collective-permute-start(bf16[2,3,4,1,16,512]{5,4,3,2,1,0:T(8,128)(2,1)} %slice.143), channel_id=1, source_target_pairs={{0,30},{2,0},{4,2},{6,4},{8,6},{10,8},{12,10},{14,12},{16,14},{18,... | collective-permute-start | bytes 1179656 | tf_op jit(solution)/shard_map/ppermute | solution.py:94
  23.5 2.8 %copy-start.9 = (bf16[1,3,4,4,16,512]{5,4,3,2,1,0:T(8,128)(2,1)S(1)}, bf16[1,3,4,4,16,512]{5,4,3,2,1,0:T(8,128)(2,1)}, u32[]{:S(2)}) copy-start(bf16[1,3,4,4,16,512]{5,4,3,2,1,0:T(8,128)(2,1)} %get-tuple-element.26) | copy-start | bytes 2359300
  23.5 4.5 %copy-start.10 = (bf16[2,64,2048]{2,1,0:T(8,128)(2,1)S(1)}, bf16[2,64,2048]{2,1,0:T(8,128)(2,1)}, u32[]{:S(2)}) copy-start(bf16[2,64,2048]{2,1,0:T(8,128)(2,1)} %param.9) | copy-start | bytes 1572868
  34.3 2.2 %copy-start.62 = (s32[4]{0:T(128)S(1)}, s32[4]{0:T(128)}, u32[]{:S(2)}) copy-start(s32[4]{0:T(128)} %param.7) | copy-start | bytes 52
  34.4 2.8 %copy-start.2 = (bf16[1,3,4,4,16,512]{5,4,3,2,1,0:T(8,128)(2,1)S(1)}, bf16[1,3,4,4,16,512]{5,4,3,2,1,0:T(8,128)(2,1)}, u32[]{:S(2)}) copy-start(bf16[1,3,4,4,16,512]{5,4,3,2,1,0:T(8,128)(2,1)} %copy-done.1) | copy-start | bytes 2359300
  34.4 2.8 %copy-start.4 = (bf16[1,3,4,4,16,512]{5,4,3,2,1,0:T(8,128)(2,1)S(1)}, bf16[1,3,4,4,16,512]{5,4,3,2,1,0:T(8,128)(2,1)}, u32[]{:S(2)}) copy-start(bf16[1,3,4,4,16,512]{5,4,3,2,1,0:T(8,128)(2,1)} %copy-done.3) | copy-start | bytes 2359300
  40.7 1.5 copy-start.5
  40.8 15.4 %collective-permute-start.19 = (f32[2,2,2,2,1,2,16,512]{7,6,0,5,4,3,2,1:T(8,128)S(1)}, f32[2,2,2,2,1,2,16,512]{7,6,0,5,4,3,2,1:T(8,128)S(1)}, u32[]{:S(2)}, u32[]{:S(2)}) collective-permute-start(f32[2,2,2,2,1,2,16,512]{7,6,0,5,4,3,2,1:T(8,128)S(1)} %constant_dynamic-slice_fusion.4), channel_id=1, source_target_pairs={{0,2},{1,3},{2,0},{3,1},{4,6},{5,7},{6,4},{7,5},{8,10},{9,11},{10,... | collective-permute-start | bytes 3145736 | tf_op jit(solution)/shard_map/ppermute | solution.py:67
  46.9 11.1 %collective-permute-start.7 = (f32[2,2,2,2,1,2,16,512]{7,6,0,5,4,3,2,1:T(8,128)S(1)}, f32[2,2,2,2,1,2,16,512]{7,6,0,5,4,3,2,1:T(8,128)S(1)}, u32[]{:S(2)}, u32[]{:S(2)}) collective-permute-start(f32[2,2,2,2,1,2,16,512]{7,6,0,5,4,3,2,1:T(8,128)S(1)} %constant_dynamic-slice_fusion.14), channel_id=1, source_target_pairs={{0,2},{1,3},{2,0},{3,1},{4,6},{5,7},{6,4},{7,5},{8,10},{9,11},{10,... | collective-permute-start | bytes 3145736 | tf_op jit(solution)/shard_map/ppermute | solution.py:67
  50.4 1.4 copy-start.38
  50.4 1.4 copy-start.40
  50.4 1.4 copy-start.42
  50.4 1.4 copy-start.58
  50.5 1.4 copy-start.59
  50.5 7.9 %collective-permute-start.13 = (f32[2,2,2,2,1,2,16,512]{7,6,5,4,3,2,1,0:T(8,128)S(1)}, f32[2,2,2,2,1,2,16,512]{7,6,5,4,3,2,1,0:T(8,128)S(1)}, u32[]{:S(2)}, u32[]{:S(2)}) collective-permute-start(f32[2,2,2,2,1,2,16,512]{7,6,5,4,3,2,1,0:T(8,128)S(1)} %constant_dynamic-slice_fusion.9), channel_id=1, source_target_pairs={{0,2},{1,3},{2,0},{3,1},{4,6},{5,7},{6,4},{7,5},{8,10},{9,11},{10,... | collective-permute-start | bytes 3145736 | tf_op jit(solution)/shard_map/ppermute | solution.py:67
  55.9 3.2 %collective-permute-start.1 = (f32[2,2,2,2,1,2,16,512]{7,6,5,4,3,2,1,0:T(8,128)S(1)}, f32[2,2,2,2,1,2,16,512]{7,6,5,4,3,2,1,0:T(8,128)S(1)}, u32[]{:S(2)}, u32[]{:S(2)}) collective-permute-start(f32[2,2,2,2,1,2,16,512]{7,6,5,4,3,2,1,0:T(8,128)S(1)} %constant_dynamic-slice_fusion.19), channel_id=1, source_target_pairs={{0,2},{1,3},{2,0},{3,1},{4,6},{5,7},{6,4},{7,5},{8,10},{9,11},{10,... | collective-permute-start | bytes 3145736 | tf_op jit(solution)/shard_map/ppermute | solution.py:67
  56.4 14.9 %collective-permute-start.20 = (f32[2,2,2,2,1,1,16,512]{7,6,0,5,4,3,2,1:T(8,128)S(1)}, f32[2,2,2,2,1,1,16,512]{7,6,0,5,4,3,2,1:T(8,128)S(1)}, u32[]{:S(2)}, u32[]{:S(2)}) collective-permute-start(f32[2,2,2,2,1,1,16,512]{7,6,0,5,4,3,2,1:T(8,128)S(1)} %constant_dynamic-slice_fusion.3), channel_id=1, source_target_pairs={{0,1},{1,0},{2,3},{3,2},{4,5},{5,4},{6,7},{7,6},{8,9},{9,8},{10,11... | collective-permute-start | bytes 1572872 | tf_op jit(solution)/shard_map/ppermute | solution.py:67
  58.3 14.0 %collective-permute-start.8 = (f32[2,2,2,1,1,2,16,512]{7,6,0,5,4,3,2,1:T(8,128)S(1)}, f32[2,2,2,1,1,2,16,512]{7,6,0,5,4,3,2,1:T(8,128)S(1)}, u32[]{:S(2)}, u32[]{:S(2)}) collective-permute-start(f32[2,2,2,1,1,2,16,512]{7,6,0,5,4,3,2,1:T(8,128)S(1)} %constant_dynamic-slice_fusion.13), channel_id=1, source_target_pairs={{0,4},{1,5},{2,6},{3,7},{4,0},{5,1},{6,2},{7,3},{8,12},{9,13},{10,... | collective-permute-start | bytes 1572872 | tf_op jit(solution)/shard_map/ppermute | solution.py:67
  58.7 21.9 %collective-permute-start.14 = (f32[2,2,1,2,1,2,16,512]{7,6,5,4,3,2,1,0:T(8,128)S(1)}, f32[2,2,1,2,1,2,16,512]{7,6,5,4,3,2,1,0:T(8,128)S(1)}, u32[]{:S(2)}, u32[]{:S(2)}) collective-permute-start(f32[2,2,1,2,1,2,16,512]{7,6,5,4,3,2,1,0:T(8,128)S(1)} %constant_dynamic-slice_fusion.8), channel_id=1, source_target_pairs={{0,8},{1,9},{2,10},{3,11},{4,12},{5,13},{6,14},{7,15},{8,0},{9,1},... | collective-permute-start | bytes 1572872 | tf_op jit(solution)/shard_map/ppermute | solution.py:67
  59.4 23.6 %collective-permute-start.2 = (f32[2,2,2,2,1,1,16,512]{7,6,5,4,3,2,1,0:T(8,128)S(1)}, f32[2,2,2,2,1,1,16,512]{7,6,5,4,3,2,1,0:T(8,128)S(1)}, u32[]{:S(2)}, u32[]{:S(2)}) collective-permute-start(f32[2,2,2,2,1,1,16,512]{7,6,5,4,3,2,1,0:T(8,128)S(1)} %constant_dynamic-slice_fusion.18), channel_id=1, source_target_pairs={{0,1},{1,0},{2,3},{3,2},{4,5},{5,4},{6,7},{7,6},{8,9},{9,8},{10,11... | collective-permute-start | bytes 1572872 | tf_op jit(solution)/shard_map/ppermute | solution.py:67
  71.4 7.2 %collective-permute-start.21 = (f32[2,2,2,1,1,1,16,512]{7,6,0,5,4,3,2,1:T(8,128)S(1)}, f32[2,2,2,1,1,1,16,512]{7,6,0,5,4,3,2,1:T(8,128)S(1)}, u32[]{:S(2)}, u32[]{:S(2)}) collective-permute-start(f32[2,2,2,1,1,1,16,512]{7,6,0,5,4,3,2,1:T(8,128)S(1)} %constant_dynamic-slice_fusion.2), channel_id=1, source_target_pairs={{0,4},{1,5},{2,6},{3,7},{4,0},{5,1},{6,2},{7,3},{8,12},{9,13},{10,... | collective-permute-start | bytes 786440 | tf_op jit(solution)/shard_map/ppermute | solution.py:67
  72.4 8.1 %collective-permute-start.9 = (f32[2,2,1,1,1,2,16,512]{7,6,0,5,4,3,2,1:T(8,128)S(1)}, f32[2,2,1,1,1,2,16,512]{7,6,0,5,4,3,2,1:T(8,128)S(1)}, u32[]{:S(2)}, u32[]{:S(2)}) collective-permute-start(f32[2,2,1,1,1,2,16,512]{7,6,0,5,4,3,2,1:T(8,128)S(1)} %constant_dynamic-slice_fusion.12), channel_id=1, source_target_pairs={{0,8},{1,9},{2,10},{3,11},{4,12},{5,13},{6,14},{7,15},{8,0},{9,1},... | collective-permute-start | bytes 786440 | tf_op jit(solution)/shard_map/ppermute | solution.py:67
  78.6 5.3 %collective-permute-start.22 = (f32[2,2,1,1,1,1,16,512]{7,6,0,5,4,3,2,1:T(8,128)S(1)}, f32[2,2,1,1,1,1,16,512]{7,6,0,5,4,3,2,1:T(8,128)S(1)}, u32[]{:S(2)}, u32[]{:S(2)}) collective-permute-start(f32[2,2,1,1,1,1,16,512]{7,6,0,5,4,3,2,1:T(8,128)S(1)} %constant_dynamic-slice_fusion.1), channel_id=1, source_target_pairs={{0,8},{1,9},{2,10},{3,11},{4,12},{5,13},{6,14},{7,15},{8,0},{9,1},... | collective-permute-start | bytes 393224 | tf_op jit(solution)/shard_map/ppermute | solution.py:67
  80.5 6.4 %collective-permute-start.10 = (f32[2,2,1,1,1,1,16,512]{7,6,0,5,4,3,2,1:T(8,128)S(1)}, f32[2,2,1,1,1,1,16,512]{7,6,0,5,4,3,2,1:T(8,128)S(1)}, u32[]{:S(2)}, u32[]{:S(2)}) collective-permute-start(f32[2,2,1,1,1,1,16,512]{7,6,0,5,4,3,2,1:T(8,128)S(1)} %constant_dynamic-slice_fusion.11), channel_id=1, source_target_pairs={{0,1},{1,0},{2,3},{3,2},{4,5},{5,4},{6,7},{7,6},{8,9},{9,8},{10,11... | collective-permute-start | bytes 393224 | tf_op jit(solution)/shard_map/ppermute | solution.py:67
  80.8 18.2 %collective-permute-start.15 = (f32[2,2,1,2,1,1,16,512]{7,6,5,4,3,2,1,0:T(8,128)S(1)}, f32[2,2,1,2,1,1,16,512]{7,6,5,4,3,2,1,0:T(8,128)S(1)}, u32[]{:S(2)}, u32[]{:S(2)}) collective-permute-start(f32[2,2,1,2,1,1,16,512]{7,6,5,4,3,2,1,0:T(8,128)S(1)} %constant_dynamic-slice_fusion.7), channel_id=1, source_target_pairs={{0,1},{1,0},{2,3},{3,2},{4,5},{5,4},{6,7},{7,6},{8,9},{9,8},{10,11... | collective-permute-start | bytes 786440 | tf_op jit(solution)/shard_map/ppermute | solution.py:67
  83.2 16.8 %collective-permute-start.3 = (f32[2,2,2,1,1,1,16,512]{7,6,5,4,3,2,1,0:T(8,128)S(1)}, f32[2,2,2,1,1,1,16,512]{7,6,5,4,3,2,1,0:T(8,128)S(1)}, u32[]{:S(2)}, u32[]{:S(2)}) collective-permute-start(f32[2,2,2,1,1,1,16,512]{7,6,5,4,3,2,1,0:T(8,128)S(1)} %constant_dynamic-slice_fusion.17), channel_id=1, source_target_pairs={{0,4},{1,5},{2,6},{3,7},{4,0},{5,1},{6,2},{7,3},{8,12},{9,13},{10,... | collective-permute-start | bytes 786440 | tf_op jit(solution)/shard_map/ppermute | solution.py:67
  84.0 6.5 %collective-permute-start.23 = (f32[2,1,1,1,1,1,16,512]{7,6,0,5,4,3,2,1:T(8,128)S(1)}, f32[2,1,1,1,1,1,16,512]{7,6,0,5,4,3,2,1:T(8,128)S(1)}, u32[]{:S(2)}, u32[]{:S(2)}) collective-permute-start(f32[2,1,1,1,1,1,16,512]{7,6,0,5,4,3,2,1:T(8,128)S(1)} %constant_dynamic-slice_fusion), channel_id=1, source_target_pairs={{0,16},{1,17},{2,18},{3,19},{4,20},{5,21},{6,22},{7,23},{8,24},{9,... | collective-permute-start | bytes 196616 | tf_op jit(solution)/shard_map/ppermute | solution.py:67
  87.0 6.0 %collective-permute-start.11 = (f32[2,1,1,1,1,1,16,512]{7,6,0,5,4,3,2,1:T(8,128)S(1)}, f32[2,1,1,1,1,1,16,512]{7,6,0,5,4,3,2,1:T(8,128)S(1)}, u32[]{:S(2)}, u32[]{:S(2)}) collective-permute-start(f32[2,1,1,1,1,1,16,512]{7,6,0,5,4,3,2,1:T(8,128)S(1)} %constant_dynamic-slice_fusion.10), channel_id=1, source_target_pairs={{0,16},{1,17},{2,18},{3,19},{4,20},{5,21},{6,22},{7,23},{8,24},{9,... | collective-permute-start | bytes 196616 | tf_op jit(solution)/shard_map/ppermute | solution.py:67
  90.5 4.9 %collective-permute-start.40 = (bf16[2,1,1,1,1,1,16,512]{7,6,5,4,3,2,1,0:T(8,128)(2,1)S(1)}, bf16[2,1,1,1,1,1,16,512]{7,6,5,4,3,2,1,0:T(8,128)(2,1)S(1)}, u32[]{:S(2)}, u32[]{:S(2)}) collective-permute-start(bf16[2,1,1,1,1,1,16,512]{7,6,5,4,3,2,1,0:T(8,128)(2,1)S(1)} %get-tuple-element.64), channel_id=1, source_target_pairs={{0,16},{1,17},{2,18},{3,19},{4,20},{5,21},{6,22},{7,23},{8,24},{9,... | collective-permute-start | bytes 98312 | tf_op jit(solution)/shard_map/ppermute | solution.py:76
  93.0 4.9 %collective-permute-start.30 = (bf16[2,1,1,1,1,1,16,512]{7,6,0,5,4,3,2,1:T(8,128)(2,1)S(1)}, bf16[2,1,1,1,1,1,16,512]{7,6,0,5,4,3,2,1:T(8,128)(2,1)S(1)}, u32[]{:S(2)}, u32[]{:S(2)}) collective-permute-start(bf16[2,1,1,1,1,1,16,512]{7,6,0,5,4,3,2,1:T(8,128)(2,1)S(1)} %get-tuple-element.60), channel_id=1, source_target_pairs={{0,16},{1,17},{2,18},{3,19},{4,20},{5,21},{6,22},{7,23},{8,24},{9,... | collective-permute-start | bytes 98312 | tf_op jit(solution)/shard_map/ppermute | solution.py:76
  95.4 5.0 %collective-permute-start.41 = (bf16[2,2,1,1,1,1,16,512]{7,6,5,4,3,2,1,0:T(8,128)(2,1)S(1)}, bf16[2,2,1,1,1,1,16,512]{7,6,5,4,3,2,1,0:T(8,128)(2,1)S(1)}, u32[]{:S(2)}, u32[]{:S(2)}) collective-permute-start(bf16[2,2,1,1,1,1,16,512]{7,6,5,4,3,2,1,0:T(8,128)(2,1)S(1)} %pad_maximum_fusion.28), channel_id=1, source_target_pairs={{0,8},{1,9},{2,10},{3,11},{4,12},{5,13},{6,14},{7,15},{8,0},{9,1},... | collective-permute-start | bytes 196616 | tf_op jit(solution)/shard_map/ppermute | solution.py:76
  97.9 4.3 %collective-permute-start.31 = (bf16[2,2,1,1,1,1,16,512]{7,6,0,5,4,3,2,1:T(8,128)(2,1)S(1)}, bf16[2,2,1,1,1,1,16,512]{7,6,0,5,4,3,2,1:T(8,128)(2,1)S(1)}, u32[]{:S(2)}, u32[]{:S(2)}) collective-permute-start(bf16[2,2,1,1,1,1,16,512]{7,6,0,5,4,3,2,1:T(8,128)(2,1)S(1)} %pad_maximum_fusion.26), channel_id=1, source_target_pairs={{0,1},{1,0},{2,3},{3,2},{4,5},{5,4},{6,7},{7,6},{8,9},{9,8},{10,11... | collective-permute-start | bytes 196616 | tf_op jit(solution)/shard_map/ppermute | solution.py:76
  99.1 5.0 %collective-permute-start.16 = (f32[2,2,1,1,1,1,16,512]{7,6,5,4,3,2,1,0:T(8,128)S(1)}, f32[2,2,1,1,1,1,16,512]{7,6,5,4,3,2,1,0:T(8,128)S(1)}, u32[]{:S(2)}, u32[]{:S(2)}) collective-permute-start(f32[2,2,1,1,1,1,16,512]{7,6,5,4,3,2,1,0:T(8,128)S(1)} %constant_dynamic-slice_fusion.6), channel_id=1, source_target_pairs={{0,4},{1,5},{2,6},{3,7},{4,0},{5,1},{6,2},{7,3},{8,12},{9,13},{10,... | collective-permute-start | bytes 393224 | tf_op jit(solution)/shard_map/ppermute | solution.py:67
  100.1 6.2 %collective-permute-start.4 = (f32[2,2,1,1,1,1,16,512]{7,6,5,4,3,2,1,0:T(8,128)S(1)}, f32[2,2,1,1,1,1,16,512]{7,6,5,4,3,2,1,0:T(8,128)S(1)}, u32[]{:S(2)}, u32[]{:S(2)}) collective-permute-start(f32[2,2,1,1,1,1,16,512]{7,6,5,4,3,2,1,0:T(8,128)S(1)} %constant_dynamic-slice_fusion.16), channel_id=1, source_target_pairs={{0,8},{1,9},{2,10},{3,11},{4,12},{5,13},{6,14},{7,15},{8,0},{9,1},... | collective-permute-start | bytes 393224 | tf_op jit(solution)/shard_map/ppermute | solution.py:67
  100.5 6.8 %collective-permute-start.42 = (bf16[2,2,2,1,1,1,16,512]{7,6,5,4,3,2,1,0:T(8,128)(2,1)S(1)}, bf16[2,2,2,1,1,1,16,512]{7,6,5,4,3,2,1,0:T(8,128)(2,1)S(1)}, u32[]{:S(2)}, u32[]{:S(2)}) collective-permute-start(bf16[2,2,2,1,1,1,16,512]{7,6,5,4,3,2,1,0:T(8,128)(2,1)S(1)} %pad_maximum_fusion.24), channel_id=1, source_target_pairs={{0,4},{1,5},{2,6},{3,7},{4,0},{5,1},{6,2},{7,3},{8,12},{9,13},{10,... | collective-permute-start | bytes 393224 | tf_op jit(solution)/shard_map/ppermute | solution.py:76
  102.3 6.1 %collective-permute-start.32 = (bf16[2,2,1,1,1,2,16,512]{7,6,0,5,4,3,2,1:T(8,128)(2,1)S(1)}, bf16[2,2,1,1,1,2,16,512]{7,6,0,5,4,3,2,1:T(8,128)(2,1)S(1)}, u32[]{:S(2)}, u32[]{:S(2)}) collective-permute-start(bf16[2,2,1,1,1,2,16,512]{7,6,0,5,4,3,2,1:T(8,128)(2,1)S(1)} %pad_maximum_fusion.22), channel_id=1, source_target_pairs={{0,8},{1,9},{2,10},{3,11},{4,12},{5,13},{6,14},{7,15},{8,0},{9,1},... | collective-permute-start | bytes 393224 | tf_op jit(solution)/shard_map/ppermute | solution.py:76
  104.1 5.8 %collective-permute-start.17 = (f32[2,1,1,1,1,1,16,512]{7,6,5,4,3,2,1,0:T(8,128)S(1)}, f32[2,1,1,1,1,1,16,512]{7,6,5,4,3,2,1,0:T(8,128)S(1)}, u32[]{:S(2)}, u32[]{:S(2)}) collective-permute-start(f32[2,1,1,1,1,1,16,512]{7,6,5,4,3,2,1,0:T(8,128)S(1)} %constant_dynamic-slice_fusion.5), channel_id=1, source_target_pairs={{0,16},{1,17},{2,18},{3,19},{4,20},{5,21},{6,22},{7,23},{8,24},{9,... | collective-permute-start | bytes 196616 | tf_op jit(solution)/shard_map/ppermute | solution.py:67
  106.3 5.8 %collective-permute-start.5 = (f32[2,1,1,1,1,1,16,512]{7,6,5,4,3,2,1,0:T(8,128)S(1)}, f32[2,1,1,1,1,1,16,512]{7,6,5,4,3,2,1,0:T(8,128)S(1)}, u32[]{:S(2)}, u32[]{:S(2)}) collective-permute-start(f32[2,1,1,1,1,1,16,512]{7,6,5,4,3,2,1,0:T(8,128)S(1)} %constant_dynamic-slice_fusion.15), channel_id=1, source_target_pairs={{0,16},{1,17},{2,18},{3,19},{4,20},{5,21},{6,22},{7,23},{8,24},{9,... | collective-permute-start | bytes 196616 | tf_op jit(solution)/shard_map/ppermute | solution.py:67
  107.3 17.3 %collective-permute-start.43 = (bf16[2,2,2,2,1,1,16,512]{7,6,5,4,3,2,1,0:T(8,128)(2,1)S(1)}, bf16[2,2,2,2,1,1,16,512]{7,6,5,4,3,2,1,0:T(8,128)(2,1)S(1)}, u32[]{:S(2)}, u32[]{:S(2)}) collective-permute-start(bf16[2,2,2,2,1,1,16,512]{7,6,5,4,3,2,1,0:T(8,128)(2,1)S(1)} %pad_maximum_fusion.19), channel_id=1, source_target_pairs={{0,1},{1,0},{2,3},{3,2},{4,5},{5,4},{6,7},{7,6},{8,9},{9,8},{10,11... | collective-permute-start | bytes 786440 | tf_op jit(solution)/shard_map/ppermute | solution.py:76
  108.5 16.4 %collective-permute-start.33 = (bf16[2,2,2,1,1,2,16,512]{7,6,0,5,4,3,2,1:T(8,128)(2,1)S(1)}, bf16[2,2,2,1,1,2,16,512]{7,6,0,5,4,3,2,1:T(8,128)(2,1)S(1)}, u32[]{:S(2)}, u32[]{:S(2)}) collective-permute-start(bf16[2,2,2,1,1,2,16,512]{7,6,0,5,4,3,2,1:T(8,128)(2,1)S(1)} %pad_maximum_fusion.17), channel_id=1, source_target_pairs={{0,4},{1,5},{2,6},{3,7},{4,0},{5,1},{6,2},{7,3},{8,12},{9,13},{10,... | collective-permute-start | bytes 786440 | tf_op jit(solution)/shard_map/ppermute | solution.py:76
  109.9 5.0 %collective-permute-start.35 = (bf16[2,1,1,1,1,1,16,512]{7,6,5,4,3,2,1,0:T(8,128)(2,1)S(1)}, bf16[2,1,1,1,1,1,16,512]{7,6,5,4,3,2,1,0:T(8,128)(2,1)S(1)}, u32[]{:S(2)}, u32[]{:S(2)}) collective-permute-start(bf16[2,1,1,1,1,1,16,512]{7,6,5,4,3,2,1,0:T(8,128)(2,1)S(1)} %get-tuple-element.62), channel_id=1, source_target_pairs={{0,16},{1,17},{2,18},{3,19},{4,20},{5,21},{6,22},{7,23},{8,24},{9,... | collective-permute-start | bytes 98312 | tf_op jit(solution)/shard_map/ppermute | solution.py:76
  112.8 16.5 %collective-permute-start.24 = (f32[4,2,1,1,1,1,1,16,512]{8,7,1,0,6,5,4,3,2:T(8,128)S(1)}, f32[4,2,1,1,1,1,1,16,512]{8,7,1,0,6,5,4,3,2:T(8,128)S(1)}, u32[]{:S(2)}, u32[]{:S(2)}) collective-permute-start(f32[4,2,1,1,1,1,1,16,512]{8,7,1,0,6,5,4,3,2:T(8,128)S(1)} %bitcast.549), channel_id=1, source_target_pairs={{0,1},{1,0},{2,3},{3,2},{4,5},{5,4},{6,7},{7,6},{8,9},{9,8},{10,11... | collective-permute-start | bytes 786440 | tf_op jit(solution)/shard_map/ppermute | solution.py:76
  114.1 5.2 %collective-permute-start.25 = (bf16[2,1,1,1,1,1,16,512]{7,6,5,4,3,2,1,0:T(8,128)(2,1)S(1)}, bf16[2,1,1,1,1,1,16,512]{7,6,5,4,3,2,1,0:T(8,128)(2,1)S(1)}, u32[]{:S(2)}, u32[]{:S(2)}) collective-permute-start(bf16[2,1,1,1,1,1,16,512]{7,6,5,4,3,2,1,0:T(8,128)(2,1)S(1)} %get-tuple-element.58), channel_id=1, source_target_pairs={{0,16},{1,17},{2,18},{3,19},{4,20},{5,21},{6,22},{7,23},{8,24},{9,... | collective-permute-start | bytes 98312 | tf_op jit(solution)/shard_map/ppermute | solution.py:76
  115.0 5.0 %collective-permute-start.36 = (bf16[2,2,1,1,1,1,16,512]{7,6,5,4,3,2,1,0:T(8,128)(2,1)S(1)}, bf16[2,2,1,1,1,1,16,512]{7,6,5,4,3,2,1,0:T(8,128)(2,1)S(1)}, u32[]{:S(2)}, u32[]{:S(2)}) collective-permute-start(bf16[2,2,1,1,1,1,16,512]{7,6,5,4,3,2,1,0:T(8,128)(2,1)S(1)} %pad_maximum_fusion.27), channel_id=1, source_target_pairs={{0,4},{1,5},{2,6},{3,7},{4,0},{5,1},{6,2},{7,3},{8,12},{9,13},{10,... | collective-permute-start | bytes 196616 | tf_op jit(solution)/shard_map/ppermute | solution.py:76
  119.3 4.3 %collective-permute-start.26 = (bf16[2,2,1,1,1,1,16,512]{7,6,5,4,3,2,1,0:T(8,128)(2,1)S(1)}, bf16[2,2,1,1,1,1,16,512]{7,6,5,4,3,2,1,0:T(8,128)(2,1)S(1)}, u32[]{:S(2)}, u32[]{:S(2)}) collective-permute-start(bf16[2,2,1,1,1,1,16,512]{7,6,5,4,3,2,1,0:T(8,128)(2,1)S(1)} %pad_maximum_fusion.25), channel_id=1, source_target_pairs={{0,8},{1,9},{2,10},{3,11},{4,12},{5,13},{6,14},{7,15},{8,0},{9,1},... | collective-permute-start | bytes 196616 | tf_op jit(solution)/shard_map/ppermute | solution.py:76
  120.0 5.5 %collective-permute-start.37 = (bf16[2,2,1,2,1,1,16,512]{7,6,5,4,3,2,1,0:T(8,128)(2,1)S(1)}, bf16[2,2,1,2,1,1,16,512]{7,6,5,4,3,2,1,0:T(8,128)(2,1)S(1)}, u32[]{:S(2)}, u32[]{:S(2)}) collective-permute-start(bf16[2,2,1,2,1,1,16,512]{7,6,5,4,3,2,1,0:T(8,128)(2,1)S(1)} %pad_maximum_fusion.23), channel_id=1, source_target_pairs={{0,1},{1,0},{2,3},{3,2},{4,5},{5,4},{6,7},{7,6},{8,9},{9,8},{10,11... | collective-permute-start | bytes 393224 | tf_op jit(solution)/shard_map/ppermute | solution.py:76
  123.7 5.0 %collective-permute-start.27 = (bf16[2,2,2,1,1,1,16,512]{7,6,5,4,3,2,1,0:T(8,128)(2,1)S(1)}, bf16[2,2,2,1,1,1,16,512]{7,6,5,4,3,2,1,0:T(8,128)(2,1)S(1)}, u32[]{:S(2)}, u32[]{:S(2)}) collective-permute-start(bf16[2,2,2,1,1,1,16,512]{7,6,5,4,3,2,1,0:T(8,128)(2,1)S(1)} %pad_maximum_fusion.21), channel_id=1, source_target_pairs={{0,4},{1,5},{2,6},{3,7},{4,0},{5,1},{6,2},{7,3},{8,12},{9,13},{10,... | collective-permute-start | bytes 393224 | tf_op jit(solution)/shard_map/ppermute | solution.py:76
  124.8 11.4 %collective-permute-start.44 = (bf16[2,2,2,2,1,2,16,512]{7,6,5,4,3,2,1,0:T(8,128)(2,1)S(1)}, bf16[2,2,2,2,1,2,16,512]{7,6,5,4,3,2,1,0:T(8,128)(2,1)S(1)}, u32[]{:S(2)}, u32[]{:S(2)}) collective-permute-start(bf16[2,2,2,2,1,2,16,512]{7,6,5,4,3,2,1,0:T(8,128)(2,1)S(1)} %pad_maximum_fusion.13), channel_id=1, source_target_pairs={{0,2},{1,3},{2,0},{3,1},{4,6},{5,7},{6,4},{7,5},{8,10},{9,11},{10,... | collective-permute-start | bytes 1572872 | tf_op jit(solution)/shard_map/ppermute | solution.py:76
  125.0 13.1 %collective-permute-start.34 = (bf16[2,2,2,2,1,2,16,512]{7,6,0,5,4,3,2,1:T(8,128)(2,1)S(1)}, bf16[2,2,2,2,1,2,16,512]{7,6,0,5,4,3,2,1:T(8,128)(2,1)S(1)}, u32[]{:S(2)}, u32[]{:S(2)}) collective-permute-start(bf16[2,2,2,2,1,2,16,512]{7,6,0,5,4,3,2,1:T(8,128)(2,1)S(1)} %pad_maximum_fusion.11), channel_id=1, source_target_pairs={{0,2},{1,3},{2,0},{3,1},{4,6},{5,7},{6,4},{7,5},{8,10},{9,11},{10,... | collective-permute-start | bytes 1572872 | tf_op jit(solution)/shard_map/ppermute | solution.py:76
  125.6 8.3 %collective-permute-start.38 = (bf16[2,2,1,2,1,2,16,512]{7,6,5,4,3,2,1,0:T(8,128)(2,1)S(1)}, bf16[2,2,1,2,1,2,16,512]{7,6,5,4,3,2,1,0:T(8,128)(2,1)S(1)}, u32[]{:S(2)}, u32[]{:S(2)}) collective-permute-start(bf16[2,2,1,2,1,2,16,512]{7,6,5,4,3,2,1,0:T(8,128)(2,1)S(1)} %pad_maximum_fusion.18), channel_id=1, source_target_pairs={{0,8},{1,9},{2,10},{3,11},{4,12},{5,13},{6,14},{7,15},{8,0},{9,1},... | collective-permute-start | bytes 786440 | tf_op jit(solution)/shard_map/ppermute | solution.py:76
  128.8 6.4 %collective-permute-start.28 = (bf16[2,2,2,2,1,1,16,512]{7,6,5,4,3,2,1,0:T(8,128)(2,1)S(1)}, bf16[2,2,2,2,1,1,16,512]{7,6,5,4,3,2,1,0:T(8,128)(2,1)S(1)}, u32[]{:S(2)}, u32[]{:S(2)}) collective-permute-start(bf16[2,2,2,2,1,1,16,512]{7,6,5,4,3,2,1,0:T(8,128)(2,1)S(1)} %pad_maximum_fusion.16), channel_id=1, source_target_pairs={{0,1},{1,0},{2,3},{3,2},{4,5},{5,4},{6,7},{7,6},{8,9},{9,8},{10,11... | collective-permute-start | bytes 786440 | tf_op jit(solution)/shard_map/ppermute | solution.py:76
  134.8 7.8 %collective-permute-start.39 = (bf16[2,2,2,2,1,2,16,512]{7,6,5,4,3,2,1,0:T(8,128)(2,1)}, bf16[2,2,2,2,1,2,16,512]{7,6,5,4,3,2,1,0:T(8,128)(2,1)}, u32[]{:S(2)}, u32[]{:S(2)}) collective-permute-start(bf16[2,2,2,2,1,2,16,512]{7,6,5,4,3,2,1,0:T(8,128)(2,1)} %pad_maximum_fusion.12), channel_id=1, source_target_pairs={{0,2},{1,3},{2,0},{3,1},{4,6},{5,7},{6,4},{7,5},{8,10},{9,11},{10,... | collective-permute-start | bytes 1572872 | tf_op jit(solution)/shard_map/ppermute | solution.py:76
  136.1 9.6 %collective-permute-start.29 = (bf16[2,2,2,2,1,2,16,512]{7,6,5,4,3,2,1,0:T(8,128)(2,1)}, bf16[2,2,2,2,1,2,16,512]{7,6,5,4,3,2,1,0:T(8,128)(2,1)}, u32[]{:S(2)}, u32[]{:S(2)}) collective-permute-start(bf16[2,2,2,2,1,2,16,512]{7,6,5,4,3,2,1,0:T(8,128)(2,1)} %pad_maximum_fusion.10), channel_id=1, source_target_pairs={{0,2},{1,3},{2,0},{3,1},{4,6},{5,7},{6,4},{7,5},{8,10},{9,11},{10,... | collective-permute-start | bytes 1572872 | tf_op jit(solution)/shard_map/ppermute | solution.py:76
  (45 other events, 37.7 us)

commit v9 on v8

--- a/solution.py
+++ b/solution.py
@@ -123,12 +123,18 @@
 
         prows = perambulator.shape[1]
         nspin = perambulator.shape[2] // nev
-        p_re = perambulator[0].reshape(prows * nspin, nev)
-        p_im = perambulator[1].reshape(prows * nspin, nev)
+        onehot = (spin_map[:, None] == jnp.arange(nspin, dtype=spin_map.dtype)[None, :]).astype(
+            perambulator.dtype
+        )
+        chosen = jnp.einsum(
+            "prtn,st->prsn", perambulator.reshape(2, prows, nspin, nev), onehot,
+            preferred_element_type=jnp.float32,
+        ).astype(perambulator.dtype)
+        p_re = chosen[0].reshape(prows * nspin, nev)
+        p_im = chosen[1].reshape(prows * nspin, nev)
         lhs = jnp.stack(
             [jnp.concatenate([p_re, -p_im], -1), jnp.concatenate([p_im, p_re], -1)], 0
-        ).reshape(2, prows, nspin, 2 * nev)
-        lhs = jnp.take(lhs, spin_map, axis=2, mode="clip").reshape(2 * prows * nspin, 2 * nev)
+        ).reshape(2 * prows * nspin, 2 * nev)
 
         own = []
         products = []

time: 153 us -> 149 us (0.974)
  local copies, waits for them, and re-layouts: 27.2 us -> 21.7 us
  starting transfers between devices: 36.2 us -> 34.6 us
  waiting for transfers between devices: 45.2 us -> 46.8 us
    gather x2 -> x0, local copies, waits for them, and re-layouts: 3.77 us -> none  [local(): jnp.take(lhs, spin_map, axis=2, mode='clip')]
    unnamed x127 -> x111, local copies, waits for them, and re-layouts: 5.39 us -> 4.34 us
  transfers between devices with their start and end apart: 45 -> 45, of which waited for: 21 -> 21; matrix products, arithmetic and copies ran while one was open for 33% -> 32% of each run, Pallas kernels for 0% -> 0%
where the time goes in v9:
time: 149 us; the launch traced here: 148 us
  waiting for transfers between devices  46.8 us (31%)
  starting transfers between devices  34.6 us (23%)
  other arithmetic  27.4 us (18%)
  local copies, waits for them, and re-layouts  21.7 us (15%)
  matrix products  15.8 us (11%)
  between operations  2.17 us (1%)
    ppermute x20, waiting for transfers between devices, reduce_scatter(): buf = keep + lax.ppermute(send, ALL, xor_pairs(count, b))  30.1 us
    ppermute x21, waiting for transfers between devices, all_gather(): other = lax.ppermute(buf, ALL, xor_pairs(count, b))  16.6 us
    ppermute x21, starting transfers between devices, all_gather(): other = lax.ppermute(buf, ALL, xor_pairs(count, b))  15.5 us
    ppermute x20, starting transfers between devices, reduce_scatter(): buf = keep + lax.ppermute(send, ALL, xor_pairs(count, b))  12.1 us
    dot_general x4, matrix products, local(): jnp.dot(left, field.reshape(2 * depth, nev), preferred_element_type=jnp.f...  7.12 us
    another operation x12, other arithmetic  6.04 us
    dot_general x2, matrix products, local(): lax.dot_general(unit, flat[c], (((1,), (1,)), ((), ())), preferred_elemen...  4.55 us
    unnamed x111, local copies, waits for them, and re-layouts  4.34 us
  transfers between devices with their start and end apart: 45, of which 21 were waited for; matrix products, arithmetic and copies ran while one was open for 32% of the time, Pallas kernels for 0%

profile of v9, /device:TPU:0, one launch (start us, length us, event | category | flops | bytes accessed | tf_op | source)
XLA Modules:
  0.0 148.5 jit_solution(5141523106490032435)
XLA Ops:
  0.6 1.0 slice_bitcast_fusion.19
  2.4 1.9 %convert_element_type.82 = f32[2,3,4,4,16,512]{5,4,3,2,1,0:T(8,128)S(1)} convert(bf16[2,3,4,4,16,512]{5,4,3,2,1,0:T(8,128)(2,1)} %param.5) | non-fusion elementwise | flops 786432 | bytes 4718592 | tf_op jit(solution)/shard_map/convert_element_type | solution.py:13
  6.8 1.0 pad_maximum_fusion.21
  7.8 3.0 %collective-permute-start.18 = (bf16[2,3,4,4,1,512]{5,4,3,2,1,0:T(2,128)(2,1)}, bf16[2,3,4,4,1,512]{5,4,3,2,1,0:T(2,128)(2,1)}, u32[]{:S(2)}, u32[]{:S(2)}) collective-permute-start(bf16[2,3,4,4,1,512]{5,4,3,2,1,0:T(2,128)(2,1)} %pad_maximum_fusion.21), channel_id=1, source_target_pairs={{0,1},{1,0},{2,3},{3,2},{4,5},{5,4},{6,7},{7,6},{8,9},{9,8},{10,11... | collective-permute-start | bytes 294920 | tf_op jit(solution)/shard_map/ppermute | solution.py:97
  15.8 4.0 %collective-permute-start = (bf16[2,3,4,1,16,512]{5,4,3,2,1,0:T(8,128)(2,1)}, bf16[2,3,4,1,16,512]{5,4,3,2,1,0:T(8,128)(2,1)}, u32[]{:S(2)}, u32[]{:S(2)}) collective-permute-start(bf16[2,3,4,1,16,512]{5,4,3,2,1,0:T(8,128)(2,1)} %slice.143), channel_id=1, source_target_pairs={{0,30},{2,0},{4,2},{6,4},{8,6},{10,8},{12,10},{14,12},{16,14},{18,... | collective-permute-start | bytes 1179656 | tf_op jit(solution)/shard_map/ppermute | solution.py:94
  19.8 1.4 fusion.35
  21.2 1.8 %slice.169 = bf16[2,3,4,4,15,512]{5,4,3,2,1,0:T(8,128)(2,1)} slice(bf16[2,3,4,4,16,512]{5,4,3,2,1,0:T(8,128)(2,1)S(1)} %copy-done), slice={[0:2], [0:3], [0:4], [0:4], [1:16], [0:512]} | slice | bytes 2949120 | tf_op jit(solution)/shard_map/slice | solution.py:99
  23.0 2.7 %convolution_convert_fusion.1 = bf16[512,768]{1,0:T(8,128)(2,1)} fusion(bf16[768,512]{1,0:T(8,128)(2,1)} %bitcast.556), kind=kOutput, calls=%fused_computation.17 | convolution fusion | flops 403308544 | bytes 1572864 | tf_op jit(solution)/shard_map/dot_general | solution.py:110
  25.8 1.8 %fusion.37 = (bf16[512,768]{1,0:T(8,128)(2,1)}, bf16[512,768]{1,0:T(8,128)(2,1)}) fusion(bf16[768,512]{1,0:T(8,128)(2,1)S(1)} %bitcast.555), kind=kOutput, calls=%fused_computation.254 | convolution fusion | flops 403701760 | bytes 2359296 | tf_op jit(solution)/shard_map/dot_general | solution.py:110
  29.0 1.1 pad_maximum_fusion.5
  30.1 2.2 %maximum_maximum_fusion = bf16[1024,1536]{1,0:T(8,128)(2,1)S(1)} fusion(bf16[512,768]{1,0:T(8,128)(2,1)} %convolution_convert_fusion.1, bf16[512,768]{1,0:T(8,128)(2,1)} %get-tuple-element.138, bf16[512,768]{1,0:T(8,128)(2,1)} %get-tuple-element.139), kind=kLoop, calls=%fused_computation.2 | loop fusion | flops 12582912 | bytes 5505024 | tf_op jit(solution)/shard_map/concatenate | solution.py:115
  32.4 1.7 %fusion.4 = bf16[2,3,4,4,16,512]{5,4,3,2,1,0:T(8,128)(2,1)S(1)} fusion(bf16[1,3,4,4,16,512]{5,4,3,2,1,0:T(8,128)(2,1)S(1)} %copy-done.2, bf16[1,3,4,4,16,512]{5,4,3,2,1,0:T(8,128)(2,1)S(1)} %copy-done.4, bf16[2,3,4,4,1,512]{5,4,3,2,1,0:T(2,128)(2,1)} %collective-permute-done.18), kind=kLoop, calls=%fused_computation.9 | loop fusion | flops 4718592 | bytes 3244032 | tf_op jit(solution)/shard_map/concatenate | solution.py:104
  34.1 1.8 %fusion = f32[2,2,2,2,2,2,16,512]{7,6,0,5,4,3,2,1:T(8,128)S(1)} fusion(bf16[1536,512,1,1,1,1,1,1]{1,0,2,7,6,5,4,3:T(8,128)(2,1)S(1)} %bitcast.543, bf16[2,2,2,2,2,2,16,1536]{7,6,5,4,3,2,1,0:T(8,128)(2,1)S(1)} %bitcast.538), kind=kOutput, calls=%fused_computation.3 | convolution fusion | flops 1610612736 | bytes 6815744 | tf_op jit(solution)/shard_map/dot_general | solution.py:143
  36.1 1.2 copy.33
  40.3 1.8 %fusion.2 = f32[2,2,2,2,2,2,16,512]{7,6,0,5,4,3,2,1:T(8,128)S(1)} fusion(bf16[1536,512,1,1,1,1,1,1]{1,0,2,7,6,5,4,3:T(8,128)(2,1)S(1)} %bitcast.545, bf16[2,2,2,2,2,2,16,1536]{7,6,5,4,3,2,1,0:T(8,128)(2,1)S(1)} %bitcast.539), kind=kOutput, calls=%fused_computation.5 | convolution fusion | flops 1610612736 | bytes 6815744 | tf_op jit(solution)/shard_map/dot_general | solution.py:143
  42.5 1.2 fusion.5
  43.7 1.8 %fusion.39 = f32[2,2,2,2,2,2,16,512]{7,6,5,4,3,2,1,0:T(8,128)S(1)} fusion(bf16[2,2,2,2,2,2,16,1536]{7,6,5,4,3,2,1,0:T(8,128)(2,1)S(1)} %bitcast.540, bf16[1536,512,1,1,1,1,1,1]{1,0,7,6,5,4,3,2:T(8,128)(2,1)S(1)} %bitcast.542), kind=kOutput, calls=%fused_computation.256 | convolution fusion | flops 1610612736 | bytes 6815744 | tf_op jit(solution)/shard_map/dot_general | solution.py:143
  45.9 0.9 slice-done
  46.8 1.2 maximum_convert_fusion
  50.4 1.8 %fusion.38 = f32[2,2,2,2,2,2,16,512]{7,6,5,4,3,2,1,0:T(8,128)S(1)} fusion(bf16[2,2,2,2,2,2,16,1536]{7,6,5,4,3,2,1,0:T(8,128)(2,1)S(1)} %bitcast.541, bf16[1536,512,1,1,1,1,1,1]{1,0,7,6,5,4,3,2:T(8,128)(2,1)S(1)} %bitcast.544), kind=kOutput, calls=%fused_computation.255 | convolution fusion | flops 1610612736 | bytes 6815744 | tf_op jit(solution)/shard_map/dot_general | solution.py:143
  52.8 1.6 %collective-permute-start.20 = (f32[2,2,2,2,1,1,16,512]{7,6,0,5,4,3,2,1:T(8,128)S(1)}, f32[2,2,2,2,1,1,16,512]{7,6,0,5,4,3,2,1:T(8,128)S(1)}, u32[]{:S(2)}, u32[]{:S(2)}) collective-permute-start(f32[2,2,2,2,1,1,16,512]{7,6,0,5,4,3,2,1:T(8,128)S(1)} %constant_dynamic-slice_fusion.3), channel_id=1, source_target_pairs={{0,1},{1,0},{2,3},{3,2},{4,5},{5,4},{6,7},{7,6},{8,9},{9,8},{10,11... | collective-permute-start | bytes 1572872 | tf_op jit(solution)/shard_map/ppermute | solution.py:67
  55.8 1.2 collective-permute-start.2
  57.0 10.7 %collective-permute-done.20 = f32[2,2,2,2,1,1,16,512]{7,6,0,5,4,3,2,1:T(8,128)S(1)} collective-permute-done((f32[2,2,2,2,1,1,16,512]{7,6,0,5,4,3,2,1:T(8,128)S(1)}, f32[2,2,2,2,1,1,16,512]{7,6,0,5,4,3,2,1:T(8,128)S(1)}, u32[]{:S(2)}, u32[]{:S(2)}) %collective-permute-start.20) | collective-permute-done | bytes 524320 | tf_op jit(solution)/shard_map/ppermute | solution.py:67
  68.9 6.1 %collective-permute-done.21 = f32[2,2,2,1,1,1,16,512]{7,6,0,5,4,3,2,1:T(8,128)S(1)} collective-permute-done((f32[2,2,2,1,1,1,16,512]{7,6,0,5,4,3,2,1:T(8,128)S(1)}, f32[2,2,2,1,1,1,16,512]{7,6,0,5,4,3,2,1:T(8,128)S(1)}, u32[]{:S(2)}, u32[]{:S(2)}) %collective-permute-start.21) | collective-permute-done | bytes 262176 | tf_op jit(solution)/shard_map/ppermute | solution.py:67
  75.1 1.8 %collective-permute-done.9 = f32[2,2,1,1,1,2,16,512]{7,6,0,5,4,3,2,1:T(8,128)S(1)} collective-permute-done((f32[2,2,1,1,1,2,16,512]{7,6,0,5,4,3,2,1:T(8,128)S(1)}, f32[2,2,1,1,1,2,16,512]{7,6,0,5,4,3,2,1:T(8,128)S(1)}, u32[]{:S(2)}, u32[]{:S(2)}) %collective-permute-start.9) | collective-permute-done | bytes 262176 | tf_op jit(solution)/shard_map/ppermute | solution.py:67
  77.2 2.1 %collective-permute-start.15 = (f32[2,2,1,2,1,1,16,512]{7,6,5,4,3,2,1,0:T(8,128)S(1)}, f32[2,2,1,2,1,1,16,512]{7,6,5,4,3,2,1,0:T(8,128)S(1)}, u32[]{:S(2)}, u32[]{:S(2)}) collective-permute-start(f32[2,2,1,2,1,1,16,512]{7,6,5,4,3,2,1,0:T(8,128)S(1)} %constant_dynamic-slice_fusion.7), channel_id=1, source_target_pairs={{0,1},{1,0},{2,3},{3,2},{4,5},{5,4},{6,7},{7,6},{8,9},{9,8},{10,11... | collective-permute-start | bytes 786440 | tf_op jit(solution)/shard_map/ppermute | solution.py:67
  80.1 0.9 collective-permute-start.23
  81.0 2.3 %collective-permute-done.10 = f32[2,2,1,1,1,1,16,512]{7,6,0,5,4,3,2,1:T(8,128)S(1)} collective-permute-done((f32[2,2,1,1,1,1,16,512]{7,6,0,5,4,3,2,1:T(8,128)S(1)}, f32[2,2,1,1,1,1,16,512]{7,6,0,5,4,3,2,1:T(8,128)S(1)}, u32[]{:S(2)}, u32[]{:S(2)}) %collective-permute-start.10) | collective-permute-done | bytes 131104 | tf_op jit(solution)/shard_map/ppermute | solution.py:67
  84.2 2.7 %collective-permute-done.23 = f32[2,1,1,1,1,1,16,512]{7,6,0,5,4,3,2,1:T(8,128)S(1)} collective-permute-done((f32[2,1,1,1,1,1,16,512]{7,6,0,5,4,3,2,1:T(8,128)S(1)}, f32[2,1,1,1,1,1,16,512]{7,6,0,5,4,3,2,1:T(8,128)S(1)}, u32[]{:S(2)}, u32[]{:S(2)}) %collective-permute-start.23) | collective-permute-done | bytes 65568 | tf_op jit(solution)/shard_map/ppermute | solution.py:67
  87.0 2.5 %collective-permute-done.11 = f32[2,1,1,1,1,1,16,512]{7,6,0,5,4,3,2,1:T(8,128)S(1)} collective-permute-done((f32[2,1,1,1,1,1,16,512]{7,6,0,5,4,3,2,1:T(8,128)S(1)}, f32[2,1,1,1,1,1,16,512]{7,6,0,5,4,3,2,1:T(8,128)S(1)}, u32[]{:S(2)}, u32[]{:S(2)}) %collective-permute-start.11) | collective-permute-done | bytes 65568 | tf_op jit(solution)/shard_map/ppermute | solution.py:67
  89.9 1.8 %collective-permute-done.40 = bf16[2,1,1,1,1,1,16,512]{7,6,5,4,3,2,1,0:T(8,128)(2,1)S(1)} collective-permute-done((bf16[2,1,1,1,1,1,16,512]{7,6,5,4,3,2,1,0:T(8,128)(2,1)S(1)}, bf16[2,1,1,1,1,1,16,512]{7,6,5,4,3,2,1,0:T(8,128)(2,1)S(1)}, u32[]{:S(2)}, u32[]{:S(2)}) %collective-permute-start.40) | collective-permute-done | bytes 32800 | tf_op jit(solution)/shard_map/ppermute | solution.py:76
  92.1 2.2 %collective-permute-done.30 = bf16[2,1,1,1,1,1,16,512]{7,6,0,5,4,3,2,1:T(8,128)(2,1)S(1)} collective-permute-done((bf16[2,1,1,1,1,1,16,512]{7,6,0,5,4,3,2,1:T(8,128)(2,1)S(1)}, bf16[2,1,1,1,1,1,16,512]{7,6,0,5,4,3,2,1:T(8,128)(2,1)S(1)}, u32[]{:S(2)}, u32[]{:S(2)}) %collective-permute-start.30) | collective-permute-done | bytes 32800 | tf_op jit(solution)/shard_map/ppermute | solution.py:76
  94.3 1.0 collective-permute-start.31
  95.5 0.9 collective-permute-start.16
  96.9 1.3 collective-permute-start.42
  98.7 1.2 collective-permute-start.32
  100.5 1.1 collective-permute-start.17
  101.6 1.1 collective-permute-done.4
  102.8 0.8 collective-permute-start.5
  103.7 1.1 collective-permute-start.43
  105.3 1.0 collective-permute-done.17
  106.3 1.5 collective-permute-start.35
  109.0 1.3 collective-permute-start.24
  110.3 1.1 collective-permute-start.25
  111.5 1.2 collective-permute-start.36
  112.7 2.8 %collective-permute-done.25 = bf16[2,1,1,1,1,1,16,512]{7,6,5,4,3,2,1,0:T(8,128)(2,1)S(1)} collective-permute-done((bf16[2,1,1,1,1,1,16,512]{7,6,5,4,3,2,1,0:T(8,128)(2,1)S(1)}, bf16[2,1,1,1,1,1,16,512]{7,6,5,4,3,2,1,0:T(8,128)(2,1)S(1)}, u32[]{:S(2)}, u32[]{:S(2)}) %collective-permute-start.25) | collective-permute-done | bytes 32800 | tf_op jit(solution)/shard_map/ppermute | solution.py:76
  117.3 2.6 %collective-permute-done.26 = bf16[2,2,1,1,1,1,16,512]{7,6,5,4,3,2,1,0:T(8,128)(2,1)S(1)} collective-permute-done((bf16[2,2,1,1,1,1,16,512]{7,6,5,4,3,2,1,0:T(8,128)(2,1)S(1)}, bf16[2,2,1,1,1,1,16,512]{7,6,5,4,3,2,1,0:T(8,128)(2,1)S(1)}, u32[]{:S(2)}, u32[]{:S(2)}) %collective-permute-start.26) | collective-permute-done | bytes 65568 | tf_op jit(solution)/shard_map/ppermute | solution.py:76
  119.9 0.9 collective-permute-start.27
  121.7 1.1 collective-permute-start.38
  122.8 2.1 %collective-permute-done.27 = bf16[2,2,2,1,1,1,16,512]{7,6,5,4,3,2,1,0:T(8,128)(2,1)S(1)} collective-permute-done((bf16[2,2,2,1,1,1,16,512]{7,6,5,4,3,2,1,0:T(8,128)(2,1)S(1)}, bf16[2,2,2,1,1,1,16,512]{7,6,5,4,3,2,1,0:T(8,128)(2,1)S(1)}, u32[]{:S(2)}, u32[]{:S(2)}) %collective-permute-start.27) | collective-permute-done | bytes 131104 | tf_op jit(solution)/shard_map/ppermute | solution.py:76
  125.8 0.8 copy.39
  126.6 3.4 %collective-permute-done.38 = bf16[2,2,1,2,1,2,16,512]{7,6,5,4,3,2,1,0:T(8,128)(2,1)S(1)} collective-permute-done((bf16[2,2,1,2,1,2,16,512]{7,6,5,4,3,2,1,0:T(8,128)(2,1)S(1)}, bf16[2,2,1,2,1,2,16,512]{7,6,5,4,3,2,1,0:T(8,128)(2,1)S(1)}, u32[]{:S(2)}, u32[]{:S(2)}) %collective-permute-start.38) | collective-permute-done | bytes 262176 | tf_op jit(solution)/shard_map/ppermute | solution.py:76
  130.1 0.8 pad_maximum_fusion.13
  131.5 0.8 pad_maximum_fusion.11
  132.5 1.0 copy-done.6
  134.9 1.0 copy-done.7
  135.9 1.5 %convolution_convert_fusion.5 = bf16[512,512]{1,0:T(8,128)(2,1)} fusion(bf16[512,1024]{1,0:T(8,128)(2,1)S(1)} %bitcast.547, bf16[1024,512]{1,0:T(8,128)(2,1)S(1)} %bitcast.553), kind=kOutput, calls=%fused_computation.21 | convolution fusion | flops 537133056 | bytes 2621440 | tf_op jit(solution)/shard_map/dot_general | solution.py:150
  137.4 1.4 stack_reshape.13
  138.8 1.2 broadcast_select_fusion.3
  140.8 1.1 stack_reshape.14
  141.9 1.1 broadcast_select_fusion.7
  143.9 1.1 stack_reshape.12
  145.0 1.5 pad_maximum_fusion
  146.5 2.0 %gather_fusion.1 = bf16[4,2,64,2048]{3,2,1,0:T(8,128)(2,1)} fusion(bf16[4,2,64,2048]{3,2,1,0:T(8,128)(2,1)S(1)} %pad_maximum_fusion, s32[1024]{0:T(1024)S(1)} %pad_clamp_fusion), kind=kCustom, calls=%fused_computation.1 | custom fusion | bytes 4194320 | tf_op jit(solution)/shard_map/jit(_take)/gather | solution.py:159
  (287 shorter events, 32.4 us)
Async XLA Ops:
  2.3 2.0 %copy-start.11 = (f32[4,4,16]{2,1,0:T(4,128)}, f32[4,4,16]{2,1,0:T(4,128)S(1)}, u32[]{:S(2)}) copy-start(f32[4,4,16]{2,1,0:T(4,128)S(1)} %get-tuple-element.94) | copy-start | bytes 3076
  2.3 2.0 %copy-start.23 = (f32[4,4,16]{2,1,0:T(4,128)}, f32[4,4,16]{2,1,0:T(4,128)S(1)}, u32[]{:S(2)}) copy-start(f32[4,4,16]{2,1,0:T(4,128)S(1)} %get-tuple-element.88) | copy-start | bytes 3076
  2.3 2.5 %copy-start.13 = (f32[4,4,16]{2,1,0:T(4,128)}, f32[4,4,16]{2,1,0:T(4,128)S(1)}, u32[]{:S(2)}) copy-start(f32[4,4,16]{2,1,0:T(4,128)S(1)} %get-tuple-element.96) | copy-start | bytes 3076
  2.3 2.5 %copy-start.25 = (f32[4,4,16]{2,1,0:T(4,128)}, f32[4,4,16]{2,1,0:T(4,128)S(1)}, u32[]{:S(2)}) copy-start(f32[4,4,16]{2,1,0:T(4,128)S(1)} %get-tuple-element.90) | copy-start | bytes 3076
  2.3 3.0 %copy-start.15 = (f32[4,4,16]{2,1,0:T(4,128)}, f32[4,4,16]{2,1,0:T(4,128)S(1)}, u32[]{:S(2)}) copy-start(f32[4,4,16]{2,1,0:T(4,128)S(1)} %get-tuple-element.98) | copy-start | bytes 3076
  2.3 3.0 %copy-start.27 = (f32[4,4,16]{2,1,0:T(4,128)}, f32[4,4,16]{2,1,0:T(4,128)S(1)}, u32[]{:S(2)}) copy-start(f32[4,4,16]{2,1,0:T(4,128)S(1)} %get-tuple-element.92) | copy-start | bytes 3076
  7.8 24.5 %collective-permute-start.18 = (bf16[2,3,4,4,1,512]{5,4,3,2,1,0:T(2,128)(2,1)}, bf16[2,3,4,4,1,512]{5,4,3,2,1,0:T(2,128)(2,1)}, u32[]{:S(2)}, u32[]{:S(2)}) collective-permute-start(bf16[2,3,4,4,1,512]{5,4,3,2,1,0:T(2,128)(2,1)} %pad_maximum_fusion.21), channel_id=1, source_target_pairs={{0,1},{1,0},{2,3},{3,2},{4,5},{5,4},{6,7},{7,6},{8,9},{9,8},{10,11... | collective-permute-start | bytes 294920 | tf_op jit(solution)/shard_map/ppermute | solution.py:97
  13.2 1.6 %copy-start = (bf16[2,3,4,4,16,512]{5,4,3,2,1,0:T(8,128)(2,1)S(1)}, bf16[2,3,4,4,16,512]{5,4,3,2,1,0:T(8,128)(2,1)}, u32[]{:S(2)}) copy-start(bf16[2,3,4,4,16,512]{5,4,3,2,1,0:T(8,128)(2,1)} %param.5) | copy-start | bytes 4718596
  14.1 28.5 %collective-permute-start.12 = (bf16[2,3,4,1,16,512]{5,4,3,2,1,0:T(8,128)(2,1)}, bf16[2,3,4,1,16,512]{5,4,3,2,1,0:T(8,128)(2,1)}, u32[]{:S(2)}, u32[]{:S(2)}) collective-permute-start(bf16[2,3,4,1,16,512]{5,4,3,2,1,0:T(8,128)(2,1)} %pad_maximum_fusion.15), channel_id=1, source_target_pairs={{0,2},{2,4},{4,6},{6,8},{8,10},{10,12},{12,14},{14,16},{16,18},{18... | collective-permute-start | bytes 1179656 | tf_op jit(solution)/shard_map/ppermute | solution.py:95
  15.0 21.2 %collective-permute-start.6 = (bf16[2,3,4,4,1,512]{5,3,4,2,1,0:T(4,128)(2,1)S(1)}, bf16[2,3,4,4,1,512]{5,3,4,2,1,0:T(4,128)(2,1)}, u32[]{:S(2)}, u32[]{:S(2)}) collective-permute-start(bf16[2,3,4,4,1,512]{5,3,4,2,1,0:T(4,128)(2,1)S(1)} %copy.54), channel_id=1, source_target_pairs={{0,1},{1,0},{2,3},{3,2},{4,5},{5,4},{6,7},{7,6},{8,9},{9,8},{10,11... | collective-permute-start | bytes 294920 | tf_op jit(solution)/shard_map/ppermute | solution.py:96
  15.8 30.1 %collective-permute-start = (bf16[2,3,4,1,16,512]{5,4,3,2,1,0:T(8,128)(2,1)}, bf16[2,3,4,1,16,512]{5,4,3,2,1,0:T(8,128)(2,1)}, u32[]{:S(2)}, u32[]{:S(2)}) collective-permute-start(bf16[2,3,4,1,16,512]{5,4,3,2,1,0:T(8,128)(2,1)} %slice.143), channel_id=1, source_target_pairs={{0,30},{2,0},{4,2},{6,4},{8,6},{10,8},{12,10},{14,12},{16,14},{18,... | collective-permute-start | bytes 1179656 | tf_op jit(solution)/shard_map/ppermute | solution.py:94
  23.0 2.8 %copy-start.9 = (bf16[1,3,4,4,16,512]{5,4,3,2,1,0:T(8,128)(2,1)S(1)}, bf16[1,3,4,4,16,512]{5,4,3,2,1,0:T(8,128)(2,1)}, u32[]{:S(2)}) copy-start(bf16[1,3,4,4,16,512]{5,4,3,2,1,0:T(8,128)(2,1)} %get-tuple-element.26) | copy-start | bytes 2359300
  23.0 4.6 %copy-start.10 = (bf16[2,64,2048]{2,1,0:T(8,128)(2,1)S(1)}, bf16[2,64,2048]{2,1,0:T(8,128)(2,1)}, u32[]{:S(2)}) copy-start(bf16[2,64,2048]{2,1,0:T(8,128)(2,1)} %param.9) | copy-start | bytes 1572868
  25.8 2.2 %copy-start.53 = (s32[4]{0:T(128)S(1)}, s32[4]{0:T(128)}, u32[]{:S(2)}) copy-start(s32[4]{0:T(128)} %param.8) | copy-start | bytes 52
  30.1 2.2 %copy-start.54 = (s32[4]{0:T(128)S(1)}, s32[4]{0:T(128)}, u32[]{:S(2)}) copy-start(s32[4]{0:T(128)} %param.7) | copy-start | bytes 52
  30.1 2.2 %copy-start.2 = (bf16[1,3,4,4,16,512]{5,4,3,2,1,0:T(8,128)(2,1)S(1)}, bf16[1,3,4,4,16,512]{5,4,3,2,1,0:T(8,128)(2,1)}, u32[]{:S(2)}) copy-start(bf16[1,3,4,4,16,512]{5,4,3,2,1,0:T(8,128)(2,1)} %copy-done.1) | copy-start | bytes 2359300
  30.1 2.3 %copy-start.4 = (bf16[1,3,4,4,16,512]{5,4,3,2,1,0:T(8,128)(2,1)S(1)}, bf16[1,3,4,4,16,512]{5,4,3,2,1,0:T(8,128)(2,1)}, u32[]{:S(2)}) copy-start(bf16[1,3,4,4,16,512]{5,4,3,2,1,0:T(8,128)(2,1)} %copy-done.3) | copy-start | bytes 2359300
  36.1 16.5 %collective-permute-start.19 = (f32[2,2,2,2,1,2,16,512]{7,6,0,5,4,3,2,1:T(8,128)S(1)}, f32[2,2,2,2,1,2,16,512]{7,6,0,5,4,3,2,1:T(8,128)S(1)}, u32[]{:S(2)}, u32[]{:S(2)}) collective-permute-start(f32[2,2,2,2,1,2,16,512]{7,6,0,5,4,3,2,1:T(8,128)S(1)} %constant_dynamic-slice_fusion.4), channel_id=1, source_target_pairs={{0,2},{1,3},{2,0},{3,1},{4,6},{5,7},{6,4},{7,5},{8,10},{9,11},{10,... | collective-permute-start | bytes 3145736 | tf_op jit(solution)/shard_map/ppermute | solution.py:67
  42.1 12.3 %collective-permute-start.7 = (f32[2,2,2,2,1,2,16,512]{7,6,0,5,4,3,2,1:T(8,128)S(1)}, f32[2,2,2,2,1,2,16,512]{7,6,0,5,4,3,2,1:T(8,128)S(1)}, u32[]{:S(2)}, u32[]{:S(2)}) collective-permute-start(f32[2,2,2,2,1,2,16,512]{7,6,0,5,4,3,2,1:T(8,128)S(1)} %constant_dynamic-slice_fusion.14), channel_id=1, source_target_pairs={{0,2},{1,3},{2,0},{3,1},{4,6},{5,7},{6,4},{7,5},{8,10},{9,11},{10,... | collective-permute-start | bytes 3145736 | tf_op jit(solution)/shard_map/ppermute | solution.py:67
  45.6 2.4 %copy-start.30 = (f32[4,4,16]{2,1,0:T(4,128)S(1)}, f32[4,4,16]{2,1,0:T(4,128)}, u32[]{:S(2)}) copy-start(f32[4,4,16]{2,1,0:T(4,128)} %copy-done.29) | copy-start | bytes 3076
  45.6 2.4 %copy-start.32 = (f32[4,4,16]{2,1,0:T(4,128)S(1)}, f32[4,4,16]{2,1,0:T(4,128)}, u32[]{:S(2)}) copy-start(f32[4,4,16]{2,1,0:T(4,128)} %copy-done.31) | copy-start | bytes 3076
  45.6 2.4 %copy-start.34 = (f32[4,4,16]{2,1,0:T(4,128)S(1)}, f32[4,4,16]{2,1,0:T(4,128)}, u32[]{:S(2)}) copy-start(f32[4,4,16]{2,1,0:T(4,128)} %copy-done.33) | copy-start | bytes 3076
  45.7 2.4 %copy-start.50 = (f32[4,4,16]{2,1,0:T(4,128)S(1)}, f32[4,4,16]{2,1,0:T(4,128)}, u32[]{:S(2)}) copy-start(f32[4,4,16]{2,1,0:T(4,128)} %get-tuple-element.69) | copy-start | bytes 3076
  45.7 2.4 %copy-start.51 = (f32[4,4,16]{2,1,0:T(4,128)S(1)}, f32[4,4,16]{2,1,0:T(4,128)}, u32[]{:S(2)}) copy-start(f32[4,4,16]{2,1,0:T(4,128)} %get-tuple-element.71) | copy-start | bytes 3076
  45.7 2.4 %copy-start.52 = (f32[4,4,16]{2,1,0:T(4,128)S(1)}, f32[4,4,16]{2,1,0:T(4,128)}, u32[]{:S(2)}) copy-start(f32[4,4,16]{2,1,0:T(4,128)} %get-tuple-element.73) | copy-start | bytes 3076
  45.7 9.1 %collective-permute-start.13 = (f32[2,2,2,2,1,2,16,512]{7,6,5,4,3,2,1,0:T(8,128)S(1)}, f32[2,2,2,2,1,2,16,512]{7,6,5,4,3,2,1,0:T(8,128)S(1)}, u32[]{:S(2)}, u32[]{:S(2)}) collective-permute-start(f32[2,2,2,2,1,2,16,512]{7,6,5,4,3,2,1,0:T(8,128)S(1)} %constant_dynamic-slice_fusion.9), channel_id=1, source_target_pairs={{0,2},{1,3},{2,0},{3,1},{4,6},{5,7},{6,4},{7,5},{8,10},{9,11},{10,... | collective-permute-start | bytes 3145736 | tf_op jit(solution)/shard_map/ppermute | solution.py:67
  52.3 3.2 %collective-permute-start.1 = (f32[2,2,2,2,1,2,16,512]{7,6,5,4,3,2,1,0:T(8,128)S(1)}, f32[2,2,2,2,1,2,16,512]{7,6,5,4,3,2,1,0:T(8,128)S(1)}, u32[]{:S(2)}, u32[]{:S(2)}) collective-permute-start(f32[2,2,2,2,1,2,16,512]{7,6,5,4,3,2,1,0:T(8,128)S(1)} %constant_dynamic-slice_fusion.19), channel_id=1, source_target_pairs={{0,2},{1,3},{2,0},{3,1},{4,6},{5,7},{6,4},{7,5},{8,10},{9,11},{10,... | collective-permute-start | bytes 3145736 | tf_op jit(solution)/shard_map/ppermute | solution.py:67
  52.8 14.9 %collective-permute-start.20 = (f32[2,2,2,2,1,1,16,512]{7,6,0,5,4,3,2,1:T(8,128)S(1)}, f32[2,2,2,2,1,1,16,512]{7,6,0,5,4,3,2,1:T(8,128)S(1)}, u32[]{:S(2)}, u32[]{:S(2)}) collective-permute-start(f32[2,2,2,2,1,1,16,512]{7,6,0,5,4,3,2,1:T(8,128)S(1)} %constant_dynamic-slice_fusion.3), channel_id=1, source_target_pairs={{0,1},{1,0},{2,3},{3,2},{4,5},{5,4},{6,7},{7,6},{8,9},{9,8},{10,11... | collective-permute-start | bytes 1572872 | tf_op jit(solution)/shard_map/ppermute | solution.py:67
  54.7 14.0 %collective-permute-start.8 = (f32[2,2,2,1,1,2,16,512]{7,6,0,5,4,3,2,1:T(8,128)S(1)}, f32[2,2,2,1,1,2,16,512]{7,6,0,5,4,3,2,1:T(8,128)S(1)}, u32[]{:S(2)}, u32[]{:S(2)}) collective-permute-start(f32[2,2,2,1,1,2,16,512]{7,6,0,5,4,3,2,1:T(8,128)S(1)} %constant_dynamic-slice_fusion.13), channel_id=1, source_target_pairs={{0,4},{1,5},{2,6},{3,7},{4,0},{5,1},{6,2},{7,3},{8,12},{9,13},{10,... | collective-permute-start | bytes 1572872 | tf_op jit(solution)/shard_map/ppermute | solution.py:67
  55.1 21.9 %collective-permute-start.14 = (f32[2,2,1,2,1,2,16,512]{7,6,5,4,3,2,1,0:T(8,128)S(1)}, f32[2,2,1,2,1,2,16,512]{7,6,5,4,3,2,1,0:T(8,128)S(1)}, u32[]{:S(2)}, u32[]{:S(2)}) collective-permute-start(f32[2,2,1,2,1,2,16,512]{7,6,5,4,3,2,1,0:T(8,128)S(1)} %constant_dynamic-slice_fusion.8), channel_id=1, source_target_pairs={{0,8},{1,9},{2,10},{3,11},{4,12},{5,13},{6,14},{7,15},{8,0},{9,1},... | collective-permute-start | bytes 1572872 | tf_op jit(solution)/shard_map/ppermute | solution.py:67
  55.8 23.4 %collective-permute-start.2 = (f32[2,2,2,2,1,1,16,512]{7,6,5,4,3,2,1,0:T(8,128)S(1)}, f32[2,2,2,2,1,1,16,512]{7,6,5,4,3,2,1,0:T(8,128)S(1)}, u32[]{:S(2)}, u32[]{:S(2)}) collective-permute-start(f32[2,2,2,2,1,1,16,512]{7,6,5,4,3,2,1,0:T(8,128)S(1)} %constant_dynamic-slice_fusion.18), channel_id=1, source_target_pairs={{0,1},{1,0},{2,3},{3,2},{4,5},{5,4},{6,7},{7,6},{8,9},{9,8},{10,11... | collective-permute-start | bytes 1572872 | tf_op jit(solution)/shard_map/ppermute | solution.py:67
  67.8 7.1 %collective-permute-start.21 = (f32[2,2,2,1,1,1,16,512]{7,6,0,5,4,3,2,1:T(8,128)S(1)}, f32[2,2,2,1,1,1,16,512]{7,6,0,5,4,3,2,1:T(8,128)S(1)}, u32[]{:S(2)}, u32[]{:S(2)}) collective-permute-start(f32[2,2,2,1,1,1,16,512]{7,6,0,5,4,3,2,1:T(8,128)S(1)} %constant_dynamic-slice_fusion.2), channel_id=1, source_target_pairs={{0,4},{1,5},{2,6},{3,7},{4,0},{5,1},{6,2},{7,3},{8,12},{9,13},{10,... | collective-permute-start | bytes 786440 | tf_op jit(solution)/shard_map/ppermute | solution.py:67
  68.8 8.1 %collective-permute-start.9 = (f32[2,2,1,1,1,2,16,512]{7,6,0,5,4,3,2,1:T(8,128)S(1)}, f32[2,2,1,1,1,2,16,512]{7,6,0,5,4,3,2,1:T(8,128)S(1)}, u32[]{:S(2)}, u32[]{:S(2)}) collective-permute-start(f32[2,2,1,1,1,2,16,512]{7,6,0,5,4,3,2,1:T(8,128)S(1)} %constant_dynamic-slice_fusion.12), channel_id=1, source_target_pairs={{0,8},{1,9},{2,10},{3,11},{4,12},{5,13},{6,14},{7,15},{8,0},{9,1},... | collective-permute-start | bytes 786440 | tf_op jit(solution)/shard_map/ppermute | solution.py:67
  75.0 5.1 %collective-permute-start.22 = (f32[2,2,1,1,1,1,16,512]{7,6,0,5,4,3,2,1:T(8,128)S(1)}, f32[2,2,1,1,1,1,16,512]{7,6,0,5,4,3,2,1:T(8,128)S(1)}, u32[]{:S(2)}, u32[]{:S(2)}) collective-permute-start(f32[2,2,1,1,1,1,16,512]{7,6,0,5,4,3,2,1:T(8,128)S(1)} %constant_dynamic-slice_fusion.1), channel_id=1, source_target_pairs={{0,8},{1,9},{2,10},{3,11},{4,12},{5,13},{6,14},{7,15},{8,0},{9,1},... | collective-permute-start | bytes 393224 | tf_op jit(solution)/shard_map/ppermute | solution.py:67
  76.9 6.4 %collective-permute-start.10 = (f32[2,2,1,1,1,1,16,512]{7,6,0,5,4,3,2,1:T(8,128)S(1)}, f32[2,2,1,1,1,1,16,512]{7,6,0,5,4,3,2,1:T(8,128)S(1)}, u32[]{:S(2)}, u32[]{:S(2)}) collective-permute-start(f32[2,2,1,1,1,1,16,512]{7,6,0,5,4,3,2,1:T(8,128)S(1)} %constant_dynamic-slice_fusion.11), channel_id=1, source_target_pairs={{0,1},{1,0},{2,3},{3,2},{4,5},{5,4},{6,7},{7,6},{8,9},{9,8},{10,11... | collective-permute-start | bytes 393224 | tf_op jit(solution)/shard_map/ppermute | solution.py:67
  77.2 18.2 %collective-permute-start.15 = (f32[2,2,1,2,1,1,16,512]{7,6,5,4,3,2,1,0:T(8,128)S(1)}, f32[2,2,1,2,1,1,16,512]{7,6,5,4,3,2,1,0:T(8,128)S(1)}, u32[]{:S(2)}, u32[]{:S(2)}) collective-permute-start(f32[2,2,1,2,1,1,16,512]{7,6,5,4,3,2,1,0:T(8,128)S(1)} %constant_dynamic-slice_fusion.7), channel_id=1, source_target_pairs={{0,1},{1,0},{2,3},{3,2},{4,5},{5,4},{6,7},{7,6},{8,9},{9,8},{10,11... | collective-permute-start | bytes 786440 | tf_op jit(solution)/shard_map/ppermute | solution.py:67
  79.4 17.0 %collective-permute-start.3 = (f32[2,2,2,1,1,1,16,512]{7,6,5,4,3,2,1,0:T(8,128)S(1)}, f32[2,2,2,1,1,1,16,512]{7,6,5,4,3,2,1,0:T(8,128)S(1)}, u32[]{:S(2)}, u32[]{:S(2)}) collective-permute-start(f32[2,2,2,1,1,1,16,512]{7,6,5,4,3,2,1,0:T(8,128)S(1)} %constant_dynamic-slice_fusion.17), channel_id=1, source_target_pairs={{0,4},{1,5},{2,6},{3,7},{4,0},{5,1},{6,2},{7,3},{8,12},{9,13},{10,... | collective-permute-start | bytes 786440 | tf_op jit(solution)/shard_map/ppermute | solution.py:67
  80.1 6.7 %collective-permute-start.23 = (f32[2,1,1,1,1,1,16,512]{7,6,0,5,4,3,2,1:T(8,128)S(1)}, f32[2,1,1,1,1,1,16,512]{7,6,0,5,4,3,2,1:T(8,128)S(1)}, u32[]{:S(2)}, u32[]{:S(2)}) collective-permute-start(f32[2,1,1,1,1,1,16,512]{7,6,0,5,4,3,2,1:T(8,128)S(1)} %constant_dynamic-slice_fusion), channel_id=1, source_target_pairs={{0,16},{1,17},{2,18},{3,19},{4,20},{5,21},{6,22},{7,23},{8,24},{9,... | collective-permute-start | bytes 196616 | tf_op jit(solution)/shard_map/ppermute | solution.py:67
  83.4 6.0 %collective-permute-start.11 = (f32[2,1,1,1,1,1,16,512]{7,6,0,5,4,3,2,1:T(8,128)S(1)}, f32[2,1,1,1,1,1,16,512]{7,6,0,5,4,3,2,1:T(8,128)S(1)}, u32[]{:S(2)}, u32[]{:S(2)}) collective-permute-start(f32[2,1,1,1,1,1,16,512]{7,6,0,5,4,3,2,1:T(8,128)S(1)} %constant_dynamic-slice_fusion.10), channel_id=1, source_target_pairs={{0,16},{1,17},{2,18},{3,19},{4,20},{5,21},{6,22},{7,23},{8,24},{9,... | collective-permute-start | bytes 196616 | tf_op jit(solution)/shard_map/ppermute | solution.py:67
  86.9 4.9 %collective-permute-start.40 = (bf16[2,1,1,1,1,1,16,512]{7,6,5,4,3,2,1,0:T(8,128)(2,1)S(1)}, bf16[2,1,1,1,1,1,16,512]{7,6,5,4,3,2,1,0:T(8,128)(2,1)S(1)}, u32[]{:S(2)}, u32[]{:S(2)}) collective-permute-start(bf16[2,1,1,1,1,1,16,512]{7,6,5,4,3,2,1,0:T(8,128)(2,1)S(1)} %get-tuple-element.66), channel_id=1, source_target_pairs={{0,16},{1,17},{2,18},{3,19},{4,20},{5,21},{6,22},{7,23},{8,24},{9,... | collective-permute-start | bytes 98312 | tf_op jit(solution)/shard_map/ppermute | solution.py:76
  89.4 4.9 %collective-permute-start.30 = (bf16[2,1,1,1,1,1,16,512]{7,6,0,5,4,3,2,1:T(8,128)(2,1)S(1)}, bf16[2,1,1,1,1,1,16,512]{7,6,0,5,4,3,2,1:T(8,128)(2,1)S(1)}, u32[]{:S(2)}, u32[]{:S(2)}) collective-permute-start(bf16[2,1,1,1,1,1,16,512]{7,6,0,5,4,3,2,1:T(8,128)(2,1)S(1)} %get-tuple-element.62), channel_id=1, source_target_pairs={{0,16},{1,17},{2,18},{3,19},{4,20},{5,21},{6,22},{7,23},{8,24},{9,... | collective-permute-start | bytes 98312 | tf_op jit(solution)/shard_map/ppermute | solution.py:76
  91.8 5.0 %collective-permute-start.41 = (bf16[2,2,1,1,1,1,16,512]{7,6,5,4,3,2,1,0:T(8,128)(2,1)S(1)}, bf16[2,2,1,1,1,1,16,512]{7,6,5,4,3,2,1,0:T(8,128)(2,1)S(1)}, u32[]{:S(2)}, u32[]{:S(2)}) collective-permute-start(bf16[2,2,1,1,1,1,16,512]{7,6,5,4,3,2,1,0:T(8,128)(2,1)S(1)} %pad_maximum_fusion.29), channel_id=1, source_target_pairs={{0,8},{1,9},{2,10},{3,11},{4,12},{5,13},{6,14},{7,15},{8,0},{9,1},... | collective-permute-start | bytes 196616 | tf_op jit(solution)/shard_map/ppermute | solution.py:76
  94.3 4.3 %collective-permute-start.31 = (bf16[2,2,1,1,1,1,16,512]{7,6,0,5,4,3,2,1:T(8,128)(2,1)S(1)}, bf16[2,2,1,1,1,1,16,512]{7,6,0,5,4,3,2,1:T(8,128)(2,1)S(1)}, u32[]{:S(2)}, u32[]{:S(2)}) collective-permute-start(bf16[2,2,1,1,1,1,16,512]{7,6,0,5,4,3,2,1:T(8,128)(2,1)S(1)} %pad_maximum_fusion.27), channel_id=1, source_target_pairs={{0,1},{1,0},{2,3},{3,2},{4,5},{5,4},{6,7},{7,6},{8,9},{9,8},{10,11... | collective-permute-start | bytes 196616 | tf_op jit(solution)/shard_map/ppermute | solution.py:76
  95.5 5.0 %collective-permute-start.16 = (f32[2,2,1,1,1,1,16,512]{7,6,5,4,3,2,1,0:T(8,128)S(1)}, f32[2,2,1,1,1,1,16,512]{7,6,5,4,3,2,1,0:T(8,128)S(1)}, u32[]{:S(2)}, u32[]{:S(2)}) collective-permute-start(f32[2,2,1,1,1,1,16,512]{7,6,5,4,3,2,1,0:T(8,128)S(1)} %constant_dynamic-slice_fusion.6), channel_id=1, source_target_pairs={{0,4},{1,5},{2,6},{3,7},{4,0},{5,1},{6,2},{7,3},{8,12},{9,13},{10,... | collective-permute-start | bytes 393224 | tf_op jit(solution)/shard_map/ppermute | solution.py:67
  96.4 6.3 %collective-permute-start.4 = (f32[2,2,1,1,1,1,16,512]{7,6,5,4,3,2,1,0:T(8,128)S(1)}, f32[2,2,1,1,1,1,16,512]{7,6,5,4,3,2,1,0:T(8,128)S(1)}, u32[]{:S(2)}, u32[]{:S(2)}) collective-permute-start(f32[2,2,1,1,1,1,16,512]{7,6,5,4,3,2,1,0:T(8,128)S(1)} %constant_dynamic-slice_fusion.16), channel_id=1, source_target_pairs={{0,8},{1,9},{2,10},{3,11},{4,12},{5,13},{6,14},{7,15},{8,0},{9,1},... | collective-permute-start | bytes 393224 | tf_op jit(solution)/shard_map/ppermute | solution.py:67
  96.9 6.8 %collective-permute-start.42 = (bf16[2,2,2,1,1,1,16,512]{7,6,5,4,3,2,1,0:T(8,128)(2,1)S(1)}, bf16[2,2,2,1,1,1,16,512]{7,6,5,4,3,2,1,0:T(8,128)(2,1)S(1)}, u32[]{:S(2)}, u32[]{:S(2)}) collective-permute-start(bf16[2,2,2,1,1,1,16,512]{7,6,5,4,3,2,1,0:T(8,128)(2,1)S(1)} %pad_maximum_fusion.25), channel_id=1, source_target_pairs={{0,4},{1,5},{2,6},{3,7},{4,0},{5,1},{6,2},{7,3},{8,12},{9,13},{10,... | collective-permute-start | bytes 393224 | tf_op jit(solution)/shard_map/ppermute | solution.py:76
  98.7 6.1 %collective-permute-start.32 = (bf16[2,2,1,1,1,2,16,512]{7,6,0,5,4,3,2,1:T(8,128)(2,1)S(1)}, bf16[2,2,1,1,1,2,16,512]{7,6,0,5,4,3,2,1:T(8,128)(2,1)S(1)}, u32[]{:S(2)}, u32[]{:S(2)}) collective-permute-start(bf16[2,2,1,1,1,2,16,512]{7,6,0,5,4,3,2,1:T(8,128)(2,1)S(1)} %pad_maximum_fusion.23), channel_id=1, source_target_pairs={{0,8},{1,9},{2,10},{3,11},{4,12},{5,13},{6,14},{7,15},{8,0},{9,1},... | collective-permute-start | bytes 393224 | tf_op jit(solution)/shard_map/ppermute | solution.py:76
  100.5 5.8 %collective-permute-start.17 = (f32[2,1,1,1,1,1,16,512]{7,6,5,4,3,2,1,0:T(8,128)S(1)}, f32[2,1,1,1,1,1,16,512]{7,6,5,4,3,2,1,0:T(8,128)S(1)}, u32[]{:S(2)}, u32[]{:S(2)}) collective-permute-start(f32[2,1,1,1,1,1,16,512]{7,6,5,4,3,2,1,0:T(8,128)S(1)} %constant_dynamic-slice_fusion.5), channel_id=1, source_target_pairs={{0,16},{1,17},{2,18},{3,19},{4,20},{5,21},{6,22},{7,23},{8,24},{9,... | collective-permute-start | bytes 196616 | tf_op jit(solution)/shard_map/ppermute | solution.py:67
  102.8 5.6 %collective-permute-start.5 = (f32[2,1,1,1,1,1,16,512]{7,6,5,4,3,2,1,0:T(8,128)S(1)}, f32[2,1,1,1,1,1,16,512]{7,6,5,4,3,2,1,0:T(8,128)S(1)}, u32[]{:S(2)}, u32[]{:S(2)}) collective-permute-start(f32[2,1,1,1,1,1,16,512]{7,6,5,4,3,2,1,0:T(8,128)S(1)} %constant_dynamic-slice_fusion.15), channel_id=1, source_target_pairs={{0,16},{1,17},{2,18},{3,19},{4,20},{5,21},{6,22},{7,23},{8,24},{9,... | collective-permute-start | bytes 196616 | tf_op jit(solution)/shard_map/ppermute | solution.py:67
  103.7 17.1 %collective-permute-start.43 = (bf16[2,2,2,2,1,1,16,512]{7,6,5,4,3,2,1,0:T(8,128)(2,1)S(1)}, bf16[2,2,2,2,1,1,16,512]{7,6,5,4,3,2,1,0:T(8,128)(2,1)S(1)}, u32[]{:S(2)}, u32[]{:S(2)}) collective-permute-start(bf16[2,2,2,2,1,1,16,512]{7,6,5,4,3,2,1,0:T(8,128)(2,1)S(1)} %pad_maximum_fusion.20), channel_id=1, source_target_pairs={{0,1},{1,0},{2,3},{3,2},{4,5},{5,4},{6,7},{7,6},{8,9},{9,8},{10,11... | collective-permute-start | bytes 786440 | tf_op jit(solution)/shard_map/ppermute | solution.py:76
  104.9 16.1 %collective-permute-start.33 = (bf16[2,2,2,1,1,2,16,512]{7,6,0,5,4,3,2,1:T(8,128)(2,1)S(1)}, bf16[2,2,2,1,1,2,16,512]{7,6,0,5,4,3,2,1:T(8,128)(2,1)S(1)}, u32[]{:S(2)}, u32[]{:S(2)}) collective-permute-start(bf16[2,2,2,1,1,2,16,512]{7,6,0,5,4,3,2,1:T(8,128)(2,1)S(1)} %pad_maximum_fusion.18), channel_id=1, source_target_pairs={{0,4},{1,5},{2,6},{3,7},{4,0},{5,1},{6,2},{7,3},{8,12},{9,13},{10,... | collective-permute-start | bytes 786440 | tf_op jit(solution)/shard_map/ppermute | solution.py:76
  106.3 5.1 %collective-permute-start.35 = (bf16[2,1,1,1,1,1,16,512]{7,6,5,4,3,2,1,0:T(8,128)(2,1)S(1)}, bf16[2,1,1,1,1,1,16,512]{7,6,5,4,3,2,1,0:T(8,128)(2,1)S(1)}, u32[]{:S(2)}, u32[]{:S(2)}) collective-permute-start(bf16[2,1,1,1,1,1,16,512]{7,6,5,4,3,2,1,0:T(8,128)(2,1)S(1)} %get-tuple-element.64), channel_id=1, source_target_pairs={{0,16},{1,17},{2,18},{3,19},{4,20},{5,21},{6,22},{7,23},{8,24},{9,... | collective-permute-start | bytes 98312 | tf_op jit(solution)/shard_map/ppermute | solution.py:76
  109.0 16.6 %collective-permute-start.24 = (f32[4,2,1,1,1,1,1,16,512]{8,7,1,0,6,5,4,3,2:T(8,128)S(1)}, f32[4,2,1,1,1,1,1,16,512]{8,7,1,0,6,5,4,3,2:T(8,128)S(1)}, u32[]{:S(2)}, u32[]{:S(2)}) collective-permute-start(f32[4,2,1,1,1,1,1,16,512]{8,7,1,0,6,5,4,3,2:T(8,128)S(1)} %bitcast.554), channel_id=1, source_target_pairs={{0,1},{1,0},{2,3},{3,2},{4,5},{5,4},{6,7},{7,6},{8,9},{9,8},{10,11... | collective-permute-start | bytes 786440 | tf_op jit(solution)/shard_map/ppermute | solution.py:76
  110.3 5.2 %collective-permute-start.25 = (bf16[2,1,1,1,1,1,16,512]{7,6,5,4,3,2,1,0:T(8,128)(2,1)S(1)}, bf16[2,1,1,1,1,1,16,512]{7,6,5,4,3,2,1,0:T(8,128)(2,1)S(1)}, u32[]{:S(2)}, u32[]{:S(2)}) collective-permute-start(bf16[2,1,1,1,1,1,16,512]{7,6,5,4,3,2,1,0:T(8,128)(2,1)S(1)} %get-tuple-element.60), channel_id=1, source_target_pairs={{0,16},{1,17},{2,18},{3,19},{4,20},{5,21},{6,22},{7,23},{8,24},{9,... | collective-permute-start | bytes 98312 | tf_op jit(solution)/shard_map/ppermute | solution.py:76
  111.5 5.0 %collective-permute-start.36 = (bf16[2,2,1,1,1,1,16,512]{7,6,5,4,3,2,1,0:T(8,128)(2,1)S(1)}, bf16[2,2,1,1,1,1,16,512]{7,6,5,4,3,2,1,0:T(8,128)(2,1)S(1)}, u32[]{:S(2)}, u32[]{:S(2)}) collective-permute-start(bf16[2,2,1,1,1,1,16,512]{7,6,5,4,3,2,1,0:T(8,128)(2,1)S(1)} %pad_maximum_fusion.28), channel_id=1, source_target_pairs={{0,4},{1,5},{2,6},{3,7},{4,0},{5,1},{6,2},{7,3},{8,12},{9,13},{10,... | collective-permute-start | bytes 196616 | tf_op jit(solution)/shard_map/ppermute | solution.py:76
  115.5 4.3 %collective-permute-start.26 = (bf16[2,2,1,1,1,1,16,512]{7,6,5,4,3,2,1,0:T(8,128)(2,1)S(1)}, bf16[2,2,1,1,1,1,16,512]{7,6,5,4,3,2,1,0:T(8,128)(2,1)S(1)}, u32[]{:S(2)}, u32[]{:S(2)}) collective-permute-start(bf16[2,2,1,1,1,1,16,512]{7,6,5,4,3,2,1,0:T(8,128)(2,1)S(1)} %pad_maximum_fusion.26), channel_id=1, source_target_pairs={{0,8},{1,9},{2,10},{3,11},{4,12},{5,13},{6,14},{7,15},{8,0},{9,1},... | collective-permute-start | bytes 196616 | tf_op jit(solution)/shard_map/ppermute | solution.py:76
  116.5 5.1 %collective-permute-start.37 = (bf16[2,2,1,2,1,1,16,512]{7,6,5,4,3,2,1,0:T(8,128)(2,1)S(1)}, bf16[2,2,1,2,1,1,16,512]{7,6,5,4,3,2,1,0:T(8,128)(2,1)S(1)}, u32[]{:S(2)}, u32[]{:S(2)}) collective-permute-start(bf16[2,2,1,2,1,1,16,512]{7,6,5,4,3,2,1,0:T(8,128)(2,1)S(1)} %pad_maximum_fusion.24), channel_id=1, source_target_pairs={{0,1},{1,0},{2,3},{3,2},{4,5},{5,4},{6,7},{7,6},{8,9},{9,8},{10,11... | collective-permute-start | bytes 393224 | tf_op jit(solution)/shard_map/ppermute | solution.py:76
  119.9 5.0 %collective-permute-start.27 = (bf16[2,2,2,1,1,1,16,512]{7,6,5,4,3,2,1,0:T(8,128)(2,1)S(1)}, bf16[2,2,2,1,1,1,16,512]{7,6,5,4,3,2,1,0:T(8,128)(2,1)S(1)}, u32[]{:S(2)}, u32[]{:S(2)}) collective-permute-start(bf16[2,2,2,1,1,1,16,512]{7,6,5,4,3,2,1,0:T(8,128)(2,1)S(1)} %pad_maximum_fusion.22), channel_id=1, source_target_pairs={{0,4},{1,5},{2,6},{3,7},{4,0},{5,1},{6,2},{7,3},{8,12},{9,13},{10,... | collective-permute-start | bytes 393224 | tf_op jit(solution)/shard_map/ppermute | solution.py:76
  120.9 11.4 %collective-permute-start.44 = (bf16[2,2,2,2,1,2,16,512]{7,6,5,4,3,2,1,0:T(8,128)(2,1)S(1)}, bf16[2,2,2,2,1,2,16,512]{7,6,5,4,3,2,1,0:T(8,128)(2,1)S(1)}, u32[]{:S(2)}, u32[]{:S(2)}) collective-permute-start(bf16[2,2,2,2,1,2,16,512]{7,6,5,4,3,2,1,0:T(8,128)(2,1)S(1)} %pad_maximum_fusion.14), channel_id=1, source_target_pairs={{0,2},{1,3},{2,0},{3,1},{4,6},{5,7},{6,4},{7,5},{8,10},{9,11},{10,... | collective-permute-start | bytes 1572872 | tf_op jit(solution)/shard_map/ppermute | solution.py:76
  121.1 13.1 %collective-permute-start.34 = (bf16[2,2,2,2,1,2,16,512]{7,6,0,5,4,3,2,1:T(8,128)(2,1)S(1)}, bf16[2,2,2,2,1,2,16,512]{7,6,0,5,4,3,2,1:T(8,128)(2,1)S(1)}, u32[]{:S(2)}, u32[]{:S(2)}) collective-permute-start(bf16[2,2,2,2,1,2,16,512]{7,6,0,5,4,3,2,1:T(8,128)(2,1)S(1)} %pad_maximum_fusion.12), channel_id=1, source_target_pairs={{0,2},{1,3},{2,0},{3,1},{4,6},{5,7},{6,4},{7,5},{8,10},{9,11},{10,... | collective-permute-start | bytes 1572872 | tf_op jit(solution)/shard_map/ppermute | solution.py:76
  121.7 8.3 %collective-permute-start.38 = (bf16[2,2,1,2,1,2,16,512]{7,6,5,4,3,2,1,0:T(8,128)(2,1)S(1)}, bf16[2,2,1,2,1,2,16,512]{7,6,5,4,3,2,1,0:T(8,128)(2,1)S(1)}, u32[]{:S(2)}, u32[]{:S(2)}) collective-permute-start(bf16[2,2,1,2,1,2,16,512]{7,6,5,4,3,2,1,0:T(8,128)(2,1)S(1)} %pad_maximum_fusion.19), channel_id=1, source_target_pairs={{0,8},{1,9},{2,10},{3,11},{4,12},{5,13},{6,14},{7,15},{8,0},{9,1},... | collective-permute-start | bytes 786440 | tf_op jit(solution)/shard_map/ppermute | solution.py:76
  125.0 6.4 %collective-permute-start.28 = (bf16[2,2,2,2,1,1,16,512]{7,6,5,4,3,2,1,0:T(8,128)(2,1)S(1)}, bf16[2,2,2,2,1,1,16,512]{7,6,5,4,3,2,1,0:T(8,128)(2,1)S(1)}, u32[]{:S(2)}, u32[]{:S(2)}) collective-permute-start(bf16[2,2,2,2,1,1,16,512]{7,6,5,4,3,2,1,0:T(8,128)(2,1)S(1)} %pad_maximum_fusion.17), channel_id=1, source_target_pairs={{0,1},{1,0},{2,3},{3,2},{4,5},{5,4},{6,7},{7,6},{8,9},{9,8},{10,11... | collective-permute-start | bytes 786440 | tf_op jit(solution)/shard_map/ppermute | solution.py:76
  130.9 7.9 %collective-permute-start.39 = (bf16[2,2,2,2,1,2,16,512]{7,6,5,4,3,2,1,0:T(8,128)(2,1)}, bf16[2,2,2,2,1,2,16,512]{7,6,5,4,3,2,1,0:T(8,128)(2,1)}, u32[]{:S(2)}, u32[]{:S(2)}) collective-permute-start(bf16[2,2,2,2,1,2,16,512]{7,6,5,4,3,2,1,0:T(8,128)(2,1)} %pad_maximum_fusion.13), channel_id=1, source_target_pairs={{0,2},{1,3},{2,0},{3,1},{4,6},{5,7},{6,4},{7,5},{8,10},{9,11},{10,... | collective-permute-start | bytes 1572872 | tf_op jit(solution)/shard_map/ppermute | solution.py:76
  132.3 9.6 %collective-permute-start.29 = (bf16[2,2,2,2,1,2,16,512]{7,6,5,4,3,2,1,0:T(8,128)(2,1)}, bf16[2,2,2,2,1,2,16,512]{7,6,5,4,3,2,1,0:T(8,128)(2,1)}, u32[]{:S(2)}, u32[]{:S(2)}) collective-permute-start(bf16[2,2,2,2,1,2,16,512]{7,6,5,4,3,2,1,0:T(8,128)(2,1)} %pad_maximum_fusion.11), channel_id=1, source_target_pairs={{0,2},{1,3},{2,0},{3,1},{4,6},{5,7},{6,4},{7,5},{8,10},{9,11},{10,... | collective-permute-start | bytes 1572872 | tf_op jit(solution)/shard_map/ppermute | solution.py:76
  (37 other events, 31.4 us)

commit v10 on v9

--- a/solution.py
+++ b/solution.py
@@ -156,7 +156,12 @@
             own.reshape([ndisp, 2] + [1] * nbits + [rows, nev]), gy_bits, nbits, count, 2
         )
         elem = grown.reshape(ndisp, 2, ny * rows, nev)
-        contracted = jnp.take(jnp.stack(products, 0), directions, axis=0, mode="clip")
+        pick = (directions[:, None] == jnp.arange(ndisp, dtype=directions.dtype)[None, :]).astype(
+            products[0].dtype
+        )
+        contracted = jnp.einsum(
+            "kd,dcrm->kcrm", pick, jnp.stack(products, 0), preferred_element_type=jnp.float32
+        ).astype(products[0].dtype)
         return (elem, contracted)
 
     return local

time: 149 us -> 165 us (1.11)
  local copies, waits for them, and re-layouts: 21.7 us -> 31.2 us
  matrix products: 15.8 us -> 23.5 us
    another operation x4, local copies, waits for them, and re-layouts: 3.89 us -> 12.8 us  [local(): jnp.stack(products, 0)]
    dot_general x0 -> x1, matrix products: none -> 6.2 us  [local(): jnp.einsum('kd,dcrm->kcrm', pick, jnp.stack(products, 0), preferred_eleme...]
    unnamed x111 -> x116, local copies, waits for them, and re-layouts: 4.34 us -> 6.88 us
    gather x1 -> x0, local copies, waits for them, and re-layouts: 2 us -> none  [local(): jnp.take(jnp.stack(products, 0), directions, axis=0, mode='clip')]
    another operation x13 -> x12, other arithmetic: 7.5 us -> 6.04 us
  transfers between devices with their start and end apart: 45 -> 45, of which waited for: 21 -> 21; matrix products, arithmetic and copies ran while one was open for 32% -> 33% of each run, Pallas kernels for 0% -> 0%
where the time goes in v10:
time: 165 us; the launch traced here: 164 us
  waiting for transfers between devices  46.7 us (28%)
  starting transfers between devices  34.6 us (21%)
  local copies, waits for them, and re-layouts  31.2 us (19%)
  other arithmetic  26.1 us (16%)
  matrix products  23.5 us (14%)
  between operations  2.16 us (1%)
    ppermute x20, waiting for transfers between devices, reduce_scatter(): buf = keep + lax.ppermute(send, ALL, xor_pairs(count, b))  30.1 us
    ppermute x21, waiting for transfers between devices, all_gather(): other = lax.ppermute(buf, ALL, xor_pairs(count, b))  16.6 us
    ppermute x21, starting transfers between devices, all_gather(): other = lax.ppermute(buf, ALL, xor_pairs(count, b))  15.6 us
    another operation x4, local copies, waits for them, and re-layouts, local(): jnp.stack(products, 0)  12.8 us
    ppermute x20, starting transfers between devices, reduce_scatter(): buf = keep + lax.ppermute(send, ALL, xor_pairs(count, b))  12.1 us
    dot_general x4, matrix products, local(): jnp.dot(left, field.reshape(2 * depth, nev), preferred_element_type=jnp.f...  7.12 us
    unnamed x116, local copies, waits for them, and re-layouts  6.88 us
    dot_general x1, matrix products, local(): jnp.einsum('kd,dcrm->kcrm', pick, jnp.stack(products, 0), preferred_eleme...  6.2 us
  transfers between devices with their start and end apart: 45, of which 21 were waited for; matrix products, arithmetic and copies ran while one was open for 33% of the time, Pallas kernels for 0%

profile of v10, /device:TPU:0, one launch (start us, length us, event | category | flops | bytes accessed | tf_op | source)
XLA Modules:
  0.0 164.3 jit_solution(5284973540589988320)
XLA Ops:
  0.6 1.0 slice_bitcast_fusion.19
  2.4 1.9 %convert_element_type.86 = f32[2,3,4,4,16,512]{5,4,3,2,1,0:T(8,128)S(1)} convert(bf16[2,3,4,4,16,512]{5,4,3,2,1,0:T(8,128)(2,1)} %param.5) | non-fusion elementwise | flops 786432 | bytes 4718592 | tf_op jit(solution)/shard_map/convert_element_type | solution.py:13
  6.9 1.0 pad_maximum_fusion.20
  7.8 3.0 %collective-permute-start.18 = (bf16[2,3,4,4,1,512]{5,4,3,2,1,0:T(2,128)(2,1)}, bf16[2,3,4,4,1,512]{5,4,3,2,1,0:T(2,128)(2,1)}, u32[]{:S(2)}, u32[]{:S(2)}) collective-permute-start(bf16[2,3,4,4,1,512]{5,4,3,2,1,0:T(2,128)(2,1)} %pad_maximum_fusion.20), channel_id=1, source_target_pairs={{0,1},{1,0},{2,3},{3,2},{4,5},{5,4},{6,7},{7,6},{8,9},{9,8},{10,11... | collective-permute-start | bytes 294920 | tf_op jit(solution)/shard_map/ppermute | solution.py:97
  15.8 4.0 %collective-permute-start = (bf16[2,3,4,1,16,512]{5,4,3,2,1,0:T(8,128)(2,1)}, bf16[2,3,4,1,16,512]{5,4,3,2,1,0:T(8,128)(2,1)}, u32[]{:S(2)}, u32[]{:S(2)}) collective-permute-start(bf16[2,3,4,1,16,512]{5,4,3,2,1,0:T(8,128)(2,1)} %slice.143), channel_id=1, source_target_pairs={{0,30},{2,0},{4,2},{6,4},{8,6},{10,8},{12,10},{14,12},{16,14},{18,... | collective-permute-start | bytes 1179656 | tf_op jit(solution)/shard_map/ppermute | solution.py:94
  19.8 1.3 fusion.46
  21.1 1.8 %slice.169 = bf16[2,3,4,4,15,512]{5,4,3,2,1,0:T(8,128)(2,1)} slice(bf16[2,3,4,4,16,512]{5,4,3,2,1,0:T(8,128)(2,1)S(1)} %copy-done), slice={[0:2], [0:3], [0:4], [0:4], [1:16], [0:512]} | slice | bytes 2949120 | tf_op jit(solution)/shard_map/slice | solution.py:99
  23.0 2.7 %convolution_convert_fusion.2 = bf16[512,768]{1,0:T(8,128)(2,1)} fusion(bf16[768,512]{1,0:T(8,128)(2,1)} %bitcast.561), kind=kOutput, calls=%fused_computation.23 | convolution fusion | flops 403308544 | bytes 1572864 | tf_op jit(solution)/shard_map/dot_general | solution.py:110
  25.7 1.8 %fusion.48 = (bf16[512,768]{1,0:T(8,128)(2,1)}, bf16[512,768]{1,0:T(8,128)(2,1)}) fusion(bf16[768,512]{1,0:T(8,128)(2,1)S(1)} %bitcast.560), kind=kOutput, calls=%fused_computation.264 | convolution fusion | flops 403701760 | bytes 2359296 | tf_op jit(solution)/shard_map/dot_general | solution.py:110
  28.9 1.1 pad_maximum_fusion.4
  30.0 2.2 %maximum_maximum_fusion = bf16[1024,1536]{1,0:T(8,128)(2,1)S(1)} fusion(bf16[512,768]{1,0:T(8,128)(2,1)} %convolution_convert_fusion.2, bf16[512,768]{1,0:T(8,128)(2,1)} %get-tuple-element.144, bf16[512,768]{1,0:T(8,128)(2,1)} %get-tuple-element.145), kind=kLoop, calls=%fused_computation.1 | loop fusion | flops 12582912 | bytes 5505024 | tf_op jit(solution)/shard_map/concatenate | solution.py:115
  32.3 1.7 %fusion.11 = bf16[2,3,4,4,16,512]{5,4,3,2,1,0:T(8,128)(2,1)S(1)} fusion(bf16[1,3,4,4,16,512]{5,4,3,2,1,0:T(8,128)(2,1)S(1)} %copy-done.2, bf16[1,3,4,4,16,512]{5,4,3,2,1,0:T(8,128)(2,1)S(1)} %copy-done.4, bf16[2,3,4,4,1,512]{5,4,3,2,1,0:T(2,128)(2,1)} %collective-permute-done.18), kind=kLoop, calls=%fused_computation.15 | loop fusion | flops 4718592 | bytes 3244032 | tf_op jit(solution)/shard_map/concatenate | solution.py:104
  34.1 1.8 %fusion = f32[2,2,2,2,2,2,16,512]{7,6,0,5,4,3,2,1:T(8,128)S(1)} fusion(bf16[1536,512,1,1,1,1,1,1]{1,0,2,7,6,5,4,3:T(8,128)(2,1)S(1)} %bitcast.548, bf16[2,2,2,2,2,2,16,1536]{7,6,5,4,3,2,1,0:T(8,128)(2,1)S(1)} %bitcast.543), kind=kOutput, calls=%fused_computation.3 | convolution fusion | flops 1610612736 | bytes 6815744 | tf_op jit(solution)/shard_map/dot_general | solution.py:143
  36.1 1.2 copy.43
  40.2 1.8 %fusion.2 = f32[2,2,2,2,2,2,16,512]{7,6,0,5,4,3,2,1:T(8,128)S(1)} fusion(bf16[1536,512,1,1,1,1,1,1]{1,0,2,7,6,5,4,3:T(8,128)(2,1)S(1)} %bitcast.550, bf16[2,2,2,2,2,2,16,1536]{7,6,5,4,3,2,1,0:T(8,128)(2,1)S(1)} %bitcast.544), kind=kOutput, calls=%fused_computation.5 | convolution fusion | flops 1610612736 | bytes 6815744 | tf_op jit(solution)/shard_map/dot_general | solution.py:143
  42.5 1.2 fusion.12
  43.7 1.8 %fusion.50 = f32[2,2,2,2,2,2,16,512]{7,6,5,4,3,2,1,0:T(8,128)S(1)} fusion(bf16[2,2,2,2,2,2,16,1536]{7,6,5,4,3,2,1,0:T(8,128)(2,1)S(1)} %bitcast.545, bf16[1536,512,1,1,1,1,1,1]{1,0,7,6,5,4,3,2:T(8,128)(2,1)S(1)} %bitcast.547), kind=kOutput, calls=%fused_computation.266 | convolution fusion | flops 1610612736 | bytes 6815744 | tf_op jit(solution)/shard_map/dot_general | solution.py:143
  45.9 0.9 slice-done
  46.7 1.2 maximum_convert_fusion
  50.4 1.8 %fusion.49 = f32[2,2,2,2,2,2,16,512]{7,6,5,4,3,2,1,0:T(8,128)S(1)} fusion(bf16[2,2,2,2,2,2,16,1536]{7,6,5,4,3,2,1,0:T(8,128)(2,1)S(1)} %bitcast.546, bf16[1536,512,1,1,1,1,1,1]{1,0,7,6,5,4,3,2:T(8,128)(2,1)S(1)} %bitcast.549), kind=kOutput, calls=%fused_computation.265 | convolution fusion | flops 1610612736 | bytes 6815744 | tf_op jit(solution)/shard_map/dot_general | solution.py:143
  52.8 1.6 collective-permute-start.20
  55.8 1.2 collective-permute-start.2
  57.0 10.7 %collective-permute-done.20 = f32[2,2,2,2,1,1,16,512]{7,6,0,5,4,3,2,1:T(8,128)S(1)} collective-permute-done((f32[2,2,2,2,1,1,16,512]{7,6,0,5,4,3,2,1:T(8,128)S(1)}, f32[2,2,2,2,1,1,16,512]{7,6,0,5,4,3,2,1:T(8,128)S(1)}, u32[]{:S(2)}, u32[]{:S(2)}) %collective-permute-start.20) | collective-permute-done | bytes 524320 | tf_op jit(solution)/shard_map/ppermute | solution.py:67
  68.8 6.1 %collective-permute-done.21 = f32[2,2,2,1,1,1,16,512]{7,6,0,5,4,3,2,1:T(8,128)S(1)} collective-permute-done((f32[2,2,2,1,1,1,16,512]{7,6,0,5,4,3,2,1:T(8,128)S(1)}, f32[2,2,2,1,1,1,16,512]{7,6,0,5,4,3,2,1:T(8,128)S(1)}, u32[]{:S(2)}, u32[]{:S(2)}) %collective-permute-start.21) | collective-permute-done | bytes 262176 | tf_op jit(solution)/shard_map/ppermute | solution.py:67
  75.1 1.8 %collective-permute-done.9 = f32[2,2,1,1,1,2,16,512]{7,6,0,5,4,3,2,1:T(8,128)S(1)} collective-permute-done((f32[2,2,1,1,1,2,16,512]{7,6,0,5,4,3,2,1:T(8,128)S(1)}, f32[2,2,1,1,1,2,16,512]{7,6,0,5,4,3,2,1:T(8,128)S(1)}, u32[]{:S(2)}, u32[]{:S(2)}) %collective-permute-start.9) | collective-permute-done | bytes 262176 | tf_op jit(solution)/shard_map/ppermute | solution.py:67
  77.1 2.1 %collective-permute-start.15 = (f32[2,2,1,2,1,1,16,512]{7,6,5,4,3,2,1,0:T(8,128)S(1)}, f32[2,2,1,2,1,1,16,512]{7,6,5,4,3,2,1,0:T(8,128)S(1)}, u32[]{:S(2)}, u32[]{:S(2)}) collective-permute-start(f32[2,2,1,2,1,1,16,512]{7,6,5,4,3,2,1,0:T(8,128)S(1)} %constant_dynamic-slice_fusion.7), channel_id=1, source_target_pairs={{0,1},{1,0},{2,3},{3,2},{4,5},{5,4},{6,7},{7,6},{8,9},{9,8},{10,11... | collective-permute-start | bytes 786440 | tf_op jit(solution)/shard_map/ppermute | solution.py:67
  80.1 0.9 collective-permute-start.23
  81.0 2.3 %collective-permute-done.10 = f32[2,2,1,1,1,1,16,512]{7,6,0,5,4,3,2,1:T(8,128)S(1)} collective-permute-done((f32[2,2,1,1,1,1,16,512]{7,6,0,5,4,3,2,1:T(8,128)S(1)}, f32[2,2,1,1,1,1,16,512]{7,6,0,5,4,3,2,1:T(8,128)S(1)}, u32[]{:S(2)}, u32[]{:S(2)}) %collective-permute-start.10) | collective-permute-done | bytes 131104 | tf_op jit(solution)/shard_map/ppermute | solution.py:67
  84.2 2.6 %collective-permute-done.23 = f32[2,1,1,1,1,1,16,512]{7,6,0,5,4,3,2,1:T(8,128)S(1)} collective-permute-done((f32[2,1,1,1,1,1,16,512]{7,6,0,5,4,3,2,1:T(8,128)S(1)}, f32[2,1,1,1,1,1,16,512]{7,6,0,5,4,3,2,1:T(8,128)S(1)}, u32[]{:S(2)}, u32[]{:S(2)}) %collective-permute-start.23) | collective-permute-done | bytes 65568 | tf_op jit(solution)/shard_map/ppermute | solution.py:67
  86.9 2.5 %collective-permute-done.11 = f32[2,1,1,1,1,1,16,512]{7,6,0,5,4,3,2,1:T(8,128)S(1)} collective-permute-done((f32[2,1,1,1,1,1,16,512]{7,6,0,5,4,3,2,1:T(8,128)S(1)}, f32[2,1,1,1,1,1,16,512]{7,6,0,5,4,3,2,1:T(8,128)S(1)}, u32[]{:S(2)}, u32[]{:S(2)}) %collective-permute-start.11) | collective-permute-done | bytes 65568 | tf_op jit(solution)/shard_map/ppermute | solution.py:67
  89.9 1.8 %collective-permute-done.40 = bf16[2,1,1,1,1,1,16,512]{7,6,5,4,3,2,1,0:T(8,128)(2,1)S(1)} collective-permute-done((bf16[2,1,1,1,1,1,16,512]{7,6,5,4,3,2,1,0:T(8,128)(2,1)S(1)}, bf16[2,1,1,1,1,1,16,512]{7,6,5,4,3,2,1,0:T(8,128)(2,1)S(1)}, u32[]{:S(2)}, u32[]{:S(2)}) %collective-permute-start.40) | collective-permute-done | bytes 32800 | tf_op jit(solution)/shard_map/ppermute | solution.py:76
  92.0 2.2 %collective-permute-done.30 = bf16[2,1,1,1,1,1,16,512]{7,6,0,5,4,3,2,1:T(8,128)(2,1)S(1)} collective-permute-done((bf16[2,1,1,1,1,1,16,512]{7,6,0,5,4,3,2,1:T(8,128)(2,1)S(1)}, bf16[2,1,1,1,1,1,16,512]{7,6,0,5,4,3,2,1:T(8,128)(2,1)S(1)}, u32[]{:S(2)}, u32[]{:S(2)}) %collective-permute-start.30) | collective-permute-done | bytes 32800 | tf_op jit(solution)/shard_map/ppermute | solution.py:76
  94.3 1.0 collective-permute-start.31
  95.4 0.9 collective-permute-start.16
  96.8 1.3 collective-permute-start.42
  98.7 1.2 collective-permute-start.32
  100.5 1.1 collective-permute-start.17
  101.6 1.1 collective-permute-done.4
  103.7 1.1 collective-permute-start.43
  105.2 1.0 collective-permute-done.17
  106.3 1.5 collective-permute-start.35
  109.0 1.3 collective-permute-start.24
  110.3 1.1 collective-permute-start.25
  111.4 1.2 collective-permute-start.36
  112.6 2.8 %collective-permute-done.25 = bf16[2,1,1,1,1,1,16,512]{7,6,5,4,3,2,1,0:T(8,128)(2,1)S(1)} collective-permute-done((bf16[2,1,1,1,1,1,16,512]{7,6,5,4,3,2,1,0:T(8,128)(2,1)S(1)}, bf16[2,1,1,1,1,1,16,512]{7,6,5,4,3,2,1,0:T(8,128)(2,1)S(1)}, u32[]{:S(2)}, u32[]{:S(2)}) %collective-permute-start.25) | collective-permute-done | bytes 32800 | tf_op jit(solution)/shard_map/ppermute | solution.py:76
  117.2 2.6 %collective-permute-done.26 = bf16[2,2,1,1,1,1,16,512]{7,6,5,4,3,2,1,0:T(8,128)(2,1)S(1)} collective-permute-done((bf16[2,2,1,1,1,1,16,512]{7,6,5,4,3,2,1,0:T(8,128)(2,1)S(1)}, bf16[2,2,1,1,1,1,16,512]{7,6,5,4,3,2,1,0:T(8,128)(2,1)S(1)}, u32[]{:S(2)}, u32[]{:S(2)}) %collective-permute-start.26) | collective-permute-done | bytes 65568 | tf_op jit(solution)/shard_map/ppermute | solution.py:76
  119.8 0.9 collective-permute-start.27
  121.7 1.1 collective-permute-start.38
  122.7 2.1 %collective-permute-done.27 = bf16[2,2,2,1,1,1,16,512]{7,6,5,4,3,2,1,0:T(8,128)(2,1)S(1)} collective-permute-done((bf16[2,2,2,1,1,1,16,512]{7,6,5,4,3,2,1,0:T(8,128)(2,1)S(1)}, bf16[2,2,2,1,1,1,16,512]{7,6,5,4,3,2,1,0:T(8,128)(2,1)S(1)}, u32[]{:S(2)}, u32[]{:S(2)}) %collective-permute-start.27) | collective-permute-done | bytes 131104 | tf_op jit(solution)/shard_map/ppermute | solution.py:76
  126.6 3.4 %collective-permute-done.38 = bf16[2,2,1,2,1,2,16,512]{7,6,5,4,3,2,1,0:T(8,128)(2,1)S(1)} collective-permute-done((bf16[2,2,1,2,1,2,16,512]{7,6,5,4,3,2,1,0:T(8,128)(2,1)S(1)}, bf16[2,2,1,2,1,2,16,512]{7,6,5,4,3,2,1,0:T(8,128)(2,1)S(1)}, u32[]{:S(2)}, u32[]{:S(2)}) %collective-permute-start.38) | collective-permute-done | bytes 262176 | tf_op jit(solution)/shard_map/ppermute | solution.py:76
  131.4 0.9 pad_maximum_fusion.10
  132.5 1.0 copy-done.7
  133.5 1.5 convolution_convert_fusion.4
  135.1 3.7 %stack_reshape.19 = bf16[1,2,64,2048]{3,0,2,1:T(2,128)(2,1)S(1)} reshape(bf16[512,512]{1,0:T(8,128)(2,1)} %convolution_convert_fusion.4) | data formatting | bytes 1048576 | tf_op jit(solution)/shard_map/stack;reshape | solution.py:163
  138.9 1.0 copy-done.8
  140.0 1.5 convolution_convert_fusion.6
  141.5 3.4 %stack_reshape.17 = bf16[1,2,64,2048]{3,0,2,1:T(2,128)(2,1)S(1)} reshape(bf16[512,512]{1,0:T(8,128)(2,1)} %convolution_convert_fusion.6) | data formatting | bytes 1048576 | tf_op jit(solution)/shard_map/stack;reshape | solution.py:163
  144.9 1.2 broadcast_select_fusion.3
  146.9 1.6 stack_reshape.18
  148.6 1.2 broadcast_select_fusion.7
  150.0 1.5 convolution_convert_fusion.7
  151.5 4.2 %stack_reshape.16 = bf16[1,2,64,2048]{3,0,2,1:T(2,128)(2,1)} reshape(bf16[512,512]{1,0:T(8,128)(2,1)} %convolution_convert_fusion.7) | data formatting | bytes 1048576 | tf_op jit(solution)/shard_map/stack;reshape | solution.py:163
  155.6 6.2 %convolution_convert_fusion = bf16[4,2,64,2048]{3,0,2,1:T(4,128)(2,1)S(1)} fusion(bf16[1,2,64,2048]{3,0,2,1:T(2,128)(2,1)S(1)} %stack_reshape.19, bf16[1,2,64,2048]{3,0,2,1:T(2,128)(2,1)S(1)} %copy-done.6, bf16[1,2,64,2048]{3,0,2,1:T(2,128)(2,1)S(1)} %stack_reshape.17, bf16[1,2,64,2048]{3,0,2,1:T(2,128)(2,1)} %stack_reshape.16, s32[4]{0:T(128)S(1)} %copy-done.56), kind=kOutput, calls=%fused_computation.2 | convolution fusion | flops 17825808 | bytes 4194320 | tf_op jit(solution)/shard_map/kd,dcrm->kcrm/dot_general | solution.py:162
  161.8 2.5 %copy.60 = bf16[4,2,64,2048]{3,2,1,0:T(8,128)(2,1)} copy(bf16[4,2,64,2048]{3,0,2,1:T(4,128)(2,1)S(1)} %convolution_convert_fusion) | data formatting | bytes 4194304
  (291 shorter events, 33.3 us)
Async XLA Ops:
  2.3 2.0 %copy-start.13 = (f32[4,4,16]{2,1,0:T(4,128)}, f32[4,4,16]{2,1,0:T(4,128)S(1)}, u32[]{:S(2)}) copy-start(f32[4,4,16]{2,1,0:T(4,128)S(1)} %get-tuple-element.100) | copy-start | bytes 3076
  2.3 2.0 %copy-start.25 = (f32[4,4,16]{2,1,0:T(4,128)}, f32[4,4,16]{2,1,0:T(4,128)S(1)}, u32[]{:S(2)}) copy-start(f32[4,4,16]{2,1,0:T(4,128)S(1)} %get-tuple-element.94) | copy-start | bytes 3076
  2.3 2.5 %copy-start.15 = (f32[4,4,16]{2,1,0:T(4,128)}, f32[4,4,16]{2,1,0:T(4,128)S(1)}, u32[]{:S(2)}) copy-start(f32[4,4,16]{2,1,0:T(4,128)S(1)} %get-tuple-element.102) | copy-start | bytes 3076
  2.3 2.5 %copy-start.27 = (f32[4,4,16]{2,1,0:T(4,128)}, f32[4,4,16]{2,1,0:T(4,128)S(1)}, u32[]{:S(2)}) copy-start(f32[4,4,16]{2,1,0:T(4,128)S(1)} %get-tuple-element.96) | copy-start | bytes 3076
  2.3 3.0 %copy-start.17 = (f32[4,4,16]{2,1,0:T(4,128)}, f32[4,4,16]{2,1,0:T(4,128)S(1)}, u32[]{:S(2)}) copy-start(f32[4,4,16]{2,1,0:T(4,128)S(1)} %get-tuple-element.104) | copy-start | bytes 3076
  2.3 3.0 %copy-start.29 = (f32[4,4,16]{2,1,0:T(4,128)}, f32[4,4,16]{2,1,0:T(4,128)S(1)}, u32[]{:S(2)}) copy-start(f32[4,4,16]{2,1,0:T(4,128)S(1)} %get-tuple-element.98) | copy-start | bytes 3076
  7.8 24.4 %collective-permute-start.18 = (bf16[2,3,4,4,1,512]{5,4,3,2,1,0:T(2,128)(2,1)}, bf16[2,3,4,4,1,512]{5,4,3,2,1,0:T(2,128)(2,1)}, u32[]{:S(2)}, u32[]{:S(2)}) collective-permute-start(bf16[2,3,4,4,1,512]{5,4,3,2,1,0:T(2,128)(2,1)} %pad_maximum_fusion.20), channel_id=1, source_target_pairs={{0,1},{1,0},{2,3},{3,2},{4,5},{5,4},{6,7},{7,6},{8,9},{9,8},{10,11... | collective-permute-start | bytes 294920 | tf_op jit(solution)/shard_map/ppermute | solution.py:97
  14.1 28.4 %collective-permute-start.12 = (bf16[2,3,4,1,16,512]{5,4,3,2,1,0:T(8,128)(2,1)}, bf16[2,3,4,1,16,512]{5,4,3,2,1,0:T(8,128)(2,1)}, u32[]{:S(2)}, u32[]{:S(2)}) collective-permute-start(bf16[2,3,4,1,16,512]{5,4,3,2,1,0:T(8,128)(2,1)} %pad_maximum_fusion.14), channel_id=1, source_target_pairs={{0,2},{2,4},{4,6},{6,8},{8,10},{10,12},{12,14},{14,16},{16,18},{18... | collective-permute-start | bytes 1179656 | tf_op jit(solution)/shard_map/ppermute | solution.py:95
  15.0 21.1 %collective-permute-start.6 = (bf16[2,3,4,4,1,512]{5,3,4,2,1,0:T(4,128)(2,1)S(1)}, bf16[2,3,4,4,1,512]{5,3,4,2,1,0:T(4,128)(2,1)}, u32[]{:S(2)}, u32[]{:S(2)}) collective-permute-start(bf16[2,3,4,4,1,512]{5,3,4,2,1,0:T(4,128)(2,1)S(1)} %copy.70), channel_id=1, source_target_pairs={{0,1},{1,0},{2,3},{3,2},{4,5},{5,4},{6,7},{7,6},{8,9},{9,8},{10,11... | collective-permute-start | bytes 294920 | tf_op jit(solution)/shard_map/ppermute | solution.py:96
  15.8 30.0 %collective-permute-start = (bf16[2,3,4,1,16,512]{5,4,3,2,1,0:T(8,128)(2,1)}, bf16[2,3,4,1,16,512]{5,4,3,2,1,0:T(8,128)(2,1)}, u32[]{:S(2)}, u32[]{:S(2)}) collective-permute-start(bf16[2,3,4,1,16,512]{5,4,3,2,1,0:T(8,128)(2,1)} %slice.143), channel_id=1, source_target_pairs={{0,30},{2,0},{4,2},{6,4},{8,6},{10,8},{12,10},{14,12},{16,14},{18,... | collective-permute-start | bytes 1179656 | tf_op jit(solution)/shard_map/ppermute | solution.py:94
  23.0 2.8 %copy-start.11 = (bf16[1,3,4,4,16,512]{5,4,3,2,1,0:T(8,128)(2,1)S(1)}, bf16[1,3,4,4,16,512]{5,4,3,2,1,0:T(8,128)(2,1)}, u32[]{:S(2)}) copy-start(bf16[1,3,4,4,16,512]{5,4,3,2,1,0:T(8,128)(2,1)} %get-tuple-element.32) | copy-start | bytes 2359300
  23.0 4.5 %copy-start.12 = (bf16[2,64,2048]{2,1,0:T(8,128)(2,1)S(1)}, bf16[2,64,2048]{2,1,0:T(8,128)(2,1)}, u32[]{:S(2)}) copy-start(bf16[2,64,2048]{2,1,0:T(8,128)(2,1)} %param.9) | copy-start | bytes 1572868
  25.7 2.2 %copy-start.55 = (s32[4]{0:T(128)S(1)}, s32[4]{0:T(128)}, u32[]{:S(2)}) copy-start(s32[4]{0:T(128)} %param.8) | copy-start | bytes 52
  30.0 2.2 %copy-start.56 = (s32[4]{0:T(128)S(1)}, s32[4]{0:T(128)}, u32[]{:S(2)}) copy-start(s32[4]{0:T(128)} %param.7) | copy-start | bytes 52
  30.0 2.2 %copy-start.2 = (bf16[1,3,4,4,16,512]{5,4,3,2,1,0:T(8,128)(2,1)S(1)}, bf16[1,3,4,4,16,512]{5,4,3,2,1,0:T(8,128)(2,1)}, u32[]{:S(2)}) copy-start(bf16[1,3,4,4,16,512]{5,4,3,2,1,0:T(8,128)(2,1)} %copy-done.1) | copy-start | bytes 2359300
  30.0 2.3 %copy-start.4 = (bf16[1,3,4,4,16,512]{5,4,3,2,1,0:T(8,128)(2,1)S(1)}, bf16[1,3,4,4,16,512]{5,4,3,2,1,0:T(8,128)(2,1)}, u32[]{:S(2)}) copy-start(bf16[1,3,4,4,16,512]{5,4,3,2,1,0:T(8,128)(2,1)} %copy-done.3) | copy-start | bytes 2359300
  36.0 16.5 %collective-permute-start.19 = (f32[2,2,2,2,1,2,16,512]{7,6,0,5,4,3,2,1:T(8,128)S(1)}, f32[2,2,2,2,1,2,16,512]{7,6,0,5,4,3,2,1:T(8,128)S(1)}, u32[]{:S(2)}, u32[]{:S(2)}) collective-permute-start(f32[2,2,2,2,1,2,16,512]{7,6,0,5,4,3,2,1:T(8,128)S(1)} %constant_dynamic-slice_fusion.4), channel_id=1, source_target_pairs={{0,2},{1,3},{2,0},{3,1},{4,6},{5,7},{6,4},{7,5},{8,10},{9,11},{10,... | collective-permute-start | bytes 3145736 | tf_op jit(solution)/shard_map/ppermute | solution.py:67
  42.1 12.3 %collective-permute-start.7 = (f32[2,2,2,2,1,2,16,512]{7,6,0,5,4,3,2,1:T(8,128)S(1)}, f32[2,2,2,2,1,2,16,512]{7,6,0,5,4,3,2,1:T(8,128)S(1)}, u32[]{:S(2)}, u32[]{:S(2)}) collective-permute-start(f32[2,2,2,2,1,2,16,512]{7,6,0,5,4,3,2,1:T(8,128)S(1)} %constant_dynamic-slice_fusion.14), channel_id=1, source_target_pairs={{0,2},{1,3},{2,0},{3,1},{4,6},{5,7},{6,4},{7,5},{8,10},{9,11},{10,... | collective-permute-start | bytes 3145736 | tf_op jit(solution)/shard_map/ppermute | solution.py:67
  45.6 2.4 %copy-start.32 = (f32[4,4,16]{2,1,0:T(4,128)S(1)}, f32[4,4,16]{2,1,0:T(4,128)}, u32[]{:S(2)}) copy-start(f32[4,4,16]{2,1,0:T(4,128)} %copy-done.31) | copy-start | bytes 3076
  45.6 2.4 %copy-start.34 = (f32[4,4,16]{2,1,0:T(4,128)S(1)}, f32[4,4,16]{2,1,0:T(4,128)}, u32[]{:S(2)}) copy-start(f32[4,4,16]{2,1,0:T(4,128)} %copy-done.33) | copy-start | bytes 3076
  45.6 2.4 %copy-start.36 = (f32[4,4,16]{2,1,0:T(4,128)S(1)}, f32[4,4,16]{2,1,0:T(4,128)}, u32[]{:S(2)}) copy-start(f32[4,4,16]{2,1,0:T(4,128)} %copy-done.35) | copy-start | bytes 3076
  45.6 2.4 %copy-start.52 = (f32[4,4,16]{2,1,0:T(4,128)S(1)}, f32[4,4,16]{2,1,0:T(4,128)}, u32[]{:S(2)}) copy-start(f32[4,4,16]{2,1,0:T(4,128)} %get-tuple-element.75) | copy-start | bytes 3076
  45.6 2.4 %copy-start.53 = (f32[4,4,16]{2,1,0:T(4,128)S(1)}, f32[4,4,16]{2,1,0:T(4,128)}, u32[]{:S(2)}) copy-start(f32[4,4,16]{2,1,0:T(4,128)} %get-tuple-element.77) | copy-start | bytes 3076
  45.6 2.4 %copy-start.54 = (f32[4,4,16]{2,1,0:T(4,128)S(1)}, f32[4,4,16]{2,1,0:T(4,128)}, u32[]{:S(2)}) copy-start(f32[4,4,16]{2,1,0:T(4,128)} %get-tuple-element.79) | copy-start | bytes 3076
  45.6 9.1 %collective-permute-start.13 = (f32[2,2,2,2,1,2,16,512]{7,6,5,4,3,2,1,0:T(8,128)S(1)}, f32[2,2,2,2,1,2,16,512]{7,6,5,4,3,2,1,0:T(8,128)S(1)}, u32[]{:S(2)}, u32[]{:S(2)}) collective-permute-start(f32[2,2,2,2,1,2,16,512]{7,6,5,4,3,2,1,0:T(8,128)S(1)} %constant_dynamic-slice_fusion.9), channel_id=1, source_target_pairs={{0,2},{1,3},{2,0},{3,1},{4,6},{5,7},{6,4},{7,5},{8,10},{9,11},{10,... | collective-permute-start | bytes 3145736 | tf_op jit(solution)/shard_map/ppermute | solution.py:67
  52.3 3.2 %collective-permute-start.1 = (f32[2,2,2,2,1,2,16,512]{7,6,5,4,3,2,1,0:T(8,128)S(1)}, f32[2,2,2,2,1,2,16,512]{7,6,5,4,3,2,1,0:T(8,128)S(1)}, u32[]{:S(2)}, u32[]{:S(2)}) collective-permute-start(f32[2,2,2,2,1,2,16,512]{7,6,5,4,3,2,1,0:T(8,128)S(1)} %constant_dynamic-slice_fusion.19), channel_id=1, source_target_pairs={{0,2},{1,3},{2,0},{3,1},{4,6},{5,7},{6,4},{7,5},{8,10},{9,11},{10,... | collective-permute-start | bytes 3145736 | tf_op jit(solution)/shard_map/ppermute | solution.py:67
  52.8 14.9 %collective-permute-start.20 = (f32[2,2,2,2,1,1,16,512]{7,6,0,5,4,3,2,1:T(8,128)S(1)}, f32[2,2,2,2,1,1,16,512]{7,6,0,5,4,3,2,1:T(8,128)S(1)}, u32[]{:S(2)}, u32[]{:S(2)}) collective-permute-start(f32[2,2,2,2,1,1,16,512]{7,6,0,5,4,3,2,1:T(8,128)S(1)} %constant_dynamic-slice_fusion.3), channel_id=1, source_target_pairs={{0,1},{1,0},{2,3},{3,2},{4,5},{5,4},{6,7},{7,6},{8,9},{9,8},{10,11... | collective-permute-start | bytes 1572872 | tf_op jit(solution)/shard_map/ppermute | solution.py:67
  54.7 14.0 %collective-permute-start.8 = (f32[2,2,2,1,1,2,16,512]{7,6,0,5,4,3,2,1:T(8,128)S(1)}, f32[2,2,2,1,1,2,16,512]{7,6,0,5,4,3,2,1:T(8,128)S(1)}, u32[]{:S(2)}, u32[]{:S(2)}) collective-permute-start(f32[2,2,2,1,1,2,16,512]{7,6,0,5,4,3,2,1:T(8,128)S(1)} %constant_dynamic-slice_fusion.13), channel_id=1, source_target_pairs={{0,4},{1,5},{2,6},{3,7},{4,0},{5,1},{6,2},{7,3},{8,12},{9,13},{10,... | collective-permute-start | bytes 1572872 | tf_op jit(solution)/shard_map/ppermute | solution.py:67
  55.0 21.9 %collective-permute-start.14 = (f32[2,2,1,2,1,2,16,512]{7,6,5,4,3,2,1,0:T(8,128)S(1)}, f32[2,2,1,2,1,2,16,512]{7,6,5,4,3,2,1,0:T(8,128)S(1)}, u32[]{:S(2)}, u32[]{:S(2)}) collective-permute-start(f32[2,2,1,2,1,2,16,512]{7,6,5,4,3,2,1,0:T(8,128)S(1)} %constant_dynamic-slice_fusion.8), channel_id=1, source_target_pairs={{0,8},{1,9},{2,10},{3,11},{4,12},{5,13},{6,14},{7,15},{8,0},{9,1},... | collective-permute-start | bytes 1572872 | tf_op jit(solution)/shard_map/ppermute | solution.py:67
  55.8 23.4 %collective-permute-start.2 = (f32[2,2,2,2,1,1,16,512]{7,6,5,4,3,2,1,0:T(8,128)S(1)}, f32[2,2,2,2,1,1,16,512]{7,6,5,4,3,2,1,0:T(8,128)S(1)}, u32[]{:S(2)}, u32[]{:S(2)}) collective-permute-start(f32[2,2,2,2,1,1,16,512]{7,6,5,4,3,2,1,0:T(8,128)S(1)} %constant_dynamic-slice_fusion.18), channel_id=1, source_target_pairs={{0,1},{1,0},{2,3},{3,2},{4,5},{5,4},{6,7},{7,6},{8,9},{9,8},{10,11... | collective-permute-start | bytes 1572872 | tf_op jit(solution)/shard_map/ppermute | solution.py:67
  67.8 7.1 %collective-permute-start.21 = (f32[2,2,2,1,1,1,16,512]{7,6,0,5,4,3,2,1:T(8,128)S(1)}, f32[2,2,2,1,1,1,16,512]{7,6,0,5,4,3,2,1:T(8,128)S(1)}, u32[]{:S(2)}, u32[]{:S(2)}) collective-permute-start(f32[2,2,2,1,1,1,16,512]{7,6,0,5,4,3,2,1:T(8,128)S(1)} %constant_dynamic-slice_fusion.2), channel_id=1, source_target_pairs={{0,4},{1,5},{2,6},{3,7},{4,0},{5,1},{6,2},{7,3},{8,12},{9,13},{10,... | collective-permute-start | bytes 786440 | tf_op jit(solution)/shard_map/ppermute | solution.py:67
  68.7 8.1 %collective-permute-start.9 = (f32[2,2,1,1,1,2,16,512]{7,6,0,5,4,3,2,1:T(8,128)S(1)}, f32[2,2,1,1,1,2,16,512]{7,6,0,5,4,3,2,1:T(8,128)S(1)}, u32[]{:S(2)}, u32[]{:S(2)}) collective-permute-start(f32[2,2,1,1,1,2,16,512]{7,6,0,5,4,3,2,1:T(8,128)S(1)} %constant_dynamic-slice_fusion.12), channel_id=1, source_target_pairs={{0,8},{1,9},{2,10},{3,11},{4,12},{5,13},{6,14},{7,15},{8,0},{9,1},... | collective-permute-start | bytes 786440 | tf_op jit(solution)/shard_map/ppermute | solution.py:67
  75.0 5.1 %collective-permute-start.22 = (f32[2,2,1,1,1,1,16,512]{7,6,0,5,4,3,2,1:T(8,128)S(1)}, f32[2,2,1,1,1,1,16,512]{7,6,0,5,4,3,2,1:T(8,128)S(1)}, u32[]{:S(2)}, u32[]{:S(2)}) collective-permute-start(f32[2,2,1,1,1,1,16,512]{7,6,0,5,4,3,2,1:T(8,128)S(1)} %constant_dynamic-slice_fusion.1), channel_id=1, source_target_pairs={{0,8},{1,9},{2,10},{3,11},{4,12},{5,13},{6,14},{7,15},{8,0},{9,1},... | collective-permute-start | bytes 393224 | tf_op jit(solution)/shard_map/ppermute | solution.py:67
  76.9 6.4 %collective-permute-start.10 = (f32[2,2,1,1,1,1,16,512]{7,6,0,5,4,3,2,1:T(8,128)S(1)}, f32[2,2,1,1,1,1,16,512]{7,6,0,5,4,3,2,1:T(8,128)S(1)}, u32[]{:S(2)}, u32[]{:S(2)}) collective-permute-start(f32[2,2,1,1,1,1,16,512]{7,6,0,5,4,3,2,1:T(8,128)S(1)} %constant_dynamic-slice_fusion.11), channel_id=1, source_target_pairs={{0,1},{1,0},{2,3},{3,2},{4,5},{5,4},{6,7},{7,6},{8,9},{9,8},{10,11... | collective-permute-start | bytes 393224 | tf_op jit(solution)/shard_map/ppermute | solution.py:67
  77.1 18.2 %collective-permute-start.15 = (f32[2,2,1,2,1,1,16,512]{7,6,5,4,3,2,1,0:T(8,128)S(1)}, f32[2,2,1,2,1,1,16,512]{7,6,5,4,3,2,1,0:T(8,128)S(1)}, u32[]{:S(2)}, u32[]{:S(2)}) collective-permute-start(f32[2,2,1,2,1,1,16,512]{7,6,5,4,3,2,1,0:T(8,128)S(1)} %constant_dynamic-slice_fusion.7), channel_id=1, source_target_pairs={{0,1},{1,0},{2,3},{3,2},{4,5},{5,4},{6,7},{7,6},{8,9},{9,8},{10,11... | collective-permute-start | bytes 786440 | tf_op jit(solution)/shard_map/ppermute | solution.py:67
  79.3 17.0 %collective-permute-start.3 = (f32[2,2,2,1,1,1,16,512]{7,6,5,4,3,2,1,0:T(8,128)S(1)}, f32[2,2,2,1,1,1,16,512]{7,6,5,4,3,2,1,0:T(8,128)S(1)}, u32[]{:S(2)}, u32[]{:S(2)}) collective-permute-start(f32[2,2,2,1,1,1,16,512]{7,6,5,4,3,2,1,0:T(8,128)S(1)} %constant_dynamic-slice_fusion.17), channel_id=1, source_target_pairs={{0,4},{1,5},{2,6},{3,7},{4,0},{5,1},{6,2},{7,3},{8,12},{9,13},{10,... | collective-permute-start | bytes 786440 | tf_op jit(solution)/shard_map/ppermute | solution.py:67
  80.1 6.7 %collective-permute-start.23 = (f32[2,1,1,1,1,1,16,512]{7,6,0,5,4,3,2,1:T(8,128)S(1)}, f32[2,1,1,1,1,1,16,512]{7,6,0,5,4,3,2,1:T(8,128)S(1)}, u32[]{:S(2)}, u32[]{:S(2)}) collective-permute-start(f32[2,1,1,1,1,1,16,512]{7,6,0,5,4,3,2,1:T(8,128)S(1)} %constant_dynamic-slice_fusion), channel_id=1, source_target_pairs={{0,16},{1,17},{2,18},{3,19},{4,20},{5,21},{6,22},{7,23},{8,24},{9,... | collective-permute-start | bytes 196616 | tf_op jit(solution)/shard_map/ppermute | solution.py:67
  83.4 6.0 %collective-permute-start.11 = (f32[2,1,1,1,1,1,16,512]{7,6,0,5,4,3,2,1:T(8,128)S(1)}, f32[2,1,1,1,1,1,16,512]{7,6,0,5,4,3,2,1:T(8,128)S(1)}, u32[]{:S(2)}, u32[]{:S(2)}) collective-permute-start(f32[2,1,1,1,1,1,16,512]{7,6,0,5,4,3,2,1:T(8,128)S(1)} %constant_dynamic-slice_fusion.10), channel_id=1, source_target_pairs={{0,16},{1,17},{2,18},{3,19},{4,20},{5,21},{6,22},{7,23},{8,24},{9,... | collective-permute-start | bytes 196616 | tf_op jit(solution)/shard_map/ppermute | solution.py:67
  86.8 4.9 %collective-permute-start.40 = (bf16[2,1,1,1,1,1,16,512]{7,6,5,4,3,2,1,0:T(8,128)(2,1)S(1)}, bf16[2,1,1,1,1,1,16,512]{7,6,5,4,3,2,1,0:T(8,128)(2,1)S(1)}, u32[]{:S(2)}, u32[]{:S(2)}) collective-permute-start(bf16[2,1,1,1,1,1,16,512]{7,6,5,4,3,2,1,0:T(8,128)(2,1)S(1)} %get-tuple-element.72), channel_id=1, source_target_pairs={{0,16},{1,17},{2,18},{3,19},{4,20},{5,21},{6,22},{7,23},{8,24},{9,... | collective-permute-start | bytes 98312 | tf_op jit(solution)/shard_map/ppermute | solution.py:76
  89.4 4.9 %collective-permute-start.30 = (bf16[2,1,1,1,1,1,16,512]{7,6,0,5,4,3,2,1:T(8,128)(2,1)S(1)}, bf16[2,1,1,1,1,1,16,512]{7,6,0,5,4,3,2,1:T(8,128)(2,1)S(1)}, u32[]{:S(2)}, u32[]{:S(2)}) collective-permute-start(bf16[2,1,1,1,1,1,16,512]{7,6,0,5,4,3,2,1:T(8,128)(2,1)S(1)} %get-tuple-element.68), channel_id=1, source_target_pairs={{0,16},{1,17},{2,18},{3,19},{4,20},{5,21},{6,22},{7,23},{8,24},{9,... | collective-permute-start | bytes 98312 | tf_op jit(solution)/shard_map/ppermute | solution.py:76
  91.7 5.0 %collective-permute-start.41 = (bf16[2,2,1,1,1,1,16,512]{7,6,5,4,3,2,1,0:T(8,128)(2,1)S(1)}, bf16[2,2,1,1,1,1,16,512]{7,6,5,4,3,2,1,0:T(8,128)(2,1)S(1)}, u32[]{:S(2)}, u32[]{:S(2)}) collective-permute-start(bf16[2,2,1,1,1,1,16,512]{7,6,5,4,3,2,1,0:T(8,128)(2,1)S(1)} %pad_maximum_fusion.28), channel_id=1, source_target_pairs={{0,8},{1,9},{2,10},{3,11},{4,12},{5,13},{6,14},{7,15},{8,0},{9,1},... | collective-permute-start | bytes 196616 | tf_op jit(solution)/shard_map/ppermute | solution.py:76
  94.3 4.3 %collective-permute-start.31 = (bf16[2,2,1,1,1,1,16,512]{7,6,0,5,4,3,2,1:T(8,128)(2,1)S(1)}, bf16[2,2,1,1,1,1,16,512]{7,6,0,5,4,3,2,1:T(8,128)(2,1)S(1)}, u32[]{:S(2)}, u32[]{:S(2)}) collective-permute-start(bf16[2,2,1,1,1,1,16,512]{7,6,0,5,4,3,2,1:T(8,128)(2,1)S(1)} %pad_maximum_fusion.26), channel_id=1, source_target_pairs={{0,1},{1,0},{2,3},{3,2},{4,5},{5,4},{6,7},{7,6},{8,9},{9,8},{10,11... | collective-permute-start | bytes 196616 | tf_op jit(solution)/shard_map/ppermute | solution.py:76
  95.4 5.0 %collective-permute-start.16 = (f32[2,2,1,1,1,1,16,512]{7,6,5,4,3,2,1,0:T(8,128)S(1)}, f32[2,2,1,1,1,1,16,512]{7,6,5,4,3,2,1,0:T(8,128)S(1)}, u32[]{:S(2)}, u32[]{:S(2)}) collective-permute-start(f32[2,2,1,1,1,1,16,512]{7,6,5,4,3,2,1,0:T(8,128)S(1)} %constant_dynamic-slice_fusion.6), channel_id=1, source_target_pairs={{0,4},{1,5},{2,6},{3,7},{4,0},{5,1},{6,2},{7,3},{8,12},{9,13},{10,... | collective-permute-start | bytes 393224 | tf_op jit(solution)/shard_map/ppermute | solution.py:67
  96.4 6.3 %collective-permute-start.4 = (f32[2,2,1,1,1,1,16,512]{7,6,5,4,3,2,1,0:T(8,128)S(1)}, f32[2,2,1,1,1,1,16,512]{7,6,5,4,3,2,1,0:T(8,128)S(1)}, u32[]{:S(2)}, u32[]{:S(2)}) collective-permute-start(f32[2,2,1,1,1,1,16,512]{7,6,5,4,3,2,1,0:T(8,128)S(1)} %constant_dynamic-slice_fusion.16), channel_id=1, source_target_pairs={{0,8},{1,9},{2,10},{3,11},{4,12},{5,13},{6,14},{7,15},{8,0},{9,1},... | collective-permute-start | bytes 393224 | tf_op jit(solution)/shard_map/ppermute | solution.py:67
  96.8 6.8 %collective-permute-start.42 = (bf16[2,2,2,1,1,1,16,512]{7,6,5,4,3,2,1,0:T(8,128)(2,1)S(1)}, bf16[2,2,2,1,1,1,16,512]{7,6,5,4,3,2,1,0:T(8,128)(2,1)S(1)}, u32[]{:S(2)}, u32[]{:S(2)}) collective-permute-start(bf16[2,2,2,1,1,1,16,512]{7,6,5,4,3,2,1,0:T(8,128)(2,1)S(1)} %pad_maximum_fusion.24), channel_id=1, source_target_pairs={{0,4},{1,5},{2,6},{3,7},{4,0},{5,1},{6,2},{7,3},{8,12},{9,13},{10,... | collective-permute-start | bytes 393224 | tf_op jit(solution)/shard_map/ppermute | solution.py:76
  98.7 6.1 %collective-permute-start.32 = (bf16[2,2,1,1,1,2,16,512]{7,6,0,5,4,3,2,1:T(8,128)(2,1)S(1)}, bf16[2,2,1,1,1,2,16,512]{7,6,0,5,4,3,2,1:T(8,128)(2,1)S(1)}, u32[]{:S(2)}, u32[]{:S(2)}) collective-permute-start(bf16[2,2,1,1,1,2,16,512]{7,6,0,5,4,3,2,1:T(8,128)(2,1)S(1)} %pad_maximum_fusion.22), channel_id=1, source_target_pairs={{0,8},{1,9},{2,10},{3,11},{4,12},{5,13},{6,14},{7,15},{8,0},{9,1},... | collective-permute-start | bytes 393224 | tf_op jit(solution)/shard_map/ppermute | solution.py:76
  100.5 5.8 %collective-permute-start.17 = (f32[2,1,1,1,1,1,16,512]{7,6,5,4,3,2,1,0:T(8,128)S(1)}, f32[2,1,1,1,1,1,16,512]{7,6,5,4,3,2,1,0:T(8,128)S(1)}, u32[]{:S(2)}, u32[]{:S(2)}) collective-permute-start(f32[2,1,1,1,1,1,16,512]{7,6,5,4,3,2,1,0:T(8,128)S(1)} %constant_dynamic-slice_fusion.5), channel_id=1, source_target_pairs={{0,16},{1,17},{2,18},{3,19},{4,20},{5,21},{6,22},{7,23},{8,24},{9,... | collective-permute-start | bytes 196616 | tf_op jit(solution)/shard_map/ppermute | solution.py:67
  102.7 5.6 %collective-permute-start.5 = (f32[2,1,1,1,1,1,16,512]{7,6,5,4,3,2,1,0:T(8,128)S(1)}, f32[2,1,1,1,1,1,16,512]{7,6,5,4,3,2,1,0:T(8,128)S(1)}, u32[]{:S(2)}, u32[]{:S(2)}) collective-permute-start(f32[2,1,1,1,1,1,16,512]{7,6,5,4,3,2,1,0:T(8,128)S(1)} %constant_dynamic-slice_fusion.15), channel_id=1, source_target_pairs={{0,16},{1,17},{2,18},{3,19},{4,20},{5,21},{6,22},{7,23},{8,24},{9,... | collective-permute-start | bytes 196616 | tf_op jit(solution)/shard_map/ppermute | solution.py:67
  103.7 17.1 %collective-permute-start.43 = (bf16[2,2,2,2,1,1,16,512]{7,6,5,4,3,2,1,0:T(8,128)(2,1)S(1)}, bf16[2,2,2,2,1,1,16,512]{7,6,5,4,3,2,1,0:T(8,128)(2,1)S(1)}, u32[]{:S(2)}, u32[]{:S(2)}) collective-permute-start(bf16[2,2,2,2,1,1,16,512]{7,6,5,4,3,2,1,0:T(8,128)(2,1)S(1)} %pad_maximum_fusion.19), channel_id=1, source_target_pairs={{0,1},{1,0},{2,3},{3,2},{4,5},{5,4},{6,7},{7,6},{8,9},{9,8},{10,11... | collective-permute-start | bytes 786440 | tf_op jit(solution)/shard_map/ppermute | solution.py:76
  104.8 16.1 %collective-permute-start.33 = (bf16[2,2,2,1,1,2,16,512]{7,6,0,5,4,3,2,1:T(8,128)(2,1)S(1)}, bf16[2,2,2,1,1,2,16,512]{7,6,0,5,4,3,2,1:T(8,128)(2,1)S(1)}, u32[]{:S(2)}, u32[]{:S(2)}) collective-permute-start(bf16[2,2,2,1,1,2,16,512]{7,6,0,5,4,3,2,1:T(8,128)(2,1)S(1)} %pad_maximum_fusion.17), channel_id=1, source_target_pairs={{0,4},{1,5},{2,6},{3,7},{4,0},{5,1},{6,2},{7,3},{8,12},{9,13},{10,... | collective-permute-start | bytes 786440 | tf_op jit(solution)/shard_map/ppermute | solution.py:76
  106.3 5.1 %collective-permute-start.35 = (bf16[2,1,1,1,1,1,16,512]{7,6,5,4,3,2,1,0:T(8,128)(2,1)S(1)}, bf16[2,1,1,1,1,1,16,512]{7,6,5,4,3,2,1,0:T(8,128)(2,1)S(1)}, u32[]{:S(2)}, u32[]{:S(2)}) collective-permute-start(bf16[2,1,1,1,1,1,16,512]{7,6,5,4,3,2,1,0:T(8,128)(2,1)S(1)} %get-tuple-element.70), channel_id=1, source_target_pairs={{0,16},{1,17},{2,18},{3,19},{4,20},{5,21},{6,22},{7,23},{8,24},{9,... | collective-permute-start | bytes 98312 | tf_op jit(solution)/shard_map/ppermute | solution.py:76
  109.0 16.6 %collective-permute-start.24 = (f32[4,2,1,1,1,1,1,16,512]{8,7,1,0,6,5,4,3,2:T(8,128)S(1)}, f32[4,2,1,1,1,1,1,16,512]{8,7,1,0,6,5,4,3,2:T(8,128)S(1)}, u32[]{:S(2)}, u32[]{:S(2)}) collective-permute-start(f32[4,2,1,1,1,1,1,16,512]{8,7,1,0,6,5,4,3,2:T(8,128)S(1)} %bitcast.559), channel_id=1, source_target_pairs={{0,1},{1,0},{2,3},{3,2},{4,5},{5,4},{6,7},{7,6},{8,9},{9,8},{10,11... | collective-permute-start | bytes 786440 | tf_op jit(solution)/shard_map/ppermute | solution.py:76
  110.3 5.2 %collective-permute-start.25 = (bf16[2,1,1,1,1,1,16,512]{7,6,5,4,3,2,1,0:T(8,128)(2,1)S(1)}, bf16[2,1,1,1,1,1,16,512]{7,6,5,4,3,2,1,0:T(8,128)(2,1)S(1)}, u32[]{:S(2)}, u32[]{:S(2)}) collective-permute-start(bf16[2,1,1,1,1,1,16,512]{7,6,5,4,3,2,1,0:T(8,128)(2,1)S(1)} %get-tuple-element.66), channel_id=1, source_target_pairs={{0,16},{1,17},{2,18},{3,19},{4,20},{5,21},{6,22},{7,23},{8,24},{9,... | collective-permute-start | bytes 98312 | tf_op jit(solution)/shard_map/ppermute | solution.py:76
  111.4 5.0 %collective-permute-start.36 = (bf16[2,2,1,1,1,1,16,512]{7,6,5,4,3,2,1,0:T(8,128)(2,1)S(1)}, bf16[2,2,1,1,1,1,16,512]{7,6,5,4,3,2,1,0:T(8,128)(2,1)S(1)}, u32[]{:S(2)}, u32[]{:S(2)}) collective-permute-start(bf16[2,2,1,1,1,1,16,512]{7,6,5,4,3,2,1,0:T(8,128)(2,1)S(1)} %pad_maximum_fusion.27), channel_id=1, source_target_pairs={{0,4},{1,5},{2,6},{3,7},{4,0},{5,1},{6,2},{7,3},{8,12},{9,13},{10,... | collective-permute-start | bytes 196616 | tf_op jit(solution)/shard_map/ppermute | solution.py:76
  115.5 4.3 %collective-permute-start.26 = (bf16[2,2,1,1,1,1,16,512]{7,6,5,4,3,2,1,0:T(8,128)(2,1)S(1)}, bf16[2,2,1,1,1,1,16,512]{7,6,5,4,3,2,1,0:T(8,128)(2,1)S(1)}, u32[]{:S(2)}, u32[]{:S(2)}) collective-permute-start(bf16[2,2,1,1,1,1,16,512]{7,6,5,4,3,2,1,0:T(8,128)(2,1)S(1)} %pad_maximum_fusion.25), channel_id=1, source_target_pairs={{0,8},{1,9},{2,10},{3,11},{4,12},{5,13},{6,14},{7,15},{8,0},{9,1},... | collective-permute-start | bytes 196616 | tf_op jit(solution)/shard_map/ppermute | solution.py:76
  116.5 5.1 %collective-permute-start.37 = (bf16[2,2,1,2,1,1,16,512]{7,6,5,4,3,2,1,0:T(8,128)(2,1)S(1)}, bf16[2,2,1,2,1,1,16,512]{7,6,5,4,3,2,1,0:T(8,128)(2,1)S(1)}, u32[]{:S(2)}, u32[]{:S(2)}) collective-permute-start(bf16[2,2,1,2,1,1,16,512]{7,6,5,4,3,2,1,0:T(8,128)(2,1)S(1)} %pad_maximum_fusion.23), channel_id=1, source_target_pairs={{0,1},{1,0},{2,3},{3,2},{4,5},{5,4},{6,7},{7,6},{8,9},{9,8},{10,11... | collective-permute-start | bytes 393224 | tf_op jit(solution)/shard_map/ppermute | solution.py:76
  119.8 5.0 %collective-permute-start.27 = (bf16[2,2,2,1,1,1,16,512]{7,6,5,4,3,2,1,0:T(8,128)(2,1)S(1)}, bf16[2,2,2,1,1,1,16,512]{7,6,5,4,3,2,1,0:T(8,128)(2,1)S(1)}, u32[]{:S(2)}, u32[]{:S(2)}) collective-permute-start(bf16[2,2,2,1,1,1,16,512]{7,6,5,4,3,2,1,0:T(8,128)(2,1)S(1)} %pad_maximum_fusion.21), channel_id=1, source_target_pairs={{0,4},{1,5},{2,6},{3,7},{4,0},{5,1},{6,2},{7,3},{8,12},{9,13},{10,... | collective-permute-start | bytes 393224 | tf_op jit(solution)/shard_map/ppermute | solution.py:76
  120.8 11.4 %collective-permute-start.44 = (bf16[2,2,2,2,1,2,16,512]{7,6,5,4,3,2,1,0:T(8,128)(2,1)S(1)}, bf16[2,2,2,2,1,2,16,512]{7,6,5,4,3,2,1,0:T(8,128)(2,1)S(1)}, u32[]{:S(2)}, u32[]{:S(2)}) collective-permute-start(bf16[2,2,2,2,1,2,16,512]{7,6,5,4,3,2,1,0:T(8,128)(2,1)S(1)} %pad_maximum_fusion.13), channel_id=1, source_target_pairs={{0,2},{1,3},{2,0},{3,1},{4,6},{5,7},{6,4},{7,5},{8,10},{9,11},{10,... | collective-permute-start | bytes 1572872 | tf_op jit(solution)/shard_map/ppermute | solution.py:76
  121.0 13.9 %collective-permute-start.34 = (bf16[2,2,2,2,1,2,16,512]{7,6,0,5,4,3,2,1:T(8,128)(2,1)S(1)}, bf16[2,2,2,2,1,2,16,512]{7,6,0,5,4,3,2,1:T(8,128)(2,1)S(1)}, u32[]{:S(2)}, u32[]{:S(2)}) collective-permute-start(bf16[2,2,2,2,1,2,16,512]{7,6,0,5,4,3,2,1:T(8,128)(2,1)S(1)} %pad_maximum_fusion.11), channel_id=1, source_target_pairs={{0,2},{1,3},{2,0},{3,1},{4,6},{5,7},{6,4},{7,5},{8,10},{9,11},{10,... | collective-permute-start | bytes 1572872 | tf_op jit(solution)/shard_map/ppermute | solution.py:76
  121.7 8.3 %collective-permute-start.38 = (bf16[2,2,1,2,1,2,16,512]{7,6,5,4,3,2,1,0:T(8,128)(2,1)S(1)}, bf16[2,2,1,2,1,2,16,512]{7,6,5,4,3,2,1,0:T(8,128)(2,1)S(1)}, u32[]{:S(2)}, u32[]{:S(2)}) collective-permute-start(bf16[2,2,1,2,1,2,16,512]{7,6,5,4,3,2,1,0:T(8,128)(2,1)S(1)} %pad_maximum_fusion.18), channel_id=1, source_target_pairs={{0,8},{1,9},{2,10},{3,11},{4,12},{5,13},{6,14},{7,15},{8,0},{9,1},... | collective-permute-start | bytes 786440 | tf_op jit(solution)/shard_map/ppermute | solution.py:76
  124.9 6.4 %collective-permute-start.28 = (bf16[2,2,2,2,1,1,16,512]{7,6,5,4,3,2,1,0:T(8,128)(2,1)S(1)}, bf16[2,2,2,2,1,1,16,512]{7,6,5,4,3,2,1,0:T(8,128)(2,1)S(1)}, u32[]{:S(2)}, u32[]{:S(2)}) collective-permute-start(bf16[2,2,2,2,1,1,16,512]{7,6,5,4,3,2,1,0:T(8,128)(2,1)S(1)} %pad_maximum_fusion.16), channel_id=1, source_target_pairs={{0,1},{1,0},{2,3},{3,2},{4,5},{5,4},{6,7},{7,6},{8,9},{9,8},{10,11... | collective-permute-start | bytes 786440 | tf_op jit(solution)/shard_map/ppermute | solution.py:76
  130.8 14.0 %collective-permute-start.39 = (bf16[2,2,2,2,1,2,16,512]{7,6,5,4,3,2,1,0:T(8,128)(2,1)}, bf16[2,2,2,2,1,2,16,512]{7,6,5,4,3,2,1,0:T(8,128)(2,1)}, u32[]{:S(2)}, u32[]{:S(2)}) collective-permute-start(bf16[2,2,2,2,1,2,16,512]{7,6,5,4,3,2,1,0:T(8,128)(2,1)} %pad_maximum_fusion.12), channel_id=1, source_target_pairs={{0,2},{1,3},{2,0},{3,1},{4,6},{5,7},{6,4},{7,5},{8,10},{9,11},{10,... | collective-permute-start | bytes 1572872 | tf_op jit(solution)/shard_map/ppermute | solution.py:76
  132.3 16.3 %collective-permute-start.29 = (bf16[2,2,2,2,1,2,16,512]{7,6,5,4,3,2,1,0:T(8,128)(2,1)}, bf16[2,2,2,2,1,2,16,512]{7,6,5,4,3,2,1,0:T(8,128)(2,1)}, u32[]{:S(2)}, u32[]{:S(2)}) collective-permute-start(bf16[2,2,2,2,1,2,16,512]{7,6,5,4,3,2,1,0:T(8,128)(2,1)} %pad_maximum_fusion.10), channel_id=1, source_target_pairs={{0,2},{1,3},{2,0},{3,1},{4,6},{5,7},{6,4},{7,5},{8,10},{9,11},{10,... | collective-permute-start | bytes 1572872 | tf_op jit(solution)/shard_map/ppermute | solution.py:76
  150.0 5.7 %copy-start.6 = (bf16[1,2,64,2048]{3,0,2,1:T(2,128)(2,1)S(1)}, bf16[1,2,64,2048]{3,0,2,1:T(2,128)(2,1)}, u32[]{:S(2)}) copy-start(bf16[1,2,64,2048]{3,0,2,1:T(2,128)(2,1)} %stack_reshape.18) | copy-start | bytes 1572868
  (39 other events, 34.3 us)

commit v11 on v9

--- a/solution.py
+++ b/solution.py
@@ -10,7 +10,7 @@
 
 
 def colour_apply(gauge_link, colour_field, dagger):
-    values = colour_field.astype(jnp.float32)
+    values = colour_field
     rows_re = []
     rows_im = []
     for row in range(3):

time: 149 us -> 162 us (1.087)
  other arithmetic: 27.4 us -> 39.5 us
  starting transfers between devices: 34.6 us -> 43 us
  waiting for transfers between devices: 46.8 us -> 39.8 us
    concatenate x1, other arithmetic: 2.18 us -> 13 us  [local(): jnp.concatenate([jnp.concatenate([turned[0], turned[1]], axis=1), jnp.con...]
    ppermute x21, starting transfers between devices: 15.5 us -> 21 us  [all_gather(): other = lax.ppermute(buf, ALL, xor_pairs(count, b))]
    another operation x12, other arithmetic: 6.04 us -> 11.2 us
    ppermute x21, waiting for transfers between devices: 16.6 us -> 12 us  [all_gather(): other = lax.ppermute(buf, ALL, xor_pairs(count, b))]
    convert_element_type x3 -> x0, other arithmetic: 3.71 us -> none  [colour_apply(): values = colour_field.astype(jnp.float32)]
    ppermute x20, starting transfers between devices: 12.1 us -> 14.6 us  [reduce_scatter(): buf = keep + lax.ppermute(send, ALL, xor_pairs(count, b))]
    ppermute x20, waiting for transfers between devices: 30.1 us -> 27.8 us  [reduce_scatter(): buf = keep + lax.ppermute(send, ALL, xor_pairs(count, b))]
    unnamed x111 -> x72, local copies, waits for them, and re-layouts: 4.34 us -> 4.9 us
  transfers between devices with their start and end apart: 45 -> 45, of which waited for: 21 -> 18; matrix products, arithmetic and copies ran while one was open for 32% -> 36% of each run, Pallas kernels for 0% -> 0%
where the time goes in v11:
time: 162 us
  starting transfers between devices  43 us (27%)
  waiting for transfers between devices  39.8 us (25%)
  other arithmetic  39.5 us (24%)
  local copies, waits for them, and re-layouts  21.7 us (13%)
  matrix products  15.8 us (10%)
  between operations  1.88 us (1%)
    ppermute x20, waiting for transfers between devices, reduce_scatter(): buf = keep + lax.ppermute(send, ALL, xor_pairs(count, b))  27.8 us
    ppermute x21, starting transfers between devices, all_gather(): other = lax.ppermute(buf, ALL, xor_pairs(count, b))  21 us
    ppermute x20, starting transfers between devices, reduce_scatter(): buf = keep + lax.ppermute(send, ALL, xor_pairs(count, b))  14.6 us
    concatenate x1, other arithmetic, local(): jnp.concatenate([jnp.concatenate([turned[0], turned[1]], axis=1), jnp.con...  13 us
    ppermute x21, waiting for transfers between devices, all_gather(): other = lax.ppermute(buf, ALL, xor_pairs(count, b))  12 us
    another operation x12, other arithmetic  11.2 us
    dot_general x4, matrix products, local(): jnp.dot(left, field.reshape(2 * depth, nev), preferred_element_type=jnp.f...  7.12 us
    unnamed x72, local copies, waits for them, and re-layouts  4.9 us
  transfers between devices with their start and end apart: 45, of which 18 were waited for; matrix products, arithmetic and copies ran while one was open for 36% of the time, Pallas kernels for 0%

profile of v11, /device:TPU:0, one launch (start us, length us, event | category | flops | bytes accessed | tf_op | source)
XLA Modules:
  0.0 161.6 jit_solution(18154852657910440206)
XLA Ops:
  0.6 1.1 slice_bitcast_fusion.1
  2.5 2.0 %fusion.132 = (bf16[1,4,4,16,512]{4,3,2,1,0:T(8,128)(2,1)S(1)}, bf16[1,4,4,16,512]{4,3,2,1,0:T(8,128)(2,1)S(1)}) fusion(f32[4,4,16]{2,1,0:T(4,128)S(1)} %get-tuple-element.161, f32[4,4,16]{2,1,0:T(4,128)S(1)} %get-tuple-element.158, f32[4,4,16]{2,1,0:T(4,128)S(1)} %get-tuple-element.155, f32[4,4,16]{2,1,0:T(4,128)S(1)} %get-tuple-element.102, ...), kind=kLoop, calls=%fused_computation.329 | loop fusion | flops 3932160 | bytes 2103296 | tf_op jit(solution)/shard_map/convert.27
  5.9 1.1 pad_maximum_fusion.23
  7.0 3.0 %collective-permute-start.18 = (bf16[2,3,4,4,1,512]{5,4,3,2,1,0:T(2,128)(2,1)}, bf16[2,3,4,4,1,512]{5,4,3,2,1,0:T(2,128)(2,1)}, u32[]{:S(2)}, u32[]{:S(2)}) collective-permute-start(bf16[2,3,4,4,1,512]{5,4,3,2,1,0:T(2,128)(2,1)} %pad_maximum_fusion.23), channel_id=1, source_target_pairs={{0,1},{1,0},{2,3},{3,2},{4,5},{5,4},{6,7},{7,6},{8,9},{9,8},{10,11... | collective-permute-start | bytes 294920 | tf_op jit(solution)/shard_map/ppermute | solution.py:97
  13.5 0.8 slice.170
  15.1 4.4 %collective-permute-start = (bf16[2,3,4,1,16,512]{5,4,3,2,1,0:T(8,128)(2,1)}, bf16[2,3,4,1,16,512]{5,4,3,2,1,0:T(8,128)(2,1)}, u32[]{:S(2)}, u32[]{:S(2)}) collective-permute-start(bf16[2,3,4,1,16,512]{5,4,3,2,1,0:T(8,128)(2,1)} %slice.143), channel_id=1, source_target_pairs={{0,30},{2,0},{4,2},{6,4},{8,6},{10,8},{12,10},{14,12},{16,14},{18,... | collective-permute-start | bytes 1179656 | tf_op jit(solution)/shard_map/ppermute | solution.py:94
  19.6 1.4 fusion.213
  20.9 1.8 %slice.169 = bf16[2,3,4,4,15,512]{5,4,3,2,1,0:T(8,128)(2,1)} slice(bf16[2,3,4,4,16,512]{5,4,3,2,1,0:T(8,128)(2,1)S(1)} %copy-done), slice={[0:2], [0:3], [0:4], [0:4], [1:16], [0:512]} | slice | bytes 2949120 | tf_op jit(solution)/shard_map/slice | solution.py:99
  22.8 2.7 %convolution_convert_fusion.1 = bf16[512,768]{1,0:T(8,128)(2,1)} fusion(bf16[768,512]{1,0:T(8,128)(2,1)} %bitcast.364), kind=kOutput, calls=%fused_computation.102 | convolution fusion | flops 403308544 | bytes 1572864 | tf_op jit(solution)/shard_map/dot_general | solution.py:110
  25.5 1.8 %fusion.215 = (bf16[512,768]{1,0:T(8,128)(2,1)}, bf16[512,768]{1,0:T(8,128)(2,1)}) fusion(bf16[768,512]{1,0:T(8,128)(2,1)S(1)} %bitcast.363), kind=kOutput, calls=%fused_computation.542 | convolution fusion | flops 403701760 | bytes 2359296 | tf_op jit(solution)/shard_map/dot_general | solution.py:110
  28.7 1.1 pad_maximum_fusion.5
  30.6 13.0 %maximum_maximum_fusion = bf16[1024,1536]{1,0:T(8,128)(2,1)S(1)} fusion(bf16[512,768]{1,0:T(8,128)(2,1)S(1)} %copy-done.9, bf16[512,768]{1,0:T(8,128)(2,1)S(1)} %copy-done.10, bf16[512,768]{1,0:T(8,128)(2,1)S(1)} %copy-done.11), kind=kLoop, calls=%fused_computation.12 | loop fusion | flops 12582912 | bytes 5505024 | tf_op jit(solution)/shard_map/concatenate | solution.py:115
  43.6 1.7 %fusion.4 = bf16[2,3,4,4,16,512]{5,4,3,2,1,0:T(8,128)(2,1)S(1)} fusion(bf16[1,3,4,4,16,512]{5,4,3,2,1,0:T(8,128)(2,1)S(1)} %copy-done.2, bf16[1,3,4,4,16,512]{5,4,3,2,1,0:T(8,128)(2,1)S(1)} %copy-done.4, bf16[2,3,4,4,1,512]{5,4,3,2,1,0:T(2,128)(2,1)} %collective-permute-done.18), kind=kLoop, calls=%fused_computation.96 | loop fusion | flops 4718592 | bytes 3244032 | tf_op jit(solution)/shard_map/concatenate | solution.py:104
  45.4 1.8 %fusion = f32[2,2,2,2,2,2,16,512]{7,6,0,5,4,3,2,1:T(8,128)S(1)} fusion(bf16[1536,512,1,1,1,1,1,1]{1,0,2,7,6,5,4,3:T(8,128)(2,1)S(1)} %bitcast.351, bf16[2,2,2,2,2,2,16,1536]{7,6,5,4,3,2,1,0:T(8,128)(2,1)S(1)} %bitcast.346), kind=kOutput, calls=%fused_computation.13 | convolution fusion | flops 1610612736 | bytes 6815744 | tf_op jit(solution)/shard_map/dot_general | solution.py:143
  47.4 1.2 copy-done.5
  48.6 1.6 fusion.48
  51.0 1.1 fusion.54
  52.4 1.8 %fusion.2 = f32[2,2,2,2,2,2,16,512]{7,6,0,5,4,3,2,1:T(8,128)S(1)} fusion(bf16[1536,512,1,1,1,1,1,1]{1,0,2,7,6,5,4,3:T(8,128)(2,1)S(1)} %bitcast.353, bf16[2,2,2,2,2,2,16,1536]{7,6,5,4,3,2,1,0:T(8,128)(2,1)S(1)} %bitcast.347), kind=kOutput, calls=%fused_computation.15 | convolution fusion | flops 1610612736 | bytes 6815744 | tf_op jit(solution)/shard_map/dot_general | solution.py:143
  54.4 1.2 fusion.5
  55.6 1.8 %fusion.217 = f32[2,2,2,2,2,2,16,512]{7,6,5,4,3,2,1,0:T(8,128)S(1)} fusion(bf16[2,2,2,2,2,2,16,1536]{7,6,5,4,3,2,1,0:T(8,128)(2,1)S(1)} %bitcast.348, bf16[1536,512,1,1,1,1,1,1]{1,0,7,6,5,4,3,2:T(8,128)(2,1)S(1)} %bitcast.350), kind=kOutput, calls=%fused_computation.544 | convolution fusion | flops 1610612736 | bytes 6815744 | tf_op jit(solution)/shard_map/dot_general | solution.py:143
  58.7 1.4 fusion.12
  60.8 1.3 fusion.18
  62.5 1.8 %fusion.216 = f32[2,2,2,2,2,2,16,512]{7,6,5,4,3,2,1,0:T(8,128)S(1)} fusion(bf16[2,2,2,2,2,2,16,1536]{7,6,5,4,3,2,1,0:T(8,128)(2,1)S(1)} %bitcast.349, bf16[1536,512,1,1,1,1,1,1]{1,0,7,6,5,4,3,2:T(8,128)(2,1)S(1)} %bitcast.352), kind=kOutput, calls=%fused_computation.543 | convolution fusion | flops 1610612736 | bytes 6815744 | tf_op jit(solution)/shard_map/dot_general | solution.py:143
  65.2 1.8 %collective-permute-start.20 = (f32[2,2,2,2,1,1,16,512]{7,6,0,5,4,3,2,1:T(8,128)S(1)}, f32[2,2,2,2,1,1,16,512]{7,6,0,5,4,3,2,1:T(8,128)S(1)}, u32[]{:S(2)}, u32[]{:S(2)}) collective-permute-start(f32[2,2,2,2,1,1,16,512]{7,6,0,5,4,3,2,1:T(8,128)S(1)} %constant_dynamic-slice_fusion.3), channel_id=1, source_target_pairs={{0,1},{1,0},{2,3},{3,2},{4,5},{5,4},{6,7},{7,6},{8,9},{9,8},{10,11... | collective-permute-start | bytes 1572872 | tf_op jit(solution)/shard_map/ppermute | solution.py:67
  68.4 0.9 collective-permute-start.2
  69.3 10.8 %collective-permute-done.20 = f32[2,2,2,2,1,1,16,512]{7,6,0,5,4,3,2,1:T(8,128)S(1)} collective-permute-done((f32[2,2,2,2,1,1,16,512]{7,6,0,5,4,3,2,1:T(8,128)S(1)}, f32[2,2,2,2,1,1,16,512]{7,6,0,5,4,3,2,1:T(8,128)S(1)}, u32[]{:S(2)}, u32[]{:S(2)}) %collective-permute-start.20) | collective-permute-done | bytes 524320 | tf_op jit(solution)/shard_map/ppermute | solution.py:67
  81.2 5.6 %collective-permute-done.21 = f32[2,2,2,1,1,1,16,512]{7,6,0,5,4,3,2,1:T(8,128)S(1)} collective-permute-done((f32[2,2,2,1,1,1,16,512]{7,6,0,5,4,3,2,1:T(8,128)S(1)}, f32[2,2,2,1,1,1,16,512]{7,6,0,5,4,3,2,1:T(8,128)S(1)}, u32[]{:S(2)}, u32[]{:S(2)}) %collective-permute-start.21) | collective-permute-done | bytes 262176 | tf_op jit(solution)/shard_map/ppermute | solution.py:67
  86.9 2.8 %collective-permute-done.9 = f32[2,2,1,1,1,2,16,512]{7,6,0,5,4,3,2,1:T(8,128)S(1)} collective-permute-done((f32[2,2,1,1,1,2,16,512]{7,6,0,5,4,3,2,1:T(8,128)S(1)}, f32[2,2,1,1,1,2,16,512]{7,6,0,5,4,3,2,1:T(8,128)S(1)}, u32[]{:S(2)}, u32[]{:S(2)}) %collective-permute-start.9) | collective-permute-done | bytes 262176 | tf_op jit(solution)/shard_map/ppermute | solution.py:67
  90.0 2.1 %collective-permute-start.15 = (f32[2,2,1,2,1,1,16,512]{7,6,5,4,3,2,1,0:T(8,128)S(1)}, f32[2,2,1,2,1,1,16,512]{7,6,5,4,3,2,1,0:T(8,128)S(1)}, u32[]{:S(2)}, u32[]{:S(2)}) collective-permute-start(f32[2,2,1,2,1,1,16,512]{7,6,5,4,3,2,1,0:T(8,128)S(1)} %constant_dynamic-slice_fusion.7), channel_id=1, source_target_pairs={{0,1},{1,0},{2,3},{3,2},{4,5},{5,4},{6,7},{7,6},{8,9},{9,8},{10,11... | collective-permute-start | bytes 786440 | tf_op jit(solution)/shard_map/ppermute | solution.py:67
  92.9 1.1 collective-permute-start.23
  94.0 2.0 %collective-permute-done.10 = f32[2,2,1,1,1,1,16,512]{7,6,0,5,4,3,2,1:T(8,128)S(1)} collective-permute-done((f32[2,2,1,1,1,1,16,512]{7,6,0,5,4,3,2,1:T(8,128)S(1)}, f32[2,2,1,1,1,1,16,512]{7,6,0,5,4,3,2,1:T(8,128)S(1)}, u32[]{:S(2)}, u32[]{:S(2)}) %collective-permute-start.10) | collective-permute-done | bytes 131104 | tf_op jit(solution)/shard_map/ppermute | solution.py:67
  96.8 2.4 %collective-permute-done.23 = f32[2,1,1,1,1,1,16,512]{7,6,0,5,4,3,2,1:T(8,128)S(1)} collective-permute-done((f32[2,1,1,1,1,1,16,512]{7,6,0,5,4,3,2,1:T(8,128)S(1)}, f32[2,1,1,1,1,1,16,512]{7,6,0,5,4,3,2,1:T(8,128)S(1)}, u32[]{:S(2)}, u32[]{:S(2)}) %collective-permute-start.23) | collective-permute-done | bytes 65568 | tf_op jit(solution)/shard_map/ppermute | solution.py:67
  99.6 2.5 %collective-permute-done.11 = f32[2,1,1,1,1,1,16,512]{7,6,0,5,4,3,2,1:T(8,128)S(1)} collective-permute-done((f32[2,1,1,1,1,1,16,512]{7,6,0,5,4,3,2,1:T(8,128)S(1)}, f32[2,1,1,1,1,1,16,512]{7,6,0,5,4,3,2,1:T(8,128)S(1)}, u32[]{:S(2)}, u32[]{:S(2)}) %collective-permute-start.11) | collective-permute-done | bytes 65568 | tf_op jit(solution)/shard_map/ppermute | solution.py:67
  102.3 1.8 %collective-permute-done.40 = bf16[2,1,1,1,1,1,16,512]{7,6,5,4,3,2,1,0:T(8,128)(2,1)S(1)} collective-permute-done((bf16[2,1,1,1,1,1,16,512]{7,6,5,4,3,2,1,0:T(8,128)(2,1)S(1)}, bf16[2,1,1,1,1,1,16,512]{7,6,5,4,3,2,1,0:T(8,128)(2,1)S(1)}, u32[]{:S(2)}, u32[]{:S(2)}) %collective-permute-start.40) | collective-permute-done | bytes 32800 | tf_op jit(solution)/shard_map/ppermute | solution.py:76
  104.7 2.5 %collective-permute-done.30 = bf16[2,1,1,1,1,1,16,512]{7,6,0,5,4,3,2,1:T(8,128)(2,1)S(1)} collective-permute-done((bf16[2,1,1,1,1,1,16,512]{7,6,0,5,4,3,2,1:T(8,128)(2,1)S(1)}, bf16[2,1,1,1,1,1,16,512]{7,6,0,5,4,3,2,1:T(8,128)(2,1)S(1)}, u32[]{:S(2)}, u32[]{:S(2)}) %collective-permute-start.30) | collective-permute-done | bytes 32800 | tf_op jit(solution)/shard_map/ppermute | solution.py:76
  107.8 1.3 collective-permute-start.16
  109.2 0.8 collective-permute-start.4
  110.1 2.0 %collective-permute-start.42 = (bf16[2,2,2,1,1,1,16,512]{7,6,5,4,3,2,1,0:T(8,128)(2,1)S(1)}, bf16[2,2,2,1,1,1,16,512]{7,6,5,4,3,2,1,0:T(8,128)(2,1)S(1)}, u32[]{:S(2)}, u32[]{:S(2)}) collective-permute-start(bf16[2,2,2,1,1,1,16,512]{7,6,5,4,3,2,1,0:T(8,128)(2,1)S(1)} %pad_maximum_fusion.27), channel_id=1, source_target_pairs={{0,4},{1,5},{2,6},{3,7},{4,0},{5,1},{6,2},{7,3},{8,12},{9,13},{10,... | collective-permute-start | bytes 393224 | tf_op jit(solution)/shard_map/ppermute | solution.py:76
  112.9 1.3 collective-permute-start.17
  114.3 1.7 %collective-permute-start.5 = (f32[2,1,1,1,1,1,16,512]{7,6,5,4,3,2,1,0:T(8,128)S(1)}, f32[2,1,1,1,1,1,16,512]{7,6,5,4,3,2,1,0:T(8,128)S(1)}, u32[]{:S(2)}, u32[]{:S(2)}) collective-permute-start(f32[2,1,1,1,1,1,16,512]{7,6,5,4,3,2,1,0:T(8,128)S(1)} %constant_dynamic-slice_fusion.15), channel_id=1, source_target_pairs={{0,16},{1,17},{2,18},{3,19},{4,20},{5,21},{6,22},{7,23},{8,24},{9,... | collective-permute-start | bytes 196616 | tf_op jit(solution)/shard_map/ppermute | solution.py:67
  116.6 1.5 collective-permute-start.43
  119.5 2.4 %collective-permute-start.35 = (bf16[2,1,1,1,1,1,16,512]{7,6,5,4,3,2,1,0:T(8,128)(2,1)S(1)}, bf16[2,1,1,1,1,1,16,512]{7,6,5,4,3,2,1,0:T(8,128)(2,1)S(1)}, u32[]{:S(2)}, u32[]{:S(2)}) collective-permute-start(bf16[2,1,1,1,1,1,16,512]{7,6,5,4,3,2,1,0:T(8,128)(2,1)S(1)} %get-tuple-element.78), channel_id=1, source_target_pairs={{0,16},{1,17},{2,18},{3,19},{4,20},{5,21},{6,22},{7,23},{8,24},{9,... | collective-permute-start | bytes 98312 | tf_op jit(solution)/shard_map/ppermute | solution.py:76
  123.0 2.3 %collective-permute-start.25 = (bf16[2,1,1,1,1,1,16,512]{7,6,5,4,3,2,1,0:T(8,128)(2,1)S(1)}, bf16[2,1,1,1,1,1,16,512]{7,6,5,4,3,2,1,0:T(8,128)(2,1)S(1)}, u32[]{:S(2)}, u32[]{:S(2)}) collective-permute-start(bf16[2,1,1,1,1,1,16,512]{7,6,5,4,3,2,1,0:T(8,128)(2,1)S(1)} %get-tuple-element.74), channel_id=1, source_target_pairs={{0,16},{1,17},{2,18},{3,19},{4,20},{5,21},{6,22},{7,23},{8,24},{9,... | collective-permute-start | bytes 98312 | tf_op jit(solution)/shard_map/ppermute | solution.py:76
  125.3 1.2 collective-permute-start.36
  126.5 1.3 collective-permute-done.25
  127.8 1.9 %collective-permute-start.26 = (bf16[2,2,1,1,1,1,16,512]{7,6,5,4,3,2,1,0:T(8,128)(2,1)S(1)}, bf16[2,2,1,1,1,1,16,512]{7,6,5,4,3,2,1,0:T(8,128)(2,1)S(1)}, u32[]{:S(2)}, u32[]{:S(2)}) collective-permute-start(bf16[2,2,1,1,1,1,16,512]{7,6,5,4,3,2,1,0:T(8,128)(2,1)S(1)} %pad_maximum_fusion.28), channel_id=1, source_target_pairs={{0,8},{1,9},{2,10},{3,11},{4,12},{5,13},{6,14},{7,15},{8,0},{9,1},... | collective-permute-start | bytes 196616 | tf_op jit(solution)/shard_map/ppermute | solution.py:76
  129.8 1.1 collective-permute-start.37
  130.9 1.2 collective-permute-done.26
  132.2 1.7 %collective-permute-start.27 = (bf16[2,2,2,1,1,1,16,512]{7,6,5,4,3,2,1,0:T(8,128)(2,1)S(1)}, bf16[2,2,2,1,1,1,16,512]{7,6,5,4,3,2,1,0:T(8,128)(2,1)S(1)}, u32[]{:S(2)}, u32[]{:S(2)}) collective-permute-start(bf16[2,2,2,1,1,1,16,512]{7,6,5,4,3,2,1,0:T(8,128)(2,1)S(1)} %pad_maximum_fusion.24), channel_id=1, source_target_pairs={{0,4},{1,5},{2,6},{3,7},{4,0},{5,1},{6,2},{7,3},{8,12},{9,13},{10,... | collective-permute-start | bytes 393224 | tf_op jit(solution)/shard_map/ppermute | solution.py:76
  134.9 0.9 collective-permute-start.38
  135.8 1.4 collective-permute-done.27
  137.3 1.7 %collective-permute-start.28 = (bf16[2,2,2,2,1,1,16,512]{7,6,5,4,3,2,1,0:T(8,128)(2,1)S(1)}, bf16[2,2,2,2,1,1,16,512]{7,6,5,4,3,2,1,0:T(8,128)(2,1)S(1)}, u32[]{:S(2)}, u32[]{:S(2)}) collective-permute-start(bf16[2,2,2,2,1,1,16,512]{7,6,5,4,3,2,1,0:T(8,128)(2,1)S(1)} %pad_maximum_fusion.19), channel_id=1, source_target_pairs={{0,1},{1,0},{2,3},{3,2},{4,5},{5,4},{6,7},{7,6},{8,9},{9,8},{10,11... | collective-permute-start | bytes 786440 | tf_op jit(solution)/shard_map/ppermute | solution.py:76
  140.0 3.2 %collective-permute-done.38 = bf16[2,2,1,2,1,2,16,512]{7,6,5,4,3,2,1,0:T(8,128)(2,1)S(1)} collective-permute-done((bf16[2,2,1,2,1,2,16,512]{7,6,5,4,3,2,1,0:T(8,128)(2,1)S(1)}, bf16[2,2,1,2,1,2,16,512]{7,6,5,4,3,2,1,0:T(8,128)(2,1)S(1)}, u32[]{:S(2)}, u32[]{:S(2)}) %collective-permute-start.38) | collective-permute-done | bytes 262176 | tf_op jit(solution)/shard_map/ppermute | solution.py:76
  144.1 0.9 pad_maximum_fusion.11
  145.6 1.1 copy-done.6
  148.1 1.1 copy-done.7
  149.2 1.5 convolution_convert_fusion.5
  150.7 1.4 stack_reshape.13
  152.1 1.1 broadcast_select_fusion.3
  154.0 1.1 stack_reshape.14
  155.1 1.1 broadcast_select_fusion.7
  157.1 1.1 stack_reshape.12
  158.2 1.5 pad_maximum_fusion
  159.6 2.0 %gather_fusion.1 = bf16[4,2,64,2048]{3,2,1,0:T(8,128)(2,1)} fusion(bf16[4,2,64,2048]{3,2,1,0:T(8,128)(2,1)S(1)} %pad_maximum_fusion, s32[1024]{0:T(1024)S(1)} %pad_clamp_fusion), kind=kCustom, calls=%fused_computation.1 | custom fusion | bytes 4194320 | tf_op jit(solution)/shard_map/jit(_take)/gather | solution.py:159
  (244 shorter events, 29.9 us)
Async XLA Ops:
  0.6 3.8 %copy-start = (bf16[2,3,4,4,16,512]{5,4,3,2,1,0:T(8,128)(2,1)S(1)}, bf16[2,3,4,4,16,512]{5,4,3,2,1,0:T(8,128)(2,1)}, u32[]{:S(2)}) copy-start(bf16[2,3,4,4,16,512]{5,4,3,2,1,0:T(8,128)(2,1)} %param.5) | copy-start | bytes 4718596
  2.4 2.6 %copy-start.13 = (f32[4,4,16]{2,1,0:T(4,128)}, f32[4,4,16]{2,1,0:T(4,128)S(1)}, u32[]{:S(2)}) copy-start(f32[4,4,16]{2,1,0:T(4,128)S(1)} %get-tuple-element.108) | copy-start | bytes 3076
  2.4 2.7 %copy-start.15 = (f32[4,4,16]{2,1,0:T(4,128)}, f32[4,4,16]{2,1,0:T(4,128)S(1)}, u32[]{:S(2)}) copy-start(f32[4,4,16]{2,1,0:T(4,128)S(1)} %get-tuple-element.110) | copy-start | bytes 3076
  2.4 2.7 %copy-start.17 = (f32[4,4,16]{2,1,0:T(4,128)}, f32[4,4,16]{2,1,0:T(4,128)S(1)}, u32[]{:S(2)}) copy-start(f32[4,4,16]{2,1,0:T(4,128)S(1)} %get-tuple-element.111) | copy-start | bytes 3076
  5.9 4.1 %copy-start.3 = (bf16[1,3,4,4,16,512]{5,4,3,2,1,0:T(8,128)(2,1)}, bf16[1,3,4,4,16,512]{5,4,3,2,1,0:T(8,128)(2,1)S(1)}, u32[]{:S(2)}) copy-start(bf16[1,3,4,4,16,512]{5,4,3,2,1,0:T(8,128)(2,1)S(1)} %maximum_bitcast_fusion.6) | copy-start | bytes 2359300
  7.0 36.6 %collective-permute-start.18 = (bf16[2,3,4,4,1,512]{5,4,3,2,1,0:T(2,128)(2,1)}, bf16[2,3,4,4,1,512]{5,4,3,2,1,0:T(2,128)(2,1)}, u32[]{:S(2)}, u32[]{:S(2)}) collective-permute-start(bf16[2,3,4,4,1,512]{5,4,3,2,1,0:T(2,128)(2,1)} %pad_maximum_fusion.23), channel_id=1, source_target_pairs={{0,1},{1,0},{2,3},{3,2},{4,5},{5,4},{6,7},{7,6},{8,9},{9,8},{10,11... | collective-permute-start | bytes 294920 | tf_op jit(solution)/shard_map/ppermute | solution.py:97
  13.5 40.9 %collective-permute-start.12 = (bf16[2,3,4,1,16,512]{5,4,3,2,1,0:T(8,128)(2,1)}, bf16[2,3,4,1,16,512]{5,4,3,2,1,0:T(8,128)(2,1)}, u32[]{:S(2)}, u32[]{:S(2)}) collective-permute-start(bf16[2,3,4,1,16,512]{5,4,3,2,1,0:T(8,128)(2,1)} %pad_maximum_fusion.15), channel_id=1, source_target_pairs={{0,2},{2,4},{4,6},{6,8},{8,10},{10,12},{12,14},{14,16},{16,18},{18... | collective-permute-start | bytes 1179656 | tf_op jit(solution)/shard_map/ppermute | solution.py:95
  14.3 33.1 %collective-permute-start.6 = (bf16[2,3,4,4,1,512]{5,4,3,2,1,0:T(2,128)(2,1)}, bf16[2,3,4,4,1,512]{5,4,3,2,1,0:T(2,128)(2,1)}, u32[]{:S(2)}, u32[]{:S(2)}) collective-permute-start(bf16[2,3,4,4,1,512]{5,4,3,2,1,0:T(2,128)(2,1)} %slice.170), channel_id=1, source_target_pairs={{0,1},{1,0},{2,3},{3,2},{4,5},{5,4},{6,7},{7,6},{8,9},{9,8},{10,11... | collective-permute-start | bytes 294920 | tf_op jit(solution)/shard_map/ppermute | solution.py:96
  15.1 43.0 %collective-permute-start = (bf16[2,3,4,1,16,512]{5,4,3,2,1,0:T(8,128)(2,1)}, bf16[2,3,4,1,16,512]{5,4,3,2,1,0:T(8,128)(2,1)}, u32[]{:S(2)}, u32[]{:S(2)}) collective-permute-start(bf16[2,3,4,1,16,512]{5,4,3,2,1,0:T(8,128)(2,1)} %slice.143), channel_id=1, source_target_pairs={{0,30},{2,0},{4,2},{6,4},{8,6},{10,8},{12,10},{14,12},{16,14},{18,... | collective-permute-start | bytes 1179656 | tf_op jit(solution)/shard_map/ppermute | solution.py:94
  22.8 2.7 %copy-start.8 = (bf16[1,3,4,4,16,512]{5,4,3,2,1,0:T(8,128)(2,1)S(1)}, bf16[1,3,4,4,16,512]{5,4,3,2,1,0:T(8,128)(2,1)}, u32[]{:S(2)}) copy-start(bf16[1,3,4,4,16,512]{5,4,3,2,1,0:T(8,128)(2,1)} %get-tuple-element.40) | copy-start | bytes 2359300
  25.5 1.8 %copy-start.12 = (bf16[2,64,2048]{2,1,0:T(8,128)(2,1)S(1)}, bf16[2,64,2048]{2,1,0:T(8,128)(2,1)}, u32[]{:S(2)}) copy-start(bf16[2,64,2048]{2,1,0:T(8,128)(2,1)} %param.9) | copy-start | bytes 1572868
  25.5 2.2 %copy-start.34 = (s32[4]{0:T(128)S(1)}, s32[4]{0:T(128)}, u32[]{:S(2)}) copy-start(s32[4]{0:T(128)} %param.8) | copy-start | bytes 52
  28.6 1.3 copy-start.9
  28.6 1.7 %copy-start.10 = (bf16[512,768]{1,0:T(8,128)(2,1)S(1)}, bf16[512,768]{1,0:T(8,128)(2,1)}, u32[]{:S(2)}) copy-start(bf16[512,768]{1,0:T(8,128)(2,1)} %get-tuple-element.152) | copy-start | bytes 2359300
  28.6 2.0 %copy-start.11 = (bf16[512,768]{1,0:T(8,128)(2,1)S(1)}, bf16[512,768]{1,0:T(8,128)(2,1)}, u32[]{:S(2)}) copy-start(bf16[512,768]{1,0:T(8,128)(2,1)} %get-tuple-element.153) | copy-start | bytes 2359300
  30.6 13.0 %copy-start.35 = (s32[4]{0:T(128)S(1)}, s32[4]{0:T(128)}, u32[]{:S(2)}) copy-start(s32[4]{0:T(128)} %param.7) | copy-start | bytes 52
  30.6 13.1 %copy-start.2 = (bf16[1,3,4,4,16,512]{5,4,3,2,1,0:T(8,128)(2,1)S(1)}, bf16[1,3,4,4,16,512]{5,4,3,2,1,0:T(8,128)(2,1)}, u32[]{:S(2)}) copy-start(bf16[1,3,4,4,16,512]{5,4,3,2,1,0:T(8,128)(2,1)} %copy-done.1) | copy-start | bytes 2359300
  30.6 13.1 %copy-start.4 = (bf16[1,3,4,4,16,512]{5,4,3,2,1,0:T(8,128)(2,1)S(1)}, bf16[1,3,4,4,16,512]{5,4,3,2,1,0:T(8,128)(2,1)}, u32[]{:S(2)}) copy-start(bf16[1,3,4,4,16,512]{5,4,3,2,1,0:T(8,128)(2,1)} %copy-done.3) | copy-start | bytes 2359300
  47.2 1.4 copy-start.5
  47.2 1.4 copy-start.19
  47.2 1.4 copy-start.20
  47.2 1.4 copy-start.21
  47.3 17.6 %collective-permute-start.19 = (f32[2,2,2,2,1,2,16,512]{7,6,0,5,4,3,2,1:T(8,128)S(1)}, f32[2,2,2,2,1,2,16,512]{7,6,0,5,4,3,2,1:T(8,128)S(1)}, u32[]{:S(2)}, u32[]{:S(2)}) collective-permute-start(f32[2,2,2,2,1,2,16,512]{7,6,0,5,4,3,2,1:T(8,128)S(1)} %constant_dynamic-slice_fusion.4), channel_id=1, source_target_pairs={{0,2},{1,3},{2,0},{3,1},{4,6},{5,7},{6,4},{7,5},{8,10},{9,11},{10,... | collective-permute-start | bytes 3145736 | tf_op jit(solution)/shard_map/ppermute | solution.py:67
  54.3 12.7 %collective-permute-start.7 = (f32[2,2,2,2,1,2,16,512]{7,6,0,5,4,3,2,1:T(8,128)S(1)}, f32[2,2,2,2,1,2,16,512]{7,6,0,5,4,3,2,1:T(8,128)S(1)}, u32[]{:S(2)}, u32[]{:S(2)}) collective-permute-start(f32[2,2,2,2,1,2,16,512]{7,6,0,5,4,3,2,1:T(8,128)S(1)} %constant_dynamic-slice_fusion.14), channel_id=1, source_target_pairs={{0,2},{1,3},{2,0},{3,1},{4,6},{5,7},{6,4},{7,5},{8,10},{9,11},{10,... | collective-permute-start | bytes 3145736 | tf_op jit(solution)/shard_map/ppermute | solution.py:67
  57.4 1.3 slice-start
  57.5 9.9 %collective-permute-start.13 = (f32[2,2,2,2,1,2,16,512]{7,6,5,4,3,2,1,0:T(8,128)S(1)}, f32[2,2,2,2,1,2,16,512]{7,6,5,4,3,2,1,0:T(8,128)S(1)}, u32[]{:S(2)}, u32[]{:S(2)}) collective-permute-start(f32[2,2,2,2,1,2,16,512]{7,6,5,4,3,2,1,0:T(8,128)S(1)} %constant_dynamic-slice_fusion.9), channel_id=1, source_target_pairs={{0,2},{1,3},{2,0},{3,1},{4,6},{5,7},{6,4},{7,5},{8,10},{9,11},{10,... | collective-permute-start | bytes 3145736 | tf_op jit(solution)/shard_map/ppermute | solution.py:67
  64.4 3.7 %collective-permute-start.1 = (f32[2,2,2,2,1,2,16,512]{7,6,5,4,3,2,1,0:T(8,128)S(1)}, f32[2,2,2,2,1,2,16,512]{7,6,5,4,3,2,1,0:T(8,128)S(1)}, u32[]{:S(2)}, u32[]{:S(2)}) collective-permute-start(f32[2,2,2,2,1,2,16,512]{7,6,5,4,3,2,1,0:T(8,128)S(1)} %constant_dynamic-slice_fusion.19), channel_id=1, source_target_pairs={{0,2},{1,3},{2,0},{3,1},{4,6},{5,7},{6,4},{7,5},{8,10},{9,11},{10,... | collective-permute-start | bytes 3145736 | tf_op jit(solution)/shard_map/ppermute | solution.py:67
  65.2 14.9 %collective-permute-start.20 = (f32[2,2,2,2,1,1,16,512]{7,6,0,5,4,3,2,1:T(8,128)S(1)}, f32[2,2,2,2,1,1,16,512]{7,6,0,5,4,3,2,1:T(8,128)S(1)}, u32[]{:S(2)}, u32[]{:S(2)}) collective-permute-start(f32[2,2,2,2,1,1,16,512]{7,6,0,5,4,3,2,1:T(8,128)S(1)} %constant_dynamic-slice_fusion.3), channel_id=1, source_target_pairs={{0,1},{1,0},{2,3},{3,2},{4,5},{5,4},{6,7},{7,6},{8,9},{9,8},{10,11... | collective-permute-start | bytes 1572872 | tf_op jit(solution)/shard_map/ppermute | solution.py:67
  67.3 13.6 %collective-permute-start.8 = (f32[2,2,2,1,1,2,16,512]{7,6,0,5,4,3,2,1:T(8,128)S(1)}, f32[2,2,2,1,1,2,16,512]{7,6,0,5,4,3,2,1:T(8,128)S(1)}, u32[]{:S(2)}, u32[]{:S(2)}) collective-permute-start(f32[2,2,2,1,1,2,16,512]{7,6,0,5,4,3,2,1:T(8,128)S(1)} %constant_dynamic-slice_fusion.13), channel_id=1, source_target_pairs={{0,4},{1,5},{2,6},{3,7},{4,0},{5,1},{6,2},{7,3},{8,12},{9,13},{10,... | collective-permute-start | bytes 1572872 | tf_op jit(solution)/shard_map/ppermute | solution.py:67
  67.7 22.1 %collective-permute-start.14 = (f32[2,2,1,2,1,2,16,512]{7,6,5,4,3,2,1,0:T(8,128)S(1)}, f32[2,2,1,2,1,2,16,512]{7,6,5,4,3,2,1,0:T(8,128)S(1)}, u32[]{:S(2)}, u32[]{:S(2)}) collective-permute-start(f32[2,2,1,2,1,2,16,512]{7,6,5,4,3,2,1,0:T(8,128)S(1)} %constant_dynamic-slice_fusion.8), channel_id=1, source_target_pairs={{0,8},{1,9},{2,10},{3,11},{4,12},{5,13},{6,14},{7,15},{8,0},{9,1},... | collective-permute-start | bytes 1572872 | tf_op jit(solution)/shard_map/ppermute | solution.py:67
  68.4 23.6 %collective-permute-start.2 = (f32[2,2,2,2,1,1,16,512]{7,6,5,4,3,2,1,0:T(8,128)S(1)}, f32[2,2,2,2,1,1,16,512]{7,6,5,4,3,2,1,0:T(8,128)S(1)}, u32[]{:S(2)}, u32[]{:S(2)}) collective-permute-start(f32[2,2,2,2,1,1,16,512]{7,6,5,4,3,2,1,0:T(8,128)S(1)} %constant_dynamic-slice_fusion.18), channel_id=1, source_target_pairs={{0,1},{1,0},{2,3},{3,2},{4,5},{5,4},{6,7},{7,6},{8,9},{9,8},{10,11... | collective-permute-start | bytes 1572872 | tf_op jit(solution)/shard_map/ppermute | solution.py:67
  80.2 6.5 %collective-permute-start.21 = (f32[2,2,2,1,1,1,16,512]{7,6,0,5,4,3,2,1:T(8,128)S(1)}, f32[2,2,2,1,1,1,16,512]{7,6,0,5,4,3,2,1:T(8,128)S(1)}, u32[]{:S(2)}, u32[]{:S(2)}) collective-permute-start(f32[2,2,2,1,1,1,16,512]{7,6,0,5,4,3,2,1:T(8,128)S(1)} %constant_dynamic-slice_fusion.2), channel_id=1, source_target_pairs={{0,4},{1,5},{2,6},{3,7},{4,0},{5,1},{6,2},{7,3},{8,12},{9,13},{10,... | collective-permute-start | bytes 786440 | tf_op jit(solution)/shard_map/ppermute | solution.py:67
  81.1 8.6 %collective-permute-start.9 = (f32[2,2,1,1,1,2,16,512]{7,6,0,5,4,3,2,1:T(8,128)S(1)}, f32[2,2,1,1,1,2,16,512]{7,6,0,5,4,3,2,1:T(8,128)S(1)}, u32[]{:S(2)}, u32[]{:S(2)}) collective-permute-start(f32[2,2,1,1,1,2,16,512]{7,6,0,5,4,3,2,1:T(8,128)S(1)} %constant_dynamic-slice_fusion.12), channel_id=1, source_target_pairs={{0,8},{1,9},{2,10},{3,11},{4,12},{5,13},{6,14},{7,15},{8,0},{9,1},... | collective-permute-start | bytes 786440 | tf_op jit(solution)/shard_map/ppermute | solution.py:67
  86.8 6.1 %collective-permute-start.22 = (f32[2,2,1,1,1,1,16,512]{7,6,0,5,4,3,2,1:T(8,128)S(1)}, f32[2,2,1,1,1,1,16,512]{7,6,0,5,4,3,2,1:T(8,128)S(1)}, u32[]{:S(2)}, u32[]{:S(2)}) collective-permute-start(f32[2,2,1,1,1,1,16,512]{7,6,0,5,4,3,2,1:T(8,128)S(1)} %constant_dynamic-slice_fusion.1), channel_id=1, source_target_pairs={{0,8},{1,9},{2,10},{3,11},{4,12},{5,13},{6,14},{7,15},{8,0},{9,1},... | collective-permute-start | bytes 393224 | tf_op jit(solution)/shard_map/ppermute | solution.py:67
  89.7 6.3 %collective-permute-start.10 = (f32[2,2,1,1,1,1,16,512]{7,6,0,5,4,3,2,1:T(8,128)S(1)}, f32[2,2,1,1,1,1,16,512]{7,6,0,5,4,3,2,1:T(8,128)S(1)}, u32[]{:S(2)}, u32[]{:S(2)}) collective-permute-start(f32[2,2,1,1,1,1,16,512]{7,6,0,5,4,3,2,1:T(8,128)S(1)} %constant_dynamic-slice_fusion.11), channel_id=1, source_target_pairs={{0,1},{1,0},{2,3},{3,2},{4,5},{5,4},{6,7},{7,6},{8,9},{9,8},{10,11... | collective-permute-start | bytes 393224 | tf_op jit(solution)/shard_map/ppermute | solution.py:67
  90.0 17.8 %collective-permute-start.15 = (f32[2,2,1,2,1,1,16,512]{7,6,5,4,3,2,1,0:T(8,128)S(1)}, f32[2,2,1,2,1,1,16,512]{7,6,5,4,3,2,1,0:T(8,128)S(1)}, u32[]{:S(2)}, u32[]{:S(2)}) collective-permute-start(f32[2,2,1,2,1,1,16,512]{7,6,5,4,3,2,1,0:T(8,128)S(1)} %constant_dynamic-slice_fusion.7), channel_id=1, source_target_pairs={{0,1},{1,0},{2,3},{3,2},{4,5},{5,4},{6,7},{7,6},{8,9},{9,8},{10,11... | collective-permute-start | bytes 786440 | tf_op jit(solution)/shard_map/ppermute | solution.py:67
  92.2 17.0 %collective-permute-start.3 = (f32[2,2,2,1,1,1,16,512]{7,6,5,4,3,2,1,0:T(8,128)S(1)}, f32[2,2,2,1,1,1,16,512]{7,6,5,4,3,2,1,0:T(8,128)S(1)}, u32[]{:S(2)}, u32[]{:S(2)}) collective-permute-start(f32[2,2,2,1,1,1,16,512]{7,6,5,4,3,2,1,0:T(8,128)S(1)} %constant_dynamic-slice_fusion.17), channel_id=1, source_target_pairs={{0,4},{1,5},{2,6},{3,7},{4,0},{5,1},{6,2},{7,3},{8,12},{9,13},{10,... | collective-permute-start | bytes 786440 | tf_op jit(solution)/shard_map/ppermute | solution.py:67
  92.9 6.3 %collective-permute-start.23 = (f32[2,1,1,1,1,1,16,512]{7,6,0,5,4,3,2,1:T(8,128)S(1)}, f32[2,1,1,1,1,1,16,512]{7,6,0,5,4,3,2,1:T(8,128)S(1)}, u32[]{:S(2)}, u32[]{:S(2)}) collective-permute-start(f32[2,1,1,1,1,1,16,512]{7,6,0,5,4,3,2,1:T(8,128)S(1)} %constant_dynamic-slice_fusion), channel_id=1, source_target_pairs={{0,16},{1,17},{2,18},{3,19},{4,20},{5,21},{6,22},{7,23},{8,24},{9,... | collective-permute-start | bytes 196616 | tf_op jit(solution)/shard_map/ppermute | solution.py:67
  96.0 6.1 %collective-permute-start.11 = (f32[2,1,1,1,1,1,16,512]{7,6,0,5,4,3,2,1:T(8,128)S(1)}, f32[2,1,1,1,1,1,16,512]{7,6,0,5,4,3,2,1:T(8,128)S(1)}, u32[]{:S(2)}, u32[]{:S(2)}) collective-permute-start(f32[2,1,1,1,1,1,16,512]{7,6,0,5,4,3,2,1:T(8,128)S(1)} %constant_dynamic-slice_fusion.10), channel_id=1, source_target_pairs={{0,16},{1,17},{2,18},{3,19},{4,20},{5,21},{6,22},{7,23},{8,24},{9,... | collective-permute-start | bytes 196616 | tf_op jit(solution)/shard_map/ppermute | solution.py:67
  99.2 4.9 %collective-permute-start.40 = (bf16[2,1,1,1,1,1,16,512]{7,6,5,4,3,2,1,0:T(8,128)(2,1)S(1)}, bf16[2,1,1,1,1,1,16,512]{7,6,5,4,3,2,1,0:T(8,128)(2,1)S(1)}, u32[]{:S(2)}, u32[]{:S(2)}) collective-permute-start(bf16[2,1,1,1,1,1,16,512]{7,6,5,4,3,2,1,0:T(8,128)(2,1)S(1)} %get-tuple-element.80), channel_id=1, source_target_pairs={{0,16},{1,17},{2,18},{3,19},{4,20},{5,21},{6,22},{7,23},{8,24},{9,... | collective-permute-start | bytes 98312 | tf_op jit(solution)/shard_map/ppermute | solution.py:76
  102.2 5.0 %collective-permute-start.30 = (bf16[2,1,1,1,1,1,16,512]{7,6,0,5,4,3,2,1:T(8,128)(2,1)S(1)}, bf16[2,1,1,1,1,1,16,512]{7,6,0,5,4,3,2,1:T(8,128)(2,1)S(1)}, u32[]{:S(2)}, u32[]{:S(2)}) collective-permute-start(bf16[2,1,1,1,1,1,16,512]{7,6,0,5,4,3,2,1:T(8,128)(2,1)S(1)} %get-tuple-element.76), channel_id=1, source_target_pairs={{0,16},{1,17},{2,18},{3,19},{4,20},{5,21},{6,22},{7,23},{8,24},{9,... | collective-permute-start | bytes 98312 | tf_op jit(solution)/shard_map/ppermute | solution.py:76
  104.1 5.9 %collective-permute-start.41 = (bf16[2,2,1,1,1,1,16,512]{7,6,5,4,3,2,1,0:T(8,128)(2,1)S(1)}, bf16[2,2,1,1,1,1,16,512]{7,6,5,4,3,2,1,0:T(8,128)(2,1)S(1)}, u32[]{:S(2)}, u32[]{:S(2)}) collective-permute-start(bf16[2,2,1,1,1,1,16,512]{7,6,5,4,3,2,1,0:T(8,128)(2,1)S(1)} %pad_maximum_fusion.31), channel_id=1, source_target_pairs={{0,8},{1,9},{2,10},{3,11},{4,12},{5,13},{6,14},{7,15},{8,0},{9,1},... | collective-permute-start | bytes 196616 | tf_op jit(solution)/shard_map/ppermute | solution.py:76
  107.2 4.9 %collective-permute-start.31 = (bf16[2,2,1,1,1,1,16,512]{7,6,0,5,4,3,2,1:T(8,128)(2,1)S(1)}, bf16[2,2,1,1,1,1,16,512]{7,6,0,5,4,3,2,1:T(8,128)(2,1)S(1)}, u32[]{:S(2)}, u32[]{:S(2)}) collective-permute-start(bf16[2,2,1,1,1,1,16,512]{7,6,0,5,4,3,2,1:T(8,128)(2,1)S(1)} %pad_maximum_fusion.29), channel_id=1, source_target_pairs={{0,1},{1,0},{2,3},{3,2},{4,5},{5,4},{6,7},{7,6},{8,9},{9,8},{10,11... | collective-permute-start | bytes 196616 | tf_op jit(solution)/shard_map/ppermute | solution.py:76
  107.8 5.1 %collective-permute-start.16 = (f32[2,2,1,1,1,1,16,512]{7,6,5,4,3,2,1,0:T(8,128)S(1)}, f32[2,2,1,1,1,1,16,512]{7,6,5,4,3,2,1,0:T(8,128)S(1)}, u32[]{:S(2)}, u32[]{:S(2)}) collective-permute-start(f32[2,2,1,1,1,1,16,512]{7,6,5,4,3,2,1,0:T(8,128)S(1)} %constant_dynamic-slice_fusion.6), channel_id=1, source_target_pairs={{0,4},{1,5},{2,6},{3,7},{4,0},{5,1},{6,2},{7,3},{8,12},{9,13},{10,... | collective-permute-start | bytes 393224 | tf_op jit(solution)/shard_map/ppermute | solution.py:67
  109.2 5.1 %collective-permute-start.4 = (f32[2,2,1,1,1,1,16,512]{7,6,5,4,3,2,1,0:T(8,128)S(1)}, f32[2,2,1,1,1,1,16,512]{7,6,5,4,3,2,1,0:T(8,128)S(1)}, u32[]{:S(2)}, u32[]{:S(2)}) collective-permute-start(f32[2,2,1,1,1,1,16,512]{7,6,5,4,3,2,1,0:T(8,128)S(1)} %constant_dynamic-slice_fusion.16), channel_id=1, source_target_pairs={{0,8},{1,9},{2,10},{3,11},{4,12},{5,13},{6,14},{7,15},{8,0},{9,1},... | collective-permute-start | bytes 393224 | tf_op jit(solution)/shard_map/ppermute | solution.py:67
  110.1 6.4 %collective-permute-start.42 = (bf16[2,2,2,1,1,1,16,512]{7,6,5,4,3,2,1,0:T(8,128)(2,1)S(1)}, bf16[2,2,2,1,1,1,16,512]{7,6,5,4,3,2,1,0:T(8,128)(2,1)S(1)}, u32[]{:S(2)}, u32[]{:S(2)}) collective-permute-start(bf16[2,2,2,1,1,1,16,512]{7,6,5,4,3,2,1,0:T(8,128)(2,1)S(1)} %pad_maximum_fusion.27), channel_id=1, source_target_pairs={{0,4},{1,5},{2,6},{3,7},{4,0},{5,1},{6,2},{7,3},{8,12},{9,13},{10,... | collective-permute-start | bytes 393224 | tf_op jit(solution)/shard_map/ppermute | solution.py:76
  112.1 5.9 %collective-permute-start.32 = (bf16[2,2,1,1,1,2,16,512]{7,6,0,5,4,3,2,1:T(8,128)(2,1)S(1)}, bf16[2,2,1,1,1,2,16,512]{7,6,0,5,4,3,2,1:T(8,128)(2,1)S(1)}, u32[]{:S(2)}, u32[]{:S(2)}) collective-permute-start(bf16[2,2,1,1,1,2,16,512]{7,6,0,5,4,3,2,1:T(8,128)(2,1)S(1)} %pad_maximum_fusion.25), channel_id=1, source_target_pairs={{0,8},{1,9},{2,10},{3,11},{4,12},{5,13},{6,14},{7,15},{8,0},{9,1},... | collective-permute-start | bytes 393224 | tf_op jit(solution)/shard_map/ppermute | solution.py:76
  112.9 6.5 %collective-permute-start.17 = (f32[2,1,1,1,1,1,16,512]{7,6,5,4,3,2,1,0:T(8,128)S(1)}, f32[2,1,1,1,1,1,16,512]{7,6,5,4,3,2,1,0:T(8,128)S(1)}, u32[]{:S(2)}, u32[]{:S(2)}) collective-permute-start(f32[2,1,1,1,1,1,16,512]{7,6,5,4,3,2,1,0:T(8,128)S(1)} %constant_dynamic-slice_fusion.5), channel_id=1, source_target_pairs={{0,16},{1,17},{2,18},{3,19},{4,20},{5,21},{6,22},{7,23},{8,24},{9,... | collective-permute-start | bytes 196616 | tf_op jit(solution)/shard_map/ppermute | solution.py:67
  114.3 7.6 %collective-permute-start.5 = (f32[2,1,1,1,1,1,16,512]{7,6,5,4,3,2,1,0:T(8,128)S(1)}, f32[2,1,1,1,1,1,16,512]{7,6,5,4,3,2,1,0:T(8,128)S(1)}, u32[]{:S(2)}, u32[]{:S(2)}) collective-permute-start(f32[2,1,1,1,1,1,16,512]{7,6,5,4,3,2,1,0:T(8,128)S(1)} %constant_dynamic-slice_fusion.15), channel_id=1, source_target_pairs={{0,16},{1,17},{2,18},{3,19},{4,20},{5,21},{6,22},{7,23},{8,24},{9,... | collective-permute-start | bytes 196616 | tf_op jit(solution)/shard_map/ppermute | solution.py:67
  116.6 17.3 %collective-permute-start.43 = (bf16[2,2,2,2,1,1,16,512]{7,6,5,4,3,2,1,0:T(8,128)(2,1)S(1)}, bf16[2,2,2,2,1,1,16,512]{7,6,5,4,3,2,1,0:T(8,128)(2,1)S(1)}, u32[]{:S(2)}, u32[]{:S(2)}) collective-permute-start(bf16[2,2,2,2,1,1,16,512]{7,6,5,4,3,2,1,0:T(8,128)(2,1)S(1)} %pad_maximum_fusion.22), channel_id=1, source_target_pairs={{0,1},{1,0},{2,3},{3,2},{4,5},{5,4},{6,7},{7,6},{8,9},{9,8},{10,11... | collective-permute-start | bytes 786440 | tf_op jit(solution)/shard_map/ppermute | solution.py:76
  118.1 16.0 %collective-permute-start.33 = (bf16[2,2,2,1,1,2,16,512]{7,6,0,5,4,3,2,1:T(8,128)(2,1)S(1)}, bf16[2,2,2,1,1,2,16,512]{7,6,0,5,4,3,2,1:T(8,128)(2,1)S(1)}, u32[]{:S(2)}, u32[]{:S(2)}) collective-permute-start(bf16[2,2,2,1,1,2,16,512]{7,6,0,5,4,3,2,1:T(8,128)(2,1)S(1)} %pad_maximum_fusion.20), channel_id=1, source_target_pairs={{0,4},{1,5},{2,6},{3,7},{4,0},{5,1},{6,2},{7,3},{8,12},{9,13},{10,... | collective-permute-start | bytes 786440 | tf_op jit(solution)/shard_map/ppermute | solution.py:76
  119.5 5.8 %collective-permute-start.35 = (bf16[2,1,1,1,1,1,16,512]{7,6,5,4,3,2,1,0:T(8,128)(2,1)S(1)}, bf16[2,1,1,1,1,1,16,512]{7,6,5,4,3,2,1,0:T(8,128)(2,1)S(1)}, u32[]{:S(2)}, u32[]{:S(2)}) collective-permute-start(bf16[2,1,1,1,1,1,16,512]{7,6,5,4,3,2,1,0:T(8,128)(2,1)S(1)} %get-tuple-element.78), channel_id=1, source_target_pairs={{0,16},{1,17},{2,18},{3,19},{4,20},{5,21},{6,22},{7,23},{8,24},{9,... | collective-permute-start | bytes 98312 | tf_op jit(solution)/shard_map/ppermute | solution.py:76
  122.5 16.5 %collective-permute-start.24 = (f32[4,2,1,1,1,1,1,16,512]{8,7,1,0,6,5,4,3,2:T(8,128)S(1)}, f32[4,2,1,1,1,1,1,16,512]{8,7,1,0,6,5,4,3,2:T(8,128)S(1)}, u32[]{:S(2)}, u32[]{:S(2)}) collective-permute-start(f32[4,2,1,1,1,1,1,16,512]{8,7,1,0,6,5,4,3,2:T(8,128)S(1)} %bitcast.362), channel_id=1, source_target_pairs={{0,1},{1,0},{2,3},{3,2},{4,5},{5,4},{6,7},{7,6},{8,9},{9,8},{10,11... | collective-permute-start | bytes 786440 | tf_op jit(solution)/shard_map/ppermute | solution.py:76
  123.0 4.8 %collective-permute-start.25 = (bf16[2,1,1,1,1,1,16,512]{7,6,5,4,3,2,1,0:T(8,128)(2,1)S(1)}, bf16[2,1,1,1,1,1,16,512]{7,6,5,4,3,2,1,0:T(8,128)(2,1)S(1)}, u32[]{:S(2)}, u32[]{:S(2)}) collective-permute-start(bf16[2,1,1,1,1,1,16,512]{7,6,5,4,3,2,1,0:T(8,128)(2,1)S(1)} %get-tuple-element.74), channel_id=1, source_target_pairs={{0,16},{1,17},{2,18},{3,19},{4,20},{5,21},{6,22},{7,23},{8,24},{9,... | collective-permute-start | bytes 98312 | tf_op jit(solution)/shard_map/ppermute | solution.py:76
  125.3 4.5 %collective-permute-start.36 = (bf16[2,2,1,1,1,1,16,512]{7,6,5,4,3,2,1,0:T(8,128)(2,1)S(1)}, bf16[2,2,1,1,1,1,16,512]{7,6,5,4,3,2,1,0:T(8,128)(2,1)S(1)}, u32[]{:S(2)}, u32[]{:S(2)}) collective-permute-start(bf16[2,2,1,1,1,1,16,512]{7,6,5,4,3,2,1,0:T(8,128)(2,1)S(1)} %pad_maximum_fusion.30), channel_id=1, source_target_pairs={{0,4},{1,5},{2,6},{3,7},{4,0},{5,1},{6,2},{7,3},{8,12},{9,13},{10,... | collective-permute-start | bytes 196616 | tf_op jit(solution)/shard_map/ppermute | solution.py:76
  127.8 4.3 %collective-permute-start.26 = (bf16[2,2,1,1,1,1,16,512]{7,6,5,4,3,2,1,0:T(8,128)(2,1)S(1)}, bf16[2,2,1,1,1,1,16,512]{7,6,5,4,3,2,1,0:T(8,128)(2,1)S(1)}, u32[]{:S(2)}, u32[]{:S(2)}) collective-permute-start(bf16[2,2,1,1,1,1,16,512]{7,6,5,4,3,2,1,0:T(8,128)(2,1)S(1)} %pad_maximum_fusion.28), channel_id=1, source_target_pairs={{0,8},{1,9},{2,10},{3,11},{4,12},{5,13},{6,14},{7,15},{8,0},{9,1},... | collective-permute-start | bytes 196616 | tf_op jit(solution)/shard_map/ppermute | solution.py:76
  129.8 5.0 %collective-permute-start.37 = (bf16[2,2,1,2,1,1,16,512]{7,6,5,4,3,2,1,0:T(8,128)(2,1)S(1)}, bf16[2,2,1,2,1,1,16,512]{7,6,5,4,3,2,1,0:T(8,128)(2,1)S(1)}, u32[]{:S(2)}, u32[]{:S(2)}) collective-permute-start(bf16[2,2,1,2,1,1,16,512]{7,6,5,4,3,2,1,0:T(8,128)(2,1)S(1)} %pad_maximum_fusion.26), channel_id=1, source_target_pairs={{0,1},{1,0},{2,3},{3,2},{4,5},{5,4},{6,7},{7,6},{8,9},{9,8},{10,11... | collective-permute-start | bytes 393224 | tf_op jit(solution)/shard_map/ppermute | solution.py:76
  132.2 5.0 %collective-permute-start.27 = (bf16[2,2,2,1,1,1,16,512]{7,6,5,4,3,2,1,0:T(8,128)(2,1)S(1)}, bf16[2,2,2,1,1,1,16,512]{7,6,5,4,3,2,1,0:T(8,128)(2,1)S(1)}, u32[]{:S(2)}, u32[]{:S(2)}) collective-permute-start(bf16[2,2,2,1,1,1,16,512]{7,6,5,4,3,2,1,0:T(8,128)(2,1)S(1)} %pad_maximum_fusion.24), channel_id=1, source_target_pairs={{0,4},{1,5},{2,6},{3,7},{4,0},{5,1},{6,2},{7,3},{8,12},{9,13},{10,... | collective-permute-start | bytes 393224 | tf_op jit(solution)/shard_map/ppermute | solution.py:76
  134.0 11.4 %collective-permute-start.44 = (bf16[2,2,2,2,1,2,16,512]{7,6,5,4,3,2,1,0:T(8,128)(2,1)S(1)}, bf16[2,2,2,2,1,2,16,512]{7,6,5,4,3,2,1,0:T(8,128)(2,1)S(1)}, u32[]{:S(2)}, u32[]{:S(2)}) collective-permute-start(bf16[2,2,2,2,1,2,16,512]{7,6,5,4,3,2,1,0:T(8,128)(2,1)S(1)} %pad_maximum_fusion.14), channel_id=1, source_target_pairs={{0,2},{1,3},{2,0},{3,1},{4,6},{5,7},{6,4},{7,5},{8,10},{9,11},{10,... | collective-permute-start | bytes 1572872 | tf_op jit(solution)/shard_map/ppermute | solution.py:76
  134.2 13.2 %collective-permute-start.34 = (bf16[2,2,2,2,1,2,16,512]{7,6,0,5,4,3,2,1:T(8,128)(2,1)S(1)}, bf16[2,2,2,2,1,2,16,512]{7,6,0,5,4,3,2,1:T(8,128)(2,1)S(1)}, u32[]{:S(2)}, u32[]{:S(2)}) collective-permute-start(bf16[2,2,2,2,1,2,16,512]{7,6,0,5,4,3,2,1:T(8,128)(2,1)S(1)} %pad_maximum_fusion.12), channel_id=1, source_target_pairs={{0,2},{1,3},{2,0},{3,1},{4,6},{5,7},{6,4},{7,5},{8,10},{9,11},{10,... | collective-permute-start | bytes 1572872 | tf_op jit(solution)/shard_map/ppermute | solution.py:76
  134.9 8.2 %collective-permute-start.38 = (bf16[2,2,1,2,1,2,16,512]{7,6,5,4,3,2,1,0:T(8,128)(2,1)S(1)}, bf16[2,2,1,2,1,2,16,512]{7,6,5,4,3,2,1,0:T(8,128)(2,1)S(1)}, u32[]{:S(2)}, u32[]{:S(2)}) collective-permute-start(bf16[2,2,1,2,1,2,16,512]{7,6,5,4,3,2,1,0:T(8,128)(2,1)S(1)} %pad_maximum_fusion.21), channel_id=1, source_target_pairs={{0,8},{1,9},{2,10},{3,11},{4,12},{5,13},{6,14},{7,15},{8,0},{9,1},... | collective-permute-start | bytes 786440 | tf_op jit(solution)/shard_map/ppermute | solution.py:76
  137.3 6.8 %collective-permute-start.28 = (bf16[2,2,2,2,1,1,16,512]{7,6,5,4,3,2,1,0:T(8,128)(2,1)S(1)}, bf16[2,2,2,2,1,1,16,512]{7,6,5,4,3,2,1,0:T(8,128)(2,1)S(1)}, u32[]{:S(2)}, u32[]{:S(2)}) collective-permute-start(bf16[2,2,2,2,1,1,16,512]{7,6,5,4,3,2,1,0:T(8,128)(2,1)S(1)} %pad_maximum_fusion.19), channel_id=1, source_target_pairs={{0,1},{1,0},{2,3},{3,2},{4,5},{5,4},{6,7},{7,6},{8,9},{9,8},{10,11... | collective-permute-start | bytes 786440 | tf_op jit(solution)/shard_map/ppermute | solution.py:76
  144.0 8.1 %collective-permute-start.39 = (bf16[2,2,2,2,1,2,16,512]{7,6,5,4,3,2,1,0:T(8,128)(2,1)}, bf16[2,2,2,2,1,2,16,512]{7,6,5,4,3,2,1,0:T(8,128)(2,1)}, u32[]{:S(2)}, u32[]{:S(2)}) collective-permute-start(bf16[2,2,2,2,1,2,16,512]{7,6,5,4,3,2,1,0:T(8,128)(2,1)} %pad_maximum_fusion.13), channel_id=1, source_target_pairs={{0,2},{1,3},{2,0},{3,1},{4,6},{5,7},{6,4},{7,5},{8,10},{9,11},{10,... | collective-permute-start | bytes 1572872 | tf_op jit(solution)/shard_map/ppermute | solution.py:76
  144.9 10.2 %collective-permute-start.29 = (bf16[2,2,2,2,1,2,16,512]{7,6,5,4,3,2,1,0:T(8,128)(2,1)}, bf16[2,2,2,2,1,2,16,512]{7,6,5,4,3,2,1,0:T(8,128)(2,1)}, u32[]{:S(2)}, u32[]{:S(2)}) collective-permute-start(bf16[2,2,2,2,1,2,16,512]{7,6,5,4,3,2,1,0:T(8,128)(2,1)} %pad_maximum_fusion.11), channel_id=1, source_target_pairs={{0,2},{1,3},{2,0},{3,1},{4,6},{5,7},{6,4},{7,5},{8,10},{9,11},{10,... | collective-permute-start | bytes 1572872 | tf_op jit(solution)/shard_map/ppermute | solution.py:76
  (18 other events, 14.5 us)

commit v12 on v9

--- a/solution.py
+++ b/solution.py
@@ -74,9 +74,11 @@
         ax = lead + nbits - 1 - b
         mine = (idx >> b) & 1
         other = lax.ppermute(buf, ALL, xor_pairs(count, b))
-        lo = jnp.where(mine == 0, buf, other)
-        hi = jnp.where(mine == 0, other, buf)
-        buf = jnp.concatenate([lo, hi], axis=ax)
+        buf = jnp.where(
+            mine == 0,
+            jnp.concatenate([buf, other], axis=ax),
+            jnp.concatenate([other, buf], axis=ax),
+        )
     return buf
 
 

time: 149 us -> 148 us (level)
    concatenate x21 -> x12, other arithmetic: 2.45 us -> 0.32 us  [all_gather(): jnp.concatenate([buf, other], axis=ax)]
    unnamed x111 -> x109, local copies, waits for them, and re-layouts: 4.34 us -> 3.37 us
  transfers between devices with their start and end apart: 45 -> 45, of which waited for: 21 -> 21; matrix products, arithmetic and copies ran while one was open for 32% -> 31% of each run, Pallas kernels for 0% -> 0%
where the time goes in v12:
time: 148 us; the launch traced here: 147 us
  waiting for transfers between devices  47.2 us (32%)
  starting transfers between devices  35 us (24%)
  other arithmetic  26.1 us (18%)
  local copies, waits for them, and re-layouts  20.8 us (14%)
  matrix products  15.8 us (11%)
  between operations  2.17 us (1%)
    ppermute x20, waiting for transfers between devices, reduce_scatter(): buf = keep + lax.ppermute(send, ALL, xor_pairs(count, b))  30 us
    ppermute x21, waiting for transfers between devices, all_gather(): other = lax.ppermute(buf, ALL, xor_pairs(count, b))  17.2 us
    ppermute x21, starting transfers between devices, all_gather(): other = lax.ppermute(buf, ALL, xor_pairs(count, b))  15.9 us
    ppermute x20, starting transfers between devices, reduce_scatter(): buf = keep + lax.ppermute(send, ALL, xor_pairs(count, b))  12.1 us
    dot_general x4, matrix products, local(): jnp.dot(left, field.reshape(2 * depth, nev), preferred_element_type=jnp.f...  7.13 us
    another operation x12, other arithmetic  6.04 us
    dot_general x2, matrix products, local(): lax.dot_general(unit, flat[c], (((1,), (1,)), ((), ())), preferred_elemen...  4.54 us
    ppermute x1, starting transfers between devices, local(): lax.ppermute(ev[:, :, :, 0:1], 'gx', [(i, (i - 1) % nx) for i in range(nx)])  3.96 us
  transfers between devices with their start and end apart: 45, of which 21 were waited for; matrix products, arithmetic and copies ran while one was open for 31% of the time, Pallas kernels for 0%

profile of v12, /device:TPU:0, one launch (start us, length us, event | category | flops | bytes accessed | tf_op | source)
XLA Modules:
  0.0 147.0 jit_solution(16605499322369300892)
XLA Ops:
  0.6 1.0 slice_bitcast_fusion.19
  2.4 1.9 %convert_element_type.82 = f32[2,3,4,4,16,512]{5,4,3,2,1,0:T(8,128)S(1)} convert(bf16[2,3,4,4,16,512]{5,4,3,2,1,0:T(8,128)(2,1)} %param.5) | non-fusion elementwise | flops 786432 | bytes 4718592 | tf_op jit(solution)/shard_map/convert_element_type | solution.py:13
  6.8 1.0 pad_maximum_fusion.11
  7.8 3.0 %collective-permute-start.18 = (bf16[2,3,4,4,1,512]{5,4,3,2,1,0:T(2,128)(2,1)}, bf16[2,3,4,4,1,512]{5,4,3,2,1,0:T(2,128)(2,1)}, u32[]{:S(2)}, u32[]{:S(2)}) collective-permute-start(bf16[2,3,4,4,1,512]{5,4,3,2,1,0:T(2,128)(2,1)} %pad_maximum_fusion.11), channel_id=1, source_target_pairs={{0,1},{1,0},{2,3},{3,2},{4,5},{5,4},{6,7},{7,6},{8,9},{9,8},{10,11... | collective-permute-start | bytes 294920 | tf_op jit(solution)/shard_map/ppermute | solution.py:99
  13.3 0.8 pad_maximum_fusion.7
  15.9 4.0 %collective-permute-start = (bf16[2,3,4,1,16,512]{5,4,3,2,1,0:T(8,128)(2,1)}, bf16[2,3,4,1,16,512]{5,4,3,2,1,0:T(8,128)(2,1)}, u32[]{:S(2)}, u32[]{:S(2)}) collective-permute-start(bf16[2,3,4,1,16,512]{5,4,3,2,1,0:T(8,128)(2,1)} %slice.143), channel_id=1, source_target_pairs={{0,30},{2,0},{4,2},{6,4},{8,6},{10,8},{12,10},{14,12},{16,14},{18,... | collective-permute-start | bytes 1179656 | tf_op jit(solution)/shard_map/ppermute | solution.py:96
  19.8 1.3 fusion.60
  21.1 1.8 %slice.169 = bf16[2,3,4,4,15,512]{5,4,3,2,1,0:T(8,128)(2,1)} slice(bf16[2,3,4,4,16,512]{5,4,3,2,1,0:T(8,128)(2,1)S(1)} %copy-done), slice={[0:2], [0:3], [0:4], [0:4], [1:16], [0:512]} | slice | bytes 2949120 | tf_op jit(solution)/shard_map/slice | solution.py:101
  23.0 2.8 %convolution_convert_fusion.1 = bf16[512,768]{1,0:T(8,128)(2,1)} fusion(bf16[768,512]{1,0:T(8,128)(2,1)} %bitcast.639), kind=kOutput, calls=%fused_computation.19 | convolution fusion | flops 403308544 | bytes 1572864 | tf_op jit(solution)/shard_map/dot_general | solution.py:112
  25.7 1.8 %fusion.62 = (bf16[512,768]{1,0:T(8,128)(2,1)}, bf16[512,768]{1,0:T(8,128)(2,1)}) fusion(bf16[768,512]{1,0:T(8,128)(2,1)S(1)} %bitcast.638), kind=kOutput, calls=%fused_computation.256 | convolution fusion | flops 403701760 | bytes 2359296 | tf_op jit(solution)/shard_map/dot_general | solution.py:112
  28.9 1.1 pad_maximum_fusion.5
  30.0 2.2 %maximum_maximum_fusion = bf16[1024,1536]{1,0:T(8,128)(2,1)S(1)} fusion(bf16[512,768]{1,0:T(8,128)(2,1)} %convolution_convert_fusion.1, bf16[512,768]{1,0:T(8,128)(2,1)} %get-tuple-element.114, bf16[512,768]{1,0:T(8,128)(2,1)} %get-tuple-element.115), kind=kLoop, calls=%fused_computation.2 | loop fusion | flops 12582912 | bytes 5505024 | tf_op jit(solution)/shard_map/concatenate | solution.py:117
  32.4 1.7 %fusion.6 = bf16[2,3,4,4,16,512]{5,4,3,2,1,0:T(8,128)(2,1)S(1)} fusion(bf16[1,3,4,4,16,512]{5,4,3,2,1,0:T(8,128)(2,1)S(1)} %copy-done.2, bf16[1,3,4,4,16,512]{5,4,3,2,1,0:T(8,128)(2,1)S(1)} %copy-done.4, bf16[2,3,4,4,1,512]{5,4,3,2,1,0:T(2,128)(2,1)} %collective-permute-done.18), kind=kLoop, calls=%fused_computation.11 | loop fusion | flops 4718592 | bytes 3244032 | tf_op jit(solution)/shard_map/concatenate | solution.py:106
  34.1 1.8 %fusion.2 = f32[2,2,2,2,2,2,16,512]{7,6,0,5,4,3,2,1:T(8,128)S(1)} fusion(bf16[1536,512,1,1,1,1,1,1]{1,0,2,7,6,5,4,3:T(8,128)(2,1)S(1)} %bitcast.623, bf16[2,2,2,2,2,2,16,1536]{7,6,5,4,3,2,1,0:T(8,128)(2,1)S(1)} %bitcast.618), kind=kOutput, calls=%fused_computation.5 | convolution fusion | flops 1610612736 | bytes 6815744 | tf_op jit(solution)/shard_map/dot_general | solution.py:145
  36.1 1.2 copy.100
  40.2 1.8 %fusion = f32[2,2,2,2,2,2,16,512]{7,6,0,1,5,4,3,2:T(8,128)S(1)} fusion(bf16[1536,512,1,1,1,1,1,1]{1,0,2,3,7,6,5,4:T(8,128)(2,1)S(1)} %bitcast.625, bf16[2,2,2,2,2,2,16,1536]{7,6,5,4,3,2,1,0:T(8,128)(2,1)S(1)} %bitcast.619), kind=kOutput, calls=%fused_computation.3 | convolution fusion | flops 1610612736 | bytes 6815744 | tf_op jit(solution)/shard_map/dot_general | solution.py:145
  42.5 1.2 fusion.7
  43.7 1.8 %fusion.4 = f32[2,2,2,2,2,2,16,512]{7,6,0,5,4,3,2,1:T(8,128)S(1)} fusion(bf16[1536,512,1,1,1,1,1,1]{1,0,2,7,6,5,4,3:T(8,128)(2,1)S(1)} %bitcast.622, bf16[2,2,2,2,2,2,16,1536]{7,6,5,4,3,2,1,0:T(8,128)(2,1)S(1)} %bitcast.620), kind=kOutput, calls=%fused_computation.7 | convolution fusion | flops 1610612736 | bytes 6815744 | tf_op jit(solution)/shard_map/dot_general | solution.py:145
  45.9 0.8 slice-done
  46.8 1.2 maximum_convert_fusion
  50.4 1.8 %fusion.63 = f32[2,2,2,2,2,2,16,512]{7,6,5,4,3,2,1,0:T(8,128)S(1)} fusion(bf16[2,2,2,2,2,2,16,1536]{7,6,5,4,3,2,1,0:T(8,128)(2,1)S(1)} %bitcast.621, bf16[1536,512,1,1,1,1,1,1]{1,0,7,6,5,4,3,2:T(8,128)(2,1)S(1)} %bitcast.624), kind=kOutput, calls=%fused_computation.257 | convolution fusion | flops 1610612736 | bytes 6815744 | tf_op jit(solution)/shard_map/dot_general | solution.py:145
  52.8 1.6 %collective-permute-start.20 = (f32[2,2,2,2,1,1,16,512]{7,6,0,5,4,3,2,1:T(8,128)S(1)}, f32[2,2,2,2,1,1,16,512]{7,6,0,5,4,3,2,1:T(8,128)S(1)}, u32[]{:S(2)}, u32[]{:S(2)}) collective-permute-start(f32[2,2,2,2,1,1,16,512]{7,6,0,5,4,3,2,1:T(8,128)S(1)} %constant_dynamic-slice_fusion.3), channel_id=1, source_target_pairs={{0,1},{1,0},{2,3},{3,2},{4,5},{5,4},{6,7},{7,6},{8,9},{9,8},{10,11... | collective-permute-start | bytes 1572872 | tf_op jit(solution)/shard_map/ppermute | solution.py:67
  55.8 1.2 collective-permute-start.2
  57.0 10.7 %collective-permute-done.20 = f32[2,2,2,2,1,1,16,512]{7,6,0,5,4,3,2,1:T(8,128)S(1)} collective-permute-done((f32[2,2,2,2,1,1,16,512]{7,6,0,5,4,3,2,1:T(8,128)S(1)}, f32[2,2,2,2,1,1,16,512]{7,6,0,5,4,3,2,1:T(8,128)S(1)}, u32[]{:S(2)}, u32[]{:S(2)}) %collective-permute-start.20) | collective-permute-done | bytes 524320 | tf_op jit(solution)/shard_map/ppermute | solution.py:67
  68.9 6.1 %collective-permute-done.21 = f32[2,2,2,1,1,1,16,512]{7,6,0,5,4,3,2,1:T(8,128)S(1)} collective-permute-done((f32[2,2,2,1,1,1,16,512]{7,6,0,5,4,3,2,1:T(8,128)S(1)}, f32[2,2,2,1,1,1,16,512]{7,6,0,5,4,3,2,1:T(8,128)S(1)}, u32[]{:S(2)}, u32[]{:S(2)}) %collective-permute-start.21) | collective-permute-done | bytes 262176 | tf_op jit(solution)/shard_map/ppermute | solution.py:67
  75.1 1.8 %collective-permute-done.9 = f32[2,2,1,1,1,2,16,512]{7,6,0,1,5,4,3,2:T(8,128)S(1)} collective-permute-done((f32[2,2,1,1,1,2,16,512]{7,6,0,1,5,4,3,2:T(8,128)S(1)}, f32[2,2,1,1,1,2,16,512]{7,6,0,1,5,4,3,2:T(8,128)S(1)}, u32[]{:S(2)}, u32[]{:S(2)}) %collective-permute-start.9) | collective-permute-done | bytes 262176 | tf_op jit(solution)/shard_map/ppermute | solution.py:67
  77.2 2.1 %collective-permute-start.15 = (f32[2,2,1,2,1,1,16,512]{7,6,0,5,4,3,2,1:T(8,128)S(1)}, f32[2,2,1,2,1,1,16,512]{7,6,0,5,4,3,2,1:T(8,128)S(1)}, u32[]{:S(2)}, u32[]{:S(2)}) collective-permute-start(f32[2,2,1,2,1,1,16,512]{7,6,0,5,4,3,2,1:T(8,128)S(1)} %constant_dynamic-slice_fusion.7), channel_id=1, source_target_pairs={{0,1},{1,0},{2,3},{3,2},{4,5},{5,4},{6,7},{7,6},{8,9},{9,8},{10,11... | collective-permute-start | bytes 786440 | tf_op jit(solution)/shard_map/ppermute | solution.py:67
  80.1 0.9 collective-permute-start.23
  81.0 2.4 %collective-permute-done.10 = f32[2,2,1,1,1,1,16,512]{7,6,0,1,5,4,3,2:T(8,128)S(1)} collective-permute-done((f32[2,2,1,1,1,1,16,512]{7,6,0,1,5,4,3,2:T(8,128)S(1)}, f32[2,2,1,1,1,1,16,512]{7,6,0,1,5,4,3,2:T(8,128)S(1)}, u32[]{:S(2)}, u32[]{:S(2)}) %collective-permute-start.10) | collective-permute-done | bytes 131104 | tf_op jit(solution)/shard_map/ppermute | solution.py:67
  84.2 2.7 %collective-permute-done.23 = f32[2,1,1,1,1,1,16,512]{7,6,0,5,4,3,2,1:T(8,128)S(1)} collective-permute-done((f32[2,1,1,1,1,1,16,512]{7,6,0,5,4,3,2,1:T(8,128)S(1)}, f32[2,1,1,1,1,1,16,512]{7,6,0,5,4,3,2,1:T(8,128)S(1)}, u32[]{:S(2)}, u32[]{:S(2)}) %collective-permute-start.23) | collective-permute-done | bytes 65568 | tf_op jit(solution)/shard_map/ppermute | solution.py:67
  86.9 2.5 %collective-permute-done.11 = f32[2,1,1,1,1,1,16,512]{7,6,0,1,5,4,3,2:T(8,128)S(1)} collective-permute-done((f32[2,1,1,1,1,1,16,512]{7,6,0,1,5,4,3,2:T(8,128)S(1)}, f32[2,1,1,1,1,1,16,512]{7,6,0,1,5,4,3,2:T(8,128)S(1)}, u32[]{:S(2)}, u32[]{:S(2)}) %collective-permute-start.11) | collective-permute-done | bytes 65568 | tf_op jit(solution)/shard_map/ppermute | solution.py:67
  89.9 1.8 %collective-permute-done.40 = bf16[2,1,1,1,1,1,16,512]{7,6,0,5,4,3,2,1:T(8,128)(2,1)S(1)} collective-permute-done((bf16[2,1,1,1,1,1,16,512]{7,6,0,5,4,3,2,1:T(8,128)(2,1)S(1)}, bf16[2,1,1,1,1,1,16,512]{7,6,0,5,4,3,2,1:T(8,128)(2,1)S(1)}, u32[]{:S(2)}, u32[]{:S(2)}) %collective-permute-start.40) | collective-permute-done | bytes 32800 | tf_op jit(solution)/shard_map/ppermute | solution.py:76
  92.0 2.3 %collective-permute-done.30 = bf16[2,1,1,1,1,1,16,512]{7,6,0,1,5,4,3,2:T(8,128)(2,1)S(1)} collective-permute-done((bf16[2,1,1,1,1,1,16,512]{7,6,0,1,5,4,3,2:T(8,128)(2,1)S(1)}, bf16[2,1,1,1,1,1,16,512]{7,6,0,1,5,4,3,2:T(8,128)(2,1)S(1)}, u32[]{:S(2)}, u32[]{:S(2)}) %collective-permute-start.30) | collective-permute-done | bytes 32800 | tf_op jit(solution)/shard_map/ppermute | solution.py:76
  94.3 1.0 collective-permute-start.31
  95.5 0.9 collective-permute-start.16
  96.8 1.3 collective-permute-start.42
  98.7 1.2 collective-permute-start.32
  100.5 1.1 collective-permute-start.17
  101.6 1.1 collective-permute-done.4
  102.8 0.8 collective-permute-start.5
  103.7 1.1 collective-permute-start.43
  105.3 1.0 collective-permute-done.17
  106.3 1.6 %collective-permute-start.35 = (bf16[2,1,1,1,1,1,16,512]{7,6,0,5,4,3,2,1:T(8,128)(2,1)S(1)}, bf16[2,1,1,1,1,1,16,512]{7,6,0,5,4,3,2,1:T(8,128)(2,1)S(1)}, u32[]{:S(2)}, u32[]{:S(2)}) collective-permute-start(bf16[2,1,1,1,1,1,16,512]{7,6,0,5,4,3,2,1:T(8,128)(2,1)S(1)} %get-tuple-element.38), channel_id=1, source_target_pairs={{0,16},{1,17},{2,18},{3,19},{4,20},{5,21},{6,22},{7,23},{8,24},{9,... | collective-permute-start | bytes 98312 | tf_op jit(solution)/shard_map/ppermute | solution.py:76
  109.0 1.3 collective-permute-start.24
  110.3 1.1 collective-permute-start.25
  111.5 1.2 collective-permute-start.36
  112.7 2.8 %collective-permute-done.25 = bf16[2,1,1,1,1,1,16,512]{7,6,0,5,4,3,2,1:T(8,128)(2,1)S(1)} collective-permute-done((bf16[2,1,1,1,1,1,16,512]{7,6,0,5,4,3,2,1:T(8,128)(2,1)S(1)}, bf16[2,1,1,1,1,1,16,512]{7,6,0,5,4,3,2,1:T(8,128)(2,1)S(1)}, u32[]{:S(2)}, u32[]{:S(2)}) %collective-permute-start.25) | collective-permute-done | bytes 32800 | tf_op jit(solution)/shard_map/ppermute | solution.py:76
  116.5 0.8 collective-permute-start.37
  117.3 2.5 %collective-permute-done.26 = bf16[2,2,1,1,1,1,16,512]{7,6,5,4,3,2,1,0:T(8,128)(2,1)S(1)} collective-permute-done((bf16[2,2,1,1,1,1,16,512]{7,6,5,4,3,2,1,0:T(8,128)(2,1)S(1)}, bf16[2,2,1,1,1,1,16,512]{7,6,5,4,3,2,1,0:T(8,128)(2,1)S(1)}, u32[]{:S(2)}, u32[]{:S(2)}) %collective-permute-start.26) | collective-permute-done | bytes 65568 | tf_op jit(solution)/shard_map/ppermute | solution.py:76
  119.9 0.9 collective-permute-start.27
  121.7 1.2 collective-permute-start.38
  122.9 2.0 %collective-permute-done.27 = bf16[2,2,2,1,1,1,16,512]{7,6,5,4,3,2,1,0:T(8,128)(2,1)S(1)} collective-permute-done((bf16[2,2,2,1,1,1,16,512]{7,6,5,4,3,2,1,0:T(8,128)(2,1)S(1)}, bf16[2,2,2,1,1,1,16,512]{7,6,5,4,3,2,1,0:T(8,128)(2,1)S(1)}, u32[]{:S(2)}, u32[]{:S(2)}) %collective-permute-start.27) | collective-permute-done | bytes 131104 | tf_op jit(solution)/shard_map/ppermute | solution.py:76
  125.8 0.8 copy.109
  126.6 3.4 %collective-permute-done.38 = bf16[2,2,1,2,1,2,16,512]{7,6,0,5,4,3,2,1:T(8,128)(2,1)S(1)} collective-permute-done((bf16[2,2,1,2,1,2,16,512]{7,6,0,5,4,3,2,1:T(8,128)(2,1)S(1)}, bf16[2,2,1,2,1,2,16,512]{7,6,0,5,4,3,2,1:T(8,128)(2,1)S(1)}, u32[]{:S(2)}, u32[]{:S(2)}) %collective-permute-start.38) | collective-permute-done | bytes 262176 | tf_op jit(solution)/shard_map/ppermute | solution.py:76
  130.2 1.3 collective-permute-done.28
  132.0 1.0 copy-done.6
  133.7 1.5 %convolution_convert_fusion.5 = bf16[512,512]{1,0:T(8,128)(2,1)} fusion(bf16[512,1024]{1,0:T(8,128)(2,1)S(1)} %bitcast.631, bf16[1024,512]{1,0:T(8,128)(2,1)S(1)} %bitcast.634), kind=kOutput, calls=%fused_computation.23 | convolution fusion | flops 537133056 | bytes 2621440 | tf_op jit(solution)/shard_map/dot_general | solution.py:152
  135.5 1.4 stack_reshape.13
  136.9 1.3 maximum_select_fusion.2
  139.0 1.1 stack_reshape.14
  140.1 1.4 maximum_select_fusion
  142.4 1.1 stack_reshape.12
  143.5 1.5 pad_maximum_fusion
  145.0 2.0 %gather_fusion.1 = bf16[4,2,64,2048]{3,2,1,0:T(8,128)(2,1)} fusion(bf16[4,2,64,2048]{3,2,1,0:T(8,128)(2,1)S(1)} %pad_maximum_fusion, s32[1024]{0:T(1024)S(1)} %pad_clamp_fusion), kind=kCustom, calls=%fused_computation.1 | custom fusion | bytes 4194320 | tf_op jit(solution)/shard_map/jit(_take)/gather | solution.py:161
  (279 shorter events, 30.2 us)
Async XLA Ops:
  2.3 2.0 %copy-start.10 = (f32[4,4,16]{2,1,0:T(4,128)}, f32[4,4,16]{2,1,0:T(4,128)S(1)}, u32[]{:S(2)}) copy-start(f32[4,4,16]{2,1,0:T(4,128)S(1)} %get-tuple-element.68) | copy-start | bytes 3076
  2.3 2.0 %copy-start.22 = (f32[4,4,16]{2,1,0:T(4,128)}, f32[4,4,16]{2,1,0:T(4,128)S(1)}, u32[]{:S(2)}) copy-start(f32[4,4,16]{2,1,0:T(4,128)S(1)} %get-tuple-element.62) | copy-start | bytes 3076
  2.3 2.5 %copy-start.12 = (f32[4,4,16]{2,1,0:T(4,128)}, f32[4,4,16]{2,1,0:T(4,128)S(1)}, u32[]{:S(2)}) copy-start(f32[4,4,16]{2,1,0:T(4,128)S(1)} %get-tuple-element.70) | copy-start | bytes 3076
  2.3 2.5 %copy-start.24 = (f32[4,4,16]{2,1,0:T(4,128)}, f32[4,4,16]{2,1,0:T(4,128)S(1)}, u32[]{:S(2)}) copy-start(f32[4,4,16]{2,1,0:T(4,128)S(1)} %get-tuple-element.64) | copy-start | bytes 3076
  2.3 3.0 %copy-start.14 = (f32[4,4,16]{2,1,0:T(4,128)}, f32[4,4,16]{2,1,0:T(4,128)S(1)}, u32[]{:S(2)}) copy-start(f32[4,4,16]{2,1,0:T(4,128)S(1)} %get-tuple-element.72) | copy-start | bytes 3076
  2.3 3.0 %copy-start.26 = (f32[4,4,16]{2,1,0:T(4,128)}, f32[4,4,16]{2,1,0:T(4,128)S(1)}, u32[]{:S(2)}) copy-start(f32[4,4,16]{2,1,0:T(4,128)S(1)} %get-tuple-element.66) | copy-start | bytes 3076
  7.8 24.4 %collective-permute-start.18 = (bf16[2,3,4,4,1,512]{5,4,3,2,1,0:T(2,128)(2,1)}, bf16[2,3,4,4,1,512]{5,4,3,2,1,0:T(2,128)(2,1)}, u32[]{:S(2)}, u32[]{:S(2)}) collective-permute-start(bf16[2,3,4,4,1,512]{5,4,3,2,1,0:T(2,128)(2,1)} %pad_maximum_fusion.11), channel_id=1, source_target_pairs={{0,1},{1,0},{2,3},{3,2},{4,5},{5,4},{6,7},{7,6},{8,9},{9,8},{10,11... | collective-permute-start | bytes 294920 | tf_op jit(solution)/shard_map/ppermute | solution.py:99
  13.2 1.6 %copy-start = (bf16[2,3,4,4,16,512]{5,4,3,2,1,0:T(8,128)(2,1)S(1)}, bf16[2,3,4,4,16,512]{5,4,3,2,1,0:T(8,128)(2,1)}, u32[]{:S(2)}) copy-start(bf16[2,3,4,4,16,512]{5,4,3,2,1,0:T(8,128)(2,1)} %param.5) | copy-start | bytes 4718596
  14.1 28.4 %collective-permute-start.12 = (bf16[2,3,4,1,16,512]{5,4,3,2,1,0:T(8,128)(2,1)}, bf16[2,3,4,1,16,512]{5,4,3,2,1,0:T(8,128)(2,1)}, u32[]{:S(2)}, u32[]{:S(2)}) collective-permute-start(bf16[2,3,4,1,16,512]{5,4,3,2,1,0:T(8,128)(2,1)} %pad_maximum_fusion.7), channel_id=1, source_target_pairs={{0,2},{2,4},{4,6},{6,8},{8,10},{10,12},{12,14},{14,16},{16,18},{18... | collective-permute-start | bytes 1179656 | tf_op jit(solution)/shard_map/ppermute | solution.py:97
  15.0 21.1 %collective-permute-start.6 = (bf16[2,3,4,4,1,512]{5,3,4,2,1,0:T(4,128)(2,1)S(1)}, bf16[2,3,4,4,1,512]{5,3,4,2,1,0:T(4,128)(2,1)}, u32[]{:S(2)}, u32[]{:S(2)}) collective-permute-start(bf16[2,3,4,4,1,512]{5,3,4,2,1,0:T(4,128)(2,1)S(1)} %copy.159), channel_id=1, source_target_pairs={{0,1},{1,0},{2,3},{3,2},{4,5},{5,4},{6,7},{7,6},{8,9},{9,8},{10,11... | collective-permute-start | bytes 294920 | tf_op jit(solution)/shard_map/ppermute | solution.py:98
  15.9 30.0 %collective-permute-start = (bf16[2,3,4,1,16,512]{5,4,3,2,1,0:T(8,128)(2,1)}, bf16[2,3,4,1,16,512]{5,4,3,2,1,0:T(8,128)(2,1)}, u32[]{:S(2)}, u32[]{:S(2)}) collective-permute-start(bf16[2,3,4,1,16,512]{5,4,3,2,1,0:T(8,128)(2,1)} %slice.143), channel_id=1, source_target_pairs={{0,30},{2,0},{4,2},{6,4},{8,6},{10,8},{12,10},{14,12},{16,14},{18,... | collective-permute-start | bytes 1179656 | tf_op jit(solution)/shard_map/ppermute | solution.py:96
  23.0 2.8 %copy-start.8 = (bf16[1,3,4,4,16,512]{5,4,3,2,1,0:T(8,128)(2,1)S(1)}, bf16[1,3,4,4,16,512]{5,4,3,2,1,0:T(8,128)(2,1)}, u32[]{:S(2)}) copy-start(bf16[1,3,4,4,16,512]{5,4,3,2,1,0:T(8,128)(2,1)} %get-tuple-element.26) | copy-start | bytes 2359300
  23.0 4.6 %copy-start.9 = (bf16[2,64,2048]{2,1,0:T(8,128)(2,1)S(1)}, bf16[2,64,2048]{2,1,0:T(8,128)(2,1)}, u32[]{:S(2)}) copy-start(bf16[2,64,2048]{2,1,0:T(8,128)(2,1)} %param.9) | copy-start | bytes 1572868
  25.7 2.2 %copy-start.52 = (s32[4]{0:T(128)S(1)}, s32[4]{0:T(128)}, u32[]{:S(2)}) copy-start(s32[4]{0:T(128)} %param.8) | copy-start | bytes 52
  30.0 2.2 %copy-start.53 = (s32[4]{0:T(128)S(1)}, s32[4]{0:T(128)}, u32[]{:S(2)}) copy-start(s32[4]{0:T(128)} %param.7) | copy-start | bytes 52
  30.0 2.2 %copy-start.2 = (bf16[1,3,4,4,16,512]{5,4,3,2,1,0:T(8,128)(2,1)S(1)}, bf16[1,3,4,4,16,512]{5,4,3,2,1,0:T(8,128)(2,1)}, u32[]{:S(2)}) copy-start(bf16[1,3,4,4,16,512]{5,4,3,2,1,0:T(8,128)(2,1)} %copy-done.1) | copy-start | bytes 2359300
  30.0 2.3 %copy-start.4 = (bf16[1,3,4,4,16,512]{5,4,3,2,1,0:T(8,128)(2,1)S(1)}, bf16[1,3,4,4,16,512]{5,4,3,2,1,0:T(8,128)(2,1)}, u32[]{:S(2)}) copy-start(bf16[1,3,4,4,16,512]{5,4,3,2,1,0:T(8,128)(2,1)} %copy-done.3) | copy-start | bytes 2359300
  36.0 16.5 %collective-permute-start.19 = (f32[2,2,2,2,1,2,16,512]{7,6,0,5,4,3,2,1:T(8,128)S(1)}, f32[2,2,2,2,1,2,16,512]{7,6,0,5,4,3,2,1:T(8,128)S(1)}, u32[]{:S(2)}, u32[]{:S(2)}) collective-permute-start(f32[2,2,2,2,1,2,16,512]{7,6,0,5,4,3,2,1:T(8,128)S(1)} %constant_dynamic-slice_fusion.4), channel_id=1, source_target_pairs={{0,2},{1,3},{2,0},{3,1},{4,6},{5,7},{6,4},{7,5},{8,10},{9,11},{10,... | collective-permute-start | bytes 3145736 | tf_op jit(solution)/shard_map/ppermute | solution.py:67
  42.1 12.3 %collective-permute-start.7 = (f32[2,2,2,2,1,2,16,512]{7,6,0,1,5,4,3,2:T(8,128)S(1)}, f32[2,2,2,2,1,2,16,512]{7,6,0,1,5,4,3,2:T(8,128)S(1)}, u32[]{:S(2)}, u32[]{:S(2)}) collective-permute-start(f32[2,2,2,2,1,2,16,512]{7,6,0,1,5,4,3,2:T(8,128)S(1)} %constant_dynamic-slice_fusion.14), channel_id=1, source_target_pairs={{0,2},{1,3},{2,0},{3,1},{4,6},{5,7},{6,4},{7,5},{8,10},{9,11},{10,... | collective-permute-start | bytes 3145736 | tf_op jit(solution)/shard_map/ppermute | solution.py:67
  45.6 2.4 %copy-start.29 = (f32[4,4,16]{2,1,0:T(4,128)S(1)}, f32[4,4,16]{2,1,0:T(4,128)}, u32[]{:S(2)}) copy-start(f32[4,4,16]{2,1,0:T(4,128)} %copy-done.28) | copy-start | bytes 3076
  45.6 2.4 %copy-start.31 = (f32[4,4,16]{2,1,0:T(4,128)S(1)}, f32[4,4,16]{2,1,0:T(4,128)}, u32[]{:S(2)}) copy-start(f32[4,4,16]{2,1,0:T(4,128)} %copy-done.30) | copy-start | bytes 3076
  45.6 2.4 %copy-start.33 = (f32[4,4,16]{2,1,0:T(4,128)S(1)}, f32[4,4,16]{2,1,0:T(4,128)}, u32[]{:S(2)}) copy-start(f32[4,4,16]{2,1,0:T(4,128)} %copy-done.32) | copy-start | bytes 3076
  45.6 2.4 %copy-start.49 = (f32[4,4,16]{2,1,0:T(4,128)S(1)}, f32[4,4,16]{2,1,0:T(4,128)}, u32[]{:S(2)}) copy-start(f32[4,4,16]{2,1,0:T(4,128)} %get-tuple-element.43) | copy-start | bytes 3076
  45.6 2.4 %copy-start.50 = (f32[4,4,16]{2,1,0:T(4,128)S(1)}, f32[4,4,16]{2,1,0:T(4,128)}, u32[]{:S(2)}) copy-start(f32[4,4,16]{2,1,0:T(4,128)} %get-tuple-element.45) | copy-start | bytes 3076
  45.7 2.4 %copy-start.51 = (f32[4,4,16]{2,1,0:T(4,128)S(1)}, f32[4,4,16]{2,1,0:T(4,128)}, u32[]{:S(2)}) copy-start(f32[4,4,16]{2,1,0:T(4,128)} %get-tuple-element.47) | copy-start | bytes 3076
  45.7 9.1 %collective-permute-start.13 = (f32[2,2,2,2,1,2,16,512]{7,6,0,5,4,3,2,1:T(8,128)S(1)}, f32[2,2,2,2,1,2,16,512]{7,6,0,5,4,3,2,1:T(8,128)S(1)}, u32[]{:S(2)}, u32[]{:S(2)}) collective-permute-start(f32[2,2,2,2,1,2,16,512]{7,6,0,5,4,3,2,1:T(8,128)S(1)} %constant_dynamic-slice_fusion.9), channel_id=1, source_target_pairs={{0,2},{1,3},{2,0},{3,1},{4,6},{5,7},{6,4},{7,5},{8,10},{9,11},{10,... | collective-permute-start | bytes 3145736 | tf_op jit(solution)/shard_map/ppermute | solution.py:67
  52.3 3.2 %collective-permute-start.1 = (f32[2,2,2,2,1,2,16,512]{7,6,5,4,3,2,1,0:T(8,128)S(1)}, f32[2,2,2,2,1,2,16,512]{7,6,5,4,3,2,1,0:T(8,128)S(1)}, u32[]{:S(2)}, u32[]{:S(2)}) collective-permute-start(f32[2,2,2,2,1,2,16,512]{7,6,5,4,3,2,1,0:T(8,128)S(1)} %constant_dynamic-slice_fusion.19), channel_id=1, source_target_pairs={{0,2},{1,3},{2,0},{3,1},{4,6},{5,7},{6,4},{7,5},{8,10},{9,11},{10,... | collective-permute-start | bytes 3145736 | tf_op jit(solution)/shard_map/ppermute | solution.py:67
  52.8 14.9 %collective-permute-start.20 = (f32[2,2,2,2,1,1,16,512]{7,6,0,5,4,3,2,1:T(8,128)S(1)}, f32[2,2,2,2,1,1,16,512]{7,6,0,5,4,3,2,1:T(8,128)S(1)}, u32[]{:S(2)}, u32[]{:S(2)}) collective-permute-start(f32[2,2,2,2,1,1,16,512]{7,6,0,5,4,3,2,1:T(8,128)S(1)} %constant_dynamic-slice_fusion.3), channel_id=1, source_target_pairs={{0,1},{1,0},{2,3},{3,2},{4,5},{5,4},{6,7},{7,6},{8,9},{9,8},{10,11... | collective-permute-start | bytes 1572872 | tf_op jit(solution)/shard_map/ppermute | solution.py:67
  54.7 14.0 %collective-permute-start.8 = (f32[2,2,2,1,1,2,16,512]{7,6,0,1,5,4,3,2:T(8,128)S(1)}, f32[2,2,2,1,1,2,16,512]{7,6,0,1,5,4,3,2:T(8,128)S(1)}, u32[]{:S(2)}, u32[]{:S(2)}) collective-permute-start(f32[2,2,2,1,1,2,16,512]{7,6,0,1,5,4,3,2:T(8,128)S(1)} %constant_dynamic-slice_fusion.13), channel_id=1, source_target_pairs={{0,4},{1,5},{2,6},{3,7},{4,0},{5,1},{6,2},{7,3},{8,12},{9,13},{10,... | collective-permute-start | bytes 1572872 | tf_op jit(solution)/shard_map/ppermute | solution.py:67
  55.0 22.0 %collective-permute-start.14 = (f32[2,2,1,2,1,2,16,512]{7,6,0,5,4,3,2,1:T(8,128)S(1)}, f32[2,2,1,2,1,2,16,512]{7,6,0,5,4,3,2,1:T(8,128)S(1)}, u32[]{:S(2)}, u32[]{:S(2)}) collective-permute-start(f32[2,2,1,2,1,2,16,512]{7,6,0,5,4,3,2,1:T(8,128)S(1)} %constant_dynamic-slice_fusion.8), channel_id=1, source_target_pairs={{0,8},{1,9},{2,10},{3,11},{4,12},{5,13},{6,14},{7,15},{8,0},{9,1},... | collective-permute-start | bytes 1572872 | tf_op jit(solution)/shard_map/ppermute | solution.py:67
  55.8 23.4 %collective-permute-start.2 = (f32[2,2,2,2,1,1,16,512]{7,6,5,4,3,2,1,0:T(8,128)S(1)}, f32[2,2,2,2,1,1,16,512]{7,6,5,4,3,2,1,0:T(8,128)S(1)}, u32[]{:S(2)}, u32[]{:S(2)}) collective-permute-start(f32[2,2,2,2,1,1,16,512]{7,6,5,4,3,2,1,0:T(8,128)S(1)} %constant_dynamic-slice_fusion.18), channel_id=1, source_target_pairs={{0,1},{1,0},{2,3},{3,2},{4,5},{5,4},{6,7},{7,6},{8,9},{9,8},{10,11... | collective-permute-start | bytes 1572872 | tf_op jit(solution)/shard_map/ppermute | solution.py:67
  67.8 7.1 %collective-permute-start.21 = (f32[2,2,2,1,1,1,16,512]{7,6,0,5,4,3,2,1:T(8,128)S(1)}, f32[2,2,2,1,1,1,16,512]{7,6,0,5,4,3,2,1:T(8,128)S(1)}, u32[]{:S(2)}, u32[]{:S(2)}) collective-permute-start(f32[2,2,2,1,1,1,16,512]{7,6,0,5,4,3,2,1:T(8,128)S(1)} %constant_dynamic-slice_fusion.2), channel_id=1, source_target_pairs={{0,4},{1,5},{2,6},{3,7},{4,0},{5,1},{6,2},{7,3},{8,12},{9,13},{10,... | collective-permute-start | bytes 786440 | tf_op jit(solution)/shard_map/ppermute | solution.py:67
  68.8 8.1 %collective-permute-start.9 = (f32[2,2,1,1,1,2,16,512]{7,6,0,1,5,4,3,2:T(8,128)S(1)}, f32[2,2,1,1,1,2,16,512]{7,6,0,1,5,4,3,2:T(8,128)S(1)}, u32[]{:S(2)}, u32[]{:S(2)}) collective-permute-start(f32[2,2,1,1,1,2,16,512]{7,6,0,1,5,4,3,2:T(8,128)S(1)} %constant_dynamic-slice_fusion.12), channel_id=1, source_target_pairs={{0,8},{1,9},{2,10},{3,11},{4,12},{5,13},{6,14},{7,15},{8,0},{9,1},... | collective-permute-start | bytes 786440 | tf_op jit(solution)/shard_map/ppermute | solution.py:67
  75.0 5.1 %collective-permute-start.22 = (f32[2,2,1,1,1,1,16,512]{7,6,0,5,4,3,2,1:T(8,128)S(1)}, f32[2,2,1,1,1,1,16,512]{7,6,0,5,4,3,2,1:T(8,128)S(1)}, u32[]{:S(2)}, u32[]{:S(2)}) collective-permute-start(f32[2,2,1,1,1,1,16,512]{7,6,0,5,4,3,2,1:T(8,128)S(1)} %constant_dynamic-slice_fusion.1), channel_id=1, source_target_pairs={{0,8},{1,9},{2,10},{3,11},{4,12},{5,13},{6,14},{7,15},{8,0},{9,1},... | collective-permute-start | bytes 393224 | tf_op jit(solution)/shard_map/ppermute | solution.py:67
  76.9 6.4 %collective-permute-start.10 = (f32[2,2,1,1,1,1,16,512]{7,6,0,1,5,4,3,2:T(8,128)S(1)}, f32[2,2,1,1,1,1,16,512]{7,6,0,1,5,4,3,2:T(8,128)S(1)}, u32[]{:S(2)}, u32[]{:S(2)}) collective-permute-start(f32[2,2,1,1,1,1,16,512]{7,6,0,1,5,4,3,2:T(8,128)S(1)} %constant_dynamic-slice_fusion.11), channel_id=1, source_target_pairs={{0,1},{1,0},{2,3},{3,2},{4,5},{5,4},{6,7},{7,6},{8,9},{9,8},{10,11... | collective-permute-start | bytes 393224 | tf_op jit(solution)/shard_map/ppermute | solution.py:67
  77.2 18.2 %collective-permute-start.15 = (f32[2,2,1,2,1,1,16,512]{7,6,0,5,4,3,2,1:T(8,128)S(1)}, f32[2,2,1,2,1,1,16,512]{7,6,0,5,4,3,2,1:T(8,128)S(1)}, u32[]{:S(2)}, u32[]{:S(2)}) collective-permute-start(f32[2,2,1,2,1,1,16,512]{7,6,0,5,4,3,2,1:T(8,128)S(1)} %constant_dynamic-slice_fusion.7), channel_id=1, source_target_pairs={{0,1},{1,0},{2,3},{3,2},{4,5},{5,4},{6,7},{7,6},{8,9},{9,8},{10,11... | collective-permute-start | bytes 786440 | tf_op jit(solution)/shard_map/ppermute | solution.py:67
  79.4 17.0 %collective-permute-start.3 = (f32[2,2,2,1,1,1,16,512]{7,6,5,4,3,2,1,0:T(8,128)S(1)}, f32[2,2,2,1,1,1,16,512]{7,6,5,4,3,2,1,0:T(8,128)S(1)}, u32[]{:S(2)}, u32[]{:S(2)}) collective-permute-start(f32[2,2,2,1,1,1,16,512]{7,6,5,4,3,2,1,0:T(8,128)S(1)} %constant_dynamic-slice_fusion.17), channel_id=1, source_target_pairs={{0,4},{1,5},{2,6},{3,7},{4,0},{5,1},{6,2},{7,3},{8,12},{9,13},{10,... | collective-permute-start | bytes 786440 | tf_op jit(solution)/shard_map/ppermute | solution.py:67
  80.1 6.7 %collective-permute-start.23 = (f32[2,1,1,1,1,1,16,512]{7,6,0,5,4,3,2,1:T(8,128)S(1)}, f32[2,1,1,1,1,1,16,512]{7,6,0,5,4,3,2,1:T(8,128)S(1)}, u32[]{:S(2)}, u32[]{:S(2)}) collective-permute-start(f32[2,1,1,1,1,1,16,512]{7,6,0,5,4,3,2,1:T(8,128)S(1)} %constant_dynamic-slice_fusion), channel_id=1, source_target_pairs={{0,16},{1,17},{2,18},{3,19},{4,20},{5,21},{6,22},{7,23},{8,24},{9,... | collective-permute-start | bytes 196616 | tf_op jit(solution)/shard_map/ppermute | solution.py:67
  83.4 6.0 %collective-permute-start.11 = (f32[2,1,1,1,1,1,16,512]{7,6,0,1,5,4,3,2:T(8,128)S(1)}, f32[2,1,1,1,1,1,16,512]{7,6,0,1,5,4,3,2:T(8,128)S(1)}, u32[]{:S(2)}, u32[]{:S(2)}) collective-permute-start(f32[2,1,1,1,1,1,16,512]{7,6,0,1,5,4,3,2:T(8,128)S(1)} %constant_dynamic-slice_fusion.10), channel_id=1, source_target_pairs={{0,16},{1,17},{2,18},{3,19},{4,20},{5,21},{6,22},{7,23},{8,24},{9,... | collective-permute-start | bytes 196616 | tf_op jit(solution)/shard_map/ppermute | solution.py:67
  86.9 4.9 %collective-permute-start.40 = (bf16[2,1,1,1,1,1,16,512]{7,6,0,5,4,3,2,1:T(8,128)(2,1)S(1)}, bf16[2,1,1,1,1,1,16,512]{7,6,0,5,4,3,2,1:T(8,128)(2,1)S(1)}, u32[]{:S(2)}, u32[]{:S(2)}) collective-permute-start(bf16[2,1,1,1,1,1,16,512]{7,6,0,5,4,3,2,1:T(8,128)(2,1)S(1)} %get-tuple-element.40), channel_id=1, source_target_pairs={{0,16},{1,17},{2,18},{3,19},{4,20},{5,21},{6,22},{7,23},{8,24},{9,... | collective-permute-start | bytes 98312 | tf_op jit(solution)/shard_map/ppermute | solution.py:76
  89.4 4.9 %collective-permute-start.30 = (bf16[2,1,1,1,1,1,16,512]{7,6,0,1,5,4,3,2:T(8,128)(2,1)S(1)}, bf16[2,1,1,1,1,1,16,512]{7,6,0,1,5,4,3,2:T(8,128)(2,1)S(1)}, u32[]{:S(2)}, u32[]{:S(2)}) collective-permute-start(bf16[2,1,1,1,1,1,16,512]{7,6,0,1,5,4,3,2:T(8,128)(2,1)S(1)} %get-tuple-element.36), channel_id=1, source_target_pairs={{0,16},{1,17},{2,18},{3,19},{4,20},{5,21},{6,22},{7,23},{8,24},{9,... | collective-permute-start | bytes 98312 | tf_op jit(solution)/shard_map/ppermute | solution.py:76
  91.8 5.0 %collective-permute-start.41 = (bf16[2,2,1,1,1,1,16,512]{7,6,1,0,5,4,3,2:T(8,128)(2,1)S(1)}, bf16[2,2,1,1,1,1,16,512]{7,6,1,0,5,4,3,2:T(8,128)(2,1)S(1)}, u32[]{:S(2)}, u32[]{:S(2)}) collective-permute-start(bf16[2,2,1,1,1,1,16,512]{7,6,1,0,5,4,3,2:T(8,128)(2,1)S(1)} %copy.144), channel_id=1, source_target_pairs={{0,8},{1,9},{2,10},{3,11},{4,12},{5,13},{6,14},{7,15},{8,0},{9,1},... | collective-permute-start | bytes 196616 | tf_op jit(solution)/shard_map/ppermute | solution.py:76
  94.3 4.3 %collective-permute-start.31 = (bf16[2,2,1,1,1,1,16,512]{7,6,0,1,5,4,3,2:T(8,128)(2,1)S(1)}, bf16[2,2,1,1,1,1,16,512]{7,6,0,1,5,4,3,2:T(8,128)(2,1)S(1)}, u32[]{:S(2)}, u32[]{:S(2)}) collective-permute-start(bf16[2,2,1,1,1,1,16,512]{7,6,0,1,5,4,3,2:T(8,128)(2,1)S(1)} %maximum_select_fusion.27), channel_id=1, source_target_pairs={{0,1},{1,0},{2,3},{3,2},{4,5},{5,4},{6,7},{7,6},{8,9},{9,8},{10,11... | collective-permute-start | bytes 196616 | tf_op jit(solution)/shard_map/ppermute | solution.py:76
  95.5 5.0 %collective-permute-start.16 = (f32[2,2,1,1,1,1,16,512]{7,6,0,5,4,3,2,1:T(8,128)S(1)}, f32[2,2,1,1,1,1,16,512]{7,6,0,5,4,3,2,1:T(8,128)S(1)}, u32[]{:S(2)}, u32[]{:S(2)}) collective-permute-start(f32[2,2,1,1,1,1,16,512]{7,6,0,5,4,3,2,1:T(8,128)S(1)} %constant_dynamic-slice_fusion.6), channel_id=1, source_target_pairs={{0,4},{1,5},{2,6},{3,7},{4,0},{5,1},{6,2},{7,3},{8,12},{9,13},{10,... | collective-permute-start | bytes 393224 | tf_op jit(solution)/shard_map/ppermute | solution.py:67
  96.5 6.3 %collective-permute-start.4 = (f32[2,2,1,1,1,1,16,512]{7,6,5,4,3,2,1,0:T(8,128)S(1)}, f32[2,2,1,1,1,1,16,512]{7,6,5,4,3,2,1,0:T(8,128)S(1)}, u32[]{:S(2)}, u32[]{:S(2)}) collective-permute-start(f32[2,2,1,1,1,1,16,512]{7,6,5,4,3,2,1,0:T(8,128)S(1)} %constant_dynamic-slice_fusion.16), channel_id=1, source_target_pairs={{0,8},{1,9},{2,10},{3,11},{4,12},{5,13},{6,14},{7,15},{8,0},{9,1},... | collective-permute-start | bytes 393224 | tf_op jit(solution)/shard_map/ppermute | solution.py:67
  96.8 6.8 %collective-permute-start.42 = (bf16[2,2,2,1,1,1,16,512]{7,6,5,4,3,2,1,0:T(8,128)(2,1)S(1)}, bf16[2,2,2,1,1,1,16,512]{7,6,5,4,3,2,1,0:T(8,128)(2,1)S(1)}, u32[]{:S(2)}, u32[]{:S(2)}) collective-permute-start(bf16[2,2,2,1,1,1,16,512]{7,6,5,4,3,2,1,0:T(8,128)(2,1)S(1)} %copy.146), channel_id=1, source_target_pairs={{0,4},{1,5},{2,6},{3,7},{4,0},{5,1},{6,2},{7,3},{8,12},{9,13},{10,... | collective-permute-start | bytes 393224 | tf_op jit(solution)/shard_map/ppermute | solution.py:76
  98.7 6.1 %collective-permute-start.32 = (bf16[2,2,1,1,1,2,16,512]{7,6,0,1,5,4,3,2:T(8,128)(2,1)S(1)}, bf16[2,2,1,1,1,2,16,512]{7,6,0,1,5,4,3,2:T(8,128)(2,1)S(1)}, u32[]{:S(2)}, u32[]{:S(2)}) collective-permute-start(bf16[2,2,1,1,1,2,16,512]{7,6,0,1,5,4,3,2:T(8,128)(2,1)S(1)} %maximum_select_fusion.20), channel_id=1, source_target_pairs={{0,8},{1,9},{2,10},{3,11},{4,12},{5,13},{6,14},{7,15},{8,0},{9,1},... | collective-permute-start | bytes 393224 | tf_op jit(solution)/shard_map/ppermute | solution.py:76
  100.5 5.8 %collective-permute-start.17 = (f32[2,1,1,1,1,1,16,512]{7,6,0,5,4,3,2,1:T(8,128)S(1)}, f32[2,1,1,1,1,1,16,512]{7,6,0,5,4,3,2,1:T(8,128)S(1)}, u32[]{:S(2)}, u32[]{:S(2)}) collective-permute-start(f32[2,1,1,1,1,1,16,512]{7,6,0,5,4,3,2,1:T(8,128)S(1)} %constant_dynamic-slice_fusion.5), channel_id=1, source_target_pairs={{0,16},{1,17},{2,18},{3,19},{4,20},{5,21},{6,22},{7,23},{8,24},{9,... | collective-permute-start | bytes 196616 | tf_op jit(solution)/shard_map/ppermute | solution.py:67
  102.8 5.6 %collective-permute-start.5 = (f32[2,1,1,1,1,1,16,512]{7,6,5,4,3,2,1,0:T(8,128)S(1)}, f32[2,1,1,1,1,1,16,512]{7,6,5,4,3,2,1,0:T(8,128)S(1)}, u32[]{:S(2)}, u32[]{:S(2)}) collective-permute-start(f32[2,1,1,1,1,1,16,512]{7,6,5,4,3,2,1,0:T(8,128)S(1)} %constant_dynamic-slice_fusion.15), channel_id=1, source_target_pairs={{0,16},{1,17},{2,18},{3,19},{4,20},{5,21},{6,22},{7,23},{8,24},{9,... | collective-permute-start | bytes 196616 | tf_op jit(solution)/shard_map/ppermute | solution.py:67
  103.7 17.2 %collective-permute-start.43 = (bf16[2,2,2,2,1,1,16,512]{7,6,5,4,3,2,1,0:T(8,128)(2,1)S(1)}, bf16[2,2,2,2,1,1,16,512]{7,6,5,4,3,2,1,0:T(8,128)(2,1)S(1)}, u32[]{:S(2)}, u32[]{:S(2)}) collective-permute-start(bf16[2,2,2,2,1,1,16,512]{7,6,5,4,3,2,1,0:T(8,128)(2,1)S(1)} %maximum_select_fusion.16), channel_id=1, source_target_pairs={{0,1},{1,0},{2,3},{3,2},{4,5},{5,4},{6,7},{7,6},{8,9},{9,8},{10,11... | collective-permute-start | bytes 786440 | tf_op jit(solution)/shard_map/ppermute | solution.py:76
  104.8 16.2 %collective-permute-start.33 = (bf16[2,2,2,1,1,2,16,512]{7,6,0,1,5,4,3,2:T(8,128)(2,1)S(1)}, bf16[2,2,2,1,1,2,16,512]{7,6,0,1,5,4,3,2:T(8,128)(2,1)S(1)}, u32[]{:S(2)}, u32[]{:S(2)}) collective-permute-start(bf16[2,2,2,1,1,2,16,512]{7,6,0,1,5,4,3,2:T(8,128)(2,1)S(1)} %maximum_select_fusion.12), channel_id=1, source_target_pairs={{0,4},{1,5},{2,6},{3,7},{4,0},{5,1},{6,2},{7,3},{8,12},{9,13},{10,... | collective-permute-start | bytes 786440 | tf_op jit(solution)/shard_map/ppermute | solution.py:76
  106.3 5.2 %collective-permute-start.35 = (bf16[2,1,1,1,1,1,16,512]{7,6,0,5,4,3,2,1:T(8,128)(2,1)S(1)}, bf16[2,1,1,1,1,1,16,512]{7,6,0,5,4,3,2,1:T(8,128)(2,1)S(1)}, u32[]{:S(2)}, u32[]{:S(2)}) collective-permute-start(bf16[2,1,1,1,1,1,16,512]{7,6,0,5,4,3,2,1:T(8,128)(2,1)S(1)} %get-tuple-element.38), channel_id=1, source_target_pairs={{0,16},{1,17},{2,18},{3,19},{4,20},{5,21},{6,22},{7,23},{8,24},{9,... | collective-permute-start | bytes 98312 | tf_op jit(solution)/shard_map/ppermute | solution.py:76
  109.0 16.7 %collective-permute-start.24 = (f32[4,2,1,1,1,1,1,16,512]{8,7,1,0,6,5,4,3,2:T(8,128)S(1)}, f32[4,2,1,1,1,1,1,16,512]{8,7,1,0,6,5,4,3,2:T(8,128)S(1)}, u32[]{:S(2)}, u32[]{:S(2)}) collective-permute-start(f32[4,2,1,1,1,1,1,16,512]{8,7,1,0,6,5,4,3,2:T(8,128)S(1)} %bitcast.636), channel_id=1, source_target_pairs={{0,1},{1,0},{2,3},{3,2},{4,5},{5,4},{6,7},{7,6},{8,9},{9,8},{10,11... | collective-permute-start | bytes 786440 | tf_op jit(solution)/shard_map/ppermute | solution.py:76
  110.3 5.2 %collective-permute-start.25 = (bf16[2,1,1,1,1,1,16,512]{7,6,0,5,4,3,2,1:T(8,128)(2,1)S(1)}, bf16[2,1,1,1,1,1,16,512]{7,6,0,5,4,3,2,1:T(8,128)(2,1)S(1)}, u32[]{:S(2)}, u32[]{:S(2)}) collective-permute-start(bf16[2,1,1,1,1,1,16,512]{7,6,0,5,4,3,2,1:T(8,128)(2,1)S(1)} %bitcast.645), channel_id=1, source_target_pairs={{0,16},{1,17},{2,18},{3,19},{4,20},{5,21},{6,22},{7,23},{8,24},{9,... | collective-permute-start | bytes 98312 | tf_op jit(solution)/shard_map/ppermute | solution.py:76
  111.5 5.0 %collective-permute-start.36 = (bf16[2,2,1,1,1,1,16,512]{7,6,0,5,4,3,2,1:T(8,128)(2,1)S(1)}, bf16[2,2,1,1,1,1,16,512]{7,6,0,5,4,3,2,1:T(8,128)(2,1)S(1)}, u32[]{:S(2)}, u32[]{:S(2)}) collective-permute-start(bf16[2,2,1,1,1,1,16,512]{7,6,0,5,4,3,2,1:T(8,128)(2,1)S(1)} %bitcast_select_fusion.1), channel_id=1, source_target_pairs={{0,4},{1,5},{2,6},{3,7},{4,0},{5,1},{6,2},{7,3},{8,12},{9,13},{10,... | collective-permute-start | bytes 196616 | tf_op jit(solution)/shard_map/ppermute | solution.py:76
  115.5 4.3 %collective-permute-start.26 = (bf16[2,2,1,1,1,1,16,512]{7,6,5,4,3,2,1,0:T(8,128)(2,1)S(1)}, bf16[2,2,1,1,1,1,16,512]{7,6,5,4,3,2,1,0:T(8,128)(2,1)S(1)}, u32[]{:S(2)}, u32[]{:S(2)}) collective-permute-start(bf16[2,2,1,1,1,1,16,512]{7,6,5,4,3,2,1,0:T(8,128)(2,1)S(1)} %maximum_select_fusion.26), channel_id=1, source_target_pairs={{0,8},{1,9},{2,10},{3,11},{4,12},{5,13},{6,14},{7,15},{8,0},{9,1},... | collective-permute-start | bytes 196616 | tf_op jit(solution)/shard_map/ppermute | solution.py:76
  116.5 5.1 %collective-permute-start.37 = (bf16[2,2,1,2,1,1,16,512]{7,6,0,5,4,3,2,1:T(8,128)(2,1)S(1)}, bf16[2,2,1,2,1,1,16,512]{7,6,0,5,4,3,2,1:T(8,128)(2,1)S(1)}, u32[]{:S(2)}, u32[]{:S(2)}) collective-permute-start(bf16[2,2,1,2,1,1,16,512]{7,6,0,5,4,3,2,1:T(8,128)(2,1)S(1)} %maximum_select_fusion.22), channel_id=1, source_target_pairs={{0,1},{1,0},{2,3},{3,2},{4,5},{5,4},{6,7},{7,6},{8,9},{9,8},{10,11... | collective-permute-start | bytes 393224 | tf_op jit(solution)/shard_map/ppermute | solution.py:76
  119.9 5.0 %collective-permute-start.27 = (bf16[2,2,2,1,1,1,16,512]{7,6,5,4,3,2,1,0:T(8,128)(2,1)S(1)}, bf16[2,2,2,1,1,1,16,512]{7,6,5,4,3,2,1,0:T(8,128)(2,1)S(1)}, u32[]{:S(2)}, u32[]{:S(2)}) collective-permute-start(bf16[2,2,2,1,1,1,16,512]{7,6,5,4,3,2,1,0:T(8,128)(2,1)S(1)} %maximum_select_fusion.18), channel_id=1, source_target_pairs={{0,4},{1,5},{2,6},{3,7},{4,0},{5,1},{6,2},{7,3},{8,12},{9,13},{10,... | collective-permute-start | bytes 393224 | tf_op jit(solution)/shard_map/ppermute | solution.py:76
  120.9 10.9 %collective-permute-start.44 = (bf16[2,2,2,2,1,2,16,512]{7,6,5,4,3,2,1,0:T(8,128)(2,1)S(1)}, bf16[2,2,2,2,1,2,16,512]{7,6,5,4,3,2,1,0:T(8,128)(2,1)S(1)}, u32[]{:S(2)}, u32[]{:S(2)}) collective-permute-start(bf16[2,2,2,2,1,2,16,512]{7,6,5,4,3,2,1,0:T(8,128)(2,1)S(1)} %maximum_select_fusion.8), channel_id=1, source_target_pairs={{0,2},{1,3},{2,0},{3,1},{4,6},{5,7},{6,4},{7,5},{8,10},{9,11},{10,... | collective-permute-start | bytes 1572872 | tf_op jit(solution)/shard_map/ppermute | solution.py:76
  121.1 10.6 %collective-permute-start.34 = (bf16[2,2,2,2,1,2,16,512]{7,6,0,1,5,4,3,2:T(8,128)(2,1)S(1)}, bf16[2,2,2,2,1,2,16,512]{7,6,0,1,5,4,3,2:T(8,128)(2,1)S(1)}, u32[]{:S(2)}, u32[]{:S(2)}) collective-permute-start(bf16[2,2,2,2,1,2,16,512]{7,6,0,1,5,4,3,2:T(8,128)(2,1)S(1)} %maximum_select_fusion.6), channel_id=1, source_target_pairs={{0,2},{1,3},{2,0},{3,1},{4,6},{5,7},{6,4},{7,5},{8,10},{9,11},{10,... | collective-permute-start | bytes 1572872 | tf_op jit(solution)/shard_map/ppermute | solution.py:76
  121.7 8.3 %collective-permute-start.38 = (bf16[2,2,1,2,1,2,16,512]{7,6,0,5,4,3,2,1:T(8,128)(2,1)S(1)}, bf16[2,2,1,2,1,2,16,512]{7,6,0,5,4,3,2,1:T(8,128)(2,1)S(1)}, u32[]{:S(2)}, u32[]{:S(2)}) collective-permute-start(bf16[2,2,1,2,1,2,16,512]{7,6,0,5,4,3,2,1:T(8,128)(2,1)S(1)} %maximum_select_fusion.14), channel_id=1, source_target_pairs={{0,8},{1,9},{2,10},{3,11},{4,12},{5,13},{6,14},{7,15},{8,0},{9,1},... | collective-permute-start | bytes 786440 | tf_op jit(solution)/shard_map/ppermute | solution.py:76
  125.0 6.4 %collective-permute-start.28 = (bf16[2,2,2,2,1,1,16,512]{7,6,5,4,3,2,1,0:T(8,128)(2,1)S(1)}, bf16[2,2,2,2,1,1,16,512]{7,6,5,4,3,2,1,0:T(8,128)(2,1)S(1)}, u32[]{:S(2)}, u32[]{:S(2)}) collective-permute-start(bf16[2,2,2,2,1,1,16,512]{7,6,5,4,3,2,1,0:T(8,128)(2,1)S(1)} %maximum_select_fusion.10), channel_id=1, source_target_pairs={{0,1},{1,0},{2,3},{3,2},{4,5},{5,4},{6,7},{7,6},{8,9},{9,8},{10,11... | collective-permute-start | bytes 786440 | tf_op jit(solution)/shard_map/ppermute | solution.py:76
  130.1 6.8 %collective-permute-start.39 = (bf16[2,2,2,2,1,2,16,512]{7,6,0,5,4,3,2,1:T(8,128)(2,1)S(1)}, bf16[2,2,2,2,1,2,16,512]{7,6,0,5,4,3,2,1:T(8,128)(2,1)}, u32[]{:S(2)}, u32[]{:S(2)}) collective-permute-start(bf16[2,2,2,2,1,2,16,512]{7,6,0,5,4,3,2,1:T(8,128)(2,1)S(1)} %maximum_select_fusion.7), channel_id=1, source_target_pairs={{0,2},{1,3},{2,0},{3,1},{4,6},{5,7},{6,4},{7,5},{8,10},{9,11},{10,... | collective-permute-start | bytes 1572872 | tf_op jit(solution)/shard_map/ppermute | solution.py:76
  131.5 8.6 %collective-permute-start.29 = (bf16[2,2,2,2,1,2,16,512]{7,6,5,4,3,2,1,0:T(8,128)(2,1)S(1)}, bf16[2,2,2,2,1,2,16,512]{7,6,5,4,3,2,1,0:T(8,128)(2,1)}, u32[]{:S(2)}, u32[]{:S(2)}) collective-permute-start(bf16[2,2,2,2,1,2,16,512]{7,6,5,4,3,2,1,0:T(8,128)(2,1)S(1)} %maximum_select_fusion.5), channel_id=1, source_target_pairs={{0,2},{1,3},{2,0},{3,1},{4,6},{5,7},{6,4},{7,5},{8,10},{9,11},{10,... | collective-permute-start | bytes 1572872 | tf_op jit(solution)/shard_map/ppermute | solution.py:76
  (36 other events, 30.5 us)
